TPU v7x, 32 devices: a whole 2x2x4 slice. The times are simulated.
32 devices in a mesh: pipe: 4 (over z), sx: 4 (over y, x), sy: 2 (over core).
Axes of the slice: x: 2, y: 2, z: 4, core: 2. Of those that a mesh axis runs over, the one named last changes fastest.
Arguments:
- segment_inputs: bfloat16 [4, 1, 4, 2, 512, 128], P('pipe', None, 'sx', 'sy'), may hold values from -6 to 6
- out_cotangent: bfloat16 [1, 4, 2, 512, 128], P(None, 'sx', 'sy'), may hold values from -6 to 6
- neighbours: int32 [1, 4, 2, 1, 27], P(None, 'sx', 'sy'), may hold values from 0 to 1, as said below
- block_counts: int32 [1, 4, 2], P(None, 'sx', 'sy'), may hold values from 1 to 1, as said below
- norm_gain: float32 [4, 128], P('pipe'), may hold values from 0.1 to 1.9
- kernel: bfloat16 [4, 3456, 128], P('pipe', 'sx'), may hold values from -0.109375 to 0.109375
Outputs:
- grad_inputs: bfloat16 [4, 1, 4, 2, 512, 128], P('pipe', None, 'sx', 'sy')
- kernel_grad: float32 [4, 3456, 128], P('pipe', 'sx')
Inputs may be any that keep to these rules, and one draw needn't show every extreme that they name: `neighbours`: entry [m, a, b, s, (i + 1) * 9 + (j + 1) * 3 + (k + 1)], i, j, k in -1..1, is the slot in the list of slab (a + i, b + j) of the occupied block lying i, j, k blocks from slot s of slab (a, b) along x, y, z, or 1 where that block is not occupied, the slab is off the grid, or slot s is padding; it never names a padding slot. `block_counts`: slots 0 to count - 1 of a slab's list hold its occupied blocks; later slots are padding.
All inputs are finite; a program needn't handle non-finite values.
Results may differ from a plain program's by a relative error of at most 0.014.
Values may be sent and summed in bfloat16 or wider, within the bound.
No kernel may reach another device: no remote copies, remote signals or barrier semaphores. Data moves between devices by JAX's collectives and lax.ppermute only.
A program may use at most 64 MiB of HBM per device.

v0:
```python
import jax
import jax.numpy as jnp
from jax import lax
from jax.sharding import PartitionSpec as P

OFFSETS = (-1, 0, 1)


def source_range(offset):
    if offset < 0:
        return slice(7, 8)
    if offset > 0:
        return slice(0, 1)
    return slice(0, 8)


def activate(values, gain_row):
    floats = values.astype(jnp.float32)
    square = jnp.mean(floats * floats, axis=-1, keepdims=True)
    return jax.nn.silu(floats * lax.rsqrt(square + 1e-06) * gain_row)


def with_blank(blocks_in):
    return jnp.concatenate([blocks_in, jnp.zeros_like(blocks_in)], axis=0)


def face_piece(cube, shift_x, shift_y):
    return cube[:, source_range(shift_x), source_range(shift_y)]


def directions():
    return [(sx, sy) for sx in OFFSETS for sy in OFFSETS if (sx, sy) != (0, 0)]


def assemble(centre, received, table):
    slabs_x = []
    for shift_x in OFFSETS:
        rows_y = []
        for shift_y in OFFSETS:
            column = (shift_x + 1) * 3 + (shift_y + 1)
            source = with_blank(centre if (shift_x, shift_y) == (0, 0) else received[(shift_x, shift_y)])
            parts_z = []
            for shift_z in OFFSETS:
                direction = column * 3 + shift_z + 1
                picked = source[table[:, direction]]
                parts_z.append(picked[:, :, :, source_range(shift_z), :])
            rows_y.append(jnp.concatenate(parts_z, axis=3))
        slabs_x.append(jnp.concatenate(rows_y, axis=2))
    return jnp.concatenate(slabs_x, axis=1)


def exchange(cube, axes, sizes, pipe_step):
    received = {}
    for shift_x, shift_y in directions():
        piece = face_piece(cube, shift_x, shift_y)
        route = []
        if pipe_step:
            n_pipe, n_x, n_y = sizes
            for p in range(pipe_step, n_pipe):
                for a in range(n_x):
                    for b in range(n_y):
                        ta, tb = a - shift_x, b - shift_y
                        if 0 <= ta < n_x and 0 <= tb < n_y:
                            route.append(((p * n_x + a) * n_y + b, ((p - pipe_step) * n_x + ta) * n_y + tb))
        else:
            n_x, n_y = sizes
            for a in range(n_x):
                for b in range(n_y):
                    ta, tb = a - shift_x, b - shift_y
                    if 0 <= ta < n_x and 0 <= tb < n_y:
                        route.append((a * n_y + b, ta * n_y + tb))
        received[(shift_x, shift_y)] = lax.ppermute(piece, axes, route)
    return received


def columns(padded, rows, sign):
    taps = []
    for tap_x in OFFSETS:
        for tap_y in OFFSETS:
            for tap_z in OFFSETS:
                taps.append(
                    padded[
                        :,
                        1 + sign * tap_x : 9 + sign * tap_x,
                        1 + sign * tap_y : 9 + sign * tap_y,
                        1 + sign * tap_z : 9 + sign * tap_z,
                        :,
                    ]
                )
    stacked = jnp.stack(taps, axis=-2)
    return stacked.reshape(rows, len(taps) * padded.shape[-1])


def finish_grad(values, grad_live, live_now, grad_act, gain_row):
    _, pullback = jax.vjp(lambda floats: activate(floats, gain_row), values.astype(jnp.float32))
    (through,) = pullback(grad_act)
    summed = grad_live.astype(jnp.float32) + through
    result = jnp.where(live_now[:, None], summed, jnp.zeros_like(summed))
    return result.astype(jnp.bfloat16)


def shards(segment_inputs, out_cotangent, neighbours, block_counts, norm_gain, kernel):
    n_pipe = lax.axis_size("pipe")
    n_x = lax.axis_size("sx")
    n_y = lax.axis_size("sy")
    segment_place = lax.axis_index("pipe")
    micro_count = segment_inputs.shape[1]
    row_count = segment_inputs.shape[4]
    channels = segment_inputs.shape[5]
    blocks = row_count // 512
    taps = 27
    weights = lax.all_gather(kernel[0], "sx", axis=0, tiled=True)
    flipped = weights.reshape(taps, channels, channels).transpose(0, 2, 1).reshape(taps * channels, channels)
    gain_row = norm_gain[0]
    inputs = segment_inputs[0, :, 0, 0]
    cotangent = out_cotangent[:, 0, 0]
    tables = neighbours[:, 0, 0]
    slot_ids = jnp.arange(row_count, dtype=jnp.int32) // 512
    live_rows = slot_ids[None, :] < block_counts[:, 0, 0][:, None]

    def cube(values):
        return values.reshape(blocks, 8, 8, 8, channels)

    grads_out = []
    kernel_total = jnp.zeros((taps * channels, channels), jnp.float32)
    for micro in range(micro_count):
        table = tables[micro]
        live_now = live_rows[micro]
        values = inputs[micro]
        activation = activate(values, gain_row).astype(jnp.bfloat16)
        start = cotangent[micro]
        start = jnp.where(live_now[:, None], start, jnp.zeros_like(start))
        both = jnp.concatenate([cube(activation), cube(start)], axis=-1)
        got = exchange(both, ("sx", "sy"), (n_x, n_y), 0)
        act_pad = assemble(cube(activation), {k: v[..., :channels] for k, v in got.items()}, table)
        act_cols = columns(act_pad, row_count, 1)
        centre = start
        received = {k: v[..., channels:] for k, v in got.items()}
        kept_dy = start
        kept_grad = jnp.zeros((row_count, channels), jnp.bfloat16)
        for tick in range(n_pipe):
            active = segment_place == n_pipe - 1 - tick
            grad_pad = assemble(cube(centre), received, table)
            grad_act = jnp.dot(columns(grad_pad, row_count, -1), flipped, preferred_element_type=jnp.float32)
            result = finish_grad(values, centre, live_now, grad_act, gain_row)
            kept_dy = jnp.where(active, centre, kept_dy)
            kept_grad = jnp.where(active, result, kept_grad)
            if tick < n_pipe - 1:
                down = [(p, p - 1) for p in range(1, n_pipe)]
                centre = lax.ppermute(result, "pipe", down)
                received = exchange(cube(result), ("pipe", "sx", "sy"), (n_pipe, n_x, n_y), 1)
        kernel_total = kernel_total + lax.dot_general(
            act_cols, kept_dy, (((0,), (0,)), ((), ())), preferred_element_type=jnp.float32
        )
        grads_out.append(kept_grad)
    grad_store = jnp.stack(grads_out)
    norm_scale = float(n_x * n_y * micro_count * row_count) ** (-0.5)
    kernel_term = kernel_total * norm_scale
    shard_rows = kernel.shape[1]
    summed = lax.psum(kernel_term.astype(jnp.bfloat16), "sy").astype(jnp.float32)
    kernel_share = lax.psum_scatter(
        lax.slice_in_dim(summed, 0, shard_rows * n_x, axis=0).astype(jnp.bfloat16),
        "sx",
        scatter_dimension=0,
        tiled=True,
    ).astype(jnp.float32)
    return (grad_store[None, :, None, None], kernel_share[None])


def solution(mesh):
    return jax.shard_map(
        shards,
        mesh=mesh,
        in_specs=(
            P("pipe", None, "sx", "sy", None, None),
            P(None, "sx", "sy", None, None),
            P(None, "sx", "sy", None, None),
            P(None, "sx", "sy"),
            P("pipe", None),
            P("pipe", "sx", None),
        ),
        out_specs=(P("pipe", None, "sx", "sy", None, None), P("pipe", "sx", None)),
        check_vma=False,
    )
```

profile of v0, /device:TPU:21, one launch (start us, length us, event | category | flops | bytes accessed | tf_op | source)
XLA Modules:
  0.0 276.5 jit_solution(7714859741776979580)
XLA Ops:
  7.2 1.1 fusion.13
  9.1 1.0 broadcast_select_fusion
  10.1 1.1 multiply_convert_fusion
  11.2 3.6 %collective-permute-start.4 = (bf16[1,1,1,8,256]{4,3,2,1,0:T(8,128)(2,1)S(1)}, bf16[1,1,1,8,256]{4,3,2,1,0:T(8,128)(2,1)S(1)}, u32[]{:S(2)}, u32[]{:S(2)}) collective-permute-start(bf16[1,1,1,8,256]{4,3,2,1,0:T(8,128)(2,1)S(1)} %get-tuple-element.1489), channel_id=1, source_target_pairs={{3,0},{5,2},{7,4},{11,8},{13,10},{15,12},{19,16},{21,18},{23,20},{... | collective-permute-start | bytes 12296 | tf_op jit(solution)/shard_map/ppermute | solution.py:72
  14.8 2.2 collective-permute-start.6
  17.1 4.0 %collective-permute-start.3 = (bf16[1,1,8,8,256]{4,3,2,1,0:T(8,128)(2,1)S(1)}, bf16[1,1,8,8,256]{4,3,2,1,0:T(8,128)(2,1)S(1)}, u32[]{:S(2)}, u32[]{:S(2)}) collective-permute-start(bf16[1,1,8,8,256]{4,3,2,1,0:T(8,128)(2,1)S(1)} %get-tuple-element.1492), channel_id=1, source_target_pairs={{2,0},{3,1},{4,2},{5,3},{6,4},{7,5},{10,8},{11,9},{12,10},{13,11},... | collective-permute-start | bytes 98312 | tf_op jit(solution)/shard_map/ppermute | solution.py:72
  21.0 1.3 collective-permute-start.2
  22.4 2.9 %collective-permute-start.1 = (bf16[1,8,1,8,256]{4,3,2,1,0:T(8,128)(2,1)S(1)}, bf16[1,8,1,8,256]{4,3,2,1,0:T(8,128)(2,1)S(1)}, u32[]{:S(2)}, u32[]{:S(2)}) collective-permute-start(bf16[1,8,1,8,256]{4,3,2,1,0:T(8,128)(2,1)S(1)} %get-tuple-element.1494), channel_id=1, source_target_pairs={{1,0},{3,2},{5,4},{7,6},{9,8},{11,10},{13,12},{15,14},{17,16},{19,... | collective-permute-start | bytes 98312 | tf_op jit(solution)/shard_map/ppermute | solution.py:72
  25.3 2.1 fusion.89
  41.2 1.6 fusion.90
  50.8 13.0 %all-gather = bf16[1,3456,128]{2,1,0:T(8,128)(2,1)S(1)} all-gather(bf16[1,864,128]{2,1,0:T(8,128)(2,1)} %param.11), channel_id=2, replica_groups=mesh['pipe'=4,'sx'=4,'sy'=2] {'sx'}, dimensions={1}, use_global_device_ids=true | all-gather | bytes 1105920 | tf_op jit(solution)/shard_map/all_gather | solution.py:112
  78.4 1.3 copy.138
  94.9 1.3 collective-permute-start
  96.2 3.5 %collective-permute-start.7 = (bf16[1,1,1,8,256]{4,3,2,1,0:T(8,128)(2,1)S(1)}, bf16[1,1,1,8,256]{4,3,2,1,0:T(8,128)(2,1)S(1)}, u32[]{:S(2)}, u32[]{:S(2)}) collective-permute-start(bf16[1,1,1,8,256]{4,3,2,1,0:T(8,128)(2,1)S(1)} %get-tuple-element.1490), channel_id=1, source_target_pairs={{1,2},{3,4},{5,6},{9,10},{11,12},{13,14},{17,18},{19,20},{21,22},{... | collective-permute-start | bytes 12296 | tf_op jit(solution)/shard_map/ppermute | solution.py:72
  100.5 1.3 collective-permute-start.5
  101.8 4.5 %collective-permute-done.5 = bf16[1,1,1,8,256]{4,3,2,1,0:T(8,128)(2,1)S(1)} collective-permute-done((bf16[1,1,1,8,256]{4,3,2,1,0:T(8,128)(2,1)S(1)}, bf16[1,1,1,8,256]{4,3,2,1,0:T(8,128)(2,1)S(1)}, u32[]{:S(2)}, u32[]{:S(2)}) %collective-permute-start.5) | collective-permute-done | bytes 4128 | tf_op jit(solution)/shard_map/ppermute | solution.py:72
  109.5 1.2 fusion.35
  111.1 2.1 collective-permute-start.8
  113.3 2.1 collective-permute-start.13
  115.5 1.9 collective-permute-start.12
  117.4 1.3 collective-permute-start.11
  118.7 1.3 collective-permute-start.10
  123.1 1.3 collective-permute-start.9
  124.4 1.3 collective-permute-start.16
  126.5 1.3 collective-permute-start.14
  127.8 5.4 %collective-permute-done.14 = bf16[1,1,1,8,128]{4,3,2,1,0:T(8,128)(2,1)S(1)} collective-permute-done((bf16[1,1,1,8,128]{4,3,2,1,0:T(8,128)(2,1)S(1)}, bf16[1,1,1,8,128]{4,3,2,1,0:T(8,128)(2,1)S(1)}, u32[]{:S(2)}, u32[]{:S(2)}) %collective-permute-start.14) | collective-permute-done | bytes 2080 | tf_op jit(solution)/shard_map/ppermute | solution.py:72
  133.2 5.8 %collective-permute-start.15 = (bf16[1,1,8,8,128]{4,3,2,1,0:T(8,128)(2,1)S(1)}, bf16[1,1,8,8,128]{4,3,2,1,0:T(8,128)(2,1)S(1)}, u32[]{:S(2)}, u32[]{:S(2)}) collective-permute-start(bf16[1,1,8,8,128]{4,3,2,1,0:T(8,128)(2,1)S(1)} %get-tuple-element.1531), channel_id=1, source_target_pairs={{8,2},{9,3},{10,4},{11,5},{12,6},{13,7},{16,10},{17,11},{18,12},{1... | collective-permute-start | bytes 49160 | tf_op jit(solution)/shard_map/ppermute | solution.py:72
  142.5 1.2 fusion.36
  144.1 3.6 %collective-permute-start.17 = (bf16[512,128]{1,0:T(8,128)(2,1)S(1)}, bf16[512,128]{1,0:T(8,128)(2,1)S(1)}, u32[]{:S(2)}, u32[]{:S(2)}) collective-permute-start(bf16[512,128]{1,0:T(8,128)(2,1)S(1)} %fusion.6), channel_id=1, source_target_pairs={{8,0},{16,8},{24,16},{9,1},{17,9},{25,17},{10,2},{18,10},{26,18},{... | collective-permute-start | bytes 393224 | tf_op jit(solution)/shard_map/ppermute | solution.py:150
  147.7 1.3 collective-permute-start.22
  149.1 1.9 collective-permute-start.21
  151.0 1.3 collective-permute-start.20
  152.3 1.3 collective-permute-start.19
  153.6 1.3 collective-permute-start.18
  154.9 1.9 collective-permute-done.20
  156.8 1.3 collective-permute-start.25
  158.8 1.3 collective-permute-start.23
  160.1 5.4 %collective-permute-done.23 = bf16[1,1,1,8,128]{4,3,2,1,0:T(8,128)(2,1)S(1)} collective-permute-done((bf16[1,1,1,8,128]{4,3,2,1,0:T(8,128)(2,1)S(1)}, bf16[1,1,1,8,128]{4,3,2,1,0:T(8,128)(2,1)S(1)}, u32[]{:S(2)}, u32[]{:S(2)}) %collective-permute-start.23) | collective-permute-done | bytes 2080 | tf_op jit(solution)/shard_map/ppermute | solution.py:72
  165.5 3.9 %collective-permute-start.24 = (bf16[1,1,8,8,128]{4,3,2,1,0:T(8,128)(2,1)S(1)}, bf16[1,1,8,8,128]{4,3,2,1,0:T(8,128)(2,1)S(1)}, u32[]{:S(2)}, u32[]{:S(2)}) collective-permute-start(bf16[1,1,8,8,128]{4,3,2,1,0:T(8,128)(2,1)S(1)} %get-tuple-element.1521), channel_id=1, source_target_pairs={{8,2},{9,3},{10,4},{11,5},{12,6},{13,7},{16,10},{17,11},{18,12},{1... | collective-permute-start | bytes 49160 | tf_op jit(solution)/shard_map/ppermute | solution.py:72
  169.7 2.1 collective-permute-done.24
  174.6 1.2 fusion.37
  176.2 1.9 collective-permute-start.26
  178.1 1.3 collective-permute-start.31
  179.5 1.9 collective-permute-start.30
  181.4 1.3 collective-permute-start.29
  182.7 1.7 collective-permute-start.28
  184.4 1.3 collective-permute-start.27
  185.8 1.6 collective-permute-done.29
  187.3 1.3 collective-permute-start.34
  189.3 1.3 collective-permute-start.32
  190.7 5.4 %collective-permute-done.32 = bf16[1,1,1,8,128]{4,3,2,1,0:T(8,128)(2,1)S(1)} collective-permute-done((bf16[1,1,1,8,128]{4,3,2,1,0:T(8,128)(2,1)S(1)}, bf16[1,1,1,8,128]{4,3,2,1,0:T(8,128)(2,1)S(1)}, u32[]{:S(2)}, u32[]{:S(2)}) %collective-permute-start.32) | collective-permute-done | bytes 2080 | tf_op jit(solution)/shard_map/ppermute | solution.py:72
  196.0 4.0 %collective-permute-start.33 = (bf16[1,1,8,8,128]{4,3,2,1,0:T(8,128)(2,1)S(1)}, bf16[1,1,8,8,128]{4,3,2,1,0:T(8,128)(2,1)S(1)}, u32[]{:S(2)}, u32[]{:S(2)}) collective-permute-start(bf16[1,1,8,8,128]{4,3,2,1,0:T(8,128)(2,1)S(1)} %get-tuple-element.1511), channel_id=1, source_target_pairs={{8,2},{9,3},{10,4},{11,5},{12,6},{13,7},{16,10},{17,11},{18,12},{1... | collective-permute-start | bytes 49160 | tf_op jit(solution)/shard_map/ppermute | solution.py:72
  200.4 2.3 collective-permute-done.33
  212.0 0.7 constant_dynamic-update-slice_fusion.95
  213.5 0.7 constant_dynamic-update-slice_fusion.93
  218.7 2.2 fusion
  221.0 0.8 constant_dynamic-update-slice_fusion.86
  221.7 0.7 constant_dynamic-update-slice_fusion.85
  223.9 0.7 constant_dynamic-update-slice_fusion.82
  225.3 3.2 %fusion.38 = (f32[512]{0:T(512)S(1)}, f32[512,128]{1,0:T(8,128)S(1)}) fusion(bf16[1,1,1,1,512,128]{5,4,3,2,1,0:T(8,128)(2,1)S(1)} %copy-done, f32[128]{0:T(128)S(1)} %bitcast.970, f32[512]{0:T(512)S(1)} %fusion.70, bf16[512,3456]{1,0:T(8,128)(2,1)} %bitcast.281, bf16[3456,128]{1,0:T(8,128)(2,1)S(1)} %bitcast.950), kind=kOutput, calls=%fused_computation.238 | convolution fusion | flops 453967360 | bytes 4821504 | tf_op jit(solution)/shard_map/dot_general | solution.py:144
  228.6 18.1 %reduce-scatter.2.cloned.1.call-done = bf16[864,128]{1,0:T(8,128)(2,1)} async-done(((bf16[3456,128]{1,0:T(8,128)(2,1)}), bf16[864,128]{1,0:T(8,128)(2,1)}) %reduce-scatter.2.cloned.1.call-update) | async-done | bytes 221200 | tf_op jit(solution)/shard_map/reduce_scatter | solution.py:161
  246.6 1.0 fusion.40
  247.6 20.3 %all-reduce.47.cloned.1.call-done = bf16[864,128]{1,0:T(8,128)(2,1)} async-done(((bf16[864,128]{1,0:T(8,128)(2,1)}), bf16[864,128]{1,0:T(8,128)(2,1)}) %all-reduce.47.cloned.1.call-update) | async-done | bytes 221200 | tf_op jit(solution)/shard_map/psum | solution.py:160
  267.9 1.7 bitcast_convert_fusion
  (314 shorter events, 33.6 us)
Async XLA Ops:
  7.2 239.4 %reduce-scatter.2.cloned.1.call-start = ((), (), s32[]{:S(2)}) async-start(), calls=%async_computation.1 | async-start | bytes 1105920 | tf_op jit(solution)/shard_map/reduce_scatter | solution.py:161
  11.2 83.7 %collective-permute-start.4 = (bf16[1,1,1,8,256]{4,3,2,1,0:T(8,128)(2,1)S(1)}, bf16[1,1,1,8,256]{4,3,2,1,0:T(8,128)(2,1)S(1)}, u32[]{:S(2)}, u32[]{:S(2)}) collective-permute-start(bf16[1,1,1,8,256]{4,3,2,1,0:T(8,128)(2,1)S(1)} %get-tuple-element.1489), channel_id=1, source_target_pairs={{3,0},{5,2},{7,4},{11,8},{13,10},{15,12},{19,16},{21,18},{23,20},{... | collective-permute-start | bytes 12296 | tf_op jit(solution)/shard_map/ppermute | solution.py:72
  14.8 91.9 %collective-permute-start.6 = (bf16[1,1,8,8,256]{4,3,2,1,0:T(8,128)(2,1)S(1)}, bf16[1,1,8,8,256]{4,3,2,1,0:T(8,128)(2,1)S(1)}, u32[]{:S(2)}, u32[]{:S(2)}) collective-permute-start(bf16[1,1,8,8,256]{4,3,2,1,0:T(8,128)(2,1)S(1)} %get-tuple-element.1491), channel_id=1, source_target_pairs={{0,2},{1,3},{2,4},{3,5},{4,6},{5,7},{8,10},{9,11},{10,12},{11,13},... | collective-permute-start | bytes 98312 | tf_op jit(solution)/shard_map/ppermute | solution.py:72
  17.1 89.4 %collective-permute-start.3 = (bf16[1,1,8,8,256]{4,3,2,1,0:T(8,128)(2,1)S(1)}, bf16[1,1,8,8,256]{4,3,2,1,0:T(8,128)(2,1)S(1)}, u32[]{:S(2)}, u32[]{:S(2)}) collective-permute-start(bf16[1,1,8,8,256]{4,3,2,1,0:T(8,128)(2,1)S(1)} %get-tuple-element.1492), channel_id=1, source_target_pairs={{2,0},{3,1},{4,2},{5,3},{6,4},{7,5},{10,8},{11,9},{12,10},{13,11},... | collective-permute-start | bytes 98312 | tf_op jit(solution)/shard_map/ppermute | solution.py:72
  21.0 75.2 %collective-permute-start.2 = (bf16[1,1,1,8,256]{4,3,2,1,0:T(8,128)(2,1)S(1)}, bf16[1,1,1,8,256]{4,3,2,1,0:T(8,128)(2,1)S(1)}, u32[]{:S(2)}, u32[]{:S(2)}) collective-permute-start(bf16[1,1,1,8,256]{4,3,2,1,0:T(8,128)(2,1)S(1)} %get-tuple-element.1488), channel_id=1, source_target_pairs={{2,1},{4,3},{6,5},{10,9},{12,11},{14,13},{18,17},{20,19},{22,21},{... | collective-permute-start | bytes 12296 | tf_op jit(solution)/shard_map/ppermute | solution.py:72
  22.4 84.2 %collective-permute-start.1 = (bf16[1,8,1,8,256]{4,3,2,1,0:T(8,128)(2,1)S(1)}, bf16[1,8,1,8,256]{4,3,2,1,0:T(8,128)(2,1)S(1)}, u32[]{:S(2)}, u32[]{:S(2)}) collective-permute-start(bf16[1,8,1,8,256]{4,3,2,1,0:T(8,128)(2,1)S(1)} %get-tuple-element.1494), channel_id=1, source_target_pairs={{1,0},{3,2},{5,4},{7,6},{9,8},{11,10},{13,12},{15,14},{17,16},{19,... | collective-permute-start | bytes 98312 | tf_op jit(solution)/shard_map/ppermute | solution.py:72
  94.9 11.7 %collective-permute-start = (bf16[1,8,1,8,256]{4,3,2,1,0:T(8,128)(2,1)S(1)}, bf16[1,8,1,8,256]{4,3,2,1,0:T(8,128)(2,1)S(1)}, u32[]{:S(2)}, u32[]{:S(2)}) collective-permute-start(bf16[1,8,1,8,256]{4,3,2,1,0:T(8,128)(2,1)S(1)} %get-tuple-element.1493), channel_id=1, source_target_pairs={{0,1},{2,3},{4,5},{6,7},{8,9},{10,11},{12,13},{14,15},{16,17},{18,... | collective-permute-start | bytes 98312 | tf_op jit(solution)/shard_map/ppermute | solution.py:72
  96.2 4.2 %collective-permute-start.7 = (bf16[1,1,1,8,256]{4,3,2,1,0:T(8,128)(2,1)S(1)}, bf16[1,1,1,8,256]{4,3,2,1,0:T(8,128)(2,1)S(1)}, u32[]{:S(2)}, u32[]{:S(2)}) collective-permute-start(bf16[1,1,1,8,256]{4,3,2,1,0:T(8,128)(2,1)S(1)} %get-tuple-element.1490), channel_id=1, source_target_pairs={{1,2},{3,4},{5,6},{9,10},{11,12},{13,14},{17,18},{19,20},{21,22},{... | collective-permute-start | bytes 12296 | tf_op jit(solution)/shard_map/ppermute | solution.py:72
  100.5 5.8 %collective-permute-start.5 = (bf16[1,1,1,8,256]{4,3,2,1,0:T(8,128)(2,1)S(1)}, bf16[1,1,1,8,256]{4,3,2,1,0:T(8,128)(2,1)S(1)}, u32[]{:S(2)}, u32[]{:S(2)}) collective-permute-start(bf16[1,1,1,8,256]{4,3,2,1,0:T(8,128)(2,1)S(1)} %get-tuple-element.1487), channel_id=1, source_target_pairs={{0,3},{2,5},{4,7},{8,11},{10,13},{12,15},{16,19},{18,21},{20,23},{... | collective-permute-start | bytes 12296 | tf_op jit(solution)/shard_map/ppermute | solution.py:72
  107.5 2.0 copy-start
  107.6 2.0 copy-start.2
  109.3 1.5 copy-start.1
  111.1 28.6 %collective-permute-start.8 = (bf16[512,128]{1,0:T(8,128)(2,1)S(1)}, bf16[512,128]{1,0:T(8,128)(2,1)S(1)}, u32[]{:S(2)}, u32[]{:S(2)}) collective-permute-start(bf16[512,128]{1,0:T(8,128)(2,1)S(1)} %fusion.3), channel_id=1, source_target_pairs={{8,0},{16,8},{24,16},{9,1},{17,9},{25,17},{10,2},{18,10},{26,18},{... | collective-permute-start | bytes 393224 | tf_op jit(solution)/shard_map/ppermute | solution.py:150
  113.3 9.7 %collective-permute-start.13 = (bf16[1,1,1,8,128]{4,3,2,1,0:T(8,128)(2,1)S(1)}, bf16[1,1,1,8,128]{4,3,2,1,0:T(8,128)(2,1)S(1)}, u32[]{:S(2)}, u32[]{:S(2)}) collective-permute-start(bf16[1,1,1,8,128]{4,3,2,1,0:T(8,128)(2,1)S(1)} %get-tuple-element.1529), channel_id=1, source_target_pairs={{11,0},{13,2},{15,4},{19,8},{21,10},{23,12},{27,16},{29,18},{31,20}} | collective-permute-start | bytes 6152 | tf_op jit(solution)/shard_map/ppermute | solution.py:72
  115.5 23.7 %collective-permute-start.12 = (bf16[1,1,8,8,128]{4,3,2,1,0:T(8,128)(2,1)S(1)}, bf16[1,1,8,8,128]{4,3,2,1,0:T(8,128)(2,1)S(1)}, u32[]{:S(2)}, u32[]{:S(2)}) collective-permute-start(bf16[1,1,8,8,128]{4,3,2,1,0:T(8,128)(2,1)S(1)} %get-tuple-element.1532), channel_id=1, source_target_pairs={{10,0},{11,1},{12,2},{13,3},{14,4},{15,5},{18,8},{19,9},{20,10},{2... | collective-permute-start | bytes 49160 | tf_op jit(solution)/shard_map/ppermute | solution.py:72
  117.4 7.0 %collective-permute-start.11 = (bf16[1,1,1,8,128]{4,3,2,1,0:T(8,128)(2,1)S(1)}, bf16[1,1,1,8,128]{4,3,2,1,0:T(8,128)(2,1)S(1)}, u32[]{:S(2)}, u32[]{:S(2)}) collective-permute-start(bf16[1,1,1,8,128]{4,3,2,1,0:T(8,128)(2,1)S(1)} %get-tuple-element.1530), channel_id=1, source_target_pairs={{10,1},{12,3},{14,5},{18,9},{20,11},{22,13},{26,17},{28,19},{30,21}} | collective-permute-start | bytes 6152 | tf_op jit(solution)/shard_map/ppermute | solution.py:72
  118.7 20.5 %collective-permute-start.10 = (bf16[1,8,1,8,128]{4,3,2,1,0:T(8,128)(2,1)S(1)}, bf16[1,8,1,8,128]{4,3,2,1,0:T(8,128)(2,1)S(1)}, u32[]{:S(2)}, u32[]{:S(2)}) collective-permute-start(bf16[1,8,1,8,128]{4,3,2,1,0:T(8,128)(2,1)S(1)} %get-tuple-element.1534), channel_id=1, source_target_pairs={{9,0},{11,2},{13,4},{15,6},{17,8},{19,10},{21,12},{23,14},{25,16},... | collective-permute-start | bytes 49160 | tf_op jit(solution)/shard_map/ppermute | solution.py:72
  123.1 16.2 %collective-permute-start.9 = (bf16[1,8,1,8,128]{4,3,2,1,0:T(8,128)(2,1)S(1)}, bf16[1,8,1,8,128]{4,3,2,1,0:T(8,128)(2,1)S(1)}, u32[]{:S(2)}, u32[]{:S(2)}) collective-permute-start(bf16[1,8,1,8,128]{4,3,2,1,0:T(8,128)(2,1)S(1)} %get-tuple-element.1533), channel_id=1, source_target_pairs={{8,1},{10,3},{12,5},{14,7},{16,9},{18,11},{20,13},{22,15},{24,17},... | collective-permute-start | bytes 49160 | tf_op jit(solution)/shard_map/ppermute | solution.py:72
  124.4 2.0 collective-permute-start.16
  126.5 6.7 %collective-permute-start.14 = (bf16[1,1,1,8,128]{4,3,2,1,0:T(8,128)(2,1)S(1)}, bf16[1,1,1,8,128]{4,3,2,1,0:T(8,128)(2,1)S(1)}, u32[]{:S(2)}, u32[]{:S(2)}) collective-permute-start(bf16[1,1,1,8,128]{4,3,2,1,0:T(8,128)(2,1)S(1)} %get-tuple-element.1527), channel_id=1, source_target_pairs={{8,3},{10,5},{12,7},{16,11},{18,13},{20,15},{24,19},{26,21},{28,23}} | collective-permute-start | bytes 6152 | tf_op jit(solution)/shard_map/ppermute | solution.py:72
  133.2 6.5 %collective-permute-start.15 = (bf16[1,1,8,8,128]{4,3,2,1,0:T(8,128)(2,1)S(1)}, bf16[1,1,8,8,128]{4,3,2,1,0:T(8,128)(2,1)S(1)}, u32[]{:S(2)}, u32[]{:S(2)}) collective-permute-start(bf16[1,1,8,8,128]{4,3,2,1,0:T(8,128)(2,1)S(1)} %get-tuple-element.1531), channel_id=1, source_target_pairs={{8,2},{9,3},{10,4},{11,5},{12,6},{13,7},{16,10},{17,11},{18,12},{1... | collective-permute-start | bytes 49160 | tf_op jit(solution)/shard_map/ppermute | solution.py:72
  144.1 27.7 %collective-permute-start.17 = (bf16[512,128]{1,0:T(8,128)(2,1)S(1)}, bf16[512,128]{1,0:T(8,128)(2,1)S(1)}, u32[]{:S(2)}, u32[]{:S(2)}) collective-permute-start(bf16[512,128]{1,0:T(8,128)(2,1)S(1)} %fusion.6), channel_id=1, source_target_pairs={{8,0},{16,8},{24,16},{9,1},{17,9},{25,17},{10,2},{18,10},{26,18},{... | collective-permute-start | bytes 393224 | tf_op jit(solution)/shard_map/ppermute | solution.py:150
  147.7 5.8 %collective-permute-start.22 = (bf16[1,1,1,8,128]{4,3,2,1,0:T(8,128)(2,1)S(1)}, bf16[1,1,1,8,128]{4,3,2,1,0:T(8,128)(2,1)S(1)}, u32[]{:S(2)}, u32[]{:S(2)}) collective-permute-start(bf16[1,1,1,8,128]{4,3,2,1,0:T(8,128)(2,1)S(1)} %get-tuple-element.1519), channel_id=1, source_target_pairs={{11,0},{13,2},{15,4},{19,8},{21,10},{23,12},{27,16},{29,18},{31,20}} | collective-permute-start | bytes 6152 | tf_op jit(solution)/shard_map/ppermute | solution.py:72
  149.1 20.4 %collective-permute-start.21 = (bf16[1,1,8,8,128]{4,3,2,1,0:T(8,128)(2,1)S(1)}, bf16[1,1,8,8,128]{4,3,2,1,0:T(8,128)(2,1)S(1)}, u32[]{:S(2)}, u32[]{:S(2)}) collective-permute-start(bf16[1,1,8,8,128]{4,3,2,1,0:T(8,128)(2,1)S(1)} %get-tuple-element.1522), channel_id=1, source_target_pairs={{10,0},{11,1},{12,2},{13,3},{14,4},{15,5},{18,8},{19,9},{20,10},{2... | collective-permute-start | bytes 49160 | tf_op jit(solution)/shard_map/ppermute | solution.py:72
  151.0 5.8 %collective-permute-start.20 = (bf16[1,1,1,8,128]{4,3,2,1,0:T(8,128)(2,1)S(1)}, bf16[1,1,1,8,128]{4,3,2,1,0:T(8,128)(2,1)S(1)}, u32[]{:S(2)}, u32[]{:S(2)}) collective-permute-start(bf16[1,1,1,8,128]{4,3,2,1,0:T(8,128)(2,1)S(1)} %get-tuple-element.1520), channel_id=1, source_target_pairs={{10,1},{12,3},{14,5},{18,9},{20,11},{22,13},{26,17},{28,19},{30,21}} | collective-permute-start | bytes 6152 | tf_op jit(solution)/shard_map/ppermute | solution.py:72
  152.3 17.3 %collective-permute-start.19 = (bf16[1,8,1,8,128]{4,3,2,1,0:T(8,128)(2,1)S(1)}, bf16[1,8,1,8,128]{4,3,2,1,0:T(8,128)(2,1)S(1)}, u32[]{:S(2)}, u32[]{:S(2)}) collective-permute-start(bf16[1,8,1,8,128]{4,3,2,1,0:T(8,128)(2,1)S(1)} %get-tuple-element.1524), channel_id=1, source_target_pairs={{9,0},{11,2},{13,4},{15,6},{17,8},{19,10},{21,12},{23,14},{25,16},... | collective-permute-start | bytes 49160 | tf_op jit(solution)/shard_map/ppermute | solution.py:72
  153.6 16.0 %collective-permute-start.18 = (bf16[1,8,1,8,128]{4,3,2,1,0:T(8,128)(2,1)S(1)}, bf16[1,8,1,8,128]{4,3,2,1,0:T(8,128)(2,1)S(1)}, u32[]{:S(2)}, u32[]{:S(2)}) collective-permute-start(bf16[1,8,1,8,128]{4,3,2,1,0:T(8,128)(2,1)S(1)} %get-tuple-element.1523), channel_id=1, source_target_pairs={{8,1},{10,3},{12,5},{14,7},{16,9},{18,11},{20,13},{22,15},{24,17},... | collective-permute-start | bytes 49160 | tf_op jit(solution)/shard_map/ppermute | solution.py:72
  156.8 2.0 collective-permute-start.25
  158.8 6.7 %collective-permute-start.23 = (bf16[1,1,1,8,128]{4,3,2,1,0:T(8,128)(2,1)S(1)}, bf16[1,1,1,8,128]{4,3,2,1,0:T(8,128)(2,1)S(1)}, u32[]{:S(2)}, u32[]{:S(2)}) collective-permute-start(bf16[1,1,1,8,128]{4,3,2,1,0:T(8,128)(2,1)S(1)} %get-tuple-element.1517), channel_id=1, source_target_pairs={{8,3},{10,5},{12,7},{16,11},{18,13},{20,15},{24,19},{26,21},{28,23}} | collective-permute-start | bytes 6152 | tf_op jit(solution)/shard_map/ppermute | solution.py:72
  165.5 6.3 %collective-permute-start.24 = (bf16[1,1,8,8,128]{4,3,2,1,0:T(8,128)(2,1)S(1)}, bf16[1,1,8,8,128]{4,3,2,1,0:T(8,128)(2,1)S(1)}, u32[]{:S(2)}, u32[]{:S(2)}) collective-permute-start(bf16[1,1,8,8,128]{4,3,2,1,0:T(8,128)(2,1)S(1)} %get-tuple-element.1521), channel_id=1, source_target_pairs={{8,2},{9,3},{10,4},{11,5},{12,6},{13,7},{16,10},{17,11},{18,12},{1... | collective-permute-start | bytes 49160 | tf_op jit(solution)/shard_map/ppermute | solution.py:72
  176.2 26.5 %collective-permute-start.26 = (bf16[512,128]{1,0:T(8,128)(2,1)S(1)}, bf16[512,128]{1,0:T(8,128)(2,1)S(1)}, u32[]{:S(2)}, u32[]{:S(2)}) collective-permute-start(bf16[512,128]{1,0:T(8,128)(2,1)S(1)} %fusion.9), channel_id=1, source_target_pairs={{8,0},{16,8},{24,16},{9,1},{17,9},{25,17},{10,2},{18,10},{26,18},{... | collective-permute-start | bytes 393224 | tf_op jit(solution)/shard_map/ppermute | solution.py:150
  178.1 6.3 %collective-permute-start.31 = (bf16[1,1,1,8,128]{4,3,2,1,0:T(8,128)(2,1)S(1)}, bf16[1,1,1,8,128]{4,3,2,1,0:T(8,128)(2,1)S(1)}, u32[]{:S(2)}, u32[]{:S(2)}) collective-permute-start(bf16[1,1,1,8,128]{4,3,2,1,0:T(8,128)(2,1)S(1)} %get-tuple-element.1509), channel_id=1, source_target_pairs={{11,0},{13,2},{15,4},{19,8},{21,10},{23,12},{27,16},{29,18},{31,20}} | collective-permute-start | bytes 6152 | tf_op jit(solution)/shard_map/ppermute | solution.py:72
  179.5 20.7 %collective-permute-start.30 = (bf16[1,1,8,8,128]{4,3,2,1,0:T(8,128)(2,1)S(1)}, bf16[1,1,8,8,128]{4,3,2,1,0:T(8,128)(2,1)S(1)}, u32[]{:S(2)}, u32[]{:S(2)}) collective-permute-start(bf16[1,1,8,8,128]{4,3,2,1,0:T(8,128)(2,1)S(1)} %get-tuple-element.1512), channel_id=1, source_target_pairs={{10,0},{11,1},{12,2},{13,3},{14,4},{15,5},{18,8},{19,9},{20,10},{2... | collective-permute-start | bytes 49160 | tf_op jit(solution)/shard_map/ppermute | solution.py:72
  181.4 6.0 %collective-permute-start.29 = (bf16[1,1,1,8,128]{4,3,2,1,0:T(8,128)(2,1)S(1)}, bf16[1,1,1,8,128]{4,3,2,1,0:T(8,128)(2,1)S(1)}, u32[]{:S(2)}, u32[]{:S(2)}) collective-permute-start(bf16[1,1,1,8,128]{4,3,2,1,0:T(8,128)(2,1)S(1)} %get-tuple-element.1510), channel_id=1, source_target_pairs={{10,1},{12,3},{14,5},{18,9},{20,11},{22,13},{26,17},{28,19},{30,21}} | collective-permute-start | bytes 6152 | tf_op jit(solution)/shard_map/ppermute | solution.py:72
  182.7 17.5 %collective-permute-start.28 = (bf16[1,8,1,8,128]{4,3,2,1,0:T(8,128)(2,1)S(1)}, bf16[1,8,1,8,128]{4,3,2,1,0:T(8,128)(2,1)S(1)}, u32[]{:S(2)}, u32[]{:S(2)}) collective-permute-start(bf16[1,8,1,8,128]{4,3,2,1,0:T(8,128)(2,1)S(1)} %get-tuple-element.1514), channel_id=1, source_target_pairs={{9,0},{11,2},{13,4},{15,6},{17,8},{19,10},{21,12},{23,14},{25,16},... | collective-permute-start | bytes 49160 | tf_op jit(solution)/shard_map/ppermute | solution.py:72
  184.4 15.9 %collective-permute-start.27 = (bf16[1,8,1,8,128]{4,3,2,1,0:T(8,128)(2,1)S(1)}, bf16[1,8,1,8,128]{4,3,2,1,0:T(8,128)(2,1)S(1)}, u32[]{:S(2)}, u32[]{:S(2)}) collective-permute-start(bf16[1,8,1,8,128]{4,3,2,1,0:T(8,128)(2,1)S(1)} %get-tuple-element.1513), channel_id=1, source_target_pairs={{8,1},{10,3},{12,5},{14,7},{16,9},{18,11},{20,13},{22,15},{24,17},... | collective-permute-start | bytes 49160 | tf_op jit(solution)/shard_map/ppermute | solution.py:72
  187.3 2.0 collective-permute-start.34
  189.3 6.7 %collective-permute-start.32 = (bf16[1,1,1,8,128]{4,3,2,1,0:T(8,128)(2,1)S(1)}, bf16[1,1,1,8,128]{4,3,2,1,0:T(8,128)(2,1)S(1)}, u32[]{:S(2)}, u32[]{:S(2)}) collective-permute-start(bf16[1,1,1,8,128]{4,3,2,1,0:T(8,128)(2,1)S(1)} %get-tuple-element.1507), channel_id=1, source_target_pairs={{8,3},{10,5},{12,7},{16,11},{18,13},{20,15},{24,19},{26,21},{28,23}} | collective-permute-start | bytes 6152 | tf_op jit(solution)/shard_map/ppermute | solution.py:72
  196.0 6.6 %collective-permute-start.33 = (bf16[1,1,8,8,128]{4,3,2,1,0:T(8,128)(2,1)S(1)}, bf16[1,1,8,8,128]{4,3,2,1,0:T(8,128)(2,1)S(1)}, u32[]{:S(2)}, u32[]{:S(2)}) collective-permute-start(bf16[1,1,8,8,128]{4,3,2,1,0:T(8,128)(2,1)S(1)} %get-tuple-element.1511), channel_id=1, source_target_pairs={{8,2},{9,3},{10,4},{11,5},{12,6},{13,7},{16,10},{17,11},{18,12},{1... | collective-permute-start | bytes 49160 | tf_op jit(solution)/shard_map/ppermute | solution.py:72
  220.9 47.0 %all-reduce.47.cloned.1.call-start = ((), (), s32[]{:S(2)}) async-start(), calls=%async_computation.2 | async-start | bytes 442368 | tf_op jit(solution)/shard_map/psum | solution.py:160
Sparse Core Ops, SparseCore 0:
  221.0 25.5 reduce-scatter.1
  248.9 18.9 all-reduce.46
where the time goes:
time: 279 us; the launch traced here: 276 us
  starting transfers between devices  71.6 us (26%)
  waiting for transfers between devices  69.8 us (25%)
  between operations  67.9 us (24%)
  local copies, waits for them, and re-layouts  31.8 us (11%)
  other arithmetic  13.3 us (5%)
  blocking collectives  13 us (5%)
  matrix products  9.01 us (3%)
    ppermute x32, starting transfers between devices, exchange(): received[shift_x, shift_y] = lax.ppermute(piece, axes, route)  63.9 us
    ppermute x32, waiting for transfers between devices, exchange(): received[shift_x, shift_y] = lax.ppermute(piece, axes, route)  31.5 us
    unnamed x126, local copies, waits for them, and re-layouts  22.9 us
    psum x1, waiting for transfers between devices, shards(): lax.psum(kernel_term.astype(jnp.bfloat16), 'sy').astype(jnp.float32)  20.3 us
    reduce_scatter x1, waiting for transfers between devices, shards(): lax.psum_scatter(lax.slice_in_dim(summed, 0, shard_rows * n_x, axis=0).as...  18.1 us
    all_gather x1, blocking collectives, shards(): weights = lax.all_gather(kernel[0], 'sx', axis=0, tiled=True)  13 us
    ppermute x3, starting transfers between devices, shards(): centre = lax.ppermute(result, 'pipe', down)  7.63 us
    dot_general x4, matrix products, shards(): jnp.dot(columns(grad_pad, row_count, -1), flipped, preferred_element_type...  6.85 us
  transfers between devices with their start and end apart: 37, of which 15 were waited for; matrix products, arithmetic and copies ran while one was open for 7% of the time, Pallas kernels for 0%

commit v1 on v0

--- a/solution.py
+++ b/solution.py
@@ -73,22 +73,51 @@
     return received
 
 
-def columns(padded, rows, sign):
-    taps = []
-    for tap_x in OFFSETS:
-        for tap_y in OFFSETS:
-            for tap_z in OFFSETS:
-                taps.append(
-                    padded[
-                        :,
-                        1 + sign * tap_x : 9 + sign * tap_x,
-                        1 + sign * tap_y : 9 + sign * tap_y,
-                        1 + sign * tap_z : 9 + sign * tap_z,
-                        :,
-                    ]
-                )
-    stacked = jnp.stack(taps, axis=-2)
-    return stacked.reshape(rows, len(taps) * padded.shape[-1])
+def conv_data(padded, filters):
+    return lax.conv_general_dilated(
+        padded,
+        filters,
+        (1, 1, 1),
+        "VALID",
+        dimension_numbers=("NDHWC", "DHWIO", "NDHWC"),
+        preferred_element_type=jnp.float32,
+    )
+
+
+def conv_filter(padded, grad_cube):
+    return lax.conv_general_dilated(
+        padded,
+        grad_cube,
+        (1, 1, 1),
+        "VALID",
+        dimension_numbers=("CDHWN", "IDHWO", "NDHWC"),
+        preferred_element_type=jnp.float32,
+    )
+
+
+def gathered(shard, axis):
+    count = lax.axis_size(axis)
+    place = lax.axis_index(axis)
+    parts = [shard]
+    for step in range(1, count):
+        parts.append(lax.ppermute(shard, axis, [(i, (i + step) % count) for i in range(count)]))
+    ordered = jnp.stack(parts)
+    index = (place - jnp.arange(count)) % count
+    slots = jnp.zeros((count,), jnp.int32).at[index].set(jnp.arange(count, dtype=jnp.int32))
+    return ordered[slots].reshape(count * shard.shape[0], *shard.shape[1:])
+
+
+def scattered_sum(full, axis, share_rows):
+    count = lax.axis_size(axis)
+    place = lax.axis_index(axis)
+    total = lax.dynamic_slice_in_dim(full, place * share_rows, share_rows, axis=0).astype(jnp.float32)
+    for step in range(1, count):
+        target = (place + step) % count
+        piece = lax.dynamic_slice_in_dim(full, target * share_rows, share_rows, axis=0)
+        total = total + lax.ppermute(piece, axis, [(i, (i + step) % count) for i in range(count)]).astype(
+            jnp.float32
+        )
+    return total
 
 
 def finish_grad(values, grad_live, live_now, grad_act, gain_row):
@@ -109,8 +138,8 @@
     channels = segment_inputs.shape[5]
     blocks = row_count // 512
     taps = 27
-    weights = lax.all_gather(kernel[0], "sx", axis=0, tiled=True)
-    flipped = weights.reshape(taps, channels, channels).transpose(0, 2, 1).reshape(taps * channels, channels)
+    weights = gathered(kernel[0], "sx")
+    flipped = weights.reshape(3, 3, 3, channels, channels)[::-1, ::-1, ::-1].transpose(0, 1, 2, 4, 3)
     gain_row = norm_gain[0]
     inputs = segment_inputs[0, :, 0, 0]
     cotangent = out_cotangent[:, 0, 0]
@@ -133,7 +162,6 @@
         both = jnp.concatenate([cube(activation), cube(start)], axis=-1)
         got = exchange(both, ("sx", "sy"), (n_x, n_y), 0)
         act_pad = assemble(cube(activation), {k: v[..., :channels] for k, v in got.items()}, table)
-        act_cols = columns(act_pad, row_count, 1)
         centre = start
         received = {k: v[..., channels:] for k, v in got.items()}
         kept_dy = start
@@ -141,7 +169,7 @@
         for tick in range(n_pipe):
             active = segment_place == n_pipe - 1 - tick
             grad_pad = assemble(cube(centre), received, table)
-            grad_act = jnp.dot(columns(grad_pad, row_count, -1), flipped, preferred_element_type=jnp.float32)
+            grad_act = conv_data(grad_pad, flipped).reshape(row_count, channels)
             result = finish_grad(values, centre, live_now, grad_act, gain_row)
             kept_dy = jnp.where(active, centre, kept_dy)
             kept_grad = jnp.where(active, result, kept_grad)
@@ -149,21 +177,19 @@
                 down = [(p, p - 1) for p in range(1, n_pipe)]
                 centre = lax.ppermute(result, "pipe", down)
                 received = exchange(cube(result), ("pipe", "sx", "sy"), (n_pipe, n_x, n_y), 1)
-        kernel_total = kernel_total + lax.dot_general(
-            act_cols, kept_dy, (((0,), (0,)), ((), ())), preferred_element_type=jnp.float32
-        )
+        per_tap = conv_filter(act_pad, cube(kept_dy))
+        kernel_total = kernel_total + per_tap.transpose(1, 2, 3, 0, 4).reshape(taps * channels, channels)
         grads_out.append(kept_grad)
     grad_store = jnp.stack(grads_out)
     norm_scale = float(n_x * n_y * micro_count * row_count) ** (-0.5)
     kernel_term = kernel_total * norm_scale
     shard_rows = kernel.shape[1]
-    summed = lax.psum(kernel_term.astype(jnp.bfloat16), "sy").astype(jnp.float32)
-    kernel_share = lax.psum_scatter(
-        lax.slice_in_dim(summed, 0, shard_rows * n_x, axis=0).astype(jnp.bfloat16),
-        "sx",
-        scatter_dimension=0,
-        tiled=True,
-    ).astype(jnp.float32)
+    over_x = scattered_sum(kernel_term.astype(jnp.bfloat16), "sx", shard_rows)
+    partner = lax.ppermute(over_x, "sy", [(i, i ^ 1) for i in range(n_y)]) if n_y == 2 else None
+    if partner is not None:
+        kernel_share = over_x + partner
+    else:
+        kernel_share = lax.psum(over_x, "sy")
     return (grad_store[None, :, None, None], kernel_share[None])
 
 

time: 279 us -> 215 us (0.77)
  local copies, waits for them, and re-layouts: 31.8 us -> 7.92 us
  waiting for transfers between devices: 69.8 us -> 55.4 us
  between operations: 67.9 us -> 53.7 us
  blocking collectives: 13 us -> 0 us
  matrix products: 9.01 us -> 15.3 us
  other arithmetic: 13.3 us -> 9.33 us
    unnamed x126 -> x42, local copies, waits for them, and re-layouts: 22.9 us -> 0.33 us
    psum x1 -> x0, waiting for transfers between devices: 20.3 us -> none  [shards(): lax.psum(kernel_term.astype(jnp.bfloat16), 'sy').astype(jnp.float32)]
    reduce_scatter x1 -> x0, waiting for transfers between devices: 18.1 us -> none  [shards(): lax.psum_scatter(lax.slice_in_dim(summed, 0, shard_rows * n_x, axis=0).as...]
    all_gather x1 -> x0, blocking collectives: 13 us -> none  [shards(): weights = lax.all_gather(kernel[0], 'sx', axis=0, tiled=True)]
    ppermute x32, waiting for transfers between devices: 31.5 us -> 44 us  [exchange(): received[shift_x, shift_y] = lax.ppermute(piece, axes, route)]
    conv_general_dilated x0 -> x4, matrix products: none -> 11.6 us  [conv_data(): lax.conv_general_dilated(padded, filters, (1, 1, 1), 'VALID', dimension_n...]
    ppermute x0 -> x7, waiting for transfers between devices: none -> 11.4 us  [the longest x3 9.97 us: scattered_sum(): lax.ppermute(piece, axis, [(i, (i + step) % count) for i in range(count)])]
    dot_general x5 -> x0, matrix products: 9.01 us -> none  [the longest x4 6.85 us: shards(): jnp.dot(columns(grad_pad, row_count, -1), flipped, preferred_element_type...]
  transfers between devices with their start and end apart: 37 -> 42, of which waited for: 15 -> 21; matrix products, arithmetic and copies ran while one was open for 7% -> 5% of each run, Pallas kernels for 0% -> 0%
where the time goes in v1:
time: 215 us; the launch traced here: 213 us
  starting transfers between devices  71.1 us (33%)
  waiting for transfers between devices  55.4 us (26%)
  between operations  53.7 us (25%)
  matrix products  15.3 us (7%)
  other arithmetic  9.33 us (4%)
  local copies, waits for them, and re-layouts  7.92 us (4%)
    ppermute x32, starting transfers between devices, exchange(): received[shift_x, shift_y] = lax.ppermute(piece, axes, route)  60 us
    ppermute x32, waiting for transfers between devices, exchange(): received[shift_x, shift_y] = lax.ppermute(piece, axes, route)  44 us
    conv_general_dilated x4, matrix products, conv_data(): lax.conv_general_dilated(padded, filters, (1, 1, 1), 'VALID', dimension_n...  11.6 us
    ppermute x3, waiting for transfers between devices, scattered_sum(): lax.ppermute(piece, axis, [(i, (i + step) % count) for i in range(count)])  9.97 us
    ppermute x3, starting transfers between devices, shards(): centre = lax.ppermute(result, 'pipe', down)  5.92 us
  transfers between devices with their start and end apart: 42, of which 21 were waited for; matrix products, arithmetic and copies ran while one was open for 5% of the time, Pallas kernels for 0%

profile of v1, /device:TPU:21, one launch (start us, length us, event | category | flops | bytes accessed | tf_op | source)
XLA Modules:
  0.0 212.8 jit_solution(3644121627801519813)
XLA Ops:
  0.6 1.2 collective-permute-start.10
  1.8 1.2 collective-permute-start.9
  3.8 1.1 fusion.25
  5.0 1.0 broadcast_select_fusion
  6.0 1.1 multiply_convert_fusion.1
  7.1 5.7 %collective-permute-start.7 = (bf16[1,1,1,8,256]{4,3,2,1,0:T(8,128)(2,1)S(1)}, bf16[1,1,1,8,256]{4,3,2,1,0:T(8,128)(2,1)S(1)}, u32[]{:S(2)}, u32[]{:S(2)}) collective-permute-start(bf16[1,1,1,8,256]{4,3,2,1,0:T(8,128)(2,1)S(1)} %get-tuple-element.1501), channel_id=1, source_target_pairs={{3,0},{5,2},{7,4},{11,8},{13,10},{15,12},{19,16},{21,18},{23,20},{... | collective-permute-start | bytes 12296 | tf_op jit(solution)/shard_map/ppermute | solution.py:72
  12.8 1.9 collective-permute-start.6
  67.6 1.3 collective-permute-start.5
  69.0 3.6 %collective-permute-done.5 = bf16[1,1,1,8,256]{4,3,2,1,0:T(8,128)(2,1)S(1)} collective-permute-done((bf16[1,1,1,8,256]{4,3,2,1,0:T(8,128)(2,1)S(1)}, bf16[1,1,1,8,256]{4,3,2,1,0:T(8,128)(2,1)S(1)}, u32[]{:S(2)}, u32[]{:S(2)}) %collective-permute-start.5) | collective-permute-done | bytes 4128 | tf_op jit(solution)/shard_map/ppermute | solution.py:72
  72.6 1.9 collective-permute-start.2
  75.3 1.3 collective-permute-start
  76.6 4.5 %collective-permute-done = bf16[1,1,1,8,256]{4,3,2,1,0:T(8,128)(2,1)S(1)} collective-permute-done((bf16[1,1,1,8,256]{4,3,2,1,0:T(8,128)(2,1)S(1)}, bf16[1,1,1,8,256]{4,3,2,1,0:T(8,128)(2,1)S(1)}, u32[]{:S(2)}, u32[]{:S(2)}) %collective-permute-start) | collective-permute-done | bytes 4128 | tf_op jit(solution)/shard_map/ppermute | solution.py:72
  81.1 1.3 collective-permute-start.4
  83.2 1.3 collective-permute-start.3
  84.6 1.7 collective-permute-done.3
  86.3 1.9 collective-permute-start.1
  88.5 3.4 %collective-permute-done.1 = bf16[1,1,8,8,256]{4,3,2,1,0:T(8,128)(2,1)S(1)} collective-permute-done((bf16[1,1,8,8,256]{4,3,2,1,0:T(8,128)(2,1)S(1)}, bf16[1,1,8,8,256]{4,3,2,1,0:T(8,128)(2,1)S(1)}, u32[]{:S(2)}, u32[]{:S(2)}) %collective-permute-start.1) | collective-permute-done | bytes 32800 | tf_op jit(solution)/shard_map/ppermute | solution.py:72
  94.2 2.8 %fusion.1 = f32[1,8,8,8,128]{4,0,3,2,1:T(1,128)S(1)} fusion(bf16[3,3,3,128,128]{4,3,2,1,0:T(8,128)(2,1)S(1)} %bitcast.218, bf16[1,10,10,10,128]{4,3,2,1,0:T(8,128)(2,1)S(1)} %maximum_maximum_fusion.4), kind=kOutput, calls=%fused_computation.8 | convolution fusion | flops 452984832 | bytes 1402880 | tf_op jit(solution)/shard_map/conv_general_dilated | solution.py:77
  97.7 2.9 %collective-permute-start.19 = (bf16[1,1,1,8,128]{4,3,2,1,0:T(8,128)(2,1)S(1)}, bf16[1,1,1,8,128]{4,3,2,1,0:T(8,128)(2,1)S(1)}, u32[]{:S(2)}, u32[]{:S(2)}) collective-permute-start(bf16[1,1,1,8,128]{4,3,2,1,0:T(8,128)(2,1)S(1)} %get-tuple-element.1527), channel_id=1, source_target_pairs={{11,0},{13,2},{15,4},{19,8},{21,10},{23,12},{27,16},{29,18},{31,20}} | collective-permute-start | bytes 6152 | tf_op jit(solution)/shard_map/ppermute | solution.py:72
  100.9 2.1 collective-permute-start.11
  103.0 1.9 collective-permute-start.18
  105.0 1.3 collective-permute-start.17
  106.3 2.0 collective-permute-start.16
  108.3 1.3 collective-permute-start.15
  109.6 1.2 collective-permute-done.17
  110.8 1.3 collective-permute-start.14
  112.8 1.3 collective-permute-start.12
  114.1 5.4 %collective-permute-done.12 = bf16[1,1,1,8,128]{4,3,2,1,0:T(8,128)(2,1)S(1)} collective-permute-done((bf16[1,1,1,8,128]{4,3,2,1,0:T(8,128)(2,1)S(1)}, bf16[1,1,1,8,128]{4,3,2,1,0:T(8,128)(2,1)S(1)}, u32[]{:S(2)}, u32[]{:S(2)}) %collective-permute-start.12) | collective-permute-done | bytes 2080 | tf_op jit(solution)/shard_map/ppermute | solution.py:72
  119.5 4.0 %collective-permute-start.13 = (bf16[1,1,8,8,128]{4,3,2,1,0:T(8,128)(2,1)S(1)}, bf16[1,1,8,8,128]{4,3,2,1,0:T(8,128)(2,1)S(1)}, u32[]{:S(2)}, u32[]{:S(2)}) collective-permute-start(bf16[1,1,8,8,128]{4,3,2,1,0:T(8,128)(2,1)S(1)} %get-tuple-element.1530), channel_id=1, source_target_pairs={{8,2},{9,3},{10,4},{11,5},{12,6},{13,7},{16,10},{17,11},{18,12},{1... | collective-permute-start | bytes 49160 | tf_op jit(solution)/shard_map/ppermute | solution.py:72
  124.0 1.8 collective-permute-done.13
  126.8 2.9 %fusion.5 = f32[1,8,8,8,128]{4,0,3,2,1:T(1,128)S(1)} fusion(bf16[3,3,3,128,128]{4,3,2,1,0:T(8,128)(2,1)S(1)} %bitcast.219, bf16[1,1,10,10,128]{4,0,3,2,1:T(2,128)(2,1)S(1)} %copy.37, bf16[1,8,1,10,128]{4,0,3,2,1:T(2,128)(2,1)S(1)} %copy.35, bf16[1,8,8,1,128]{4,0,3,2,1:T(2,128)(2,1)S(1)} %get-tuple-element.1497, ...), kind=kOutput, calls=%fused_computation.12 | convolution fusion | flops 454776832 | bytes 1402880 | tf_op jit(solution)/shard_map/conv_general_dilated | solution.py:77
  130.4 1.9 collective-permute-start.20
  132.4 1.3 collective-permute-start.28
  133.7 1.9 collective-permute-start.27
  135.7 1.3 collective-permute-start.26
  137.0 1.9 collective-permute-start.25
  139.0 1.3 collective-permute-start.24
  140.3 1.3 collective-permute-done.26
  141.6 1.3 collective-permute-start.23
  143.7 1.3 collective-permute-start.21
  145.0 5.4 %collective-permute-done.21 = bf16[1,1,1,8,128]{4,0,3,2,1:T(2,128)(2,1)S(1)} collective-permute-done((bf16[1,1,1,8,128]{4,0,3,2,1:T(2,128)(2,1)S(1)}, bf16[1,1,1,8,128]{4,0,3,2,1:T(2,128)(2,1)S(1)}, u32[]{:S(2)}, u32[]{:S(2)}) %collective-permute-start.21) | collective-permute-done | bytes 2080 | tf_op jit(solution)/shard_map/ppermute | solution.py:72
  150.4 3.8 %collective-permute-start.22 = (bf16[1,1,8,8,128]{4,0,3,2,1:T(2,128)(2,1)S(1)}, bf16[1,1,8,8,128]{4,0,3,2,1:T(2,128)(2,1)S(1)}, u32[]{:S(2)}, u32[]{:S(2)}) collective-permute-start(bf16[1,1,8,8,128]{4,0,3,2,1:T(2,128)(2,1)S(1)} %copy.59), channel_id=1, source_target_pairs={{8,2},{9,3},{10,4},{11,5},{12,6},{13,7},{16,10},{17,11},{18,12},{1... | collective-permute-start | bytes 49160 | tf_op jit(solution)/shard_map/ppermute | solution.py:72
  154.6 2.7 %collective-permute-done.22 = bf16[1,1,8,8,128]{4,0,3,2,1:T(2,128)(2,1)S(1)} collective-permute-done((bf16[1,1,8,8,128]{4,0,3,2,1:T(2,128)(2,1)S(1)}, bf16[1,1,8,8,128]{4,0,3,2,1:T(2,128)(2,1)S(1)}, u32[]{:S(2)}, u32[]{:S(2)}) %collective-permute-start.22) | collective-permute-done | bytes 16416 | tf_op jit(solution)/shard_map/ppermute | solution.py:72
  158.2 2.9 %fusion.4 = f32[1,8,8,8,128]{4,0,3,2,1:T(1,128)S(1)} fusion(bf16[3,3,3,128,128]{4,3,2,1,0:T(8,128)(2,1)S(1)} %bitcast.220, bf16[1,1,1,1,128]{4,0,3,2,1:T(2,128)(2,1)S(1)} %get-tuple-element.1607, bf16[1,1,1,8,128]{4,0,3,2,1:T(2,128)(2,1)S(1)} %constant_dynamic-slice_fusion.40, bf16[1,1,1,1,128]{4,0,3,2,1:T(2,128)(2,1)S(1)} %get-tuple-element.1606, ...), kind=kOutput, calls=%fused_computation.11 | convolution fusion | flops 459896832 | bytes 1402880 | tf_op jit(solution)/shard_map/conv_general_dilated | solution.py:77
  161.8 1.9 collective-permute-start.29
  163.7 1.3 collective-permute-start.37
  165.1 1.9 collective-permute-start.36
  167.0 1.3 collective-permute-start.35
  168.4 1.3 collective-permute-start.34
  169.8 1.3 collective-permute-start.33
  171.1 1.7 collective-permute-done.35
  172.9 1.3 collective-permute-start.32
  174.9 1.3 collective-permute-start.30
  176.2 5.4 %collective-permute-done.30 = bf16[1,1,1,8,128]{4,0,3,2,1:T(2,128)(2,1)S(1)} collective-permute-done((bf16[1,1,1,8,128]{4,0,3,2,1:T(2,128)(2,1)S(1)}, bf16[1,1,1,8,128]{4,0,3,2,1:T(2,128)(2,1)S(1)}, u32[]{:S(2)}, u32[]{:S(2)}) %collective-permute-start.30) | collective-permute-done | bytes 2080 | tf_op jit(solution)/shard_map/ppermute | solution.py:72
  181.6 3.8 %collective-permute-start.31 = (bf16[1,1,8,8,128]{4,0,3,2,1:T(2,128)(2,1)S(1)}, bf16[1,1,8,8,128]{4,0,3,2,1:T(2,128)(2,1)S(1)}, u32[]{:S(2)}, u32[]{:S(2)}) collective-permute-start(bf16[1,1,8,8,128]{4,0,3,2,1:T(2,128)(2,1)S(1)} %copy.67), channel_id=1, source_target_pairs={{8,2},{9,3},{10,4},{11,5},{12,6},{13,7},{16,10},{17,11},{18,12},{1... | collective-permute-start | bytes 49160 | tf_op jit(solution)/shard_map/ppermute | solution.py:72
  185.8 2.7 %collective-permute-done.31 = bf16[1,1,8,8,128]{4,0,3,2,1:T(2,128)(2,1)S(1)} collective-permute-done((bf16[1,1,8,8,128]{4,0,3,2,1:T(2,128)(2,1)S(1)}, bf16[1,1,8,8,128]{4,0,3,2,1:T(2,128)(2,1)S(1)}, u32[]{:S(2)}, u32[]{:S(2)}) %collective-permute-start.31) | collective-permute-done | bytes 16416 | tf_op jit(solution)/shard_map/ppermute | solution.py:72
  189.4 2.9 %fusion.3 = f32[1,8,8,8,128]{4,0,3,2,1:T(1,128)S(1)} fusion(bf16[3,3,3,128,128]{4,3,2,1,0:T(8,128)(2,1)S(1)} %bitcast.221, bf16[1,1,1,1,128]{4,0,3,2,1:T(2,128)(2,1)S(1)} %get-tuple-element.1599, bf16[1,1,1,8,128]{4,0,3,2,1:T(2,128)(2,1)S(1)} %constant_dynamic-slice_fusion.13, bf16[1,1,1,1,128]{4,0,3,2,1:T(2,128)(2,1)S(1)} %get-tuple-element.1598, ...), kind=kOutput, calls=%fused_computation.10 | convolution fusion | flops 459896832 | bytes 1402880 | tf_op jit(solution)/shard_map/conv_general_dilated | solution.py:77
  192.7 1.1 select_select_fusion
  193.8 3.7 %multiply_convert_fusion = bf16[3,3,3,128,128]{4,3,2,1,0:T(8,128)(2,1)S(1)} fusion(bf16[1,10,10,10,128]{4,3,2,1,0:T(8,128)(2,1)S(1)} %copy-done.9, bf16[1,8,8,8,128]{4,3,2,1,0:T(8,128)(2,1)S(1)} %bitcast.237), kind=kOutput, calls=%fused_computation.2 | convolution fusion | flops 453869568 | bytes 1271808 | tf_op jit(solution)/shard_map/transpose | solution.py:181
  197.8 1.4 collective-permute-start.38
  199.2 5.1 %collective-permute-done.40 = bf16[864,128]{1,0:T(8,128)(2,1)S(1)} collective-permute-done((bf16[864,128]{1,0:T(8,128)(2,1)S(1)}, bf16[864,128]{1,0:T(8,128)(2,1)S(1)}, u32[]{:S(2)}, u32[]{:S(2)}) %collective-permute-start.40) | collective-permute-done | bytes 221216 | tf_op jit(solution)/shard_map/ppermute | solution.py:117
  204.3 4.8 %collective-permute-done.39 = bf16[864,128]{1,0:T(8,128)(2,1)S(1)} collective-permute-done((bf16[864,128]{1,0:T(8,128)(2,1)S(1)}, bf16[864,128]{1,0:T(8,128)(2,1)S(1)}, u32[]{:S(2)}, u32[]{:S(2)}) %collective-permute-start.39) | collective-permute-done | bytes 221216 | tf_op jit(solution)/shard_map/ppermute | solution.py:117
  209.2 1.3 collective-permute-start.41
  210.5 1.4 collective-permute-done.41
  (229 shorter events, 16.5 us)
Async XLA Ops:
  0.6 14.1 %copy-start.10 = (s32[1,1,1,1,27]{4,3,2,1,0:T(1,128)S(1)}, s32[1,1,1,1,27]{4,3,2,1,0:T(1,128)}, u32[]{:S(2)}) copy-start(s32[1,1,1,1,27]{4,3,2,1,0:T(1,128)} %param.8) | copy-start | bytes 328
  0.6 92.6 %collective-permute-start.10 = (bf16[864,128]{1,0:T(8,128)(2,1)}, bf16[864,128]{1,0:T(8,128)(2,1)S(1)}, u32[]{:S(2)}, u32[]{:S(2)}) collective-permute-start(bf16[864,128]{1,0:T(8,128)(2,1)} %bitcast.231), channel_id=1, source_target_pairs={{0,6},{2,0},{4,2},{6,4},{1,7},{3,1},{5,3},{7,5},{8,14},{10,8},{12,... | collective-permute-start | bytes 663560 | tf_op jit(solution)/shard_map/ppermute | solution.py:103
  1.8 91.4 %collective-permute-start.9 = (bf16[864,128]{1,0:T(8,128)(2,1)}, bf16[864,128]{1,0:T(8,128)(2,1)S(1)}, u32[]{:S(2)}, u32[]{:S(2)}) collective-permute-start(bf16[864,128]{1,0:T(8,128)(2,1)} %bitcast.232), channel_id=1, source_target_pairs={{0,4},{2,6},{4,0},{6,2},{1,5},{3,7},{5,1},{7,3},{8,12},{10,14},{12... | collective-permute-start | bytes 663560 | tf_op jit(solution)/shard_map/ppermute | solution.py:103
  3.1 90.2 %collective-permute-start.8 = (bf16[864,128]{1,0:T(8,128)(2,1)}, bf16[864,128]{1,0:T(8,128)(2,1)S(1)}, u32[]{:S(2)}, u32[]{:S(2)}) collective-permute-start(bf16[864,128]{1,0:T(8,128)(2,1)} %bitcast.233), channel_id=1, source_target_pairs={{0,2},{2,4},{4,6},{6,0},{1,3},{3,5},{5,7},{7,1},{8,10},{10,12},{12... | collective-permute-start | bytes 663560 | tf_op jit(solution)/shard_map/ppermute | solution.py:103
  7.1 60.5 %collective-permute-start.7 = (bf16[1,1,1,8,256]{4,3,2,1,0:T(8,128)(2,1)S(1)}, bf16[1,1,1,8,256]{4,3,2,1,0:T(8,128)(2,1)S(1)}, u32[]{:S(2)}, u32[]{:S(2)}) collective-permute-start(bf16[1,1,1,8,256]{4,3,2,1,0:T(8,128)(2,1)S(1)} %get-tuple-element.1501), channel_id=1, source_target_pairs={{3,0},{5,2},{7,4},{11,8},{13,10},{15,12},{19,16},{21,18},{23,20},{... | collective-permute-start | bytes 12296 | tf_op jit(solution)/shard_map/ppermute | solution.py:72
  12.8 75.6 %collective-permute-start.6 = (bf16[1,1,8,8,256]{4,3,2,1,0:T(8,128)(2,1)S(1)}, bf16[1,1,8,8,256]{4,3,2,1,0:T(8,128)(2,1)S(1)}, u32[]{:S(2)}, u32[]{:S(2)}) collective-permute-start(bf16[1,1,8,8,256]{4,3,2,1,0:T(8,128)(2,1)S(1)} %get-tuple-element.1503), channel_id=1, source_target_pairs={{2,0},{3,1},{4,2},{5,3},{6,4},{7,5},{10,8},{11,9},{12,10},{13,11},... | collective-permute-start | bytes 98312 | tf_op jit(solution)/shard_map/ppermute | solution.py:72
  67.6 4.9 %collective-permute-start.5 = (bf16[1,1,1,8,256]{4,3,2,1,0:T(8,128)(2,1)S(1)}, bf16[1,1,1,8,256]{4,3,2,1,0:T(8,128)(2,1)S(1)}, u32[]{:S(2)}, u32[]{:S(2)}) collective-permute-start(bf16[1,1,1,8,256]{4,3,2,1,0:T(8,128)(2,1)S(1)} %get-tuple-element.1499), channel_id=1, source_target_pairs={{2,1},{4,3},{6,5},{10,9},{12,11},{14,13},{18,17},{20,19},{22,21},{... | collective-permute-start | bytes 12296 | tf_op jit(solution)/shard_map/ppermute | solution.py:72
  72.6 2.7 %collective-permute-start.2 = (bf16[1,1,1,8,256]{4,3,2,1,0:T(8,128)(2,1)S(1)}, bf16[1,1,1,8,256]{4,3,2,1,0:T(8,128)(2,1)S(1)}, u32[]{:S(2)}, u32[]{:S(2)}) collective-permute-start(bf16[1,1,1,8,256]{4,3,2,1,0:T(8,128)(2,1)S(1)} %get-tuple-element.1500), channel_id=1, source_target_pairs={{1,2},{3,4},{5,6},{9,10},{11,12},{13,14},{17,18},{19,20},{21,22},{... | collective-permute-start | bytes 12296 | tf_op jit(solution)/shard_map/ppermute | solution.py:72
  75.3 5.8 %collective-permute-start = (bf16[1,1,1,8,256]{4,3,2,1,0:T(8,128)(2,1)S(1)}, bf16[1,1,1,8,256]{4,3,2,1,0:T(8,128)(2,1)S(1)}, u32[]{:S(2)}, u32[]{:S(2)}) collective-permute-start(bf16[1,1,1,8,256]{4,3,2,1,0:T(8,128)(2,1)S(1)} %get-tuple-element.1498), channel_id=1, source_target_pairs={{0,3},{2,5},{4,7},{8,11},{10,13},{12,15},{16,19},{18,21},{20,23},{... | collective-permute-start | bytes 12296 | tf_op jit(solution)/shard_map/ppermute | solution.py:72
  81.1 2.1 %collective-permute-start.4 = (bf16[1,8,1,8,256]{4,3,2,1,0:T(8,128)(2,1)S(1)}, bf16[1,8,1,8,256]{4,3,2,1,0:T(8,128)(2,1)S(1)}, u32[]{:S(2)}, u32[]{:S(2)}) collective-permute-start(bf16[1,8,1,8,256]{4,3,2,1,0:T(8,128)(2,1)S(1)} %get-tuple-element.1505), channel_id=1, source_target_pairs={{1,0},{3,2},{5,4},{7,6},{9,8},{11,10},{13,12},{15,14},{17,16},{19,... | collective-permute-start | bytes 98312 | tf_op jit(solution)/shard_map/ppermute | solution.py:72
  83.2 3.1 %collective-permute-start.3 = (bf16[1,8,1,8,256]{4,3,2,1,0:T(8,128)(2,1)S(1)}, bf16[1,8,1,8,256]{4,3,2,1,0:T(8,128)(2,1)S(1)}, u32[]{:S(2)}, u32[]{:S(2)}) collective-permute-start(bf16[1,8,1,8,256]{4,3,2,1,0:T(8,128)(2,1)S(1)} %get-tuple-element.1504), channel_id=1, source_target_pairs={{0,1},{2,3},{4,5},{6,7},{8,9},{10,11},{12,13},{14,15},{16,17},{18,... | collective-permute-start | bytes 98312 | tf_op jit(solution)/shard_map/ppermute | solution.py:72
  86.3 5.5 %collective-permute-start.1 = (bf16[1,1,8,8,256]{4,3,2,1,0:T(8,128)(2,1)S(1)}, bf16[1,1,8,8,256]{4,3,2,1,0:T(8,128)(2,1)S(1)}, u32[]{:S(2)}, u32[]{:S(2)}) collective-permute-start(bf16[1,1,8,8,256]{4,3,2,1,0:T(8,128)(2,1)S(1)} %get-tuple-element.1502), channel_id=1, source_target_pairs={{0,2},{1,3},{2,4},{3,5},{4,6},{5,7},{8,10},{9,11},{10,12},{11,13},... | collective-permute-start | bytes 98312 | tf_op jit(solution)/shard_map/ppermute | solution.py:72
  88.5 4.8 %copy-start.11 = (bf16[1,864,128]{2,1,0:T(8,128)(2,1)S(1)}, bf16[1,864,128]{2,1,0:T(8,128)(2,1)}, u32[]{:S(2)}) copy-start(bf16[1,864,128]{2,1,0:T(8,128)(2,1)} %param.11) | copy-start | bytes 663556
  94.1 2.8 %copy-start = (bf16[1,1,1,1,512,128]{5,4,3,2,1,0:T(8,128)(2,1)S(1)}, bf16[1,1,1,1,512,128]{5,4,3,2,1,0:T(8,128)(2,1)}, u32[]{:S(2)}) copy-start(bf16[1,1,1,1,512,128]{5,4,3,2,1,0:T(8,128)(2,1)} %param.6) | copy-start | bytes 393220
  94.1 2.8 %copy-start.12 = (f32[1,128]{1,0:T(1,128)S(1)}, f32[1,128]{1,0:T(1,128)}, u32[]{:S(2)}) copy-start(f32[1,128]{1,0:T(1,128)} %param.10) | copy-start | bytes 1540
  94.1 3.3 %copy-start.1 = (bf16[1,1,1,512,128]{4,3,2,1,0:T(8,128)(2,1)S(1)}, bf16[1,1,1,512,128]{4,3,2,1,0:T(8,128)(2,1)}, u32[]{:S(2)}) copy-start(bf16[1,1,1,512,128]{4,3,2,1,0:T(8,128)(2,1)} %param.7) | copy-start | bytes 393220
  97.7 10.5 %collective-permute-start.19 = (bf16[1,1,1,8,128]{4,3,2,1,0:T(8,128)(2,1)S(1)}, bf16[1,1,1,8,128]{4,3,2,1,0:T(8,128)(2,1)S(1)}, u32[]{:S(2)}, u32[]{:S(2)}) collective-permute-start(bf16[1,1,1,8,128]{4,3,2,1,0:T(8,128)(2,1)S(1)} %get-tuple-element.1527), channel_id=1, source_target_pairs={{11,0},{13,2},{15,4},{19,8},{21,10},{23,12},{27,16},{29,18},{31,20}} | collective-permute-start | bytes 6152 | tf_op jit(solution)/shard_map/ppermute | solution.py:72
  100.9 25.9 %copy-start.7 = (bf16[512,128]{1,0:T(8,128)(2,1)}, bf16[512,128]{1,0:T(8,128)(2,1)S(1)}, u32[]{:S(2)}) copy-start(bf16[512,128]{1,0:T(8,128)(2,1)S(1)} %fusion.8) | copy-start | bytes 393220
  100.9 25.0 %collective-permute-start.11 = (bf16[512,128]{1,0:T(8,128)(2,1)S(1)}, bf16[512,128]{1,0:T(8,128)(2,1)S(1)}, u32[]{:S(2)}, u32[]{:S(2)}) collective-permute-start(bf16[512,128]{1,0:T(8,128)(2,1)S(1)} %fusion.8), channel_id=1, source_target_pairs={{8,0},{16,8},{24,16},{9,1},{17,9},{25,17},{10,2},{18,10},{26,18},{... | collective-permute-start | bytes 393224 | tf_op jit(solution)/shard_map/ppermute | solution.py:178
  103.0 20.6 %collective-permute-start.18 = (bf16[1,1,8,8,128]{4,3,2,1,0:T(8,128)(2,1)S(1)}, bf16[1,1,8,8,128]{4,3,2,1,0:T(8,128)(2,1)S(1)}, u32[]{:S(2)}, u32[]{:S(2)}) collective-permute-start(bf16[1,1,8,8,128]{4,3,2,1,0:T(8,128)(2,1)S(1)} %get-tuple-element.1531), channel_id=1, source_target_pairs={{10,0},{11,1},{12,2},{13,3},{14,4},{15,5},{18,8},{19,9},{20,10},{2... | collective-permute-start | bytes 49160 | tf_op jit(solution)/shard_map/ppermute | solution.py:72
  105.0 5.8 %collective-permute-start.17 = (bf16[1,1,1,8,128]{4,3,2,1,0:T(8,128)(2,1)S(1)}, bf16[1,1,1,8,128]{4,3,2,1,0:T(8,128)(2,1)S(1)}, u32[]{:S(2)}, u32[]{:S(2)}) collective-permute-start(bf16[1,1,1,8,128]{4,3,2,1,0:T(8,128)(2,1)S(1)} %get-tuple-element.1528), channel_id=1, source_target_pairs={{10,1},{12,3},{14,5},{18,9},{20,11},{22,13},{26,17},{28,19},{30,21}} | collective-permute-start | bytes 6152 | tf_op jit(solution)/shard_map/ppermute | solution.py:72
  106.3 17.5 %collective-permute-start.16 = (bf16[1,8,1,8,128]{4,3,2,1,0:T(8,128)(2,1)S(1)}, bf16[1,8,1,8,128]{4,3,2,1,0:T(8,128)(2,1)S(1)}, u32[]{:S(2)}, u32[]{:S(2)}) collective-permute-start(bf16[1,8,1,8,128]{4,3,2,1,0:T(8,128)(2,1)S(1)} %get-tuple-element.1533), channel_id=1, source_target_pairs={{9,0},{11,2},{13,4},{15,6},{17,8},{19,10},{21,12},{23,14},{25,16},... | collective-permute-start | bytes 49160 | tf_op jit(solution)/shard_map/ppermute | solution.py:72
  108.3 15.6 %collective-permute-start.15 = (bf16[1,8,1,8,128]{4,3,2,1,0:T(8,128)(2,1)S(1)}, bf16[1,8,1,8,128]{4,3,2,1,0:T(8,128)(2,1)S(1)}, u32[]{:S(2)}, u32[]{:S(2)}) collective-permute-start(bf16[1,8,1,8,128]{4,3,2,1,0:T(8,128)(2,1)S(1)} %get-tuple-element.1532), channel_id=1, source_target_pairs={{8,1},{10,3},{12,5},{14,7},{16,9},{18,11},{20,13},{22,15},{24,17},... | collective-permute-start | bytes 49160 | tf_op jit(solution)/shard_map/ppermute | solution.py:72
  110.8 2.0 collective-permute-start.14
  112.8 6.7 %collective-permute-start.12 = (bf16[1,1,1,8,128]{4,3,2,1,0:T(8,128)(2,1)S(1)}, bf16[1,1,1,8,128]{4,3,2,1,0:T(8,128)(2,1)S(1)}, u32[]{:S(2)}, u32[]{:S(2)}) collective-permute-start(bf16[1,1,1,8,128]{4,3,2,1,0:T(8,128)(2,1)S(1)} %get-tuple-element.1526), channel_id=1, source_target_pairs={{8,3},{10,5},{12,7},{16,11},{18,13},{20,15},{24,19},{26,21},{28,23}} | collective-permute-start | bytes 6152 | tf_op jit(solution)/shard_map/ppermute | solution.py:72
  119.5 6.3 %collective-permute-start.13 = (bf16[1,1,8,8,128]{4,3,2,1,0:T(8,128)(2,1)S(1)}, bf16[1,1,8,8,128]{4,3,2,1,0:T(8,128)(2,1)S(1)}, u32[]{:S(2)}, u32[]{:S(2)}) collective-permute-start(bf16[1,1,8,8,128]{4,3,2,1,0:T(8,128)(2,1)S(1)} %get-tuple-element.1530), channel_id=1, source_target_pairs={{8,2},{9,3},{10,4},{11,5},{12,6},{13,7},{16,10},{17,11},{18,12},{1... | collective-permute-start | bytes 49160 | tf_op jit(solution)/shard_map/ppermute | solution.py:72
  126.0 4.1 %copy-start.3 = (bf16[512,128]{1,0:T(8,128)(2,1)}, bf16[512,128]{1,0:T(8,128)(2,1)S(1)}, u32[]{:S(2)}) copy-start(bf16[512,128]{1,0:T(8,128)(2,1)S(1)} %collective-permute-done.11) | copy-start | bytes 393220
  130.4 27.8 %copy-start.5 = (bf16[512,128]{1,0:T(8,128)(2,1)}, bf16[512,128]{1,0:T(8,128)(2,1)S(1)}, u32[]{:S(2)}) copy-start(bf16[512,128]{1,0:T(8,128)(2,1)S(1)} %fusion.18) | copy-start | bytes 393220
  130.4 27.0 %collective-permute-start.20 = (bf16[512,128]{1,0:T(8,128)(2,1)S(1)}, bf16[512,128]{1,0:T(8,128)(2,1)S(1)}, u32[]{:S(2)}, u32[]{:S(2)}) collective-permute-start(bf16[512,128]{1,0:T(8,128)(2,1)S(1)} %fusion.18), channel_id=1, source_target_pairs={{8,0},{16,8},{24,16},{9,1},{17,9},{25,17},{10,2},{18,10},{26,18},{... | collective-permute-start | bytes 393224 | tf_op jit(solution)/shard_map/ppermute | solution.py:178
  132.4 6.6 %collective-permute-start.28 = (bf16[1,1,1,8,128]{4,0,3,2,1:T(2,128)(2,1)S(1)}, bf16[1,1,1,8,128]{4,0,3,2,1:T(2,128)(2,1)S(1)}, u32[]{:S(2)}, u32[]{:S(2)}) collective-permute-start(bf16[1,1,1,8,128]{4,0,3,2,1:T(2,128)(2,1)S(1)} %copy.65), channel_id=1, source_target_pairs={{11,0},{13,2},{15,4},{19,8},{21,10},{23,12},{27,16},{29,18},{31,20}} | collective-permute-start | bytes 6152 | tf_op jit(solution)/shard_map/ppermute | solution.py:72
  133.7 20.6 %collective-permute-start.27 = (bf16[1,1,8,8,128]{4,0,3,2,1:T(2,128)(2,1)S(1)}, bf16[1,1,8,8,128]{4,0,3,2,1:T(2,128)(2,1)S(1)}, u32[]{:S(2)}, u32[]{:S(2)}) collective-permute-start(bf16[1,1,8,8,128]{4,0,3,2,1:T(2,128)(2,1)S(1)} %copy.64), channel_id=1, source_target_pairs={{10,0},{11,1},{12,2},{13,3},{14,4},{15,5},{18,8},{19,9},{20,10},{2... | collective-permute-start | bytes 49160 | tf_op jit(solution)/shard_map/ppermute | solution.py:72
  135.7 6.0 %collective-permute-start.26 = (bf16[1,1,1,8,128]{4,0,3,2,1:T(2,128)(2,1)S(1)}, bf16[1,1,1,8,128]{4,0,3,2,1:T(2,128)(2,1)S(1)}, u32[]{:S(2)}, u32[]{:S(2)}) collective-permute-start(bf16[1,1,1,8,128]{4,0,3,2,1:T(2,128)(2,1)S(1)} %copy.63), channel_id=1, source_target_pairs={{10,1},{12,3},{14,5},{18,9},{20,11},{22,13},{26,17},{28,19},{30,21}} | collective-permute-start | bytes 6152 | tf_op jit(solution)/shard_map/ppermute | solution.py:72
  137.0 17.4 %collective-permute-start.25 = (bf16[1,8,1,8,128]{4,0,3,2,1:T(2,128)(2,1)S(1)}, bf16[1,8,1,8,128]{4,0,3,2,1:T(2,128)(2,1)S(1)}, u32[]{:S(2)}, u32[]{:S(2)}) collective-permute-start(bf16[1,8,1,8,128]{4,0,3,2,1:T(2,128)(2,1)S(1)} %copy.62), channel_id=1, source_target_pairs={{9,0},{11,2},{13,4},{15,6},{17,8},{19,10},{21,12},{23,14},{25,16},... | collective-permute-start | bytes 49160 | tf_op jit(solution)/shard_map/ppermute | solution.py:72
  139.0 15.5 %collective-permute-start.24 = (bf16[1,8,1,8,128]{4,0,3,2,1:T(2,128)(2,1)S(1)}, bf16[1,8,1,8,128]{4,0,3,2,1:T(2,128)(2,1)S(1)}, u32[]{:S(2)}, u32[]{:S(2)}) collective-permute-start(bf16[1,8,1,8,128]{4,0,3,2,1:T(2,128)(2,1)S(1)} %copy.61), channel_id=1, source_target_pairs={{8,1},{10,3},{12,5},{14,7},{16,9},{18,11},{20,13},{22,15},{24,17},... | collective-permute-start | bytes 49160 | tf_op jit(solution)/shard_map/ppermute | solution.py:72
  141.6 2.0 collective-permute-start.23
  143.7 6.7 %collective-permute-start.21 = (bf16[1,1,1,8,128]{4,0,3,2,1:T(2,128)(2,1)S(1)}, bf16[1,1,1,8,128]{4,0,3,2,1:T(2,128)(2,1)S(1)}, u32[]{:S(2)}, u32[]{:S(2)}) collective-permute-start(bf16[1,1,1,8,128]{4,0,3,2,1:T(2,128)(2,1)S(1)} %copy.58), channel_id=1, source_target_pairs={{8,3},{10,5},{12,7},{16,11},{18,13},{20,15},{24,19},{26,21},{28,23}} | collective-permute-start | bytes 6152 | tf_op jit(solution)/shard_map/ppermute | solution.py:72
  150.4 6.9 %collective-permute-start.22 = (bf16[1,1,8,8,128]{4,0,3,2,1:T(2,128)(2,1)S(1)}, bf16[1,1,8,8,128]{4,0,3,2,1:T(2,128)(2,1)S(1)}, u32[]{:S(2)}, u32[]{:S(2)}) collective-permute-start(bf16[1,1,8,8,128]{4,0,3,2,1:T(2,128)(2,1)S(1)} %copy.59), channel_id=1, source_target_pairs={{8,2},{9,3},{10,4},{11,5},{12,6},{13,7},{16,10},{17,11},{18,12},{1... | collective-permute-start | bytes 49160 | tf_op jit(solution)/shard_map/ppermute | solution.py:72
  161.8 26.8 %collective-permute-start.29 = (bf16[512,128]{1,0:T(8,128)(2,1)S(1)}, bf16[512,128]{1,0:T(8,128)(2,1)S(1)}, u32[]{:S(2)}, u32[]{:S(2)}) collective-permute-start(bf16[512,128]{1,0:T(8,128)(2,1)S(1)} %fusion.21), channel_id=1, source_target_pairs={{8,0},{16,8},{24,16},{9,1},{17,9},{25,17},{10,2},{18,10},{26,18},{... | collective-permute-start | bytes 393224 | tf_op jit(solution)/shard_map/ppermute | solution.py:178
  163.7 6.0 %collective-permute-start.37 = (bf16[1,1,1,8,128]{4,0,3,2,1:T(2,128)(2,1)S(1)}, bf16[1,1,1,8,128]{4,0,3,2,1:T(2,128)(2,1)S(1)}, u32[]{:S(2)}, u32[]{:S(2)}) collective-permute-start(bf16[1,1,1,8,128]{4,0,3,2,1:T(2,128)(2,1)S(1)} %copy.73), channel_id=1, source_target_pairs={{11,0},{13,2},{15,4},{19,8},{21,10},{23,12},{27,16},{29,18},{31,20}} | collective-permute-start | bytes 6152 | tf_op jit(solution)/shard_map/ppermute | solution.py:72
  165.1 20.3 %collective-permute-start.36 = (bf16[1,1,8,8,128]{4,0,3,2,1:T(2,128)(2,1)S(1)}, bf16[1,1,8,8,128]{4,0,3,2,1:T(2,128)(2,1)S(1)}, u32[]{:S(2)}, u32[]{:S(2)}) collective-permute-start(bf16[1,1,8,8,128]{4,0,3,2,1:T(2,128)(2,1)S(1)} %copy.72), channel_id=1, source_target_pairs={{10,0},{11,1},{12,2},{13,3},{14,4},{15,5},{18,8},{19,9},{20,10},{2... | collective-permute-start | bytes 49160 | tf_op jit(solution)/shard_map/ppermute | solution.py:72
  167.0 5.8 %collective-permute-start.35 = (bf16[1,1,1,8,128]{4,0,3,2,1:T(2,128)(2,1)S(1)}, bf16[1,1,1,8,128]{4,0,3,2,1:T(2,128)(2,1)S(1)}, u32[]{:S(2)}, u32[]{:S(2)}) collective-permute-start(bf16[1,1,1,8,128]{4,0,3,2,1:T(2,128)(2,1)S(1)} %copy.71), channel_id=1, source_target_pairs={{10,1},{12,3},{14,5},{18,9},{20,11},{22,13},{26,17},{28,19},{30,21}} | collective-permute-start | bytes 6152 | tf_op jit(solution)/shard_map/ppermute | solution.py:72
  168.4 17.2 %collective-permute-start.34 = (bf16[1,8,1,8,128]{4,0,3,2,1:T(2,128)(2,1)S(1)}, bf16[1,8,1,8,128]{4,0,3,2,1:T(2,128)(2,1)S(1)}, u32[]{:S(2)}, u32[]{:S(2)}) collective-permute-start(bf16[1,8,1,8,128]{4,0,3,2,1:T(2,128)(2,1)S(1)} %copy.70), channel_id=1, source_target_pairs={{9,0},{11,2},{13,4},{15,6},{17,8},{19,10},{21,12},{23,14},{25,16},... | collective-permute-start | bytes 49160 | tf_op jit(solution)/shard_map/ppermute | solution.py:72
  169.8 15.9 %collective-permute-start.33 = (bf16[1,8,1,8,128]{4,0,3,2,1:T(2,128)(2,1)S(1)}, bf16[1,8,1,8,128]{4,0,3,2,1:T(2,128)(2,1)S(1)}, u32[]{:S(2)}, u32[]{:S(2)}) collective-permute-start(bf16[1,8,1,8,128]{4,0,3,2,1:T(2,128)(2,1)S(1)} %copy.69), channel_id=1, source_target_pairs={{8,1},{10,3},{12,5},{14,7},{16,9},{18,11},{20,13},{22,15},{24,17},... | collective-permute-start | bytes 49160 | tf_op jit(solution)/shard_map/ppermute | solution.py:72
  172.9 2.0 collective-permute-start.32
  174.9 6.7 %collective-permute-start.30 = (bf16[1,1,1,8,128]{4,0,3,2,1:T(2,128)(2,1)S(1)}, bf16[1,1,1,8,128]{4,0,3,2,1:T(2,128)(2,1)S(1)}, u32[]{:S(2)}, u32[]{:S(2)}) collective-permute-start(bf16[1,1,1,8,128]{4,0,3,2,1:T(2,128)(2,1)S(1)} %copy.66), channel_id=1, source_target_pairs={{8,3},{10,5},{12,7},{16,11},{18,13},{20,15},{24,19},{26,21},{28,23}} | collective-permute-start | bytes 6152 | tf_op jit(solution)/shard_map/ppermute | solution.py:72
  181.6 6.9 %collective-permute-start.31 = (bf16[1,1,8,8,128]{4,0,3,2,1:T(2,128)(2,1)S(1)}, bf16[1,1,8,8,128]{4,0,3,2,1:T(2,128)(2,1)S(1)}, u32[]{:S(2)}, u32[]{:S(2)}) collective-permute-start(bf16[1,1,8,8,128]{4,0,3,2,1:T(2,128)(2,1)S(1)} %copy.67), channel_id=1, source_target_pairs={{8,2},{9,3},{10,4},{11,5},{12,6},{13,7},{16,10},{17,11},{18,12},{1... | collective-permute-start | bytes 49160 | tf_op jit(solution)/shard_map/ppermute | solution.py:72
  189.4 3.4 %copy-start.2 = (bf16[1,1,1,512,128]{4,3,2,1,0:T(8,128)(2,1)S(1)}, bf16[1,1,1,512,128]{4,3,2,1,0:T(8,128)(2,1)}, u32[]{:S(2)}) copy-start(bf16[1,1,1,512,128]{4,3,2,1,0:T(8,128)(2,1)} %param.7) | copy-start | bytes 393220
  189.4 3.3 %copy-start.4 = (bf16[512,128]{1,0:T(8,128)(2,1)S(1)}, bf16[512,128]{1,0:T(8,128)(2,1)}, u32[]{:S(2)}) copy-start(bf16[512,128]{1,0:T(8,128)(2,1)} %copy-done.3) | copy-start | bytes 393220
  189.4 3.3 %copy-start.6 = (bf16[512,128]{1,0:T(8,128)(2,1)S(1)}, bf16[512,128]{1,0:T(8,128)(2,1)}, u32[]{:S(2)}) copy-start(bf16[512,128]{1,0:T(8,128)(2,1)} %copy-done.5) | copy-start | bytes 393220
  189.4 3.3 %copy-start.8 = (bf16[512,128]{1,0:T(8,128)(2,1)S(1)}, bf16[512,128]{1,0:T(8,128)(2,1)}, u32[]{:S(2)}) copy-start(bf16[512,128]{1,0:T(8,128)(2,1)} %copy-done.7) | copy-start | bytes 393220
  192.7 1.1 copy-start.9
  197.6 6.7 %collective-permute-start.40 = (bf16[864,128]{1,0:T(8,128)(2,1)S(1)}, bf16[864,128]{1,0:T(8,128)(2,1)S(1)}, u32[]{:S(2)}, u32[]{:S(2)}) collective-permute-start(bf16[864,128]{1,0:T(8,128)(2,1)S(1)} %get-tuple-element.1490), channel_id=1, source_target_pairs={{0,6},{2,0},{4,2},{6,4},{1,7},{3,1},{5,3},{7,5},{8,14},{10,8},{12,... | collective-permute-start | bytes 663560 | tf_op jit(solution)/shard_map/ppermute | solution.py:117
  197.7 11.4 %collective-permute-start.39 = (bf16[864,128]{1,0:T(8,128)(2,1)S(1)}, bf16[864,128]{1,0:T(8,128)(2,1)S(1)}, u32[]{:S(2)}, u32[]{:S(2)}) collective-permute-start(bf16[864,128]{1,0:T(8,128)(2,1)S(1)} %get-tuple-element.1491), channel_id=1, source_target_pairs={{0,4},{2,6},{4,0},{6,2},{1,5},{3,7},{5,1},{7,3},{8,12},{10,14},{12... | collective-permute-start | bytes 663560 | tf_op jit(solution)/shard_map/ppermute | solution.py:117
  197.8 11.3 %collective-permute-start.38 = (bf16[864,128]{1,0:T(8,128)(2,1)S(1)}, bf16[864,128]{1,0:T(8,128)(2,1)S(1)}, u32[]{:S(2)}, u32[]{:S(2)}) collective-permute-start(bf16[864,128]{1,0:T(8,128)(2,1)S(1)} %get-tuple-element.1489), channel_id=1, source_target_pairs={{0,2},{2,4},{4,6},{6,0},{1,3},{3,5},{5,7},{7,1},{8,10},{10,12},{12... | collective-permute-start | bytes 663560 | tf_op jit(solution)/shard_map/ppermute | solution.py:117
  209.2 2.7 %collective-permute-start.41 = (f32[864,128]{1,0:T(8,128)S(1)}, f32[864,128]{1,0:T(8,128)S(1)}, u32[]{:S(2)}, u32[]{:S(2)}) collective-permute-start(f32[864,128]{1,0:T(8,128)S(1)} %convert_add_fusion), channel_id=1, source_target_pairs={{0,1},{1,0},{2,3},{3,2},{4,5},{5,4},{6,7},{7,6},{8,9},{9,8},{10,11... | collective-permute-start | bytes 1327112 | tf_op jit(solution)/shard_map/ppermute | solution.py:188

commit v2 on v1

--- a/solution.py
+++ b/solution.py
@@ -38,11 +38,16 @@
         rows_y = []
         for shift_y in OFFSETS:
             column = (shift_x + 1) * 3 + (shift_y + 1)
-            source = with_blank(centre if (shift_x, shift_y) == (0, 0) else received[(shift_x, shift_y)])
+            piece = centre if (shift_x, shift_y) == (0, 0) else received[(shift_x, shift_y)]
+            source = with_blank(piece)
             parts_z = []
             for shift_z in OFFSETS:
                 direction = column * 3 + shift_z + 1
-                picked = source[table[:, direction]]
+                if piece.shape[0] == 1:
+                    chosen = table[:, direction][:, None, None, None, None] == 0
+                    picked = jnp.where(chosen, piece, jnp.zeros_like(piece))
+                else:
+                    picked = source[table[:, direction]]
                 parts_z.append(picked[:, :, :, source_range(shift_z), :])
             rows_y.append(jnp.concatenate(parts_z, axis=3))
         slabs_x.append(jnp.concatenate(rows_y, axis=2))

time: 215 us -> 171 us (0.80)
  between operations: 53.7 us -> 20 us
  waiting for transfers between devices: 55.4 us -> 24.2 us
  other arithmetic: 9.33 us -> 24 us
  starting transfers between devices: 71.1 us -> 78 us
  local copies, waits for them, and re-layouts: 7.92 us -> 5.74 us
    ppermute x32, waiting for transfers between devices: 44 us -> 10.5 us  [exchange(): received[shift_x, shift_y] = lax.ppermute(piece, axes, route)]
    select_n x1 -> x79, other arithmetic: 1.04 us -> 15 us  [assemble(): picked = jnp.where(chosen, piece, jnp.zeros_like(piece))]
    ppermute x32, starting transfers between devices: 60 us -> 64 us  [exchange(): received[shift_x, shift_y] = lax.ppermute(piece, axes, route)]
    ppermute x3, waiting for transfers between devices: 0.01 us -> 3.3 us  [shards(): centre = lax.ppermute(result, 'pipe', down)]
    gather x37 -> x0, local copies, waits for them, and re-layouts: 2.41 us -> none  [assemble(): picked = source[table[:, direction]]]
    ppermute x3, starting transfers between devices: 1.51 us -> 3.74 us  [scattered_sum(): lax.ppermute(piece, axis, [(i, (i + step) % count) for i in range(count)])]
  transfers between devices with their start and end apart: 42 -> 42, of which waited for: 21 -> 14; matrix products, arithmetic and copies ran while one was open for 5% -> 13% of each run, Pallas kernels for 0% -> 0%
where the time goes in v2:
time: 171 us; the launch traced here: 168 us
  starting transfers between devices  78 us (46%)
  waiting for transfers between devices  24.2 us (14%)
  other arithmetic  24 us (14%)
  between operations  20 us (12%)
  matrix products  15.7 us (9%)
  local copies, waits for them, and re-layouts  5.74 us (3%)
    ppermute x32, starting transfers between devices, exchange(): received[shift_x, shift_y] = lax.ppermute(piece, axes, route)  64 us
    select_n x79, other arithmetic, assemble(): picked = jnp.where(chosen, piece, jnp.zeros_like(piece))  15 us
    conv_general_dilated x4, matrix products, conv_data(): lax.conv_general_dilated(padded, filters, (1, 1, 1), 'VALID', dimension_n...  11.8 us
    ppermute x32, waiting for transfers between devices, exchange(): received[shift_x, shift_y] = lax.ppermute(piece, axes, route)  10.5 us
    ppermute x3, waiting for transfers between devices, scattered_sum(): lax.ppermute(piece, axis, [(i, (i + step) % count) for i in range(count)])  9.01 us
    ppermute x3, starting transfers between devices, shards(): centre = lax.ppermute(result, 'pipe', down)  6.82 us
    transpose x1, matrix products, shards(): per_tap.transpose(1, 2, 3, 0, 4).reshape(taps * channels, channels)  3.9 us
    ppermute x3, starting transfers between devices, scattered_sum(): lax.ppermute(piece, axis, [(i, (i + step) % count) for i in range(count)])  3.74 us
  transfers between devices with their start and end apart: 42, of which 14 were waited for; matrix products, arithmetic and copies ran while one was open for 13% of the time, Pallas kernels for 0%

profile of v2, /device:TPU:21, one launch (start us, length us, event | category | flops | bytes accessed | tf_op | source)
XLA Modules:
  0.0 167.7 jit_solution(3607036244494630070)
XLA Ops:
  0.6 1.2 collective-permute-start.10
  1.8 1.2 collective-permute-start.9
  3.1 1.0 fusion.73
  4.1 0.9 convert_element_type.150
  5.8 2.1 %fusion.127 = (s32[1,1]{1,0:T(1,128)}, s32[1,1]{1,0:T(1,128)}, s32[1,1]{1,0:T(1,128)}, s32[1,1]{1,0:T(1,128)}, s32[1,1]{1,0:T(1,128)}, /*index=5*/s32[1,1]{1,0:T...) fusion(s32[1,27]{1,0:T(1,128)} %bitcast.219), kind=kLoop, calls=%fused_computation.334 | loop fusion | bytes 152 | tf_op jit(solution)/shard_map/slice | solution.py:47
  8.6 1.6 broadcast_select_fusion.1
  10.2 1.6 broadcast_select_fusion
  11.9 1.3 collective-permute-start
  13.2 4.1 %collective-permute-start.2 = (bf16[1,1,1,8,256]{4,0,3,2,1:T(2,128)(2,1)S(1)}, bf16[1,1,1,8,256]{4,0,3,2,1:T(2,128)(2,1)S(1)}, u32[]{:S(2)}, u32[]{:S(2)}) collective-permute-start(bf16[1,1,1,8,256]{4,0,3,2,1:T(2,128)(2,1)S(1)} %get-tuple-element.9), channel_id=1, source_target_pairs={{1,2},{3,4},{5,6},{9,10},{11,12},{13,14},{17,18},{19,20},{21,22},{... | collective-permute-start | bytes 12296 | tf_op jit(solution)/shard_map/ppermute | solution.py:77
  35.9 1.3 collective-permute-start.5
  38.5 5.8 %collective-permute-start.7 = (bf16[1,1,1,8,256]{4,0,3,2,1:T(2,128)(2,1)S(1)}, bf16[1,1,1,8,256]{4,0,3,2,1:T(2,128)(2,1)S(1)}, u32[]{:S(2)}, u32[]{:S(2)}) collective-permute-start(bf16[1,1,1,8,256]{4,0,3,2,1:T(2,128)(2,1)S(1)} %get-tuple-element.11), channel_id=1, source_target_pairs={{3,0},{5,2},{7,4},{11,8},{13,10},{15,12},{19,16},{21,18},{23,20},{... | collective-permute-start | bytes 12296 | tf_op jit(solution)/shard_map/ppermute | solution.py:77
  45.5 2.8 %collective-permute-start.1 = (bf16[1,1,8,8,256]{4,0,3,2,1:T(2,128)(2,1)S(1)}, bf16[1,1,8,8,256]{4,0,3,2,1:T(2,128)(2,1)S(1)}, u32[]{:S(2)}, u32[]{:S(2)}) collective-permute-start(bf16[1,1,8,8,256]{4,0,3,2,1:T(2,128)(2,1)S(1)} %get-tuple-element.12), channel_id=1, source_target_pairs={{0,2},{1,3},{2,4},{3,5},{4,6},{5,7},{8,10},{9,11},{10,12},{11,13},... | collective-permute-start | bytes 98312 | tf_op jit(solution)/shard_map/ppermute | solution.py:77
  49.5 3.4 %collective-permute-start.6 = (bf16[1,1,8,8,256]{4,0,3,2,1:T(2,128)(2,1)S(1)}, bf16[1,1,8,8,256]{4,0,3,2,1:T(2,128)(2,1)S(1)}, u32[]{:S(2)}, u32[]{:S(2)}) collective-permute-start(bf16[1,1,8,8,256]{4,0,3,2,1:T(2,128)(2,1)S(1)} %get-tuple-element.13), channel_id=1, source_target_pairs={{2,0},{3,1},{4,2},{5,3},{6,4},{7,5},{10,8},{11,9},{12,10},{13,11},... | collective-permute-start | bytes 98312 | tf_op jit(solution)/shard_map/ppermute | solution.py:77
  54.0 1.3 collective-permute-start.3
  55.3 0.7 broadcast_select_fusion.32
  56.6 3.0 %collective-permute-start.4 = (bf16[1,8,1,8,256]{4,0,3,2,1:T(2,128)(2,1)S(1)}, bf16[1,8,1,8,256]{4,0,3,2,1:T(2,128)(2,1)S(1)}, u32[]{:S(2)}, u32[]{:S(2)}) collective-permute-start(bf16[1,8,1,8,256]{4,0,3,2,1:T(2,128)(2,1)S(1)} %get-tuple-element.15), channel_id=1, source_target_pairs={{1,0},{3,2},{5,4},{7,6},{9,8},{11,10},{13,12},{15,14},{17,16},{19,... | collective-permute-start | bytes 98312 | tf_op jit(solution)/shard_map/ppermute | solution.py:77
  63.8 0.7 gather_fusion
  64.6 3.0 %fusion.56 = f32[1,8,8,8,128]{4,0,3,2,1:T(1,128)S(1)} fusion(bf16[3,3,3,128,128]{4,3,2,1,0:T(8,128)(2,1)S(1)} %bitcast.206, bf16[1,1,1,1,128]{4,0,3,2,1:T(2,128)(2,1)S(1)} %get-tuple-element.168, bf16[1,1,1,8,128]{4,0,3,2,1:T(2,128)(2,1)S(1)} %get-tuple-element.128, bf16[1,1,1,1,128]{4,0,3,2,1:T(2,128)(2,1)S(1)} %get-tuple-element.167, ...), kind=kOutput, calls=%fused_computation.68 | convolution fusion | flops 459896832 | bytes 1402880 | tf_op jit(solution)/shard_map/conv_general_dilated | solution.py:82
  68.0 2.3 %fusion.72 = bf16[1,8,8,8,128]{4,0,3,2,1:T(2,128)(2,1)S(1)} fusion(pred[8,8,8]{2,1,0:T(8,128)(4,1)S(1)} %fusion.102, f32[1,8,8,8,128]{4,0,3,2,1:T(1,128)S(1)} %bitcast.193, f32[1,8,8,8,128]{4,0,3,2,1:T(1,128)S(1)} %get-tuple-element.4, f32[1,8,8,8,128]{4,0,3,2,1:T(1,128)S(1)} %fusion.56, f32[8,8,8]{2,1,0:T(8,128)S(1)} %multiply_multiply_fusion.1, ...), kind=kLoop, calls=%fused_computation.93 | loop fusion | flops 1179648 | bytes 1053696 | tf_op jit(solution)/shard_map/convert_element_type | solution.py:133
  70.4 1.3 collective-permute-start.12
  71.7 4.9 %collective-permute-start.19 = (bf16[1,1,1,8,128]{4,0,3,2,1:T(2,128)(2,1)S(1)}, bf16[1,1,1,8,128]{4,0,3,2,1:T(2,128)(2,1)S(1)}, u32[]{:S(2)}, u32[]{:S(2)}) collective-permute-start(bf16[1,1,1,8,128]{4,0,3,2,1:T(2,128)(2,1)S(1)} %get-tuple-element.19), channel_id=1, source_target_pairs={{11,0},{13,2},{15,4},{19,8},{21,10},{23,12},{27,16},{29,18},{31,20}} | collective-permute-start | bytes 6152 | tf_op jit(solution)/shard_map/ppermute | solution.py:77
  76.7 1.3 collective-permute-start.17
  78.0 1.3 collective-permute-start.14
  79.7 1.3 collective-permute-start.15
  81.0 1.3 collective-permute-start.16
  82.3 1.9 %collective-permute-start.13 = (bf16[1,1,8,8,128]{4,0,3,2,1:T(2,128)(2,1)S(1)}, bf16[1,1,8,8,128]{4,0,3,2,1:T(2,128)(2,1)S(1)}, u32[]{:S(2)}, u32[]{:S(2)}) collective-permute-start(bf16[1,1,8,8,128]{4,0,3,2,1:T(2,128)(2,1)S(1)} %get-tuple-element.22), channel_id=1, source_target_pairs={{8,2},{9,3},{10,4},{11,5},{12,6},{13,7},{16,10},{17,11},{18,12},{1... | collective-permute-start | bytes 49160 | tf_op jit(solution)/shard_map/ppermute | solution.py:77
  84.3 1.9 %collective-permute-start.18 = (bf16[1,1,8,8,128]{4,0,3,2,1:T(2,128)(2,1)S(1)}, bf16[1,1,8,8,128]{4,0,3,2,1:T(2,128)(2,1)S(1)}, u32[]{:S(2)}, u32[]{:S(2)}) collective-permute-start(bf16[1,1,8,8,128]{4,0,3,2,1:T(2,128)(2,1)S(1)} %get-tuple-element.23), channel_id=1, source_target_pairs={{10,0},{11,1},{12,2},{13,3},{14,4},{15,5},{18,8},{19,9},{20,10},{2... | collective-permute-start | bytes 49160 | tf_op jit(solution)/shard_map/ppermute | solution.py:77
  86.3 2.1 %collective-permute-start.11 = (bf16[512,128]{1,0:T(8,128)(2,1)S(1)}, bf16[512,128]{1,0:T(8,128)(2,1)S(1)}, u32[]{:S(2)}, u32[]{:S(2)}) collective-permute-start(bf16[512,128]{1,0:T(8,128)(2,1)S(1)} %fusion.59), channel_id=1, source_target_pairs={{8,0},{16,8},{24,16},{9,1},{17,9},{25,17},{10,2},{18,10},{26,18},{... | collective-permute-start | bytes 393224 | tf_op jit(solution)/shard_map/ppermute | solution.py:183
  88.8 1.2 collective-permute-done.18
  90.1 3.3 %collective-permute-done.11 = bf16[512,128]{1,0:T(8,128)(2,1)S(1)} collective-permute-done((bf16[512,128]{1,0:T(8,128)(2,1)S(1)}, bf16[512,128]{1,0:T(8,128)(2,1)S(1)}, u32[]{:S(2)}, u32[]{:S(2)}) %collective-permute-start.11) | collective-permute-done | bytes 131104 | tf_op jit(solution)/shard_map/ppermute | solution.py:183
  93.8 2.9 %fusion.55 = f32[1,8,8,8,128]{4,0,3,2,1:T(1,128)S(1)} fusion(bf16[3,3,3,128,128]{4,3,2,1,0:T(8,128)(2,1)S(1)} %bitcast.207, bf16[1,1,1,1,128]{4,0,3,2,1:T(2,128)(2,1)S(1)} %get-tuple-element.160, bf16[1,1,1,8,128]{4,0,3,2,1:T(2,128)(2,1)S(1)} %broadcast_select_fusion.80, bf16[1,1,1,1,128]{4,0,3,2,1:T(2,128)(2,1)S(1)} %get-tuple-element.159, ...), kind=kOutput, calls=%fused_computation.67 | convolution fusion | flops 459896832 | bytes 1402880 | tf_op jit(solution)/shard_map/conv_general_dilated | solution.py:82
  97.4 2.3 %collective-permute-start.28 = (bf16[1,1,1,8,128]{4,0,3,2,1:T(2,128)(2,1)S(1)}, bf16[1,1,1,8,128]{4,0,3,2,1:T(2,128)(2,1)S(1)}, u32[]{:S(2)}, u32[]{:S(2)}) collective-permute-start(bf16[1,1,1,8,128]{4,0,3,2,1:T(2,128)(2,1)S(1)} %copy.47), channel_id=1, source_target_pairs={{11,0},{13,2},{15,4},{19,8},{21,10},{23,12},{27,16},{29,18},{31,20}} | collective-permute-start | bytes 6152 | tf_op jit(solution)/shard_map/ppermute | solution.py:77
  99.8 1.9 %collective-permute-start.20 = (bf16[512,128]{1,0:T(8,128)(2,1)S(1)}, bf16[512,128]{1,0:T(8,128)(2,1)S(1)}, u32[]{:S(2)}, u32[]{:S(2)}) collective-permute-start(bf16[512,128]{1,0:T(8,128)(2,1)S(1)} %fusion.65), channel_id=1, source_target_pairs={{8,0},{16,8},{24,16},{9,1},{17,9},{25,17},{10,2},{18,10},{26,18},{... | collective-permute-start | bytes 393224 | tf_op jit(solution)/shard_map/ppermute | solution.py:183
  101.7 1.3 collective-permute-start.23
  103.0 1.3 collective-permute-start.26
  104.3 1.3 collective-permute-start.21
  105.8 1.3 collective-permute-start.25
  107.1 1.3 collective-permute-start.24
  108.9 1.9 %collective-permute-start.27 = (bf16[1,1,8,8,128]{4,0,3,2,1:T(2,128)(2,1)S(1)}, bf16[1,1,8,8,128]{4,0,3,2,1:T(2,128)(2,1)S(1)}, u32[]{:S(2)}, u32[]{:S(2)}) collective-permute-start(bf16[1,1,8,8,128]{4,0,3,2,1:T(2,128)(2,1)S(1)} %copy.46), channel_id=1, source_target_pairs={{10,0},{11,1},{12,2},{13,3},{14,4},{15,5},{18,8},{19,9},{20,10},{2... | collective-permute-start | bytes 49160 | tf_op jit(solution)/shard_map/ppermute | solution.py:77
  111.1 1.9 %collective-permute-start.22 = (bf16[1,1,8,8,128]{4,0,3,2,1:T(2,128)(2,1)S(1)}, bf16[1,1,8,8,128]{4,0,3,2,1:T(2,128)(2,1)S(1)}, u32[]{:S(2)}, u32[]{:S(2)}) collective-permute-start(bf16[1,1,8,8,128]{4,0,3,2,1:T(2,128)(2,1)S(1)} %copy.39), channel_id=1, source_target_pairs={{8,2},{9,3},{10,4},{11,5},{12,6},{13,7},{16,10},{17,11},{18,12},{1... | collective-permute-start | bytes 49160 | tf_op jit(solution)/shard_map/ppermute | solution.py:77
  113.6 0.8 collective-permute-done.27
  114.5 3.0 %collective-permute-done.22 = bf16[1,1,8,8,128]{4,0,3,2,1:T(2,128)(2,1)S(1)} collective-permute-done((bf16[1,1,8,8,128]{4,0,3,2,1:T(2,128)(2,1)S(1)}, bf16[1,1,8,8,128]{4,0,3,2,1:T(2,128)(2,1)S(1)}, u32[]{:S(2)}, u32[]{:S(2)}) %collective-permute-start.22) | collective-permute-done | bytes 16416 | tf_op jit(solution)/shard_map/ppermute | solution.py:77
  117.9 2.9 %fusion.54 = f32[1,8,8,8,128]{4,0,3,2,1:T(1,128)S(1)} fusion(bf16[3,3,3,128,128]{4,3,2,1,0:T(8,128)(2,1)S(1)} %bitcast.208, bf16[1,1,1,1,128]{4,0,3,2,1:T(2,128)(2,1)S(1)} %get-tuple-element.152, bf16[1,1,1,8,128]{4,0,3,2,1:T(2,128)(2,1)S(1)} %broadcast_select_fusion.79, bf16[1,1,1,1,128]{4,0,3,2,1:T(2,128)(2,1)S(1)} %get-tuple-element.151, ...), kind=kOutput, calls=%fused_computation.66 | convolution fusion | flops 459896832 | bytes 1402880 | tf_op jit(solution)/shard_map/conv_general_dilated | solution.py:82
  121.6 1.7 %collective-permute-start.37 = (bf16[1,1,1,8,128]{4,0,3,2,1:T(2,128)(2,1)S(1)}, bf16[1,1,1,8,128]{4,0,3,2,1:T(2,128)(2,1)S(1)}, u32[]{:S(2)}, u32[]{:S(2)}) collective-permute-start(bf16[1,1,1,8,128]{4,0,3,2,1:T(2,128)(2,1)S(1)} %copy.57), channel_id=1, source_target_pairs={{11,0},{13,2},{15,4},{19,8},{21,10},{23,12},{27,16},{29,18},{31,20}} | collective-permute-start | bytes 6152 | tf_op jit(solution)/shard_map/ppermute | solution.py:77
  123.3 2.8 %collective-permute-start.29 = (bf16[512,128]{1,0:T(8,128)(2,1)S(1)}, bf16[512,128]{1,0:T(8,128)(2,1)S(1)}, u32[]{:S(2)}, u32[]{:S(2)}) collective-permute-start(bf16[512,128]{1,0:T(8,128)(2,1)S(1)} %fusion.68), channel_id=1, source_target_pairs={{8,0},{16,8},{24,16},{9,1},{17,9},{25,17},{10,2},{18,10},{26,18},{... | collective-permute-start | bytes 393224 | tf_op jit(solution)/shard_map/ppermute | solution.py:183
  126.2 1.3 collective-permute-start.32
  127.4 1.3 collective-permute-start.35
  128.7 1.3 collective-permute-start.30
  130.2 2.2 %collective-permute-start.34 = (bf16[1,8,1,8,128]{4,0,3,2,1:T(2,128)(2,1)S(1)}, bf16[1,8,1,8,128]{4,0,3,2,1:T(2,128)(2,1)S(1)}, u32[]{:S(2)}, u32[]{:S(2)}) collective-permute-start(bf16[1,8,1,8,128]{4,0,3,2,1:T(2,128)(2,1)S(1)} %copy.54), channel_id=1, source_target_pairs={{9,0},{11,2},{13,4},{15,6},{17,8},{19,10},{21,12},{23,14},{25,16},... | collective-permute-start | bytes 49160 | tf_op jit(solution)/shard_map/ppermute | solution.py:77
  132.4 1.3 collective-permute-start.33
  133.8 1.9 %collective-permute-start.36 = (bf16[1,1,8,8,128]{4,0,3,2,1:T(2,128)(2,1)S(1)}, bf16[1,1,8,8,128]{4,0,3,2,1:T(2,128)(2,1)S(1)}, u32[]{:S(2)}, u32[]{:S(2)}) collective-permute-start(bf16[1,1,8,8,128]{4,0,3,2,1:T(2,128)(2,1)S(1)} %copy.56), channel_id=1, source_target_pairs={{10,0},{11,1},{12,2},{13,3},{14,4},{15,5},{18,8},{19,9},{20,10},{2... | collective-permute-start | bytes 49160 | tf_op jit(solution)/shard_map/ppermute | solution.py:77
  135.8 2.1 %collective-permute-start.31 = (bf16[1,1,8,8,128]{4,0,3,2,1:T(2,128)(2,1)S(1)}, bf16[1,1,8,8,128]{4,0,3,2,1:T(2,128)(2,1)S(1)}, u32[]{:S(2)}, u32[]{:S(2)}) collective-permute-start(bf16[1,1,8,8,128]{4,0,3,2,1:T(2,128)(2,1)S(1)} %copy.49), channel_id=1, source_target_pairs={{8,2},{9,3},{10,4},{11,5},{12,6},{13,7},{16,10},{17,11},{18,12},{1... | collective-permute-start | bytes 49160 | tf_op jit(solution)/shard_map/ppermute | solution.py:77
  138.1 0.8 collective-permute-done.33
  139.4 2.8 %collective-permute-done.31 = bf16[1,1,8,8,128]{4,0,3,2,1:T(2,128)(2,1)S(1)} collective-permute-done((bf16[1,1,8,8,128]{4,0,3,2,1:T(2,128)(2,1)S(1)}, bf16[1,1,8,8,128]{4,0,3,2,1:T(2,128)(2,1)S(1)}, u32[]{:S(2)}, u32[]{:S(2)}) %collective-permute-start.31) | collective-permute-done | bytes 16416 | tf_op jit(solution)/shard_map/ppermute | solution.py:77
  142.7 2.9 %fusion.53 = f32[1,8,8,8,128]{4,0,3,2,1:T(1,128)S(1)} fusion(bf16[3,3,3,128,128]{4,3,2,1,0:T(8,128)(2,1)S(1)} %bitcast.209, bf16[1,1,1,1,128]{4,0,3,2,1:T(2,128)(2,1)S(1)} %get-tuple-element.144, bf16[1,1,1,8,128]{4,0,3,2,1:T(2,128)(2,1)S(1)} %broadcast_select_fusion.78, bf16[1,1,1,1,128]{4,0,3,2,1:T(2,128)(2,1)S(1)} %get-tuple-element.143, ...), kind=kOutput, calls=%fused_computation.65 | convolution fusion | flops 459896832 | bytes 1402880 | tf_op jit(solution)/shard_map/conv_general_dilated | solution.py:82
  146.3 1.1 select_select_fusion
  147.6 3.9 %multiply_convert_fusion = bf16[3,3,3,128,128]{4,3,2,1,0:T(8,128)(2,1)S(1)} fusion(bf16[1,1,1,1,128]{4,0,3,2,1:T(2,128)(2,1)S(1)} %copy-done.38, bf16[1,1,1,8,128]{4,0,3,2,1:T(2,128)(2,1)S(1)} %copy-done.22, bf16[1,1,1,1,128]{4,0,3,2,1:T(2,128)(2,1)S(1)} %copy-done.37, bf16[1,1,8,1,128]{4,0,3,2,1:T(2,128)(2,1)S(1)} %copy-done.26, ...), kind=kOutput, calls=%fused_computation.2 | convolution fusion | flops 460781568 | bytes 1271808 | tf_op jit(solution)/shard_map/transpose | solution.py:186
  151.6 2.5 %collective-permute-start.38 = (bf16[864,128]{1,0:T(8,128)(2,1)S(1)}, bf16[864,128]{1,0:T(8,128)(2,1)S(1)}, u32[]{:S(2)}, u32[]{:S(2)}) collective-permute-start(bf16[864,128]{1,0:T(8,128)(2,1)S(1)} %get-tuple-element.5), channel_id=1, source_target_pairs={{0,2},{2,4},{4,6},{6,0},{1,3},{3,5},{5,7},{7,1},{8,10},{10,12},{12... | collective-permute-start | bytes 663560 | tf_op jit(solution)/shard_map/ppermute | solution.py:122
  154.2 1.2 collective-permute-start.39
  155.3 3.2 %collective-permute-done.38 = bf16[864,128]{1,0:T(8,128)(2,1)S(1)} collective-permute-done((bf16[864,128]{1,0:T(8,128)(2,1)S(1)}, bf16[864,128]{1,0:T(8,128)(2,1)S(1)}, u32[]{:S(2)}, u32[]{:S(2)}) %collective-permute-start.38) | collective-permute-done | bytes 221216 | tf_op jit(solution)/shard_map/ppermute | solution.py:122
  158.5 5.8 %collective-permute-done.40 = bf16[864,128]{1,0:T(8,128)(2,1)S(1)} collective-permute-done((bf16[864,128]{1,0:T(8,128)(2,1)S(1)}, bf16[864,128]{1,0:T(8,128)(2,1)S(1)}, u32[]{:S(2)}, u32[]{:S(2)}) %collective-permute-start.40) | collective-permute-done | bytes 221216 | tf_op jit(solution)/shard_map/ppermute | solution.py:122
  164.5 1.0 collective-permute-start.41
  165.4 1.4 collective-permute-done.41
  166.8 0.8 add_bitcast_fusion
  (252 shorter events, 18.8 us)
Async XLA Ops:
  0.6 9.6 %copy-start.12 = (f32[1,128]{1,0:T(1,128)S(1)}, f32[1,128]{1,0:T(1,128)}, u32[]{:S(2)}) copy-start(f32[1,128]{1,0:T(1,128)} %param.10) | copy-start | bytes 1540
  0.6 63.0 %collective-permute-start.10 = (bf16[864,128]{1,0:T(8,128)(2,1)}, bf16[864,128]{1,0:T(8,128)(2,1)S(1)}, u32[]{:S(2)}, u32[]{:S(2)}) collective-permute-start(bf16[864,128]{1,0:T(8,128)(2,1)} %bitcast.221), channel_id=1, source_target_pairs={{0,6},{2,0},{4,2},{6,4},{1,7},{3,1},{5,3},{7,5},{8,14},{10,8},{12,... | collective-permute-start | bytes 663560 | tf_op jit(solution)/shard_map/ppermute | solution.py:108
  1.8 61.8 %collective-permute-start.9 = (bf16[864,128]{1,0:T(8,128)(2,1)}, bf16[864,128]{1,0:T(8,128)(2,1)S(1)}, u32[]{:S(2)}, u32[]{:S(2)}) collective-permute-start(bf16[864,128]{1,0:T(8,128)(2,1)} %bitcast.222), channel_id=1, source_target_pairs={{0,4},{2,6},{4,0},{6,2},{1,5},{3,7},{5,1},{7,3},{8,12},{10,14},{12... | collective-permute-start | bytes 663560 | tf_op jit(solution)/shard_map/ppermute | solution.py:108
  3.1 60.6 %collective-permute-start.8 = (bf16[864,128]{1,0:T(8,128)(2,1)}, bf16[864,128]{1,0:T(8,128)(2,1)S(1)}, u32[]{:S(2)}, u32[]{:S(2)}) collective-permute-start(bf16[864,128]{1,0:T(8,128)(2,1)} %bitcast.223), channel_id=1, source_target_pairs={{0,2},{2,4},{4,6},{6,0},{1,3},{3,5},{5,7},{7,1},{8,10},{10,12},{12... | collective-permute-start | bytes 663560 | tf_op jit(solution)/shard_map/ppermute | solution.py:108
  10.2 7.1 %copy-start.9 = (s32[1,1,1,1,27]{4,3,2,1,0:T(1,128)S(1)}, s32[1,1,1,1,27]{4,3,2,1,0:T(1,128)}, u32[]{:S(2)}) copy-start(s32[1,1,1,1,27]{4,3,2,1,0:T(1,128)} %param.8) | copy-start | bytes 328
  11.9 24.0 %collective-permute-start = (bf16[1,1,1,8,256]{4,0,3,2,1:T(2,128)(2,1)S(1)}, bf16[1,1,1,8,256]{4,0,3,2,1:T(2,128)(2,1)S(1)}, u32[]{:S(2)}, u32[]{:S(2)}) collective-permute-start(bf16[1,1,1,8,256]{4,0,3,2,1:T(2,128)(2,1)S(1)} %get-tuple-element.8), channel_id=1, source_target_pairs={{0,3},{2,5},{4,7},{8,11},{10,13},{12,15},{16,19},{18,21},{20,23},{... | collective-permute-start | bytes 12296 | tf_op jit(solution)/shard_map/ppermute | solution.py:77
  13.2 25.3 %collective-permute-start.2 = (bf16[1,1,1,8,256]{4,0,3,2,1:T(2,128)(2,1)S(1)}, bf16[1,1,1,8,256]{4,0,3,2,1:T(2,128)(2,1)S(1)}, u32[]{:S(2)}, u32[]{:S(2)}) collective-permute-start(bf16[1,1,1,8,256]{4,0,3,2,1:T(2,128)(2,1)S(1)} %get-tuple-element.9), channel_id=1, source_target_pairs={{1,2},{3,4},{5,6},{9,10},{11,12},{13,14},{17,18},{19,20},{21,22},{... | collective-permute-start | bytes 12296 | tf_op jit(solution)/shard_map/ppermute | solution.py:77
  20.1 43.6 %copy-start.11 = (bf16[1,864,128]{2,1,0:T(8,128)(2,1)S(1)}, bf16[1,864,128]{2,1,0:T(8,128)(2,1)}, u32[]{:S(2)}) copy-start(bf16[1,864,128]{2,1,0:T(8,128)(2,1)} %param.11) | copy-start | bytes 663556
  35.9 9.6 %collective-permute-start.5 = (bf16[1,1,1,8,256]{4,0,3,2,1:T(2,128)(2,1)S(1)}, bf16[1,1,1,8,256]{4,0,3,2,1:T(2,128)(2,1)S(1)}, u32[]{:S(2)}, u32[]{:S(2)}) collective-permute-start(bf16[1,1,1,8,256]{4,0,3,2,1:T(2,128)(2,1)S(1)} %get-tuple-element.10), channel_id=1, source_target_pairs={{2,1},{4,3},{6,5},{10,9},{12,11},{14,13},{18,17},{20,19},{22,21},{... | collective-permute-start | bytes 12296 | tf_op jit(solution)/shard_map/ppermute | solution.py:77
  38.5 11.0 %collective-permute-start.7 = (bf16[1,1,1,8,256]{4,0,3,2,1:T(2,128)(2,1)S(1)}, bf16[1,1,1,8,256]{4,0,3,2,1:T(2,128)(2,1)S(1)}, u32[]{:S(2)}, u32[]{:S(2)}) collective-permute-start(bf16[1,1,1,8,256]{4,0,3,2,1:T(2,128)(2,1)S(1)} %get-tuple-element.11), channel_id=1, source_target_pairs={{3,0},{5,2},{7,4},{11,8},{13,10},{15,12},{19,16},{21,18},{23,20},{... | collective-permute-start | bytes 12296 | tf_op jit(solution)/shard_map/ppermute | solution.py:77
  45.5 8.5 %collective-permute-start.1 = (bf16[1,1,8,8,256]{4,0,3,2,1:T(2,128)(2,1)S(1)}, bf16[1,1,8,8,256]{4,0,3,2,1:T(2,128)(2,1)S(1)}, u32[]{:S(2)}, u32[]{:S(2)}) collective-permute-start(bf16[1,1,8,8,256]{4,0,3,2,1:T(2,128)(2,1)S(1)} %get-tuple-element.12), channel_id=1, source_target_pairs={{0,2},{1,3},{2,4},{3,5},{4,6},{5,7},{8,10},{9,11},{10,12},{11,13},... | collective-permute-start | bytes 98312 | tf_op jit(solution)/shard_map/ppermute | solution.py:77
  49.5 7.2 %collective-permute-start.6 = (bf16[1,1,8,8,256]{4,0,3,2,1:T(2,128)(2,1)S(1)}, bf16[1,1,8,8,256]{4,0,3,2,1:T(2,128)(2,1)S(1)}, u32[]{:S(2)}, u32[]{:S(2)}) collective-permute-start(bf16[1,1,8,8,256]{4,0,3,2,1:T(2,128)(2,1)S(1)} %get-tuple-element.13), channel_id=1, source_target_pairs={{2,0},{3,1},{4,2},{5,3},{6,4},{7,5},{10,8},{11,9},{12,10},{13,11},... | collective-permute-start | bytes 98312 | tf_op jit(solution)/shard_map/ppermute | solution.py:77
  54.0 7.0 %collective-permute-start.3 = (bf16[1,8,1,8,256]{4,0,3,2,1:T(2,128)(2,1)S(1)}, bf16[1,8,1,8,256]{4,0,3,2,1:T(2,128)(2,1)S(1)}, u32[]{:S(2)}, u32[]{:S(2)}) collective-permute-start(bf16[1,8,1,8,256]{4,0,3,2,1:T(2,128)(2,1)S(1)} %get-tuple-element.14), channel_id=1, source_target_pairs={{0,1},{2,3},{4,5},{6,7},{8,9},{10,11},{12,13},{14,15},{16,17},{18,... | collective-permute-start | bytes 98312 | tf_op jit(solution)/shard_map/ppermute | solution.py:77
  56.6 5.7 %collective-permute-start.4 = (bf16[1,8,1,8,256]{4,0,3,2,1:T(2,128)(2,1)S(1)}, bf16[1,8,1,8,256]{4,0,3,2,1:T(2,128)(2,1)S(1)}, u32[]{:S(2)}, u32[]{:S(2)}) collective-permute-start(bf16[1,8,1,8,256]{4,0,3,2,1:T(2,128)(2,1)S(1)} %get-tuple-element.15), channel_id=1, source_target_pairs={{1,0},{3,2},{5,4},{7,6},{9,8},{11,10},{13,12},{15,14},{17,16},{19,... | collective-permute-start | bytes 98312 | tf_op jit(solution)/shard_map/ppermute | solution.py:77
  64.6 3.0 %copy-start = (bf16[1,1,1,1,512,128]{5,4,3,2,1,0:T(8,128)(2,1)S(1)}, bf16[1,1,1,1,512,128]{5,4,3,2,1,0:T(8,128)(2,1)}, u32[]{:S(2)}) copy-start(bf16[1,1,1,1,512,128]{5,4,3,2,1,0:T(8,128)(2,1)} %param.6) | copy-start | bytes 393220
  64.6 3.5 %copy-start.1 = (bf16[1,1,1,512,128]{4,3,2,1,0:T(8,128)(2,1)S(1)}, bf16[1,1,1,512,128]{4,3,2,1,0:T(8,128)(2,1)}, u32[]{:S(2)}) copy-start(bf16[1,1,1,512,128]{4,3,2,1,0:T(8,128)(2,1)} %param.7) | copy-start | bytes 393220
  70.4 10.5 %collective-permute-start.12 = (bf16[1,1,1,8,128]{4,0,3,2,1:T(2,128)(2,1)S(1)}, bf16[1,1,1,8,128]{4,0,3,2,1:T(2,128)(2,1)S(1)}, u32[]{:S(2)}, u32[]{:S(2)}) collective-permute-start(bf16[1,1,1,8,128]{4,0,3,2,1:T(2,128)(2,1)S(1)} %get-tuple-element.18), channel_id=1, source_target_pairs={{8,3},{10,5},{12,7},{16,11},{18,13},{20,15},{24,19},{26,21},{28,23}} | collective-permute-start | bytes 6152 | tf_op jit(solution)/shard_map/ppermute | solution.py:77
  71.7 10.6 %collective-permute-start.19 = (bf16[1,1,1,8,128]{4,0,3,2,1:T(2,128)(2,1)S(1)}, bf16[1,1,1,8,128]{4,0,3,2,1:T(2,128)(2,1)S(1)}, u32[]{:S(2)}, u32[]{:S(2)}) collective-permute-start(bf16[1,1,1,8,128]{4,0,3,2,1:T(2,128)(2,1)S(1)} %get-tuple-element.19), channel_id=1, source_target_pairs={{11,0},{13,2},{15,4},{19,8},{21,10},{23,12},{27,16},{29,18},{31,20}} | collective-permute-start | bytes 6152 | tf_op jit(solution)/shard_map/ppermute | solution.py:77
  76.7 7.6 %collective-permute-start.17 = (bf16[1,1,1,8,128]{4,0,3,2,1:T(2,128)(2,1)S(1)}, bf16[1,1,1,8,128]{4,0,3,2,1:T(2,128)(2,1)S(1)}, u32[]{:S(2)}, u32[]{:S(2)}) collective-permute-start(bf16[1,1,1,8,128]{4,0,3,2,1:T(2,128)(2,1)S(1)} %get-tuple-element.20), channel_id=1, source_target_pairs={{10,1},{12,3},{14,5},{18,9},{20,11},{22,13},{26,17},{28,19},{30,21}} | collective-permute-start | bytes 6152 | tf_op jit(solution)/shard_map/ppermute | solution.py:77
  78.0 8.3 %collective-permute-start.14 = (bf16[1,1,1,8,128]{4,0,3,2,1:T(2,128)(2,1)S(1)}, bf16[1,1,1,8,128]{4,0,3,2,1:T(2,128)(2,1)S(1)}, u32[]{:S(2)}, u32[]{:S(2)}) collective-permute-start(bf16[1,1,1,8,128]{4,0,3,2,1:T(2,128)(2,1)S(1)} %get-tuple-element.21), channel_id=1, source_target_pairs={{9,2},{11,4},{13,6},{17,10},{19,12},{21,14},{25,18},{27,20},{29,22}} | collective-permute-start | bytes 6152 | tf_op jit(solution)/shard_map/ppermute | solution.py:77
  79.6 17.1 %copy-start.7 = (bf16[512,128]{1,0:T(8,128)(2,1)}, bf16[512,128]{1,0:T(8,128)(2,1)S(1)}, u32[]{:S(2)}) copy-start(bf16[512,128]{1,0:T(8,128)(2,1)S(1)} %fusion.59) | copy-start | bytes 393220
  79.7 8.7 %collective-permute-start.15 = (bf16[1,8,1,8,128]{4,0,3,2,1:T(2,128)(2,1)S(1)}, bf16[1,8,1,8,128]{4,0,3,2,1:T(2,128)(2,1)S(1)}, u32[]{:S(2)}, u32[]{:S(2)}) collective-permute-start(bf16[1,8,1,8,128]{4,0,3,2,1:T(2,128)(2,1)S(1)} %get-tuple-element.24), channel_id=1, source_target_pairs={{8,1},{10,3},{12,5},{14,7},{16,9},{18,11},{20,13},{22,15},{24,17},... | collective-permute-start | bytes 49160 | tf_op jit(solution)/shard_map/ppermute | solution.py:77
  81.0 7.5 %collective-permute-start.16 = (bf16[1,8,1,8,128]{4,0,3,2,1:T(2,128)(2,1)S(1)}, bf16[1,8,1,8,128]{4,0,3,2,1:T(2,128)(2,1)S(1)}, u32[]{:S(2)}, u32[]{:S(2)}) collective-permute-start(bf16[1,8,1,8,128]{4,0,3,2,1:T(2,128)(2,1)S(1)} %get-tuple-element.25), channel_id=1, source_target_pairs={{9,0},{11,2},{13,4},{15,6},{17,8},{19,10},{21,12},{23,14},{25,16},... | collective-permute-start | bytes 49160 | tf_op jit(solution)/shard_map/ppermute | solution.py:77
  82.3 6.5 %collective-permute-start.13 = (bf16[1,1,8,8,128]{4,0,3,2,1:T(2,128)(2,1)S(1)}, bf16[1,1,8,8,128]{4,0,3,2,1:T(2,128)(2,1)S(1)}, u32[]{:S(2)}, u32[]{:S(2)}) collective-permute-start(bf16[1,1,8,8,128]{4,0,3,2,1:T(2,128)(2,1)S(1)} %get-tuple-element.22), channel_id=1, source_target_pairs={{8,2},{9,3},{10,4},{11,5},{12,6},{13,7},{16,10},{17,11},{18,12},{1... | collective-permute-start | bytes 49160 | tf_op jit(solution)/shard_map/ppermute | solution.py:77
  84.3 5.8 %collective-permute-start.18 = (bf16[1,1,8,8,128]{4,0,3,2,1:T(2,128)(2,1)S(1)}, bf16[1,1,8,8,128]{4,0,3,2,1:T(2,128)(2,1)S(1)}, u32[]{:S(2)}, u32[]{:S(2)}) collective-permute-start(bf16[1,1,8,8,128]{4,0,3,2,1:T(2,128)(2,1)S(1)} %get-tuple-element.23), channel_id=1, source_target_pairs={{10,0},{11,1},{12,2},{13,3},{14,4},{15,5},{18,8},{19,9},{20,10},{2... | collective-permute-start | bytes 49160 | tf_op jit(solution)/shard_map/ppermute | solution.py:77
  86.3 7.2 %collective-permute-start.11 = (bf16[512,128]{1,0:T(8,128)(2,1)S(1)}, bf16[512,128]{1,0:T(8,128)(2,1)S(1)}, u32[]{:S(2)}, u32[]{:S(2)}) collective-permute-start(bf16[512,128]{1,0:T(8,128)(2,1)S(1)} %fusion.59), channel_id=1, source_target_pairs={{8,0},{16,8},{24,16},{9,1},{17,9},{25,17},{10,2},{18,10},{26,18},{... | collective-permute-start | bytes 393224 | tf_op jit(solution)/shard_map/ppermute | solution.py:183
  93.4 3.6 %copy-start.3 = (bf16[512,128]{1,0:T(8,128)(2,1)}, bf16[512,128]{1,0:T(8,128)(2,1)S(1)}, u32[]{:S(2)}) copy-start(bf16[512,128]{1,0:T(8,128)(2,1)S(1)} %collective-permute-done.11) | copy-start | bytes 393220
  97.4 20.5 %copy-start.5 = (bf16[512,128]{1,0:T(8,128)(2,1)}, bf16[512,128]{1,0:T(8,128)(2,1)S(1)}, u32[]{:S(2)}) copy-start(bf16[512,128]{1,0:T(8,128)(2,1)S(1)} %fusion.65) | copy-start | bytes 393220
  97.4 8.4 %collective-permute-start.28 = (bf16[1,1,1,8,128]{4,0,3,2,1:T(2,128)(2,1)S(1)}, bf16[1,1,1,8,128]{4,0,3,2,1:T(2,128)(2,1)S(1)}, u32[]{:S(2)}, u32[]{:S(2)}) collective-permute-start(bf16[1,1,1,8,128]{4,0,3,2,1:T(2,128)(2,1)S(1)} %copy.47), channel_id=1, source_target_pairs={{11,0},{13,2},{15,4},{19,8},{21,10},{23,12},{27,16},{29,18},{31,20}} | collective-permute-start | bytes 6152 | tf_op jit(solution)/shard_map/ppermute | solution.py:77
  99.8 17.8 %collective-permute-start.20 = (bf16[512,128]{1,0:T(8,128)(2,1)S(1)}, bf16[512,128]{1,0:T(8,128)(2,1)S(1)}, u32[]{:S(2)}, u32[]{:S(2)}) collective-permute-start(bf16[512,128]{1,0:T(8,128)(2,1)S(1)} %fusion.65), channel_id=1, source_target_pairs={{8,0},{16,8},{24,16},{9,1},{17,9},{25,17},{10,2},{18,10},{26,18},{... | collective-permute-start | bytes 393224 | tf_op jit(solution)/shard_map/ppermute | solution.py:183
  101.7 5.4 %collective-permute-start.23 = (bf16[1,1,1,8,128]{4,0,3,2,1:T(2,128)(2,1)S(1)}, bf16[1,1,1,8,128]{4,0,3,2,1:T(2,128)(2,1)S(1)}, u32[]{:S(2)}, u32[]{:S(2)}) collective-permute-start(bf16[1,1,1,8,128]{4,0,3,2,1:T(2,128)(2,1)S(1)} %copy.40), channel_id=1, source_target_pairs={{9,2},{11,4},{13,6},{17,10},{19,12},{21,14},{25,18},{27,20},{29,22}} | collective-permute-start | bytes 6152 | tf_op jit(solution)/shard_map/ppermute | solution.py:77
  103.0 5.8 %collective-permute-start.26 = (bf16[1,1,1,8,128]{4,0,3,2,1:T(2,128)(2,1)S(1)}, bf16[1,1,1,8,128]{4,0,3,2,1:T(2,128)(2,1)S(1)}, u32[]{:S(2)}, u32[]{:S(2)}) collective-permute-start(bf16[1,1,1,8,128]{4,0,3,2,1:T(2,128)(2,1)S(1)} %copy.45), channel_id=1, source_target_pairs={{10,1},{12,3},{14,5},{18,9},{20,11},{22,13},{26,17},{28,19},{30,21}} | collective-permute-start | bytes 6152 | tf_op jit(solution)/shard_map/ppermute | solution.py:77
  104.3 6.7 %collective-permute-start.21 = (bf16[1,1,1,8,128]{4,0,3,2,1:T(2,128)(2,1)S(1)}, bf16[1,1,1,8,128]{4,0,3,2,1:T(2,128)(2,1)S(1)}, u32[]{:S(2)}, u32[]{:S(2)}) collective-permute-start(bf16[1,1,1,8,128]{4,0,3,2,1:T(2,128)(2,1)S(1)} %copy.38), channel_id=1, source_target_pairs={{8,3},{10,5},{12,7},{16,11},{18,13},{20,15},{24,19},{26,21},{28,23}} | collective-permute-start | bytes 6152 | tf_op jit(solution)/shard_map/ppermute | solution.py:77
  105.8 7.2 %collective-permute-start.25 = (bf16[1,8,1,8,128]{4,0,3,2,1:T(2,128)(2,1)S(1)}, bf16[1,8,1,8,128]{4,0,3,2,1:T(2,128)(2,1)S(1)}, u32[]{:S(2)}, u32[]{:S(2)}) collective-permute-start(bf16[1,8,1,8,128]{4,0,3,2,1:T(2,128)(2,1)S(1)} %copy.44), channel_id=1, source_target_pairs={{9,0},{11,2},{13,4},{15,6},{17,8},{19,10},{21,12},{23,14},{25,16},... | collective-permute-start | bytes 49160 | tf_op jit(solution)/shard_map/ppermute | solution.py:77
  107.1 6.4 %collective-permute-start.24 = (bf16[1,8,1,8,128]{4,0,3,2,1:T(2,128)(2,1)S(1)}, bf16[1,8,1,8,128]{4,0,3,2,1:T(2,128)(2,1)S(1)}, u32[]{:S(2)}, u32[]{:S(2)}) collective-permute-start(bf16[1,8,1,8,128]{4,0,3,2,1:T(2,128)(2,1)S(1)} %copy.41), channel_id=1, source_target_pairs={{8,1},{10,3},{12,5},{14,7},{16,9},{18,11},{20,13},{22,15},{24,17},... | collective-permute-start | bytes 49160 | tf_op jit(solution)/shard_map/ppermute | solution.py:77
  108.9 5.5 %collective-permute-start.27 = (bf16[1,1,8,8,128]{4,0,3,2,1:T(2,128)(2,1)S(1)}, bf16[1,1,8,8,128]{4,0,3,2,1:T(2,128)(2,1)S(1)}, u32[]{:S(2)}, u32[]{:S(2)}) collective-permute-start(bf16[1,1,8,8,128]{4,0,3,2,1:T(2,128)(2,1)S(1)} %copy.46), channel_id=1, source_target_pairs={{10,0},{11,1},{12,2},{13,3},{14,4},{15,5},{18,8},{19,9},{20,10},{2... | collective-permute-start | bytes 49160 | tf_op jit(solution)/shard_map/ppermute | solution.py:77
  111.1 6.4 %collective-permute-start.22 = (bf16[1,1,8,8,128]{4,0,3,2,1:T(2,128)(2,1)S(1)}, bf16[1,1,8,8,128]{4,0,3,2,1:T(2,128)(2,1)S(1)}, u32[]{:S(2)}, u32[]{:S(2)}) collective-permute-start(bf16[1,1,8,8,128]{4,0,3,2,1:T(2,128)(2,1)S(1)} %copy.39), channel_id=1, source_target_pairs={{8,2},{9,3},{10,4},{11,5},{12,6},{13,7},{16,10},{17,11},{18,12},{1... | collective-permute-start | bytes 49160 | tf_op jit(solution)/shard_map/ppermute | solution.py:77
  121.6 8.6 %collective-permute-start.37 = (bf16[1,1,1,8,128]{4,0,3,2,1:T(2,128)(2,1)S(1)}, bf16[1,1,1,8,128]{4,0,3,2,1:T(2,128)(2,1)S(1)}, u32[]{:S(2)}, u32[]{:S(2)}) collective-permute-start(bf16[1,1,1,8,128]{4,0,3,2,1:T(2,128)(2,1)S(1)} %copy.57), channel_id=1, source_target_pairs={{11,0},{13,2},{15,4},{19,8},{21,10},{23,12},{27,16},{29,18},{31,20}} | collective-permute-start | bytes 6152 | tf_op jit(solution)/shard_map/ppermute | solution.py:77
  123.3 19.0 %collective-permute-start.29 = (bf16[512,128]{1,0:T(8,128)(2,1)S(1)}, bf16[512,128]{1,0:T(8,128)(2,1)S(1)}, u32[]{:S(2)}, u32[]{:S(2)}) collective-permute-start(bf16[512,128]{1,0:T(8,128)(2,1)S(1)} %fusion.68), channel_id=1, source_target_pairs={{8,0},{16,8},{24,16},{9,1},{17,9},{25,17},{10,2},{18,10},{26,18},{... | collective-permute-start | bytes 393224 | tf_op jit(solution)/shard_map/ppermute | solution.py:183
  126.2 6.3 %collective-permute-start.32 = (bf16[1,1,1,8,128]{4,0,3,2,1:T(2,128)(2,1)S(1)}, bf16[1,1,1,8,128]{4,0,3,2,1:T(2,128)(2,1)S(1)}, u32[]{:S(2)}, u32[]{:S(2)}) collective-permute-start(bf16[1,1,1,8,128]{4,0,3,2,1:T(2,128)(2,1)S(1)} %copy.50), channel_id=1, source_target_pairs={{9,2},{11,4},{13,6},{17,10},{19,12},{21,14},{25,18},{27,20},{29,22}} | collective-permute-start | bytes 6152 | tf_op jit(solution)/shard_map/ppermute | solution.py:77
  127.4 6.3 %collective-permute-start.35 = (bf16[1,1,1,8,128]{4,0,3,2,1:T(2,128)(2,1)S(1)}, bf16[1,1,1,8,128]{4,0,3,2,1:T(2,128)(2,1)S(1)}, u32[]{:S(2)}, u32[]{:S(2)}) collective-permute-start(bf16[1,1,1,8,128]{4,0,3,2,1:T(2,128)(2,1)S(1)} %copy.55), channel_id=1, source_target_pairs={{10,1},{12,3},{14,5},{18,9},{20,11},{22,13},{26,17},{28,19},{30,21}} | collective-permute-start | bytes 6152 | tf_op jit(solution)/shard_map/ppermute | solution.py:77
  128.7 7.0 %collective-permute-start.30 = (bf16[1,1,1,8,128]{4,0,3,2,1:T(2,128)(2,1)S(1)}, bf16[1,1,1,8,128]{4,0,3,2,1:T(2,128)(2,1)S(1)}, u32[]{:S(2)}, u32[]{:S(2)}) collective-permute-start(bf16[1,1,1,8,128]{4,0,3,2,1:T(2,128)(2,1)S(1)} %copy.48), channel_id=1, source_target_pairs={{8,3},{10,5},{12,7},{16,11},{18,13},{20,15},{24,19},{26,21},{28,23}} | collective-permute-start | bytes 6152 | tf_op jit(solution)/shard_map/ppermute | solution.py:77
  130.2 7.8 %collective-permute-start.34 = (bf16[1,8,1,8,128]{4,0,3,2,1:T(2,128)(2,1)S(1)}, bf16[1,8,1,8,128]{4,0,3,2,1:T(2,128)(2,1)S(1)}, u32[]{:S(2)}, u32[]{:S(2)}) collective-permute-start(bf16[1,8,1,8,128]{4,0,3,2,1:T(2,128)(2,1)S(1)} %copy.54), channel_id=1, source_target_pairs={{9,0},{11,2},{13,4},{15,6},{17,8},{19,10},{21,12},{23,14},{25,16},... | collective-permute-start | bytes 49160 | tf_op jit(solution)/shard_map/ppermute | solution.py:77
  132.4 6.4 %collective-permute-start.33 = (bf16[1,8,1,8,128]{4,0,3,2,1:T(2,128)(2,1)S(1)}, bf16[1,8,1,8,128]{4,0,3,2,1:T(2,128)(2,1)S(1)}, u32[]{:S(2)}, u32[]{:S(2)}) collective-permute-start(bf16[1,8,1,8,128]{4,0,3,2,1:T(2,128)(2,1)S(1)} %copy.51), channel_id=1, source_target_pairs={{8,1},{10,3},{12,5},{14,7},{16,9},{18,11},{20,13},{22,15},{24,17},... | collective-permute-start | bytes 49160 | tf_op jit(solution)/shard_map/ppermute | solution.py:77
  133.8 5.6 %collective-permute-start.36 = (bf16[1,1,8,8,128]{4,0,3,2,1:T(2,128)(2,1)S(1)}, bf16[1,1,8,8,128]{4,0,3,2,1:T(2,128)(2,1)S(1)}, u32[]{:S(2)}, u32[]{:S(2)}) collective-permute-start(bf16[1,1,8,8,128]{4,0,3,2,1:T(2,128)(2,1)S(1)} %copy.56), channel_id=1, source_target_pairs={{10,0},{11,1},{12,2},{13,3},{14,4},{15,5},{18,8},{19,9},{20,10},{2... | collective-permute-start | bytes 49160 | tf_op jit(solution)/shard_map/ppermute | solution.py:77
  135.8 6.5 %collective-permute-start.31 = (bf16[1,1,8,8,128]{4,0,3,2,1:T(2,128)(2,1)S(1)}, bf16[1,1,8,8,128]{4,0,3,2,1:T(2,128)(2,1)S(1)}, u32[]{:S(2)}, u32[]{:S(2)}) collective-permute-start(bf16[1,1,8,8,128]{4,0,3,2,1:T(2,128)(2,1)S(1)} %copy.49), channel_id=1, source_target_pairs={{8,2},{9,3},{10,4},{11,5},{12,6},{13,7},{16,10},{17,11},{18,12},{1... | collective-permute-start | bytes 49160 | tf_op jit(solution)/shard_map/ppermute | solution.py:77
  142.7 3.6 %copy-start.2 = (bf16[1,1,1,512,128]{4,3,2,1,0:T(8,128)(2,1)S(1)}, bf16[1,1,1,512,128]{4,3,2,1,0:T(8,128)(2,1)}, u32[]{:S(2)}) copy-start(bf16[1,1,1,512,128]{4,3,2,1,0:T(8,128)(2,1)} %param.7) | copy-start | bytes 393220
  142.7 3.6 %copy-start.4 = (bf16[512,128]{1,0:T(8,128)(2,1)S(1)}, bf16[512,128]{1,0:T(8,128)(2,1)}, u32[]{:S(2)}) copy-start(bf16[512,128]{1,0:T(8,128)(2,1)} %copy-done.3) | copy-start | bytes 393220
  142.7 3.6 %copy-start.6 = (bf16[512,128]{1,0:T(8,128)(2,1)S(1)}, bf16[512,128]{1,0:T(8,128)(2,1)}, u32[]{:S(2)}) copy-start(bf16[512,128]{1,0:T(8,128)(2,1)} %copy-done.5) | copy-start | bytes 393220
  142.7 3.6 %copy-start.8 = (bf16[512,128]{1,0:T(8,128)(2,1)S(1)}, bf16[512,128]{1,0:T(8,128)(2,1)}, u32[]{:S(2)}) copy-start(bf16[512,128]{1,0:T(8,128)(2,1)} %copy-done.7) | copy-start | bytes 393220
  146.0 1.4 copy-start.10
  146.0 1.4 copy-start.13
  146.0 1.4 copy-start.14
  146.0 1.4 copy-start.15
  146.0 1.4 copy-start.16
  146.0 1.4 copy-start.17
  146.0 1.4 copy-start.18
  146.0 1.4 copy-start.19
  146.1 1.4 copy-start.20
  146.1 1.4 copy-start.21
  151.6 6.9 %collective-permute-start.38 = (bf16[864,128]{1,0:T(8,128)(2,1)S(1)}, bf16[864,128]{1,0:T(8,128)(2,1)S(1)}, u32[]{:S(2)}, u32[]{:S(2)}) collective-permute-start(bf16[864,128]{1,0:T(8,128)(2,1)S(1)} %get-tuple-element.5), channel_id=1, source_target_pairs={{0,2},{2,4},{4,6},{6,0},{1,3},{3,5},{5,7},{7,1},{8,10},{10,12},{12... | collective-permute-start | bytes 663560 | tf_op jit(solution)/shard_map/ppermute | solution.py:122
  154.1 10.3 %collective-permute-start.40 = (bf16[864,128]{1,0:T(8,128)(2,1)S(1)}, bf16[864,128]{1,0:T(8,128)(2,1)S(1)}, u32[]{:S(2)}, u32[]{:S(2)}) collective-permute-start(bf16[864,128]{1,0:T(8,128)(2,1)S(1)} %get-tuple-element.6), channel_id=1, source_target_pairs={{0,6},{2,0},{4,2},{6,4},{1,7},{3,1},{5,3},{7,5},{8,14},{10,8},{12,... | collective-permute-start | bytes 663560 | tf_op jit(solution)/shard_map/ppermute | solution.py:122
  154.2 10.2 %collective-permute-start.39 = (bf16[864,128]{1,0:T(8,128)(2,1)S(1)}, bf16[864,128]{1,0:T(8,128)(2,1)S(1)}, u32[]{:S(2)}, u32[]{:S(2)}) collective-permute-start(bf16[864,128]{1,0:T(8,128)(2,1)S(1)} %get-tuple-element.7), channel_id=1, source_target_pairs={{0,4},{2,6},{4,0},{6,2},{1,5},{3,7},{5,1},{7,3},{8,12},{10,14},{12... | collective-permute-start | bytes 663560 | tf_op jit(solution)/shard_map/ppermute | solution.py:122
  164.5 2.4 %collective-permute-start.41 = (f32[864,128]{1,0:T(8,128)S(1)}, f32[864,128]{1,0:T(8,128)S(1)}, u32[]{:S(2)}, u32[]{:S(2)}) collective-permute-start(f32[864,128]{1,0:T(8,128)S(1)} %convert_add_fusion), channel_id=1, source_target_pairs={{0,1},{1,0},{2,3},{3,2},{4,5},{5,4},{6,7},{7,6},{8,9},{9,8},{10,11... | collective-permute-start | bytes 1327112 | tf_op jit(solution)/shard_map/ppermute | solution.py:193
  (17 other events, 23.5 us)

commit v3 on v2

--- a/solution.py
+++ b/solution.py
@@ -55,26 +55,39 @@
 
 
 def exchange(cube, axes, sizes, pipe_step):
-    received = {}
-    for shift_x, shift_y in directions():
-        piece = face_piece(cube, shift_x, shift_y)
+    n_pipe, n_x, n_y = sizes if pipe_step else (pipe_step + 1, *sizes)
+
+    def linear(p, a, b):
+        return (p * n_x + a) * n_y + b if pipe_step else a * n_y + b
+
+    def send(piece, moves):
         route = []
-        if pipe_step:
-            n_pipe, n_x, n_y = sizes
-            for p in range(pipe_step, n_pipe):
-                for a in range(n_x):
-                    for b in range(n_y):
-                        ta, tb = a - shift_x, b - shift_y
-                        if 0 <= ta < n_x and 0 <= tb < n_y:
-                            route.append(((p * n_x + a) * n_y + b, ((p - pipe_step) * n_x + ta) * n_y + tb))
-        else:
-            n_x, n_y = sizes
+        for p in range(pipe_step, n_pipe):
             for a in range(n_x):
                 for b in range(n_y):
-                    ta, tb = a - shift_x, b - shift_y
+                    ta, tb = moves(a, b)
                     if 0 <= ta < n_x and 0 <= tb < n_y:
-                        route.append((a * n_y + b, ta * n_y + tb))
-        received[(shift_x, shift_y)] = lax.ppermute(piece, axes, route)
+                        route.append((linear(p, a, b), linear(p - pipe_step, ta, tb)))
+        return lax.ppermute(piece, axes, route)
+
+    received = {}
+    if n_y == 2:
+        place_y = lax.axis_index("sy")
+        for shift_x in OFFSETS:
+            if shift_x != 0:
+                received[(shift_x, 0)] = send(
+                    face_piece(cube, shift_x, 0), lambda a, b, i=shift_x: (a - i, b)
+                )
+            row = lax.dynamic_slice_in_dim(cube[:, source_range(shift_x)], (1 - place_y) * 7, 1, axis=2)
+            got = send(row, lambda a, b, i=shift_x: (a - i, 1 - b))
+            blank = jnp.zeros_like(got)
+            received[(shift_x, 1)] = jnp.where(place_y == 0, got, blank)
+            received[(shift_x, -1)] = jnp.where(place_y == 1, got, blank)
+        return received
+    for shift_x, shift_y in directions():
+        received[(shift_x, shift_y)] = send(
+            face_piece(cube, shift_x, shift_y), lambda a, b, i=shift_x, j=shift_y: (a - i, b - j)
+        )
     return received
 
 
@@ -166,14 +179,15 @@
         start = jnp.where(live_now[:, None], start, jnp.zeros_like(start))
         both = jnp.concatenate([cube(activation), cube(start)], axis=-1)
         got = exchange(both, ("sx", "sy"), (n_x, n_y), 0)
-        act_pad = assemble(cube(activation), {k: v[..., :channels] for k, v in got.items()}, table)
+        both_pad = assemble(both, got, table)
+        act_pad = both_pad[..., :channels]
         centre = start
-        received = {k: v[..., channels:] for k, v in got.items()}
+        received = None
         kept_dy = start
         kept_grad = jnp.zeros((row_count, channels), jnp.bfloat16)
         for tick in range(n_pipe):
             active = segment_place == n_pipe - 1 - tick
-            grad_pad = assemble(cube(centre), received, table)
+            grad_pad = both_pad[..., channels:] if tick == 0 else assemble(cube(centre), received, table)
             grad_act = conv_data(grad_pad, flipped).reshape(row_count, channels)
             result = finish_grad(values, centre, live_now, grad_act, gain_row)
             kept_dy = jnp.where(active, centre, kept_dy)

time: 171 us -> 148 us (0.87); the launches traced: 168 us -> 147 us
  starting transfers between devices: 78 us -> 61.9 us
  other arithmetic: 24 us -> 13.8 us
  waiting for transfers between devices: 24.2 us -> 27.8 us
    select_n x79 -> x43, other arithmetic: 15 us -> 1.33 us  [assemble(): picked = jnp.where(chosen, piece, jnp.zeros_like(piece))]
    ppermute x32 -> x20, starting transfers between devices: 64 us -> 50.5 us  [send(): return lax.ppermute(piece, axes, route)]
    concatenate x0 -> x22, other arithmetic: none -> 2.94 us  [the longest x1 2.13 us: assemble(): return jnp.concatenate(slabs_x, axis=1)]
    ppermute x32 -> x20, waiting for transfers between devices: 10.5 us -> 12.5 us  [send(): return lax.ppermute(piece, axes, route)]
    convert_element_type x4, other arithmetic: 3.17 us -> 1.21 us  [finish_grad(): return result.astype(jnp.bfloat16)]
  transfers between devices with their start and end apart: 42 -> 30, of which waited for: 14 -> 12; matrix products, arithmetic and copies ran while one was open for 13% -> 8% of each run, Pallas kernels for 0% -> 0%
where the time goes in v3:
time: 148 us; the launch traced here: 147 us
  starting transfers between devices  61.9 us (42%)
  waiting for transfers between devices  27.8 us (19%)
  between operations  19.8 us (13%)
  matrix products  16.8 us (11%)
  other arithmetic  13.8 us (9%)
  local copies, waits for them, and re-layouts  7.02 us (5%)
    ppermute x20, starting transfers between devices, send(): return lax.ppermute(piece, axes, route)  50.5 us
    conv_general_dilated x4, matrix products, conv_data(): lax.conv_general_dilated(padded, filters, (1, 1, 1), 'VALID', dimension_n...  13 us
    ppermute x20, waiting for transfers between devices, send(): return lax.ppermute(piece, axes, route)  12.5 us
    ppermute x3, waiting for transfers between devices, scattered_sum(): lax.ppermute(piece, axis, [(i, (i + step) % count) for i in range(count)])  10.6 us
    ppermute x3, starting transfers between devices, shards(): centre = lax.ppermute(result, 'pipe', down)  5.94 us
    transpose x1, matrix products, shards(): per_tap.transpose(1, 2, 3, 0, 4).reshape(taps * channels, channels)  3.77 us
    ppermute x3, waiting for transfers between devices, shards(): centre = lax.ppermute(result, 'pipe', down)  3.3 us
  transfers between devices with their start and end apart: 30, of which 12 were waited for; matrix products, arithmetic and copies ran while one was open for 8% of the time, Pallas kernels for 0%

profile of v3, /device:TPU:21, one launch (start us, length us, event | category | flops | bytes accessed | tf_op | source)
XLA Modules:
  0.0 147.0 jit_solution(14116033852282115546)
XLA Ops:
  0.6 1.2 collective-permute-start.7
  1.8 1.2 collective-permute-start.6
  3.1 1.0 fusion.25
  4.1 0.9 convert_element_type.160
  5.9 1.0 broadcast_select_fusion.12
  7.0 0.8 multiply_convert_fusion.2
  7.8 3.3 %collective-permute-start.1 = (bf16[1,1,8,8,256]{4,3,2,1,0:T(8,128)(2,1)S(1)}, bf16[1,1,8,8,256]{4,3,2,1,0:T(8,128)(2,1)S(1)}, u32[]{:S(2)}, u32[]{:S(2)}) collective-permute-start(bf16[1,1,8,8,256]{4,3,2,1,0:T(8,128)(2,1)S(1)} %fusion.55), channel_id=1, source_target_pairs={{0,2},{1,3},{2,4},{3,5},{4,6},{5,7},{8,10},{9,11},{10,12},{11,13},... | collective-permute-start | bytes 98312 | tf_op jit(solution)/shard_map/ppermute | solution.py:71
  11.2 2.7 %collective-permute-start = (bf16[1,1,1,8,256]{4,3,2,1,0:T(8,128)(2,1)S(1)}, bf16[1,1,1,8,256]{4,3,2,1,0:T(8,128)(2,1)S(1)}, u32[]{:S(2)}, u32[]{:S(2)}) collective-permute-start(bf16[1,1,1,8,256]{4,3,2,1,0:T(8,128)(2,1)S(1)} %constant_dynamic-slice_fusion.14), channel_id=1, source_target_pairs={{0,3},{1,2},{2,5},{3,4},{4,7},{5,6},{8,11},{9,10},{10,13},{11,12},... | collective-permute-start | bytes 12296 | tf_op jit(solution)/shard_map/ppermute | solution.py:71
  13.9 0.7 fusion.77
  14.6 0.7 fusion.76
  15.4 0.6 scatter_custom_fusion
  18.5 0.4 copy_dynamic-update-slice_fusion
  18.9 0.6 broadcast_select_fusion
  34.6 3.8 %collective-permute-start.3 = (bf16[1,1,1,8,256]{4,3,2,1,0:T(8,128)(2,1)S(1)}, bf16[1,1,1,8,256]{4,3,2,1,0:T(8,128)(2,1)S(1)}, u32[]{:S(2)}, u32[]{:S(2)}) collective-permute-start(bf16[1,1,1,8,256]{4,3,2,1,0:T(8,128)(2,1)S(1)} %fusion.59), channel_id=1, source_target_pairs={{2,1},{3,0},{4,3},{5,2},{6,5},{7,4},{10,9},{11,8},{12,11},{13,10},... | collective-permute-start | bytes 12296 | tf_op jit(solution)/shard_map/ppermute | solution.py:71
  38.4 1.1 collective-permute-done.3
  39.5 6.1 %collective-permute-start.4 = (bf16[1,1,8,8,256]{4,3,2,1,0:T(8,128)(2,1)S(1)}, bf16[1,1,8,8,256]{4,3,2,1,0:T(8,128)(2,1)S(1)}, u32[]{:S(2)}, u32[]{:S(2)}) collective-permute-start(bf16[1,1,8,8,256]{4,3,2,1,0:T(8,128)(2,1)S(1)} %get-tuple-element.24), channel_id=1, source_target_pairs={{2,0},{3,1},{4,2},{5,3},{6,4},{7,5},{10,8},{11,9},{12,10},{13,11},... | collective-permute-start | bytes 98312 | tf_op jit(solution)/shard_map/ppermute | solution.py:71
  45.6 1.0 collective-permute-done.4
  46.6 0.7 collective-permute-start.2
  47.7 0.5 collective-permute-done.2
  48.5 2.1 %pad_maximum_fusion = bf16[1,10,10,10,256]{4,0,3,2,1:T(2,128)(2,1)S(1)} fusion(bf16[1,1,10,10,256]{4,0,3,2,1:T(2,128)(2,1)S(1)} %copy.33, bf16[1,8,1,10,256]{4,0,3,2,1:T(2,128)(2,1)S(1)} %copy.31, bf16[1,8,8,1,256]{4,0,3,2,1:T(2,128)(2,1)S(1)} %get-tuple-element.33, bf16[1,8,8,8,256]{4,0,3,2,1:T(2,128)(2,1)S(1)} %broadcast_select_fusion, ...), kind=kLoop, calls=%fused_computation.4 | loop fusion | flops 1536000 | bytes 1024000 | tf_op jit(solution)/shard_map/concatenate | solution.py:54
  50.6 0.7 copy-done.4
  51.3 1.0 pad_maximum_fusion.1
  52.4 0.7 gather_fusion
  53.1 1.0 rev.3
  54.1 4.1 %fusion.1 = f32[1,8,8,8,128]{4,0,3,2,1:T(1,128)S(1)} fusion(bf16[3,3,3,128,128]{4,3,2,1,0:T(8,128)(2,1)} %rev.3, bf16[1,10,10,10,256]{4,0,3,2,1:T(2,128)(2,1)S(1)} %pad_maximum_fusion), kind=kOutput, calls=%fused_computation.10 | convolution fusion | flops 452984832 | bytes 1658880 | tf_op jit(solution)/shard_map/conv_general_dilated | solution.py:95
  58.2 0.3 fusion.47
  59.0 1.9 %collective-permute-start.10 = (bf16[1,1,8,8,128]{4,3,2,1,0:T(8,128)(2,1)S(1)}, bf16[1,1,8,8,128]{4,3,2,1,0:T(8,128)(2,1)S(1)}, u32[]{:S(2)}, u32[]{:S(2)}) collective-permute-start(bf16[1,1,8,8,128]{4,3,2,1,0:T(8,128)(2,1)S(1)} %get-tuple-element.46), channel_id=1, source_target_pairs={{8,2},{9,3},{10,4},{11,5},{12,6},{13,7},{16,10},{17,11},{18,12},{1... | collective-permute-start | bytes 49160 | tf_op jit(solution)/shard_map/ppermute | solution.py:71
  61.0 4.1 %collective-permute-start.13 = (bf16[1,1,8,8,128]{4,3,2,1,0:T(8,128)(2,1)S(1)}, bf16[1,1,8,8,128]{4,3,2,1,0:T(8,128)(2,1)S(1)}, u32[]{:S(2)}, u32[]{:S(2)}) collective-permute-start(bf16[1,1,8,8,128]{4,3,2,1,0:T(8,128)(2,1)S(1)} %get-tuple-element.47), channel_id=1, source_target_pairs={{10,0},{11,1},{12,2},{13,3},{14,4},{15,5},{18,8},{19,9},{20,10},{2... | collective-permute-start | bytes 49160 | tf_op jit(solution)/shard_map/ppermute | solution.py:71
  65.1 2.4 %collective-permute-start.12 = (bf16[1,1,1,8,128]{4,3,2,1,0:T(8,128)(2,1)S(1)}, bf16[1,1,1,8,128]{4,3,2,1,0:T(8,128)(2,1)S(1)}, u32[]{:S(2)}, u32[]{:S(2)}) collective-permute-start(bf16[1,1,1,8,128]{4,3,2,1,0:T(8,128)(2,1)S(1)} %constant_dynamic-slice_fusion.9), channel_id=1, source_target_pairs={{10,1},{11,0},{12,3},{13,2},{14,5},{15,4},{18,9},{19,8},{20,11},{2... | collective-permute-start | bytes 6152 | tf_op jit(solution)/shard_map/ppermute | solution.py:71
  67.5 1.9 %collective-permute-start.9 = (bf16[1,1,1,8,128]{4,3,2,1,0:T(8,128)(2,1)S(1)}, bf16[1,1,1,8,128]{4,3,2,1,0:T(8,128)(2,1)S(1)}, u32[]{:S(2)}, u32[]{:S(2)}) collective-permute-start(bf16[1,1,1,8,128]{4,3,2,1,0:T(8,128)(2,1)S(1)} %constant_dynamic-slice_fusion.11), channel_id=1, source_target_pairs={{8,3},{9,2},{10,5},{11,4},{12,7},{13,6},{16,11},{17,10},{18,13},{1... | collective-permute-start | bytes 6152 | tf_op jit(solution)/shard_map/ppermute | solution.py:71
  69.4 1.9 %collective-permute-start.11 = (bf16[1,8,1,8,128]{4,3,2,1,0:T(8,128)(2,1)S(1)}, bf16[1,8,1,8,128]{4,3,2,1,0:T(8,128)(2,1)S(1)}, u32[]{:S(2)}, u32[]{:S(2)}) collective-permute-start(bf16[1,8,1,8,128]{4,3,2,1,0:T(8,128)(2,1)S(1)} %constant_dynamic-slice_fusion.10), channel_id=1, source_target_pairs={{8,1},{9,0},{10,3},{11,2},{12,5},{13,4},{14,7},{15,6},{16,9},{17,8... | collective-permute-start | bytes 49160 | tf_op jit(solution)/shard_map/ppermute | solution.py:71
  71.6 2.1 %collective-permute-start.8 = (bf16[512,128]{1,0:T(8,128)(2,1)S(1)}, bf16[512,128]{1,0:T(8,128)(2,1)S(1)}, u32[]{:S(2)}, u32[]{:S(2)}) collective-permute-start(bf16[512,128]{1,0:T(8,128)(2,1)S(1)} %fusion.8), channel_id=1, source_target_pairs={{8,0},{16,8},{24,16},{9,1},{17,9},{25,17},{10,2},{18,10},{26,18},{... | collective-permute-start | bytes 393224 | tf_op jit(solution)/shard_map/ppermute | solution.py:197
  73.8 0.4 collective-permute-done.9
  74.9 3.3 %collective-permute-done.8 = bf16[512,128]{1,0:T(8,128)(2,1)S(1)} collective-permute-done((bf16[512,128]{1,0:T(8,128)(2,1)S(1)}, bf16[512,128]{1,0:T(8,128)(2,1)S(1)}, u32[]{:S(2)}, u32[]{:S(2)}) %collective-permute-start.8) | collective-permute-done | bytes 131104 | tf_op jit(solution)/shard_map/ppermute | solution.py:197
  78.5 3.0 %fusion.5 = f32[1,8,8,8,128]{4,0,3,2,1:T(1,128)S(1)} fusion(bf16[3,3,3,128,128]{4,3,2,1,0:T(8,128)(2,1)S(1)} %bitcast.203, bf16[1,1,10,10,128]{4,0,3,2,1:T(2,128)(2,1)S(1)} %copy.42, bf16[1,8,1,10,128]{4,0,3,2,1:T(2,128)(2,1)S(1)} %copy.40, bf16[1,8,8,1,128]{4,0,3,2,1:T(2,128)(2,1)S(1)} %slice_bitcast_fusion.4, bf16[1,8,8,8,128]{4,0,3,2,1:T(2,128)(2,1)S(1)} %copy.38, ...), kind=kOutput, calls=%fused_computation.14 | convolution fusion | flops 454776832 | bytes 1402880 | tf_op jit(solution)/shard_map/conv_general_dilated | solution.py:95
  81.5 0.3 fusion.48
  81.8 0.3 fusion.18
  82.2 4.2 %collective-permute-start.18 = (bf16[1,1,1,8,128]{4,3,2,1,0:T(8,128)(2,1)S(1)}, bf16[1,1,1,8,128]{4,3,2,1,0:T(8,128)(2,1)S(1)}, u32[]{:S(2)}, u32[]{:S(2)}) collective-permute-start(bf16[1,1,1,8,128]{4,3,2,1,0:T(8,128)(2,1)S(1)} %constant_dynamic-slice_fusion.6), channel_id=1, source_target_pairs={{10,1},{11,0},{12,3},{13,2},{14,5},{15,4},{18,9},{19,8},{20,11},{2... | collective-permute-start | bytes 6152 | tf_op jit(solution)/shard_map/ppermute | solution.py:71
  86.5 1.9 %collective-permute-start.16 = (bf16[1,1,8,8,128]{4,3,2,1,0:T(8,128)(2,1)S(1)}, bf16[1,1,8,8,128]{4,3,2,1,0:T(8,128)(2,1)S(1)}, u32[]{:S(2)}, u32[]{:S(2)}) collective-permute-start(bf16[1,1,8,8,128]{4,3,2,1,0:T(8,128)(2,1)S(1)} %get-tuple-element.41), channel_id=1, source_target_pairs={{8,2},{9,3},{10,4},{11,5},{12,6},{13,7},{16,10},{17,11},{18,12},{1... | collective-permute-start | bytes 49160 | tf_op jit(solution)/shard_map/ppermute | solution.py:71
  88.4 1.9 %collective-permute-start.19 = (bf16[1,1,8,8,128]{4,3,2,1,0:T(8,128)(2,1)S(1)}, bf16[1,1,8,8,128]{4,3,2,1,0:T(8,128)(2,1)S(1)}, u32[]{:S(2)}, u32[]{:S(2)}) collective-permute-start(bf16[1,1,8,8,128]{4,3,2,1,0:T(8,128)(2,1)S(1)} %get-tuple-element.42), channel_id=1, source_target_pairs={{10,0},{11,1},{12,2},{13,3},{14,4},{15,5},{18,8},{19,9},{20,10},{2... | collective-permute-start | bytes 49160 | tf_op jit(solution)/shard_map/ppermute | solution.py:71
  90.3 1.9 %collective-permute-start.14 = (bf16[512,128]{1,0:T(8,128)(2,1)S(1)}, bf16[512,128]{1,0:T(8,128)(2,1)S(1)}, u32[]{:S(2)}, u32[]{:S(2)}) collective-permute-start(bf16[512,128]{1,0:T(8,128)(2,1)S(1)} %fusion.18), channel_id=1, source_target_pairs={{8,0},{16,8},{24,16},{9,1},{17,9},{25,17},{10,2},{18,10},{26,18},{... | collective-permute-start | bytes 393224 | tf_op jit(solution)/shard_map/ppermute | solution.py:197
  92.3 1.9 %collective-permute-start.17 = (bf16[1,8,1,8,128]{4,3,2,1,0:T(8,128)(2,1)S(1)}, bf16[1,8,1,8,128]{4,3,2,1,0:T(8,128)(2,1)S(1)}, u32[]{:S(2)}, u32[]{:S(2)}) collective-permute-start(bf16[1,8,1,8,128]{4,3,2,1,0:T(8,128)(2,1)S(1)} %constant_dynamic-slice_fusion.7), channel_id=1, source_target_pairs={{8,1},{9,0},{10,3},{11,2},{12,5},{13,4},{14,7},{15,6},{16,9},{17,8... | collective-permute-start | bytes 49160 | tf_op jit(solution)/shard_map/ppermute | solution.py:71
  94.2 1.9 %collective-permute-start.15 = (bf16[1,1,1,8,128]{4,3,2,1,0:T(8,128)(2,1)S(1)}, bf16[1,1,1,8,128]{4,3,2,1,0:T(8,128)(2,1)S(1)}, u32[]{:S(2)}, u32[]{:S(2)}) collective-permute-start(bf16[1,1,1,8,128]{4,3,2,1,0:T(8,128)(2,1)S(1)} %constant_dynamic-slice_fusion.8), channel_id=1, source_target_pairs={{8,3},{9,2},{10,5},{11,4},{12,7},{13,6},{16,11},{17,10},{18,13},{1... | collective-permute-start | bytes 6152 | tf_op jit(solution)/shard_map/ppermute | solution.py:71
  96.2 4.8 %collective-permute-done.15 = bf16[1,1,1,8,128]{4,3,2,1,0:T(8,128)(2,1)S(1)} collective-permute-done((bf16[1,1,1,8,128]{4,3,2,1,0:T(8,128)(2,1)S(1)}, bf16[1,1,1,8,128]{4,3,2,1,0:T(8,128)(2,1)S(1)}, u32[]{:S(2)}, u32[]{:S(2)}) %collective-permute-start.15) | collective-permute-done | bytes 2080 | tf_op jit(solution)/shard_map/ppermute | solution.py:71
  101.8 3.0 %fusion.4 = f32[1,8,8,8,128]{4,0,3,2,1:T(1,128)S(1)} fusion(bf16[3,3,3,128,128]{4,3,2,1,0:T(8,128)(2,1)S(1)} %bitcast.204, bf16[1,1,10,10,128]{4,0,3,2,1:T(2,128)(2,1)S(1)} %copy.49, bf16[1,8,1,10,128]{4,0,3,2,1:T(2,128)(2,1)S(1)} %copy.47, bf16[1,8,8,1,128]{4,0,3,2,1:T(2,128)(2,1)S(1)} %slice_bitcast_fusion.2, bf16[1,8,8,8,128]{4,0,3,2,1:T(2,128)(2,1)S(1)} %copy.45, ...), kind=kOutput, calls=%fused_computation.13 | convolution fusion | flops 454776832 | bytes 1402880 | tf_op jit(solution)/shard_map/conv_general_dilated | solution.py:95
  104.8 0.3 fusion.49
  105.5 1.9 %collective-permute-start.24 = (bf16[1,1,1,8,128]{4,3,2,1,0:T(8,128)(2,1)S(1)}, bf16[1,1,1,8,128]{4,3,2,1,0:T(8,128)(2,1)S(1)}, u32[]{:S(2)}, u32[]{:S(2)}) collective-permute-start(bf16[1,1,1,8,128]{4,3,2,1,0:T(8,128)(2,1)S(1)} %constant_dynamic-slice_fusion.3), channel_id=1, source_target_pairs={{10,1},{11,0},{12,3},{13,2},{14,5},{15,4},{18,9},{19,8},{20,11},{2... | collective-permute-start | bytes 6152 | tf_op jit(solution)/shard_map/ppermute | solution.py:71
  107.5 1.9 %collective-permute-start.22 = (bf16[1,1,8,8,128]{4,3,2,1,0:T(8,128)(2,1)S(1)}, bf16[1,1,8,8,128]{4,3,2,1,0:T(8,128)(2,1)S(1)}, u32[]{:S(2)}, u32[]{:S(2)}) collective-permute-start(bf16[1,1,8,8,128]{4,3,2,1,0:T(8,128)(2,1)S(1)} %get-tuple-element.36), channel_id=1, source_target_pairs={{8,2},{9,3},{10,4},{11,5},{12,6},{13,7},{16,10},{17,11},{18,12},{1... | collective-permute-start | bytes 49160 | tf_op jit(solution)/shard_map/ppermute | solution.py:71
  109.4 1.9 %collective-permute-start.25 = (bf16[1,1,8,8,128]{4,3,2,1,0:T(8,128)(2,1)S(1)}, bf16[1,1,8,8,128]{4,3,2,1,0:T(8,128)(2,1)S(1)}, u32[]{:S(2)}, u32[]{:S(2)}) collective-permute-start(bf16[1,1,8,8,128]{4,3,2,1,0:T(8,128)(2,1)S(1)} %get-tuple-element.37), channel_id=1, source_target_pairs={{10,0},{11,1},{12,2},{13,3},{14,4},{15,5},{18,8},{19,9},{20,10},{2... | collective-permute-start | bytes 49160 | tf_op jit(solution)/shard_map/ppermute | solution.py:71
  111.3 1.9 %collective-permute-start.20 = (bf16[512,128]{1,0:T(8,128)(2,1)S(1)}, bf16[512,128]{1,0:T(8,128)(2,1)S(1)}, u32[]{:S(2)}, u32[]{:S(2)}) collective-permute-start(bf16[512,128]{1,0:T(8,128)(2,1)S(1)} %fusion.21), channel_id=1, source_target_pairs={{8,0},{16,8},{24,16},{9,1},{17,9},{25,17},{10,2},{18,10},{26,18},{... | collective-permute-start | bytes 393224 | tf_op jit(solution)/shard_map/ppermute | solution.py:197
  113.2 1.9 %collective-permute-start.23 = (bf16[1,8,1,8,128]{4,3,2,1,0:T(8,128)(2,1)S(1)}, bf16[1,8,1,8,128]{4,3,2,1,0:T(8,128)(2,1)S(1)}, u32[]{:S(2)}, u32[]{:S(2)}) collective-permute-start(bf16[1,8,1,8,128]{4,3,2,1,0:T(8,128)(2,1)S(1)} %constant_dynamic-slice_fusion.4), channel_id=1, source_target_pairs={{8,1},{9,0},{10,3},{11,2},{12,5},{13,4},{14,7},{15,6},{16,9},{17,8... | collective-permute-start | bytes 49160 | tf_op jit(solution)/shard_map/ppermute | solution.py:71
  115.2 2.1 %collective-permute-start.21 = (bf16[1,1,1,8,128]{4,3,2,1,0:T(8,128)(2,1)S(1)}, bf16[1,1,1,8,128]{4,3,2,1,0:T(8,128)(2,1)S(1)}, u32[]{:S(2)}, u32[]{:S(2)}) collective-permute-start(bf16[1,1,1,8,128]{4,3,2,1,0:T(8,128)(2,1)S(1)} %constant_dynamic-slice_fusion.5), channel_id=1, source_target_pairs={{8,3},{9,2},{10,5},{11,4},{12,7},{13,6},{16,11},{17,10},{18,13},{1... | collective-permute-start | bytes 6152 | tf_op jit(solution)/shard_map/ppermute | solution.py:71
  117.4 4.5 %collective-permute-done.21 = bf16[1,1,1,8,128]{4,3,2,1,0:T(8,128)(2,1)S(1)} collective-permute-done((bf16[1,1,1,8,128]{4,3,2,1,0:T(8,128)(2,1)S(1)}, bf16[1,1,1,8,128]{4,3,2,1,0:T(8,128)(2,1)S(1)}, u32[]{:S(2)}, u32[]{:S(2)}) %collective-permute-start.21) | collective-permute-done | bytes 2080 | tf_op jit(solution)/shard_map/ppermute | solution.py:71
  122.8 3.0 %fusion.3 = f32[1,8,8,8,128]{4,0,3,2,1:T(1,128)S(1)} fusion(bf16[3,3,3,128,128]{4,3,2,1,0:T(8,128)(2,1)S(1)} %bitcast.205, bf16[1,1,10,10,128]{4,0,3,2,1:T(2,128)(2,1)S(1)} %copy.56, bf16[1,8,1,10,128]{4,0,3,2,1:T(2,128)(2,1)S(1)} %copy.54, bf16[1,8,8,1,128]{4,0,3,2,1:T(2,128)(2,1)S(1)} %slice_bitcast_fusion, bf16[1,8,8,8,128]{4,0,3,2,1:T(2,128)(2,1)S(1)} %copy.52, ...), kind=kOutput, calls=%fused_computation.12 | convolution fusion | flops 454776832 | bytes 1402880 | tf_op jit(solution)/shard_map/conv_general_dilated | solution.py:95
  125.8 0.3 fusion.50
  126.1 1.1 select_select_fusion
  127.2 3.8 %multiply_convert_fusion = bf16[3,3,3,128,128]{4,3,2,1,0:T(8,128)(2,1)S(1)} fusion(bf16[1,10,10,10,256]{4,0,3,2,1:T(2,128)(2,1)S(1)} %pad_maximum_fusion, bf16[1,8,8,8,128]{4,3,2,1,0:T(8,128)(2,1)S(1)} %bitcast.241), kind=kOutput, calls=%fused_computation.2 | convolution fusion | flops 453869568 | bytes 1527808 | tf_op jit(solution)/shard_map/transpose | solution.py:200
  131.1 2.4 %collective-permute-start.28 = (bf16[864,128]{1,0:T(8,128)(2,1)S(1)}, bf16[864,128]{1,0:T(8,128)(2,1)S(1)}, u32[]{:S(2)}, u32[]{:S(2)}) collective-permute-start(bf16[864,128]{1,0:T(8,128)(2,1)S(1)} %get-tuple-element.30), channel_id=1, source_target_pairs={{0,6},{2,0},{4,2},{6,4},{1,7},{3,1},{5,3},{7,5},{8,14},{10,8},{12,... | collective-permute-start | bytes 663560 | tf_op jit(solution)/shard_map/ppermute | solution.py:135
  133.5 5.2 %collective-permute-done.26 = bf16[864,128]{1,0:T(8,128)(2,1)S(1)} collective-permute-done((bf16[864,128]{1,0:T(8,128)(2,1)S(1)}, bf16[864,128]{1,0:T(8,128)(2,1)S(1)}, u32[]{:S(2)}, u32[]{:S(2)}) %collective-permute-start.26) | collective-permute-done | bytes 221216 | tf_op jit(solution)/shard_map/ppermute | solution.py:135
  138.7 2.3 %collective-permute-done.28 = bf16[864,128]{1,0:T(8,128)(2,1)S(1)} collective-permute-done((bf16[864,128]{1,0:T(8,128)(2,1)S(1)}, bf16[864,128]{1,0:T(8,128)(2,1)S(1)}, u32[]{:S(2)}, u32[]{:S(2)}) %collective-permute-start.28) | collective-permute-done | bytes 221216 | tf_op jit(solution)/shard_map/ppermute | solution.py:135
  141.0 3.1 %collective-permute-done.27 = bf16[864,128]{1,0:T(8,128)(2,1)S(1)} collective-permute-done((bf16[864,128]{1,0:T(8,128)(2,1)S(1)}, bf16[864,128]{1,0:T(8,128)(2,1)S(1)}, u32[]{:S(2)}, u32[]{:S(2)}) %collective-permute-start.27) | collective-permute-done | bytes 221216 | tf_op jit(solution)/shard_map/ppermute | solution.py:135
  144.2 0.6 collective-permute-start.29
  144.8 1.4 collective-permute-done.29
  146.2 0.8 add_bitcast_fusion
  (179 shorter events, 5.3 us)
Async XLA Ops:
  0.6 13.3 %copy-start.2 = (s32[1,1,1,1,27]{4,3,2,1,0:T(1,128)S(1)}, s32[1,1,1,1,27]{4,3,2,1,0:T(1,128)}, u32[]{:S(2)}) copy-start(s32[1,1,1,1,27]{4,3,2,1,0:T(1,128)} %param.8) | copy-start | bytes 328
  0.6 50.0 %collective-permute-start.7 = (bf16[864,128]{1,0:T(8,128)(2,1)}, bf16[864,128]{1,0:T(8,128)(2,1)S(1)}, u32[]{:S(2)}, u32[]{:S(2)}) collective-permute-start(bf16[864,128]{1,0:T(8,128)(2,1)} %bitcast.229), channel_id=1, source_target_pairs={{0,6},{2,0},{4,2},{6,4},{1,7},{3,1},{5,3},{7,5},{8,14},{10,8},{12,... | collective-permute-start | bytes 663560 | tf_op jit(solution)/shard_map/ppermute | solution.py:121
  1.8 48.8 %collective-permute-start.6 = (bf16[864,128]{1,0:T(8,128)(2,1)}, bf16[864,128]{1,0:T(8,128)(2,1)S(1)}, u32[]{:S(2)}, u32[]{:S(2)}) collective-permute-start(bf16[864,128]{1,0:T(8,128)(2,1)} %bitcast.230), channel_id=1, source_target_pairs={{0,4},{2,6},{4,0},{6,2},{1,5},{3,7},{5,1},{7,3},{8,12},{10,14},{12... | collective-permute-start | bytes 663560 | tf_op jit(solution)/shard_map/ppermute | solution.py:121
  3.1 47.5 %collective-permute-start.5 = (bf16[864,128]{1,0:T(8,128)(2,1)}, bf16[864,128]{1,0:T(8,128)(2,1)S(1)}, u32[]{:S(2)}, u32[]{:S(2)}) collective-permute-start(bf16[864,128]{1,0:T(8,128)(2,1)} %bitcast.231), channel_id=1, source_target_pairs={{0,2},{2,4},{4,6},{6,0},{1,3},{3,5},{5,7},{7,1},{8,10},{10,12},{12... | collective-permute-start | bytes 663560 | tf_op jit(solution)/shard_map/ppermute | solution.py:121
  5.1 12.9 %copy-start.1 = (bf16[1,1,1,512,128]{4,3,2,1,0:T(8,128)(2,1)S(1)}, bf16[1,1,1,512,128]{4,3,2,1,0:T(8,128)(2,1)}, u32[]{:S(2)}) copy-start(bf16[1,1,1,512,128]{4,3,2,1,0:T(8,128)(2,1)} %param.7) | copy-start | bytes 393220
  5.9 12.2 %copy-start.5 = (f32[1,128]{1,0:T(1,128)S(1)}, f32[1,128]{1,0:T(1,128)}, u32[]{:S(2)}) copy-start(f32[1,128]{1,0:T(1,128)} %param.10) | copy-start | bytes 1540
  7.8 39.6 %collective-permute-start.1 = (bf16[1,1,8,8,256]{4,3,2,1,0:T(8,128)(2,1)S(1)}, bf16[1,1,8,8,256]{4,3,2,1,0:T(8,128)(2,1)S(1)}, u32[]{:S(2)}, u32[]{:S(2)}) collective-permute-start(bf16[1,1,8,8,256]{4,3,2,1,0:T(8,128)(2,1)S(1)} %fusion.55), channel_id=1, source_target_pairs={{0,2},{1,3},{2,4},{3,5},{4,6},{5,7},{8,10},{9,11},{10,12},{11,13},... | collective-permute-start | bytes 98312 | tf_op jit(solution)/shard_map/ppermute | solution.py:71
  11.2 23.4 %collective-permute-start = (bf16[1,1,1,8,256]{4,3,2,1,0:T(8,128)(2,1)S(1)}, bf16[1,1,1,8,256]{4,3,2,1,0:T(8,128)(2,1)S(1)}, u32[]{:S(2)}, u32[]{:S(2)}) collective-permute-start(bf16[1,1,1,8,256]{4,3,2,1,0:T(8,128)(2,1)S(1)} %constant_dynamic-slice_fusion.14), channel_id=1, source_target_pairs={{0,3},{1,2},{2,5},{3,4},{4,7},{5,6},{8,11},{9,10},{10,13},{11,12},... | collective-permute-start | bytes 12296 | tf_op jit(solution)/shard_map/ppermute | solution.py:71
  34.6 4.9 %collective-permute-start.3 = (bf16[1,1,1,8,256]{4,3,2,1,0:T(8,128)(2,1)S(1)}, bf16[1,1,1,8,256]{4,3,2,1,0:T(8,128)(2,1)S(1)}, u32[]{:S(2)}, u32[]{:S(2)}) collective-permute-start(bf16[1,1,1,8,256]{4,3,2,1,0:T(8,128)(2,1)S(1)} %fusion.59), channel_id=1, source_target_pairs={{2,1},{3,0},{4,3},{5,2},{6,5},{7,4},{10,9},{11,8},{12,11},{13,10},... | collective-permute-start | bytes 12296 | tf_op jit(solution)/shard_map/ppermute | solution.py:71
  39.5 7.1 %collective-permute-start.4 = (bf16[1,1,8,8,256]{4,3,2,1,0:T(8,128)(2,1)S(1)}, bf16[1,1,8,8,256]{4,3,2,1,0:T(8,128)(2,1)S(1)}, u32[]{:S(2)}, u32[]{:S(2)}) collective-permute-start(bf16[1,1,8,8,256]{4,3,2,1,0:T(8,128)(2,1)S(1)} %get-tuple-element.24), channel_id=1, source_target_pairs={{2,0},{3,1},{4,2},{5,3},{6,4},{7,5},{10,8},{11,9},{12,10},{13,11},... | collective-permute-start | bytes 98312 | tf_op jit(solution)/shard_map/ppermute | solution.py:71
  46.6 1.5 %collective-permute-start.2 = (bf16[1,8,1,8,256]{4,3,2,1,0:T(8,128)(2,1)S(1)}, bf16[1,8,1,8,256]{4,3,2,1,0:T(8,128)(2,1)S(1)}, u32[]{:S(2)}, u32[]{:S(2)}) collective-permute-start(bf16[1,8,1,8,256]{4,3,2,1,0:T(8,128)(2,1)S(1)} %fusion.56), channel_id=1, source_target_pairs={{0,1},{1,0},{2,3},{3,2},{4,5},{5,4},{6,7},{7,6},{8,9},{9,8},{10,11... | collective-permute-start | bytes 98312 | tf_op jit(solution)/shard_map/ppermute | solution.py:71
  48.4 2.9 %copy-start.3 = (bf16[1,864,128]{2,1,0:T(8,128)(2,1)S(1)}, bf16[1,864,128]{2,1,0:T(8,128)(2,1)}, u32[]{:S(2)}) copy-start(bf16[1,864,128]{2,1,0:T(8,128)(2,1)} %param.11) | copy-start | bytes 663556
  50.6 0.7 copy-start.4
  54.1 4.1 %copy-start = (bf16[1,1,1,1,512,128]{5,4,3,2,1,0:T(8,128)(2,1)S(1)}, bf16[1,1,1,1,512,128]{5,4,3,2,1,0:T(8,128)(2,1)}, u32[]{:S(2)}) copy-start(bf16[1,1,1,1,512,128]{5,4,3,2,1,0:T(8,128)(2,1)} %param.6) | copy-start | bytes 393220
  59.0 15.5 %collective-permute-start.10 = (bf16[1,1,8,8,128]{4,3,2,1,0:T(8,128)(2,1)S(1)}, bf16[1,1,8,8,128]{4,3,2,1,0:T(8,128)(2,1)S(1)}, u32[]{:S(2)}, u32[]{:S(2)}) collective-permute-start(bf16[1,1,8,8,128]{4,3,2,1,0:T(8,128)(2,1)S(1)} %get-tuple-element.46), channel_id=1, source_target_pairs={{8,2},{9,3},{10,4},{11,5},{12,6},{13,7},{16,10},{17,11},{18,12},{1... | collective-permute-start | bytes 49160 | tf_op jit(solution)/shard_map/ppermute | solution.py:71
  61.0 13.6 %collective-permute-start.13 = (bf16[1,1,8,8,128]{4,3,2,1,0:T(8,128)(2,1)S(1)}, bf16[1,1,8,8,128]{4,3,2,1,0:T(8,128)(2,1)S(1)}, u32[]{:S(2)}, u32[]{:S(2)}) collective-permute-start(bf16[1,1,8,8,128]{4,3,2,1,0:T(8,128)(2,1)S(1)} %get-tuple-element.47), channel_id=1, source_target_pairs={{10,0},{11,1},{12,2},{13,3},{14,4},{15,5},{18,8},{19,9},{20,10},{2... | collective-permute-start | bytes 49160 | tf_op jit(solution)/shard_map/ppermute | solution.py:71
  65.1 6.5 %collective-permute-start.12 = (bf16[1,1,1,8,128]{4,3,2,1,0:T(8,128)(2,1)S(1)}, bf16[1,1,1,8,128]{4,3,2,1,0:T(8,128)(2,1)S(1)}, u32[]{:S(2)}, u32[]{:S(2)}) collective-permute-start(bf16[1,1,1,8,128]{4,3,2,1,0:T(8,128)(2,1)S(1)} %constant_dynamic-slice_fusion.9), channel_id=1, source_target_pairs={{10,1},{11,0},{12,3},{13,2},{14,5},{15,4},{18,9},{19,8},{20,11},{2... | collective-permute-start | bytes 6152 | tf_op jit(solution)/shard_map/ppermute | solution.py:71
  67.5 6.7 %collective-permute-start.9 = (bf16[1,1,1,8,128]{4,3,2,1,0:T(8,128)(2,1)S(1)}, bf16[1,1,1,8,128]{4,3,2,1,0:T(8,128)(2,1)S(1)}, u32[]{:S(2)}, u32[]{:S(2)}) collective-permute-start(bf16[1,1,1,8,128]{4,3,2,1,0:T(8,128)(2,1)S(1)} %constant_dynamic-slice_fusion.11), channel_id=1, source_target_pairs={{8,3},{9,2},{10,5},{11,4},{12,7},{13,6},{16,11},{17,10},{18,13},{1... | collective-permute-start | bytes 6152 | tf_op jit(solution)/shard_map/ppermute | solution.py:71
  69.4 5.1 %collective-permute-start.11 = (bf16[1,8,1,8,128]{4,3,2,1,0:T(8,128)(2,1)S(1)}, bf16[1,8,1,8,128]{4,3,2,1,0:T(8,128)(2,1)S(1)}, u32[]{:S(2)}, u32[]{:S(2)}) collective-permute-start(bf16[1,8,1,8,128]{4,3,2,1,0:T(8,128)(2,1)S(1)} %constant_dynamic-slice_fusion.10), channel_id=1, source_target_pairs={{8,1},{9,0},{10,3},{11,2},{12,5},{13,4},{14,7},{15,6},{16,9},{17,8... | collective-permute-start | bytes 49160 | tf_op jit(solution)/shard_map/ppermute | solution.py:71
  71.6 6.6 %collective-permute-start.8 = (bf16[512,128]{1,0:T(8,128)(2,1)S(1)}, bf16[512,128]{1,0:T(8,128)(2,1)S(1)}, u32[]{:S(2)}, u32[]{:S(2)}) collective-permute-start(bf16[512,128]{1,0:T(8,128)(2,1)S(1)} %fusion.8), channel_id=1, source_target_pairs={{8,0},{16,8},{24,16},{9,1},{17,9},{25,17},{10,2},{18,10},{26,18},{... | collective-permute-start | bytes 393224 | tf_op jit(solution)/shard_map/ppermute | solution.py:197
  82.2 12.0 %collective-permute-start.18 = (bf16[1,1,1,8,128]{4,3,2,1,0:T(8,128)(2,1)S(1)}, bf16[1,1,1,8,128]{4,3,2,1,0:T(8,128)(2,1)S(1)}, u32[]{:S(2)}, u32[]{:S(2)}) collective-permute-start(bf16[1,1,1,8,128]{4,3,2,1,0:T(8,128)(2,1)S(1)} %constant_dynamic-slice_fusion.6), channel_id=1, source_target_pairs={{10,1},{11,0},{12,3},{13,2},{14,5},{15,4},{18,9},{19,8},{20,11},{2... | collective-permute-start | bytes 6152 | tf_op jit(solution)/shard_map/ppermute | solution.py:71
  86.5 14.6 %collective-permute-start.16 = (bf16[1,1,8,8,128]{4,3,2,1,0:T(8,128)(2,1)S(1)}, bf16[1,1,8,8,128]{4,3,2,1,0:T(8,128)(2,1)S(1)}, u32[]{:S(2)}, u32[]{:S(2)}) collective-permute-start(bf16[1,1,8,8,128]{4,3,2,1,0:T(8,128)(2,1)S(1)} %get-tuple-element.41), channel_id=1, source_target_pairs={{8,2},{9,3},{10,4},{11,5},{12,6},{13,7},{16,10},{17,11},{18,12},{1... | collective-permute-start | bytes 49160 | tf_op jit(solution)/shard_map/ppermute | solution.py:71
  88.4 12.8 %collective-permute-start.19 = (bf16[1,1,8,8,128]{4,3,2,1,0:T(8,128)(2,1)S(1)}, bf16[1,1,8,8,128]{4,3,2,1,0:T(8,128)(2,1)S(1)}, u32[]{:S(2)}, u32[]{:S(2)}) collective-permute-start(bf16[1,1,8,8,128]{4,3,2,1,0:T(8,128)(2,1)S(1)} %get-tuple-element.42), channel_id=1, source_target_pairs={{10,0},{11,1},{12,2},{13,3},{14,4},{15,5},{18,8},{19,9},{20,10},{2... | collective-permute-start | bytes 49160 | tf_op jit(solution)/shard_map/ppermute | solution.py:71
  90.3 11.2 %collective-permute-start.14 = (bf16[512,128]{1,0:T(8,128)(2,1)S(1)}, bf16[512,128]{1,0:T(8,128)(2,1)S(1)}, u32[]{:S(2)}, u32[]{:S(2)}) collective-permute-start(bf16[512,128]{1,0:T(8,128)(2,1)S(1)} %fusion.18), channel_id=1, source_target_pairs={{8,0},{16,8},{24,16},{9,1},{17,9},{25,17},{10,2},{18,10},{26,18},{... | collective-permute-start | bytes 393224 | tf_op jit(solution)/shard_map/ppermute | solution.py:197
  92.3 8.7 %collective-permute-start.17 = (bf16[1,8,1,8,128]{4,3,2,1,0:T(8,128)(2,1)S(1)}, bf16[1,8,1,8,128]{4,3,2,1,0:T(8,128)(2,1)S(1)}, u32[]{:S(2)}, u32[]{:S(2)}) collective-permute-start(bf16[1,8,1,8,128]{4,3,2,1,0:T(8,128)(2,1)S(1)} %constant_dynamic-slice_fusion.7), channel_id=1, source_target_pairs={{8,1},{9,0},{10,3},{11,2},{12,5},{13,4},{14,7},{15,6},{16,9},{17,8... | collective-permute-start | bytes 49160 | tf_op jit(solution)/shard_map/ppermute | solution.py:71
  94.2 6.7 %collective-permute-start.15 = (bf16[1,1,1,8,128]{4,3,2,1,0:T(8,128)(2,1)S(1)}, bf16[1,1,1,8,128]{4,3,2,1,0:T(8,128)(2,1)S(1)}, u32[]{:S(2)}, u32[]{:S(2)}) collective-permute-start(bf16[1,1,1,8,128]{4,3,2,1,0:T(8,128)(2,1)S(1)} %constant_dynamic-slice_fusion.8), channel_id=1, source_target_pairs={{8,3},{9,2},{10,5},{11,4},{12,7},{13,6},{16,11},{17,10},{18,13},{1... | collective-permute-start | bytes 6152 | tf_op jit(solution)/shard_map/ppermute | solution.py:71
  105.5 9.7 %collective-permute-start.24 = (bf16[1,1,1,8,128]{4,3,2,1,0:T(8,128)(2,1)S(1)}, bf16[1,1,1,8,128]{4,3,2,1,0:T(8,128)(2,1)S(1)}, u32[]{:S(2)}, u32[]{:S(2)}) collective-permute-start(bf16[1,1,1,8,128]{4,3,2,1,0:T(8,128)(2,1)S(1)} %constant_dynamic-slice_fusion.3), channel_id=1, source_target_pairs={{10,1},{11,0},{12,3},{13,2},{14,5},{15,4},{18,9},{19,8},{20,11},{2... | collective-permute-start | bytes 6152 | tf_op jit(solution)/shard_map/ppermute | solution.py:71
  107.5 14.6 %collective-permute-start.22 = (bf16[1,1,8,8,128]{4,3,2,1,0:T(8,128)(2,1)S(1)}, bf16[1,1,8,8,128]{4,3,2,1,0:T(8,128)(2,1)S(1)}, u32[]{:S(2)}, u32[]{:S(2)}) collective-permute-start(bf16[1,1,8,8,128]{4,3,2,1,0:T(8,128)(2,1)S(1)} %get-tuple-element.36), channel_id=1, source_target_pairs={{8,2},{9,3},{10,4},{11,5},{12,6},{13,7},{16,10},{17,11},{18,12},{1... | collective-permute-start | bytes 49160 | tf_op jit(solution)/shard_map/ppermute | solution.py:71
  109.4 12.8 %collective-permute-start.25 = (bf16[1,1,8,8,128]{4,3,2,1,0:T(8,128)(2,1)S(1)}, bf16[1,1,8,8,128]{4,3,2,1,0:T(8,128)(2,1)S(1)}, u32[]{:S(2)}, u32[]{:S(2)}) collective-permute-start(bf16[1,1,8,8,128]{4,3,2,1,0:T(8,128)(2,1)S(1)} %get-tuple-element.37), channel_id=1, source_target_pairs={{10,0},{11,1},{12,2},{13,3},{14,4},{15,5},{18,8},{19,9},{20,10},{2... | collective-permute-start | bytes 49160 | tf_op jit(solution)/shard_map/ppermute | solution.py:71
  111.3 11.2 %collective-permute-start.20 = (bf16[512,128]{1,0:T(8,128)(2,1)S(1)}, bf16[512,128]{1,0:T(8,128)(2,1)S(1)}, u32[]{:S(2)}, u32[]{:S(2)}) collective-permute-start(bf16[512,128]{1,0:T(8,128)(2,1)S(1)} %fusion.21), channel_id=1, source_target_pairs={{8,0},{16,8},{24,16},{9,1},{17,9},{25,17},{10,2},{18,10},{26,18},{... | collective-permute-start | bytes 393224 | tf_op jit(solution)/shard_map/ppermute | solution.py:197
  113.2 8.8 %collective-permute-start.23 = (bf16[1,8,1,8,128]{4,3,2,1,0:T(8,128)(2,1)S(1)}, bf16[1,8,1,8,128]{4,3,2,1,0:T(8,128)(2,1)S(1)}, u32[]{:S(2)}, u32[]{:S(2)}) collective-permute-start(bf16[1,8,1,8,128]{4,3,2,1,0:T(8,128)(2,1)S(1)} %constant_dynamic-slice_fusion.4), channel_id=1, source_target_pairs={{8,1},{9,0},{10,3},{11,2},{12,5},{13,4},{14,7},{15,6},{16,9},{17,8... | collective-permute-start | bytes 49160 | tf_op jit(solution)/shard_map/ppermute | solution.py:71
  115.2 6.7 %collective-permute-start.21 = (bf16[1,1,1,8,128]{4,3,2,1,0:T(8,128)(2,1)S(1)}, bf16[1,1,1,8,128]{4,3,2,1,0:T(8,128)(2,1)S(1)}, u32[]{:S(2)}, u32[]{:S(2)}) collective-permute-start(bf16[1,1,1,8,128]{4,3,2,1,0:T(8,128)(2,1)S(1)} %constant_dynamic-slice_fusion.5), channel_id=1, source_target_pairs={{8,3},{9,2},{10,5},{11,4},{12,7},{13,6},{16,11},{17,10},{18,13},{1... | collective-permute-start | bytes 6152 | tf_op jit(solution)/shard_map/ppermute | solution.py:71
  131.1 7.6 %collective-permute-start.26 = (bf16[864,128]{1,0:T(8,128)(2,1)S(1)}, bf16[864,128]{1,0:T(8,128)(2,1)S(1)}, u32[]{:S(2)}, u32[]{:S(2)}) collective-permute-start(bf16[864,128]{1,0:T(8,128)(2,1)S(1)} %get-tuple-element.29), channel_id=1, source_target_pairs={{0,2},{2,4},{4,6},{6,0},{1,3},{3,5},{5,7},{7,1},{8,10},{10,12},{12... | collective-permute-start | bytes 663560 | tf_op jit(solution)/shard_map/ppermute | solution.py:135
  131.1 9.9 %collective-permute-start.28 = (bf16[864,128]{1,0:T(8,128)(2,1)S(1)}, bf16[864,128]{1,0:T(8,128)(2,1)S(1)}, u32[]{:S(2)}, u32[]{:S(2)}) collective-permute-start(bf16[864,128]{1,0:T(8,128)(2,1)S(1)} %get-tuple-element.30), channel_id=1, source_target_pairs={{0,6},{2,0},{4,2},{6,4},{1,7},{3,1},{5,3},{7,5},{8,14},{10,8},{12,... | collective-permute-start | bytes 663560 | tf_op jit(solution)/shard_map/ppermute | solution.py:135
  133.5 10.6 %collective-permute-start.27 = (bf16[864,128]{1,0:T(8,128)(2,1)S(1)}, bf16[864,128]{1,0:T(8,128)(2,1)S(1)}, u32[]{:S(2)}, u32[]{:S(2)}) collective-permute-start(bf16[864,128]{1,0:T(8,128)(2,1)S(1)} %get-tuple-element.31), channel_id=1, source_target_pairs={{0,4},{2,6},{4,0},{6,2},{1,5},{3,7},{5,1},{7,3},{8,12},{10,14},{12... | collective-permute-start | bytes 663560 | tf_op jit(solution)/shard_map/ppermute | solution.py:135
  144.2 2.0 %collective-permute-start.29 = (f32[864,128]{1,0:T(8,128)S(1)}, f32[864,128]{1,0:T(8,128)S(1)}, u32[]{:S(2)}, u32[]{:S(2)}) collective-permute-start(f32[864,128]{1,0:T(8,128)S(1)} %convert_add_fusion), channel_id=1, source_target_pairs={{0,1},{1,0},{2,3},{3,2},{4,5},{5,4},{6,7},{7,6},{8,9},{9,8},{10,11... | collective-permute-start | bytes 1327112 | tf_op jit(solution)/shard_map/ppermute | solution.py:207

commit v4 on v3

--- a/solution.py
+++ b/solution.py
@@ -117,8 +117,22 @@
     count = lax.axis_size(axis)
     place = lax.axis_index(axis)
     parts = [shard]
-    for step in range(1, count):
-        parts.append(lax.ppermute(shard, axis, [(i, (i + step) % count) for i in range(count)]))
+    rows = shard.shape[0]
+    if lax.axis_size("sy") == 2 and rows % 2 == 0:
+        half = rows // 2
+        place_y = lax.axis_index("sy")
+        mine = lax.dynamic_slice_in_dim(shard, place_y * half, half, axis=0)
+        fetched = jnp.stack(
+            [lax.ppermute(mine, axis, [(i, (i + step) % count) for i in range(count)]) for step in range(1, count)]
+        )
+        other = lax.ppermute(fetched, "sy", [(0, 1), (1, 0)])
+        low = jnp.where(place_y == 0, fetched, other)
+        high = jnp.where(place_y == 0, other, fetched)
+        remote = jnp.concatenate([low, high], axis=1)
+        parts.extend(remote[step - 1] for step in range(1, count))
+    else:
+        for step in range(1, count):
+            parts.append(lax.ppermute(shard, axis, [(i, (i + step) % count) for i in range(count)]))
     ordered = jnp.stack(parts)
     index = (place - jnp.arange(count)) % count
     slots = jnp.zeros((count,), jnp.int32).at[index].set(jnp.arange(count, dtype=jnp.int32))

time: 148 us -> 148 us (level)
  other arithmetic: 13.8 us -> 12.2 us
  transfers between devices with their start and end apart: 30 -> 31, of which waited for: 12 -> 12; matrix products, arithmetic and copies ran while one was open for 8% -> 8% of each run, Pallas kernels for 0% -> 0%
where the time goes in v4:
time: 148 us; the launch traced here: 147 us
  starting transfers between devices  62.2 us (42%)
  waiting for transfers between devices  27.8 us (19%)
  between operations  19.7 us (13%)
  matrix products  16.9 us (11%)
  other arithmetic  12.2 us (8%)
  local copies, waits for them, and re-layouts  8.11 us (5%)
    ppermute x20, starting transfers between devices, send(): return lax.ppermute(piece, axes, route)  50.5 us
    conv_general_dilated x4, matrix products, conv_data(): lax.conv_general_dilated(padded, filters, (1, 1, 1), 'VALID', dimension_n...  13.2 us
    ppermute x20, waiting for transfers between devices, send(): return lax.ppermute(piece, axes, route)  12.5 us
    ppermute x3, waiting for transfers between devices, scattered_sum(): lax.ppermute(piece, axis, [(i, (i + step) % count) for i in range(count)])  10.6 us
    ppermute x3, starting transfers between devices, shards(): centre = lax.ppermute(result, 'pipe', down)  5.94 us
    transpose x1, matrix products, shards(): per_tap.transpose(1, 2, 3, 0, 4).reshape(taps * channels, channels)  3.77 us
    ppermute x3, waiting for transfers between devices, shards(): centre = lax.ppermute(result, 'pipe', down)  3.3 us
  transfers between devices with their start and end apart: 31, of which 12 were waited for; matrix products, arithmetic and copies ran while one was open for 8% of the time, Pallas kernels for 0%

profile of v4, /device:TPU:21, one launch (start us, length us, event | category | flops | bytes accessed | tf_op | source)
XLA Modules:
  0.0 147.0 jit_solution(2821469576101669929)
XLA Ops:
  0.7 0.9 dynamic-slice_bitcast_fusion
  1.6 1.2 collective-permute-start.7
  2.7 1.2 collective-permute-start.6
  4.0 1.0 fusion.25
  5.0 0.9 convert_element_type.160
  6.8 1.0 broadcast_select_fusion.14
  8.0 3.3 %collective-permute-start.1 = (bf16[1,1,8,8,256]{4,3,2,1,0:T(8,128)(2,1)S(1)}, bf16[1,1,8,8,256]{4,3,2,1,0:T(8,128)(2,1)S(1)}, u32[]{:S(2)}, u32[]{:S(2)}) collective-permute-start(bf16[1,1,8,8,256]{4,3,2,1,0:T(8,128)(2,1)S(1)} %fusion.55), channel_id=1, source_target_pairs={{0,2},{1,3},{2,4},{3,5},{4,6},{5,7},{8,10},{9,11},{10,12},{11,13},... | collective-permute-start | bytes 98312 | tf_op jit(solution)/shard_map/ppermute | solution.py:71
  11.4 2.7 %collective-permute-start = (bf16[1,1,1,8,256]{4,3,2,1,0:T(8,128)(2,1)S(1)}, bf16[1,1,1,8,256]{4,3,2,1,0:T(8,128)(2,1)S(1)}, u32[]{:S(2)}, u32[]{:S(2)}) collective-permute-start(bf16[1,1,1,8,256]{4,3,2,1,0:T(8,128)(2,1)S(1)} %constant_dynamic-slice_fusion.14), channel_id=1, source_target_pairs={{0,3},{1,2},{2,5},{3,4},{4,7},{5,6},{8,11},{9,10},{10,13},{11,12},... | collective-permute-start | bytes 12296 | tf_op jit(solution)/shard_map/ppermute | solution.py:71
  14.1 0.7 fusion.77
  14.8 0.7 fusion.76
  15.6 0.6 scatter_custom_fusion
  18.6 0.4 copy_dynamic-update-slice_fusion
  19.0 0.6 broadcast_select_fusion
  34.7 3.8 %collective-permute-start.3 = (bf16[1,1,1,8,256]{4,3,2,1,0:T(8,128)(2,1)S(1)}, bf16[1,1,1,8,256]{4,3,2,1,0:T(8,128)(2,1)S(1)}, u32[]{:S(2)}, u32[]{:S(2)}) collective-permute-start(bf16[1,1,1,8,256]{4,3,2,1,0:T(8,128)(2,1)S(1)} %fusion.59), channel_id=1, source_target_pairs={{2,1},{3,0},{4,3},{5,2},{6,5},{7,4},{10,9},{11,8},{12,11},{13,10},... | collective-permute-start | bytes 12296 | tf_op jit(solution)/shard_map/ppermute | solution.py:71
  38.5 1.1 collective-permute-done.3
  39.6 6.1 %collective-permute-start.4 = (bf16[1,1,8,8,256]{4,3,2,1,0:T(8,128)(2,1)S(1)}, bf16[1,1,8,8,256]{4,3,2,1,0:T(8,128)(2,1)S(1)}, u32[]{:S(2)}, u32[]{:S(2)}) collective-permute-start(bf16[1,1,8,8,256]{4,3,2,1,0:T(8,128)(2,1)S(1)} %get-tuple-element.24), channel_id=1, source_target_pairs={{2,0},{3,1},{4,2},{5,3},{6,4},{7,5},{10,8},{11,9},{12,10},{13,11},... | collective-permute-start | bytes 98312 | tf_op jit(solution)/shard_map/ppermute | solution.py:71
  45.8 1.0 collective-permute-done.4
  46.7 0.7 collective-permute-start.2
  47.8 0.5 collective-permute-done.2
  48.6 0.4 collective-permute-start.8
  49.1 2.1 %pad_maximum_fusion = bf16[1,10,10,10,256]{4,0,3,2,1:T(2,128)(2,1)S(1)} fusion(bf16[1,1,10,10,256]{4,0,3,2,1:T(2,128)(2,1)S(1)} %copy.33, bf16[1,8,1,10,256]{4,0,3,2,1:T(2,128)(2,1)S(1)} %copy.31, bf16[1,8,8,1,256]{4,0,3,2,1:T(2,128)(2,1)S(1)} %get-tuple-element.35, bf16[1,8,8,8,256]{4,0,3,2,1:T(2,128)(2,1)S(1)} %broadcast_select_fusion, ...), kind=kLoop, calls=%fused_computation.4 | loop fusion | flops 1536000 | bytes 1024000 | tf_op jit(solution)/shard_map/concatenate | solution.py:54
  51.3 0.8 copy-done.2
  52.2 0.7 gather_fusion
  52.9 1.0 rev.3
  53.9 4.1 %fusion.1 = f32[1,8,8,8,128]{4,0,3,2,1:T(1,128)S(1)} fusion(bf16[3,3,3,128,128]{4,3,2,1,0:T(8,128)(2,1)} %rev.3, bf16[1,10,10,10,256]{4,0,3,2,1:T(2,128)(2,1)S(1)} %pad_maximum_fusion), kind=kOutput, calls=%fused_computation.10 | convolution fusion | flops 452984832 | bytes 1658880 | tf_op jit(solution)/shard_map/conv_general_dilated | solution.py:95
  58.0 0.3 fusion.47
  58.8 1.9 %collective-permute-start.11 = (bf16[1,1,8,8,128]{4,3,2,1,0:T(8,128)(2,1)S(1)}, bf16[1,1,8,8,128]{4,3,2,1,0:T(8,128)(2,1)S(1)}, u32[]{:S(2)}, u32[]{:S(2)}) collective-permute-start(bf16[1,1,8,8,128]{4,3,2,1,0:T(8,128)(2,1)S(1)} %get-tuple-element.48), channel_id=1, source_target_pairs={{8,2},{9,3},{10,4},{11,5},{12,6},{13,7},{16,10},{17,11},{18,12},{1... | collective-permute-start | bytes 49160 | tf_op jit(solution)/shard_map/ppermute | solution.py:71
  60.8 4.0 %collective-permute-start.14 = (bf16[1,1,8,8,128]{4,3,2,1,0:T(8,128)(2,1)S(1)}, bf16[1,1,8,8,128]{4,3,2,1,0:T(8,128)(2,1)S(1)}, u32[]{:S(2)}, u32[]{:S(2)}) collective-permute-start(bf16[1,1,8,8,128]{4,3,2,1,0:T(8,128)(2,1)S(1)} %get-tuple-element.49), channel_id=1, source_target_pairs={{10,0},{11,1},{12,2},{13,3},{14,4},{15,5},{18,8},{19,9},{20,10},{2... | collective-permute-start | bytes 49160 | tf_op jit(solution)/shard_map/ppermute | solution.py:71
  64.8 2.2 %collective-permute-start.13 = (bf16[1,1,1,8,128]{4,3,2,1,0:T(8,128)(2,1)S(1)}, bf16[1,1,1,8,128]{4,3,2,1,0:T(8,128)(2,1)S(1)}, u32[]{:S(2)}, u32[]{:S(2)}) collective-permute-start(bf16[1,1,1,8,128]{4,3,2,1,0:T(8,128)(2,1)S(1)} %constant_dynamic-slice_fusion.9), channel_id=1, source_target_pairs={{10,1},{11,0},{12,3},{13,2},{14,5},{15,4},{18,9},{19,8},{20,11},{2... | collective-permute-start | bytes 6152 | tf_op jit(solution)/shard_map/ppermute | solution.py:71
  67.1 1.9 %collective-permute-start.10 = (bf16[1,1,1,8,128]{4,3,2,1,0:T(8,128)(2,1)S(1)}, bf16[1,1,1,8,128]{4,3,2,1,0:T(8,128)(2,1)S(1)}, u32[]{:S(2)}, u32[]{:S(2)}) collective-permute-start(bf16[1,1,1,8,128]{4,3,2,1,0:T(8,128)(2,1)S(1)} %constant_dynamic-slice_fusion.11), channel_id=1, source_target_pairs={{8,3},{9,2},{10,5},{11,4},{12,7},{13,6},{16,11},{17,10},{18,13},{1... | collective-permute-start | bytes 6152 | tf_op jit(solution)/shard_map/ppermute | solution.py:71
  69.0 1.9 %collective-permute-start.12 = (bf16[1,8,1,8,128]{4,3,2,1,0:T(8,128)(2,1)S(1)}, bf16[1,8,1,8,128]{4,3,2,1,0:T(8,128)(2,1)S(1)}, u32[]{:S(2)}, u32[]{:S(2)}) collective-permute-start(bf16[1,8,1,8,128]{4,3,2,1,0:T(8,128)(2,1)S(1)} %constant_dynamic-slice_fusion.10), channel_id=1, source_target_pairs={{8,1},{9,0},{10,3},{11,2},{12,5},{13,4},{14,7},{15,6},{16,9},{17,8... | collective-permute-start | bytes 49160 | tf_op jit(solution)/shard_map/ppermute | solution.py:71
  71.3 2.1 %collective-permute-start.9 = (bf16[512,128]{1,0:T(8,128)(2,1)S(1)}, bf16[512,128]{1,0:T(8,128)(2,1)S(1)}, u32[]{:S(2)}, u32[]{:S(2)}) collective-permute-start(bf16[512,128]{1,0:T(8,128)(2,1)S(1)} %fusion.8), channel_id=1, source_target_pairs={{8,0},{16,8},{24,16},{9,1},{17,9},{25,17},{10,2},{18,10},{26,18},{... | collective-permute-start | bytes 393224 | tf_op jit(solution)/shard_map/ppermute | solution.py:211
  73.4 0.4 collective-permute-done.10
  74.5 3.3 %collective-permute-done.9 = bf16[512,128]{1,0:T(8,128)(2,1)S(1)} collective-permute-done((bf16[512,128]{1,0:T(8,128)(2,1)S(1)}, bf16[512,128]{1,0:T(8,128)(2,1)S(1)}, u32[]{:S(2)}, u32[]{:S(2)}) %collective-permute-start.9) | collective-permute-done | bytes 131104 | tf_op jit(solution)/shard_map/ppermute | solution.py:211
  78.2 3.0 %fusion.5 = f32[1,8,8,8,128]{4,0,3,2,1:T(1,128)S(1)} fusion(bf16[3,3,3,128,128]{4,3,2,1,0:T(8,128)(2,1)S(1)} %bitcast.204, bf16[1,1,10,10,128]{4,0,3,2,1:T(2,128)(2,1)S(1)} %copy.42, bf16[1,8,1,10,128]{4,0,3,2,1:T(2,128)(2,1)S(1)} %copy.40, bf16[1,8,8,1,128]{4,0,3,2,1:T(2,128)(2,1)S(1)} %slice_bitcast_fusion.4, bf16[1,8,8,8,128]{4,0,3,2,1:T(2,128)(2,1)S(1)} %copy.38, ...), kind=kOutput, calls=%fused_computation.14 | convolution fusion | flops 454776832 | bytes 1402880 | tf_op jit(solution)/shard_map/conv_general_dilated | solution.py:95
  81.2 0.3 fusion.48
  81.5 0.3 fusion.18
  81.9 4.4 %collective-permute-start.19 = (bf16[1,1,1,8,128]{4,3,2,1,0:T(8,128)(2,1)S(1)}, bf16[1,1,1,8,128]{4,3,2,1,0:T(8,128)(2,1)S(1)}, u32[]{:S(2)}, u32[]{:S(2)}) collective-permute-start(bf16[1,1,1,8,128]{4,3,2,1,0:T(8,128)(2,1)S(1)} %constant_dynamic-slice_fusion.6), channel_id=1, source_target_pairs={{10,1},{11,0},{12,3},{13,2},{14,5},{15,4},{18,9},{19,8},{20,11},{2... | collective-permute-start | bytes 6152 | tf_op jit(solution)/shard_map/ppermute | solution.py:71
  86.4 1.9 %collective-permute-start.17 = (bf16[1,1,8,8,128]{4,3,2,1,0:T(8,128)(2,1)S(1)}, bf16[1,1,8,8,128]{4,3,2,1,0:T(8,128)(2,1)S(1)}, u32[]{:S(2)}, u32[]{:S(2)}) collective-permute-start(bf16[1,1,8,8,128]{4,3,2,1,0:T(8,128)(2,1)S(1)} %get-tuple-element.43), channel_id=1, source_target_pairs={{8,2},{9,3},{10,4},{11,5},{12,6},{13,7},{16,10},{17,11},{18,12},{1... | collective-permute-start | bytes 49160 | tf_op jit(solution)/shard_map/ppermute | solution.py:71
  88.3 1.9 %collective-permute-start.20 = (bf16[1,1,8,8,128]{4,3,2,1,0:T(8,128)(2,1)S(1)}, bf16[1,1,8,8,128]{4,3,2,1,0:T(8,128)(2,1)S(1)}, u32[]{:S(2)}, u32[]{:S(2)}) collective-permute-start(bf16[1,1,8,8,128]{4,3,2,1,0:T(8,128)(2,1)S(1)} %get-tuple-element.44), channel_id=1, source_target_pairs={{10,0},{11,1},{12,2},{13,3},{14,4},{15,5},{18,8},{19,9},{20,10},{2... | collective-permute-start | bytes 49160 | tf_op jit(solution)/shard_map/ppermute | solution.py:71
  90.2 1.9 %collective-permute-start.15 = (bf16[512,128]{1,0:T(8,128)(2,1)S(1)}, bf16[512,128]{1,0:T(8,128)(2,1)S(1)}, u32[]{:S(2)}, u32[]{:S(2)}) collective-permute-start(bf16[512,128]{1,0:T(8,128)(2,1)S(1)} %fusion.18), channel_id=1, source_target_pairs={{8,0},{16,8},{24,16},{9,1},{17,9},{25,17},{10,2},{18,10},{26,18},{... | collective-permute-start | bytes 393224 | tf_op jit(solution)/shard_map/ppermute | solution.py:211
  92.1 1.9 %collective-permute-start.18 = (bf16[1,8,1,8,128]{4,3,2,1,0:T(8,128)(2,1)S(1)}, bf16[1,8,1,8,128]{4,3,2,1,0:T(8,128)(2,1)S(1)}, u32[]{:S(2)}, u32[]{:S(2)}) collective-permute-start(bf16[1,8,1,8,128]{4,3,2,1,0:T(8,128)(2,1)S(1)} %constant_dynamic-slice_fusion.7), channel_id=1, source_target_pairs={{8,1},{9,0},{10,3},{11,2},{12,5},{13,4},{14,7},{15,6},{16,9},{17,8... | collective-permute-start | bytes 49160 | tf_op jit(solution)/shard_map/ppermute | solution.py:71
  94.1 1.9 %collective-permute-start.16 = (bf16[1,1,1,8,128]{4,3,2,1,0:T(8,128)(2,1)S(1)}, bf16[1,1,1,8,128]{4,3,2,1,0:T(8,128)(2,1)S(1)}, u32[]{:S(2)}, u32[]{:S(2)}) collective-permute-start(bf16[1,1,1,8,128]{4,3,2,1,0:T(8,128)(2,1)S(1)} %constant_dynamic-slice_fusion.8), channel_id=1, source_target_pairs={{8,3},{9,2},{10,5},{11,4},{12,7},{13,6},{16,11},{17,10},{18,13},{1... | collective-permute-start | bytes 6152 | tf_op jit(solution)/shard_map/ppermute | solution.py:71
  96.0 4.8 %collective-permute-done.16 = bf16[1,1,1,8,128]{4,3,2,1,0:T(8,128)(2,1)S(1)} collective-permute-done((bf16[1,1,1,8,128]{4,3,2,1,0:T(8,128)(2,1)S(1)}, bf16[1,1,1,8,128]{4,3,2,1,0:T(8,128)(2,1)S(1)}, u32[]{:S(2)}, u32[]{:S(2)}) %collective-permute-start.16) | collective-permute-done | bytes 2080 | tf_op jit(solution)/shard_map/ppermute | solution.py:71
  101.7 3.0 %fusion.4 = f32[1,8,8,8,128]{4,0,3,2,1:T(1,128)S(1)} fusion(bf16[3,3,3,128,128]{4,3,2,1,0:T(8,128)(2,1)S(1)} %bitcast.205, bf16[1,1,10,10,128]{4,0,3,2,1:T(2,128)(2,1)S(1)} %copy.49, bf16[1,8,1,10,128]{4,0,3,2,1:T(2,128)(2,1)S(1)} %copy.47, bf16[1,8,8,1,128]{4,0,3,2,1:T(2,128)(2,1)S(1)} %slice_bitcast_fusion.2, bf16[1,8,8,8,128]{4,0,3,2,1:T(2,128)(2,1)S(1)} %copy.45, ...), kind=kOutput, calls=%fused_computation.13 | convolution fusion | flops 454776832 | bytes 1402880 | tf_op jit(solution)/shard_map/conv_general_dilated | solution.py:95
  104.8 0.3 fusion.49
  105.5 1.9 %collective-permute-start.25 = (bf16[1,1,1,8,128]{4,3,2,1,0:T(8,128)(2,1)S(1)}, bf16[1,1,1,8,128]{4,3,2,1,0:T(8,128)(2,1)S(1)}, u32[]{:S(2)}, u32[]{:S(2)}) collective-permute-start(bf16[1,1,1,8,128]{4,3,2,1,0:T(8,128)(2,1)S(1)} %constant_dynamic-slice_fusion.3), channel_id=1, source_target_pairs={{10,1},{11,0},{12,3},{13,2},{14,5},{15,4},{18,9},{19,8},{20,11},{2... | collective-permute-start | bytes 6152 | tf_op jit(solution)/shard_map/ppermute | solution.py:71
  107.4 1.9 %collective-permute-start.23 = (bf16[1,1,8,8,128]{4,3,2,1,0:T(8,128)(2,1)S(1)}, bf16[1,1,8,8,128]{4,3,2,1,0:T(8,128)(2,1)S(1)}, u32[]{:S(2)}, u32[]{:S(2)}) collective-permute-start(bf16[1,1,8,8,128]{4,3,2,1,0:T(8,128)(2,1)S(1)} %get-tuple-element.38), channel_id=1, source_target_pairs={{8,2},{9,3},{10,4},{11,5},{12,6},{13,7},{16,10},{17,11},{18,12},{1... | collective-permute-start | bytes 49160 | tf_op jit(solution)/shard_map/ppermute | solution.py:71
  109.3 1.9 %collective-permute-start.26 = (bf16[1,1,8,8,128]{4,3,2,1,0:T(8,128)(2,1)S(1)}, bf16[1,1,8,8,128]{4,3,2,1,0:T(8,128)(2,1)S(1)}, u32[]{:S(2)}, u32[]{:S(2)}) collective-permute-start(bf16[1,1,8,8,128]{4,3,2,1,0:T(8,128)(2,1)S(1)} %get-tuple-element.39), channel_id=1, source_target_pairs={{10,0},{11,1},{12,2},{13,3},{14,4},{15,5},{18,8},{19,9},{20,10},{2... | collective-permute-start | bytes 49160 | tf_op jit(solution)/shard_map/ppermute | solution.py:71
  111.3 1.9 %collective-permute-start.21 = (bf16[512,128]{1,0:T(8,128)(2,1)S(1)}, bf16[512,128]{1,0:T(8,128)(2,1)S(1)}, u32[]{:S(2)}, u32[]{:S(2)}) collective-permute-start(bf16[512,128]{1,0:T(8,128)(2,1)S(1)} %fusion.21), channel_id=1, source_target_pairs={{8,0},{16,8},{24,16},{9,1},{17,9},{25,17},{10,2},{18,10},{26,18},{... | collective-permute-start | bytes 393224 | tf_op jit(solution)/shard_map/ppermute | solution.py:211
  113.2 1.9 %collective-permute-start.24 = (bf16[1,8,1,8,128]{4,3,2,1,0:T(8,128)(2,1)S(1)}, bf16[1,8,1,8,128]{4,3,2,1,0:T(8,128)(2,1)S(1)}, u32[]{:S(2)}, u32[]{:S(2)}) collective-permute-start(bf16[1,8,1,8,128]{4,3,2,1,0:T(8,128)(2,1)S(1)} %constant_dynamic-slice_fusion.4), channel_id=1, source_target_pairs={{8,1},{9,0},{10,3},{11,2},{12,5},{13,4},{14,7},{15,6},{16,9},{17,8... | collective-permute-start | bytes 49160 | tf_op jit(solution)/shard_map/ppermute | solution.py:71
  115.1 2.1 %collective-permute-start.22 = (bf16[1,1,1,8,128]{4,3,2,1,0:T(8,128)(2,1)S(1)}, bf16[1,1,1,8,128]{4,3,2,1,0:T(8,128)(2,1)S(1)}, u32[]{:S(2)}, u32[]{:S(2)}) collective-permute-start(bf16[1,1,1,8,128]{4,3,2,1,0:T(8,128)(2,1)S(1)} %constant_dynamic-slice_fusion.5), channel_id=1, source_target_pairs={{8,3},{9,2},{10,5},{11,4},{12,7},{13,6},{16,11},{17,10},{18,13},{1... | collective-permute-start | bytes 6152 | tf_op jit(solution)/shard_map/ppermute | solution.py:71
  117.3 4.5 %collective-permute-done.22 = bf16[1,1,1,8,128]{4,3,2,1,0:T(8,128)(2,1)S(1)} collective-permute-done((bf16[1,1,1,8,128]{4,3,2,1,0:T(8,128)(2,1)S(1)}, bf16[1,1,1,8,128]{4,3,2,1,0:T(8,128)(2,1)S(1)}, u32[]{:S(2)}, u32[]{:S(2)}) %collective-permute-start.22) | collective-permute-done | bytes 2080 | tf_op jit(solution)/shard_map/ppermute | solution.py:71
  122.8 3.0 %fusion.3 = f32[1,8,8,8,128]{4,0,3,2,1:T(1,128)S(1)} fusion(bf16[3,3,3,128,128]{4,3,2,1,0:T(8,128)(2,1)S(1)} %bitcast.206, bf16[1,1,10,10,128]{4,0,3,2,1:T(2,128)(2,1)S(1)} %copy.56, bf16[1,8,1,10,128]{4,0,3,2,1:T(2,128)(2,1)S(1)} %copy.54, bf16[1,8,8,1,128]{4,0,3,2,1:T(2,128)(2,1)S(1)} %slice_bitcast_fusion, bf16[1,8,8,8,128]{4,0,3,2,1:T(2,128)(2,1)S(1)} %copy.52, ...), kind=kOutput, calls=%fused_computation.12 | convolution fusion | flops 454776832 | bytes 1402880 | tf_op jit(solution)/shard_map/conv_general_dilated | solution.py:95
  125.8 0.3 fusion.50
  126.1 1.1 select_select_fusion
  127.2 3.8 %multiply_convert_fusion = bf16[3,3,3,128,128]{4,3,2,1,0:T(8,128)(2,1)S(1)} fusion(bf16[1,10,10,10,256]{4,0,3,2,1:T(2,128)(2,1)S(1)} %pad_maximum_fusion, bf16[1,8,8,8,128]{4,3,2,1,0:T(8,128)(2,1)S(1)} %bitcast.242), kind=kOutput, calls=%fused_computation.2 | convolution fusion | flops 453869568 | bytes 1527808 | tf_op jit(solution)/shard_map/transpose | solution.py:214
  131.1 2.4 %collective-permute-start.29 = (bf16[864,128]{1,0:T(8,128)(2,1)S(1)}, bf16[864,128]{1,0:T(8,128)(2,1)S(1)}, u32[]{:S(2)}, u32[]{:S(2)}) collective-permute-start(bf16[864,128]{1,0:T(8,128)(2,1)S(1)} %get-tuple-element.30), channel_id=1, source_target_pairs={{0,6},{2,0},{4,2},{6,4},{1,7},{3,1},{5,3},{7,5},{8,14},{10,8},{12,... | collective-permute-start | bytes 663560 | tf_op jit(solution)/shard_map/ppermute | solution.py:149
  133.5 5.2 %collective-permute-done.27 = bf16[864,128]{1,0:T(8,128)(2,1)S(1)} collective-permute-done((bf16[864,128]{1,0:T(8,128)(2,1)S(1)}, bf16[864,128]{1,0:T(8,128)(2,1)S(1)}, u32[]{:S(2)}, u32[]{:S(2)}) %collective-permute-start.27) | collective-permute-done | bytes 221216 | tf_op jit(solution)/shard_map/ppermute | solution.py:149
  138.7 2.2 %collective-permute-done.29 = bf16[864,128]{1,0:T(8,128)(2,1)S(1)} collective-permute-done((bf16[864,128]{1,0:T(8,128)(2,1)S(1)}, bf16[864,128]{1,0:T(8,128)(2,1)S(1)}, u32[]{:S(2)}, u32[]{:S(2)}) %collective-permute-start.29) | collective-permute-done | bytes 221216 | tf_op jit(solution)/shard_map/ppermute | solution.py:149
  140.9 3.2 %collective-permute-done.28 = bf16[864,128]{1,0:T(8,128)(2,1)S(1)} collective-permute-done((bf16[864,128]{1,0:T(8,128)(2,1)S(1)}, bf16[864,128]{1,0:T(8,128)(2,1)S(1)}, u32[]{:S(2)}, u32[]{:S(2)}) %collective-permute-start.28) | collective-permute-done | bytes 221216 | tf_op jit(solution)/shard_map/ppermute | solution.py:149
  144.2 0.6 collective-permute-start.30
  144.8 1.4 collective-permute-done.30
  146.2 0.8 add_bitcast_fusion
  (182 shorter events, 5.6 us)
Async XLA Ops:
  0.6 7.2 %copy-start.4 = (f32[1,128]{1,0:T(1,128)S(1)}, f32[1,128]{1,0:T(1,128)}, u32[]{:S(2)}) copy-start(f32[1,128]{1,0:T(1,128)} %param.10) | copy-start | bytes 1540
  0.6 13.5 %copy-start.3 = (s32[1,1,1,1,27]{4,3,2,1,0:T(1,128)S(1)}, s32[1,1,1,1,27]{4,3,2,1,0:T(1,128)}, u32[]{:S(2)}) copy-start(s32[1,1,1,1,27]{4,3,2,1,0:T(1,128)} %param.8) | copy-start | bytes 328
  1.6 47.0 %collective-permute-start.7 = (bf16[432,128]{1,0:T(8,128)(2,1)S(1)}, bf16[432,128]{1,0:T(8,128)(2,1)S(1)}, u32[]{:S(2)}, u32[]{:S(2)}) collective-permute-start(bf16[432,128]{1,0:T(8,128)(2,1)S(1)} %dynamic-slice_bitcast_fusion), channel_id=1, source_target_pairs={{0,6},{2,0},{4,2},{6,4},{1,7},{3,1},{5,3},{7,5},{8,14},{10,8},{12,... | collective-permute-start | bytes 331784 | tf_op jit(solution)/shard_map/ppermute | solution.py:126
  2.7 45.9 %collective-permute-start.6 = (bf16[432,128]{1,0:T(8,128)(2,1)S(1)}, bf16[432,128]{1,0:T(8,128)(2,1)S(1)}, u32[]{:S(2)}, u32[]{:S(2)}) collective-permute-start(bf16[432,128]{1,0:T(8,128)(2,1)S(1)} %dynamic-slice_bitcast_fusion), channel_id=1, source_target_pairs={{0,4},{2,6},{4,0},{6,2},{1,5},{3,7},{5,1},{7,3},{8,12},{10,14},{12... | collective-permute-start | bytes 331784 | tf_op jit(solution)/shard_map/ppermute | solution.py:126
  4.0 44.6 %collective-permute-start.5 = (bf16[432,128]{1,0:T(8,128)(2,1)S(1)}, bf16[432,128]{1,0:T(8,128)(2,1)S(1)}, u32[]{:S(2)}, u32[]{:S(2)}) collective-permute-start(bf16[432,128]{1,0:T(8,128)(2,1)S(1)} %dynamic-slice_bitcast_fusion), channel_id=1, source_target_pairs={{0,2},{2,4},{4,6},{6,0},{1,3},{3,5},{5,7},{7,1},{8,10},{10,12},{12... | collective-permute-start | bytes 331784 | tf_op jit(solution)/shard_map/ppermute | solution.py:126
  5.9 12.1 %copy-start.1 = (bf16[1,1,1,512,128]{4,3,2,1,0:T(8,128)(2,1)S(1)}, bf16[1,1,1,512,128]{4,3,2,1,0:T(8,128)(2,1)}, u32[]{:S(2)}) copy-start(bf16[1,1,1,512,128]{4,3,2,1,0:T(8,128)(2,1)} %param.7) | copy-start | bytes 393220
  8.0 39.5 %collective-permute-start.1 = (bf16[1,1,8,8,256]{4,3,2,1,0:T(8,128)(2,1)S(1)}, bf16[1,1,8,8,256]{4,3,2,1,0:T(8,128)(2,1)S(1)}, u32[]{:S(2)}, u32[]{:S(2)}) collective-permute-start(bf16[1,1,8,8,256]{4,3,2,1,0:T(8,128)(2,1)S(1)} %fusion.55), channel_id=1, source_target_pairs={{0,2},{1,3},{2,4},{3,5},{4,6},{5,7},{8,10},{9,11},{10,12},{11,13},... | collective-permute-start | bytes 98312 | tf_op jit(solution)/shard_map/ppermute | solution.py:71
  11.4 23.3 %collective-permute-start = (bf16[1,1,1,8,256]{4,3,2,1,0:T(8,128)(2,1)S(1)}, bf16[1,1,1,8,256]{4,3,2,1,0:T(8,128)(2,1)S(1)}, u32[]{:S(2)}, u32[]{:S(2)}) collective-permute-start(bf16[1,1,1,8,256]{4,3,2,1,0:T(8,128)(2,1)S(1)} %constant_dynamic-slice_fusion.14), channel_id=1, source_target_pairs={{0,3},{1,2},{2,5},{3,4},{4,7},{5,6},{8,11},{9,10},{10,13},{11,12},... | collective-permute-start | bytes 12296 | tf_op jit(solution)/shard_map/ppermute | solution.py:71
  34.7 4.9 %collective-permute-start.3 = (bf16[1,1,1,8,256]{4,3,2,1,0:T(8,128)(2,1)S(1)}, bf16[1,1,1,8,256]{4,3,2,1,0:T(8,128)(2,1)S(1)}, u32[]{:S(2)}, u32[]{:S(2)}) collective-permute-start(bf16[1,1,1,8,256]{4,3,2,1,0:T(8,128)(2,1)S(1)} %fusion.59), channel_id=1, source_target_pairs={{2,1},{3,0},{4,3},{5,2},{6,5},{7,4},{10,9},{11,8},{12,11},{13,10},... | collective-permute-start | bytes 12296 | tf_op jit(solution)/shard_map/ppermute | solution.py:71
  39.6 7.1 %collective-permute-start.4 = (bf16[1,1,8,8,256]{4,3,2,1,0:T(8,128)(2,1)S(1)}, bf16[1,1,8,8,256]{4,3,2,1,0:T(8,128)(2,1)S(1)}, u32[]{:S(2)}, u32[]{:S(2)}) collective-permute-start(bf16[1,1,8,8,256]{4,3,2,1,0:T(8,128)(2,1)S(1)} %get-tuple-element.24), channel_id=1, source_target_pairs={{2,0},{3,1},{4,2},{5,3},{6,4},{7,5},{10,8},{11,9},{12,10},{13,11},... | collective-permute-start | bytes 98312 | tf_op jit(solution)/shard_map/ppermute | solution.py:71
  46.7 1.5 %collective-permute-start.2 = (bf16[1,8,1,8,256]{4,3,2,1,0:T(8,128)(2,1)S(1)}, bf16[1,8,1,8,256]{4,3,2,1,0:T(8,128)(2,1)S(1)}, u32[]{:S(2)}, u32[]{:S(2)}) collective-permute-start(bf16[1,8,1,8,256]{4,3,2,1,0:T(8,128)(2,1)S(1)} %fusion.56), channel_id=1, source_target_pairs={{0,1},{1,0},{2,3},{3,2},{4,5},{5,4},{6,7},{7,6},{8,9},{9,8},{10,11... | collective-permute-start | bytes 98312 | tf_op jit(solution)/shard_map/ppermute | solution.py:71
  48.6 2.5 %collective-permute-start.8 = (bf16[3,432,128]{2,1,0:T(8,128)(2,1)S(1)}, bf16[3,432,128]{2,1,0:T(8,128)(2,1)S(1)}, u32[]{:S(2)}, u32[]{:S(2)}) collective-permute-start(bf16[3,432,128]{2,1,0:T(8,128)(2,1)S(1)} %pad_maximum_fusion.7), channel_id=1, source_target_pairs={{0,1},{1,0},{2,3},{3,2},{4,5},{5,4},{6,7},{7,6},{8,9},{9,8},{10,11... | collective-permute-start | bytes 995336 | tf_op jit(solution)/shard_map/ppermute | solution.py:128
  51.2 0.9 copy-start.2
  53.9 4.1 %copy-start = (bf16[1,1,1,1,512,128]{5,4,3,2,1,0:T(8,128)(2,1)S(1)}, bf16[1,1,1,1,512,128]{5,4,3,2,1,0:T(8,128)(2,1)}, u32[]{:S(2)}) copy-start(bf16[1,1,1,1,512,128]{5,4,3,2,1,0:T(8,128)(2,1)} %param.6) | copy-start | bytes 393220
  58.8 15.3 %collective-permute-start.11 = (bf16[1,1,8,8,128]{4,3,2,1,0:T(8,128)(2,1)S(1)}, bf16[1,1,8,8,128]{4,3,2,1,0:T(8,128)(2,1)S(1)}, u32[]{:S(2)}, u32[]{:S(2)}) collective-permute-start(bf16[1,1,8,8,128]{4,3,2,1,0:T(8,128)(2,1)S(1)} %get-tuple-element.48), channel_id=1, source_target_pairs={{8,2},{9,3},{10,4},{11,5},{12,6},{13,7},{16,10},{17,11},{18,12},{1... | collective-permute-start | bytes 49160 | tf_op jit(solution)/shard_map/ppermute | solution.py:71
  60.8 13.4 %collective-permute-start.14 = (bf16[1,1,8,8,128]{4,3,2,1,0:T(8,128)(2,1)S(1)}, bf16[1,1,8,8,128]{4,3,2,1,0:T(8,128)(2,1)S(1)}, u32[]{:S(2)}, u32[]{:S(2)}) collective-permute-start(bf16[1,1,8,8,128]{4,3,2,1,0:T(8,128)(2,1)S(1)} %get-tuple-element.49), channel_id=1, source_target_pairs={{10,0},{11,1},{12,2},{13,3},{14,4},{15,5},{18,8},{19,9},{20,10},{2... | collective-permute-start | bytes 49160 | tf_op jit(solution)/shard_map/ppermute | solution.py:71
  64.8 6.4 %collective-permute-start.13 = (bf16[1,1,1,8,128]{4,3,2,1,0:T(8,128)(2,1)S(1)}, bf16[1,1,1,8,128]{4,3,2,1,0:T(8,128)(2,1)S(1)}, u32[]{:S(2)}, u32[]{:S(2)}) collective-permute-start(bf16[1,1,1,8,128]{4,3,2,1,0:T(8,128)(2,1)S(1)} %constant_dynamic-slice_fusion.9), channel_id=1, source_target_pairs={{10,1},{11,0},{12,3},{13,2},{14,5},{15,4},{18,9},{19,8},{20,11},{2... | collective-permute-start | bytes 6152 | tf_op jit(solution)/shard_map/ppermute | solution.py:71
  67.1 6.7 %collective-permute-start.10 = (bf16[1,1,1,8,128]{4,3,2,1,0:T(8,128)(2,1)S(1)}, bf16[1,1,1,8,128]{4,3,2,1,0:T(8,128)(2,1)S(1)}, u32[]{:S(2)}, u32[]{:S(2)}) collective-permute-start(bf16[1,1,1,8,128]{4,3,2,1,0:T(8,128)(2,1)S(1)} %constant_dynamic-slice_fusion.11), channel_id=1, source_target_pairs={{8,3},{9,2},{10,5},{11,4},{12,7},{13,6},{16,11},{17,10},{18,13},{1... | collective-permute-start | bytes 6152 | tf_op jit(solution)/shard_map/ppermute | solution.py:71
  69.0 5.1 %collective-permute-start.12 = (bf16[1,8,1,8,128]{4,3,2,1,0:T(8,128)(2,1)S(1)}, bf16[1,8,1,8,128]{4,3,2,1,0:T(8,128)(2,1)S(1)}, u32[]{:S(2)}, u32[]{:S(2)}) collective-permute-start(bf16[1,8,1,8,128]{4,3,2,1,0:T(8,128)(2,1)S(1)} %constant_dynamic-slice_fusion.10), channel_id=1, source_target_pairs={{8,1},{9,0},{10,3},{11,2},{12,5},{13,4},{14,7},{15,6},{16,9},{17,8... | collective-permute-start | bytes 49160 | tf_op jit(solution)/shard_map/ppermute | solution.py:71
  71.3 6.6 %collective-permute-start.9 = (bf16[512,128]{1,0:T(8,128)(2,1)S(1)}, bf16[512,128]{1,0:T(8,128)(2,1)S(1)}, u32[]{:S(2)}, u32[]{:S(2)}) collective-permute-start(bf16[512,128]{1,0:T(8,128)(2,1)S(1)} %fusion.8), channel_id=1, source_target_pairs={{8,0},{16,8},{24,16},{9,1},{17,9},{25,17},{10,2},{18,10},{26,18},{... | collective-permute-start | bytes 393224 | tf_op jit(solution)/shard_map/ppermute | solution.py:211
  81.9 12.2 %collective-permute-start.19 = (bf16[1,1,1,8,128]{4,3,2,1,0:T(8,128)(2,1)S(1)}, bf16[1,1,1,8,128]{4,3,2,1,0:T(8,128)(2,1)S(1)}, u32[]{:S(2)}, u32[]{:S(2)}) collective-permute-start(bf16[1,1,1,8,128]{4,3,2,1,0:T(8,128)(2,1)S(1)} %constant_dynamic-slice_fusion.6), channel_id=1, source_target_pairs={{10,1},{11,0},{12,3},{13,2},{14,5},{15,4},{18,9},{19,8},{20,11},{2... | collective-permute-start | bytes 6152 | tf_op jit(solution)/shard_map/ppermute | solution.py:71
  86.4 14.6 %collective-permute-start.17 = (bf16[1,1,8,8,128]{4,3,2,1,0:T(8,128)(2,1)S(1)}, bf16[1,1,8,8,128]{4,3,2,1,0:T(8,128)(2,1)S(1)}, u32[]{:S(2)}, u32[]{:S(2)}) collective-permute-start(bf16[1,1,8,8,128]{4,3,2,1,0:T(8,128)(2,1)S(1)} %get-tuple-element.43), channel_id=1, source_target_pairs={{8,2},{9,3},{10,4},{11,5},{12,6},{13,7},{16,10},{17,11},{18,12},{1... | collective-permute-start | bytes 49160 | tf_op jit(solution)/shard_map/ppermute | solution.py:71
  88.3 12.8 %collective-permute-start.20 = (bf16[1,1,8,8,128]{4,3,2,1,0:T(8,128)(2,1)S(1)}, bf16[1,1,8,8,128]{4,3,2,1,0:T(8,128)(2,1)S(1)}, u32[]{:S(2)}, u32[]{:S(2)}) collective-permute-start(bf16[1,1,8,8,128]{4,3,2,1,0:T(8,128)(2,1)S(1)} %get-tuple-element.44), channel_id=1, source_target_pairs={{10,0},{11,1},{12,2},{13,3},{14,4},{15,5},{18,8},{19,9},{20,10},{2... | collective-permute-start | bytes 49160 | tf_op jit(solution)/shard_map/ppermute | solution.py:71
  90.2 11.2 %collective-permute-start.15 = (bf16[512,128]{1,0:T(8,128)(2,1)S(1)}, bf16[512,128]{1,0:T(8,128)(2,1)S(1)}, u32[]{:S(2)}, u32[]{:S(2)}) collective-permute-start(bf16[512,128]{1,0:T(8,128)(2,1)S(1)} %fusion.18), channel_id=1, source_target_pairs={{8,0},{16,8},{24,16},{9,1},{17,9},{25,17},{10,2},{18,10},{26,18},{... | collective-permute-start | bytes 393224 | tf_op jit(solution)/shard_map/ppermute | solution.py:211
  92.1 8.7 %collective-permute-start.18 = (bf16[1,8,1,8,128]{4,3,2,1,0:T(8,128)(2,1)S(1)}, bf16[1,8,1,8,128]{4,3,2,1,0:T(8,128)(2,1)S(1)}, u32[]{:S(2)}, u32[]{:S(2)}) collective-permute-start(bf16[1,8,1,8,128]{4,3,2,1,0:T(8,128)(2,1)S(1)} %constant_dynamic-slice_fusion.7), channel_id=1, source_target_pairs={{8,1},{9,0},{10,3},{11,2},{12,5},{13,4},{14,7},{15,6},{16,9},{17,8... | collective-permute-start | bytes 49160 | tf_op jit(solution)/shard_map/ppermute | solution.py:71
  94.1 6.7 %collective-permute-start.16 = (bf16[1,1,1,8,128]{4,3,2,1,0:T(8,128)(2,1)S(1)}, bf16[1,1,1,8,128]{4,3,2,1,0:T(8,128)(2,1)S(1)}, u32[]{:S(2)}, u32[]{:S(2)}) collective-permute-start(bf16[1,1,1,8,128]{4,3,2,1,0:T(8,128)(2,1)S(1)} %constant_dynamic-slice_fusion.8), channel_id=1, source_target_pairs={{8,3},{9,2},{10,5},{11,4},{12,7},{13,6},{16,11},{17,10},{18,13},{1... | collective-permute-start | bytes 6152 | tf_op jit(solution)/shard_map/ppermute | solution.py:71
  105.5 9.7 %collective-permute-start.25 = (bf16[1,1,1,8,128]{4,3,2,1,0:T(8,128)(2,1)S(1)}, bf16[1,1,1,8,128]{4,3,2,1,0:T(8,128)(2,1)S(1)}, u32[]{:S(2)}, u32[]{:S(2)}) collective-permute-start(bf16[1,1,1,8,128]{4,3,2,1,0:T(8,128)(2,1)S(1)} %constant_dynamic-slice_fusion.3), channel_id=1, source_target_pairs={{10,1},{11,0},{12,3},{13,2},{14,5},{15,4},{18,9},{19,8},{20,11},{2... | collective-permute-start | bytes 6152 | tf_op jit(solution)/shard_map/ppermute | solution.py:71
  107.4 14.6 %collective-permute-start.23 = (bf16[1,1,8,8,128]{4,3,2,1,0:T(8,128)(2,1)S(1)}, bf16[1,1,8,8,128]{4,3,2,1,0:T(8,128)(2,1)S(1)}, u32[]{:S(2)}, u32[]{:S(2)}) collective-permute-start(bf16[1,1,8,8,128]{4,3,2,1,0:T(8,128)(2,1)S(1)} %get-tuple-element.38), channel_id=1, source_target_pairs={{8,2},{9,3},{10,4},{11,5},{12,6},{13,7},{16,10},{17,11},{18,12},{1... | collective-permute-start | bytes 49160 | tf_op jit(solution)/shard_map/ppermute | solution.py:71
  109.3 12.8 %collective-permute-start.26 = (bf16[1,1,8,8,128]{4,3,2,1,0:T(8,128)(2,1)S(1)}, bf16[1,1,8,8,128]{4,3,2,1,0:T(8,128)(2,1)S(1)}, u32[]{:S(2)}, u32[]{:S(2)}) collective-permute-start(bf16[1,1,8,8,128]{4,3,2,1,0:T(8,128)(2,1)S(1)} %get-tuple-element.39), channel_id=1, source_target_pairs={{10,0},{11,1},{12,2},{13,3},{14,4},{15,5},{18,8},{19,9},{20,10},{2... | collective-permute-start | bytes 49160 | tf_op jit(solution)/shard_map/ppermute | solution.py:71
  111.3 11.2 %collective-permute-start.21 = (bf16[512,128]{1,0:T(8,128)(2,1)S(1)}, bf16[512,128]{1,0:T(8,128)(2,1)S(1)}, u32[]{:S(2)}, u32[]{:S(2)}) collective-permute-start(bf16[512,128]{1,0:T(8,128)(2,1)S(1)} %fusion.21), channel_id=1, source_target_pairs={{8,0},{16,8},{24,16},{9,1},{17,9},{25,17},{10,2},{18,10},{26,18},{... | collective-permute-start | bytes 393224 | tf_op jit(solution)/shard_map/ppermute | solution.py:211
  113.2 8.7 %collective-permute-start.24 = (bf16[1,8,1,8,128]{4,3,2,1,0:T(8,128)(2,1)S(1)}, bf16[1,8,1,8,128]{4,3,2,1,0:T(8,128)(2,1)S(1)}, u32[]{:S(2)}, u32[]{:S(2)}) collective-permute-start(bf16[1,8,1,8,128]{4,3,2,1,0:T(8,128)(2,1)S(1)} %constant_dynamic-slice_fusion.4), channel_id=1, source_target_pairs={{8,1},{9,0},{10,3},{11,2},{12,5},{13,4},{14,7},{15,6},{16,9},{17,8... | collective-permute-start | bytes 49160 | tf_op jit(solution)/shard_map/ppermute | solution.py:71
  115.1 6.7 %collective-permute-start.22 = (bf16[1,1,1,8,128]{4,3,2,1,0:T(8,128)(2,1)S(1)}, bf16[1,1,1,8,128]{4,3,2,1,0:T(8,128)(2,1)S(1)}, u32[]{:S(2)}, u32[]{:S(2)}) collective-permute-start(bf16[1,1,1,8,128]{4,3,2,1,0:T(8,128)(2,1)S(1)} %constant_dynamic-slice_fusion.5), channel_id=1, source_target_pairs={{8,3},{9,2},{10,5},{11,4},{12,7},{13,6},{16,11},{17,10},{18,13},{1... | collective-permute-start | bytes 6152 | tf_op jit(solution)/shard_map/ppermute | solution.py:71
  131.1 7.6 %collective-permute-start.27 = (bf16[864,128]{1,0:T(8,128)(2,1)S(1)}, bf16[864,128]{1,0:T(8,128)(2,1)S(1)}, u32[]{:S(2)}, u32[]{:S(2)}) collective-permute-start(bf16[864,128]{1,0:T(8,128)(2,1)S(1)} %get-tuple-element.29), channel_id=1, source_target_pairs={{0,2},{2,4},{4,6},{6,0},{1,3},{3,5},{5,7},{7,1},{8,10},{10,12},{12... | collective-permute-start | bytes 663560 | tf_op jit(solution)/shard_map/ppermute | solution.py:149
  131.1 9.7 %collective-permute-start.29 = (bf16[864,128]{1,0:T(8,128)(2,1)S(1)}, bf16[864,128]{1,0:T(8,128)(2,1)S(1)}, u32[]{:S(2)}, u32[]{:S(2)}) collective-permute-start(bf16[864,128]{1,0:T(8,128)(2,1)S(1)} %get-tuple-element.30), channel_id=1, source_target_pairs={{0,6},{2,0},{4,2},{6,4},{1,7},{3,1},{5,3},{7,5},{8,14},{10,8},{12,... | collective-permute-start | bytes 663560 | tf_op jit(solution)/shard_map/ppermute | solution.py:149
  133.5 10.6 %collective-permute-start.28 = (bf16[864,128]{1,0:T(8,128)(2,1)S(1)}, bf16[864,128]{1,0:T(8,128)(2,1)S(1)}, u32[]{:S(2)}, u32[]{:S(2)}) collective-permute-start(bf16[864,128]{1,0:T(8,128)(2,1)S(1)} %get-tuple-element.31), channel_id=1, source_target_pairs={{0,4},{2,6},{4,0},{6,2},{1,5},{3,7},{5,1},{7,3},{8,12},{10,14},{12... | collective-permute-start | bytes 663560 | tf_op jit(solution)/shard_map/ppermute | solution.py:149
  144.2 2.0 %collective-permute-start.30 = (f32[864,128]{1,0:T(8,128)S(1)}, f32[864,128]{1,0:T(8,128)S(1)}, u32[]{:S(2)}, u32[]{:S(2)}) collective-permute-start(f32[864,128]{1,0:T(8,128)S(1)} %convert_add_fusion), channel_id=1, source_target_pairs={{0,1},{1,0},{2,3},{3,2},{4,5},{5,4},{6,7},{7,6},{8,9},{9,8},{10,11... | collective-permute-start | bytes 1327112 | tf_op jit(solution)/shard_map/ppermute | solution.py:221

commit v5 on v3

--- a/solution.py
+++ b/solution.py
@@ -170,6 +170,9 @@
 
     grads_out = []
     kernel_total = jnp.zeros((taps * channels, channels), jnp.float32)
+    norm_scale = float(n_x * n_y * micro_count * row_count) ** (-0.5)
+    shard_rows = kernel.shape[1]
+    kernel_term = None
     for micro in range(micro_count):
         table = tables[micro]
         live_now = live_rows[micro]
@@ -187,23 +190,26 @@
         kept_grad = jnp.zeros((row_count, channels), jnp.bfloat16)
         for tick in range(n_pipe):
             active = segment_place == n_pipe - 1 - tick
+            kept_dy = jnp.where(active, centre, kept_dy)
+            if tick == n_pipe - 1:
+                per_tap = conv_filter(act_pad, cube(kept_dy))
+                kernel_total = kernel_total + per_tap.transpose(1, 2, 3, 0, 4).reshape(taps * channels, channels)
+                if micro == micro_count - 1:
+                    kernel_term = (kernel_total * norm_scale).astype(jnp.bfloat16)
+                    kernel_term, centre, received, both_pad = lax.optimization_barrier(
+                        (kernel_term, centre, received, both_pad)
+                    )
             grad_pad = both_pad[..., channels:] if tick == 0 else assemble(cube(centre), received, table)
             grad_act = conv_data(grad_pad, flipped).reshape(row_count, channels)
             result = finish_grad(values, centre, live_now, grad_act, gain_row)
-            kept_dy = jnp.where(active, centre, kept_dy)
             kept_grad = jnp.where(active, result, kept_grad)
             if tick < n_pipe - 1:
                 down = [(p, p - 1) for p in range(1, n_pipe)]
                 centre = lax.ppermute(result, "pipe", down)
                 received = exchange(cube(result), ("pipe", "sx", "sy"), (n_pipe, n_x, n_y), 1)
-        per_tap = conv_filter(act_pad, cube(kept_dy))
-        kernel_total = kernel_total + per_tap.transpose(1, 2, 3, 0, 4).reshape(taps * channels, channels)
         grads_out.append(kept_grad)
     grad_store = jnp.stack(grads_out)
-    norm_scale = float(n_x * n_y * micro_count * row_count) ** (-0.5)
-    kernel_term = kernel_total * norm_scale
-    shard_rows = kernel.shape[1]
-    over_x = scattered_sum(kernel_term.astype(jnp.bfloat16), "sx", shard_rows)
+    over_x = scattered_sum(kernel_term, "sx", shard_rows)
     partner = lax.ppermute(over_x, "sy", [(i, i ^ 1) for i in range(n_y)]) if n_y == 2 else None
     if partner is not None:
         kernel_share = over_x + partner

time: 148 us -> 146 us (0.986)
  starting transfers between devices: 61.9 us -> 59.1 us
    ppermute x20, waiting for transfers between devices: 12.5 us -> 20 us  [send(): return lax.ppermute(piece, axes, route)]
    ppermute x20, starting transfers between devices: 50.5 us -> 46.2 us  [send(): return lax.ppermute(piece, axes, route)]
    ppermute x3, waiting for transfers between devices: 10.6 us -> 7.31 us  [scattered_sum(): lax.ppermute(piece, axis, [(i, (i + step) % count) for i in range(count)])]
    ppermute x3, waiting for transfers between devices: 3.3 us -> 0.01 us  [shards(): centre = lax.ppermute(result, 'pipe', down)]
  transfers between devices with their start and end apart: 30 -> 30, of which waited for: 12 -> 10; matrix products, arithmetic and copies ran while one was open for 8% -> 14% of each run, Pallas kernels for 0% -> 0%
where the time goes in v5:
time: 146 us; the launch traced here: 145 us
  starting transfers between devices  59.1 us (40%)
  waiting for transfers between devices  27.7 us (19%)
  between operations  20 us (14%)
  matrix products  16.8 us (12%)
  other arithmetic  14.1 us (10%)
  local copies, waits for them, and re-layouts  7.22 us (5%)
    ppermute x20, starting transfers between devices, send(): return lax.ppermute(piece, axes, route)  46.2 us
    ppermute x20, waiting for transfers between devices, send(): return lax.ppermute(piece, axes, route)  20 us
    conv_general_dilated x4, matrix products, conv_data(): lax.conv_general_dilated(padded, filters, (1, 1, 1), 'VALID', dimension_n...  13 us
    ppermute x3, waiting for transfers between devices, scattered_sum(): lax.ppermute(piece, axis, [(i, (i + step) % count) for i in range(count)])  7.31 us
    ppermute x3, starting transfers between devices, shards(): centre = lax.ppermute(result, 'pipe', down)  6.37 us
    transpose x1, matrix products, shards(): per_tap.transpose(1, 2, 3, 0, 4).reshape(taps * channels, channels)  3.77 us
  transfers between devices with their start and end apart: 30, of which 10 were waited for; matrix products, arithmetic and copies ran while one was open for 14% of the time, Pallas kernels for 0%

profile of v5, /device:TPU:21, one launch (start us, length us, event | category | flops | bytes accessed | tf_op | source)
XLA Modules:
  0.0 144.9 jit_solution(5861989615720159072)
XLA Ops:
  0.6 1.2 collective-permute-start.7
  1.8 1.2 collective-permute-start.6
  3.1 0.9 convert_element_type.160
  4.0 1.1 fusion.25
  5.9 1.0 broadcast_select_fusion.12
  7.0 0.8 multiply_convert_fusion.2
  7.8 5.8 %collective-permute-start.3 = (bf16[1,1,1,8,256]{4,3,2,1,0:T(8,128)(2,1)S(1)}, bf16[1,1,1,8,256]{4,3,2,1,0:T(8,128)(2,1)S(1)}, u32[]{:S(2)}, u32[]{:S(2)}) collective-permute-start(bf16[1,1,1,8,256]{4,3,2,1,0:T(8,128)(2,1)S(1)} %fusion.59), channel_id=1, source_target_pairs={{2,1},{3,0},{4,3},{5,2},{6,5},{7,4},{10,9},{11,8},{12,11},{13,10},... | collective-permute-start | bytes 12296 | tf_op jit(solution)/shard_map/ppermute | solution.py:71
  13.6 1.9 %collective-permute-start.1 = (bf16[1,1,8,8,256]{4,3,2,1,0:T(8,128)(2,1)S(1)}, bf16[1,1,8,8,256]{4,3,2,1,0:T(8,128)(2,1)S(1)}, u32[]{:S(2)}, u32[]{:S(2)}) collective-permute-start(bf16[1,1,8,8,256]{4,3,2,1,0:T(8,128)(2,1)S(1)} %fusion.55), channel_id=1, source_target_pairs={{0,2},{1,3},{2,4},{3,5},{4,6},{5,7},{8,10},{9,11},{10,12},{11,13},... | collective-permute-start | bytes 98312 | tf_op jit(solution)/shard_map/ppermute | solution.py:71
  15.6 0.7 fusion.76
  16.3 0.7 fusion.77
  19.4 0.6 scatter_custom_fusion
  20.0 0.4 copy_dynamic-update-slice_fusion
  20.4 0.6 broadcast_select_fusion
  36.5 1.9 %collective-permute-start = (bf16[1,1,1,8,256]{4,3,2,1,0:T(8,128)(2,1)S(1)}, bf16[1,1,1,8,256]{4,3,2,1,0:T(8,128)(2,1)S(1)}, u32[]{:S(2)}, u32[]{:S(2)}) collective-permute-start(bf16[1,1,1,8,256]{4,3,2,1,0:T(8,128)(2,1)S(1)} %constant_dynamic-slice_fusion.14), channel_id=1, source_target_pairs={{0,3},{1,2},{2,5},{3,4},{4,7},{5,6},{8,11},{9,10},{10,13},{11,12},... | collective-permute-start | bytes 12296 | tf_op jit(solution)/shard_map/ppermute | solution.py:71
  38.4 3.9 %collective-permute-done = bf16[1,1,1,8,256]{4,3,2,1,0:T(8,128)(2,1)S(1)} collective-permute-done((bf16[1,1,1,8,256]{4,3,2,1,0:T(8,128)(2,1)S(1)}, bf16[1,1,1,8,256]{4,3,2,1,0:T(8,128)(2,1)S(1)}, u32[]{:S(2)}, u32[]{:S(2)}) %collective-permute-start) | collective-permute-done | bytes 4128 | tf_op jit(solution)/shard_map/ppermute | solution.py:71
  42.4 1.1 collective-permute-done.2
  43.5 3.4 %collective-permute-start.4 = (bf16[1,1,8,8,256]{4,3,2,1,0:T(8,128)(2,1)S(1)}, bf16[1,1,8,8,256]{4,3,2,1,0:T(8,128)(2,1)S(1)}, u32[]{:S(2)}, u32[]{:S(2)}) collective-permute-start(bf16[1,1,8,8,256]{4,3,2,1,0:T(8,128)(2,1)S(1)} %get-tuple-element.40), channel_id=1, source_target_pairs={{2,0},{3,1},{4,2},{5,3},{6,4},{7,5},{10,8},{11,9},{12,10},{13,11},... | collective-permute-start | bytes 98312 | tf_op jit(solution)/shard_map/ppermute | solution.py:71
  47.0 1.1 collective-permute-done.4
  48.7 2.1 %pad_maximum_fusion = bf16[1,10,10,10,256]{4,0,3,2,1:T(2,128)(2,1)S(1)} fusion(bf16[1,1,10,10,256]{4,0,3,2,1:T(2,128)(2,1)S(1)} %copy.33, bf16[1,8,1,10,256]{4,0,3,2,1:T(2,128)(2,1)S(1)} %copy.31, bf16[1,8,8,1,256]{4,0,3,2,1:T(2,128)(2,1)S(1)} %get-tuple-element.49, bf16[1,8,8,8,256]{4,0,3,2,1:T(2,128)(2,1)S(1)} %broadcast_select_fusion, ...), kind=kLoop, calls=%fused_computation.4 | loop fusion | flops 1536000 | bytes 1024000 | tf_op jit(solution)/shard_map/concatenate | solution.py:54
  50.9 0.6 copy-done.8
  51.7 1.3 pad_maximum_fusion.1
  52.9 0.7 gather_fusion
  53.7 1.1 rev.3
  54.7 4.1 %fusion.1 = f32[1,8,8,8,128]{4,0,3,2,1:T(1,128)S(1)} fusion(bf16[3,3,3,128,128]{4,3,2,1,0:T(8,128)(2,1)} %rev.3, bf16[1,10,10,10,256]{4,0,3,2,1:T(2,128)(2,1)S(1)} %pad_maximum_fusion), kind=kOutput, calls=%fused_computation.10 | convolution fusion | flops 452984832 | bytes 1658880 | tf_op jit(solution)/shard_map/conv_general_dilated | solution.py:95
  58.8 0.3 fusion.47
  59.6 4.1 %collective-permute-start.13 = (bf16[1,1,8,8,128]{4,3,2,1,0:T(8,128)(2,1)S(1)}, bf16[1,1,8,8,128]{4,3,2,1,0:T(8,128)(2,1)S(1)}, u32[]{:S(2)}, u32[]{:S(2)}) collective-permute-start(bf16[1,1,8,8,128]{4,3,2,1,0:T(8,128)(2,1)S(1)} %get-tuple-element.61), channel_id=1, source_target_pairs={{10,0},{11,1},{12,2},{13,3},{14,4},{15,5},{18,8},{19,9},{20,10},{2... | collective-permute-start | bytes 49160 | tf_op jit(solution)/shard_map/ppermute | solution.py:71
  63.8 1.9 %collective-permute-start.10 = (bf16[1,1,8,8,128]{4,3,2,1,0:T(8,128)(2,1)S(1)}, bf16[1,1,8,8,128]{4,3,2,1,0:T(8,128)(2,1)S(1)}, u32[]{:S(2)}, u32[]{:S(2)}) collective-permute-start(bf16[1,1,8,8,128]{4,3,2,1,0:T(8,128)(2,1)S(1)} %get-tuple-element.60), channel_id=1, source_target_pairs={{8,2},{9,3},{10,4},{11,5},{12,6},{13,7},{16,10},{17,11},{18,12},{1... | collective-permute-start | bytes 49160 | tf_op jit(solution)/shard_map/ppermute | solution.py:71
  65.8 3.1 %collective-permute-start.12 = (bf16[1,1,1,8,128]{4,3,2,1,0:T(8,128)(2,1)S(1)}, bf16[1,1,1,8,128]{4,3,2,1,0:T(8,128)(2,1)S(1)}, u32[]{:S(2)}, u32[]{:S(2)}) collective-permute-start(bf16[1,1,1,8,128]{4,3,2,1,0:T(8,128)(2,1)S(1)} %constant_dynamic-slice_fusion.9), channel_id=1, source_target_pairs={{10,1},{11,0},{12,3},{13,2},{14,5},{15,4},{18,9},{19,8},{20,11},{2... | collective-permute-start | bytes 6152 | tf_op jit(solution)/shard_map/ppermute | solution.py:71
  69.2 1.9 %collective-permute-start.8 = (bf16[512,128]{1,0:T(8,128)(2,1)S(1)}, bf16[512,128]{1,0:T(8,128)(2,1)S(1)}, u32[]{:S(2)}, u32[]{:S(2)}) collective-permute-start(bf16[512,128]{1,0:T(8,128)(2,1)S(1)} %fusion.8), channel_id=1, source_target_pairs={{8,0},{16,8},{24,16},{9,1},{17,9},{25,17},{10,2},{18,10},{26,18},{... | collective-permute-start | bytes 393224 | tf_op jit(solution)/shard_map/ppermute | solution.py:208
  71.1 2.4 %collective-permute-start.11 = (bf16[1,8,1,8,128]{4,3,2,1,0:T(8,128)(2,1)S(1)}, bf16[1,8,1,8,128]{4,3,2,1,0:T(8,128)(2,1)S(1)}, u32[]{:S(2)}, u32[]{:S(2)}) collective-permute-start(bf16[1,8,1,8,128]{4,3,2,1,0:T(8,128)(2,1)S(1)} %constant_dynamic-slice_fusion.10), channel_id=1, source_target_pairs={{8,1},{9,0},{10,3},{11,2},{12,5},{13,4},{14,7},{15,6},{16,9},{17,8... | collective-permute-start | bytes 49160 | tf_op jit(solution)/shard_map/ppermute | solution.py:71
  73.5 2.1 %collective-permute-start.9 = (bf16[1,1,1,8,128]{4,3,2,1,0:T(8,128)(2,1)S(1)}, bf16[1,1,1,8,128]{4,3,2,1,0:T(8,128)(2,1)S(1)}, u32[]{:S(2)}, u32[]{:S(2)}) collective-permute-start(bf16[1,1,1,8,128]{4,3,2,1,0:T(8,128)(2,1)S(1)} %constant_dynamic-slice_fusion.11), channel_id=1, source_target_pairs={{8,3},{9,2},{10,5},{11,4},{12,7},{13,6},{16,11},{17,10},{18,13},{1... | collective-permute-start | bytes 6152 | tf_op jit(solution)/shard_map/ppermute | solution.py:71
  75.6 4.6 %collective-permute-done.9 = bf16[1,1,1,8,128]{4,3,2,1,0:T(8,128)(2,1)S(1)} collective-permute-done((bf16[1,1,1,8,128]{4,3,2,1,0:T(8,128)(2,1)S(1)}, bf16[1,1,1,8,128]{4,3,2,1,0:T(8,128)(2,1)S(1)}, u32[]{:S(2)}, u32[]{:S(2)}) %collective-permute-start.9) | collective-permute-done | bytes 2080 | tf_op jit(solution)/shard_map/ppermute | solution.py:71
  81.2 3.0 %fusion.5 = f32[1,8,8,8,128]{4,0,3,2,1:T(1,128)S(1)} fusion(bf16[3,3,3,128,128]{4,3,2,1,0:T(8,128)(2,1)S(1)} %bitcast.202, bf16[1,1,10,10,128]{4,0,3,2,1:T(2,128)(2,1)S(1)} %copy.42, bf16[1,8,1,10,128]{4,0,3,2,1:T(2,128)(2,1)S(1)} %copy.40, bf16[1,8,8,1,128]{4,0,3,2,1:T(2,128)(2,1)S(1)} %slice_bitcast_fusion.4, bf16[1,8,8,8,128]{4,0,3,2,1:T(2,128)(2,1)S(1)} %copy.38, ...), kind=kOutput, calls=%fused_computation.14 | convolution fusion | flops 454776832 | bytes 1402880 | tf_op jit(solution)/shard_map/conv_general_dilated | solution.py:95
  84.1 0.3 fusion.48
  84.5 0.3 fusion.18
  84.8 2.5 %collective-permute-start.14 = (bf16[512,128]{1,0:T(8,128)(2,1)S(1)}, bf16[512,128]{1,0:T(8,128)(2,1)S(1)}, u32[]{:S(2)}, u32[]{:S(2)}) collective-permute-start(bf16[512,128]{1,0:T(8,128)(2,1)S(1)} %fusion.18), channel_id=1, source_target_pairs={{8,0},{16,8},{24,16},{9,1},{17,9},{25,17},{10,2},{18,10},{26,18},{... | collective-permute-start | bytes 393224 | tf_op jit(solution)/shard_map/ppermute | solution.py:208
  87.3 1.9 %collective-permute-start.19 = (bf16[1,1,8,8,128]{4,3,2,1,0:T(8,128)(2,1)S(1)}, bf16[1,1,8,8,128]{4,3,2,1,0:T(8,128)(2,1)S(1)}, u32[]{:S(2)}, u32[]{:S(2)}) collective-permute-start(bf16[1,1,8,8,128]{4,3,2,1,0:T(8,128)(2,1)S(1)} %get-tuple-element.56), channel_id=1, source_target_pairs={{10,0},{11,1},{12,2},{13,3},{14,4},{15,5},{18,8},{19,9},{20,10},{2... | collective-permute-start | bytes 49160 | tf_op jit(solution)/shard_map/ppermute | solution.py:71
  89.3 1.9 %collective-permute-start.18 = (bf16[1,1,1,8,128]{4,3,2,1,0:T(8,128)(2,1)S(1)}, bf16[1,1,1,8,128]{4,3,2,1,0:T(8,128)(2,1)S(1)}, u32[]{:S(2)}, u32[]{:S(2)}) collective-permute-start(bf16[1,1,1,8,128]{4,3,2,1,0:T(8,128)(2,1)S(1)} %constant_dynamic-slice_fusion.6), channel_id=1, source_target_pairs={{10,1},{11,0},{12,3},{13,2},{14,5},{15,4},{18,9},{19,8},{20,11},{2... | collective-permute-start | bytes 6152 | tf_op jit(solution)/shard_map/ppermute | solution.py:71
  91.2 1.9 %collective-permute-start.16 = (bf16[1,1,8,8,128]{4,3,2,1,0:T(8,128)(2,1)S(1)}, bf16[1,1,8,8,128]{4,3,2,1,0:T(8,128)(2,1)S(1)}, u32[]{:S(2)}, u32[]{:S(2)}) collective-permute-start(bf16[1,1,8,8,128]{4,3,2,1,0:T(8,128)(2,1)S(1)} %get-tuple-element.55), channel_id=1, source_target_pairs={{8,2},{9,3},{10,4},{11,5},{12,6},{13,7},{16,10},{17,11},{18,12},{1... | collective-permute-start | bytes 49160 | tf_op jit(solution)/shard_map/ppermute | solution.py:71
  93.2 1.9 %collective-permute-start.17 = (bf16[1,8,1,8,128]{4,3,2,1,0:T(8,128)(2,1)S(1)}, bf16[1,8,1,8,128]{4,3,2,1,0:T(8,128)(2,1)S(1)}, u32[]{:S(2)}, u32[]{:S(2)}) collective-permute-start(bf16[1,8,1,8,128]{4,3,2,1,0:T(8,128)(2,1)S(1)} %constant_dynamic-slice_fusion.7), channel_id=1, source_target_pairs={{8,1},{9,0},{10,3},{11,2},{12,5},{13,4},{14,7},{15,6},{16,9},{17,8... | collective-permute-start | bytes 49160 | tf_op jit(solution)/shard_map/ppermute | solution.py:71
  95.1 1.9 %collective-permute-start.15 = (bf16[1,1,1,8,128]{4,3,2,1,0:T(8,128)(2,1)S(1)}, bf16[1,1,1,8,128]{4,3,2,1,0:T(8,128)(2,1)S(1)}, u32[]{:S(2)}, u32[]{:S(2)}) collective-permute-start(bf16[1,1,1,8,128]{4,3,2,1,0:T(8,128)(2,1)S(1)} %constant_dynamic-slice_fusion.8), channel_id=1, source_target_pairs={{8,3},{9,2},{10,5},{11,4},{12,7},{13,6},{16,11},{17,10},{18,13},{1... | collective-permute-start | bytes 6152 | tf_op jit(solution)/shard_map/ppermute | solution.py:71
  97.0 4.8 %collective-permute-done.15 = bf16[1,1,1,8,128]{4,3,2,1,0:T(8,128)(2,1)S(1)} collective-permute-done((bf16[1,1,1,8,128]{4,3,2,1,0:T(8,128)(2,1)S(1)}, bf16[1,1,1,8,128]{4,3,2,1,0:T(8,128)(2,1)S(1)}, u32[]{:S(2)}, u32[]{:S(2)}) %collective-permute-start.15) | collective-permute-done | bytes 2080 | tf_op jit(solution)/shard_map/ppermute | solution.py:71
  102.7 3.0 %fusion.4 = f32[1,8,8,8,128]{4,0,3,2,1:T(1,128)S(1)} fusion(bf16[3,3,3,128,128]{4,3,2,1,0:T(8,128)(2,1)S(1)} %bitcast.203, bf16[1,1,10,10,128]{4,0,3,2,1:T(2,128)(2,1)S(1)} %copy.49, bf16[1,8,1,10,128]{4,0,3,2,1:T(2,128)(2,1)S(1)} %copy.47, bf16[1,8,8,1,128]{4,0,3,2,1:T(2,128)(2,1)S(1)} %slice_bitcast_fusion.2, bf16[1,8,8,8,128]{4,0,3,2,1:T(2,128)(2,1)S(1)} %copy.45, ...), kind=kOutput, calls=%fused_computation.13 | convolution fusion | flops 454776832 | bytes 1402880 | tf_op jit(solution)/shard_map/conv_general_dilated | solution.py:95
  105.7 0.3 fusion.49
  106.1 0.3 fusion.21
  106.4 2.0 %collective-permute-start.20 = (bf16[512,128]{1,0:T(8,128)(2,1)S(1)}, bf16[512,128]{1,0:T(8,128)(2,1)S(1)}, u32[]{:S(2)}, u32[]{:S(2)}) collective-permute-start(bf16[512,128]{1,0:T(8,128)(2,1)S(1)} %fusion.21), channel_id=1, source_target_pairs={{8,0},{16,8},{24,16},{9,1},{17,9},{25,17},{10,2},{18,10},{26,18},{... | collective-permute-start | bytes 393224 | tf_op jit(solution)/shard_map/ppermute | solution.py:208
  108.4 1.9 %collective-permute-start.22 = (bf16[1,1,8,8,128]{4,3,2,1,0:T(8,128)(2,1)S(1)}, bf16[1,1,8,8,128]{4,3,2,1,0:T(8,128)(2,1)S(1)}, u32[]{:S(2)}, u32[]{:S(2)}) collective-permute-start(bf16[1,1,8,8,128]{4,3,2,1,0:T(8,128)(2,1)S(1)} %get-tuple-element.54), channel_id=1, source_target_pairs={{8,2},{9,3},{10,4},{11,5},{12,6},{13,7},{16,10},{17,11},{18,12},{1... | collective-permute-start | bytes 49160 | tf_op jit(solution)/shard_map/ppermute | solution.py:71
  110.3 1.9 %collective-permute-start.21 = (bf16[1,1,1,8,128]{4,3,2,1,0:T(8,128)(2,1)S(1)}, bf16[1,1,1,8,128]{4,3,2,1,0:T(8,128)(2,1)S(1)}, u32[]{:S(2)}, u32[]{:S(2)}) collective-permute-start(bf16[1,1,1,8,128]{4,3,2,1,0:T(8,128)(2,1)S(1)} %constant_dynamic-slice_fusion.5), channel_id=1, source_target_pairs={{8,3},{9,2},{10,5},{11,4},{12,7},{13,6},{16,11},{17,10},{18,13},{1... | collective-permute-start | bytes 6152 | tf_op jit(solution)/shard_map/ppermute | solution.py:71
  112.3 1.9 %collective-permute-start.25 = (bf16[1,1,8,8,128]{4,3,2,1,0:T(8,128)(2,1)S(1)}, bf16[1,1,8,8,128]{4,3,2,1,0:T(8,128)(2,1)S(1)}, u32[]{:S(2)}, u32[]{:S(2)}) collective-permute-start(bf16[1,1,8,8,128]{4,3,2,1,0:T(8,128)(2,1)S(1)} %get-tuple-element.53), channel_id=1, source_target_pairs={{10,0},{11,1},{12,2},{13,3},{14,4},{15,5},{18,8},{19,9},{20,10},{2... | collective-permute-start | bytes 49160 | tf_op jit(solution)/shard_map/ppermute | solution.py:71
  114.2 1.9 %collective-permute-start.23 = (bf16[1,8,1,8,128]{4,3,2,1,0:T(8,128)(2,1)S(1)}, bf16[1,8,1,8,128]{4,3,2,1,0:T(8,128)(2,1)S(1)}, u32[]{:S(2)}, u32[]{:S(2)}) collective-permute-start(bf16[1,8,1,8,128]{4,3,2,1,0:T(8,128)(2,1)S(1)} %constant_dynamic-slice_fusion.4), channel_id=1, source_target_pairs={{8,1},{9,0},{10,3},{11,2},{12,5},{13,4},{14,7},{15,6},{16,9},{17,8... | collective-permute-start | bytes 49160 | tf_op jit(solution)/shard_map/ppermute | solution.py:71
  116.1 0.9 collective-permute-done.21
  117.0 2.1 %collective-permute-start.24 = (bf16[1,1,1,8,128]{4,3,2,1,0:T(8,128)(2,1)S(1)}, bf16[1,1,1,8,128]{4,3,2,1,0:T(8,128)(2,1)S(1)}, u32[]{:S(2)}, u32[]{:S(2)}) collective-permute-start(bf16[1,1,1,8,128]{4,3,2,1,0:T(8,128)(2,1)S(1)} %constant_dynamic-slice_fusion.3), channel_id=1, source_target_pairs={{10,1},{11,0},{12,3},{13,2},{14,5},{15,4},{18,9},{19,8},{20,11},{2... | collective-permute-start | bytes 6152 | tf_op jit(solution)/shard_map/ppermute | solution.py:71
  119.2 3.6 %collective-permute-done.24 = bf16[1,1,1,8,128]{4,3,2,1,0:T(8,128)(2,1)S(1)} collective-permute-done((bf16[1,1,1,8,128]{4,3,2,1,0:T(8,128)(2,1)S(1)}, bf16[1,1,1,8,128]{4,3,2,1,0:T(8,128)(2,1)S(1)}, u32[]{:S(2)}, u32[]{:S(2)}) %collective-permute-start.24) | collective-permute-done | bytes 2080 | tf_op jit(solution)/shard_map/ppermute | solution.py:71
  123.0 3.8 %multiply_convert_fusion = bf16[3,3,3,128,128]{4,3,2,1,0:T(8,128)(2,1)S(1)} fusion(bf16[1,10,10,10,256]{4,0,3,2,1:T(2,128)(2,1)S(1)} %pad_maximum_fusion, bf16[1,8,8,8,128]{4,3,2,1,0:T(8,128)(2,1)S(1)} %bitcast.240), kind=kOutput, calls=%fused_computation.2 | convolution fusion | flops 453869568 | bytes 1527808 | tf_op jit(solution)/shard_map/transpose | solution.py:196
  127.8 2.2 %collective-permute-start.28 = (bf16[864,128]{1,0:T(8,128)(2,1)S(1)}, bf16[864,128]{1,0:T(8,128)(2,1)S(1)}, u32[]{:S(2)}, u32[]{:S(2)}) collective-permute-start(bf16[864,128]{1,0:T(8,128)(2,1)S(1)} %get-tuple-element.46), channel_id=1, source_target_pairs={{0,6},{2,0},{4,2},{6,4},{1,7},{3,1},{5,3},{7,5},{8,14},{10,8},{12,... | collective-permute-start | bytes 663560 | tf_op jit(solution)/shard_map/ppermute | solution.py:135
  130.0 0.4 collective-permute-start.26
  130.3 3.0 %fusion.3 = f32[1,8,8,8,128]{4,0,3,2,1:T(1,128)S(1)} fusion(bf16[3,3,3,128,128]{4,3,2,1,0:T(8,128)(2,1)S(1)} %bitcast.204, bf16[1,1,10,10,128]{4,0,3,2,1:T(2,128)(2,1)S(1)} %copy.57, bf16[1,8,1,10,128]{4,0,3,2,1:T(2,128)(2,1)S(1)} %copy.55, bf16[1,8,8,1,128]{4,0,3,2,1:T(2,128)(2,1)S(1)} %slice_bitcast_fusion, bf16[1,8,8,8,128]{4,0,3,2,1:T(2,128)(2,1)S(1)} %copy.53, ...), kind=kOutput, calls=%fused_computation.12 | convolution fusion | flops 454776832 | bytes 1402880 | tf_op jit(solution)/shard_map/conv_general_dilated | solution.py:95
  133.4 0.3 fusion.50
  133.7 0.8 collective-permute-done.28
  134.5 6.5 %collective-permute-done.27 = bf16[864,128]{1,0:T(8,128)(2,1)S(1)} collective-permute-done((bf16[864,128]{1,0:T(8,128)(2,1)S(1)}, bf16[864,128]{1,0:T(8,128)(2,1)S(1)}, u32[]{:S(2)}, u32[]{:S(2)}) %collective-permute-start.27) | collective-permute-done | bytes 221216 | tf_op jit(solution)/shard_map/ppermute | solution.py:135
  141.1 1.6 %collective-permute-start.29 = (f32[864,128]{1,0:T(8,128)S(1)}, f32[864,128]{1,0:T(8,128)S(1)}, u32[]{:S(2)}, u32[]{:S(2)}) collective-permute-start(f32[864,128]{1,0:T(8,128)S(1)} %convert_add_fusion), channel_id=1, source_target_pairs={{0,1},{1,0},{2,3},{3,2},{4,5},{5,4},{6,7},{7,6},{8,9},{9,8},{10,11... | collective-permute-start | bytes 1327112 | tf_op jit(solution)/shard_map/ppermute | solution.py:213
  142.7 1.0 fusion.53
  143.8 0.4 collective-permute-done.29
  144.1 0.8 add_bitcast_fusion
  (198 shorter events, 5.2 us)
Async XLA Ops:
  0.6 50.2 %collective-permute-start.7 = (bf16[864,128]{1,0:T(8,128)(2,1)}, bf16[864,128]{1,0:T(8,128)(2,1)S(1)}, u32[]{:S(2)}, u32[]{:S(2)}) collective-permute-start(bf16[864,128]{1,0:T(8,128)(2,1)} %bitcast.228), channel_id=1, source_target_pairs={{0,6},{2,0},{4,2},{6,4},{1,7},{3,1},{5,3},{7,5},{8,14},{10,8},{12,... | collective-permute-start | bytes 663560 | tf_op jit(solution)/shard_map/ppermute | solution.py:121
  1.8 49.0 %collective-permute-start.6 = (bf16[864,128]{1,0:T(8,128)(2,1)}, bf16[864,128]{1,0:T(8,128)(2,1)S(1)}, u32[]{:S(2)}, u32[]{:S(2)}) collective-permute-start(bf16[864,128]{1,0:T(8,128)(2,1)} %bitcast.229), channel_id=1, source_target_pairs={{0,4},{2,6},{4,0},{6,2},{1,5},{3,7},{5,1},{7,3},{8,12},{10,14},{12... | collective-permute-start | bytes 663560 | tf_op jit(solution)/shard_map/ppermute | solution.py:121
  3.1 47.8 %collective-permute-start.5 = (bf16[864,128]{1,0:T(8,128)(2,1)}, bf16[864,128]{1,0:T(8,128)(2,1)S(1)}, u32[]{:S(2)}, u32[]{:S(2)}) collective-permute-start(bf16[864,128]{1,0:T(8,128)(2,1)} %bitcast.230), channel_id=1, source_target_pairs={{0,2},{2,4},{4,6},{6,0},{1,3},{3,5},{5,7},{7,1},{8,10},{10,12},{12... | collective-permute-start | bytes 663560 | tf_op jit(solution)/shard_map/ppermute | solution.py:121
  4.0 11.6 %copy-start.6 = (s32[1,1,1,1,27]{4,3,2,1,0:T(1,128)S(1)}, s32[1,1,1,1,27]{4,3,2,1,0:T(1,128)}, u32[]{:S(2)}) copy-start(s32[1,1,1,1,27]{4,3,2,1,0:T(1,128)} %param.8) | copy-start | bytes 328
  4.0 13.1 %copy-start.11 = (f32[1,128]{1,0:T(1,128)S(1)}, f32[1,128]{1,0:T(1,128)}, u32[]{:S(2)}) copy-start(f32[1,128]{1,0:T(1,128)} %param.10) | copy-start | bytes 1540
  7.8 9.7 %copy-start.1 = (bf16[1,1,1,512,128]{4,3,2,1,0:T(8,128)(2,1)S(1)}, bf16[1,1,1,512,128]{4,3,2,1,0:T(8,128)(2,1)}, u32[]{:S(2)}) copy-start(bf16[1,1,1,512,128]{4,3,2,1,0:T(8,128)(2,1)} %param.7) | copy-start | bytes 393220
  7.8 28.6 %collective-permute-start.3 = (bf16[1,1,1,8,256]{4,3,2,1,0:T(8,128)(2,1)S(1)}, bf16[1,1,1,8,256]{4,3,2,1,0:T(8,128)(2,1)S(1)}, u32[]{:S(2)}, u32[]{:S(2)}) collective-permute-start(bf16[1,1,1,8,256]{4,3,2,1,0:T(8,128)(2,1)S(1)} %fusion.59), channel_id=1, source_target_pairs={{2,1},{3,0},{4,3},{5,2},{6,5},{7,4},{10,9},{11,8},{12,11},{13,10},... | collective-permute-start | bytes 12296 | tf_op jit(solution)/shard_map/ppermute | solution.py:71
  13.6 34.8 %collective-permute-start.1 = (bf16[1,1,8,8,256]{4,3,2,1,0:T(8,128)(2,1)S(1)}, bf16[1,1,8,8,256]{4,3,2,1,0:T(8,128)(2,1)S(1)}, u32[]{:S(2)}, u32[]{:S(2)}) collective-permute-start(bf16[1,1,8,8,256]{4,3,2,1,0:T(8,128)(2,1)S(1)} %fusion.55), channel_id=1, source_target_pairs={{0,2},{1,3},{2,4},{3,5},{4,6},{5,7},{8,10},{9,11},{10,12},{11,13},... | collective-permute-start | bytes 98312 | tf_op jit(solution)/shard_map/ppermute | solution.py:71
  36.5 5.8 %collective-permute-start = (bf16[1,1,1,8,256]{4,3,2,1,0:T(8,128)(2,1)S(1)}, bf16[1,1,1,8,256]{4,3,2,1,0:T(8,128)(2,1)S(1)}, u32[]{:S(2)}, u32[]{:S(2)}) collective-permute-start(bf16[1,1,1,8,256]{4,3,2,1,0:T(8,128)(2,1)S(1)} %constant_dynamic-slice_fusion.14), channel_id=1, source_target_pairs={{0,3},{1,2},{2,5},{3,4},{4,7},{5,6},{8,11},{9,10},{10,13},{11,12},... | collective-permute-start | bytes 12296 | tf_op jit(solution)/shard_map/ppermute | solution.py:71
  42.3 1.2 collective-permute-start.2
  43.5 4.6 %collective-permute-start.4 = (bf16[1,1,8,8,256]{4,3,2,1,0:T(8,128)(2,1)S(1)}, bf16[1,1,8,8,256]{4,3,2,1,0:T(8,128)(2,1)S(1)}, u32[]{:S(2)}, u32[]{:S(2)}) collective-permute-start(bf16[1,1,8,8,256]{4,3,2,1,0:T(8,128)(2,1)S(1)} %get-tuple-element.40), channel_id=1, source_target_pairs={{2,0},{3,1},{4,2},{5,3},{6,4},{7,5},{10,8},{11,9},{12,10},{13,11},... | collective-permute-start | bytes 98312 | tf_op jit(solution)/shard_map/ppermute | solution.py:71
  48.7 3.0 %copy-start.7 = (bf16[1,864,128]{2,1,0:T(8,128)(2,1)S(1)}, bf16[1,864,128]{2,1,0:T(8,128)(2,1)}, u32[]{:S(2)}) copy-start(bf16[1,864,128]{2,1,0:T(8,128)(2,1)} %param.11) | copy-start | bytes 663556
  50.8 0.7 copy-start.8
  50.9 0.7 copy-start.9
  50.9 0.8 copy-start.10
  54.7 4.1 %copy-start = (bf16[1,1,1,1,512,128]{5,4,3,2,1,0:T(8,128)(2,1)S(1)}, bf16[1,1,1,1,512,128]{5,4,3,2,1,0:T(8,128)(2,1)}, u32[]{:S(2)}) copy-start(bf16[1,1,1,1,512,128]{5,4,3,2,1,0:T(8,128)(2,1)} %param.6) | copy-start | bytes 393220
  59.6 20.8 %collective-permute-start.13 = (bf16[1,1,8,8,128]{4,3,2,1,0:T(8,128)(2,1)S(1)}, bf16[1,1,8,8,128]{4,3,2,1,0:T(8,128)(2,1)S(1)}, u32[]{:S(2)}, u32[]{:S(2)}) collective-permute-start(bf16[1,1,8,8,128]{4,3,2,1,0:T(8,128)(2,1)S(1)} %get-tuple-element.61), channel_id=1, source_target_pairs={{10,0},{11,1},{12,2},{13,3},{14,4},{15,5},{18,8},{19,9},{20,10},{2... | collective-permute-start | bytes 49160 | tf_op jit(solution)/shard_map/ppermute | solution.py:71
  63.8 16.7 %collective-permute-start.10 = (bf16[1,1,8,8,128]{4,3,2,1,0:T(8,128)(2,1)S(1)}, bf16[1,1,8,8,128]{4,3,2,1,0:T(8,128)(2,1)S(1)}, u32[]{:S(2)}, u32[]{:S(2)}) collective-permute-start(bf16[1,1,8,8,128]{4,3,2,1,0:T(8,128)(2,1)S(1)} %get-tuple-element.60), channel_id=1, source_target_pairs={{8,2},{9,3},{10,4},{11,5},{12,6},{13,7},{16,10},{17,11},{18,12},{1... | collective-permute-start | bytes 49160 | tf_op jit(solution)/shard_map/ppermute | solution.py:71
  65.8 7.7 %collective-permute-start.12 = (bf16[1,1,1,8,128]{4,3,2,1,0:T(8,128)(2,1)S(1)}, bf16[1,1,1,8,128]{4,3,2,1,0:T(8,128)(2,1)S(1)}, u32[]{:S(2)}, u32[]{:S(2)}) collective-permute-start(bf16[1,1,1,8,128]{4,3,2,1,0:T(8,128)(2,1)S(1)} %constant_dynamic-slice_fusion.9), channel_id=1, source_target_pairs={{10,1},{11,0},{12,3},{13,2},{14,5},{15,4},{18,9},{19,8},{20,11},{2... | collective-permute-start | bytes 6152 | tf_op jit(solution)/shard_map/ppermute | solution.py:71
  69.2 14.9 %copy-start.4 = (bf16[512,128]{1,0:T(8,128)(2,1)}, bf16[512,128]{1,0:T(8,128)(2,1)S(1)}, u32[]{:S(2)}) copy-start(bf16[512,128]{1,0:T(8,128)(2,1)S(1)} %fusion.8) | copy-start | bytes 393220
  69.2 11.6 %collective-permute-start.8 = (bf16[512,128]{1,0:T(8,128)(2,1)S(1)}, bf16[512,128]{1,0:T(8,128)(2,1)S(1)}, u32[]{:S(2)}, u32[]{:S(2)}) collective-permute-start(bf16[512,128]{1,0:T(8,128)(2,1)S(1)} %fusion.8), channel_id=1, source_target_pairs={{8,0},{16,8},{24,16},{9,1},{17,9},{25,17},{10,2},{18,10},{26,18},{... | collective-permute-start | bytes 393224 | tf_op jit(solution)/shard_map/ppermute | solution.py:208
  71.1 9.2 %collective-permute-start.11 = (bf16[1,8,1,8,128]{4,3,2,1,0:T(8,128)(2,1)S(1)}, bf16[1,8,1,8,128]{4,3,2,1,0:T(8,128)(2,1)S(1)}, u32[]{:S(2)}, u32[]{:S(2)}) collective-permute-start(bf16[1,8,1,8,128]{4,3,2,1,0:T(8,128)(2,1)S(1)} %constant_dynamic-slice_fusion.10), channel_id=1, source_target_pairs={{8,1},{9,0},{10,3},{11,2},{12,5},{13,4},{14,7},{15,6},{16,9},{17,8... | collective-permute-start | bytes 49160 | tf_op jit(solution)/shard_map/ppermute | solution.py:71
  73.5 6.7 %collective-permute-start.9 = (bf16[1,1,1,8,128]{4,3,2,1,0:T(8,128)(2,1)S(1)}, bf16[1,1,1,8,128]{4,3,2,1,0:T(8,128)(2,1)S(1)}, u32[]{:S(2)}, u32[]{:S(2)}) collective-permute-start(bf16[1,1,1,8,128]{4,3,2,1,0:T(8,128)(2,1)S(1)} %constant_dynamic-slice_fusion.11), channel_id=1, source_target_pairs={{8,3},{9,2},{10,5},{11,4},{12,7},{13,6},{16,11},{17,10},{18,13},{1... | collective-permute-start | bytes 6152 | tf_op jit(solution)/shard_map/ppermute | solution.py:71
  84.8 17.9 %copy-start.2 = (bf16[512,128]{1,0:T(8,128)(2,1)}, bf16[512,128]{1,0:T(8,128)(2,1)S(1)}, u32[]{:S(2)}) copy-start(bf16[512,128]{1,0:T(8,128)(2,1)S(1)} %fusion.18) | copy-start | bytes 393220
  84.8 17.6 %collective-permute-start.14 = (bf16[512,128]{1,0:T(8,128)(2,1)S(1)}, bf16[512,128]{1,0:T(8,128)(2,1)S(1)}, u32[]{:S(2)}, u32[]{:S(2)}) collective-permute-start(bf16[512,128]{1,0:T(8,128)(2,1)S(1)} %fusion.18), channel_id=1, source_target_pairs={{8,0},{16,8},{24,16},{9,1},{17,9},{25,17},{10,2},{18,10},{26,18},{... | collective-permute-start | bytes 393224 | tf_op jit(solution)/shard_map/ppermute | solution.py:208
  87.3 14.7 %collective-permute-start.19 = (bf16[1,1,8,8,128]{4,3,2,1,0:T(8,128)(2,1)S(1)}, bf16[1,1,8,8,128]{4,3,2,1,0:T(8,128)(2,1)S(1)}, u32[]{:S(2)}, u32[]{:S(2)}) collective-permute-start(bf16[1,1,8,8,128]{4,3,2,1,0:T(8,128)(2,1)S(1)} %get-tuple-element.56), channel_id=1, source_target_pairs={{10,0},{11,1},{12,2},{13,3},{14,4},{15,5},{18,8},{19,9},{20,10},{2... | collective-permute-start | bytes 49160 | tf_op jit(solution)/shard_map/ppermute | solution.py:71
  89.3 5.8 %collective-permute-start.18 = (bf16[1,1,1,8,128]{4,3,2,1,0:T(8,128)(2,1)S(1)}, bf16[1,1,1,8,128]{4,3,2,1,0:T(8,128)(2,1)S(1)}, u32[]{:S(2)}, u32[]{:S(2)}) collective-permute-start(bf16[1,1,1,8,128]{4,3,2,1,0:T(8,128)(2,1)S(1)} %constant_dynamic-slice_fusion.6), channel_id=1, source_target_pairs={{10,1},{11,0},{12,3},{13,2},{14,5},{15,4},{18,9},{19,8},{20,11},{2... | collective-permute-start | bytes 6152 | tf_op jit(solution)/shard_map/ppermute | solution.py:71
  91.2 10.9 %collective-permute-start.16 = (bf16[1,1,8,8,128]{4,3,2,1,0:T(8,128)(2,1)S(1)}, bf16[1,1,8,8,128]{4,3,2,1,0:T(8,128)(2,1)S(1)}, u32[]{:S(2)}, u32[]{:S(2)}) collective-permute-start(bf16[1,1,8,8,128]{4,3,2,1,0:T(8,128)(2,1)S(1)} %get-tuple-element.55), channel_id=1, source_target_pairs={{8,2},{9,3},{10,4},{11,5},{12,6},{13,7},{16,10},{17,11},{18,12},{1... | collective-permute-start | bytes 49160 | tf_op jit(solution)/shard_map/ppermute | solution.py:71
  93.2 8.7 %collective-permute-start.17 = (bf16[1,8,1,8,128]{4,3,2,1,0:T(8,128)(2,1)S(1)}, bf16[1,8,1,8,128]{4,3,2,1,0:T(8,128)(2,1)S(1)}, u32[]{:S(2)}, u32[]{:S(2)}) collective-permute-start(bf16[1,8,1,8,128]{4,3,2,1,0:T(8,128)(2,1)S(1)} %constant_dynamic-slice_fusion.7), channel_id=1, source_target_pairs={{8,1},{9,0},{10,3},{11,2},{12,5},{13,4},{14,7},{15,6},{16,9},{17,8... | collective-permute-start | bytes 49160 | tf_op jit(solution)/shard_map/ppermute | solution.py:71
  95.1 6.7 %collective-permute-start.15 = (bf16[1,1,1,8,128]{4,3,2,1,0:T(8,128)(2,1)S(1)}, bf16[1,1,1,8,128]{4,3,2,1,0:T(8,128)(2,1)S(1)}, u32[]{:S(2)}, u32[]{:S(2)}) collective-permute-start(bf16[1,1,1,8,128]{4,3,2,1,0:T(8,128)(2,1)S(1)} %constant_dynamic-slice_fusion.8), channel_id=1, source_target_pairs={{8,3},{9,2},{10,5},{11,4},{12,7},{13,6},{16,11},{17,10},{18,13},{1... | collective-permute-start | bytes 6152 | tf_op jit(solution)/shard_map/ppermute | solution.py:71
  106.4 16.5 %collective-permute-start.20 = (bf16[512,128]{1,0:T(8,128)(2,1)S(1)}, bf16[512,128]{1,0:T(8,128)(2,1)S(1)}, u32[]{:S(2)}, u32[]{:S(2)}) collective-permute-start(bf16[512,128]{1,0:T(8,128)(2,1)S(1)} %fusion.21), channel_id=1, source_target_pairs={{8,0},{16,8},{24,16},{9,1},{17,9},{25,17},{10,2},{18,10},{26,18},{... | collective-permute-start | bytes 393224 | tf_op jit(solution)/shard_map/ppermute | solution.py:208
  108.4 18.4 %collective-permute-start.22 = (bf16[1,1,8,8,128]{4,3,2,1,0:T(8,128)(2,1)S(1)}, bf16[1,1,8,8,128]{4,3,2,1,0:T(8,128)(2,1)S(1)}, u32[]{:S(2)}, u32[]{:S(2)}) collective-permute-start(bf16[1,1,8,8,128]{4,3,2,1,0:T(8,128)(2,1)S(1)} %get-tuple-element.54), channel_id=1, source_target_pairs={{8,2},{9,3},{10,4},{11,5},{12,6},{13,7},{16,10},{17,11},{18,12},{1... | collective-permute-start | bytes 49160 | tf_op jit(solution)/shard_map/ppermute | solution.py:71
  110.3 6.7 %collective-permute-start.21 = (bf16[1,1,1,8,128]{4,3,2,1,0:T(8,128)(2,1)S(1)}, bf16[1,1,1,8,128]{4,3,2,1,0:T(8,128)(2,1)S(1)}, u32[]{:S(2)}, u32[]{:S(2)}) collective-permute-start(bf16[1,1,1,8,128]{4,3,2,1,0:T(8,128)(2,1)S(1)} %constant_dynamic-slice_fusion.5), channel_id=1, source_target_pairs={{8,3},{9,2},{10,5},{11,4},{12,7},{13,6},{16,11},{17,10},{18,13},{1... | collective-permute-start | bytes 6152 | tf_op jit(solution)/shard_map/ppermute | solution.py:71
  112.3 14.5 %collective-permute-start.25 = (bf16[1,1,8,8,128]{4,3,2,1,0:T(8,128)(2,1)S(1)}, bf16[1,1,8,8,128]{4,3,2,1,0:T(8,128)(2,1)S(1)}, u32[]{:S(2)}, u32[]{:S(2)}) collective-permute-start(bf16[1,1,8,8,128]{4,3,2,1,0:T(8,128)(2,1)S(1)} %get-tuple-element.53), channel_id=1, source_target_pairs={{10,0},{11,1},{12,2},{13,3},{14,4},{15,5},{18,8},{19,9},{20,10},{2... | collective-permute-start | bytes 49160 | tf_op jit(solution)/shard_map/ppermute | solution.py:71
  114.2 8.6 %collective-permute-start.23 = (bf16[1,8,1,8,128]{4,3,2,1,0:T(8,128)(2,1)S(1)}, bf16[1,8,1,8,128]{4,3,2,1,0:T(8,128)(2,1)S(1)}, u32[]{:S(2)}, u32[]{:S(2)}) collective-permute-start(bf16[1,8,1,8,128]{4,3,2,1,0:T(8,128)(2,1)S(1)} %constant_dynamic-slice_fusion.4), channel_id=1, source_target_pairs={{8,1},{9,0},{10,3},{11,2},{12,5},{13,4},{14,7},{15,6},{16,9},{17,8... | collective-permute-start | bytes 49160 | tf_op jit(solution)/shard_map/ppermute | solution.py:71
  117.0 5.8 %collective-permute-start.24 = (bf16[1,1,1,8,128]{4,3,2,1,0:T(8,128)(2,1)S(1)}, bf16[1,1,1,8,128]{4,3,2,1,0:T(8,128)(2,1)S(1)}, u32[]{:S(2)}, u32[]{:S(2)}) collective-permute-start(bf16[1,1,1,8,128]{4,3,2,1,0:T(8,128)(2,1)S(1)} %constant_dynamic-slice_fusion.3), channel_id=1, source_target_pairs={{10,1},{11,0},{12,3},{13,2},{14,5},{15,4},{18,9},{19,8},{20,11},{2... | collective-permute-start | bytes 6152 | tf_op jit(solution)/shard_map/ppermute | solution.py:71
  127.8 6.7 %collective-permute-start.28 = (bf16[864,128]{1,0:T(8,128)(2,1)S(1)}, bf16[864,128]{1,0:T(8,128)(2,1)S(1)}, u32[]{:S(2)}, u32[]{:S(2)}) collective-permute-start(bf16[864,128]{1,0:T(8,128)(2,1)S(1)} %get-tuple-element.46), channel_id=1, source_target_pairs={{0,6},{2,0},{4,2},{6,4},{1,7},{3,1},{5,3},{7,5},{8,14},{10,8},{12,... | collective-permute-start | bytes 663560 | tf_op jit(solution)/shard_map/ppermute | solution.py:135
  130.0 11.0 %collective-permute-start.27 = (bf16[864,128]{1,0:T(8,128)(2,1)S(1)}, bf16[864,128]{1,0:T(8,128)(2,1)S(1)}, u32[]{:S(2)}, u32[]{:S(2)}) collective-permute-start(bf16[864,128]{1,0:T(8,128)(2,1)S(1)} %get-tuple-element.47), channel_id=1, source_target_pairs={{0,4},{2,6},{4,0},{6,2},{1,5},{3,7},{5,1},{7,3},{8,12},{10,14},{12... | collective-permute-start | bytes 663560 | tf_op jit(solution)/shard_map/ppermute | solution.py:135
  130.0 11.0 %collective-permute-start.26 = (bf16[864,128]{1,0:T(8,128)(2,1)S(1)}, bf16[864,128]{1,0:T(8,128)(2,1)S(1)}, u32[]{:S(2)}, u32[]{:S(2)}) collective-permute-start(bf16[864,128]{1,0:T(8,128)(2,1)S(1)} %get-tuple-element.45), channel_id=1, source_target_pairs={{0,2},{2,4},{4,6},{6,0},{1,3},{3,5},{5,7},{7,1},{8,10},{10,12},{12... | collective-permute-start | bytes 663560 | tf_op jit(solution)/shard_map/ppermute | solution.py:135
  133.3 9.4 %copy-start.3 = (bf16[512,128]{1,0:T(8,128)(2,1)S(1)}, bf16[512,128]{1,0:T(8,128)(2,1)}, u32[]{:S(2)}) copy-start(bf16[512,128]{1,0:T(8,128)(2,1)} %copy-done.2) | copy-start | bytes 393220
  133.3 9.4 %copy-start.5 = (bf16[512,128]{1,0:T(8,128)(2,1)S(1)}, bf16[512,128]{1,0:T(8,128)(2,1)}, u32[]{:S(2)}) copy-start(bf16[512,128]{1,0:T(8,128)(2,1)} %copy-done.4) | copy-start | bytes 393220
  141.1 3.0 %collective-permute-start.29 = (f32[864,128]{1,0:T(8,128)S(1)}, f32[864,128]{1,0:T(8,128)S(1)}, u32[]{:S(2)}, u32[]{:S(2)}) collective-permute-start(f32[864,128]{1,0:T(8,128)S(1)} %convert_add_fusion), channel_id=1, source_target_pairs={{0,1},{1,0},{2,3},{3,2},{4,5},{5,4},{6,7},{7,6},{8,9},{9,8},{10,11... | collective-permute-start | bytes 1327112 | tf_op jit(solution)/shard_map/ppermute | solution.py:213

commit v6 on v5

--- a/solution.py
+++ b/solution.py
@@ -54,7 +54,7 @@
     return jnp.concatenate(slabs_x, axis=1)
 
 
-def exchange(cube, axes, sizes, pipe_step):
+def exchange(cube, axes, sizes, pipe_step, carry=None, carried=None):
     n_pipe, n_x, n_y = sizes if pipe_step else (pipe_step + 1, *sizes)
 
     def linear(p, a, b):
@@ -70,14 +70,22 @@
                         route.append((linear(p, a, b), linear(p - pipe_step, ta, tb)))
         return lax.ppermute(piece, axes, route)
 
+    def face_x(shift_x):
+        face = face_piece(cube, shift_x, 0)
+        if carry is None:
+            return send(face, lambda a, b: (a - shift_x, b))
+        rows = carry.shape[-1]
+        payload = jnp.concatenate([carry, face.reshape(-1, rows)], axis=0)
+        got = send(payload, lambda a, b: ((a - shift_x) % n_x, b))
+        carried[(-shift_x) % n_x] = got[: carry.shape[0]]
+        return got[carry.shape[0] :].reshape(face.shape)
+
     received = {}
     if n_y == 2:
         place_y = lax.axis_index("sy")
         for shift_x in OFFSETS:
             if shift_x != 0:
-                received[(shift_x, 0)] = send(
-                    face_piece(cube, shift_x, 0), lambda a, b, i=shift_x: (a - i, b)
-                )
+                received[(shift_x, 0)] = face_x(shift_x)
             row = lax.dynamic_slice_in_dim(cube[:, source_range(shift_x)], (1 - place_y) * 7, 1, axis=2)
             got = send(row, lambda a, b, i=shift_x: (a - i, 1 - b))
             blank = jnp.zeros_like(got)
@@ -85,6 +93,9 @@
             received[(shift_x, -1)] = jnp.where(place_y == 1, got, blank)
         return received
     for shift_x, shift_y in directions():
+        if shift_y == 0:
+            received[(shift_x, 0)] = face_x(shift_x)
+            continue
         received[(shift_x, shift_y)] = send(
             face_piece(cube, shift_x, shift_y), lambda a, b, i=shift_x, j=shift_y: (a - i, b - j)
         )
@@ -113,12 +124,15 @@
     )
 
 
-def gathered(shard, axis):
+def gathered(shard, axis, given):
     count = lax.axis_size(axis)
     place = lax.axis_index(axis)
     parts = [shard]
     for step in range(1, count):
-        parts.append(lax.ppermute(shard, axis, [(i, (i + step) % count) for i in range(count)]))
+        if step in given:
+            parts.append(given[step])
+        else:
+            parts.append(lax.ppermute(shard, axis, [(i, (i + step) % count) for i in range(count)]))
     ordered = jnp.stack(parts)
     index = (place - jnp.arange(count)) % count
     slots = jnp.zeros((count,), jnp.int32).at[index].set(jnp.arange(count, dtype=jnp.int32))
@@ -156,8 +170,6 @@
     channels = segment_inputs.shape[5]
     blocks = row_count // 512
     taps = 27
-    weights = gathered(kernel[0], "sx")
-    flipped = weights.reshape(3, 3, 3, channels, channels)[::-1, ::-1, ::-1].transpose(0, 1, 2, 4, 3)
     gain_row = norm_gain[0]
     inputs = segment_inputs[0, :, 0, 0]
     cotangent = out_cotangent[:, 0, 0]
@@ -181,7 +193,14 @@
         start = cotangent[micro]
         start = jnp.where(live_now[:, None], start, jnp.zeros_like(start))
         both = jnp.concatenate([cube(activation), cube(start)], axis=-1)
-        got = exchange(both, ("sx", "sy"), (n_x, n_y), 0)
+        if micro == 0:
+            carried = {}
+            riding = kernel[0] if n_x >= 3 else None
+            got = exchange(both, ("sx", "sy"), (n_x, n_y), 0, riding, carried)
+            weights = gathered(kernel[0], "sx", carried)
+            flipped = weights.reshape(3, 3, 3, channels, channels)[::-1, ::-1, ::-1].transpose(0, 1, 2, 4, 3)
+        else:
+            got = exchange(both, ("sx", "sy"), (n_x, n_y), 0)
         both_pad = assemble(both, got, table)
         act_pad = both_pad[..., :channels]
         centre = start

time: 146 us -> 145 us (level)
  starting transfers between devices: 59.1 us -> 51 us
  other arithmetic: 14.1 us -> 20.7 us
  waiting for transfers between devices: 27.7 us -> 29.3 us
    concatenate x1, other arithmetic: 2.13 us -> 7.83 us  [assemble(): return jnp.concatenate(slabs_x, axis=1)]
    ppermute x20, starting transfers between devices: 46.2 us -> 41.6 us  [send(): return lax.ppermute(piece, axes, route)]
    ppermute x3 -> x1, starting transfers between devices: 2.45 us -> 0.33 us  [gathered(): lax.ppermute(shard, axis, [(i, (i + step) % count) for i in range(count)])]
    ppermute x20, waiting for transfers between devices: 20 us -> 21.6 us  [send(): return lax.ppermute(piece, axes, route)]
  transfers between devices with their start and end apart: 30 -> 28, of which waited for: 10 -> 8; matrix products, arithmetic and copies ran while one was open for 14% -> 10% of each run, Pallas kernels for 0% -> 0%
where the time goes in v6:
time: 145 us; the launch traced here: 144 us
  starting transfers between devices  51 us (35%)
  waiting for transfers between devices  29.3 us (20%)
  other arithmetic  20.7 us (14%)
  between operations  19.8 us (14%)
  matrix products  15.8 us (11%)
  local copies, waits for them, and re-layouts  7.1 us (5%)
    ppermute x20, starting transfers between devices, send(): return lax.ppermute(piece, axes, route)  41.6 us
    ppermute x20, waiting for transfers between devices, send(): return lax.ppermute(piece, axes, route)  21.6 us
    conv_general_dilated x4, matrix products, conv_data(): lax.conv_general_dilated(padded, filters, (1, 1, 1), 'VALID', dimension_n...  11.8 us
    concatenate x1, other arithmetic, assemble(): return jnp.concatenate(slabs_x, axis=1)  7.83 us
    ppermute x3, waiting for transfers between devices, scattered_sum(): lax.ppermute(piece, axis, [(i, (i + step) % count) for i in range(count)])  7.33 us
    ppermute x3, starting transfers between devices, shards(): centre = lax.ppermute(result, 'pipe', down)  5.76 us
    transpose x1, matrix products, shards(): per_tap.transpose(1, 2, 3, 0, 4).reshape(taps * channels, channels)  3.93 us
  transfers between devices with their start and end apart: 28, of which 8 were waited for; matrix products, arithmetic and copies ran while one was open for 10% of the time, Pallas kernels for 0%

profile of v6, /device:TPU:21, one launch (start us, length us, event | category | flops | bytes accessed | tf_op | source)
XLA Modules:
  0.0 143.5 jit_solution(2939854064643318327)
XLA Ops:
  0.6 1.0 convert_element_type.160
  1.6 1.1 fusion.25
  3.5 1.0 broadcast_select_fusion.12
  4.5 0.8 multiply_convert_fusion.2
  5.4 3.6 %collective-permute-start.3 = (bf16[1,1,1,8,256]{4,3,2,1,0:T(8,128)(2,1)S(1)}, bf16[1,1,1,8,256]{4,3,2,1,0:T(8,128)(2,1)S(1)}, u32[]{:S(2)}, u32[]{:S(2)}) collective-permute-start(bf16[1,1,1,8,256]{4,3,2,1,0:T(8,128)(2,1)S(1)} %fusion.59), channel_id=1, source_target_pairs={{2,1},{3,0},{4,3},{5,2},{6,5},{7,4},{10,9},{11,8},{12,11},{13,10},... | collective-permute-start | bytes 12296 | tf_op jit(solution)/shard_map/ppermute | solution.py:71
  9.1 1.9 %collective-permute-start = (bf16[1,1,1,8,256]{4,3,2,1,0:T(8,128)(2,1)S(1)}, bf16[1,1,1,8,256]{4,3,2,1,0:T(8,128)(2,1)S(1)}, u32[]{:S(2)}, u32[]{:S(2)}) collective-permute-start(bf16[1,1,1,8,256]{4,3,2,1,0:T(8,128)(2,1)S(1)} %constant_dynamic-slice_fusion.14), channel_id=1, source_target_pairs={{0,3},{1,2},{2,5},{3,4},{4,7},{5,6},{8,11},{9,10},{10,13},{11,12},... | collective-permute-start | bytes 12296 | tf_op jit(solution)/shard_map/ppermute | solution.py:71
  11.0 0.3 collective-permute-start.5
  11.4 1.9 %collective-permute-start.4 = (bf16[992,128]{1,0:T(8,128)(2,1)S(1)}, bf16[992,128]{1,0:T(8,128)(2,1)S(1)}, u32[]{:S(2)}, u32[]{:S(2)}) collective-permute-start(bf16[992,128]{1,0:T(8,128)(2,1)S(1)} %get-tuple-element.57), channel_id=1, source_target_pairs={{0,6},{1,7},{2,0},{3,1},{4,2},{5,3},{6,4},{7,5},{8,14},{9,15},{10,... | collective-permute-start | bytes 761864 | tf_op jit(solution)/shard_map/ppermute | solution.py:71
  13.3 1.0 collective-permute-start.2
  14.4 0.7 fusion.76
  15.1 0.7 fusion.77
  18.1 0.6 scatter_custom_fusion
  18.7 0.6 pad_clamp_fusion
  19.3 0.5 fusion.60
  19.8 0.4 copy_dynamic-update-slice_fusion
  20.2 0.6 broadcast_select_fusion
  35.9 0.3 collective-permute-start.1
  36.9 7.7 %collective-permute-done.1 = bf16[992,128]{1,0:T(8,128)(2,1)S(1)} collective-permute-done((bf16[992,128]{1,0:T(8,128)(2,1)S(1)}, bf16[992,128]{1,0:T(8,128)(2,1)S(1)}, u32[]{:S(2)}, u32[]{:S(2)}) %collective-permute-start.1) | collective-permute-done | bytes 253984 | tf_op jit(solution)/shard_map/ppermute | solution.py:71
  44.7 0.5 copy-done.11
  45.2 1.0 pad_maximum_fusion
  46.3 0.8 gather_fusion
  47.1 1.0 rev.3
  48.1 7.8 %maximum_maximum_fusion = bf16[1,10,10,10,256]{4,0,3,2,1:T(2,128)(2,1)S(1)} fusion(bf16[1,1,1,10,256]{4,0,3,2,1:T(2,128)(2,1)S(1)} %copy.47, bf16[1,1,8,1,256]{4,0,3,2,1:T(2,128)(2,1)S(1)} %slice.562, bf16[1,1,8,8,256]{4,0,3,2,1:T(2,128)(2,1)S(1)} %select_n.1002, bf16[1,1,8,1,256]{4,0,3,2,1:T(2,128)(2,1)S(1)} %slice.561, ...), kind=kLoop, calls=%fused_computation.4 | loop fusion | flops 3584000 | bytes 1024000 | tf_op jit(solution)/shard_map/concatenate | solution.py:54
  56.0 2.9 %fusion.1 = f32[1,8,8,8,128]{4,0,3,2,1:T(1,128)S(1)} fusion(bf16[3,3,3,128,128]{4,3,2,1,0:T(8,128)(2,1)S(1)} %copy-done.4, bf16[1,10,10,10,256]{4,0,3,2,1:T(2,128)(2,1)S(1)} %maximum_maximum_fusion), kind=kOutput, calls=%fused_computation.10 | convolution fusion | flops 452984832 | bytes 1658880 | tf_op jit(solution)/shard_map/conv_general_dilated | solution.py:106
  59.0 0.3 fusion.47
  59.8 2.6 %collective-permute-start.11 = (bf16[1,1,8,8,128]{4,3,2,1,0:T(8,128)(2,1)S(1)}, bf16[1,1,8,8,128]{4,3,2,1,0:T(8,128)(2,1)S(1)}, u32[]{:S(2)}, u32[]{:S(2)}) collective-permute-start(bf16[1,1,8,8,128]{4,3,2,1,0:T(8,128)(2,1)S(1)} %get-tuple-element.69), channel_id=1, source_target_pairs={{10,0},{11,1},{12,2},{13,3},{14,4},{15,5},{18,8},{19,9},{20,10},{2... | collective-permute-start | bytes 49160 | tf_op jit(solution)/shard_map/ppermute | solution.py:71
  62.4 2.5 %collective-permute-start.8 = (bf16[1,1,8,8,128]{4,3,2,1,0:T(8,128)(2,1)S(1)}, bf16[1,1,8,8,128]{4,3,2,1,0:T(8,128)(2,1)S(1)}, u32[]{:S(2)}, u32[]{:S(2)}) collective-permute-start(bf16[1,1,8,8,128]{4,3,2,1,0:T(8,128)(2,1)S(1)} %get-tuple-element.68), channel_id=1, source_target_pairs={{8,2},{9,3},{10,4},{11,5},{12,6},{13,7},{16,10},{17,11},{18,12},{1... | collective-permute-start | bytes 49160 | tf_op jit(solution)/shard_map/ppermute | solution.py:71
  64.9 4.3 %collective-permute-start.10 = (bf16[1,1,1,8,128]{4,3,2,1,0:T(8,128)(2,1)S(1)}, bf16[1,1,1,8,128]{4,3,2,1,0:T(8,128)(2,1)S(1)}, u32[]{:S(2)}, u32[]{:S(2)}) collective-permute-start(bf16[1,1,1,8,128]{4,3,2,1,0:T(8,128)(2,1)S(1)} %constant_dynamic-slice_fusion.9), channel_id=1, source_target_pairs={{10,1},{11,0},{12,3},{13,2},{14,5},{15,4},{18,9},{19,8},{20,11},{2... | collective-permute-start | bytes 6152 | tf_op jit(solution)/shard_map/ppermute | solution.py:71
  69.6 1.9 %collective-permute-start.6 = (bf16[512,128]{1,0:T(8,128)(2,1)S(1)}, bf16[512,128]{1,0:T(8,128)(2,1)S(1)}, u32[]{:S(2)}, u32[]{:S(2)}) collective-permute-start(bf16[512,128]{1,0:T(8,128)(2,1)S(1)} %fusion.8), channel_id=1, source_target_pairs={{8,0},{16,8},{24,16},{9,1},{17,9},{25,17},{10,2},{18,10},{26,18},{... | collective-permute-start | bytes 393224 | tf_op jit(solution)/shard_map/ppermute | solution.py:227
  71.5 1.9 %collective-permute-start.9 = (bf16[1,8,1,8,128]{4,3,2,1,0:T(8,128)(2,1)S(1)}, bf16[1,8,1,8,128]{4,3,2,1,0:T(8,128)(2,1)S(1)}, u32[]{:S(2)}, u32[]{:S(2)}) collective-permute-start(bf16[1,8,1,8,128]{4,3,2,1,0:T(8,128)(2,1)S(1)} %constant_dynamic-slice_fusion.10), channel_id=1, source_target_pairs={{8,1},{9,0},{10,3},{11,2},{12,5},{13,4},{14,7},{15,6},{16,9},{17,8... | collective-permute-start | bytes 49160 | tf_op jit(solution)/shard_map/ppermute | solution.py:71
  73.4 2.1 %collective-permute-start.7 = (bf16[1,1,1,8,128]{4,3,2,1,0:T(8,128)(2,1)S(1)}, bf16[1,1,1,8,128]{4,3,2,1,0:T(8,128)(2,1)S(1)}, u32[]{:S(2)}, u32[]{:S(2)}) collective-permute-start(bf16[1,1,1,8,128]{4,3,2,1,0:T(8,128)(2,1)S(1)} %constant_dynamic-slice_fusion.11), channel_id=1, source_target_pairs={{8,3},{9,2},{10,5},{11,4},{12,7},{13,6},{16,11},{17,10},{18,13},{1... | collective-permute-start | bytes 6152 | tf_op jit(solution)/shard_map/ppermute | solution.py:71
  75.6 4.6 %collective-permute-done.7 = bf16[1,1,1,8,128]{4,3,2,1,0:T(8,128)(2,1)S(1)} collective-permute-done((bf16[1,1,1,8,128]{4,3,2,1,0:T(8,128)(2,1)S(1)}, bf16[1,1,1,8,128]{4,3,2,1,0:T(8,128)(2,1)S(1)}, u32[]{:S(2)}, u32[]{:S(2)}) %collective-permute-start.7) | collective-permute-done | bytes 2080 | tf_op jit(solution)/shard_map/ppermute | solution.py:71
  81.1 2.9 %fusion.5 = f32[1,8,8,8,128]{4,0,3,2,1:T(1,128)S(1)} fusion(bf16[3,3,3,128,128]{4,3,2,1,0:T(8,128)(2,1)S(1)} %bitcast.208, bf16[1,1,10,10,128]{4,0,3,2,1:T(2,128)(2,1)S(1)} %copy.56, bf16[1,8,1,10,128]{4,0,3,2,1:T(2,128)(2,1)S(1)} %copy.54, bf16[1,8,8,1,128]{4,0,3,2,1:T(2,128)(2,1)S(1)} %slice_bitcast_fusion.6, bf16[1,8,8,8,128]{4,0,3,2,1:T(2,128)(2,1)S(1)} %copy.52, ...), kind=kOutput, calls=%fused_computation.14 | convolution fusion | flops 454776832 | bytes 1402880 | tf_op jit(solution)/shard_map/conv_general_dilated | solution.py:106
  84.1 0.3 fusion.48
  84.4 0.3 fusion.18
  84.7 1.9 %collective-permute-start.12 = (bf16[512,128]{1,0:T(8,128)(2,1)S(1)}, bf16[512,128]{1,0:T(8,128)(2,1)S(1)}, u32[]{:S(2)}, u32[]{:S(2)}) collective-permute-start(bf16[512,128]{1,0:T(8,128)(2,1)S(1)} %fusion.18), channel_id=1, source_target_pairs={{8,0},{16,8},{24,16},{9,1},{17,9},{25,17},{10,2},{18,10},{26,18},{... | collective-permute-start | bytes 393224 | tf_op jit(solution)/shard_map/ppermute | solution.py:227
  86.7 1.9 %collective-permute-start.17 = (bf16[1,1,8,8,128]{4,3,2,1,0:T(8,128)(2,1)S(1)}, bf16[1,1,8,8,128]{4,3,2,1,0:T(8,128)(2,1)S(1)}, u32[]{:S(2)}, u32[]{:S(2)}) collective-permute-start(bf16[1,1,8,8,128]{4,3,2,1,0:T(8,128)(2,1)S(1)} %get-tuple-element.64), channel_id=1, source_target_pairs={{10,0},{11,1},{12,2},{13,3},{14,4},{15,5},{18,8},{19,9},{20,10},{2... | collective-permute-start | bytes 49160 | tf_op jit(solution)/shard_map/ppermute | solution.py:71
  88.6 1.9 %collective-permute-start.16 = (bf16[1,1,1,8,128]{4,3,2,1,0:T(8,128)(2,1)S(1)}, bf16[1,1,1,8,128]{4,3,2,1,0:T(8,128)(2,1)S(1)}, u32[]{:S(2)}, u32[]{:S(2)}) collective-permute-start(bf16[1,1,1,8,128]{4,3,2,1,0:T(8,128)(2,1)S(1)} %constant_dynamic-slice_fusion.6), channel_id=1, source_target_pairs={{10,1},{11,0},{12,3},{13,2},{14,5},{15,4},{18,9},{19,8},{20,11},{2... | collective-permute-start | bytes 6152 | tf_op jit(solution)/shard_map/ppermute | solution.py:71
  90.6 1.9 %collective-permute-start.14 = (bf16[1,1,8,8,128]{4,3,2,1,0:T(8,128)(2,1)S(1)}, bf16[1,1,8,8,128]{4,3,2,1,0:T(8,128)(2,1)S(1)}, u32[]{:S(2)}, u32[]{:S(2)}) collective-permute-start(bf16[1,1,8,8,128]{4,3,2,1,0:T(8,128)(2,1)S(1)} %get-tuple-element.63), channel_id=1, source_target_pairs={{8,2},{9,3},{10,4},{11,5},{12,6},{13,7},{16,10},{17,11},{18,12},{1... | collective-permute-start | bytes 49160 | tf_op jit(solution)/shard_map/ppermute | solution.py:71
  92.5 1.9 %collective-permute-start.15 = (bf16[1,8,1,8,128]{4,3,2,1,0:T(8,128)(2,1)S(1)}, bf16[1,8,1,8,128]{4,3,2,1,0:T(8,128)(2,1)S(1)}, u32[]{:S(2)}, u32[]{:S(2)}) collective-permute-start(bf16[1,8,1,8,128]{4,3,2,1,0:T(8,128)(2,1)S(1)} %constant_dynamic-slice_fusion.7), channel_id=1, source_target_pairs={{8,1},{9,0},{10,3},{11,2},{12,5},{13,4},{14,7},{15,6},{16,9},{17,8... | collective-permute-start | bytes 49160 | tf_op jit(solution)/shard_map/ppermute | solution.py:71
  94.4 1.9 %collective-permute-start.13 = (bf16[1,1,1,8,128]{4,3,2,1,0:T(8,128)(2,1)S(1)}, bf16[1,1,1,8,128]{4,3,2,1,0:T(8,128)(2,1)S(1)}, u32[]{:S(2)}, u32[]{:S(2)}) collective-permute-start(bf16[1,1,1,8,128]{4,3,2,1,0:T(8,128)(2,1)S(1)} %constant_dynamic-slice_fusion.8), channel_id=1, source_target_pairs={{8,3},{9,2},{10,5},{11,4},{12,7},{13,6},{16,11},{17,10},{18,13},{1... | collective-permute-start | bytes 6152 | tf_op jit(solution)/shard_map/ppermute | solution.py:71
  96.4 4.8 %collective-permute-done.13 = bf16[1,1,1,8,128]{4,3,2,1,0:T(8,128)(2,1)S(1)} collective-permute-done((bf16[1,1,1,8,128]{4,3,2,1,0:T(8,128)(2,1)S(1)}, bf16[1,1,1,8,128]{4,3,2,1,0:T(8,128)(2,1)S(1)}, u32[]{:S(2)}, u32[]{:S(2)}) %collective-permute-start.13) | collective-permute-done | bytes 2080 | tf_op jit(solution)/shard_map/ppermute | solution.py:71
  102.1 2.9 %fusion.4 = f32[1,8,8,8,128]{4,0,3,2,1:T(1,128)S(1)} fusion(bf16[3,3,3,128,128]{4,3,2,1,0:T(8,128)(2,1)S(1)} %bitcast.209, bf16[1,1,10,10,128]{4,0,3,2,1:T(2,128)(2,1)S(1)} %copy.63, bf16[1,8,1,10,128]{4,0,3,2,1:T(2,128)(2,1)S(1)} %copy.61, bf16[1,8,8,1,128]{4,0,3,2,1:T(2,128)(2,1)S(1)} %slice_bitcast_fusion.4, bf16[1,8,8,8,128]{4,0,3,2,1:T(2,128)(2,1)S(1)} %copy.59, ...), kind=kOutput, calls=%fused_computation.13 | convolution fusion | flops 454776832 | bytes 1402880 | tf_op jit(solution)/shard_map/conv_general_dilated | solution.py:106
  105.1 0.3 fusion.49
  105.4 0.3 fusion.21
  105.7 1.9 %collective-permute-start.18 = (bf16[512,128]{1,0:T(8,128)(2,1)S(1)}, bf16[512,128]{1,0:T(8,128)(2,1)S(1)}, u32[]{:S(2)}, u32[]{:S(2)}) collective-permute-start(bf16[512,128]{1,0:T(8,128)(2,1)S(1)} %fusion.21), channel_id=1, source_target_pairs={{8,0},{16,8},{24,16},{9,1},{17,9},{25,17},{10,2},{18,10},{26,18},{... | collective-permute-start | bytes 393224 | tf_op jit(solution)/shard_map/ppermute | solution.py:227
  107.7 1.9 %collective-permute-start.20 = (bf16[1,1,8,8,128]{4,3,2,1,0:T(8,128)(2,1)S(1)}, bf16[1,1,8,8,128]{4,3,2,1,0:T(8,128)(2,1)S(1)}, u32[]{:S(2)}, u32[]{:S(2)}) collective-permute-start(bf16[1,1,8,8,128]{4,3,2,1,0:T(8,128)(2,1)S(1)} %get-tuple-element.62), channel_id=1, source_target_pairs={{8,2},{9,3},{10,4},{11,5},{12,6},{13,7},{16,10},{17,11},{18,12},{1... | collective-permute-start | bytes 49160 | tf_op jit(solution)/shard_map/ppermute | solution.py:71
  109.6 1.9 %collective-permute-start.19 = (bf16[1,1,1,8,128]{4,3,2,1,0:T(8,128)(2,1)S(1)}, bf16[1,1,1,8,128]{4,3,2,1,0:T(8,128)(2,1)S(1)}, u32[]{:S(2)}, u32[]{:S(2)}) collective-permute-start(bf16[1,1,1,8,128]{4,3,2,1,0:T(8,128)(2,1)S(1)} %constant_dynamic-slice_fusion.5), channel_id=1, source_target_pairs={{8,3},{9,2},{10,5},{11,4},{12,7},{13,6},{16,11},{17,10},{18,13},{1... | collective-permute-start | bytes 6152 | tf_op jit(solution)/shard_map/ppermute | solution.py:71
  111.6 1.9 %collective-permute-start.23 = (bf16[1,1,8,8,128]{4,3,2,1,0:T(8,128)(2,1)S(1)}, bf16[1,1,8,8,128]{4,3,2,1,0:T(8,128)(2,1)S(1)}, u32[]{:S(2)}, u32[]{:S(2)}) collective-permute-start(bf16[1,1,8,8,128]{4,3,2,1,0:T(8,128)(2,1)S(1)} %get-tuple-element.61), channel_id=1, source_target_pairs={{10,0},{11,1},{12,2},{13,3},{14,4},{15,5},{18,8},{19,9},{20,10},{2... | collective-permute-start | bytes 49160 | tf_op jit(solution)/shard_map/ppermute | solution.py:71
  113.5 1.9 %collective-permute-start.21 = (bf16[1,8,1,8,128]{4,3,2,1,0:T(8,128)(2,1)S(1)}, bf16[1,8,1,8,128]{4,3,2,1,0:T(8,128)(2,1)S(1)}, u32[]{:S(2)}, u32[]{:S(2)}) collective-permute-start(bf16[1,8,1,8,128]{4,3,2,1,0:T(8,128)(2,1)S(1)} %constant_dynamic-slice_fusion.4), channel_id=1, source_target_pairs={{8,1},{9,0},{10,3},{11,2},{12,5},{13,4},{14,7},{15,6},{16,9},{17,8... | collective-permute-start | bytes 49160 | tf_op jit(solution)/shard_map/ppermute | solution.py:71
  115.4 0.9 collective-permute-done.19
  116.3 2.1 %collective-permute-start.22 = (bf16[1,1,1,8,128]{4,3,2,1,0:T(8,128)(2,1)S(1)}, bf16[1,1,1,8,128]{4,3,2,1,0:T(8,128)(2,1)S(1)}, u32[]{:S(2)}, u32[]{:S(2)}) collective-permute-start(bf16[1,1,1,8,128]{4,3,2,1,0:T(8,128)(2,1)S(1)} %constant_dynamic-slice_fusion.3), channel_id=1, source_target_pairs={{10,1},{11,0},{12,3},{13,2},{14,5},{15,4},{18,9},{19,8},{20,11},{2... | collective-permute-start | bytes 6152 | tf_op jit(solution)/shard_map/ppermute | solution.py:71
  118.5 3.6 %collective-permute-done.22 = bf16[1,1,1,8,128]{4,3,2,1,0:T(8,128)(2,1)S(1)} collective-permute-done((bf16[1,1,1,8,128]{4,3,2,1,0:T(8,128)(2,1)S(1)}, bf16[1,1,1,8,128]{4,3,2,1,0:T(8,128)(2,1)S(1)}, u32[]{:S(2)}, u32[]{:S(2)}) %collective-permute-start.22) | collective-permute-done | bytes 2080 | tf_op jit(solution)/shard_map/ppermute | solution.py:71
  122.3 3.9 %multiply_convert_fusion = bf16[3,3,3,128,128]{4,3,2,1,0:T(8,128)(2,1)S(1)} fusion(bf16[1,10,10,10,256]{4,0,3,2,1:T(2,128)(2,1)S(1)} %copy-done.3, bf16[1,8,8,8,128]{4,3,2,1,0:T(8,128)(2,1)S(1)} %bitcast.242), kind=kOutput, calls=%fused_computation.2 | convolution fusion | flops 453869568 | bytes 1527808 | tf_op jit(solution)/shard_map/transpose | solution.py:215
  127.3 1.3 collective-permute-start.26
  128.5 0.4 collective-permute-start.24
  128.9 3.0 %fusion.3 = f32[1,8,8,8,128]{4,0,3,2,1:T(1,128)S(1)} fusion(bf16[3,3,3,128,128]{4,3,2,1,0:T(8,128)(2,1)S(1)} %bitcast.210, bf16[1,1,10,10,128]{4,0,3,2,1:T(2,128)(2,1)S(1)} %copy.71, bf16[1,8,1,10,128]{4,0,3,2,1:T(2,128)(2,1)S(1)} %copy.69, bf16[1,8,8,1,128]{4,0,3,2,1:T(2,128)(2,1)S(1)} %slice_bitcast_fusion.2, bf16[1,8,8,8,128]{4,0,3,2,1:T(2,128)(2,1)S(1)} %copy.67, ...), kind=kOutput, calls=%fused_computation.12 | convolution fusion | flops 454776832 | bytes 1402880 | tf_op jit(solution)/shard_map/conv_general_dilated | solution.py:106
  131.9 0.3 fusion.50
  132.3 2.1 %collective-permute-done.26 = bf16[864,128]{1,0:T(8,128)(2,1)S(1)} collective-permute-done((bf16[864,128]{1,0:T(8,128)(2,1)S(1)}, bf16[864,128]{1,0:T(8,128)(2,1)S(1)}, u32[]{:S(2)}, u32[]{:S(2)}) %collective-permute-start.26) | collective-permute-done | bytes 221216 | tf_op jit(solution)/shard_map/ppermute | solution.py:149
  134.3 5.3 %collective-permute-done.25 = bf16[864,128]{1,0:T(8,128)(2,1)S(1)} collective-permute-done((bf16[864,128]{1,0:T(8,128)(2,1)S(1)}, bf16[864,128]{1,0:T(8,128)(2,1)S(1)}, u32[]{:S(2)}, u32[]{:S(2)}) %collective-permute-start.25) | collective-permute-done | bytes 221216 | tf_op jit(solution)/shard_map/ppermute | solution.py:149
  139.7 1.6 %collective-permute-start.27 = (f32[864,128]{1,0:T(8,128)S(1)}, f32[864,128]{1,0:T(8,128)S(1)}, u32[]{:S(2)}, u32[]{:S(2)}) collective-permute-start(f32[864,128]{1,0:T(8,128)S(1)} %convert_add_fusion), channel_id=1, source_target_pairs={{0,1},{1,0},{2,3},{3,2},{4,5},{5,4},{6,7},{7,6},{8,9},{9,8},{10,11... | collective-permute-start | bytes 1327112 | tf_op jit(solution)/shard_map/ppermute | solution.py:232
  141.3 1.0 fusion.53
  142.3 0.4 collective-permute-done.27
  142.7 0.8 add_bitcast_fusion
  (217 shorter events, 5.0 us)
Async XLA Ops:
  0.6 10.4 %copy-start.5 = (bf16[1,864,128]{2,1,0:T(8,128)(2,1)S(1)}, bf16[1,864,128]{2,1,0:T(8,128)(2,1)}, u32[]{:S(2)}) copy-start(bf16[1,864,128]{2,1,0:T(8,128)(2,1)} %param.11) | copy-start | bytes 663556
  5.3 9.0 %copy-start.10 = (s32[1,1,1,1,27]{4,3,2,1,0:T(1,128)S(1)}, s32[1,1,1,1,27]{4,3,2,1,0:T(1,128)}, u32[]{:S(2)}) copy-start(s32[1,1,1,1,27]{4,3,2,1,0:T(1,128)} %param.8) | copy-start | bytes 328
  5.4 10.4 %copy-start.12 = (f32[1,128]{1,0:T(1,128)S(1)}, f32[1,128]{1,0:T(1,128)}, u32[]{:S(2)}) copy-start(f32[1,128]{1,0:T(1,128)} %param.10) | copy-start | bytes 1540
  5.4 30.5 %collective-permute-start.3 = (bf16[1,1,1,8,256]{4,3,2,1,0:T(8,128)(2,1)S(1)}, bf16[1,1,1,8,256]{4,3,2,1,0:T(8,128)(2,1)S(1)}, u32[]{:S(2)}, u32[]{:S(2)}) collective-permute-start(bf16[1,1,1,8,256]{4,3,2,1,0:T(8,128)(2,1)S(1)} %fusion.59), channel_id=1, source_target_pairs={{2,1},{3,0},{4,3},{5,2},{6,5},{7,4},{10,9},{11,8},{12,11},{13,10},... | collective-permute-start | bytes 12296 | tf_op jit(solution)/shard_map/ppermute | solution.py:71
  9.1 27.1 %collective-permute-start = (bf16[1,1,1,8,256]{4,3,2,1,0:T(8,128)(2,1)S(1)}, bf16[1,1,1,8,256]{4,3,2,1,0:T(8,128)(2,1)S(1)}, u32[]{:S(2)}, u32[]{:S(2)}) collective-permute-start(bf16[1,1,1,8,256]{4,3,2,1,0:T(8,128)(2,1)S(1)} %constant_dynamic-slice_fusion.14), channel_id=1, source_target_pairs={{0,3},{1,2},{2,5},{3,4},{4,7},{5,6},{8,11},{9,10},{10,13},{11,12},... | collective-permute-start | bytes 12296 | tf_op jit(solution)/shard_map/ppermute | solution.py:71
  11.0 33.7 %collective-permute-start.5 = (bf16[864,128]{1,0:T(8,128)(2,1)S(1)}, bf16[864,128]{1,0:T(8,128)(2,1)}, u32[]{:S(2)}, u32[]{:S(2)}) collective-permute-start(bf16[864,128]{1,0:T(8,128)(2,1)S(1)} %bitcast.223), channel_id=1, source_target_pairs={{0,4},{2,6},{4,0},{6,2},{1,5},{3,7},{5,1},{7,3},{8,12},{10,14},{12... | collective-permute-start | bytes 663560 | tf_op jit(solution)/shard_map/ppermute | solution.py:135
  11.4 4.8 %copy-start.1 = (bf16[1,1,1,512,128]{4,3,2,1,0:T(8,128)(2,1)S(1)}, bf16[1,1,1,512,128]{4,3,2,1,0:T(8,128)(2,1)}, u32[]{:S(2)}) copy-start(bf16[1,1,1,512,128]{4,3,2,1,0:T(8,128)(2,1)} %param.7) | copy-start | bytes 393220
  11.4 25.3 %collective-permute-start.4 = (bf16[992,128]{1,0:T(8,128)(2,1)S(1)}, bf16[992,128]{1,0:T(8,128)(2,1)S(1)}, u32[]{:S(2)}, u32[]{:S(2)}) collective-permute-start(bf16[992,128]{1,0:T(8,128)(2,1)S(1)} %get-tuple-element.57), channel_id=1, source_target_pairs={{0,6},{1,7},{2,0},{3,1},{4,2},{5,3},{6,4},{7,5},{8,14},{9,15},{10,... | collective-permute-start | bytes 761864 | tf_op jit(solution)/shard_map/ppermute | solution.py:71
  13.3 23.1 %collective-permute-start.2 = (bf16[1,8,1,8,256]{4,3,2,1,0:T(8,128)(2,1)S(1)}, bf16[1,8,1,8,256]{4,3,2,1,0:T(8,128)(2,1)S(1)}, u32[]{:S(2)}, u32[]{:S(2)}) collective-permute-start(bf16[1,8,1,8,256]{4,3,2,1,0:T(8,128)(2,1)S(1)} %fusion.56), channel_id=1, source_target_pairs={{0,1},{1,0},{2,3},{3,2},{4,5},{5,4},{6,7},{7,6},{8,9},{9,8},{10,11... | collective-permute-start | bytes 98312 | tf_op jit(solution)/shard_map/ppermute | solution.py:71
  35.9 8.7 %collective-permute-start.1 = (bf16[992,128]{1,0:T(8,128)(2,1)S(1)}, bf16[992,128]{1,0:T(8,128)(2,1)S(1)}, u32[]{:S(2)}, u32[]{:S(2)}) collective-permute-start(bf16[992,128]{1,0:T(8,128)(2,1)S(1)} %get-tuple-element.56), channel_id=1, source_target_pairs={{0,2},{1,3},{2,4},{3,5},{4,6},{5,7},{6,0},{7,1},{8,10},{9,11},{10,... | collective-permute-start | bytes 761864 | tf_op jit(solution)/shard_map/ppermute | solution.py:71
  44.6 0.6 copy-start.11
  47.1 1.0 slice-start
  48.1 7.8 %copy-start.4 = (bf16[3,3,3,128,128]{4,3,2,1,0:T(8,128)(2,1)S(1)}, bf16[3,3,3,128,128]{4,3,2,1,0:T(8,128)(2,1)}, u32[]{:S(2)}) copy-start(bf16[3,3,3,128,128]{4,3,2,1,0:T(8,128)(2,1)} %rev.3) | copy-start | bytes 2654212
  56.0 3.0 %copy-start.2 = (bf16[1,10,10,10,256]{4,0,3,2,1:T(2,128)(2,1)}, bf16[1,10,10,10,256]{4,0,3,2,1:T(2,128)(2,1)S(1)}, u32[]{:S(2)}) copy-start(bf16[1,10,10,10,256]{4,0,3,2,1:T(2,128)(2,1)S(1)} %maximum_maximum_fusion) | copy-start | bytes 1536004
  56.0 3.0 %copy-start = (bf16[1,1,1,1,512,128]{5,4,3,2,1,0:T(8,128)(2,1)S(1)}, bf16[1,1,1,1,512,128]{5,4,3,2,1,0:T(8,128)(2,1)}, u32[]{:S(2)}) copy-start(bf16[1,1,1,1,512,128]{5,4,3,2,1,0:T(8,128)(2,1)} %param.6) | copy-start | bytes 393220
  59.0 10.3 %copy-start.13 = (pred[512]{0:T(512)(128)(4,1)S(1)}, pred[512]{0:T(512)(128)(4,1)}, u32[]{:S(2)}) copy-start(pred[512]{0:T(512)(128)(4,1)} %fusion.60) | copy-start | bytes 1540
  59.8 20.5 %collective-permute-start.11 = (bf16[1,1,8,8,128]{4,3,2,1,0:T(8,128)(2,1)S(1)}, bf16[1,1,8,8,128]{4,3,2,1,0:T(8,128)(2,1)S(1)}, u32[]{:S(2)}, u32[]{:S(2)}) collective-permute-start(bf16[1,1,8,8,128]{4,3,2,1,0:T(8,128)(2,1)S(1)} %get-tuple-element.69), channel_id=1, source_target_pairs={{10,0},{11,1},{12,2},{13,3},{14,4},{15,5},{18,8},{19,9},{20,10},{2... | collective-permute-start | bytes 49160 | tf_op jit(solution)/shard_map/ppermute | solution.py:71
  62.4 18.1 %collective-permute-start.8 = (bf16[1,1,8,8,128]{4,3,2,1,0:T(8,128)(2,1)S(1)}, bf16[1,1,8,8,128]{4,3,2,1,0:T(8,128)(2,1)S(1)}, u32[]{:S(2)}, u32[]{:S(2)}) collective-permute-start(bf16[1,1,8,8,128]{4,3,2,1,0:T(8,128)(2,1)S(1)} %get-tuple-element.68), channel_id=1, source_target_pairs={{8,2},{9,3},{10,4},{11,5},{12,6},{13,7},{16,10},{17,11},{18,12},{1... | collective-permute-start | bytes 49160 | tf_op jit(solution)/shard_map/ppermute | solution.py:71
  64.9 8.6 %collective-permute-start.10 = (bf16[1,1,1,8,128]{4,3,2,1,0:T(8,128)(2,1)S(1)}, bf16[1,1,1,8,128]{4,3,2,1,0:T(8,128)(2,1)S(1)}, u32[]{:S(2)}, u32[]{:S(2)}) collective-permute-start(bf16[1,1,1,8,128]{4,3,2,1,0:T(8,128)(2,1)S(1)} %constant_dynamic-slice_fusion.9), channel_id=1, source_target_pairs={{10,1},{11,0},{12,3},{13,2},{14,5},{15,4},{18,9},{19,8},{20,11},{2... | collective-permute-start | bytes 6152 | tf_op jit(solution)/shard_map/ppermute | solution.py:71
  69.6 14.5 %copy-start.8 = (bf16[512,128]{1,0:T(8,128)(2,1)}, bf16[512,128]{1,0:T(8,128)(2,1)S(1)}, u32[]{:S(2)}) copy-start(bf16[512,128]{1,0:T(8,128)(2,1)S(1)} %fusion.8) | copy-start | bytes 393220
  69.6 11.2 %collective-permute-start.6 = (bf16[512,128]{1,0:T(8,128)(2,1)S(1)}, bf16[512,128]{1,0:T(8,128)(2,1)S(1)}, u32[]{:S(2)}, u32[]{:S(2)}) collective-permute-start(bf16[512,128]{1,0:T(8,128)(2,1)S(1)} %fusion.8), channel_id=1, source_target_pairs={{8,0},{16,8},{24,16},{9,1},{17,9},{25,17},{10,2},{18,10},{26,18},{... | collective-permute-start | bytes 393224 | tf_op jit(solution)/shard_map/ppermute | solution.py:227
  71.5 8.7 %collective-permute-start.9 = (bf16[1,8,1,8,128]{4,3,2,1,0:T(8,128)(2,1)S(1)}, bf16[1,8,1,8,128]{4,3,2,1,0:T(8,128)(2,1)S(1)}, u32[]{:S(2)}, u32[]{:S(2)}) collective-permute-start(bf16[1,8,1,8,128]{4,3,2,1,0:T(8,128)(2,1)S(1)} %constant_dynamic-slice_fusion.10), channel_id=1, source_target_pairs={{8,1},{9,0},{10,3},{11,2},{12,5},{13,4},{14,7},{15,6},{16,9},{17,8... | collective-permute-start | bytes 49160 | tf_op jit(solution)/shard_map/ppermute | solution.py:71
  73.4 6.7 %collective-permute-start.7 = (bf16[1,1,1,8,128]{4,3,2,1,0:T(8,128)(2,1)S(1)}, bf16[1,1,1,8,128]{4,3,2,1,0:T(8,128)(2,1)S(1)}, u32[]{:S(2)}, u32[]{:S(2)}) collective-permute-start(bf16[1,1,1,8,128]{4,3,2,1,0:T(8,128)(2,1)S(1)} %constant_dynamic-slice_fusion.11), channel_id=1, source_target_pairs={{8,3},{9,2},{10,5},{11,4},{12,7},{13,6},{16,11},{17,10},{18,13},{1... | collective-permute-start | bytes 6152 | tf_op jit(solution)/shard_map/ppermute | solution.py:71
  84.7 17.4 %copy-start.6 = (bf16[512,128]{1,0:T(8,128)(2,1)}, bf16[512,128]{1,0:T(8,128)(2,1)S(1)}, u32[]{:S(2)}) copy-start(bf16[512,128]{1,0:T(8,128)(2,1)S(1)} %fusion.18) | copy-start | bytes 393220
  84.7 17.0 %collective-permute-start.12 = (bf16[512,128]{1,0:T(8,128)(2,1)S(1)}, bf16[512,128]{1,0:T(8,128)(2,1)S(1)}, u32[]{:S(2)}, u32[]{:S(2)}) collective-permute-start(bf16[512,128]{1,0:T(8,128)(2,1)S(1)} %fusion.18), channel_id=1, source_target_pairs={{8,0},{16,8},{24,16},{9,1},{17,9},{25,17},{10,2},{18,10},{26,18},{... | collective-permute-start | bytes 393224 | tf_op jit(solution)/shard_map/ppermute | solution.py:227
  86.7 14.7 %collective-permute-start.17 = (bf16[1,1,8,8,128]{4,3,2,1,0:T(8,128)(2,1)S(1)}, bf16[1,1,8,8,128]{4,3,2,1,0:T(8,128)(2,1)S(1)}, u32[]{:S(2)}, u32[]{:S(2)}) collective-permute-start(bf16[1,1,8,8,128]{4,3,2,1,0:T(8,128)(2,1)S(1)} %get-tuple-element.64), channel_id=1, source_target_pairs={{10,0},{11,1},{12,2},{13,3},{14,4},{15,5},{18,8},{19,9},{20,10},{2... | collective-permute-start | bytes 49160 | tf_op jit(solution)/shard_map/ppermute | solution.py:71
  88.6 5.8 %collective-permute-start.16 = (bf16[1,1,1,8,128]{4,3,2,1,0:T(8,128)(2,1)S(1)}, bf16[1,1,1,8,128]{4,3,2,1,0:T(8,128)(2,1)S(1)}, u32[]{:S(2)}, u32[]{:S(2)}) collective-permute-start(bf16[1,1,1,8,128]{4,3,2,1,0:T(8,128)(2,1)S(1)} %constant_dynamic-slice_fusion.6), channel_id=1, source_target_pairs={{10,1},{11,0},{12,3},{13,2},{14,5},{15,4},{18,9},{19,8},{20,11},{2... | collective-permute-start | bytes 6152 | tf_op jit(solution)/shard_map/ppermute | solution.py:71
  90.6 10.9 %collective-permute-start.14 = (bf16[1,1,8,8,128]{4,3,2,1,0:T(8,128)(2,1)S(1)}, bf16[1,1,8,8,128]{4,3,2,1,0:T(8,128)(2,1)S(1)}, u32[]{:S(2)}, u32[]{:S(2)}) collective-permute-start(bf16[1,1,8,8,128]{4,3,2,1,0:T(8,128)(2,1)S(1)} %get-tuple-element.63), channel_id=1, source_target_pairs={{8,2},{9,3},{10,4},{11,5},{12,6},{13,7},{16,10},{17,11},{18,12},{1... | collective-permute-start | bytes 49160 | tf_op jit(solution)/shard_map/ppermute | solution.py:71
  92.5 8.7 %collective-permute-start.15 = (bf16[1,8,1,8,128]{4,3,2,1,0:T(8,128)(2,1)S(1)}, bf16[1,8,1,8,128]{4,3,2,1,0:T(8,128)(2,1)S(1)}, u32[]{:S(2)}, u32[]{:S(2)}) collective-permute-start(bf16[1,8,1,8,128]{4,3,2,1,0:T(8,128)(2,1)S(1)} %constant_dynamic-slice_fusion.7), channel_id=1, source_target_pairs={{8,1},{9,0},{10,3},{11,2},{12,5},{13,4},{14,7},{15,6},{16,9},{17,8... | collective-permute-start | bytes 49160 | tf_op jit(solution)/shard_map/ppermute | solution.py:71
  94.4 6.7 %collective-permute-start.13 = (bf16[1,1,1,8,128]{4,3,2,1,0:T(8,128)(2,1)S(1)}, bf16[1,1,1,8,128]{4,3,2,1,0:T(8,128)(2,1)S(1)}, u32[]{:S(2)}, u32[]{:S(2)}) collective-permute-start(bf16[1,1,1,8,128]{4,3,2,1,0:T(8,128)(2,1)S(1)} %constant_dynamic-slice_fusion.8), channel_id=1, source_target_pairs={{8,3},{9,2},{10,5},{11,4},{12,7},{13,6},{16,11},{17,10},{18,13},{1... | collective-permute-start | bytes 6152 | tf_op jit(solution)/shard_map/ppermute | solution.py:71
  105.0 17.3 %copy-start.3 = (bf16[1,10,10,10,256]{4,0,3,2,1:T(2,128)(2,1)S(1)}, bf16[1,10,10,10,256]{4,0,3,2,1:T(2,128)(2,1)}, u32[]{:S(2)}) copy-start(bf16[1,10,10,10,256]{4,0,3,2,1:T(2,128)(2,1)} %copy-done.2) | copy-start | bytes 1536004
  105.7 16.4 %collective-permute-start.18 = (bf16[512,128]{1,0:T(8,128)(2,1)S(1)}, bf16[512,128]{1,0:T(8,128)(2,1)S(1)}, u32[]{:S(2)}, u32[]{:S(2)}) collective-permute-start(bf16[512,128]{1,0:T(8,128)(2,1)S(1)} %fusion.21), channel_id=1, source_target_pairs={{8,0},{16,8},{24,16},{9,1},{17,9},{25,17},{10,2},{18,10},{26,18},{... | collective-permute-start | bytes 393224 | tf_op jit(solution)/shard_map/ppermute | solution.py:227
  107.7 18.6 %collective-permute-start.20 = (bf16[1,1,8,8,128]{4,3,2,1,0:T(8,128)(2,1)S(1)}, bf16[1,1,8,8,128]{4,3,2,1,0:T(8,128)(2,1)S(1)}, u32[]{:S(2)}, u32[]{:S(2)}) collective-permute-start(bf16[1,1,8,8,128]{4,3,2,1,0:T(8,128)(2,1)S(1)} %get-tuple-element.62), channel_id=1, source_target_pairs={{8,2},{9,3},{10,4},{11,5},{12,6},{13,7},{16,10},{17,11},{18,12},{1... | collective-permute-start | bytes 49160 | tf_op jit(solution)/shard_map/ppermute | solution.py:71
  109.6 6.7 %collective-permute-start.19 = (bf16[1,1,1,8,128]{4,3,2,1,0:T(8,128)(2,1)S(1)}, bf16[1,1,1,8,128]{4,3,2,1,0:T(8,128)(2,1)S(1)}, u32[]{:S(2)}, u32[]{:S(2)}) collective-permute-start(bf16[1,1,1,8,128]{4,3,2,1,0:T(8,128)(2,1)S(1)} %constant_dynamic-slice_fusion.5), channel_id=1, source_target_pairs={{8,3},{9,2},{10,5},{11,4},{12,7},{13,6},{16,11},{17,10},{18,13},{1... | collective-permute-start | bytes 6152 | tf_op jit(solution)/shard_map/ppermute | solution.py:71
  111.6 14.7 %collective-permute-start.23 = (bf16[1,1,8,8,128]{4,3,2,1,0:T(8,128)(2,1)S(1)}, bf16[1,1,8,8,128]{4,3,2,1,0:T(8,128)(2,1)S(1)}, u32[]{:S(2)}, u32[]{:S(2)}) collective-permute-start(bf16[1,1,8,8,128]{4,3,2,1,0:T(8,128)(2,1)S(1)} %get-tuple-element.61), channel_id=1, source_target_pairs={{10,0},{11,1},{12,2},{13,3},{14,4},{15,5},{18,8},{19,9},{20,10},{2... | collective-permute-start | bytes 49160 | tf_op jit(solution)/shard_map/ppermute | solution.py:71
  113.5 8.6 %collective-permute-start.21 = (bf16[1,8,1,8,128]{4,3,2,1,0:T(8,128)(2,1)S(1)}, bf16[1,8,1,8,128]{4,3,2,1,0:T(8,128)(2,1)S(1)}, u32[]{:S(2)}, u32[]{:S(2)}) collective-permute-start(bf16[1,8,1,8,128]{4,3,2,1,0:T(8,128)(2,1)S(1)} %constant_dynamic-slice_fusion.4), channel_id=1, source_target_pairs={{8,1},{9,0},{10,3},{11,2},{12,5},{13,4},{14,7},{15,6},{16,9},{17,8... | collective-permute-start | bytes 49160 | tf_op jit(solution)/shard_map/ppermute | solution.py:71
  116.3 5.8 %collective-permute-start.22 = (bf16[1,1,1,8,128]{4,3,2,1,0:T(8,128)(2,1)S(1)}, bf16[1,1,1,8,128]{4,3,2,1,0:T(8,128)(2,1)S(1)}, u32[]{:S(2)}, u32[]{:S(2)}) collective-permute-start(bf16[1,1,1,8,128]{4,3,2,1,0:T(8,128)(2,1)S(1)} %constant_dynamic-slice_fusion.3), channel_id=1, source_target_pairs={{10,1},{11,0},{12,3},{13,2},{14,5},{15,4},{18,9},{19,8},{20,11},{2... | collective-permute-start | bytes 6152 | tf_op jit(solution)/shard_map/ppermute | solution.py:71
  127.3 7.1 %collective-permute-start.26 = (bf16[864,128]{1,0:T(8,128)(2,1)S(1)}, bf16[864,128]{1,0:T(8,128)(2,1)S(1)}, u32[]{:S(2)}, u32[]{:S(2)}) collective-permute-start(bf16[864,128]{1,0:T(8,128)(2,1)S(1)} %get-tuple-element.46), channel_id=1, source_target_pairs={{0,6},{2,0},{4,2},{6,4},{1,7},{3,1},{5,3},{7,5},{8,14},{10,8},{12,... | collective-permute-start | bytes 663560 | tf_op jit(solution)/shard_map/ppermute | solution.py:149
  128.5 11.0 %collective-permute-start.25 = (bf16[864,128]{1,0:T(8,128)(2,1)S(1)}, bf16[864,128]{1,0:T(8,128)(2,1)S(1)}, u32[]{:S(2)}, u32[]{:S(2)}) collective-permute-start(bf16[864,128]{1,0:T(8,128)(2,1)S(1)} %get-tuple-element.47), channel_id=1, source_target_pairs={{0,4},{2,6},{4,0},{6,2},{1,5},{3,7},{5,1},{7,3},{8,12},{10,14},{12... | collective-permute-start | bytes 663560 | tf_op jit(solution)/shard_map/ppermute | solution.py:149
  128.5 11.0 %collective-permute-start.24 = (bf16[864,128]{1,0:T(8,128)(2,1)S(1)}, bf16[864,128]{1,0:T(8,128)(2,1)S(1)}, u32[]{:S(2)}, u32[]{:S(2)}) collective-permute-start(bf16[864,128]{1,0:T(8,128)(2,1)S(1)} %get-tuple-element.45), channel_id=1, source_target_pairs={{0,2},{2,4},{4,6},{6,0},{1,3},{3,5},{5,7},{7,1},{8,10},{10,12},{12... | collective-permute-start | bytes 663560 | tf_op jit(solution)/shard_map/ppermute | solution.py:149
  131.9 9.4 %copy-start.7 = (bf16[512,128]{1,0:T(8,128)(2,1)S(1)}, bf16[512,128]{1,0:T(8,128)(2,1)}, u32[]{:S(2)}) copy-start(bf16[512,128]{1,0:T(8,128)(2,1)} %copy-done.6) | copy-start | bytes 393220
  131.9 9.4 %copy-start.9 = (bf16[512,128]{1,0:T(8,128)(2,1)S(1)}, bf16[512,128]{1,0:T(8,128)(2,1)}, u32[]{:S(2)}) copy-start(bf16[512,128]{1,0:T(8,128)(2,1)} %copy-done.8) | copy-start | bytes 393220
  139.7 3.0 %collective-permute-start.27 = (f32[864,128]{1,0:T(8,128)S(1)}, f32[864,128]{1,0:T(8,128)S(1)}, u32[]{:S(2)}, u32[]{:S(2)}) collective-permute-start(f32[864,128]{1,0:T(8,128)S(1)} %convert_add_fusion), channel_id=1, source_target_pairs={{0,1},{1,0},{2,3},{3,2},{4,5},{5,4},{6,7},{7,6},{8,9},{9,8},{10,11... | collective-permute-start | bytes 1327112 | tf_op jit(solution)/shard_map/ppermute | solution.py:232

commit v7 on v6

--- a/solution.py
+++ b/solution.py
@@ -32,7 +32,7 @@
     return [(sx, sy) for sx in OFFSETS for sy in OFFSETS if (sx, sy) != (0, 0)]
 
 
-def assemble(centre, received, table):
+def assemble(centre, received, table, split=False):
     slabs_x = []
     for shift_x in OFFSETS:
         rows_y = []
@@ -51,6 +51,8 @@
                 parts_z.append(picked[:, :, :, source_range(shift_z), :])
             rows_y.append(jnp.concatenate(parts_z, axis=3))
         slabs_x.append(jnp.concatenate(rows_y, axis=2))
+    if split:
+        slabs_x[0], slabs_x[2] = lax.optimization_barrier((slabs_x[0], slabs_x[2]))
     return jnp.concatenate(slabs_x, axis=1)
 
 
@@ -201,7 +203,7 @@
             flipped = weights.reshape(3, 3, 3, channels, channels)[::-1, ::-1, ::-1].transpose(0, 1, 2, 4, 3)
         else:
             got = exchange(both, ("sx", "sy"), (n_x, n_y), 0)
-        both_pad = assemble(both, got, table)
+        both_pad = assemble(both, got, table, split=True)
         act_pad = both_pad[..., :channels]
         centre = start
         received = None

time: 145 us -> 132 us (0.910)
  waiting for transfers between devices: 29.3 us -> 22.3 us
  other arithmetic: 20.7 us -> 15.5 us
    ppermute x20, waiting for transfers between devices: 21.6 us -> 14.5 us  [send(): return lax.ppermute(piece, axes, route)]
    concatenate x1, other arithmetic: 7.83 us -> 2.11 us  [assemble(): return jnp.concatenate(slabs_x, axis=1)]
  transfers between devices with their start and end apart: 28 -> 28, of which waited for: 8 -> 8; matrix products, arithmetic and copies ran while one was open for 10% -> 12% of each run, Pallas kernels for 0% -> 0%
where the time goes in v7:
time: 132 us; the launch traced here: 131 us
  starting transfers between devices  50.8 us (38%)
  waiting for transfers between devices  22.3 us (17%)
  between operations  19.9 us (15%)
  matrix products  15.8 us (12%)
  other arithmetic  15.5 us (12%)
  local copies, waits for them, and re-layouts  6.65 us (5%)
    ppermute x20, starting transfers between devices, send(): return lax.ppermute(piece, axes, route)  41.4 us
    ppermute x20, waiting for transfers between devices, send(): return lax.ppermute(piece, axes, route)  14.5 us
    conv_general_dilated x4, matrix products, conv_data(): lax.conv_general_dilated(padded, filters, (1, 1, 1), 'VALID', dimension_n...  11.9 us
    ppermute x3, waiting for transfers between devices, scattered_sum(): lax.ppermute(piece, axis, [(i, (i + step) % count) for i in range(count)])  7.33 us
    ppermute x3, starting transfers between devices, shards(): centre = lax.ppermute(result, 'pipe', down)  5.76 us
    transpose x1, matrix products, shards(): per_tap.transpose(1, 2, 3, 0, 4).reshape(taps * channels, channels)  3.93 us
  transfers between devices with their start and end apart: 28, of which 8 were waited for; matrix products, arithmetic and copies ran while one was open for 12% of the time, Pallas kernels for 0%

profile of v7, /device:TPU:21, one launch (start us, length us, event | category | flops | bytes accessed | tf_op | source)
XLA Modules:
  0.0 130.8 jit_solution(11606074648777758649)
XLA Ops:
  0.6 1.0 convert_element_type.160
  1.6 1.1 fusion.25
  3.5 1.0 broadcast_select_fusion.12
  4.5 0.9 multiply_convert_fusion.2
  5.5 3.6 %collective-permute-start.2 = (bf16[1,1,1,8,256]{4,3,2,1,0:T(8,128)(2,1)S(1)}, bf16[1,1,1,8,256]{4,3,2,1,0:T(8,128)(2,1)S(1)}, u32[]{:S(2)}, u32[]{:S(2)}) collective-permute-start(bf16[1,1,1,8,256]{4,3,2,1,0:T(8,128)(2,1)S(1)} %constant_dynamic-slice_fusion.12), channel_id=1, source_target_pairs={{2,1},{3,0},{4,3},{5,2},{6,5},{7,4},{10,9},{11,8},{12,11},{13,10},... | collective-permute-start | bytes 12296 | tf_op jit(solution)/shard_map/ppermute | solution.py:73
  9.1 1.9 %collective-permute-start = (bf16[1,1,1,8,256]{4,3,2,1,0:T(8,128)(2,1)S(1)}, bf16[1,1,1,8,256]{4,3,2,1,0:T(8,128)(2,1)S(1)}, u32[]{:S(2)}, u32[]{:S(2)}) collective-permute-start(bf16[1,1,1,8,256]{4,3,2,1,0:T(8,128)(2,1)S(1)} %constant_dynamic-slice_fusion.13), channel_id=1, source_target_pairs={{0,3},{1,2},{2,5},{3,4},{4,7},{5,6},{8,11},{9,10},{10,13},{11,12},... | collective-permute-start | bytes 12296 | tf_op jit(solution)/shard_map/ppermute | solution.py:73
  11.1 0.3 collective-permute-start.5
  11.5 2.1 %collective-permute-start.1 = (bf16[992,128]{1,0:T(8,128)(2,1)S(1)}, bf16[992,128]{1,0:T(8,128)(2,1)S(1)}, u32[]{:S(2)}, u32[]{:S(2)}) collective-permute-start(bf16[992,128]{1,0:T(8,128)(2,1)S(1)} %get-tuple-element.60), channel_id=1, source_target_pairs={{0,2},{1,3},{2,4},{3,5},{4,6},{5,7},{6,0},{7,1},{8,10},{9,11},{10,... | collective-permute-start | bytes 761864 | tf_op jit(solution)/shard_map/ppermute | solution.py:73
  13.6 0.3 collective-permute-start.3
  13.9 0.7 fusion.76
  14.6 0.7 fusion.75
  17.9 0.6 scatter_custom_fusion
  18.5 0.6 pad_clamp_fusion
  19.1 0.6 fusion.60
  19.7 0.4 copy_dynamic-update-slice_fusion
  20.1 0.6 broadcast_select_fusion
  35.7 1.5 %collective-permute-start.4 = (bf16[1,8,1,8,256]{4,3,2,1,0:T(8,128)(2,1)S(1)}, bf16[1,8,1,8,256]{4,3,2,1,0:T(8,128)(2,1)S(1)}, u32[]{:S(2)}, u32[]{:S(2)}) collective-permute-start(bf16[1,8,1,8,256]{4,3,2,1,0:T(8,128)(2,1)S(1)} %fusion.57), channel_id=1, source_target_pairs={{0,1},{1,0},{2,3},{3,2},{4,5},{5,4},{6,7},{7,6},{8,9},{9,8},{10,11... | collective-permute-start | bytes 98312 | tf_op jit(solution)/shard_map/ppermute | solution.py:73
  37.4 0.6 collective-permute-done.4
  39.1 1.0 pad_maximum_fusion.1
  40.2 0.8 gather_fusion
  41.0 1.0 rev.3
  42.1 2.1 %pad_maximum_fusion = bf16[1,10,10,10,256]{4,0,3,2,1:T(2,128)(2,1)S(1)} fusion(bf16[1,1,10,10,256]{4,0,3,2,1:T(2,128)(2,1)S(1)} %pad_maximum_fusion.11, bf16[1,8,1,10,256]{4,0,3,2,1:T(2,128)(2,1)S(1)} %copy.47, bf16[1,8,8,1,256]{4,0,3,2,1:T(2,128)(2,1)S(1)} %get-tuple-element.50, bf16[1,8,8,8,256]{4,0,3,2,1:T(2,128)(2,1)S(1)} %broadcast_select_fusion, ...), kind=kLoop, calls=%fused_computation.4 | loop fusion | flops 1536000 | bytes 1024000 | tf_op jit(solution)/shard_map/concatenate | solution.py:56
  44.2 3.0 %fusion.1 = f32[1,8,8,8,128]{4,0,3,2,1:T(1,128)S(1)} fusion(bf16[3,3,3,128,128]{4,3,2,1,0:T(8,128)(2,1)S(1)} %copy-done.4, bf16[1,10,10,10,256]{4,0,3,2,1:T(2,128)(2,1)S(1)} %pad_maximum_fusion), kind=kOutput, calls=%fused_computation.10 | convolution fusion | flops 452984832 | bytes 1658880 | tf_op jit(solution)/shard_map/conv_general_dilated | solution.py:108
  47.2 0.3 fusion.47
  48.0 2.5 %collective-permute-start.11 = (bf16[1,1,8,8,128]{4,3,2,1,0:T(8,128)(2,1)S(1)}, bf16[1,1,8,8,128]{4,3,2,1,0:T(8,128)(2,1)S(1)}, u32[]{:S(2)}, u32[]{:S(2)}) collective-permute-start(bf16[1,1,8,8,128]{4,3,2,1,0:T(8,128)(2,1)S(1)} %get-tuple-element.72), channel_id=1, source_target_pairs={{10,0},{11,1},{12,2},{13,3},{14,4},{15,5},{18,8},{19,9},{20,10},{2... | collective-permute-start | bytes 49160 | tf_op jit(solution)/shard_map/ppermute | solution.py:73
  50.5 2.1 %collective-permute-start.8 = (bf16[1,1,8,8,128]{4,3,2,1,0:T(8,128)(2,1)S(1)}, bf16[1,1,8,8,128]{4,3,2,1,0:T(8,128)(2,1)S(1)}, u32[]{:S(2)}, u32[]{:S(2)}) collective-permute-start(bf16[1,1,8,8,128]{4,3,2,1,0:T(8,128)(2,1)S(1)} %get-tuple-element.71), channel_id=1, source_target_pairs={{8,2},{9,3},{10,4},{11,5},{12,6},{13,7},{16,10},{17,11},{18,12},{1... | collective-permute-start | bytes 49160 | tf_op jit(solution)/shard_map/ppermute | solution.py:73
  52.6 3.9 %collective-permute-start.10 = (bf16[1,1,1,8,128]{4,3,2,1,0:T(8,128)(2,1)S(1)}, bf16[1,1,1,8,128]{4,3,2,1,0:T(8,128)(2,1)S(1)}, u32[]{:S(2)}, u32[]{:S(2)}) collective-permute-start(bf16[1,1,1,8,128]{4,3,2,1,0:T(8,128)(2,1)S(1)} %constant_dynamic-slice_fusion.9), channel_id=1, source_target_pairs={{10,1},{11,0},{12,3},{13,2},{14,5},{15,4},{18,9},{19,8},{20,11},{2... | collective-permute-start | bytes 6152 | tf_op jit(solution)/shard_map/ppermute | solution.py:73
  56.5 0.3 fusion.8
  56.8 1.9 %collective-permute-start.6 = (bf16[512,128]{1,0:T(8,128)(2,1)S(1)}, bf16[512,128]{1,0:T(8,128)(2,1)S(1)}, u32[]{:S(2)}, u32[]{:S(2)}) collective-permute-start(bf16[512,128]{1,0:T(8,128)(2,1)S(1)} %fusion.8), channel_id=1, source_target_pairs={{8,0},{16,8},{24,16},{9,1},{17,9},{25,17},{10,2},{18,10},{26,18},{... | collective-permute-start | bytes 393224 | tf_op jit(solution)/shard_map/ppermute | solution.py:229
  58.8 1.9 %collective-permute-start.9 = (bf16[1,8,1,8,128]{4,3,2,1,0:T(8,128)(2,1)S(1)}, bf16[1,8,1,8,128]{4,3,2,1,0:T(8,128)(2,1)S(1)}, u32[]{:S(2)}, u32[]{:S(2)}) collective-permute-start(bf16[1,8,1,8,128]{4,3,2,1,0:T(8,128)(2,1)S(1)} %constant_dynamic-slice_fusion.10), channel_id=1, source_target_pairs={{8,1},{9,0},{10,3},{11,2},{12,5},{13,4},{14,7},{15,6},{16,9},{17,8... | collective-permute-start | bytes 49160 | tf_op jit(solution)/shard_map/ppermute | solution.py:73
  60.7 2.1 %collective-permute-start.7 = (bf16[1,1,1,8,128]{4,3,2,1,0:T(8,128)(2,1)S(1)}, bf16[1,1,1,8,128]{4,3,2,1,0:T(8,128)(2,1)S(1)}, u32[]{:S(2)}, u32[]{:S(2)}) collective-permute-start(bf16[1,1,1,8,128]{4,3,2,1,0:T(8,128)(2,1)S(1)} %constant_dynamic-slice_fusion.11), channel_id=1, source_target_pairs={{8,3},{9,2},{10,5},{11,4},{12,7},{13,6},{16,11},{17,10},{18,13},{1... | collective-permute-start | bytes 6152 | tf_op jit(solution)/shard_map/ppermute | solution.py:73
  62.8 4.6 %collective-permute-done.7 = bf16[1,1,1,8,128]{4,3,2,1,0:T(8,128)(2,1)S(1)} collective-permute-done((bf16[1,1,1,8,128]{4,3,2,1,0:T(8,128)(2,1)S(1)}, bf16[1,1,1,8,128]{4,3,2,1,0:T(8,128)(2,1)S(1)}, u32[]{:S(2)}, u32[]{:S(2)}) %collective-permute-start.7) | collective-permute-done | bytes 2080 | tf_op jit(solution)/shard_map/ppermute | solution.py:73
  68.3 2.9 %fusion.5 = f32[1,8,8,8,128]{4,0,3,2,1:T(1,128)S(1)} fusion(bf16[3,3,3,128,128]{4,3,2,1,0:T(8,128)(2,1)S(1)} %bitcast.208, bf16[1,1,10,10,128]{4,0,3,2,1:T(2,128)(2,1)S(1)} %copy.56, bf16[1,8,1,10,128]{4,0,3,2,1:T(2,128)(2,1)S(1)} %copy.54, bf16[1,8,8,1,128]{4,0,3,2,1:T(2,128)(2,1)S(1)} %slice_bitcast_fusion.6, bf16[1,8,8,8,128]{4,0,3,2,1:T(2,128)(2,1)S(1)} %copy.52, ...), kind=kOutput, calls=%fused_computation.14 | convolution fusion | flops 454776832 | bytes 1402880 | tf_op jit(solution)/shard_map/conv_general_dilated | solution.py:108
  71.3 0.3 fusion.48
  71.7 0.3 fusion.18
  72.0 1.9 %collective-permute-start.12 = (bf16[512,128]{1,0:T(8,128)(2,1)S(1)}, bf16[512,128]{1,0:T(8,128)(2,1)S(1)}, u32[]{:S(2)}, u32[]{:S(2)}) collective-permute-start(bf16[512,128]{1,0:T(8,128)(2,1)S(1)} %fusion.18), channel_id=1, source_target_pairs={{8,0},{16,8},{24,16},{9,1},{17,9},{25,17},{10,2},{18,10},{26,18},{... | collective-permute-start | bytes 393224 | tf_op jit(solution)/shard_map/ppermute | solution.py:229
  73.9 1.9 %collective-permute-start.17 = (bf16[1,1,8,8,128]{4,3,2,1,0:T(8,128)(2,1)S(1)}, bf16[1,1,8,8,128]{4,3,2,1,0:T(8,128)(2,1)S(1)}, u32[]{:S(2)}, u32[]{:S(2)}) collective-permute-start(bf16[1,1,8,8,128]{4,3,2,1,0:T(8,128)(2,1)S(1)} %get-tuple-element.67), channel_id=1, source_target_pairs={{10,0},{11,1},{12,2},{13,3},{14,4},{15,5},{18,8},{19,9},{20,10},{2... | collective-permute-start | bytes 49160 | tf_op jit(solution)/shard_map/ppermute | solution.py:73
  75.9 1.9 %collective-permute-start.16 = (bf16[1,1,1,8,128]{4,3,2,1,0:T(8,128)(2,1)S(1)}, bf16[1,1,1,8,128]{4,3,2,1,0:T(8,128)(2,1)S(1)}, u32[]{:S(2)}, u32[]{:S(2)}) collective-permute-start(bf16[1,1,1,8,128]{4,3,2,1,0:T(8,128)(2,1)S(1)} %constant_dynamic-slice_fusion.6), channel_id=1, source_target_pairs={{10,1},{11,0},{12,3},{13,2},{14,5},{15,4},{18,9},{19,8},{20,11},{2... | collective-permute-start | bytes 6152 | tf_op jit(solution)/shard_map/ppermute | solution.py:73
  77.8 1.9 %collective-permute-start.14 = (bf16[1,1,8,8,128]{4,3,2,1,0:T(8,128)(2,1)S(1)}, bf16[1,1,8,8,128]{4,3,2,1,0:T(8,128)(2,1)S(1)}, u32[]{:S(2)}, u32[]{:S(2)}) collective-permute-start(bf16[1,1,8,8,128]{4,3,2,1,0:T(8,128)(2,1)S(1)} %get-tuple-element.66), channel_id=1, source_target_pairs={{8,2},{9,3},{10,4},{11,5},{12,6},{13,7},{16,10},{17,11},{18,12},{1... | collective-permute-start | bytes 49160 | tf_op jit(solution)/shard_map/ppermute | solution.py:73
  79.8 1.9 %collective-permute-start.15 = (bf16[1,8,1,8,128]{4,3,2,1,0:T(8,128)(2,1)S(1)}, bf16[1,8,1,8,128]{4,3,2,1,0:T(8,128)(2,1)S(1)}, u32[]{:S(2)}, u32[]{:S(2)}) collective-permute-start(bf16[1,8,1,8,128]{4,3,2,1,0:T(8,128)(2,1)S(1)} %constant_dynamic-slice_fusion.7), channel_id=1, source_target_pairs={{8,1},{9,0},{10,3},{11,2},{12,5},{13,4},{14,7},{15,6},{16,9},{17,8... | collective-permute-start | bytes 49160 | tf_op jit(solution)/shard_map/ppermute | solution.py:73
  81.7 1.9 %collective-permute-start.13 = (bf16[1,1,1,8,128]{4,3,2,1,0:T(8,128)(2,1)S(1)}, bf16[1,1,1,8,128]{4,3,2,1,0:T(8,128)(2,1)S(1)}, u32[]{:S(2)}, u32[]{:S(2)}) collective-permute-start(bf16[1,1,1,8,128]{4,3,2,1,0:T(8,128)(2,1)S(1)} %constant_dynamic-slice_fusion.8), channel_id=1, source_target_pairs={{8,3},{9,2},{10,5},{11,4},{12,7},{13,6},{16,11},{17,10},{18,13},{1... | collective-permute-start | bytes 6152 | tf_op jit(solution)/shard_map/ppermute | solution.py:73
  83.7 4.8 %collective-permute-done.13 = bf16[1,1,1,8,128]{4,3,2,1,0:T(8,128)(2,1)S(1)} collective-permute-done((bf16[1,1,1,8,128]{4,3,2,1,0:T(8,128)(2,1)S(1)}, bf16[1,1,1,8,128]{4,3,2,1,0:T(8,128)(2,1)S(1)}, u32[]{:S(2)}, u32[]{:S(2)}) %collective-permute-start.13) | collective-permute-done | bytes 2080 | tf_op jit(solution)/shard_map/ppermute | solution.py:73
  89.3 2.9 %fusion.4 = f32[1,8,8,8,128]{4,0,3,2,1:T(1,128)S(1)} fusion(bf16[3,3,3,128,128]{4,3,2,1,0:T(8,128)(2,1)S(1)} %bitcast.209, bf16[1,1,10,10,128]{4,0,3,2,1:T(2,128)(2,1)S(1)} %copy.63, bf16[1,8,1,10,128]{4,0,3,2,1:T(2,128)(2,1)S(1)} %copy.61, bf16[1,8,8,1,128]{4,0,3,2,1:T(2,128)(2,1)S(1)} %slice_bitcast_fusion.4, bf16[1,8,8,8,128]{4,0,3,2,1:T(2,128)(2,1)S(1)} %copy.59, ...), kind=kOutput, calls=%fused_computation.13 | convolution fusion | flops 454776832 | bytes 1402880 | tf_op jit(solution)/shard_map/conv_general_dilated | solution.py:108
  92.3 0.3 fusion.49
  92.7 0.3 fusion.21
  93.0 1.9 %collective-permute-start.18 = (bf16[512,128]{1,0:T(8,128)(2,1)S(1)}, bf16[512,128]{1,0:T(8,128)(2,1)S(1)}, u32[]{:S(2)}, u32[]{:S(2)}) collective-permute-start(bf16[512,128]{1,0:T(8,128)(2,1)S(1)} %fusion.21), channel_id=1, source_target_pairs={{8,0},{16,8},{24,16},{9,1},{17,9},{25,17},{10,2},{18,10},{26,18},{... | collective-permute-start | bytes 393224 | tf_op jit(solution)/shard_map/ppermute | solution.py:229
  94.9 1.9 %collective-permute-start.20 = (bf16[1,1,8,8,128]{4,3,2,1,0:T(8,128)(2,1)S(1)}, bf16[1,1,8,8,128]{4,3,2,1,0:T(8,128)(2,1)S(1)}, u32[]{:S(2)}, u32[]{:S(2)}) collective-permute-start(bf16[1,1,8,8,128]{4,3,2,1,0:T(8,128)(2,1)S(1)} %get-tuple-element.65), channel_id=1, source_target_pairs={{8,2},{9,3},{10,4},{11,5},{12,6},{13,7},{16,10},{17,11},{18,12},{1... | collective-permute-start | bytes 49160 | tf_op jit(solution)/shard_map/ppermute | solution.py:73
  96.9 1.9 %collective-permute-start.19 = (bf16[1,1,1,8,128]{4,3,2,1,0:T(8,128)(2,1)S(1)}, bf16[1,1,1,8,128]{4,3,2,1,0:T(8,128)(2,1)S(1)}, u32[]{:S(2)}, u32[]{:S(2)}) collective-permute-start(bf16[1,1,1,8,128]{4,3,2,1,0:T(8,128)(2,1)S(1)} %constant_dynamic-slice_fusion.5), channel_id=1, source_target_pairs={{8,3},{9,2},{10,5},{11,4},{12,7},{13,6},{16,11},{17,10},{18,13},{1... | collective-permute-start | bytes 6152 | tf_op jit(solution)/shard_map/ppermute | solution.py:73
  98.8 1.9 %collective-permute-start.23 = (bf16[1,1,8,8,128]{4,3,2,1,0:T(8,128)(2,1)S(1)}, bf16[1,1,8,8,128]{4,3,2,1,0:T(8,128)(2,1)S(1)}, u32[]{:S(2)}, u32[]{:S(2)}) collective-permute-start(bf16[1,1,8,8,128]{4,3,2,1,0:T(8,128)(2,1)S(1)} %get-tuple-element.64), channel_id=1, source_target_pairs={{10,0},{11,1},{12,2},{13,3},{14,4},{15,5},{18,8},{19,9},{20,10},{2... | collective-permute-start | bytes 49160 | tf_op jit(solution)/shard_map/ppermute | solution.py:73
  100.8 1.9 %collective-permute-start.21 = (bf16[1,8,1,8,128]{4,3,2,1,0:T(8,128)(2,1)S(1)}, bf16[1,8,1,8,128]{4,3,2,1,0:T(8,128)(2,1)S(1)}, u32[]{:S(2)}, u32[]{:S(2)}) collective-permute-start(bf16[1,8,1,8,128]{4,3,2,1,0:T(8,128)(2,1)S(1)} %constant_dynamic-slice_fusion.4), channel_id=1, source_target_pairs={{8,1},{9,0},{10,3},{11,2},{12,5},{13,4},{14,7},{15,6},{16,9},{17,8... | collective-permute-start | bytes 49160 | tf_op jit(solution)/shard_map/ppermute | solution.py:73
  102.7 0.9 collective-permute-done.19
  103.6 2.1 %collective-permute-start.22 = (bf16[1,1,1,8,128]{4,3,2,1,0:T(8,128)(2,1)S(1)}, bf16[1,1,1,8,128]{4,3,2,1,0:T(8,128)(2,1)S(1)}, u32[]{:S(2)}, u32[]{:S(2)}) collective-permute-start(bf16[1,1,1,8,128]{4,3,2,1,0:T(8,128)(2,1)S(1)} %constant_dynamic-slice_fusion.3), channel_id=1, source_target_pairs={{10,1},{11,0},{12,3},{13,2},{14,5},{15,4},{18,9},{19,8},{20,11},{2... | collective-permute-start | bytes 6152 | tf_op jit(solution)/shard_map/ppermute | solution.py:73
  105.7 3.6 %collective-permute-done.22 = bf16[1,1,1,8,128]{4,3,2,1,0:T(8,128)(2,1)S(1)} collective-permute-done((bf16[1,1,1,8,128]{4,3,2,1,0:T(8,128)(2,1)S(1)}, bf16[1,1,1,8,128]{4,3,2,1,0:T(8,128)(2,1)S(1)}, u32[]{:S(2)}, u32[]{:S(2)}) %collective-permute-start.22) | collective-permute-done | bytes 2080 | tf_op jit(solution)/shard_map/ppermute | solution.py:73
  109.6 3.9 %multiply_convert_fusion = bf16[3,3,3,128,128]{4,3,2,1,0:T(8,128)(2,1)S(1)} fusion(bf16[1,10,10,10,256]{4,0,3,2,1:T(2,128)(2,1)S(1)} %copy-done.3, bf16[1,8,8,8,128]{4,3,2,1,0:T(8,128)(2,1)S(1)} %bitcast.242), kind=kOutput, calls=%fused_computation.2 | convolution fusion | flops 453869568 | bytes 1527808 | tf_op jit(solution)/shard_map/transpose | solution.py:217
  114.5 1.3 collective-permute-start.26
  115.8 0.4 collective-permute-start.24
  116.2 3.0 %fusion.3 = f32[1,8,8,8,128]{4,0,3,2,1:T(1,128)S(1)} fusion(bf16[3,3,3,128,128]{4,3,2,1,0:T(8,128)(2,1)S(1)} %bitcast.210, bf16[1,1,10,10,128]{4,0,3,2,1:T(2,128)(2,1)S(1)} %copy.71, bf16[1,8,1,10,128]{4,0,3,2,1:T(2,128)(2,1)S(1)} %copy.69, bf16[1,8,8,1,128]{4,0,3,2,1:T(2,128)(2,1)S(1)} %slice_bitcast_fusion.2, bf16[1,8,8,8,128]{4,0,3,2,1:T(2,128)(2,1)S(1)} %copy.67, ...), kind=kOutput, calls=%fused_computation.12 | convolution fusion | flops 454776832 | bytes 1402880 | tf_op jit(solution)/shard_map/conv_general_dilated | solution.py:108
  119.2 0.3 fusion.50
  119.5 2.1 %collective-permute-done.26 = bf16[864,128]{1,0:T(8,128)(2,1)S(1)} collective-permute-done((bf16[864,128]{1,0:T(8,128)(2,1)S(1)}, bf16[864,128]{1,0:T(8,128)(2,1)S(1)}, u32[]{:S(2)}, u32[]{:S(2)}) %collective-permute-start.26) | collective-permute-done | bytes 221216 | tf_op jit(solution)/shard_map/ppermute | solution.py:151
  121.6 5.3 %collective-permute-done.25 = bf16[864,128]{1,0:T(8,128)(2,1)S(1)} collective-permute-done((bf16[864,128]{1,0:T(8,128)(2,1)S(1)}, bf16[864,128]{1,0:T(8,128)(2,1)S(1)}, u32[]{:S(2)}, u32[]{:S(2)}) %collective-permute-start.25) | collective-permute-done | bytes 221216 | tf_op jit(solution)/shard_map/ppermute | solution.py:151
  127.0 1.6 %collective-permute-start.27 = (f32[864,128]{1,0:T(8,128)S(1)}, f32[864,128]{1,0:T(8,128)S(1)}, u32[]{:S(2)}, u32[]{:S(2)}) collective-permute-start(f32[864,128]{1,0:T(8,128)S(1)} %convert_add_fusion), channel_id=1, source_target_pairs={{0,1},{1,0},{2,3},{3,2},{4,5},{5,4},{6,7},{7,6},{8,9},{9,8},{10,11... | collective-permute-start | bytes 1327112 | tf_op jit(solution)/shard_map/ppermute | solution.py:234
  128.6 1.0 fusion.53
  129.6 0.4 collective-permute-done.27
  130.0 0.8 add_bitcast_fusion
  (215 shorter events, 5.0 us)
Async XLA Ops:
  0.6 10.4 %copy-start.5 = (bf16[1,864,128]{2,1,0:T(8,128)(2,1)S(1)}, bf16[1,864,128]{2,1,0:T(8,128)(2,1)}, u32[]{:S(2)}) copy-start(bf16[1,864,128]{2,1,0:T(8,128)(2,1)} %param.11) | copy-start | bytes 663556
  2.8 11.1 %copy-start.10 = (s32[1,1,1,1,27]{4,3,2,1,0:T(1,128)S(1)}, s32[1,1,1,1,27]{4,3,2,1,0:T(1,128)}, u32[]{:S(2)}) copy-start(s32[1,1,1,1,27]{4,3,2,1,0:T(1,128)} %param.8) | copy-start | bytes 328
  4.5 10.9 %copy-start.11 = (f32[1,128]{1,0:T(1,128)S(1)}, f32[1,128]{1,0:T(1,128)}, u32[]{:S(2)}) copy-start(f32[1,128]{1,0:T(1,128)} %param.10) | copy-start | bytes 1540
  5.5 30.2 %collective-permute-start.2 = (bf16[1,1,1,8,256]{4,3,2,1,0:T(8,128)(2,1)S(1)}, bf16[1,1,1,8,256]{4,3,2,1,0:T(8,128)(2,1)S(1)}, u32[]{:S(2)}, u32[]{:S(2)}) collective-permute-start(bf16[1,1,1,8,256]{4,3,2,1,0:T(8,128)(2,1)S(1)} %constant_dynamic-slice_fusion.12), channel_id=1, source_target_pairs={{2,1},{3,0},{4,3},{5,2},{6,5},{7,4},{10,9},{11,8},{12,11},{13,10},... | collective-permute-start | bytes 12296 | tf_op jit(solution)/shard_map/ppermute | solution.py:73
  9.1 28.1 %collective-permute-start = (bf16[1,1,1,8,256]{4,3,2,1,0:T(8,128)(2,1)S(1)}, bf16[1,1,1,8,256]{4,3,2,1,0:T(8,128)(2,1)S(1)}, u32[]{:S(2)}, u32[]{:S(2)}) collective-permute-start(bf16[1,1,1,8,256]{4,3,2,1,0:T(8,128)(2,1)S(1)} %constant_dynamic-slice_fusion.13), channel_id=1, source_target_pairs={{0,3},{1,2},{2,5},{3,4},{4,7},{5,6},{8,11},{9,10},{10,13},{11,12},... | collective-permute-start | bytes 12296 | tf_op jit(solution)/shard_map/ppermute | solution.py:73
  11.1 28.0 %collective-permute-start.5 = (bf16[864,128]{1,0:T(8,128)(2,1)S(1)}, bf16[864,128]{1,0:T(8,128)(2,1)}, u32[]{:S(2)}, u32[]{:S(2)}) collective-permute-start(bf16[864,128]{1,0:T(8,128)(2,1)S(1)} %bitcast.223), channel_id=1, source_target_pairs={{0,4},{2,6},{4,0},{6,2},{1,5},{3,7},{5,1},{7,3},{8,12},{10,14},{12... | collective-permute-start | bytes 663560 | tf_op jit(solution)/shard_map/ppermute | solution.py:137
  11.4 4.4 %copy-start.1 = (bf16[1,1,1,512,128]{4,3,2,1,0:T(8,128)(2,1)S(1)}, bf16[1,1,1,512,128]{4,3,2,1,0:T(8,128)(2,1)}, u32[]{:S(2)}) copy-start(bf16[1,1,1,512,128]{4,3,2,1,0:T(8,128)(2,1)} %param.7) | copy-start | bytes 393220
  11.5 26.9 %collective-permute-start.1 = (bf16[992,128]{1,0:T(8,128)(2,1)S(1)}, bf16[992,128]{1,0:T(8,128)(2,1)S(1)}, u32[]{:S(2)}, u32[]{:S(2)}) collective-permute-start(bf16[992,128]{1,0:T(8,128)(2,1)S(1)} %get-tuple-element.60), channel_id=1, source_target_pairs={{0,2},{1,3},{2,4},{3,5},{4,6},{5,7},{6,0},{7,1},{8,10},{9,11},{10,... | collective-permute-start | bytes 761864 | tf_op jit(solution)/shard_map/ppermute | solution.py:73
  13.6 24.9 %collective-permute-start.3 = (bf16[992,128]{1,0:T(8,128)(2,1)S(1)}, bf16[992,128]{1,0:T(8,128)(2,1)S(1)}, u32[]{:S(2)}, u32[]{:S(2)}) collective-permute-start(bf16[992,128]{1,0:T(8,128)(2,1)S(1)} %get-tuple-element.59), channel_id=1, source_target_pairs={{0,6},{1,7},{2,0},{3,1},{4,2},{5,3},{6,4},{7,5},{8,14},{9,15},{10,... | collective-permute-start | bytes 761864 | tf_op jit(solution)/shard_map/ppermute | solution.py:73
  35.7 2.4 %collective-permute-start.4 = (bf16[1,8,1,8,256]{4,3,2,1,0:T(8,128)(2,1)S(1)}, bf16[1,8,1,8,256]{4,3,2,1,0:T(8,128)(2,1)S(1)}, u32[]{:S(2)}, u32[]{:S(2)}) collective-permute-start(bf16[1,8,1,8,256]{4,3,2,1,0:T(8,128)(2,1)S(1)} %fusion.57), channel_id=1, source_target_pairs={{0,1},{1,0},{2,3},{3,2},{4,5},{5,4},{6,7},{7,6},{8,9},{9,8},{10,11... | collective-permute-start | bytes 98312 | tf_op jit(solution)/shard_map/ppermute | solution.py:73
  42.0 2.1 %copy-start.4 = (bf16[3,3,3,128,128]{4,3,2,1,0:T(8,128)(2,1)S(1)}, bf16[3,3,3,128,128]{4,3,2,1,0:T(8,128)(2,1)}, u32[]{:S(2)}) copy-start(bf16[3,3,3,128,128]{4,3,2,1,0:T(8,128)(2,1)} %rev.3) | copy-start | bytes 2654212
  44.2 3.0 %copy-start.2 = (bf16[1,10,10,10,256]{4,0,3,2,1:T(2,128)(2,1)}, bf16[1,10,10,10,256]{4,0,3,2,1:T(2,128)(2,1)S(1)}, u32[]{:S(2)}) copy-start(bf16[1,10,10,10,256]{4,0,3,2,1:T(2,128)(2,1)S(1)} %pad_maximum_fusion) | copy-start | bytes 1536004
  44.2 3.0 %copy-start = (bf16[1,1,1,1,512,128]{5,4,3,2,1,0:T(8,128)(2,1)S(1)}, bf16[1,1,1,1,512,128]{5,4,3,2,1,0:T(8,128)(2,1)}, u32[]{:S(2)}) copy-start(bf16[1,1,1,1,512,128]{5,4,3,2,1,0:T(8,128)(2,1)} %param.6) | copy-start | bytes 393220
  47.2 9.3 %copy-start.12 = (pred[512]{0:T(512)(128)(4,1)S(1)}, pred[512]{0:T(512)(128)(4,1)}, u32[]{:S(2)}) copy-start(pred[512]{0:T(512)(128)(4,1)} %fusion.60) | copy-start | bytes 1540
  48.0 19.6 %collective-permute-start.11 = (bf16[1,1,8,8,128]{4,3,2,1,0:T(8,128)(2,1)S(1)}, bf16[1,1,8,8,128]{4,3,2,1,0:T(8,128)(2,1)S(1)}, u32[]{:S(2)}, u32[]{:S(2)}) collective-permute-start(bf16[1,1,8,8,128]{4,3,2,1,0:T(8,128)(2,1)S(1)} %get-tuple-element.72), channel_id=1, source_target_pairs={{10,0},{11,1},{12,2},{13,3},{14,4},{15,5},{18,8},{19,9},{20,10},{2... | collective-permute-start | bytes 49160 | tf_op jit(solution)/shard_map/ppermute | solution.py:73
  50.5 17.2 %collective-permute-start.8 = (bf16[1,1,8,8,128]{4,3,2,1,0:T(8,128)(2,1)S(1)}, bf16[1,1,8,8,128]{4,3,2,1,0:T(8,128)(2,1)S(1)}, u32[]{:S(2)}, u32[]{:S(2)}) collective-permute-start(bf16[1,1,8,8,128]{4,3,2,1,0:T(8,128)(2,1)S(1)} %get-tuple-element.71), channel_id=1, source_target_pairs={{8,2},{9,3},{10,4},{11,5},{12,6},{13,7},{16,10},{17,11},{18,12},{1... | collective-permute-start | bytes 49160 | tf_op jit(solution)/shard_map/ppermute | solution.py:73
  52.6 8.1 %collective-permute-start.10 = (bf16[1,1,1,8,128]{4,3,2,1,0:T(8,128)(2,1)S(1)}, bf16[1,1,1,8,128]{4,3,2,1,0:T(8,128)(2,1)S(1)}, u32[]{:S(2)}, u32[]{:S(2)}) collective-permute-start(bf16[1,1,1,8,128]{4,3,2,1,0:T(8,128)(2,1)S(1)} %constant_dynamic-slice_fusion.9), channel_id=1, source_target_pairs={{10,1},{11,0},{12,3},{13,2},{14,5},{15,4},{18,9},{19,8},{20,11},{2... | collective-permute-start | bytes 6152 | tf_op jit(solution)/shard_map/ppermute | solution.py:73
  56.8 14.5 %copy-start.8 = (bf16[512,128]{1,0:T(8,128)(2,1)}, bf16[512,128]{1,0:T(8,128)(2,1)S(1)}, u32[]{:S(2)}) copy-start(bf16[512,128]{1,0:T(8,128)(2,1)S(1)} %fusion.8) | copy-start | bytes 393220
  56.8 11.2 %collective-permute-start.6 = (bf16[512,128]{1,0:T(8,128)(2,1)S(1)}, bf16[512,128]{1,0:T(8,128)(2,1)S(1)}, u32[]{:S(2)}, u32[]{:S(2)}) collective-permute-start(bf16[512,128]{1,0:T(8,128)(2,1)S(1)} %fusion.8), channel_id=1, source_target_pairs={{8,0},{16,8},{24,16},{9,1},{17,9},{25,17},{10,2},{18,10},{26,18},{... | collective-permute-start | bytes 393224 | tf_op jit(solution)/shard_map/ppermute | solution.py:229
  58.8 8.7 %collective-permute-start.9 = (bf16[1,8,1,8,128]{4,3,2,1,0:T(8,128)(2,1)S(1)}, bf16[1,8,1,8,128]{4,3,2,1,0:T(8,128)(2,1)S(1)}, u32[]{:S(2)}, u32[]{:S(2)}) collective-permute-start(bf16[1,8,1,8,128]{4,3,2,1,0:T(8,128)(2,1)S(1)} %constant_dynamic-slice_fusion.10), channel_id=1, source_target_pairs={{8,1},{9,0},{10,3},{11,2},{12,5},{13,4},{14,7},{15,6},{16,9},{17,8... | collective-permute-start | bytes 49160 | tf_op jit(solution)/shard_map/ppermute | solution.py:73
  60.7 6.7 %collective-permute-start.7 = (bf16[1,1,1,8,128]{4,3,2,1,0:T(8,128)(2,1)S(1)}, bf16[1,1,1,8,128]{4,3,2,1,0:T(8,128)(2,1)S(1)}, u32[]{:S(2)}, u32[]{:S(2)}) collective-permute-start(bf16[1,1,1,8,128]{4,3,2,1,0:T(8,128)(2,1)S(1)} %constant_dynamic-slice_fusion.11), channel_id=1, source_target_pairs={{8,3},{9,2},{10,5},{11,4},{12,7},{13,6},{16,11},{17,10},{18,13},{1... | collective-permute-start | bytes 6152 | tf_op jit(solution)/shard_map/ppermute | solution.py:73
  72.0 17.4 %copy-start.6 = (bf16[512,128]{1,0:T(8,128)(2,1)}, bf16[512,128]{1,0:T(8,128)(2,1)S(1)}, u32[]{:S(2)}) copy-start(bf16[512,128]{1,0:T(8,128)(2,1)S(1)} %fusion.18) | copy-start | bytes 393220
  72.0 17.0 %collective-permute-start.12 = (bf16[512,128]{1,0:T(8,128)(2,1)S(1)}, bf16[512,128]{1,0:T(8,128)(2,1)S(1)}, u32[]{:S(2)}, u32[]{:S(2)}) collective-permute-start(bf16[512,128]{1,0:T(8,128)(2,1)S(1)} %fusion.18), channel_id=1, source_target_pairs={{8,0},{16,8},{24,16},{9,1},{17,9},{25,17},{10,2},{18,10},{26,18},{... | collective-permute-start | bytes 393224 | tf_op jit(solution)/shard_map/ppermute | solution.py:229
  73.9 14.7 %collective-permute-start.17 = (bf16[1,1,8,8,128]{4,3,2,1,0:T(8,128)(2,1)S(1)}, bf16[1,1,8,8,128]{4,3,2,1,0:T(8,128)(2,1)S(1)}, u32[]{:S(2)}, u32[]{:S(2)}) collective-permute-start(bf16[1,1,8,8,128]{4,3,2,1,0:T(8,128)(2,1)S(1)} %get-tuple-element.67), channel_id=1, source_target_pairs={{10,0},{11,1},{12,2},{13,3},{14,4},{15,5},{18,8},{19,9},{20,10},{2... | collective-permute-start | bytes 49160 | tf_op jit(solution)/shard_map/ppermute | solution.py:73
  75.9 5.8 %collective-permute-start.16 = (bf16[1,1,1,8,128]{4,3,2,1,0:T(8,128)(2,1)S(1)}, bf16[1,1,1,8,128]{4,3,2,1,0:T(8,128)(2,1)S(1)}, u32[]{:S(2)}, u32[]{:S(2)}) collective-permute-start(bf16[1,1,1,8,128]{4,3,2,1,0:T(8,128)(2,1)S(1)} %constant_dynamic-slice_fusion.6), channel_id=1, source_target_pairs={{10,1},{11,0},{12,3},{13,2},{14,5},{15,4},{18,9},{19,8},{20,11},{2... | collective-permute-start | bytes 6152 | tf_op jit(solution)/shard_map/ppermute | solution.py:73
  77.8 10.9 %collective-permute-start.14 = (bf16[1,1,8,8,128]{4,3,2,1,0:T(8,128)(2,1)S(1)}, bf16[1,1,8,8,128]{4,3,2,1,0:T(8,128)(2,1)S(1)}, u32[]{:S(2)}, u32[]{:S(2)}) collective-permute-start(bf16[1,1,8,8,128]{4,3,2,1,0:T(8,128)(2,1)S(1)} %get-tuple-element.66), channel_id=1, source_target_pairs={{8,2},{9,3},{10,4},{11,5},{12,6},{13,7},{16,10},{17,11},{18,12},{1... | collective-permute-start | bytes 49160 | tf_op jit(solution)/shard_map/ppermute | solution.py:73
  79.8 8.7 %collective-permute-start.15 = (bf16[1,8,1,8,128]{4,3,2,1,0:T(8,128)(2,1)S(1)}, bf16[1,8,1,8,128]{4,3,2,1,0:T(8,128)(2,1)S(1)}, u32[]{:S(2)}, u32[]{:S(2)}) collective-permute-start(bf16[1,8,1,8,128]{4,3,2,1,0:T(8,128)(2,1)S(1)} %constant_dynamic-slice_fusion.7), channel_id=1, source_target_pairs={{8,1},{9,0},{10,3},{11,2},{12,5},{13,4},{14,7},{15,6},{16,9},{17,8... | collective-permute-start | bytes 49160 | tf_op jit(solution)/shard_map/ppermute | solution.py:73
  81.7 6.7 %collective-permute-start.13 = (bf16[1,1,1,8,128]{4,3,2,1,0:T(8,128)(2,1)S(1)}, bf16[1,1,1,8,128]{4,3,2,1,0:T(8,128)(2,1)S(1)}, u32[]{:S(2)}, u32[]{:S(2)}) collective-permute-start(bf16[1,1,1,8,128]{4,3,2,1,0:T(8,128)(2,1)S(1)} %constant_dynamic-slice_fusion.8), channel_id=1, source_target_pairs={{8,3},{9,2},{10,5},{11,4},{12,7},{13,6},{16,11},{17,10},{18,13},{1... | collective-permute-start | bytes 6152 | tf_op jit(solution)/shard_map/ppermute | solution.py:73
  92.3 17.3 %copy-start.3 = (bf16[1,10,10,10,256]{4,0,3,2,1:T(2,128)(2,1)S(1)}, bf16[1,10,10,10,256]{4,0,3,2,1:T(2,128)(2,1)}, u32[]{:S(2)}) copy-start(bf16[1,10,10,10,256]{4,0,3,2,1:T(2,128)(2,1)} %copy-done.2) | copy-start | bytes 1536004
  93.0 16.4 %collective-permute-start.18 = (bf16[512,128]{1,0:T(8,128)(2,1)S(1)}, bf16[512,128]{1,0:T(8,128)(2,1)S(1)}, u32[]{:S(2)}, u32[]{:S(2)}) collective-permute-start(bf16[512,128]{1,0:T(8,128)(2,1)S(1)} %fusion.21), channel_id=1, source_target_pairs={{8,0},{16,8},{24,16},{9,1},{17,9},{25,17},{10,2},{18,10},{26,18},{... | collective-permute-start | bytes 393224 | tf_op jit(solution)/shard_map/ppermute | solution.py:229
  94.9 18.6 %collective-permute-start.20 = (bf16[1,1,8,8,128]{4,3,2,1,0:T(8,128)(2,1)S(1)}, bf16[1,1,8,8,128]{4,3,2,1,0:T(8,128)(2,1)S(1)}, u32[]{:S(2)}, u32[]{:S(2)}) collective-permute-start(bf16[1,1,8,8,128]{4,3,2,1,0:T(8,128)(2,1)S(1)} %get-tuple-element.65), channel_id=1, source_target_pairs={{8,2},{9,3},{10,4},{11,5},{12,6},{13,7},{16,10},{17,11},{18,12},{1... | collective-permute-start | bytes 49160 | tf_op jit(solution)/shard_map/ppermute | solution.py:73
  96.9 6.7 %collective-permute-start.19 = (bf16[1,1,1,8,128]{4,3,2,1,0:T(8,128)(2,1)S(1)}, bf16[1,1,1,8,128]{4,3,2,1,0:T(8,128)(2,1)S(1)}, u32[]{:S(2)}, u32[]{:S(2)}) collective-permute-start(bf16[1,1,1,8,128]{4,3,2,1,0:T(8,128)(2,1)S(1)} %constant_dynamic-slice_fusion.5), channel_id=1, source_target_pairs={{8,3},{9,2},{10,5},{11,4},{12,7},{13,6},{16,11},{17,10},{18,13},{1... | collective-permute-start | bytes 6152 | tf_op jit(solution)/shard_map/ppermute | solution.py:73
  98.8 14.7 %collective-permute-start.23 = (bf16[1,1,8,8,128]{4,3,2,1,0:T(8,128)(2,1)S(1)}, bf16[1,1,8,8,128]{4,3,2,1,0:T(8,128)(2,1)S(1)}, u32[]{:S(2)}, u32[]{:S(2)}) collective-permute-start(bf16[1,1,8,8,128]{4,3,2,1,0:T(8,128)(2,1)S(1)} %get-tuple-element.64), channel_id=1, source_target_pairs={{10,0},{11,1},{12,2},{13,3},{14,4},{15,5},{18,8},{19,9},{20,10},{2... | collective-permute-start | bytes 49160 | tf_op jit(solution)/shard_map/ppermute | solution.py:73
  100.8 8.6 %collective-permute-start.21 = (bf16[1,8,1,8,128]{4,3,2,1,0:T(8,128)(2,1)S(1)}, bf16[1,8,1,8,128]{4,3,2,1,0:T(8,128)(2,1)S(1)}, u32[]{:S(2)}, u32[]{:S(2)}) collective-permute-start(bf16[1,8,1,8,128]{4,3,2,1,0:T(8,128)(2,1)S(1)} %constant_dynamic-slice_fusion.4), channel_id=1, source_target_pairs={{8,1},{9,0},{10,3},{11,2},{12,5},{13,4},{14,7},{15,6},{16,9},{17,8... | collective-permute-start | bytes 49160 | tf_op jit(solution)/shard_map/ppermute | solution.py:73
  103.6 5.8 %collective-permute-start.22 = (bf16[1,1,1,8,128]{4,3,2,1,0:T(8,128)(2,1)S(1)}, bf16[1,1,1,8,128]{4,3,2,1,0:T(8,128)(2,1)S(1)}, u32[]{:S(2)}, u32[]{:S(2)}) collective-permute-start(bf16[1,1,1,8,128]{4,3,2,1,0:T(8,128)(2,1)S(1)} %constant_dynamic-slice_fusion.3), channel_id=1, source_target_pairs={{10,1},{11,0},{12,3},{13,2},{14,5},{15,4},{18,9},{19,8},{20,11},{2... | collective-permute-start | bytes 6152 | tf_op jit(solution)/shard_map/ppermute | solution.py:73
  114.5 7.1 %collective-permute-start.26 = (bf16[864,128]{1,0:T(8,128)(2,1)S(1)}, bf16[864,128]{1,0:T(8,128)(2,1)S(1)}, u32[]{:S(2)}, u32[]{:S(2)}) collective-permute-start(bf16[864,128]{1,0:T(8,128)(2,1)S(1)} %get-tuple-element.47), channel_id=1, source_target_pairs={{0,6},{2,0},{4,2},{6,4},{1,7},{3,1},{5,3},{7,5},{8,14},{10,8},{12,... | collective-permute-start | bytes 663560 | tf_op jit(solution)/shard_map/ppermute | solution.py:151
  115.8 11.0 %collective-permute-start.25 = (bf16[864,128]{1,0:T(8,128)(2,1)S(1)}, bf16[864,128]{1,0:T(8,128)(2,1)S(1)}, u32[]{:S(2)}, u32[]{:S(2)}) collective-permute-start(bf16[864,128]{1,0:T(8,128)(2,1)S(1)} %get-tuple-element.48), channel_id=1, source_target_pairs={{0,4},{2,6},{4,0},{6,2},{1,5},{3,7},{5,1},{7,3},{8,12},{10,14},{12... | collective-permute-start | bytes 663560 | tf_op jit(solution)/shard_map/ppermute | solution.py:151
  115.8 11.0 %collective-permute-start.24 = (bf16[864,128]{1,0:T(8,128)(2,1)S(1)}, bf16[864,128]{1,0:T(8,128)(2,1)S(1)}, u32[]{:S(2)}, u32[]{:S(2)}) collective-permute-start(bf16[864,128]{1,0:T(8,128)(2,1)S(1)} %get-tuple-element.46), channel_id=1, source_target_pairs={{0,2},{2,4},{4,6},{6,0},{1,3},{3,5},{5,7},{7,1},{8,10},{10,12},{12... | collective-permute-start | bytes 663560 | tf_op jit(solution)/shard_map/ppermute | solution.py:151
  119.2 9.4 %copy-start.7 = (bf16[512,128]{1,0:T(8,128)(2,1)S(1)}, bf16[512,128]{1,0:T(8,128)(2,1)}, u32[]{:S(2)}) copy-start(bf16[512,128]{1,0:T(8,128)(2,1)} %copy-done.6) | copy-start | bytes 393220
  119.2 9.4 %copy-start.9 = (bf16[512,128]{1,0:T(8,128)(2,1)S(1)}, bf16[512,128]{1,0:T(8,128)(2,1)}, u32[]{:S(2)}) copy-start(bf16[512,128]{1,0:T(8,128)(2,1)} %copy-done.8) | copy-start | bytes 393220
  127.0 3.0 %collective-permute-start.27 = (f32[864,128]{1,0:T(8,128)S(1)}, f32[864,128]{1,0:T(8,128)S(1)}, u32[]{:S(2)}, u32[]{:S(2)}) collective-permute-start(f32[864,128]{1,0:T(8,128)S(1)} %convert_add_fusion), channel_id=1, source_target_pairs={{0,1},{1,0},{2,3},{3,2},{4,5},{5,4},{6,7},{7,6},{8,9},{9,8},{10,11... | collective-permute-start | bytes 1327112 | tf_op jit(solution)/shard_map/ppermute | solution.py:234

commit v8 on v7

--- a/solution.py
+++ b/solution.py
@@ -154,6 +154,13 @@
     return total
 
 
+def reduced_rows(term, share_rows):
+    over_x = scattered_sum(term, "sx", share_rows)
+    if lax.axis_size("sy") == 2:
+        return over_x + lax.ppermute(over_x, "sy", [(0, 1), (1, 0)])
+    return lax.psum(over_x, "sy")
+
+
 def finish_grad(values, grad_live, live_now, grad_act, gain_row):
     _, pullback = jax.vjp(lambda floats: activate(floats, gain_row), values.astype(jnp.float32))
     (through,) = pullback(grad_act)
@@ -187,6 +194,8 @@
     norm_scale = float(n_x * n_y * micro_count * row_count) ** (-0.5)
     shard_rows = kernel.shape[1]
     kernel_term = None
+    kernel_share = None
+    shifted = micro_count == 1 and n_pipe >= 2
     for micro in range(micro_count):
         table = tables[micro]
         live_now = live_rows[micro]
@@ -205,6 +214,8 @@
             got = exchange(both, ("sx", "sy"), (n_x, n_y), 0)
         both_pad = assemble(both, got, table, split=True)
         act_pad = both_pad[..., :channels]
+        if shifted:
+            act_up = lax.ppermute(act_pad, "pipe", [(q, (q + 1) % n_pipe) for q in range(n_pipe)])
         centre = start
         received = None
         kept_dy = start
@@ -212,7 +223,7 @@
         for tick in range(n_pipe):
             active = segment_place == n_pipe - 1 - tick
             kept_dy = jnp.where(active, centre, kept_dy)
-            if tick == n_pipe - 1:
+            if tick == n_pipe - 1 and not shifted:
                 per_tap = conv_filter(act_pad, cube(kept_dy))
                 kernel_total = kernel_total + per_tap.transpose(1, 2, 3, 0, 4).reshape(taps * channels, channels)
                 if micro == micro_count - 1:
@@ -224,18 +235,20 @@
             grad_act = conv_data(grad_pad, flipped).reshape(row_count, channels)
             result = finish_grad(values, centre, live_now, grad_act, gain_row)
             kept_grad = jnp.where(active, result, kept_grad)
+            if shifted and tick == n_pipe - 2:
+                up_dy = jnp.where(segment_place == 0, start, kept_grad)
+                per_tap = conv_filter(act_up, cube(up_dy))
+                term = per_tap.transpose(1, 2, 3, 0, 4).reshape(taps * channels, channels) * norm_scale
+                share_up = reduced_rows(term.astype(jnp.bfloat16), shard_rows)
+                kernel_share = lax.ppermute(share_up, "pipe", [(q, (q - 1) % n_pipe) for q in range(n_pipe)])
             if tick < n_pipe - 1:
                 down = [(p, p - 1) for p in range(1, n_pipe)]
                 centre = lax.ppermute(result, "pipe", down)
                 received = exchange(cube(result), ("pipe", "sx", "sy"), (n_pipe, n_x, n_y), 1)
         grads_out.append(kept_grad)
     grad_store = jnp.stack(grads_out)
-    over_x = scattered_sum(kernel_term, "sx", shard_rows)
-    partner = lax.ppermute(over_x, "sy", [(i, i ^ 1) for i in range(n_y)]) if n_y == 2 else None
-    if partner is not None:
-        kernel_share = over_x + partner
-    else:
-        kernel_share = lax.psum(over_x, "sy")
+    if not shifted:
+        kernel_share = reduced_rows(kernel_term, shard_rows)
     return (grad_store[None, :, None, None], kernel_share[None])
 
 

time: 132 us -> 160 us (1.21)
  the two profiles are of different devices: /device:TPU:21 before, /device:TPU:26 now
where the time goes in v8:
time: 160 us; the launch traced here: 159 us
  starting transfers between devices  68.5 us (43%)
  waiting for transfers between devices  31.5 us (20%)
  between operations  19.8 us (12%)
  matrix products  15.7 us (10%)
  other arithmetic  14.4 us (9%)
  local copies, waits for them, and re-layouts  8.66 us (5%)
    ppermute x20, starting transfers between devices, send(): return lax.ppermute(piece, axes, route)  53.2 us
    ppermute x1, waiting for transfers between devices, shards(): lax.ppermute(share_up, 'pipe', [(q, (q - 1) % n_pipe) for q in range(n_pi...  11.9 us
    conv_general_dilated x4, matrix products, conv_data(): lax.conv_general_dilated(padded, filters, (1, 1, 1), 'VALID', dimension_n...  11.8 us
    ppermute x3, waiting for transfers between devices, scattered_sum(): lax.ppermute(piece, axis, [(i, (i + step) % count) for i in range(count)])  11.4 us
    ppermute x20, waiting for transfers between devices, send(): return lax.ppermute(piece, axes, route)  8.13 us
    ppermute x3, starting transfers between devices, shards(): centre = lax.ppermute(result, 'pipe', down)  8.12 us
    transpose x1, matrix products, shards(): per_tap.transpose(1, 2, 3, 0, 4).reshape(taps * channels, channels)  3.92 us
  transfers between devices with their start and end apart: 30, of which 8 were waited for; matrix products, arithmetic and copies ran while one was open for 16% of the time, Pallas kernels for 0%

profile of v8, /device:TPU:26, one launch (start us, length us, event | category | flops | bytes accessed | tf_op | source)
XLA Modules:
  0.0 158.6 jit_solution(2833191427513373288)
XLA Ops:
  0.6 1.1 fusion.24
  1.7 0.9 convert_element_type.160
  3.5 1.0 broadcast_select_fusion.12
  4.6 0.9 multiply_convert_fusion.2
  5.5 2.8 %collective-permute-start = (bf16[1,1,1,8,256]{4,3,2,1,0:T(8,128)(2,1)S(1)}, bf16[1,1,1,8,256]{4,3,2,1,0:T(8,128)(2,1)S(1)}, u32[]{:S(2)}, u32[]{:S(2)}) collective-permute-start(bf16[1,1,1,8,256]{4,3,2,1,0:T(8,128)(2,1)S(1)} %constant_dynamic-slice_fusion.13), channel_id=1, source_target_pairs={{0,3},{1,2},{2,5},{3,4},{4,7},{5,6},{8,11},{9,10},{10,13},{11,12},... | collective-permute-start | bytes 12296 | tf_op jit(solution)/shard_map/ppermute | solution.py:73
  8.3 2.7 %collective-permute-start.2 = (bf16[1,1,1,8,256]{4,3,2,1,0:T(8,128)(2,1)S(1)}, bf16[1,1,1,8,256]{4,3,2,1,0:T(8,128)(2,1)S(1)}, u32[]{:S(2)}, u32[]{:S(2)}) collective-permute-start(bf16[1,1,1,8,256]{4,3,2,1,0:T(8,128)(2,1)S(1)} %constant_dynamic-slice_fusion.12), channel_id=1, source_target_pairs={{2,1},{3,0},{4,3},{5,2},{6,5},{7,4},{10,9},{11,8},{12,11},{13,10},... | collective-permute-start | bytes 12296 | tf_op jit(solution)/shard_map/ppermute | solution.py:73
  11.1 1.6 collective-permute-start.5
  12.8 1.5 collective-permute-start.3
  14.3 1.5 collective-permute-start.1
  15.8 0.7 fusion.75
  16.5 0.7 fusion.76
  19.7 0.6 scatter_custom_fusion
  20.4 0.6 fusion.59
  20.9 0.4 copy_dynamic-update-slice_fusion
  21.3 1.4 broadcast_select_fusion
  22.7 0.8 broadcast_select_fusion.2
  38.6 1.0 collective-permute-done.4
  39.8 0.7 copy.47
  41.3 0.7 gather_fusion
  42.1 1.1 rev.3
  43.3 2.1 %pad_maximum_fusion = bf16[1,10,10,10,256]{4,0,3,2,1:T(2,128)(2,1)S(1)} fusion(bf16[1,1,10,10,256]{4,0,3,2,1:T(2,128)(2,1)S(1)} %pad_maximum_fusion.11, bf16[1,8,1,10,256]{4,0,3,2,1:T(2,128)(2,1)S(1)} %copy-done.6, bf16[1,8,8,1,256]{4,0,3,2,1:T(2,128)(2,1)S(1)} %copy-done.10, bf16[1,8,8,8,256]{4,0,3,2,1:T(2,128)(2,1)S(1)} %copy-done.2, ...), kind=kLoop, calls=%fused_computation.4 | loop fusion | flops 1536000 | bytes 1024000 | tf_op jit(solution)/shard_map/concatenate | solution.py:56
  45.5 2.9 %fusion = f32[1,8,8,8,128]{4,0,3,2,1:T(1,128)S(1)} fusion(bf16[3,3,3,128,128]{4,3,2,1,0:T(8,128)(2,1)S(1)} %copy-done.3, bf16[1,10,10,10,256]{4,0,3,2,1:T(2,128)(2,1)S(1)} %pad_maximum_fusion), kind=kOutput, calls=%fused_computation.9 | convolution fusion | flops 452984832 | bytes 1658880 | tf_op jit(solution)/shard_map/conv_general_dilated | solution.py:108
  48.4 0.3 fusion.46
  49.2 1.8 %collective-permute-start.8 = (bf16[1,1,8,8,128]{4,3,2,1,0:T(8,128)(2,1)S(1)}, bf16[1,1,8,8,128]{4,3,2,1,0:T(8,128)(2,1)S(1)}, u32[]{:S(2)}, u32[]{:S(2)}) collective-permute-start(bf16[1,1,8,8,128]{4,3,2,1,0:T(8,128)(2,1)S(1)} %get-tuple-element.58), channel_id=1, source_target_pairs={{8,2},{9,3},{10,4},{11,5},{12,6},{13,7},{16,10},{17,11},{18,12},{1... | collective-permute-start | bytes 49160 | tf_op jit(solution)/shard_map/ppermute | solution.py:73
  51.1 3.8 %collective-permute-start.11 = (bf16[1,1,8,8,128]{4,3,2,1,0:T(8,128)(2,1)S(1)}, bf16[1,1,8,8,128]{4,3,2,1,0:T(8,128)(2,1)S(1)}, u32[]{:S(2)}, u32[]{:S(2)}) collective-permute-start(bf16[1,1,8,8,128]{4,3,2,1,0:T(8,128)(2,1)S(1)} %get-tuple-element.59), channel_id=1, source_target_pairs={{10,0},{11,1},{12,2},{13,3},{14,4},{15,5},{18,8},{19,9},{20,10},{2... | collective-permute-start | bytes 49160 | tf_op jit(solution)/shard_map/ppermute | solution.py:73
  54.9 0.5 slice.606
  55.4 2.3 %collective-permute-start.7 = (bf16[1,1,1,8,128]{4,3,2,1,0:T(8,128)(2,1)S(1)}, bf16[1,1,1,8,128]{4,3,2,1,0:T(8,128)(2,1)S(1)}, u32[]{:S(2)}, u32[]{:S(2)}) collective-permute-start(bf16[1,1,1,8,128]{4,3,2,1,0:T(8,128)(2,1)S(1)} %constant_dynamic-slice_fusion.11), channel_id=1, source_target_pairs={{8,3},{9,2},{10,5},{11,4},{12,7},{13,6},{16,11},{17,10},{18,13},{1... | collective-permute-start | bytes 6152 | tf_op jit(solution)/shard_map/ppermute | solution.py:73
  57.8 2.0 %collective-permute-start.9 = (bf16[1,8,1,8,128]{4,3,2,1,0:T(8,128)(2,1)S(1)}, bf16[1,8,1,8,128]{4,3,2,1,0:T(8,128)(2,1)S(1)}, u32[]{:S(2)}, u32[]{:S(2)}) collective-permute-start(bf16[1,8,1,8,128]{4,3,2,1,0:T(8,128)(2,1)S(1)} %constant_dynamic-slice_fusion.10), channel_id=1, source_target_pairs={{8,1},{9,0},{10,3},{11,2},{12,5},{13,4},{14,7},{15,6},{16,9},{17,8... | collective-permute-start | bytes 49160 | tf_op jit(solution)/shard_map/ppermute | solution.py:73
  60.1 2.0 %collective-permute-start.6 = (bf16[512,128]{1,0:T(8,128)(2,1)S(1)}, bf16[512,128]{1,0:T(8,128)(2,1)S(1)}, u32[]{:S(2)}, u32[]{:S(2)}) collective-permute-start(bf16[512,128]{1,0:T(8,128)(2,1)S(1)} %fusion.7), channel_id=1, source_target_pairs={{8,0},{16,8},{24,16},{9,1},{17,9},{25,17},{10,2},{18,10},{26,18},{... | collective-permute-start | bytes 393224 | tf_op jit(solution)/shard_map/ppermute | solution.py:246
  62.0 1.3 collective-permute-start.10
  63.4 2.0 %collective-permute-done.10 = bf16[1,1,1,8,128]{4,3,2,1,0:T(8,128)(2,1)S(1)} collective-permute-done((bf16[1,1,1,8,128]{4,3,2,1,0:T(8,128)(2,1)S(1)}, bf16[1,1,1,8,128]{4,3,2,1,0:T(8,128)(2,1)S(1)}, u32[]{:S(2)}, u32[]{:S(2)}) %collective-permute-start.10) | collective-permute-done | bytes 2080 | tf_op jit(solution)/shard_map/ppermute | solution.py:73
  65.3 1.4 collective-permute-start.24
  67.7 3.0 %fusion.4 = f32[1,8,8,8,128]{4,0,3,2,1:T(1,128)S(1)} fusion(bf16[3,3,3,128,128]{4,3,2,1,0:T(8,128)(2,1)S(1)} %bitcast.209, bf16[1,1,10,10,128]{4,0,3,2,1:T(2,128)(2,1)S(1)} %copy.56, bf16[1,8,1,10,128]{4,0,3,2,1:T(2,128)(2,1)S(1)} %copy.54, bf16[1,8,8,1,128]{4,0,3,2,1:T(2,128)(2,1)S(1)} %slice_bitcast_fusion.6, bf16[1,8,8,8,128]{4,0,3,2,1:T(2,128)(2,1)S(1)} %copy.52, ...), kind=kOutput, calls=%fused_computation.13 | convolution fusion | flops 454776832 | bytes 1402880 | tf_op jit(solution)/shard_map/conv_general_dilated | solution.py:108
  70.6 0.3 fusion.47
  71.0 0.3 fusion.17
  71.3 4.2 %collective-permute-start.14 = (bf16[1,1,8,8,128]{4,3,2,1,0:T(8,128)(2,1)S(1)}, bf16[1,1,8,8,128]{4,3,2,1,0:T(8,128)(2,1)S(1)}, u32[]{:S(2)}, u32[]{:S(2)}) collective-permute-start(bf16[1,1,8,8,128]{4,3,2,1,0:T(8,128)(2,1)S(1)} %get-tuple-element.53), channel_id=1, source_target_pairs={{8,2},{9,3},{10,4},{11,5},{12,6},{13,7},{16,10},{17,11},{18,12},{1... | collective-permute-start | bytes 49160 | tf_op jit(solution)/shard_map/ppermute | solution.py:73
  75.6 3.7 %collective-permute-start.12 = (bf16[512,128]{1,0:T(8,128)(2,1)S(1)}, bf16[512,128]{1,0:T(8,128)(2,1)S(1)}, u32[]{:S(2)}, u32[]{:S(2)}) collective-permute-start(bf16[512,128]{1,0:T(8,128)(2,1)S(1)} %fusion.17), channel_id=1, source_target_pairs={{8,0},{16,8},{24,16},{9,1},{17,9},{25,17},{10,2},{18,10},{26,18},{... | collective-permute-start | bytes 393224 | tf_op jit(solution)/shard_map/ppermute | solution.py:246
  79.3 1.3 collective-permute-start.13
  80.6 3.1 %collective-permute-start.17 = (bf16[1,1,8,8,128]{4,3,2,1,0:T(8,128)(2,1)S(1)}, bf16[1,1,8,8,128]{4,3,2,1,0:T(8,128)(2,1)S(1)}, u32[]{:S(2)}, u32[]{:S(2)}) collective-permute-start(bf16[1,1,8,8,128]{4,3,2,1,0:T(8,128)(2,1)S(1)} %get-tuple-element.54), channel_id=1, source_target_pairs={{10,0},{11,1},{12,2},{13,3},{14,4},{15,5},{18,8},{19,9},{20,10},{2... | collective-permute-start | bytes 49160 | tf_op jit(solution)/shard_map/ppermute | solution.py:73
  83.7 1.3 collective-permute-start.16
  85.1 1.3 collective-permute-done.16
  86.3 7.2 %collective-permute-start.15 = (bf16[1,8,1,8,128]{4,3,2,1,0:T(8,128)(2,1)S(1)}, bf16[1,8,1,8,128]{4,3,2,1,0:T(8,128)(2,1)S(1)}, u32[]{:S(2)}, u32[]{:S(2)}) collective-permute-start(bf16[1,8,1,8,128]{4,3,2,1,0:T(8,128)(2,1)S(1)} %constant_dynamic-slice_fusion.7), channel_id=1, source_target_pairs={{8,1},{9,0},{10,3},{11,2},{12,5},{13,4},{14,7},{15,6},{16,9},{17,8... | collective-permute-start | bytes 49160 | tf_op jit(solution)/shard_map/ppermute | solution.py:73
  93.6 1.3 collective-permute-done.15
  95.8 3.0 %fusion.3 = f32[1,8,8,8,128]{4,0,3,2,1:T(1,128)S(1)} fusion(bf16[3,3,3,128,128]{4,3,2,1,0:T(8,128)(2,1)S(1)} %bitcast.210, bf16[1,1,10,10,128]{4,0,3,2,1:T(2,128)(2,1)S(1)} %copy.63, bf16[1,8,1,10,128]{4,0,3,2,1:T(2,128)(2,1)S(1)} %copy.61, bf16[1,8,8,1,128]{4,0,3,2,1:T(2,128)(2,1)S(1)} %slice_bitcast_fusion.4, bf16[1,8,8,8,128]{4,0,3,2,1:T(2,128)(2,1)S(1)} %copy.59, ...), kind=kOutput, calls=%fused_computation.12 | convolution fusion | flops 454776832 | bytes 1402880 | tf_op jit(solution)/shard_map/conv_general_dilated | solution.py:108
  98.7 0.3 fusion.48
  99.1 0.4 broadcast_select_fusion.13
  99.5 3.9 %collective-permute-start.20 = (bf16[1,1,8,8,128]{4,3,2,1,0:T(8,128)(2,1)S(1)}, bf16[1,1,8,8,128]{4,3,2,1,0:T(8,128)(2,1)S(1)}, u32[]{:S(2)}, u32[]{:S(2)}) collective-permute-start(bf16[1,1,8,8,128]{4,3,2,1,0:T(8,128)(2,1)S(1)} %get-tuple-element.48), channel_id=1, source_target_pairs={{8,2},{9,3},{10,4},{11,5},{12,6},{13,7},{16,10},{17,11},{18,12},{1... | collective-permute-start | bytes 49160 | tf_op jit(solution)/shard_map/ppermute | solution.py:73
  103.4 2.4 %collective-permute-start.18 = (bf16[512,128]{1,0:T(8,128)(2,1)S(1)}, bf16[512,128]{1,0:T(8,128)(2,1)S(1)}, u32[]{:S(2)}, u32[]{:S(2)}) collective-permute-start(bf16[512,128]{1,0:T(8,128)(2,1)S(1)} %get-tuple-element.8), channel_id=1, source_target_pairs={{8,0},{16,8},{24,16},{9,1},{17,9},{25,17},{10,2},{18,10},{26,18},{... | collective-permute-start | bytes 393224 | tf_op jit(solution)/shard_map/ppermute | solution.py:246
  105.8 1.6 collective-permute-start.19
  107.4 4.7 %collective-permute-start.23 = (bf16[1,1,8,8,128]{4,3,2,1,0:T(8,128)(2,1)S(1)}, bf16[1,1,8,8,128]{4,3,2,1,0:T(8,128)(2,1)S(1)}, u32[]{:S(2)}, u32[]{:S(2)}) collective-permute-start(bf16[1,1,8,8,128]{4,3,2,1,0:T(8,128)(2,1)S(1)} %get-tuple-element.49), channel_id=1, source_target_pairs={{10,0},{11,1},{12,2},{13,3},{14,4},{15,5},{18,8},{19,9},{20,10},{2... | collective-permute-start | bytes 49160 | tf_op jit(solution)/shard_map/ppermute | solution.py:73
  112.2 3.9 %multiply_convert_fusion = bf16[3,3,3,128,128]{4,3,2,1,0:T(8,128)(2,1)S(1)} fusion(bf16[1,10,10,10,128]{4,0,3,2,1:T(2,128)(2,1)S(1)} %collective-permute-done.24, bf16[1,8,8,8,128]{4,3,2,1,0:T(8,128)(2,1)S(1)} %bitcast.245), kind=kOutput, calls=%fused_computation.2 | convolution fusion | flops 453869568 | bytes 1271808 | tf_op jit(solution)/shard_map/transpose | solution.py:241
  116.1 2.1 %collective-permute-start.25 = (bf16[864,128]{1,0:T(8,128)(2,1)S(1)}, bf16[864,128]{1,0:T(8,128)(2,1)S(1)}, u32[]{:S(2)}, u32[]{:S(2)}) collective-permute-start(bf16[864,128]{1,0:T(8,128)(2,1)S(1)} %get-tuple-element.33), channel_id=1, source_target_pairs={{0,2},{2,4},{4,6},{6,0},{1,3},{3,5},{5,7},{7,1},{8,10},{10,12},{12... | collective-permute-start | bytes 663560 | tf_op jit(solution)/shard_map/ppermute | solution.py:151
  118.2 1.3 collective-permute-start.22
  119.5 1.3 collective-permute-done.22
  120.8 4.9 %collective-permute-start.21 = (bf16[1,8,1,8,128]{4,3,2,1,0:T(8,128)(2,1)S(1)}, bf16[1,8,1,8,128]{4,3,2,1,0:T(8,128)(2,1)S(1)}, u32[]{:S(2)}, u32[]{:S(2)}) collective-permute-start(bf16[1,8,1,8,128]{4,3,2,1,0:T(8,128)(2,1)S(1)} %constant_dynamic-slice_fusion.4), channel_id=1, source_target_pairs={{8,1},{9,0},{10,3},{11,2},{12,5},{13,4},{14,7},{15,6},{16,9},{17,8... | collective-permute-start | bytes 49160 | tf_op jit(solution)/shard_map/ppermute | solution.py:73
  125.8 1.3 collective-permute-done.21
  127.2 0.5 collective-permute-start.27
  128.4 11.4 %collective-permute-done.26 = bf16[864,128]{1,0:T(8,128)(2,1)S(1)} collective-permute-done((bf16[864,128]{1,0:T(8,128)(2,1)S(1)}, bf16[864,128]{1,0:T(8,128)(2,1)S(1)}, u32[]{:S(2)}, u32[]{:S(2)}) %collective-permute-start.26) | collective-permute-done | bytes 221216 | tf_op jit(solution)/shard_map/ppermute | solution.py:151
  140.1 2.9 %fusion.2 = f32[1,8,8,8,128]{4,0,3,2,1:T(1,128)S(1)} fusion(bf16[3,3,3,128,128]{4,3,2,1,0:T(8,128)(2,1)S(1)} %bitcast.211, bf16[1,1,10,10,128]{4,0,3,2,1:T(2,128)(2,1)S(1)} %copy.70, bf16[1,8,1,10,128]{4,0,3,2,1:T(2,128)(2,1)S(1)} %copy.68, bf16[1,8,8,1,128]{4,0,3,2,1:T(2,128)(2,1)S(1)} %slice_bitcast_fusion.2, bf16[1,8,8,8,128]{4,0,3,2,1:T(2,128)(2,1)S(1)} %copy.66, ...), kind=kOutput, calls=%fused_computation.11 | convolution fusion | flops 454776832 | bytes 1402880 | tf_op jit(solution)/shard_map/conv_general_dilated | solution.py:108
  143.0 0.3 fusion.49
  143.4 1.5 collective-permute-start.29
  144.9 1.0 fusion.52
  145.9 11.9 %collective-permute-done.29 = f32[864,128]{1,0:T(8,128)S(1)} collective-permute-done((f32[864,128]{1,0:T(8,128)S(1)}, f32[864,128]{1,0:T(8,128)S(1)}, u32[]{:S(2)}, u32[]{:S(2)}) %collective-permute-start.29) | collective-permute-done | bytes 442400 | tf_op jit(solution)/shard_map/ppermute | solution.py:243
  157.8 0.8 copy.85
  (214 shorter events, 5.4 us)
Async XLA Ops:
  0.6 10.4 %copy-start.4 = (bf16[1,864,128]{2,1,0:T(8,128)(2,1)S(1)}, bf16[1,864,128]{2,1,0:T(8,128)(2,1)}, u32[]{:S(2)}) copy-start(bf16[1,864,128]{2,1,0:T(8,128)(2,1)} %param.11) | copy-start | bytes 663556
  2.8 0.7 copy-start.7
  2.8 13.0 %copy-start.5 = (s32[1,1,1,1,27]{4,3,2,1,0:T(1,128)S(1)}, s32[1,1,1,1,27]{4,3,2,1,0:T(1,128)}, u32[]{:S(2)}) copy-start(s32[1,1,1,1,27]{4,3,2,1,0:T(1,128)} %param.8) | copy-start | bytes 328
  4.6 12.7 %copy-start.11 = (f32[1,128]{1,0:T(1,128)S(1)}, f32[1,128]{1,0:T(1,128)}, u32[]{:S(2)}) copy-start(f32[1,128]{1,0:T(1,128)} %param.10) | copy-start | bytes 1540
  5.5 32.8 %collective-permute-start = (bf16[1,1,1,8,256]{4,3,2,1,0:T(8,128)(2,1)S(1)}, bf16[1,1,1,8,256]{4,3,2,1,0:T(8,128)(2,1)S(1)}, u32[]{:S(2)}, u32[]{:S(2)}) collective-permute-start(bf16[1,1,1,8,256]{4,3,2,1,0:T(8,128)(2,1)S(1)} %constant_dynamic-slice_fusion.13), channel_id=1, source_target_pairs={{0,3},{1,2},{2,5},{3,4},{4,7},{5,6},{8,11},{9,10},{10,13},{11,12},... | collective-permute-start | bytes 12296 | tf_op jit(solution)/shard_map/ppermute | solution.py:73
  8.3 30.0 %collective-permute-start.2 = (bf16[1,1,1,8,256]{4,3,2,1,0:T(8,128)(2,1)S(1)}, bf16[1,1,1,8,256]{4,3,2,1,0:T(8,128)(2,1)S(1)}, u32[]{:S(2)}, u32[]{:S(2)}) collective-permute-start(bf16[1,1,1,8,256]{4,3,2,1,0:T(8,128)(2,1)S(1)} %constant_dynamic-slice_fusion.12), channel_id=1, source_target_pairs={{2,1},{3,0},{4,3},{5,2},{6,5},{7,4},{10,9},{11,8},{12,11},{13,10},... | collective-permute-start | bytes 12296 | tf_op jit(solution)/shard_map/ppermute | solution.py:73
  11.1 30.1 %collective-permute-start.5 = (bf16[864,128]{1,0:T(8,128)(2,1)S(1)}, bf16[864,128]{1,0:T(8,128)(2,1)S(1)}, u32[]{:S(2)}, u32[]{:S(2)}) collective-permute-start(bf16[864,128]{1,0:T(8,128)(2,1)S(1)} %bitcast.224), channel_id=1, source_target_pairs={{0,4},{2,6},{4,0},{6,2},{1,5},{3,7},{5,1},{7,3},{8,12},{10,14},{12... | collective-permute-start | bytes 663560 | tf_op jit(solution)/shard_map/ppermute | solution.py:137
  12.7 4.9 %copy-start.1 = (bf16[1,1,1,512,128]{4,3,2,1,0:T(8,128)(2,1)S(1)}, bf16[1,1,1,512,128]{4,3,2,1,0:T(8,128)(2,1)}, u32[]{:S(2)}) copy-start(bf16[1,1,1,512,128]{4,3,2,1,0:T(8,128)(2,1)} %param.7) | copy-start | bytes 393220
  12.8 27.7 %collective-permute-start.3 = (bf16[992,128]{1,0:T(8,128)(2,1)S(1)}, bf16[992,128]{1,0:T(8,128)(2,1)S(1)}, u32[]{:S(2)}, u32[]{:S(2)}) collective-permute-start(bf16[992,128]{1,0:T(8,128)(2,1)S(1)} %get-tuple-element.47), channel_id=1, source_target_pairs={{0,6},{1,7},{2,0},{3,1},{4,2},{5,3},{6,4},{7,5},{8,14},{9,15},{10,... | collective-permute-start | bytes 761864 | tf_op jit(solution)/shard_map/ppermute | solution.py:73
  14.3 26.3 %collective-permute-start.1 = (bf16[992,128]{1,0:T(8,128)(2,1)S(1)}, bf16[992,128]{1,0:T(8,128)(2,1)S(1)}, u32[]{:S(2)}, u32[]{:S(2)}) collective-permute-start(bf16[992,128]{1,0:T(8,128)(2,1)S(1)} %get-tuple-element.46), channel_id=1, source_target_pairs={{0,2},{1,3},{2,4},{3,5},{4,6},{5,7},{6,0},{7,1},{8,10},{9,11},{10,... | collective-permute-start | bytes 761864 | tf_op jit(solution)/shard_map/ppermute | solution.py:73
  38.3 1.3 collective-permute-start.4
  42.0 1.1 copy-start.2
  42.0 1.2 copy-start.6
  42.0 1.2 copy-start.9
  42.1 1.3 copy-start.10
  43.3 2.1 %copy-start.3 = (bf16[3,3,3,128,128]{4,3,2,1,0:T(8,128)(2,1)S(1)}, bf16[3,3,3,128,128]{4,3,2,1,0:T(8,128)(2,1)}, u32[]{:S(2)}) copy-start(bf16[3,3,3,128,128]{4,3,2,1,0:T(8,128)(2,1)} %rev.3) | copy-start | bytes 2654212
  45.5 3.0 %copy-start = (bf16[1,1,1,1,512,128]{5,4,3,2,1,0:T(8,128)(2,1)S(1)}, bf16[1,1,1,1,512,128]{5,4,3,2,1,0:T(8,128)(2,1)}, u32[]{:S(2)}) copy-start(bf16[1,1,1,1,512,128]{5,4,3,2,1,0:T(8,128)(2,1)} %param.6) | copy-start | bytes 393220
  45.5 3.4 %copy-start.8 = (f32[8,8,8]{2,1,0:T(8,128)S(1)}, f32[8,8,8]{2,1,0:T(8,128)}, u32[]{:S(2)}) copy-start(f32[8,8,8]{2,1,0:T(8,128)} %copy-done.7) | copy-start | bytes 6148
  48.9 10.8 %copy-start.12 = (pred[512]{0:T(512)(128)(4,1)S(1)}, pred[512]{0:T(512)(128)(4,1)}, u32[]{:S(2)}) copy-start(pred[512]{0:T(512)(128)(4,1)} %fusion.59) | copy-start | bytes 1540
  49.2 17.7 %collective-permute-start.8 = (bf16[1,1,8,8,128]{4,3,2,1,0:T(8,128)(2,1)S(1)}, bf16[1,1,8,8,128]{4,3,2,1,0:T(8,128)(2,1)S(1)}, u32[]{:S(2)}, u32[]{:S(2)}) collective-permute-start(bf16[1,1,8,8,128]{4,3,2,1,0:T(8,128)(2,1)S(1)} %get-tuple-element.58), channel_id=1, source_target_pairs={{8,2},{9,3},{10,4},{11,5},{12,6},{13,7},{16,10},{17,11},{18,12},{1... | collective-permute-start | bytes 49160 | tf_op jit(solution)/shard_map/ppermute | solution.py:73
  51.1 16.0 %collective-permute-start.11 = (bf16[1,1,8,8,128]{4,3,2,1,0:T(8,128)(2,1)S(1)}, bf16[1,1,8,8,128]{4,3,2,1,0:T(8,128)(2,1)S(1)}, u32[]{:S(2)}, u32[]{:S(2)}) collective-permute-start(bf16[1,1,8,8,128]{4,3,2,1,0:T(8,128)(2,1)S(1)} %get-tuple-element.59), channel_id=1, source_target_pairs={{10,0},{11,1},{12,2},{13,3},{14,4},{15,5},{18,8},{19,9},{20,10},{2... | collective-permute-start | bytes 49160 | tf_op jit(solution)/shard_map/ppermute | solution.py:73
  55.4 6.6 %collective-permute-start.7 = (bf16[1,1,1,8,128]{4,3,2,1,0:T(8,128)(2,1)S(1)}, bf16[1,1,1,8,128]{4,3,2,1,0:T(8,128)(2,1)S(1)}, u32[]{:S(2)}, u32[]{:S(2)}) collective-permute-start(bf16[1,1,1,8,128]{4,3,2,1,0:T(8,128)(2,1)S(1)} %constant_dynamic-slice_fusion.11), channel_id=1, source_target_pairs={{8,3},{9,2},{10,5},{11,4},{12,7},{13,6},{16,11},{17,10},{18,13},{1... | collective-permute-start | bytes 6152 | tf_op jit(solution)/shard_map/ppermute | solution.py:73
  57.8 9.1 %collective-permute-start.9 = (bf16[1,8,1,8,128]{4,3,2,1,0:T(8,128)(2,1)S(1)}, bf16[1,8,1,8,128]{4,3,2,1,0:T(8,128)(2,1)S(1)}, u32[]{:S(2)}, u32[]{:S(2)}) collective-permute-start(bf16[1,8,1,8,128]{4,3,2,1,0:T(8,128)(2,1)S(1)} %constant_dynamic-slice_fusion.10), channel_id=1, source_target_pairs={{8,1},{9,0},{10,3},{11,2},{12,5},{13,4},{14,7},{15,6},{16,9},{17,8... | collective-permute-start | bytes 49160 | tf_op jit(solution)/shard_map/ppermute | solution.py:73
  60.1 7.3 %collective-permute-start.6 = (bf16[512,128]{1,0:T(8,128)(2,1)S(1)}, bf16[512,128]{1,0:T(8,128)(2,1)S(1)}, u32[]{:S(2)}, u32[]{:S(2)}) collective-permute-start(bf16[512,128]{1,0:T(8,128)(2,1)S(1)} %fusion.7), channel_id=1, source_target_pairs={{8,0},{16,8},{24,16},{9,1},{17,9},{25,17},{10,2},{18,10},{26,18},{... | collective-permute-start | bytes 393224 | tf_op jit(solution)/shard_map/ppermute | solution.py:246
  62.0 3.3 %collective-permute-start.10 = (bf16[1,1,1,8,128]{4,3,2,1,0:T(8,128)(2,1)S(1)}, bf16[1,1,1,8,128]{4,3,2,1,0:T(8,128)(2,1)S(1)}, u32[]{:S(2)}, u32[]{:S(2)}) collective-permute-start(bf16[1,1,1,8,128]{4,3,2,1,0:T(8,128)(2,1)S(1)} %constant_dynamic-slice_fusion.9), channel_id=1, source_target_pairs={{10,1},{11,0},{12,3},{13,2},{14,5},{15,4},{18,9},{19,8},{20,11},{2... | collective-permute-start | bytes 6152 | tf_op jit(solution)/shard_map/ppermute | solution.py:73
  65.3 46.8 %collective-permute-start.24 = (bf16[1,10,10,10,128]{4,0,3,2,1:T(2,128)(2,1)S(1)}, bf16[1,10,10,10,128]{4,0,3,2,1:T(2,128)(2,1)S(1)}, u32[]{:S(2)}, u32[]{:S(2)}) collective-permute-start(bf16[1,10,10,10,128]{4,0,3,2,1:T(2,128)(2,1)S(1)} %slice.606), channel_id=1, source_target_pairs={{0,8},{8,16},{16,24},{24,0},{1,9},{9,17},{17,25},{25,1},{2,10},{10... | collective-permute-start | bytes 768008 | tf_op jit(solution)/shard_map/ppermute | solution.py:218
  71.3 23.7 %collective-permute-start.14 = (bf16[1,1,8,8,128]{4,3,2,1,0:T(8,128)(2,1)S(1)}, bf16[1,1,8,8,128]{4,3,2,1,0:T(8,128)(2,1)S(1)}, u32[]{:S(2)}, u32[]{:S(2)}) collective-permute-start(bf16[1,1,8,8,128]{4,3,2,1,0:T(8,128)(2,1)S(1)} %get-tuple-element.53), channel_id=1, source_target_pairs={{8,2},{9,3},{10,4},{11,5},{12,6},{13,7},{16,10},{17,11},{18,12},{1... | collective-permute-start | bytes 49160 | tf_op jit(solution)/shard_map/ppermute | solution.py:73
  75.6 19.9 %collective-permute-start.12 = (bf16[512,128]{1,0:T(8,128)(2,1)S(1)}, bf16[512,128]{1,0:T(8,128)(2,1)S(1)}, u32[]{:S(2)}, u32[]{:S(2)}) collective-permute-start(bf16[512,128]{1,0:T(8,128)(2,1)S(1)} %fusion.17), channel_id=1, source_target_pairs={{8,0},{16,8},{24,16},{9,1},{17,9},{25,17},{10,2},{18,10},{26,18},{... | collective-permute-start | bytes 393224 | tf_op jit(solution)/shard_map/ppermute | solution.py:246
  79.3 4.4 %collective-permute-start.13 = (bf16[1,1,1,8,128]{4,3,2,1,0:T(8,128)(2,1)S(1)}, bf16[1,1,1,8,128]{4,3,2,1,0:T(8,128)(2,1)S(1)}, u32[]{:S(2)}, u32[]{:S(2)}) collective-permute-start(bf16[1,1,1,8,128]{4,3,2,1,0:T(8,128)(2,1)S(1)} %constant_dynamic-slice_fusion.8), channel_id=1, source_target_pairs={{8,3},{9,2},{10,5},{11,4},{12,7},{13,6},{16,11},{17,10},{18,13},{1... | collective-permute-start | bytes 6152 | tf_op jit(solution)/shard_map/ppermute | solution.py:73
  80.6 14.5 %collective-permute-start.17 = (bf16[1,1,8,8,128]{4,3,2,1,0:T(8,128)(2,1)S(1)}, bf16[1,1,8,8,128]{4,3,2,1,0:T(8,128)(2,1)S(1)}, u32[]{:S(2)}, u32[]{:S(2)}) collective-permute-start(bf16[1,1,8,8,128]{4,3,2,1,0:T(8,128)(2,1)S(1)} %get-tuple-element.54), channel_id=1, source_target_pairs={{10,0},{11,1},{12,2},{13,3},{14,4},{15,5},{18,8},{19,9},{20,10},{2... | collective-permute-start | bytes 49160 | tf_op jit(solution)/shard_map/ppermute | solution.py:73
  83.7 2.6 %collective-permute-start.16 = (bf16[1,1,1,8,128]{4,3,2,1,0:T(8,128)(2,1)S(1)}, bf16[1,1,1,8,128]{4,3,2,1,0:T(8,128)(2,1)S(1)}, u32[]{:S(2)}, u32[]{:S(2)}) collective-permute-start(bf16[1,1,1,8,128]{4,3,2,1,0:T(8,128)(2,1)S(1)} %constant_dynamic-slice_fusion.6), channel_id=1, source_target_pairs={{10,1},{11,0},{12,3},{13,2},{14,5},{15,4},{18,9},{19,8},{20,11},{2... | collective-permute-start | bytes 6152 | tf_op jit(solution)/shard_map/ppermute | solution.py:73
  86.3 8.6 %collective-permute-start.15 = (bf16[1,8,1,8,128]{4,3,2,1,0:T(8,128)(2,1)S(1)}, bf16[1,8,1,8,128]{4,3,2,1,0:T(8,128)(2,1)S(1)}, u32[]{:S(2)}, u32[]{:S(2)}) collective-permute-start(bf16[1,8,1,8,128]{4,3,2,1,0:T(8,128)(2,1)S(1)} %constant_dynamic-slice_fusion.7), channel_id=1, source_target_pairs={{8,1},{9,0},{10,3},{11,2},{12,5},{13,4},{14,7},{15,6},{16,9},{17,8... | collective-permute-start | bytes 49160 | tf_op jit(solution)/shard_map/ppermute | solution.py:73
  99.5 27.7 %collective-permute-start.20 = (bf16[1,1,8,8,128]{4,3,2,1,0:T(8,128)(2,1)S(1)}, bf16[1,1,8,8,128]{4,3,2,1,0:T(8,128)(2,1)S(1)}, u32[]{:S(2)}, u32[]{:S(2)}) collective-permute-start(bf16[1,1,8,8,128]{4,3,2,1,0:T(8,128)(2,1)S(1)} %get-tuple-element.48), channel_id=1, source_target_pairs={{8,2},{9,3},{10,4},{11,5},{12,6},{13,7},{16,10},{17,11},{18,12},{1... | collective-permute-start | bytes 49160 | tf_op jit(solution)/shard_map/ppermute | solution.py:73
  103.4 24.7 %collective-permute-start.18 = (bf16[512,128]{1,0:T(8,128)(2,1)S(1)}, bf16[512,128]{1,0:T(8,128)(2,1)S(1)}, u32[]{:S(2)}, u32[]{:S(2)}) collective-permute-start(bf16[512,128]{1,0:T(8,128)(2,1)S(1)} %get-tuple-element.8), channel_id=1, source_target_pairs={{8,0},{16,8},{24,16},{9,1},{17,9},{25,17},{10,2},{18,10},{26,18},{... | collective-permute-start | bytes 393224 | tf_op jit(solution)/shard_map/ppermute | solution.py:246
  105.8 12.4 %collective-permute-start.19 = (bf16[1,1,1,8,128]{4,3,2,1,0:T(8,128)(2,1)S(1)}, bf16[1,1,1,8,128]{4,3,2,1,0:T(8,128)(2,1)S(1)}, u32[]{:S(2)}, u32[]{:S(2)}) collective-permute-start(bf16[1,1,1,8,128]{4,3,2,1,0:T(8,128)(2,1)S(1)} %constant_dynamic-slice_fusion.5), channel_id=1, source_target_pairs={{8,3},{9,2},{10,5},{11,4},{12,7},{13,6},{16,11},{17,10},{18,13},{1... | collective-permute-start | bytes 6152 | tf_op jit(solution)/shard_map/ppermute | solution.py:73
  107.4 20.4 %collective-permute-start.23 = (bf16[1,1,8,8,128]{4,3,2,1,0:T(8,128)(2,1)S(1)}, bf16[1,1,8,8,128]{4,3,2,1,0:T(8,128)(2,1)S(1)}, u32[]{:S(2)}, u32[]{:S(2)}) collective-permute-start(bf16[1,1,8,8,128]{4,3,2,1,0:T(8,128)(2,1)S(1)} %get-tuple-element.49), channel_id=1, source_target_pairs={{10,0},{11,1},{12,2},{13,3},{14,4},{15,5},{18,8},{19,9},{20,10},{2... | collective-permute-start | bytes 49160 | tf_op jit(solution)/shard_map/ppermute | solution.py:73
  116.1 12.3 %collective-permute-start.25 = (bf16[864,128]{1,0:T(8,128)(2,1)S(1)}, bf16[864,128]{1,0:T(8,128)(2,1)S(1)}, u32[]{:S(2)}, u32[]{:S(2)}) collective-permute-start(bf16[864,128]{1,0:T(8,128)(2,1)S(1)} %get-tuple-element.33), channel_id=1, source_target_pairs={{0,2},{2,4},{4,6},{6,0},{1,3},{3,5},{5,7},{7,1},{8,10},{10,12},{12... | collective-permute-start | bytes 663560 | tf_op jit(solution)/shard_map/ppermute | solution.py:151
  118.2 2.6 %collective-permute-start.22 = (bf16[1,1,1,8,128]{4,3,2,1,0:T(8,128)(2,1)S(1)}, bf16[1,1,1,8,128]{4,3,2,1,0:T(8,128)(2,1)S(1)}, u32[]{:S(2)}, u32[]{:S(2)}) collective-permute-start(bf16[1,1,1,8,128]{4,3,2,1,0:T(8,128)(2,1)S(1)} %constant_dynamic-slice_fusion.3), channel_id=1, source_target_pairs={{10,1},{11,0},{12,3},{13,2},{14,5},{15,4},{18,9},{19,8},{20,11},{2... | collective-permute-start | bytes 6152 | tf_op jit(solution)/shard_map/ppermute | solution.py:73
  120.8 6.3 %collective-permute-start.21 = (bf16[1,8,1,8,128]{4,3,2,1,0:T(8,128)(2,1)S(1)}, bf16[1,8,1,8,128]{4,3,2,1,0:T(8,128)(2,1)S(1)}, u32[]{:S(2)}, u32[]{:S(2)}) collective-permute-start(bf16[1,8,1,8,128]{4,3,2,1,0:T(8,128)(2,1)S(1)} %constant_dynamic-slice_fusion.4), channel_id=1, source_target_pairs={{8,1},{9,0},{10,3},{11,2},{12,5},{13,4},{14,7},{15,6},{16,9},{17,8... | collective-permute-start | bytes 49160 | tf_op jit(solution)/shard_map/ppermute | solution.py:73
  127.1 12.7 %collective-permute-start.26 = (bf16[864,128]{1,0:T(8,128)(2,1)S(1)}, bf16[864,128]{1,0:T(8,128)(2,1)S(1)}, u32[]{:S(2)}, u32[]{:S(2)}) collective-permute-start(bf16[864,128]{1,0:T(8,128)(2,1)S(1)} %get-tuple-element.35), channel_id=1, source_target_pairs={{0,4},{2,6},{4,0},{6,2},{1,5},{3,7},{5,1},{7,3},{8,12},{10,14},{12... | collective-permute-start | bytes 663560 | tf_op jit(solution)/shard_map/ppermute | solution.py:151
  127.2 12.7 %collective-permute-start.27 = (bf16[864,128]{1,0:T(8,128)(2,1)S(1)}, bf16[864,128]{1,0:T(8,128)(2,1)S(1)}, u32[]{:S(2)}, u32[]{:S(2)}) collective-permute-start(bf16[864,128]{1,0:T(8,128)(2,1)S(1)} %get-tuple-element.34), channel_id=1, source_target_pairs={{0,6},{2,0},{4,2},{6,4},{1,7},{3,1},{5,3},{7,5},{8,14},{10,8},{12,... | collective-permute-start | bytes 663560 | tf_op jit(solution)/shard_map/ppermute | solution.py:151
  140.0 3.4 %collective-permute-start.28 = (f32[864,128]{1,0:T(8,128)S(1)}, f32[864,128]{1,0:T(8,128)S(1)}, u32[]{:S(2)}, u32[]{:S(2)}) collective-permute-start(f32[864,128]{1,0:T(8,128)S(1)} %convert_add_fusion), channel_id=1, source_target_pairs={{0,1},{1,0},{2,3},{3,2},{4,5},{5,4},{6,7},{7,6},{8,9},{9,8},{10,11... | collective-permute-start | bytes 1327112 | tf_op jit(solution)/shard_map/ppermute | solution.py:160
  143.4 14.4 %collective-permute-start.29 = (f32[864,128]{1,0:T(8,128)S(1)}, f32[864,128]{1,0:T(8,128)S(1)}, u32[]{:S(2)}, u32[]{:S(2)}) collective-permute-start(f32[864,128]{1,0:T(8,128)S(1)} %add.205), channel_id=1, source_target_pairs={{0,24},{8,0},{16,8},{24,16},{1,25},{9,1},{17,9},{25,17},{2,26},{10... | collective-permute-start | bytes 1327112 | tf_op jit(solution)/shard_map/ppermute | solution.py:243

commit v9 on v7

--- a/solution.py
+++ b/solution.py
@@ -110,7 +110,7 @@
         filters,
         (1, 1, 1),
         "VALID",
-        dimension_numbers=("NDHWC", "DHWIO", "NDHWC"),
+        dimension_numbers=("NDHWC", "DHWOI", "NDHWC"),
         preferred_element_type=jnp.float32,
     )
 
@@ -135,10 +135,9 @@
             parts.append(given[step])
         else:
             parts.append(lax.ppermute(shard, axis, [(i, (i + step) % count) for i in range(count)]))
-    ordered = jnp.stack(parts)
-    index = (place - jnp.arange(count)) % count
-    slots = jnp.zeros((count,), jnp.int32).at[index].set(jnp.arange(count, dtype=jnp.int32))
-    return ordered[slots].reshape(count * shard.shape[0], *shard.shape[1:])
+    backwards = jnp.stack(parts[::-1] * 2)
+    ordered = lax.dynamic_slice_in_dim(backwards, count - 1 - place, count, axis=0)
+    return ordered.reshape(count * shard.shape[0], *shard.shape[1:])
 
 
 def scattered_sum(full, axis, share_rows):
@@ -200,7 +199,7 @@
             riding = kernel[0] if n_x >= 3 else None
             got = exchange(both, ("sx", "sy"), (n_x, n_y), 0, riding, carried)
             weights = gathered(kernel[0], "sx", carried)
-            flipped = weights.reshape(3, 3, 3, channels, channels)[::-1, ::-1, ::-1].transpose(0, 1, 2, 4, 3)
+            flipped = weights.reshape(3, 3, 3, channels, channels)[::-1, ::-1, ::-1]
         else:
             got = exchange(both, ("sx", "sy"), (n_x, n_y), 0)
         both_pad = assemble(both, got, table, split=True)

time: 132 us -> 135 us (1.023)
  starting transfers between devices: 50.8 us -> 55.9 us
  other arithmetic: 15.5 us -> 13.2 us
    ppermute x20, starting transfers between devices: 41.4 us -> 46.3 us  [send(): return lax.ppermute(piece, axes, route)]
    ppermute x20, waiting for transfers between devices: 14.5 us -> 18 us  [send(): return lax.ppermute(piece, axes, route)]
    ppermute x3, waiting for transfers between devices: 7.33 us -> 4.97 us  [scattered_sum(): lax.ppermute(piece, axis, [(i, (i + step) % count) for i in range(count)])]
  transfers between devices with their start and end apart: 28 -> 28, of which waited for: 8 -> 8; matrix products, arithmetic and copies ran while one was open for 12% -> 11% of each run, Pallas kernels for 0% -> 0%
where the time goes in v9:
time: 135 us; the launch traced here: 133 us
  starting transfers between devices  55.9 us (41%)
  waiting for transfers between devices  23.4 us (17%)
  between operations  19.9 us (15%)
  matrix products  15.6 us (12%)
  other arithmetic  13.2 us (10%)
  local copies, waits for them, and re-layouts  5.46 us (4%)
    ppermute x20, starting transfers between devices, send(): return lax.ppermute(piece, axes, route)  46.3 us
    ppermute x20, waiting for transfers between devices, send(): return lax.ppermute(piece, axes, route)  18 us
    conv_general_dilated x4, matrix products, conv_data(): lax.conv_general_dilated(padded, filters, (1, 1, 1), 'VALID', dimension_n...  11.8 us
    ppermute x3, starting transfers between devices, shards(): centre = lax.ppermute(result, 'pipe', down)  5.76 us
    ppermute x3, waiting for transfers between devices, scattered_sum(): lax.ppermute(piece, axis, [(i, (i + step) % count) for i in range(count)])  4.97 us
    transpose x1, matrix products, shards(): per_tap.transpose(1, 2, 3, 0, 4).reshape(taps * channels, channels)  3.76 us
  transfers between devices with their start and end apart: 28, of which 8 were waited for; matrix products, arithmetic and copies ran while one was open for 11% of the time, Pallas kernels for 0%

profile of v9, /device:TPU:21, one launch (start us, length us, event | category | flops | bytes accessed | tf_op | source)
XLA Modules:
  0.0 133.4 jit_solution(17147734067416072146)
XLA Ops:
  0.7 1.1 fusion.25
  1.8 1.0 convert_element_type.160
  3.5 1.0 broadcast_select_fusion.12
  4.6 0.8 multiply_convert_fusion.2
  5.4 0.7 collective-permute-start.4
  6.2 3.0 %collective-permute-start = (bf16[1,1,1,8,256]{4,3,2,1,0:T(8,128)(2,1)S(1)}, bf16[1,1,1,8,256]{4,3,2,1,0:T(8,128)(2,1)S(1)}, u32[]{:S(2)}, u32[]{:S(2)}) collective-permute-start(bf16[1,1,1,8,256]{4,3,2,1,0:T(8,128)(2,1)S(1)} %constant_dynamic-slice_fusion.14), channel_id=1, source_target_pairs={{0,3},{1,2},{2,5},{3,4},{4,7},{5,6},{8,11},{9,10},{10,13},{11,12},... | collective-permute-start | bytes 12296 | tf_op jit(solution)/shard_map/ppermute | solution.py:73
  9.3 3.4 %collective-permute-start.2 = (bf16[1,1,1,8,256]{4,3,2,1,0:T(8,128)(2,1)S(1)}, bf16[1,1,1,8,256]{4,3,2,1,0:T(8,128)(2,1)S(1)}, u32[]{:S(2)}, u32[]{:S(2)}) collective-permute-start(bf16[1,1,1,8,256]{4,3,2,1,0:T(8,128)(2,1)S(1)} %constant_dynamic-slice_fusion.13), channel_id=1, source_target_pairs={{2,1},{3,0},{4,3},{5,2},{6,5},{7,4},{10,9},{11,8},{12,11},{13,10},... | collective-permute-start | bytes 12296 | tf_op jit(solution)/shard_map/ppermute | solution.py:73
  12.9 1.5 %collective-permute-start.3 = (bf16[992,128]{1,0:T(8,128)(2,1)S(1)}, bf16[992,128]{1,0:T(8,128)(2,1)S(1)}, u32[]{:S(2)}, u32[]{:S(2)}) collective-permute-start(bf16[992,128]{1,0:T(8,128)(2,1)S(1)} %get-tuple-element.59), channel_id=1, source_target_pairs={{0,6},{1,7},{2,0},{3,1},{4,2},{5,3},{6,4},{7,5},{8,14},{9,15},{10,... | collective-permute-start | bytes 761864 | tf_op jit(solution)/shard_map/ppermute | solution.py:73
  14.4 0.7 fusion.75
  15.1 0.7 fusion.76
  15.8 0.2 fusion.58
  16.0 0.2 copy_dynamic-update-slice_fusion.1
  18.2 0.4 copy_dynamic-update-slice_fusion
  18.6 0.6 broadcast_select_fusion
  35.1 7.3 %collective-permute-done.1 = bf16[992,128]{1,0:T(8,128)(2,1)S(1)} collective-permute-done((bf16[992,128]{1,0:T(8,128)(2,1)S(1)}, bf16[992,128]{1,0:T(8,128)(2,1)S(1)}, u32[]{:S(2)}, u32[]{:S(2)}) %collective-permute-start.1) | collective-permute-done | bytes 253984 | tf_op jit(solution)/shard_map/ppermute | solution.py:73
  42.5 0.2 pad_maximum_fusion.10
  42.7 0.2 pad_maximum_fusion.9
  43.2 1.1 rev.3
  44.3 2.1 %pad_maximum_fusion = bf16[1,10,10,10,256]{4,0,3,2,1:T(2,128)(2,1)S(1)} fusion(bf16[1,1,10,10,256]{4,0,3,2,1:T(2,128)(2,1)S(1)} %pad_maximum_fusion.10, bf16[1,8,1,10,256]{4,0,3,2,1:T(2,128)(2,1)S(1)} %copy.47, bf16[1,8,8,1,256]{4,0,3,2,1:T(2,128)(2,1)S(1)} %get-tuple-element.50, bf16[1,8,8,8,256]{4,0,3,2,1:T(2,128)(2,1)S(1)} %broadcast_select_fusion, ...), kind=kLoop, calls=%fused_computation.2 | loop fusion | flops 1536000 | bytes 1024000 | tf_op jit(solution)/shard_map/concatenate | solution.py:56
  46.4 2.9 %fusion.1 = f32[1,8,8,8,128]{4,0,3,2,1:T(1,128)S(1)} fusion(bf16[3,3,3,128,128]{4,3,2,1,0:T(8,128)(2,1)S(1)} %copy-done.3, bf16[1,10,10,10,256]{4,0,3,2,1:T(2,128)(2,1)S(1)} %pad_maximum_fusion), kind=kOutput, calls=%fused_computation.7 | convolution fusion | flops 452984832 | bytes 1658880 | tf_op jit(solution)/shard_map/conv_general_dilated | solution.py:108
  49.4 0.3 fusion.47
  49.8 0.3 fusion.15
  50.2 1.9 %collective-permute-start.8 = (bf16[1,1,8,8,128]{4,3,2,1,0:T(8,128)(2,1)S(1)}, bf16[1,1,8,8,128]{4,3,2,1,0:T(8,128)(2,1)S(1)}, u32[]{:S(2)}, u32[]{:S(2)}) collective-permute-start(bf16[1,1,8,8,128]{4,3,2,1,0:T(8,128)(2,1)S(1)} %get-tuple-element.71), channel_id=1, source_target_pairs={{8,2},{9,3},{10,4},{11,5},{12,6},{13,7},{16,10},{17,11},{18,12},{1... | collective-permute-start | bytes 49160 | tf_op jit(solution)/shard_map/ppermute | solution.py:73
  52.1 4.0 %collective-permute-start.11 = (bf16[1,1,8,8,128]{4,3,2,1,0:T(8,128)(2,1)S(1)}, bf16[1,1,8,8,128]{4,3,2,1,0:T(8,128)(2,1)S(1)}, u32[]{:S(2)}, u32[]{:S(2)}) collective-permute-start(bf16[1,1,8,8,128]{4,3,2,1,0:T(8,128)(2,1)S(1)} %get-tuple-element.72), channel_id=1, source_target_pairs={{10,0},{11,1},{12,2},{13,3},{14,4},{15,5},{18,8},{19,9},{20,10},{2... | collective-permute-start | bytes 49160 | tf_op jit(solution)/shard_map/ppermute | solution.py:73
  56.2 2.0 %collective-permute-start.7 = (bf16[1,1,1,8,128]{4,3,2,1,0:T(8,128)(2,1)S(1)}, bf16[1,1,1,8,128]{4,3,2,1,0:T(8,128)(2,1)S(1)}, u32[]{:S(2)}, u32[]{:S(2)}) collective-permute-start(bf16[1,1,1,8,128]{4,3,2,1,0:T(8,128)(2,1)S(1)} %constant_dynamic-slice_fusion.11), channel_id=1, source_target_pairs={{8,3},{9,2},{10,5},{11,4},{12,7},{13,6},{16,11},{17,10},{18,13},{1... | collective-permute-start | bytes 6152 | tf_op jit(solution)/shard_map/ppermute | solution.py:73
  58.2 1.9 %collective-permute-start.9 = (bf16[1,8,1,8,128]{4,3,2,1,0:T(8,128)(2,1)S(1)}, bf16[1,8,1,8,128]{4,3,2,1,0:T(8,128)(2,1)S(1)}, u32[]{:S(2)}, u32[]{:S(2)}) collective-permute-start(bf16[1,8,1,8,128]{4,3,2,1,0:T(8,128)(2,1)S(1)} %constant_dynamic-slice_fusion.10), channel_id=1, source_target_pairs={{8,1},{9,0},{10,3},{11,2},{12,5},{13,4},{14,7},{15,6},{16,9},{17,8... | collective-permute-start | bytes 49160 | tf_op jit(solution)/shard_map/ppermute | solution.py:73
  60.1 0.3 fusion.8
  60.4 1.9 %collective-permute-start.6 = (bf16[512,128]{1,0:T(8,128)(2,1)S(1)}, bf16[512,128]{1,0:T(8,128)(2,1)S(1)}, u32[]{:S(2)}, u32[]{:S(2)}) collective-permute-start(bf16[512,128]{1,0:T(8,128)(2,1)S(1)} %fusion.8), channel_id=1, source_target_pairs={{8,0},{16,8},{24,16},{9,1},{17,9},{25,17},{10,2},{18,10},{26,18},{... | collective-permute-start | bytes 393224 | tf_op jit(solution)/shard_map/ppermute | solution.py:228
  62.4 0.5 collective-permute-done.7
  62.9 3.1 %collective-permute-start.10 = (bf16[1,1,1,8,128]{4,3,2,1,0:T(8,128)(2,1)S(1)}, bf16[1,1,1,8,128]{4,3,2,1,0:T(8,128)(2,1)S(1)}, u32[]{:S(2)}, u32[]{:S(2)}) collective-permute-start(bf16[1,1,1,8,128]{4,3,2,1,0:T(8,128)(2,1)S(1)} %constant_dynamic-slice_fusion.9), channel_id=1, source_target_pairs={{10,1},{11,0},{12,3},{13,2},{14,5},{15,4},{18,9},{19,8},{20,11},{2... | collective-permute-start | bytes 6152 | tf_op jit(solution)/shard_map/ppermute | solution.py:73
  66.0 2.6 %collective-permute-done.10 = bf16[1,1,1,8,128]{4,3,2,1,0:T(8,128)(2,1)S(1)} collective-permute-done((bf16[1,1,1,8,128]{4,3,2,1,0:T(8,128)(2,1)S(1)}, bf16[1,1,1,8,128]{4,3,2,1,0:T(8,128)(2,1)S(1)}, u32[]{:S(2)}, u32[]{:S(2)}) %collective-permute-start.10) | collective-permute-done | bytes 2080 | tf_op jit(solution)/shard_map/ppermute | solution.py:73
  69.3 0.2 copy.52
  69.6 3.0 %fusion.5 = f32[1,8,8,8,128]{4,0,3,2,1:T(1,128)S(1)} fusion(bf16[3,3,3,128,128]{4,3,2,1,0:T(8,128)(2,1)S(1)} %bitcast.216, bf16[1,1,10,10,128]{4,0,3,2,1:T(2,128)(2,1)S(1)} %copy.56, bf16[1,8,1,10,128]{4,0,3,2,1:T(2,128)(2,1)S(1)} %copy.54, bf16[1,8,8,1,128]{4,0,3,2,1:T(2,128)(2,1)S(1)} %slice_bitcast_fusion.6, bf16[1,8,8,8,128]{4,0,3,2,1:T(2,128)(2,1)S(1)} %copy.52, ...), kind=kOutput, calls=%fused_computation.11 | convolution fusion | flops 454776832 | bytes 1402880 | tf_op jit(solution)/shard_map/conv_general_dilated | solution.py:108
  72.6 0.3 fusion.48
  72.9 0.3 fusion.18
  73.3 1.9 %collective-permute-start.14 = (bf16[1,1,8,8,128]{4,3,2,1,0:T(8,128)(2,1)S(1)}, bf16[1,1,8,8,128]{4,3,2,1,0:T(8,128)(2,1)S(1)}, u32[]{:S(2)}, u32[]{:S(2)}) collective-permute-start(bf16[1,1,8,8,128]{4,3,2,1,0:T(8,128)(2,1)S(1)} %get-tuple-element.66), channel_id=1, source_target_pairs={{8,2},{9,3},{10,4},{11,5},{12,6},{13,7},{16,10},{17,11},{18,12},{1... | collective-permute-start | bytes 49160 | tf_op jit(solution)/shard_map/ppermute | solution.py:73
  75.2 1.9 %collective-permute-start.12 = (bf16[512,128]{1,0:T(8,128)(2,1)S(1)}, bf16[512,128]{1,0:T(8,128)(2,1)S(1)}, u32[]{:S(2)}, u32[]{:S(2)}) collective-permute-start(bf16[512,128]{1,0:T(8,128)(2,1)S(1)} %fusion.18), channel_id=1, source_target_pairs={{8,0},{16,8},{24,16},{9,1},{17,9},{25,17},{10,2},{18,10},{26,18},{... | collective-permute-start | bytes 393224 | tf_op jit(solution)/shard_map/ppermute | solution.py:228
  77.2 1.9 %collective-permute-start.13 = (bf16[1,1,1,8,128]{4,3,2,1,0:T(8,128)(2,1)S(1)}, bf16[1,1,1,8,128]{4,3,2,1,0:T(8,128)(2,1)S(1)}, u32[]{:S(2)}, u32[]{:S(2)}) collective-permute-start(bf16[1,1,1,8,128]{4,3,2,1,0:T(8,128)(2,1)S(1)} %constant_dynamic-slice_fusion.8), channel_id=1, source_target_pairs={{8,3},{9,2},{10,5},{11,4},{12,7},{13,6},{16,11},{17,10},{18,13},{1... | collective-permute-start | bytes 6152 | tf_op jit(solution)/shard_map/ppermute | solution.py:73
  79.1 4.4 %collective-permute-start.17 = (bf16[1,1,8,8,128]{4,3,2,1,0:T(8,128)(2,1)S(1)}, bf16[1,1,8,8,128]{4,3,2,1,0:T(8,128)(2,1)S(1)}, u32[]{:S(2)}, u32[]{:S(2)}) collective-permute-start(bf16[1,1,8,8,128]{4,3,2,1,0:T(8,128)(2,1)S(1)} %get-tuple-element.67), channel_id=1, source_target_pairs={{10,0},{11,1},{12,2},{13,3},{14,4},{15,5},{18,8},{19,9},{20,10},{2... | collective-permute-start | bytes 49160 | tf_op jit(solution)/shard_map/ppermute | solution.py:73
  83.6 1.9 %collective-permute-start.15 = (bf16[1,8,1,8,128]{4,3,2,1,0:T(8,128)(2,1)S(1)}, bf16[1,8,1,8,128]{4,3,2,1,0:T(8,128)(2,1)S(1)}, u32[]{:S(2)}, u32[]{:S(2)}) collective-permute-start(bf16[1,8,1,8,128]{4,3,2,1,0:T(8,128)(2,1)S(1)} %constant_dynamic-slice_fusion.7), channel_id=1, source_target_pairs={{8,1},{9,0},{10,3},{11,2},{12,5},{13,4},{14,7},{15,6},{16,9},{17,8... | collective-permute-start | bytes 49160 | tf_op jit(solution)/shard_map/ppermute | solution.py:73
  85.5 2.8 %collective-permute-start.16 = (bf16[1,1,1,8,128]{4,3,2,1,0:T(8,128)(2,1)S(1)}, bf16[1,1,1,8,128]{4,3,2,1,0:T(8,128)(2,1)S(1)}, u32[]{:S(2)}, u32[]{:S(2)}) collective-permute-start(bf16[1,1,1,8,128]{4,3,2,1,0:T(8,128)(2,1)S(1)} %constant_dynamic-slice_fusion.6), channel_id=1, source_target_pairs={{10,1},{11,0},{12,3},{13,2},{14,5},{15,4},{18,9},{19,8},{20,11},{2... | collective-permute-start | bytes 6152 | tf_op jit(solution)/shard_map/ppermute | solution.py:73
  88.3 3.0 %collective-permute-done.16 = bf16[1,1,1,8,128]{4,3,2,1,0:T(8,128)(2,1)S(1)} collective-permute-done((bf16[1,1,1,8,128]{4,3,2,1,0:T(8,128)(2,1)S(1)}, bf16[1,1,1,8,128]{4,3,2,1,0:T(8,128)(2,1)S(1)}, u32[]{:S(2)}, u32[]{:S(2)}) %collective-permute-start.16) | collective-permute-done | bytes 2080 | tf_op jit(solution)/shard_map/ppermute | solution.py:73
  91.9 0.2 copy.59
  92.2 3.0 %fusion.4 = f32[1,8,8,8,128]{4,0,3,2,1:T(1,128)S(1)} fusion(bf16[3,3,3,128,128]{4,3,2,1,0:T(8,128)(2,1)S(1)} %bitcast.217, bf16[1,1,10,10,128]{4,0,3,2,1:T(2,128)(2,1)S(1)} %copy.63, bf16[1,8,1,10,128]{4,0,3,2,1:T(2,128)(2,1)S(1)} %copy.61, bf16[1,8,8,1,128]{4,0,3,2,1:T(2,128)(2,1)S(1)} %slice_bitcast_fusion.4, bf16[1,8,8,8,128]{4,0,3,2,1:T(2,128)(2,1)S(1)} %copy.59, ...), kind=kOutput, calls=%fused_computation.10 | convolution fusion | flops 454776832 | bytes 1402880 | tf_op jit(solution)/shard_map/conv_general_dilated | solution.py:108
  95.2 0.3 fusion.49
  95.6 0.3 fusion.21
  95.9 1.9 %collective-permute-start.18 = (bf16[512,128]{1,0:T(8,128)(2,1)S(1)}, bf16[512,128]{1,0:T(8,128)(2,1)S(1)}, u32[]{:S(2)}, u32[]{:S(2)}) collective-permute-start(bf16[512,128]{1,0:T(8,128)(2,1)S(1)} %fusion.21), channel_id=1, source_target_pairs={{8,0},{16,8},{24,16},{9,1},{17,9},{25,17},{10,2},{18,10},{26,18},{... | collective-permute-start | bytes 393224 | tf_op jit(solution)/shard_map/ppermute | solution.py:228
  97.8 3.7 %collective-permute-start.22 = (bf16[1,1,1,8,128]{4,3,2,1,0:T(8,128)(2,1)S(1)}, bf16[1,1,1,8,128]{4,3,2,1,0:T(8,128)(2,1)S(1)}, u32[]{:S(2)}, u32[]{:S(2)}) collective-permute-start(bf16[1,1,1,8,128]{4,3,2,1,0:T(8,128)(2,1)S(1)} %constant_dynamic-slice_fusion.3), channel_id=1, source_target_pairs={{10,1},{11,0},{12,3},{13,2},{14,5},{15,4},{18,9},{19,8},{20,11},{2... | collective-permute-start | bytes 6152 | tf_op jit(solution)/shard_map/ppermute | solution.py:73
  101.5 1.9 %collective-permute-start.20 = (bf16[1,1,8,8,128]{4,3,2,1,0:T(8,128)(2,1)S(1)}, bf16[1,1,8,8,128]{4,3,2,1,0:T(8,128)(2,1)S(1)}, u32[]{:S(2)}, u32[]{:S(2)}) collective-permute-start(bf16[1,1,8,8,128]{4,3,2,1,0:T(8,128)(2,1)S(1)} %get-tuple-element.65), channel_id=1, source_target_pairs={{8,2},{9,3},{10,4},{11,5},{12,6},{13,7},{16,10},{17,11},{18,12},{1... | collective-permute-start | bytes 49160 | tf_op jit(solution)/shard_map/ppermute | solution.py:73
  103.5 1.9 %collective-permute-start.23 = (bf16[1,1,8,8,128]{4,3,2,1,0:T(8,128)(2,1)S(1)}, bf16[1,1,8,8,128]{4,3,2,1,0:T(8,128)(2,1)S(1)}, u32[]{:S(2)}, u32[]{:S(2)}) collective-permute-start(bf16[1,1,8,8,128]{4,3,2,1,0:T(8,128)(2,1)S(1)} %get-tuple-element.64), channel_id=1, source_target_pairs={{10,0},{11,1},{12,2},{13,3},{14,4},{15,5},{18,8},{19,9},{20,10},{2... | collective-permute-start | bytes 49160 | tf_op jit(solution)/shard_map/ppermute | solution.py:73
  105.4 1.9 %collective-permute-start.21 = (bf16[1,8,1,8,128]{4,3,2,1,0:T(8,128)(2,1)S(1)}, bf16[1,8,1,8,128]{4,3,2,1,0:T(8,128)(2,1)S(1)}, u32[]{:S(2)}, u32[]{:S(2)}) collective-permute-start(bf16[1,8,1,8,128]{4,3,2,1,0:T(8,128)(2,1)S(1)} %constant_dynamic-slice_fusion.4), channel_id=1, source_target_pairs={{8,1},{9,0},{10,3},{11,2},{12,5},{13,4},{14,7},{15,6},{16,9},{17,8... | collective-permute-start | bytes 49160 | tf_op jit(solution)/shard_map/ppermute | solution.py:73
  107.3 2.1 %collective-permute-start.19 = (bf16[1,1,1,8,128]{4,3,2,1,0:T(8,128)(2,1)S(1)}, bf16[1,1,1,8,128]{4,3,2,1,0:T(8,128)(2,1)S(1)}, u32[]{:S(2)}, u32[]{:S(2)}) collective-permute-start(bf16[1,1,1,8,128]{4,3,2,1,0:T(8,128)(2,1)S(1)} %constant_dynamic-slice_fusion.5), channel_id=1, source_target_pairs={{8,3},{9,2},{10,5},{11,4},{12,7},{13,6},{16,11},{17,10},{18,13},{1... | collective-permute-start | bytes 6152 | tf_op jit(solution)/shard_map/ppermute | solution.py:73
  109.5 4.5 %collective-permute-done.19 = bf16[1,1,1,8,128]{4,3,2,1,0:T(8,128)(2,1)S(1)} collective-permute-done((bf16[1,1,1,8,128]{4,3,2,1,0:T(8,128)(2,1)S(1)}, bf16[1,1,1,8,128]{4,3,2,1,0:T(8,128)(2,1)S(1)}, u32[]{:S(2)}, u32[]{:S(2)}) %collective-permute-start.19) | collective-permute-done | bytes 2080 | tf_op jit(solution)/shard_map/ppermute | solution.py:73
  114.2 3.8 %multiply_convert_fusion = bf16[3,3,3,128,128]{4,3,2,1,0:T(8,128)(2,1)S(1)} fusion(bf16[1,10,10,10,256]{4,0,3,2,1:T(2,128)(2,1)S(1)} %pad_maximum_fusion, bf16[1,8,8,8,128]{4,3,2,1,0:T(8,128)(2,1)S(1)} %bitcast.250), kind=kOutput, calls=%fused_computation | convolution fusion | flops 453869568 | bytes 1527808 | tf_op jit(solution)/shard_map/transpose | solution.py:216
  118.4 2.3 %collective-permute-start.26 = (bf16[864,128]{1,0:T(8,128)(2,1)S(1)}, bf16[864,128]{1,0:T(8,128)(2,1)S(1)}, u32[]{:S(2)}, u32[]{:S(2)}) collective-permute-start(bf16[864,128]{1,0:T(8,128)(2,1)S(1)} %get-tuple-element.47), channel_id=1, source_target_pairs={{0,6},{2,0},{4,2},{6,4},{1,7},{3,1},{5,3},{7,5},{8,14},{10,8},{12,... | collective-permute-start | bytes 663560 | tf_op jit(solution)/shard_map/ppermute | solution.py:150
  120.9 0.2 copy.67
  121.4 3.0 %fusion.3 = f32[1,8,8,8,128]{4,0,3,2,1:T(1,128)S(1)} fusion(bf16[3,3,3,128,128]{4,3,2,1,0:T(8,128)(2,1)S(1)} %bitcast.218, bf16[1,1,10,10,128]{4,0,3,2,1:T(2,128)(2,1)S(1)} %copy.71, bf16[1,8,1,10,128]{4,0,3,2,1:T(2,128)(2,1)S(1)} %copy.69, bf16[1,8,8,1,128]{4,0,3,2,1:T(2,128)(2,1)S(1)} %slice_bitcast_fusion.2, bf16[1,8,8,8,128]{4,0,3,2,1:T(2,128)(2,1)S(1)} %copy.67, ...), kind=kOutput, calls=%fused_computation.9 | convolution fusion | flops 454776832 | bytes 1402880 | tf_op jit(solution)/shard_map/conv_general_dilated | solution.py:108
  124.4 0.3 fusion.50
  124.8 1.1 collective-permute-done.24
  125.8 3.9 %collective-permute-done.25 = bf16[864,128]{1,0:T(8,128)(2,1)S(1)} collective-permute-done((bf16[864,128]{1,0:T(8,128)(2,1)S(1)}, bf16[864,128]{1,0:T(8,128)(2,1)S(1)}, u32[]{:S(2)}, u32[]{:S(2)}) %collective-permute-start.25) | collective-permute-done | bytes 221216 | tf_op jit(solution)/shard_map/ppermute | solution.py:150
  129.8 1.3 collective-permute-start.27
  131.1 1.0 fusion.57
  132.2 0.4 collective-permute-done.27
  132.5 0.8 add_bitcast_fusion
  (209 shorter events, 3.9 us)
Async XLA Ops:
  0.6 15.2 %copy-start.9 = (f32[1,128]{1,0:T(1,128)S(1)}, f32[1,128]{1,0:T(1,128)}, u32[]{:S(2)}) copy-start(f32[1,128]{1,0:T(1,128)} %param.10) | copy-start | bytes 1540
  0.6 12.1 %copy-start.2 = (bf16[1,864,128]{2,1,0:T(8,128)(2,1)S(1)}, bf16[1,864,128]{2,1,0:T(8,128)(2,1)}, u32[]{:S(2)}) copy-start(bf16[1,864,128]{2,1,0:T(8,128)(2,1)} %param.11) | copy-start | bytes 663556
  0.7 13.8 %copy-start.8 = (s32[1,1,1,1,27]{4,3,2,1,0:T(1,128)S(1)}, s32[1,1,1,1,27]{4,3,2,1,0:T(1,128)}, u32[]{:S(2)}) copy-start(s32[1,1,1,1,27]{4,3,2,1,0:T(1,128)} %param.8) | copy-start | bytes 328
  1.8 14.4 %copy-start.1 = (bf16[1,1,1,512,128]{4,3,2,1,0:T(8,128)(2,1)S(1)}, bf16[1,1,1,512,128]{4,3,2,1,0:T(8,128)(2,1)}, u32[]{:S(2)}) copy-start(bf16[1,1,1,512,128]{4,3,2,1,0:T(8,128)(2,1)} %param.7) | copy-start | bytes 393220
  5.4 29.2 %collective-permute-start.4 = (bf16[1,8,1,8,256]{4,3,2,1,0:T(8,128)(2,1)S(1)}, bf16[1,8,1,8,256]{4,3,2,1,0:T(8,128)(2,1)S(1)}, u32[]{:S(2)}, u32[]{:S(2)}) collective-permute-start(bf16[1,8,1,8,256]{4,3,2,1,0:T(8,128)(2,1)S(1)} %fusion.61), channel_id=1, source_target_pairs={{0,1},{1,0},{2,3},{3,2},{4,5},{5,4},{6,7},{7,6},{8,9},{9,8},{10,11... | collective-permute-start | bytes 98312 | tf_op jit(solution)/shard_map/ppermute | solution.py:73
  6.2 28.1 %collective-permute-start = (bf16[1,1,1,8,256]{4,3,2,1,0:T(8,128)(2,1)S(1)}, bf16[1,1,1,8,256]{4,3,2,1,0:T(8,128)(2,1)S(1)}, u32[]{:S(2)}, u32[]{:S(2)}) collective-permute-start(bf16[1,1,1,8,256]{4,3,2,1,0:T(8,128)(2,1)S(1)} %constant_dynamic-slice_fusion.14), channel_id=1, source_target_pairs={{0,3},{1,2},{2,5},{3,4},{4,7},{5,6},{8,11},{9,10},{10,13},{11,12},... | collective-permute-start | bytes 12296 | tf_op jit(solution)/shard_map/ppermute | solution.py:73
  9.3 25.1 %collective-permute-start.2 = (bf16[1,1,1,8,256]{4,3,2,1,0:T(8,128)(2,1)S(1)}, bf16[1,1,1,8,256]{4,3,2,1,0:T(8,128)(2,1)S(1)}, u32[]{:S(2)}, u32[]{:S(2)}) collective-permute-start(bf16[1,1,1,8,256]{4,3,2,1,0:T(8,128)(2,1)S(1)} %constant_dynamic-slice_fusion.13), channel_id=1, source_target_pairs={{2,1},{3,0},{4,3},{5,2},{6,5},{7,4},{10,9},{11,8},{12,11},{13,10},... | collective-permute-start | bytes 12296 | tf_op jit(solution)/shard_map/ppermute | solution.py:73
  12.7 30.2 %collective-permute-start.5 = (bf16[864,128]{1,0:T(8,128)(2,1)S(1)}, bf16[864,128]{1,0:T(8,128)(2,1)S(1)}, u32[]{:S(2)}, u32[]{:S(2)}) collective-permute-start(bf16[864,128]{1,0:T(8,128)(2,1)S(1)} %bitcast.225), channel_id=1, source_target_pairs={{0,4},{2,6},{4,0},{6,2},{1,5},{3,7},{5,1},{7,3},{8,12},{10,14},{12... | collective-permute-start | bytes 663560 | tf_op jit(solution)/shard_map/ppermute | solution.py:137
  12.9 22.0 %collective-permute-start.3 = (bf16[992,128]{1,0:T(8,128)(2,1)S(1)}, bf16[992,128]{1,0:T(8,128)(2,1)S(1)}, u32[]{:S(2)}, u32[]{:S(2)}) collective-permute-start(bf16[992,128]{1,0:T(8,128)(2,1)S(1)} %get-tuple-element.59), channel_id=1, source_target_pairs={{0,6},{1,7},{2,0},{3,1},{4,2},{5,3},{6,4},{7,5},{8,14},{9,15},{10,... | collective-permute-start | bytes 761864 | tf_op jit(solution)/shard_map/ppermute | solution.py:73
  34.3 8.1 %collective-permute-start.1 = (bf16[992,128]{1,0:T(8,128)(2,1)S(1)}, bf16[992,128]{1,0:T(8,128)(2,1)S(1)}, u32[]{:S(2)}, u32[]{:S(2)}) collective-permute-start(bf16[992,128]{1,0:T(8,128)(2,1)S(1)} %get-tuple-element.60), channel_id=1, source_target_pairs={{0,2},{1,3},{2,4},{3,5},{4,6},{5,7},{6,0},{7,1},{8,10},{9,11},{10,... | collective-permute-start | bytes 761864 | tf_op jit(solution)/shard_map/ppermute | solution.py:73
  44.3 2.1 %copy-start.3 = (bf16[3,3,3,128,128]{4,3,2,1,0:T(8,128)(2,1)S(1)}, bf16[3,3,3,128,128]{4,3,2,1,0:T(8,128)(2,1)}, u32[]{:S(2)}) copy-start(bf16[3,3,3,128,128]{4,3,2,1,0:T(8,128)(2,1)} %rev.3) | copy-start | bytes 2654212
  46.4 3.0 %copy-start = (bf16[1,1,1,1,512,128]{5,4,3,2,1,0:T(8,128)(2,1)S(1)}, bf16[1,1,1,1,512,128]{5,4,3,2,1,0:T(8,128)(2,1)}, u32[]{:S(2)}) copy-start(bf16[1,1,1,1,512,128]{5,4,3,2,1,0:T(8,128)(2,1)} %param.6) | copy-start | bytes 393220
  50.2 18.7 %collective-permute-start.8 = (bf16[1,1,8,8,128]{4,3,2,1,0:T(8,128)(2,1)S(1)}, bf16[1,1,8,8,128]{4,3,2,1,0:T(8,128)(2,1)S(1)}, u32[]{:S(2)}, u32[]{:S(2)}) collective-permute-start(bf16[1,1,8,8,128]{4,3,2,1,0:T(8,128)(2,1)S(1)} %get-tuple-element.71), channel_id=1, source_target_pairs={{8,2},{9,3},{10,4},{11,5},{12,6},{13,7},{16,10},{17,11},{18,12},{1... | collective-permute-start | bytes 49160 | tf_op jit(solution)/shard_map/ppermute | solution.py:73
  52.1 16.9 %collective-permute-start.11 = (bf16[1,1,8,8,128]{4,3,2,1,0:T(8,128)(2,1)S(1)}, bf16[1,1,8,8,128]{4,3,2,1,0:T(8,128)(2,1)S(1)}, u32[]{:S(2)}, u32[]{:S(2)}) collective-permute-start(bf16[1,1,8,8,128]{4,3,2,1,0:T(8,128)(2,1)S(1)} %get-tuple-element.72), channel_id=1, source_target_pairs={{10,0},{11,1},{12,2},{13,3},{14,4},{15,5},{18,8},{19,9},{20,10},{2... | collective-permute-start | bytes 49160 | tf_op jit(solution)/shard_map/ppermute | solution.py:73
  56.2 6.7 %collective-permute-start.7 = (bf16[1,1,1,8,128]{4,3,2,1,0:T(8,128)(2,1)S(1)}, bf16[1,1,1,8,128]{4,3,2,1,0:T(8,128)(2,1)S(1)}, u32[]{:S(2)}, u32[]{:S(2)}) collective-permute-start(bf16[1,1,1,8,128]{4,3,2,1,0:T(8,128)(2,1)S(1)} %constant_dynamic-slice_fusion.11), channel_id=1, source_target_pairs={{8,3},{9,2},{10,5},{11,4},{12,7},{13,6},{16,11},{17,10},{18,13},{1... | collective-permute-start | bytes 6152 | tf_op jit(solution)/shard_map/ppermute | solution.py:73
  58.2 10.6 %collective-permute-start.9 = (bf16[1,8,1,8,128]{4,3,2,1,0:T(8,128)(2,1)S(1)}, bf16[1,8,1,8,128]{4,3,2,1,0:T(8,128)(2,1)S(1)}, u32[]{:S(2)}, u32[]{:S(2)}) collective-permute-start(bf16[1,8,1,8,128]{4,3,2,1,0:T(8,128)(2,1)S(1)} %constant_dynamic-slice_fusion.10), channel_id=1, source_target_pairs={{8,1},{9,0},{10,3},{11,2},{12,5},{13,4},{14,7},{15,6},{16,9},{17,8... | collective-permute-start | bytes 49160 | tf_op jit(solution)/shard_map/ppermute | solution.py:73
  60.4 12.1 %copy-start.6 = (bf16[512,128]{1,0:T(8,128)(2,1)}, bf16[512,128]{1,0:T(8,128)(2,1)S(1)}, u32[]{:S(2)}) copy-start(bf16[512,128]{1,0:T(8,128)(2,1)S(1)} %fusion.8) | copy-start | bytes 393220
  60.4 8.8 %collective-permute-start.6 = (bf16[512,128]{1,0:T(8,128)(2,1)S(1)}, bf16[512,128]{1,0:T(8,128)(2,1)S(1)}, u32[]{:S(2)}, u32[]{:S(2)}) collective-permute-start(bf16[512,128]{1,0:T(8,128)(2,1)S(1)} %fusion.8), channel_id=1, source_target_pairs={{8,0},{16,8},{24,16},{9,1},{17,9},{25,17},{10,2},{18,10},{26,18},{... | collective-permute-start | bytes 393224 | tf_op jit(solution)/shard_map/ppermute | solution.py:228
  62.9 5.8 %collective-permute-start.10 = (bf16[1,1,1,8,128]{4,3,2,1,0:T(8,128)(2,1)S(1)}, bf16[1,1,1,8,128]{4,3,2,1,0:T(8,128)(2,1)S(1)}, u32[]{:S(2)}, u32[]{:S(2)}) collective-permute-start(bf16[1,1,1,8,128]{4,3,2,1,0:T(8,128)(2,1)S(1)} %constant_dynamic-slice_fusion.9), channel_id=1, source_target_pairs={{10,1},{11,0},{12,3},{13,2},{14,5},{15,4},{18,9},{19,8},{20,11},{2... | collective-permute-start | bytes 6152 | tf_op jit(solution)/shard_map/ppermute | solution.py:73
  73.2 22.0 %copy-start.4 = (bf16[512,128]{1,0:T(8,128)(2,1)}, bf16[512,128]{1,0:T(8,128)(2,1)S(1)}, u32[]{:S(2)}) copy-start(bf16[512,128]{1,0:T(8,128)(2,1)S(1)} %fusion.18) | copy-start | bytes 393220
  73.3 18.2 %collective-permute-start.14 = (bf16[1,1,8,8,128]{4,3,2,1,0:T(8,128)(2,1)S(1)}, bf16[1,1,8,8,128]{4,3,2,1,0:T(8,128)(2,1)S(1)}, u32[]{:S(2)}, u32[]{:S(2)}) collective-permute-start(bf16[1,1,8,8,128]{4,3,2,1,0:T(8,128)(2,1)S(1)} %get-tuple-element.66), channel_id=1, source_target_pairs={{8,2},{9,3},{10,4},{11,5},{12,6},{13,7},{16,10},{17,11},{18,12},{1... | collective-permute-start | bytes 49160 | tf_op jit(solution)/shard_map/ppermute | solution.py:73
  75.2 16.7 %collective-permute-start.12 = (bf16[512,128]{1,0:T(8,128)(2,1)S(1)}, bf16[512,128]{1,0:T(8,128)(2,1)S(1)}, u32[]{:S(2)}, u32[]{:S(2)}) collective-permute-start(bf16[512,128]{1,0:T(8,128)(2,1)S(1)} %fusion.18), channel_id=1, source_target_pairs={{8,0},{16,8},{24,16},{9,1},{17,9},{25,17},{10,2},{18,10},{26,18},{... | collective-permute-start | bytes 393224 | tf_op jit(solution)/shard_map/ppermute | solution.py:228
  77.2 8.3 %collective-permute-start.13 = (bf16[1,1,1,8,128]{4,3,2,1,0:T(8,128)(2,1)S(1)}, bf16[1,1,1,8,128]{4,3,2,1,0:T(8,128)(2,1)S(1)}, u32[]{:S(2)}, u32[]{:S(2)}) collective-permute-start(bf16[1,1,1,8,128]{4,3,2,1,0:T(8,128)(2,1)S(1)} %constant_dynamic-slice_fusion.8), channel_id=1, source_target_pairs={{8,3},{9,2},{10,5},{11,4},{12,7},{13,6},{16,11},{17,10},{18,13},{1... | collective-permute-start | bytes 6152 | tf_op jit(solution)/shard_map/ppermute | solution.py:73
  79.1 12.5 %collective-permute-start.17 = (bf16[1,1,8,8,128]{4,3,2,1,0:T(8,128)(2,1)S(1)}, bf16[1,1,8,8,128]{4,3,2,1,0:T(8,128)(2,1)S(1)}, u32[]{:S(2)}, u32[]{:S(2)}) collective-permute-start(bf16[1,1,8,8,128]{4,3,2,1,0:T(8,128)(2,1)S(1)} %get-tuple-element.67), channel_id=1, source_target_pairs={{10,0},{11,1},{12,2},{13,3},{14,4},{15,5},{18,8},{19,9},{20,10},{2... | collective-permute-start | bytes 49160 | tf_op jit(solution)/shard_map/ppermute | solution.py:73
  83.6 7.8 %collective-permute-start.15 = (bf16[1,8,1,8,128]{4,3,2,1,0:T(8,128)(2,1)S(1)}, bf16[1,8,1,8,128]{4,3,2,1,0:T(8,128)(2,1)S(1)}, u32[]{:S(2)}, u32[]{:S(2)}) collective-permute-start(bf16[1,8,1,8,128]{4,3,2,1,0:T(8,128)(2,1)S(1)} %constant_dynamic-slice_fusion.7), channel_id=1, source_target_pairs={{8,1},{9,0},{10,3},{11,2},{12,5},{13,4},{14,7},{15,6},{16,9},{17,8... | collective-permute-start | bytes 49160 | tf_op jit(solution)/shard_map/ppermute | solution.py:73
  85.5 5.8 %collective-permute-start.16 = (bf16[1,1,1,8,128]{4,3,2,1,0:T(8,128)(2,1)S(1)}, bf16[1,1,1,8,128]{4,3,2,1,0:T(8,128)(2,1)S(1)}, u32[]{:S(2)}, u32[]{:S(2)}) collective-permute-start(bf16[1,1,1,8,128]{4,3,2,1,0:T(8,128)(2,1)S(1)} %constant_dynamic-slice_fusion.6), channel_id=1, source_target_pairs={{10,1},{11,0},{12,3},{13,2},{14,5},{15,4},{18,9},{19,8},{20,11},{2... | collective-permute-start | bytes 6152 | tf_op jit(solution)/shard_map/ppermute | solution.py:73
  95.9 18.2 %collective-permute-start.18 = (bf16[512,128]{1,0:T(8,128)(2,1)S(1)}, bf16[512,128]{1,0:T(8,128)(2,1)S(1)}, u32[]{:S(2)}, u32[]{:S(2)}) collective-permute-start(bf16[512,128]{1,0:T(8,128)(2,1)S(1)} %fusion.21), channel_id=1, source_target_pairs={{8,0},{16,8},{24,16},{9,1},{17,9},{25,17},{10,2},{18,10},{26,18},{... | collective-permute-start | bytes 393224 | tf_op jit(solution)/shard_map/ppermute | solution.py:228
  97.8 9.5 %collective-permute-start.22 = (bf16[1,1,1,8,128]{4,3,2,1,0:T(8,128)(2,1)S(1)}, bf16[1,1,1,8,128]{4,3,2,1,0:T(8,128)(2,1)S(1)}, u32[]{:S(2)}, u32[]{:S(2)}) collective-permute-start(bf16[1,1,1,8,128]{4,3,2,1,0:T(8,128)(2,1)S(1)} %constant_dynamic-slice_fusion.3), channel_id=1, source_target_pairs={{10,1},{11,0},{12,3},{13,2},{14,5},{15,4},{18,9},{19,8},{20,11},{2... | collective-permute-start | bytes 6152 | tf_op jit(solution)/shard_map/ppermute | solution.py:73
  101.5 16.4 %collective-permute-start.20 = (bf16[1,1,8,8,128]{4,3,2,1,0:T(8,128)(2,1)S(1)}, bf16[1,1,8,8,128]{4,3,2,1,0:T(8,128)(2,1)S(1)}, u32[]{:S(2)}, u32[]{:S(2)}) collective-permute-start(bf16[1,1,8,8,128]{4,3,2,1,0:T(8,128)(2,1)S(1)} %get-tuple-element.65), channel_id=1, source_target_pairs={{8,2},{9,3},{10,4},{11,5},{12,6},{13,7},{16,10},{17,11},{18,12},{1... | collective-permute-start | bytes 49160 | tf_op jit(solution)/shard_map/ppermute | solution.py:73
  103.5 14.5 %collective-permute-start.23 = (bf16[1,1,8,8,128]{4,3,2,1,0:T(8,128)(2,1)S(1)}, bf16[1,1,8,8,128]{4,3,2,1,0:T(8,128)(2,1)S(1)}, u32[]{:S(2)}, u32[]{:S(2)}) collective-permute-start(bf16[1,1,8,8,128]{4,3,2,1,0:T(8,128)(2,1)S(1)} %get-tuple-element.64), channel_id=1, source_target_pairs={{10,0},{11,1},{12,2},{13,3},{14,4},{15,5},{18,8},{19,9},{20,10},{2... | collective-permute-start | bytes 49160 | tf_op jit(solution)/shard_map/ppermute | solution.py:73
  105.4 8.7 %collective-permute-start.21 = (bf16[1,8,1,8,128]{4,3,2,1,0:T(8,128)(2,1)S(1)}, bf16[1,8,1,8,128]{4,3,2,1,0:T(8,128)(2,1)S(1)}, u32[]{:S(2)}, u32[]{:S(2)}) collective-permute-start(bf16[1,8,1,8,128]{4,3,2,1,0:T(8,128)(2,1)S(1)} %constant_dynamic-slice_fusion.4), channel_id=1, source_target_pairs={{8,1},{9,0},{10,3},{11,2},{12,5},{13,4},{14,7},{15,6},{16,9},{17,8... | collective-permute-start | bytes 49160 | tf_op jit(solution)/shard_map/ppermute | solution.py:73
  107.3 6.7 %collective-permute-start.19 = (bf16[1,1,1,8,128]{4,3,2,1,0:T(8,128)(2,1)S(1)}, bf16[1,1,1,8,128]{4,3,2,1,0:T(8,128)(2,1)S(1)}, u32[]{:S(2)}, u32[]{:S(2)}) collective-permute-start(bf16[1,1,1,8,128]{4,3,2,1,0:T(8,128)(2,1)S(1)} %constant_dynamic-slice_fusion.5), channel_id=1, source_target_pairs={{8,3},{9,2},{10,5},{11,4},{12,7},{13,6},{16,11},{17,10},{18,13},{1... | collective-permute-start | bytes 6152 | tf_op jit(solution)/shard_map/ppermute | solution.py:73
  118.2 7.6 %collective-permute-start.24 = (bf16[864,128]{1,0:T(8,128)(2,1)S(1)}, bf16[864,128]{1,0:T(8,128)(2,1)S(1)}, u32[]{:S(2)}, u32[]{:S(2)}) collective-permute-start(bf16[864,128]{1,0:T(8,128)(2,1)S(1)} %get-tuple-element.46), channel_id=1, source_target_pairs={{0,2},{2,4},{4,6},{6,0},{1,3},{3,5},{5,7},{7,1},{8,10},{10,12},{12... | collective-permute-start | bytes 663560 | tf_op jit(solution)/shard_map/ppermute | solution.py:150
  118.3 11.4 %collective-permute-start.25 = (bf16[864,128]{1,0:T(8,128)(2,1)S(1)}, bf16[864,128]{1,0:T(8,128)(2,1)S(1)}, u32[]{:S(2)}, u32[]{:S(2)}) collective-permute-start(bf16[864,128]{1,0:T(8,128)(2,1)S(1)} %get-tuple-element.48), channel_id=1, source_target_pairs={{0,4},{2,6},{4,0},{6,2},{1,5},{3,7},{5,1},{7,3},{8,12},{10,14},{12... | collective-permute-start | bytes 663560 | tf_op jit(solution)/shard_map/ppermute | solution.py:150
  118.4 11.4 %collective-permute-start.26 = (bf16[864,128]{1,0:T(8,128)(2,1)S(1)}, bf16[864,128]{1,0:T(8,128)(2,1)S(1)}, u32[]{:S(2)}, u32[]{:S(2)}) collective-permute-start(bf16[864,128]{1,0:T(8,128)(2,1)S(1)} %get-tuple-element.47), channel_id=1, source_target_pairs={{0,6},{2,0},{4,2},{6,4},{1,7},{3,1},{5,3},{7,5},{8,14},{10,8},{12,... | collective-permute-start | bytes 663560 | tf_op jit(solution)/shard_map/ppermute | solution.py:150
  124.4 6.7 %copy-start.5 = (bf16[512,128]{1,0:T(8,128)(2,1)S(1)}, bf16[512,128]{1,0:T(8,128)(2,1)}, u32[]{:S(2)}) copy-start(bf16[512,128]{1,0:T(8,128)(2,1)} %copy-done.4) | copy-start | bytes 393220
  124.4 6.7 %copy-start.7 = (bf16[512,128]{1,0:T(8,128)(2,1)S(1)}, bf16[512,128]{1,0:T(8,128)(2,1)}, u32[]{:S(2)}) copy-start(bf16[512,128]{1,0:T(8,128)(2,1)} %copy-done.6) | copy-start | bytes 393220
  129.8 2.7 %collective-permute-start.27 = (f32[864,128]{1,0:T(8,128)S(1)}, f32[864,128]{1,0:T(8,128)S(1)}, u32[]{:S(2)}, u32[]{:S(2)}) collective-permute-start(f32[864,128]{1,0:T(8,128)S(1)} %convert_add_fusion), channel_id=1, source_target_pairs={{0,1},{1,0},{2,3},{3,2},{4,5},{5,4},{6,7},{7,6},{8,9},{9,8},{10,11... | collective-permute-start | bytes 1327112 | tf_op jit(solution)/shard_map/ppermute | solution.py:233

commit v10 on v7

--- a/solution.py
+++ b/solution.py
@@ -191,10 +191,9 @@
         table = tables[micro]
         live_now = live_rows[micro]
         values = inputs[micro]
-        activation = activate(values, gain_row).astype(jnp.bfloat16)
         start = cotangent[micro]
         start = jnp.where(live_now[:, None], start, jnp.zeros_like(start))
-        both = jnp.concatenate([cube(activation), cube(start)], axis=-1)
+        both = jnp.concatenate([cube(values), cube(start)], axis=-1)
         if micro == 0:
             carried = {}
             riding = kernel[0] if n_x >= 3 else None
@@ -204,7 +203,7 @@
         else:
             got = exchange(both, ("sx", "sy"), (n_x, n_y), 0)
         both_pad = assemble(both, got, table, split=True)
-        act_pad = both_pad[..., :channels]
+        act_pad = activate(both_pad[..., :channels], gain_row).astype(jnp.bfloat16)
         centre = start
         received = None
         kept_dy = start

time: 132 us -> 140 us (1.061)
  starting transfers between devices: 50.8 us -> 55.7 us
    ppermute x20, starting transfers between devices: 41.4 us -> 46.2 us  [send(): return lax.ppermute(piece, axes, route)]
    ppermute x20, waiting for transfers between devices: 14.5 us -> 18 us  [send(): return lax.ppermute(piece, axes, route)]
    ppermute x3, waiting for transfers between devices: 7.33 us -> 4.89 us  [scattered_sum(): lax.ppermute(piece, axis, [(i, (i + step) % count) for i in range(count)])]
    convert_element_type x2 -> x0, other arithmetic: 1.83 us -> none  [the longest x1 0.97 us: activate(): floats = values.astype(jnp.float32)]
  transfers between devices with their start and end apart: 28 -> 28, of which waited for: 8 -> 8; matrix products, arithmetic and copies ran while one was open for 12% -> 15% of each run, Pallas kernels for 0% -> 0%
where the time goes in v10:
time: 140 us; the launch traced here: 138 us
  starting transfers between devices  55.7 us (40%)
  waiting for transfers between devices  23.3 us (17%)
  between operations  19.7 us (14%)
  matrix products  16.1 us (12%)
  other arithmetic  15.8 us (11%)
  local copies, waits for them, and re-layouts  7.35 us (5%)
    ppermute x20, starting transfers between devices, send(): return lax.ppermute(piece, axes, route)  46.2 us
    ppermute x20, waiting for transfers between devices, send(): return lax.ppermute(piece, axes, route)  18 us
    conv_general_dilated x4, matrix products, conv_data(): lax.conv_general_dilated(padded, filters, (1, 1, 1), 'VALID', dimension_n...  11.8 us
    ppermute x3, starting transfers between devices, shards(): centre = lax.ppermute(result, 'pipe', down)  5.76 us
    ppermute x3, waiting for transfers between devices, scattered_sum(): lax.ppermute(piece, axis, [(i, (i + step) % count) for i in range(count)])  4.89 us
    transpose x1, matrix products, shards(): per_tap.transpose(1, 2, 3, 0, 4).reshape(taps * channels, channels)  4.28 us
  transfers between devices with their start and end apart: 28, of which 8 were waited for; matrix products, arithmetic and copies ran while one was open for 15% of the time, Pallas kernels for 0%

profile of v10, /device:TPU:21, one launch (start us, length us, event | category | flops | bytes accessed | tf_op | source)
XLA Modules:
  0.0 138.0 jit_solution(13038130299283515210)
XLA Ops:
  1.4 1.0 broadcast_select_fusion.12
  2.5 0.7 fusion.69
  3.2 0.7 collective-permute-start.4
  3.9 0.7 fusion.68
  4.7 3.0 %collective-permute-start = (bf16[1,1,1,8,256]{4,3,2,1,0:T(8,128)(2,1)S(1)}, bf16[1,1,1,8,256]{4,3,2,1,0:T(8,128)(2,1)S(1)}, u32[]{:S(2)}, u32[]{:S(2)}) collective-permute-start(bf16[1,1,1,8,256]{4,3,2,1,0:T(8,128)(2,1)S(1)} %constant_dynamic-slice_fusion.13), channel_id=1, source_target_pairs={{0,3},{1,2},{2,5},{3,4},{4,7},{5,6},{8,11},{9,10},{10,13},{11,12},... | collective-permute-start | bytes 12296 | tf_op jit(solution)/shard_map/ppermute | solution.py:73
  7.7 3.4 %collective-permute-start.2 = (bf16[1,1,1,8,256]{4,3,2,1,0:T(8,128)(2,1)S(1)}, bf16[1,1,1,8,256]{4,3,2,1,0:T(8,128)(2,1)S(1)}, u32[]{:S(2)}, u32[]{:S(2)}) collective-permute-start(bf16[1,1,1,8,256]{4,3,2,1,0:T(8,128)(2,1)S(1)} %constant_dynamic-slice_fusion.12), channel_id=1, source_target_pairs={{2,1},{3,0},{4,3},{5,2},{6,5},{7,4},{10,9},{11,8},{12,11},{13,10},... | collective-permute-start | bytes 12296 | tf_op jit(solution)/shard_map/ppermute | solution.py:73
  11.4 1.5 %collective-permute-start.3 = (bf16[992,128]{1,0:T(8,128)(2,1)S(1)}, bf16[992,128]{1,0:T(8,128)(2,1)S(1)}, u32[]{:S(2)}, u32[]{:S(2)}) collective-permute-start(bf16[992,128]{1,0:T(8,128)(2,1)S(1)} %get-tuple-element.59), channel_id=1, source_target_pairs={{0,6},{1,7},{2,0},{3,1},{4,2},{5,3},{6,4},{7,5},{8,14},{9,15},{10,... | collective-permute-start | bytes 761864 | tf_op jit(solution)/shard_map/ppermute | solution.py:73
  12.9 0.7 fusion.89
  13.6 0.7 fusion.90
  14.3 0.2 copy_dynamic-update-slice_fusion.1
  16.6 0.6 scatter_custom_fusion
  17.3 0.6 multiply_add_fusion.1
  17.9 0.5 fusion.72
  18.4 0.4 copy_dynamic-update-slice_fusion
  18.8 1.4 %broadcast_select_fusion = bf16[1,8,8,8,256]{4,0,3,2,1:T(2,128)(2,1)} fusion(bf16[1,8,8,8,256]{4,0,3,2,1:T(2,128)(2,1)S(1)} %copy_dynamic-update-slice_fusion, pred[]{:T(512)} %bitcast.29), kind=kLoop, calls=%fused_computation.3 | loop fusion | flops 131072 | bytes 524289 | tf_op jit(solution)/shard_map/jit(_where)/select_n | solution.py:48
  35.0 0.7 add.179
  36.4 7.3 %collective-permute-done.1 = bf16[992,128]{1,0:T(8,128)(2,1)S(1)} collective-permute-done((bf16[992,128]{1,0:T(8,128)(2,1)S(1)}, bf16[992,128]{1,0:T(8,128)(2,1)S(1)}, u32[]{:S(2)}, u32[]{:S(2)}) %collective-permute-start.1) | collective-permute-done | bytes 253984 | tf_op jit(solution)/shard_map/ppermute | solution.py:73
  44.4 0.7 gather_fusion
  45.1 1.0 rev.3
  46.3 2.1 %pad_maximum_fusion = bf16[1,10,10,10,256]{4,0,3,2,1:T(2,128)(2,1)S(1)} fusion(bf16[1,1,10,10,256]{4,0,3,2,1:T(2,128)(2,1)S(1)} %pad_maximum_fusion.11, bf16[1,8,1,10,256]{4,0,3,2,1:T(2,128)(2,1)S(1)} %copy.49, bf16[1,8,8,1,256]{4,0,3,2,1:T(2,128)(2,1)S(1)} %get-tuple-element.50, bf16[1,8,8,8,256]{4,0,3,2,1:T(2,128)(2,1)S(1)} %copy-done.3, ...), kind=kLoop, calls=%fused_computation.4 | loop fusion | flops 1536000 | bytes 1024000 | tf_op jit(solution)/shard_map/concatenate | solution.py:56
  48.5 2.9 %fusion.5 = f32[1,8,8,8,128]{4,0,3,2,1:T(1,128)S(1)} fusion(bf16[3,3,3,128,128]{4,3,2,1,0:T(8,128)(2,1)S(1)} %copy-done.4, bf16[1,10,10,10,256]{4,0,3,2,1:T(2,128)(2,1)S(1)} %pad_maximum_fusion), kind=kOutput, calls=%fused_computation.27 | convolution fusion | flops 452984832 | bytes 1658880 | tf_op jit(solution)/shard_map/conv_general_dilated | solution.py:108
  51.5 0.3 fusion.56
  52.0 0.3 fusion.61
  52.3 1.9 %collective-permute-start.8 = (bf16[1,1,8,8,128]{4,3,2,1,0:T(8,128)(2,1)S(1)}, bf16[1,1,8,8,128]{4,3,2,1,0:T(8,128)(2,1)S(1)}, u32[]{:S(2)}, u32[]{:S(2)}) collective-permute-start(bf16[1,1,8,8,128]{4,3,2,1,0:T(8,128)(2,1)S(1)} %get-tuple-element.71), channel_id=1, source_target_pairs={{8,2},{9,3},{10,4},{11,5},{12,6},{13,7},{16,10},{17,11},{18,12},{1... | collective-permute-start | bytes 49160 | tf_op jit(solution)/shard_map/ppermute | solution.py:73
  54.3 4.0 %collective-permute-start.11 = (bf16[1,1,8,8,128]{4,3,2,1,0:T(8,128)(2,1)S(1)}, bf16[1,1,8,8,128]{4,3,2,1,0:T(8,128)(2,1)S(1)}, u32[]{:S(2)}, u32[]{:S(2)}) collective-permute-start(bf16[1,1,8,8,128]{4,3,2,1,0:T(8,128)(2,1)S(1)} %get-tuple-element.72), channel_id=1, source_target_pairs={{10,0},{11,1},{12,2},{13,3},{14,4},{15,5},{18,8},{19,9},{20,10},{2... | collective-permute-start | bytes 49160 | tf_op jit(solution)/shard_map/ppermute | solution.py:73
  58.4 2.0 %multiply_reduce_fusion = f32[10,10,10]{2,1,0:T(8,128)S(1)} fusion(bf16[1,10,10,10,256]{4,0,3,2,1:T(2,128)(2,1)S(1)} %pad_maximum_fusion), kind=kLoop, calls=%fused_computation.26 | loop fusion | flops 383000 | bytes 260000 | tf_op jit(solution)/shard_map/reduce_sum | solution.py:19
  60.3 2.0 %collective-permute-start.7 = (bf16[1,1,1,8,128]{4,3,2,1,0:T(8,128)(2,1)S(1)}, bf16[1,1,1,8,128]{4,3,2,1,0:T(8,128)(2,1)S(1)}, u32[]{:S(2)}, u32[]{:S(2)}) collective-permute-start(bf16[1,1,1,8,128]{4,3,2,1,0:T(8,128)(2,1)S(1)} %constant_dynamic-slice_fusion.11), channel_id=1, source_target_pairs={{8,3},{9,2},{10,5},{11,4},{12,7},{13,6},{16,11},{17,10},{18,13},{1... | collective-permute-start | bytes 6152 | tf_op jit(solution)/shard_map/ppermute | solution.py:73
  62.3 1.9 %collective-permute-start.9 = (bf16[1,8,1,8,128]{4,3,2,1,0:T(8,128)(2,1)S(1)}, bf16[1,8,1,8,128]{4,3,2,1,0:T(8,128)(2,1)S(1)}, u32[]{:S(2)}, u32[]{:S(2)}) collective-permute-start(bf16[1,8,1,8,128]{4,3,2,1,0:T(8,128)(2,1)S(1)} %constant_dynamic-slice_fusion.10), channel_id=1, source_target_pairs={{8,1},{9,0},{10,3},{11,2},{12,5},{13,4},{14,7},{15,6},{16,9},{17,8... | collective-permute-start | bytes 49160 | tf_op jit(solution)/shard_map/ppermute | solution.py:73
  64.3 0.3 fusion.22
  64.6 1.9 %collective-permute-start.6 = (bf16[512,128]{1,0:T(8,128)(2,1)S(1)}, bf16[512,128]{1,0:T(8,128)(2,1)S(1)}, u32[]{:S(2)}, u32[]{:S(2)}) collective-permute-start(bf16[512,128]{1,0:T(8,128)(2,1)S(1)} %fusion.22), channel_id=1, source_target_pairs={{8,0},{16,8},{24,16},{9,1},{17,9},{25,17},{10,2},{18,10},{26,18},{... | collective-permute-start | bytes 393224 | tf_op jit(solution)/shard_map/ppermute | solution.py:228
  66.5 0.5 collective-permute-done.7
  67.0 3.2 %collective-permute-start.10 = (bf16[1,1,1,8,128]{4,3,2,1,0:T(8,128)(2,1)S(1)}, bf16[1,1,1,8,128]{4,3,2,1,0:T(8,128)(2,1)S(1)}, u32[]{:S(2)}, u32[]{:S(2)}) collective-permute-start(bf16[1,1,1,8,128]{4,3,2,1,0:T(8,128)(2,1)S(1)} %constant_dynamic-slice_fusion.9), channel_id=1, source_target_pairs={{10,1},{11,0},{12,3},{13,2},{14,5},{15,4},{18,9},{19,8},{20,11},{2... | collective-permute-start | bytes 6152 | tf_op jit(solution)/shard_map/ppermute | solution.py:73
  70.2 2.6 %collective-permute-done.10 = bf16[1,1,1,8,128]{4,3,2,1,0:T(8,128)(2,1)S(1)} collective-permute-done((bf16[1,1,1,8,128]{4,3,2,1,0:T(8,128)(2,1)S(1)}, bf16[1,1,1,8,128]{4,3,2,1,0:T(8,128)(2,1)S(1)}, u32[]{:S(2)}, u32[]{:S(2)}) %collective-permute-start.10) | collective-permute-done | bytes 2080 | tf_op jit(solution)/shard_map/ppermute | solution.py:73
  73.7 3.0 %fusion.9 = f32[1,8,8,8,128]{4,0,3,2,1:T(1,128)S(1)} fusion(bf16[3,3,3,128,128]{4,3,2,1,0:T(8,128)(2,1)S(1)} %bitcast.147, bf16[1,1,10,10,128]{4,0,3,2,1:T(2,128)(2,1)S(1)} %copy.58, bf16[1,8,1,10,128]{4,0,3,2,1:T(2,128)(2,1)S(1)} %copy.56, bf16[1,8,8,1,128]{4,0,3,2,1:T(2,128)(2,1)S(1)} %slice_bitcast_fusion.6, bf16[1,8,8,8,128]{4,0,3,2,1:T(2,128)(2,1)S(1)} %copy.54, ...), kind=kOutput, calls=%fused_computation.31 | convolution fusion | flops 454776832 | bytes 1402880 | tf_op jit(solution)/shard_map/conv_general_dilated | solution.py:108
  76.7 0.3 fusion.57
  77.0 0.3 fusion.27
  77.4 1.9 %collective-permute-start.14 = (bf16[1,1,8,8,128]{4,3,2,1,0:T(8,128)(2,1)S(1)}, bf16[1,1,8,8,128]{4,3,2,1,0:T(8,128)(2,1)S(1)}, u32[]{:S(2)}, u32[]{:S(2)}) collective-permute-start(bf16[1,1,8,8,128]{4,3,2,1,0:T(8,128)(2,1)S(1)} %get-tuple-element.66), channel_id=1, source_target_pairs={{8,2},{9,3},{10,4},{11,5},{12,6},{13,7},{16,10},{17,11},{18,12},{1... | collective-permute-start | bytes 49160 | tf_op jit(solution)/shard_map/ppermute | solution.py:73
  79.4 1.9 %collective-permute-start.12 = (bf16[512,128]{1,0:T(8,128)(2,1)S(1)}, bf16[512,128]{1,0:T(8,128)(2,1)S(1)}, u32[]{:S(2)}, u32[]{:S(2)}) collective-permute-start(bf16[512,128]{1,0:T(8,128)(2,1)S(1)} %fusion.27), channel_id=1, source_target_pairs={{8,0},{16,8},{24,16},{9,1},{17,9},{25,17},{10,2},{18,10},{26,18},{... | collective-permute-start | bytes 393224 | tf_op jit(solution)/shard_map/ppermute | solution.py:228
  81.3 1.9 %collective-permute-start.13 = (bf16[1,1,1,8,128]{4,3,2,1,0:T(8,128)(2,1)S(1)}, bf16[1,1,1,8,128]{4,3,2,1,0:T(8,128)(2,1)S(1)}, u32[]{:S(2)}, u32[]{:S(2)}) collective-permute-start(bf16[1,1,1,8,128]{4,3,2,1,0:T(8,128)(2,1)S(1)} %constant_dynamic-slice_fusion.8), channel_id=1, source_target_pairs={{8,3},{9,2},{10,5},{11,4},{12,7},{13,6},{16,11},{17,10},{18,13},{1... | collective-permute-start | bytes 6152 | tf_op jit(solution)/shard_map/ppermute | solution.py:73
  83.2 4.4 %collective-permute-start.17 = (bf16[1,1,8,8,128]{4,3,2,1,0:T(8,128)(2,1)S(1)}, bf16[1,1,8,8,128]{4,3,2,1,0:T(8,128)(2,1)S(1)}, u32[]{:S(2)}, u32[]{:S(2)}) collective-permute-start(bf16[1,1,8,8,128]{4,3,2,1,0:T(8,128)(2,1)S(1)} %get-tuple-element.67), channel_id=1, source_target_pairs={{10,0},{11,1},{12,2},{13,3},{14,4},{15,5},{18,8},{19,9},{20,10},{2... | collective-permute-start | bytes 49160 | tf_op jit(solution)/shard_map/ppermute | solution.py:73
  87.7 1.9 %collective-permute-start.15 = (bf16[1,8,1,8,128]{4,3,2,1,0:T(8,128)(2,1)S(1)}, bf16[1,8,1,8,128]{4,3,2,1,0:T(8,128)(2,1)S(1)}, u32[]{:S(2)}, u32[]{:S(2)}) collective-permute-start(bf16[1,8,1,8,128]{4,3,2,1,0:T(8,128)(2,1)S(1)} %constant_dynamic-slice_fusion.7), channel_id=1, source_target_pairs={{8,1},{9,0},{10,3},{11,2},{12,5},{13,4},{14,7},{15,6},{16,9},{17,8... | collective-permute-start | bytes 49160 | tf_op jit(solution)/shard_map/ppermute | solution.py:73
  89.6 2.7 %collective-permute-start.16 = (bf16[1,1,1,8,128]{4,3,2,1,0:T(8,128)(2,1)S(1)}, bf16[1,1,1,8,128]{4,3,2,1,0:T(8,128)(2,1)S(1)}, u32[]{:S(2)}, u32[]{:S(2)}) collective-permute-start(bf16[1,1,1,8,128]{4,3,2,1,0:T(8,128)(2,1)S(1)} %constant_dynamic-slice_fusion.6), channel_id=1, source_target_pairs={{10,1},{11,0},{12,3},{13,2},{14,5},{15,4},{18,9},{19,8},{20,11},{2... | collective-permute-start | bytes 6152 | tf_op jit(solution)/shard_map/ppermute | solution.py:73
  92.4 3.0 %collective-permute-done.16 = bf16[1,1,1,8,128]{4,3,2,1,0:T(8,128)(2,1)S(1)} collective-permute-done((bf16[1,1,1,8,128]{4,3,2,1,0:T(8,128)(2,1)S(1)}, bf16[1,1,1,8,128]{4,3,2,1,0:T(8,128)(2,1)S(1)}, u32[]{:S(2)}, u32[]{:S(2)}) %collective-permute-start.16) | collective-permute-done | bytes 2080 | tf_op jit(solution)/shard_map/ppermute | solution.py:73
  96.1 0.2 copy.61
  96.4 3.0 %fusion.8 = f32[1,8,8,8,128]{4,0,3,2,1:T(1,128)S(1)} fusion(bf16[3,3,3,128,128]{4,3,2,1,0:T(8,128)(2,1)S(1)} %bitcast.148, bf16[1,1,10,10,128]{4,0,3,2,1:T(2,128)(2,1)S(1)} %copy.65, bf16[1,8,1,10,128]{4,0,3,2,1:T(2,128)(2,1)S(1)} %copy.63, bf16[1,8,8,1,128]{4,0,3,2,1:T(2,128)(2,1)S(1)} %slice_bitcast_fusion.4, bf16[1,8,8,8,128]{4,0,3,2,1:T(2,128)(2,1)S(1)} %copy.61, ...), kind=kOutput, calls=%fused_computation.30 | convolution fusion | flops 454776832 | bytes 1402880 | tf_op jit(solution)/shard_map/conv_general_dilated | solution.py:108
  99.3 0.3 fusion.58
  99.7 0.3 fusion.30
  100.0 1.9 %collective-permute-start.18 = (bf16[512,128]{1,0:T(8,128)(2,1)S(1)}, bf16[512,128]{1,0:T(8,128)(2,1)S(1)}, u32[]{:S(2)}, u32[]{:S(2)}) collective-permute-start(bf16[512,128]{1,0:T(8,128)(2,1)S(1)} %fusion.30), channel_id=1, source_target_pairs={{8,0},{16,8},{24,16},{9,1},{17,9},{25,17},{10,2},{18,10},{26,18},{... | collective-permute-start | bytes 393224 | tf_op jit(solution)/shard_map/ppermute | solution.py:228
  102.0 3.6 %collective-permute-start.22 = (bf16[1,1,1,8,128]{4,3,2,1,0:T(8,128)(2,1)S(1)}, bf16[1,1,1,8,128]{4,3,2,1,0:T(8,128)(2,1)S(1)}, u32[]{:S(2)}, u32[]{:S(2)}) collective-permute-start(bf16[1,1,1,8,128]{4,3,2,1,0:T(8,128)(2,1)S(1)} %constant_dynamic-slice_fusion.3), channel_id=1, source_target_pairs={{10,1},{11,0},{12,3},{13,2},{14,5},{15,4},{18,9},{19,8},{20,11},{2... | collective-permute-start | bytes 6152 | tf_op jit(solution)/shard_map/ppermute | solution.py:73
  105.6 1.9 %collective-permute-start.20 = (bf16[1,1,8,8,128]{4,3,2,1,0:T(8,128)(2,1)S(1)}, bf16[1,1,8,8,128]{4,3,2,1,0:T(8,128)(2,1)S(1)}, u32[]{:S(2)}, u32[]{:S(2)}) collective-permute-start(bf16[1,1,8,8,128]{4,3,2,1,0:T(8,128)(2,1)S(1)} %get-tuple-element.65), channel_id=1, source_target_pairs={{8,2},{9,3},{10,4},{11,5},{12,6},{13,7},{16,10},{17,11},{18,12},{1... | collective-permute-start | bytes 49160 | tf_op jit(solution)/shard_map/ppermute | solution.py:73
  107.6 1.9 %collective-permute-start.23 = (bf16[1,1,8,8,128]{4,3,2,1,0:T(8,128)(2,1)S(1)}, bf16[1,1,8,8,128]{4,3,2,1,0:T(8,128)(2,1)S(1)}, u32[]{:S(2)}, u32[]{:S(2)}) collective-permute-start(bf16[1,1,8,8,128]{4,3,2,1,0:T(8,128)(2,1)S(1)} %get-tuple-element.64), channel_id=1, source_target_pairs={{10,0},{11,1},{12,2},{13,3},{14,4},{15,5},{18,8},{19,9},{20,10},{2... | collective-permute-start | bytes 49160 | tf_op jit(solution)/shard_map/ppermute | solution.py:73
  109.5 1.9 %collective-permute-start.21 = (bf16[1,8,1,8,128]{4,3,2,1,0:T(8,128)(2,1)S(1)}, bf16[1,8,1,8,128]{4,3,2,1,0:T(8,128)(2,1)S(1)}, u32[]{:S(2)}, u32[]{:S(2)}) collective-permute-start(bf16[1,8,1,8,128]{4,3,2,1,0:T(8,128)(2,1)S(1)} %constant_dynamic-slice_fusion.4), channel_id=1, source_target_pairs={{8,1},{9,0},{10,3},{11,2},{12,5},{13,4},{14,7},{15,6},{16,9},{17,8... | collective-permute-start | bytes 49160 | tf_op jit(solution)/shard_map/ppermute | solution.py:73
  111.4 2.1 %collective-permute-start.19 = (bf16[1,1,1,8,128]{4,3,2,1,0:T(8,128)(2,1)S(1)}, bf16[1,1,1,8,128]{4,3,2,1,0:T(8,128)(2,1)S(1)}, u32[]{:S(2)}, u32[]{:S(2)}) collective-permute-start(bf16[1,1,1,8,128]{4,3,2,1,0:T(8,128)(2,1)S(1)} %constant_dynamic-slice_fusion.5), channel_id=1, source_target_pairs={{8,3},{9,2},{10,5},{11,4},{12,7},{13,6},{16,11},{17,10},{18,13},{1... | collective-permute-start | bytes 6152 | tf_op jit(solution)/shard_map/ppermute | solution.py:73
  113.6 4.5 %collective-permute-done.19 = bf16[1,1,1,8,128]{4,3,2,1,0:T(8,128)(2,1)S(1)} collective-permute-done((bf16[1,1,1,8,128]{4,3,2,1,0:T(8,128)(2,1)S(1)}, bf16[1,1,1,8,128]{4,3,2,1,0:T(8,128)(2,1)S(1)}, u32[]{:S(2)}, u32[]{:S(2)}) %collective-permute-start.19) | collective-permute-done | bytes 2080 | tf_op jit(solution)/shard_map/ppermute | solution.py:73
  118.3 4.3 %multiply_convert_fusion = bf16[3,3,3,128,128]{4,3,2,1,0:T(8,128)(2,1)S(1)} fusion(bf16[1,10,10,10,256]{4,0,3,2,1:T(2,128)(2,1)S(1)} %pad_maximum_fusion, bf16[1,8,8,8,128]{4,3,2,1,0:T(8,128)(2,1)S(1)} %bitcast.182, f32[128]{0:T(128)S(1)} %bitcast.190, f32[10,10,10]{2,1,0:T(8,128)S(1)} %add_rsqrt_fusion), kind=kOutput, calls=%fused_computation.2 | convolution fusion | flops 454893568 | bytes 1610240 | tf_op jit(solution)/shard_map/transpose | solution.py:216
  123.0 2.3 %collective-permute-start.26 = (bf16[864,128]{1,0:T(8,128)(2,1)S(1)}, bf16[864,128]{1,0:T(8,128)(2,1)S(1)}, u32[]{:S(2)}, u32[]{:S(2)}) collective-permute-start(bf16[864,128]{1,0:T(8,128)(2,1)S(1)} %get-tuple-element.47), channel_id=1, source_target_pairs={{0,6},{2,0},{4,2},{6,4},{1,7},{3,1},{5,3},{7,5},{8,14},{10,8},{12,... | collective-permute-start | bytes 663560 | tf_op jit(solution)/shard_map/ppermute | solution.py:151
  126.1 3.0 %fusion.7 = f32[1,8,8,8,128]{4,0,3,2,1:T(1,128)S(1)} fusion(bf16[3,3,3,128,128]{4,3,2,1,0:T(8,128)(2,1)S(1)} %bitcast.149, bf16[1,1,10,10,128]{4,0,3,2,1:T(2,128)(2,1)S(1)} %copy.73, bf16[1,8,1,10,128]{4,0,3,2,1:T(2,128)(2,1)S(1)} %copy.71, bf16[1,8,8,1,128]{4,0,3,2,1:T(2,128)(2,1)S(1)} %slice_bitcast_fusion.2, bf16[1,8,8,8,128]{4,0,3,2,1:T(2,128)(2,1)S(1)} %copy.69, ...), kind=kOutput, calls=%fused_computation.29 | convolution fusion | flops 454776832 | bytes 1402880 | tf_op jit(solution)/shard_map/conv_general_dilated | solution.py:108
  129.1 0.3 fusion.59
  129.5 1.0 collective-permute-done.24
  130.5 3.9 %collective-permute-done.25 = bf16[864,128]{1,0:T(8,128)(2,1)S(1)} collective-permute-done((bf16[864,128]{1,0:T(8,128)(2,1)S(1)}, bf16[864,128]{1,0:T(8,128)(2,1)S(1)}, u32[]{:S(2)}, u32[]{:S(2)}) %collective-permute-start.25) | collective-permute-done | bytes 221216 | tf_op jit(solution)/shard_map/ppermute | solution.py:151
  134.5 1.3 collective-permute-start.27
  135.8 1.0 fusion.66
  136.8 0.3 collective-permute-done.27
  137.2 0.8 add_bitcast_fusion
  (235 shorter events, 4.8 us)
Async XLA Ops:
  0.6 13.7 %copy-start = (bf16[1,1,1,1,512,128]{5,4,3,2,1,0:T(8,128)(2,1)S(1)}, bf16[1,1,1,1,512,128]{5,4,3,2,1,0:T(8,128)(2,1)}, u32[]{:S(2)}) copy-start(bf16[1,1,1,1,512,128]{5,4,3,2,1,0:T(8,128)(2,1)} %param.6) | copy-start | bytes 393220
  0.6 10.7 %copy-start.5 = (bf16[1,864,128]{2,1,0:T(8,128)(2,1)S(1)}, bf16[1,864,128]{2,1,0:T(8,128)(2,1)}, u32[]{:S(2)}) copy-start(bf16[1,864,128]{2,1,0:T(8,128)(2,1)} %param.11) | copy-start | bytes 663556
  0.7 12.3 %copy-start.12 = (s32[1,1,1,1,27]{4,3,2,1,0:T(1,128)S(1)}, s32[1,1,1,1,27]{4,3,2,1,0:T(1,128)}, u32[]{:S(2)}) copy-start(s32[1,1,1,1,27]{4,3,2,1,0:T(1,128)} %param.8) | copy-start | bytes 328
  1.4 14.4 %copy-start.15 = (pred[8,8,8]{2,1,0:T(8,128)(4,1)}, pred[8,8,8]{2,1,0:T(8,128)(4,1)S(1)}, u32[]{:S(2)}) copy-start(pred[8,8,8]{2,1,0:T(8,128)(4,1)S(1)} %fusion.70) | copy-start | bytes 1540
  3.2 12.7 %copy-start.2 = (bf16[1,1,1,512,128]{4,3,2,1,0:T(8,128)(2,1)S(1)}, bf16[1,1,1,512,128]{4,3,2,1,0:T(8,128)(2,1)}, u32[]{:S(2)}) copy-start(bf16[1,1,1,512,128]{4,3,2,1,0:T(8,128)(2,1)} %param.7) | copy-start | bytes 393220
  3.2 32.7 %collective-permute-start.4 = (bf16[1,8,1,8,256]{4,3,2,1,0:T(8,128)(2,1)S(1)}, bf16[1,8,1,8,256]{4,3,2,1,0:T(8,128)(2,1)S(1)}, u32[]{:S(2)}, u32[]{:S(2)}) collective-permute-start(bf16[1,8,1,8,256]{4,3,2,1,0:T(8,128)(2,1)S(1)} %fusion.69), channel_id=1, source_target_pairs={{0,1},{1,0},{2,3},{3,2},{4,5},{5,4},{6,7},{7,6},{8,9},{9,8},{10,11... | collective-permute-start | bytes 98312 | tf_op jit(solution)/shard_map/ppermute | solution.py:73
  4.7 31.0 %collective-permute-start = (bf16[1,1,1,8,256]{4,3,2,1,0:T(8,128)(2,1)S(1)}, bf16[1,1,1,8,256]{4,3,2,1,0:T(8,128)(2,1)S(1)}, u32[]{:S(2)}, u32[]{:S(2)}) collective-permute-start(bf16[1,1,1,8,256]{4,3,2,1,0:T(8,128)(2,1)S(1)} %constant_dynamic-slice_fusion.13), channel_id=1, source_target_pairs={{0,3},{1,2},{2,5},{3,4},{4,7},{5,6},{8,11},{9,10},{10,13},{11,12},... | collective-permute-start | bytes 12296 | tf_op jit(solution)/shard_map/ppermute | solution.py:73
  7.7 27.9 %collective-permute-start.2 = (bf16[1,1,1,8,256]{4,3,2,1,0:T(8,128)(2,1)S(1)}, bf16[1,1,1,8,256]{4,3,2,1,0:T(8,128)(2,1)S(1)}, u32[]{:S(2)}, u32[]{:S(2)}) collective-permute-start(bf16[1,1,1,8,256]{4,3,2,1,0:T(8,128)(2,1)S(1)} %constant_dynamic-slice_fusion.12), channel_id=1, source_target_pairs={{2,1},{3,0},{4,3},{5,2},{6,5},{7,4},{10,9},{11,8},{12,11},{13,10},... | collective-permute-start | bytes 12296 | tf_op jit(solution)/shard_map/ppermute | solution.py:73
  11.2 33.1 %collective-permute-start.5 = (bf16[864,128]{1,0:T(8,128)(2,1)}, bf16[864,128]{1,0:T(8,128)(2,1)S(1)}, u32[]{:S(2)}, u32[]{:S(2)}) collective-permute-start(bf16[864,128]{1,0:T(8,128)(2,1)} %bitcast.162), channel_id=1, source_target_pairs={{0,4},{2,6},{4,0},{6,2},{1,5},{3,7},{5,1},{7,3},{8,12},{10,14},{12... | collective-permute-start | bytes 663560 | tf_op jit(solution)/shard_map/ppermute | solution.py:137
  11.4 24.9 %collective-permute-start.3 = (bf16[992,128]{1,0:T(8,128)(2,1)S(1)}, bf16[992,128]{1,0:T(8,128)(2,1)S(1)}, u32[]{:S(2)}, u32[]{:S(2)}) collective-permute-start(bf16[992,128]{1,0:T(8,128)(2,1)S(1)} %get-tuple-element.59), channel_id=1, source_target_pairs={{0,6},{1,7},{2,0},{3,1},{4,2},{5,3},{6,4},{7,5},{8,14},{9,15},{10,... | collective-permute-start | bytes 761864 | tf_op jit(solution)/shard_map/ppermute | solution.py:73
  14.7 5.6 %copy-start.18 = (f32[512]{0:T(512)}, f32[512]{0:T(512)S(1)}, u32[]{:S(2)}) copy-start(f32[512]{0:T(512)S(1)} %fusion.34) | copy-start | bytes 6148
  35.7 8.0 %collective-permute-start.1 = (bf16[992,128]{1,0:T(8,128)(2,1)S(1)}, bf16[992,128]{1,0:T(8,128)(2,1)S(1)}, u32[]{:S(2)}, u32[]{:S(2)}) collective-permute-start(bf16[992,128]{1,0:T(8,128)(2,1)S(1)} %get-tuple-element.60), channel_id=1, source_target_pairs={{0,2},{1,3},{2,4},{3,5},{4,6},{5,7},{6,0},{7,1},{8,10},{9,11},{10,... | collective-permute-start | bytes 761864 | tf_op jit(solution)/shard_map/ppermute | solution.py:73
  45.1 1.2 copy-start.3
  46.3 2.1 %copy-start.4 = (bf16[3,3,3,128,128]{4,3,2,1,0:T(8,128)(2,1)S(1)}, bf16[3,3,3,128,128]{4,3,2,1,0:T(8,128)(2,1)}, u32[]{:S(2)}) copy-start(bf16[3,3,3,128,128]{4,3,2,1,0:T(8,128)(2,1)} %rev.3) | copy-start | bytes 2654212
  48.5 3.0 %copy-start.13 = (f32[512]{0:T(512)S(1)}, f32[512]{0:T(512)}, u32[]{:S(2)}) copy-start(f32[512]{0:T(512)} %get-tuple-element.167) | copy-start | bytes 6148
  48.5 3.0 %copy-start.21 = (f32[1,128]{1,0:T(1,128)S(1)}, f32[1,128]{1,0:T(1,128)}, u32[]{:S(2)}) copy-start(f32[1,128]{1,0:T(1,128)} %param.10) | copy-start | bytes 1540
  48.5 3.4 %copy-start.17 = (f32[8,8,8]{2,1,0:T(8,128)S(1)}, f32[8,8,8]{2,1,0:T(8,128)}, u32[]{:S(2)}) copy-start(f32[8,8,8]{2,1,0:T(8,128)} %add.179) | copy-start | bytes 6148
  48.5 3.5 %copy-start.16 = (pred[8,8,8]{2,1,0:T(8,128)(4,1)S(1)}, pred[8,8,8]{2,1,0:T(8,128)(4,1)}, u32[]{:S(2)}) copy-start(pred[8,8,8]{2,1,0:T(8,128)(4,1)} %copy-done.15) | copy-start | bytes 1540
  51.5 2.8 %copy-start.19 = (f32[512]{0:T(512)S(1)}, f32[512]{0:T(512)}, u32[]{:S(2)}) copy-start(f32[512]{0:T(512)} %copy-done.18) | copy-start | bytes 6148
  51.5 12.8 %copy-start.22 = (pred[512]{0:T(512)(128)(4,1)S(1)}, pred[512]{0:T(512)(128)(4,1)}, u32[]{:S(2)}) copy-start(pred[512]{0:T(512)(128)(4,1)} %fusion.72) | copy-start | bytes 1540
  52.3 20.7 %collective-permute-start.8 = (bf16[1,1,8,8,128]{4,3,2,1,0:T(8,128)(2,1)S(1)}, bf16[1,1,8,8,128]{4,3,2,1,0:T(8,128)(2,1)S(1)}, u32[]{:S(2)}, u32[]{:S(2)}) collective-permute-start(bf16[1,1,8,8,128]{4,3,2,1,0:T(8,128)(2,1)S(1)} %get-tuple-element.71), channel_id=1, source_target_pairs={{8,2},{9,3},{10,4},{11,5},{12,6},{13,7},{16,10},{17,11},{18,12},{1... | collective-permute-start | bytes 49160 | tf_op jit(solution)/shard_map/ppermute | solution.py:73
  54.3 18.8 %collective-permute-start.11 = (bf16[1,1,8,8,128]{4,3,2,1,0:T(8,128)(2,1)S(1)}, bf16[1,1,8,8,128]{4,3,2,1,0:T(8,128)(2,1)S(1)}, u32[]{:S(2)}, u32[]{:S(2)}) collective-permute-start(bf16[1,1,8,8,128]{4,3,2,1,0:T(8,128)(2,1)S(1)} %get-tuple-element.72), channel_id=1, source_target_pairs={{10,0},{11,1},{12,2},{13,3},{14,4},{15,5},{18,8},{19,9},{20,10},{2... | collective-permute-start | bytes 49160 | tf_op jit(solution)/shard_map/ppermute | solution.py:73
  60.3 6.7 %collective-permute-start.7 = (bf16[1,1,1,8,128]{4,3,2,1,0:T(8,128)(2,1)S(1)}, bf16[1,1,1,8,128]{4,3,2,1,0:T(8,128)(2,1)S(1)}, u32[]{:S(2)}, u32[]{:S(2)}) collective-permute-start(bf16[1,1,1,8,128]{4,3,2,1,0:T(8,128)(2,1)S(1)} %constant_dynamic-slice_fusion.11), channel_id=1, source_target_pairs={{8,3},{9,2},{10,5},{11,4},{12,7},{13,6},{16,11},{17,10},{18,13},{1... | collective-permute-start | bytes 6152 | tf_op jit(solution)/shard_map/ppermute | solution.py:73
  62.3 10.6 %collective-permute-start.9 = (bf16[1,8,1,8,128]{4,3,2,1,0:T(8,128)(2,1)S(1)}, bf16[1,8,1,8,128]{4,3,2,1,0:T(8,128)(2,1)S(1)}, u32[]{:S(2)}, u32[]{:S(2)}) collective-permute-start(bf16[1,8,1,8,128]{4,3,2,1,0:T(8,128)(2,1)S(1)} %constant_dynamic-slice_fusion.10), channel_id=1, source_target_pairs={{8,1},{9,0},{10,3},{11,2},{12,5},{13,4},{14,7},{15,6},{16,9},{17,8... | collective-permute-start | bytes 49160 | tf_op jit(solution)/shard_map/ppermute | solution.py:73
  64.6 9.1 %copy-start.10 = (bf16[512,128]{1,0:T(8,128)(2,1)}, bf16[512,128]{1,0:T(8,128)(2,1)S(1)}, u32[]{:S(2)}) copy-start(bf16[512,128]{1,0:T(8,128)(2,1)S(1)} %fusion.22) | copy-start | bytes 393220
  64.6 8.8 %collective-permute-start.6 = (bf16[512,128]{1,0:T(8,128)(2,1)S(1)}, bf16[512,128]{1,0:T(8,128)(2,1)S(1)}, u32[]{:S(2)}, u32[]{:S(2)}) collective-permute-start(bf16[512,128]{1,0:T(8,128)(2,1)S(1)} %fusion.22), channel_id=1, source_target_pairs={{8,0},{16,8},{24,16},{9,1},{17,9},{25,17},{10,2},{18,10},{26,18},{... | collective-permute-start | bytes 393224 | tf_op jit(solution)/shard_map/ppermute | solution.py:228
  67.0 5.8 %collective-permute-start.10 = (bf16[1,1,1,8,128]{4,3,2,1,0:T(8,128)(2,1)S(1)}, bf16[1,1,1,8,128]{4,3,2,1,0:T(8,128)(2,1)S(1)}, u32[]{:S(2)}, u32[]{:S(2)}) collective-permute-start(bf16[1,1,1,8,128]{4,3,2,1,0:T(8,128)(2,1)S(1)} %constant_dynamic-slice_fusion.9), channel_id=1, source_target_pairs={{10,1},{11,0},{12,3},{13,2},{14,5},{15,4},{18,9},{19,8},{20,11},{2... | collective-permute-start | bytes 6152 | tf_op jit(solution)/shard_map/ppermute | solution.py:73
  77.4 18.9 %copy-start.6 = (bf16[512,128]{1,0:T(8,128)(2,1)}, bf16[512,128]{1,0:T(8,128)(2,1)S(1)}, u32[]{:S(2)}) copy-start(bf16[512,128]{1,0:T(8,128)(2,1)S(1)} %fusion.27) | copy-start | bytes 393220
  77.4 18.2 %collective-permute-start.14 = (bf16[1,1,8,8,128]{4,3,2,1,0:T(8,128)(2,1)S(1)}, bf16[1,1,8,8,128]{4,3,2,1,0:T(8,128)(2,1)S(1)}, u32[]{:S(2)}, u32[]{:S(2)}) collective-permute-start(bf16[1,1,8,8,128]{4,3,2,1,0:T(8,128)(2,1)S(1)} %get-tuple-element.66), channel_id=1, source_target_pairs={{8,2},{9,3},{10,4},{11,5},{12,6},{13,7},{16,10},{17,11},{18,12},{1... | collective-permute-start | bytes 49160 | tf_op jit(solution)/shard_map/ppermute | solution.py:73
  79.4 16.7 %collective-permute-start.12 = (bf16[512,128]{1,0:T(8,128)(2,1)S(1)}, bf16[512,128]{1,0:T(8,128)(2,1)S(1)}, u32[]{:S(2)}, u32[]{:S(2)}) collective-permute-start(bf16[512,128]{1,0:T(8,128)(2,1)S(1)} %fusion.27), channel_id=1, source_target_pairs={{8,0},{16,8},{24,16},{9,1},{17,9},{25,17},{10,2},{18,10},{26,18},{... | collective-permute-start | bytes 393224 | tf_op jit(solution)/shard_map/ppermute | solution.py:228
  81.3 8.3 %collective-permute-start.13 = (bf16[1,1,1,8,128]{4,3,2,1,0:T(8,128)(2,1)S(1)}, bf16[1,1,1,8,128]{4,3,2,1,0:T(8,128)(2,1)S(1)}, u32[]{:S(2)}, u32[]{:S(2)}) collective-permute-start(bf16[1,1,1,8,128]{4,3,2,1,0:T(8,128)(2,1)S(1)} %constant_dynamic-slice_fusion.8), channel_id=1, source_target_pairs={{8,3},{9,2},{10,5},{11,4},{12,7},{13,6},{16,11},{17,10},{18,13},{1... | collective-permute-start | bytes 6152 | tf_op jit(solution)/shard_map/ppermute | solution.py:73
  83.2 12.5 %collective-permute-start.17 = (bf16[1,1,8,8,128]{4,3,2,1,0:T(8,128)(2,1)S(1)}, bf16[1,1,8,8,128]{4,3,2,1,0:T(8,128)(2,1)S(1)}, u32[]{:S(2)}, u32[]{:S(2)}) collective-permute-start(bf16[1,1,8,8,128]{4,3,2,1,0:T(8,128)(2,1)S(1)} %get-tuple-element.67), channel_id=1, source_target_pairs={{10,0},{11,1},{12,2},{13,3},{14,4},{15,5},{18,8},{19,9},{20,10},{2... | collective-permute-start | bytes 49160 | tf_op jit(solution)/shard_map/ppermute | solution.py:73
  87.7 7.8 %collective-permute-start.15 = (bf16[1,8,1,8,128]{4,3,2,1,0:T(8,128)(2,1)S(1)}, bf16[1,8,1,8,128]{4,3,2,1,0:T(8,128)(2,1)S(1)}, u32[]{:S(2)}, u32[]{:S(2)}) collective-permute-start(bf16[1,8,1,8,128]{4,3,2,1,0:T(8,128)(2,1)S(1)} %constant_dynamic-slice_fusion.7), channel_id=1, source_target_pairs={{8,1},{9,0},{10,3},{11,2},{12,5},{13,4},{14,7},{15,6},{16,9},{17,8... | collective-permute-start | bytes 49160 | tf_op jit(solution)/shard_map/ppermute | solution.py:73
  89.6 5.8 %collective-permute-start.16 = (bf16[1,1,1,8,128]{4,3,2,1,0:T(8,128)(2,1)S(1)}, bf16[1,1,1,8,128]{4,3,2,1,0:T(8,128)(2,1)S(1)}, u32[]{:S(2)}, u32[]{:S(2)}) collective-permute-start(bf16[1,1,1,8,128]{4,3,2,1,0:T(8,128)(2,1)S(1)} %constant_dynamic-slice_fusion.6), channel_id=1, source_target_pairs={{10,1},{11,0},{12,3},{13,2},{14,5},{15,4},{18,9},{19,8},{20,11},{2... | collective-permute-start | bytes 6152 | tf_op jit(solution)/shard_map/ppermute | solution.py:73
  100.0 22.6 %copy-start.8 = (bf16[512,128]{1,0:T(8,128)(2,1)}, bf16[512,128]{1,0:T(8,128)(2,1)S(1)}, u32[]{:S(2)}) copy-start(bf16[512,128]{1,0:T(8,128)(2,1)S(1)} %fusion.30) | copy-start | bytes 393220
  100.0 18.2 %collective-permute-start.18 = (bf16[512,128]{1,0:T(8,128)(2,1)S(1)}, bf16[512,128]{1,0:T(8,128)(2,1)S(1)}, u32[]{:S(2)}, u32[]{:S(2)}) collective-permute-start(bf16[512,128]{1,0:T(8,128)(2,1)S(1)} %fusion.30), channel_id=1, source_target_pairs={{8,0},{16,8},{24,16},{9,1},{17,9},{25,17},{10,2},{18,10},{26,18},{... | collective-permute-start | bytes 393224 | tf_op jit(solution)/shard_map/ppermute | solution.py:228
  102.0 9.4 %collective-permute-start.22 = (bf16[1,1,1,8,128]{4,3,2,1,0:T(8,128)(2,1)S(1)}, bf16[1,1,1,8,128]{4,3,2,1,0:T(8,128)(2,1)S(1)}, u32[]{:S(2)}, u32[]{:S(2)}) collective-permute-start(bf16[1,1,1,8,128]{4,3,2,1,0:T(8,128)(2,1)S(1)} %constant_dynamic-slice_fusion.3), channel_id=1, source_target_pairs={{10,1},{11,0},{12,3},{13,2},{14,5},{15,4},{18,9},{19,8},{20,11},{2... | collective-permute-start | bytes 6152 | tf_op jit(solution)/shard_map/ppermute | solution.py:73
  105.6 17.0 %collective-permute-start.20 = (bf16[1,1,8,8,128]{4,3,2,1,0:T(8,128)(2,1)S(1)}, bf16[1,1,8,8,128]{4,3,2,1,0:T(8,128)(2,1)S(1)}, u32[]{:S(2)}, u32[]{:S(2)}) collective-permute-start(bf16[1,1,8,8,128]{4,3,2,1,0:T(8,128)(2,1)S(1)} %get-tuple-element.65), channel_id=1, source_target_pairs={{8,2},{9,3},{10,4},{11,5},{12,6},{13,7},{16,10},{17,11},{18,12},{1... | collective-permute-start | bytes 49160 | tf_op jit(solution)/shard_map/ppermute | solution.py:73
  107.6 15.1 %collective-permute-start.23 = (bf16[1,1,8,8,128]{4,3,2,1,0:T(8,128)(2,1)S(1)}, bf16[1,1,8,8,128]{4,3,2,1,0:T(8,128)(2,1)S(1)}, u32[]{:S(2)}, u32[]{:S(2)}) collective-permute-start(bf16[1,1,8,8,128]{4,3,2,1,0:T(8,128)(2,1)S(1)} %get-tuple-element.64), channel_id=1, source_target_pairs={{10,0},{11,1},{12,2},{13,3},{14,4},{15,5},{18,8},{19,9},{20,10},{2... | collective-permute-start | bytes 49160 | tf_op jit(solution)/shard_map/ppermute | solution.py:73
  109.5 8.7 %collective-permute-start.21 = (bf16[1,8,1,8,128]{4,3,2,1,0:T(8,128)(2,1)S(1)}, bf16[1,8,1,8,128]{4,3,2,1,0:T(8,128)(2,1)S(1)}, u32[]{:S(2)}, u32[]{:S(2)}) collective-permute-start(bf16[1,8,1,8,128]{4,3,2,1,0:T(8,128)(2,1)S(1)} %constant_dynamic-slice_fusion.4), channel_id=1, source_target_pairs={{8,1},{9,0},{10,3},{11,2},{12,5},{13,4},{14,7},{15,6},{16,9},{17,8... | collective-permute-start | bytes 49160 | tf_op jit(solution)/shard_map/ppermute | solution.py:73
  111.4 6.7 %collective-permute-start.19 = (bf16[1,1,1,8,128]{4,3,2,1,0:T(8,128)(2,1)S(1)}, bf16[1,1,1,8,128]{4,3,2,1,0:T(8,128)(2,1)S(1)}, u32[]{:S(2)}, u32[]{:S(2)}) collective-permute-start(bf16[1,1,1,8,128]{4,3,2,1,0:T(8,128)(2,1)S(1)} %constant_dynamic-slice_fusion.5), channel_id=1, source_target_pairs={{8,3},{9,2},{10,5},{11,4},{12,7},{13,6},{16,11},{17,10},{18,13},{1... | collective-permute-start | bytes 6152 | tf_op jit(solution)/shard_map/ppermute | solution.py:73
  122.9 7.6 %collective-permute-start.24 = (bf16[864,128]{1,0:T(8,128)(2,1)S(1)}, bf16[864,128]{1,0:T(8,128)(2,1)S(1)}, u32[]{:S(2)}, u32[]{:S(2)}) collective-permute-start(bf16[864,128]{1,0:T(8,128)(2,1)S(1)} %get-tuple-element.46), channel_id=1, source_target_pairs={{0,2},{2,4},{4,6},{6,0},{1,3},{3,5},{5,7},{7,1},{8,10},{10,12},{12... | collective-permute-start | bytes 663560 | tf_op jit(solution)/shard_map/ppermute | solution.py:151
  122.9 11.4 %collective-permute-start.25 = (bf16[864,128]{1,0:T(8,128)(2,1)S(1)}, bf16[864,128]{1,0:T(8,128)(2,1)S(1)}, u32[]{:S(2)}, u32[]{:S(2)}) collective-permute-start(bf16[864,128]{1,0:T(8,128)(2,1)S(1)} %get-tuple-element.48), channel_id=1, source_target_pairs={{0,4},{2,6},{4,0},{6,2},{1,5},{3,7},{5,1},{7,3},{8,12},{10,14},{12... | collective-permute-start | bytes 663560 | tf_op jit(solution)/shard_map/ppermute | solution.py:151
  123.0 11.4 %collective-permute-start.26 = (bf16[864,128]{1,0:T(8,128)(2,1)S(1)}, bf16[864,128]{1,0:T(8,128)(2,1)S(1)}, u32[]{:S(2)}, u32[]{:S(2)}) collective-permute-start(bf16[864,128]{1,0:T(8,128)(2,1)S(1)} %get-tuple-element.47), channel_id=1, source_target_pairs={{0,6},{2,0},{4,2},{6,4},{1,7},{3,1},{5,3},{7,5},{8,14},{10,8},{12,... | collective-permute-start | bytes 663560 | tf_op jit(solution)/shard_map/ppermute | solution.py:151
  126.1 3.1 %copy-start.1 = (bf16[1,1,1,1,512,128]{5,4,3,2,1,0:T(8,128)(2,1)S(1)}, bf16[1,1,1,1,512,128]{5,4,3,2,1,0:T(8,128)(2,1)}, u32[]{:S(2)}) copy-start(bf16[1,1,1,1,512,128]{5,4,3,2,1,0:T(8,128)(2,1)} %param.6) | copy-start | bytes 393220
  126.1 3.1 %copy-start.14 = (f32[512]{0:T(512)S(1)}, f32[512]{0:T(512)}, u32[]{:S(2)}) copy-start(f32[512]{0:T(512)} %get-tuple-element.167) | copy-start | bytes 6148
  129.1 6.7 %copy-start.20 = (f32[512]{0:T(512)S(1)}, f32[512]{0:T(512)}, u32[]{:S(2)}) copy-start(f32[512]{0:T(512)} %copy-done.18) | copy-start | bytes 6148
  129.1 6.7 %copy-start.7 = (bf16[512,128]{1,0:T(8,128)(2,1)S(1)}, bf16[512,128]{1,0:T(8,128)(2,1)}, u32[]{:S(2)}) copy-start(bf16[512,128]{1,0:T(8,128)(2,1)} %copy-done.6) | copy-start | bytes 393220
  129.1 6.7 %copy-start.9 = (bf16[512,128]{1,0:T(8,128)(2,1)S(1)}, bf16[512,128]{1,0:T(8,128)(2,1)}, u32[]{:S(2)}) copy-start(bf16[512,128]{1,0:T(8,128)(2,1)} %copy-done.8) | copy-start | bytes 393220
  129.1 6.7 %copy-start.11 = (bf16[512,128]{1,0:T(8,128)(2,1)S(1)}, bf16[512,128]{1,0:T(8,128)(2,1)}, u32[]{:S(2)}) copy-start(bf16[512,128]{1,0:T(8,128)(2,1)} %copy-done.10) | copy-start | bytes 393220
  129.1 6.7 %copy-start.23 = (pred[512]{0:T(512)(128)(4,1)S(1)}, pred[512]{0:T(512)(128)(4,1)}, u32[]{:S(2)}) copy-start(pred[512]{0:T(512)(128)(4,1)} %fusion.72) | copy-start | bytes 1540
  134.5 2.7 %collective-permute-start.27 = (f32[864,128]{1,0:T(8,128)S(1)}, f32[864,128]{1,0:T(8,128)S(1)}, u32[]{:S(2)}, u32[]{:S(2)}) collective-permute-start(f32[864,128]{1,0:T(8,128)S(1)} %convert_add_fusion), channel_id=1, source_target_pairs={{0,1},{1,0},{2,3},{3,2},{4,5},{5,4},{6,7},{7,6},{8,9},{9,8},{10,11... | collective-permute-start | bytes 1327112 | tf_op jit(solution)/shard_map/ppermute | solution.py:233

commit v11 on v7

--- a/solution.py
+++ b/solution.py
@@ -209,8 +209,29 @@
         received = None
         kept_dy = start
         kept_grad = jnp.zeros((row_count, channels), jnp.bfloat16)
+        keys = directions()
+        down = [(p, p - 1) for p in range(1, n_pipe)]
+
+        def middle(tick, carry):
+            centre, pieces, kept_dy, kept_grad = carry
+            active = segment_place == n_pipe - 1 - tick
+            kept_dy = jnp.where(active, centre, kept_dy)
+            grad_pad = assemble(cube(centre), dict(zip(keys, pieces)), table)
+            grad_act = conv_data(grad_pad, flipped).reshape(row_count, channels)
+            result = finish_grad(values, centre, live_now, grad_act, gain_row)
+            kept_grad = jnp.where(active, result, kept_grad)
+            sent = exchange(cube(result), ("pipe", "sx", "sy"), (n_pipe, n_x, n_y), 1)
+            return (lax.ppermute(result, "pipe", down), tuple(sent[k] for k in keys), kept_dy, kept_grad)
+
         for tick in range(n_pipe):
             active = segment_place == n_pipe - 1 - tick
+            if 0 < tick < n_pipe - 1:
+                if tick == 1:
+                    carry = (centre, tuple(received[k] for k in keys), kept_dy, kept_grad)
+                    carry = lax.fori_loop(1, n_pipe - 1, middle, carry)
+                    centre, pieces, kept_dy, kept_grad = carry
+                    received = dict(zip(keys, pieces))
+                continue
             kept_dy = jnp.where(active, centre, kept_dy)
             if tick == n_pipe - 1:
                 per_tap = conv_filter(act_pad, cube(kept_dy))
@@ -225,7 +246,6 @@
             result = finish_grad(values, centre, live_now, grad_act, gain_row)
             kept_grad = jnp.where(active, result, kept_grad)
             if tick < n_pipe - 1:
-                down = [(p, p - 1) for p in range(1, n_pipe)]
                 centre = lax.ppermute(result, "pipe", down)
                 received = exchange(cube(result), ("pipe", "sx", "sy"), (n_pipe, n_x, n_y), 1)
         grads_out.append(kept_grad)

time: 132 us -> 149 us (1.13)
  waiting for transfers between devices: 22.3 us -> 32.9 us
  starting transfers between devices: 50.8 us -> 53.8 us
  local copies, waits for them, and re-layouts: 6.65 us -> 8.33 us
    ppermute x20, waiting for transfers between devices: 14.5 us -> 25.3 us  [send(): return lax.ppermute(piece, axes, route)]
    ppermute x0 -> x2, starting transfers between devices: none -> 4.15 us  [middle(): lax.ppermute(result, 'pipe', down)]
    ppermute x3 -> x1, starting transfers between devices: 5.76 us -> 2.1 us  [shards(): centre = lax.ppermute(result, 'pipe', down)]
    ppermute x20, starting transfers between devices: 41.4 us -> 44.4 us  [send(): return lax.ppermute(piece, axes, route)]
    ppermute x3, waiting for transfers between devices: 7.33 us -> 5.47 us  [scattered_sum(): lax.ppermute(piece, axis, [(i, (i + step) % count) for i in range(count)])]
    ppermute x3 -> x1, waiting for transfers between devices: 0.01 us -> 1.81 us  [shards(): centre = lax.ppermute(result, 'pipe', down)]
  transfers between devices with their start and end apart: 28 -> 28, of which waited for: 8 -> 11; matrix products, arithmetic and copies ran while one was open for 12% -> 8% of each run, Pallas kernels for 0% -> 0%
where the time goes in v11:
time: 149 us; the launch traced here: 147 us
  starting transfers between devices  53.8 us (36%)
  waiting for transfers between devices  32.9 us (22%)
  between operations  19.5 us (13%)
  other arithmetic  16.3 us (11%)
  matrix products  15.8 us (11%)
  local copies, waits for them, and re-layouts  8.33 us (6%)
    ppermute x20, starting transfers between devices, send(): return lax.ppermute(piece, axes, route)  44.4 us
    ppermute x20, waiting for transfers between devices, send(): return lax.ppermute(piece, axes, route)  25.3 us
    conv_general_dilated x4, matrix products, conv_data(): lax.conv_general_dilated(padded, filters, (1, 1, 1), 'VALID', dimension_n...  12 us
    ppermute x3, waiting for transfers between devices, scattered_sum(): lax.ppermute(piece, axis, [(i, (i + step) % count) for i in range(count)])  5.47 us
    ppermute x2, starting transfers between devices, middle(): lax.ppermute(result, 'pipe', down)  4.15 us
    transpose x1, matrix products, shards(): per_tap.transpose(1, 2, 3, 0, 4).reshape(taps * channels, channels)  3.76 us
  transfers between devices with their start and end apart: 28, of which 11 were waited for; matrix products, arithmetic and copies ran while one was open for 8% of the time, Pallas kernels for 0%

profile of v11, /device:TPU:21, one launch (start us, length us, event | category | flops | bytes accessed | tf_op | source)
XLA Modules:
  0.0 147.2 jit_solution(1127510411271272369)
XLA Ops:
  0.6 1.1 fusion.34
  1.7 0.9 convert_element_type.194
  3.5 1.0 broadcast_select_fusion.42
  4.6 0.9 multiply_convert_fusion.2
  5.5 3.7 %collective-permute-start.6 = (bf16[1,1,1,8,256]{4,3,2,1,0:T(8,128)(2,1)S(1)}, bf16[1,1,1,8,256]{4,3,2,1,0:T(8,128)(2,1)S(1)}, u32[]{:S(2)}, u32[]{:S(2)}) collective-permute-start(bf16[1,1,1,8,256]{4,3,2,1,0:T(8,128)(2,1)S(1)} %constant_dynamic-slice_fusion.10), channel_id=1, source_target_pairs={{0,3},{1,2},{2,5},{3,4},{4,7},{5,6},{8,11},{9,10},{10,13},{11,12},... | collective-permute-start | bytes 12296 | tf_op jit(solution)/shard_map/ppermute | solution.py:73
  9.2 2.8 %collective-permute-start.8 = (bf16[1,1,1,8,256]{4,3,2,1,0:T(8,128)(2,1)S(1)}, bf16[1,1,1,8,256]{4,3,2,1,0:T(8,128)(2,1)S(1)}, u32[]{:S(2)}, u32[]{:S(2)}) collective-permute-start(bf16[1,1,1,8,256]{4,3,2,1,0:T(8,128)(2,1)S(1)} %constant_dynamic-slice_fusion.9), channel_id=1, source_target_pairs={{2,1},{3,0},{4,3},{5,2},{6,5},{7,4},{10,9},{11,8},{12,11},{13,10},... | collective-permute-start | bytes 12296 | tf_op jit(solution)/shard_map/ppermute | solution.py:73
  12.2 1.5 %collective-permute-start.9 = (bf16[992,128]{1,0:T(8,128)(2,1)S(1)}, bf16[992,128]{1,0:T(8,128)(2,1)S(1)}, u32[]{:S(2)}, u32[]{:S(2)}) collective-permute-start(bf16[992,128]{1,0:T(8,128)(2,1)S(1)} %get-tuple-element.925), channel_id=1, source_target_pairs={{0,6},{1,7},{2,0},{3,1},{4,2},{5,3},{6,4},{7,5},{8,14},{9,15},{10,... | collective-permute-start | bytes 761864 | tf_op jit(solution)/shard_map/ppermute | solution.py:73
  13.7 0.7 fusion.73
  14.4 0.7 fusion.74
  17.6 0.6 scatter_custom_fusion
  18.2 0.4 copy_dynamic-update-slice_fusion
  18.6 0.6 broadcast_select_fusion.35
  34.4 1.3 collective-permute-start.10
  35.9 0.6 collective-permute-done.10
  37.0 4.7 %collective-permute-done.7 = bf16[992,128]{1,0:T(8,128)(2,1)S(1)} collective-permute-done((bf16[992,128]{1,0:T(8,128)(2,1)S(1)}, bf16[992,128]{1,0:T(8,128)(2,1)S(1)}, u32[]{:S(2)}, u32[]{:S(2)}) %collective-permute-start.7) | collective-permute-done | bytes 253984 | tf_op jit(solution)/shard_map/ppermute | solution.py:73
  42.2 1.0 pad_maximum_fusion.1
  43.3 0.7 gather_fusion
  44.0 1.1 rev.3
  45.1 2.1 %pad_maximum_fusion = bf16[1,10,10,10,256]{4,0,3,2,1:T(2,128)(2,1)S(1)} fusion(bf16[1,1,10,10,256]{4,0,3,2,1:T(2,128)(2,1)S(1)} %pad_maximum_fusion.5, bf16[1,8,1,10,256]{4,0,3,2,1:T(2,128)(2,1)S(1)} %copy.50, bf16[1,8,8,1,256]{4,0,3,2,1:T(2,128)(2,1)S(1)} %get-tuple-element.915, bf16[1,8,8,8,256]{4,0,3,2,1:T(2,128)(2,1)S(1)} %broadcast_select_fusion.35, ...), kind=kLoop, calls=%fused_computation.72 | loop fusion | flops 1536000 | bytes 1024000 | tf_op jit(solution)/shard_map/concatenate | solution.py:56
  47.3 3.0 %fusion.18 = f32[1,8,8,8,128]{4,0,3,2,1:T(1,128)S(1)} fusion(bf16[3,3,3,128,128]{4,3,2,1,0:T(8,128)(2,1)S(1)} %copy-done.9, bf16[1,10,10,10,256]{4,0,3,2,1:T(2,128)(2,1)S(1)} %pad_maximum_fusion), kind=kOutput, calls=%fused_computation.82 | convolution fusion | flops 452984832 | bytes 1658880 | tf_op jit(solution)/shard_map/conv_general_dilated | solution.py:108
  50.3 0.3 fusion.48
  51.1 2.1 %collective-permute-start.17 = (bf16[1,1,8,8,128]{4,3,2,1,0:T(8,128)(2,1)S(1)}, bf16[1,1,8,8,128]{4,3,2,1,0:T(8,128)(2,1)S(1)}, u32[]{:S(2)}, u32[]{:S(2)}) collective-permute-start(bf16[1,1,8,8,128]{4,3,2,1,0:T(8,128)(2,1)S(1)} %get-tuple-element.930), channel_id=1, source_target_pairs={{10,0},{11,1},{12,2},{13,3},{14,4},{15,5},{18,8},{19,9},{20,10},{2... | collective-permute-start | bytes 49160 | tf_op jit(solution)/shard_map/ppermute | solution.py:73
  53.1 3.0 %collective-permute-start.14 = (bf16[1,1,8,8,128]{4,3,2,1,0:T(8,128)(2,1)S(1)}, bf16[1,1,8,8,128]{4,3,2,1,0:T(8,128)(2,1)S(1)}, u32[]{:S(2)}, u32[]{:S(2)}) collective-permute-start(bf16[1,1,8,8,128]{4,3,2,1,0:T(8,128)(2,1)S(1)} %get-tuple-element.931), channel_id=1, source_target_pairs={{8,2},{9,3},{10,4},{11,5},{12,6},{13,7},{16,10},{17,11},{18,12},{1... | collective-permute-start | bytes 49160 | tf_op jit(solution)/shard_map/ppermute | solution.py:73
  56.2 3.3 %collective-permute-start.15 = (bf16[1,8,1,8,128]{4,3,2,1,0:T(8,128)(2,1)S(1)}, bf16[1,8,1,8,128]{4,3,2,1,0:T(8,128)(2,1)S(1)}, u32[]{:S(2)}, u32[]{:S(2)}) collective-permute-start(bf16[1,8,1,8,128]{4,3,2,1,0:T(8,128)(2,1)S(1)} %constant_dynamic-slice_fusion.7), channel_id=1, source_target_pairs={{8,1},{9,0},{10,3},{11,2},{12,5},{13,4},{14,7},{15,6},{16,9},{17,8... | collective-permute-start | bytes 49160 | tf_op jit(solution)/shard_map/ppermute | solution.py:73
  59.5 3.1 %collective-permute-start.16 = (bf16[1,1,1,8,128]{4,3,2,1,0:T(8,128)(2,1)S(1)}, bf16[1,1,1,8,128]{4,3,2,1,0:T(8,128)(2,1)S(1)}, u32[]{:S(2)}, u32[]{:S(2)}) collective-permute-start(bf16[1,1,1,8,128]{4,3,2,1,0:T(8,128)(2,1)S(1)} %constant_dynamic-slice_fusion.6), channel_id=1, source_target_pairs={{10,1},{11,0},{12,3},{13,2},{14,5},{15,4},{18,9},{19,8},{20,11},{2... | collective-permute-start | bytes 6152 | tf_op jit(solution)/shard_map/ppermute | solution.py:73
  63.1 1.4 copy.61
  64.5 1.9 %collective-permute-start.13 = (bf16[1,1,1,8,128]{4,3,2,1,0:T(8,128)(2,1)S(1)}, bf16[1,1,1,8,128]{4,3,2,1,0:T(8,128)(2,1)S(1)}, u32[]{:S(2)}, u32[]{:S(2)}) collective-permute-start(bf16[1,1,1,8,128]{4,3,2,1,0:T(8,128)(2,1)S(1)} %constant_dynamic-slice_fusion.8), channel_id=1, source_target_pairs={{8,3},{9,2},{10,5},{11,4},{12,7},{13,6},{16,11},{17,10},{18,13},{1... | collective-permute-start | bytes 6152 | tf_op jit(solution)/shard_map/ppermute | solution.py:73
  66.4 2.1 %collective-permute-start.12 = (bf16[512,128]{1,0:T(8,128)(2,1)S(1)}, bf16[512,128]{1,0:T(8,128)(2,1)S(1)}, u32[]{:S(2)}, u32[]{:S(2)}) collective-permute-start(bf16[512,128]{1,0:T(8,128)(2,1)S(1)} %get-tuple-element.852), channel_id=1, source_target_pairs={{8,0},{16,8},{24,16},{9,1},{17,9},{25,17},{10,2},{18,10},{26,18},{... | collective-permute-start | bytes 393224 | tf_op jit(solution)/shard_map/ppermute | solution.py:249
  68.6 2.6 %collective-permute-done.13 = bf16[1,1,1,8,128]{4,3,2,1,0:T(8,128)(2,1)S(1)} collective-permute-done((bf16[1,1,1,8,128]{4,3,2,1,0:T(8,128)(2,1)S(1)}, bf16[1,1,1,8,128]{4,3,2,1,0:T(8,128)(2,1)S(1)}, u32[]{:S(2)}, u32[]{:S(2)}) %collective-permute-start.13) | collective-permute-done | bytes 2080 | tf_op jit(solution)/shard_map/ppermute | solution.py:73
  71.4 1.8 %collective-permute-done.12 = bf16[512,128]{1,0:T(8,128)(2,1)S(1)} collective-permute-done((bf16[512,128]{1,0:T(8,128)(2,1)S(1)}, bf16[512,128]{1,0:T(8,128)(2,1)S(1)}, u32[]{:S(2)}, u32[]{:S(2)}) %collective-permute-start.12) | collective-permute-done | bytes 131104 | tf_op jit(solution)/shard_map/ppermute | solution.py:249
  73.2 54.8 %while.36 = (s32[]{:T(128)}, bf16[512,128]{1,0:T(8,128)(2,1)S(1)}, bf16[1,1,1,8,128]{4,0,3,2,1:T(2,128)(2,1)S(1)}, bf16[1,1,8,8,128]{4,0,3,2,1:T(2,128)(2,1)S(1)...) while((s32[]{:T(128)}, bf16[512,128]{1,0:T(8,128)(2,1)S(1)}, ...), condition=%wide.region_6.7_spmd.clone, body=%wide.region_3.6_spmd.clone.sunk | while | flops 462854656 | bytes 5178173 | solution.py:231
  74.2 3.0 %fusion.84 = f32[1,8,8,8,128]{4,0,3,2,1:T(1,128)S(1)} fusion(bf16[3,3,3,128,128]{4,3,2,1,0:T(8,128)(2,1)S(1)} %get-tuple-element.1495, bf16[1,1,1,1,128]{4,0,3,2,1:T(2,128)(2,1)S(1)} %get-tuple-element.1316, bf16[1,1,1,8,128]{4,0,3,2,1:T(2,128)(2,1)S(1)} %get-tuple-element.1317, bf16[1,1,1,1,128]{4,0,3,2,1:T(2,128)(2,1)S(1)} %get-tuple-element.1318, ...), kind=kOutput, calls=%fused_computation.4.clone.1 | convolution fusion | flops 459896832 | bytes 1402880 | tf_op jit(solution)/shard_map/while/body/eval_jaxpr/conv_general_dilated | solution.py:108
  77.6 0.7 compare_reduce_fusion.2
  78.3 0.4 broadcast_select_fusion.132
  78.7 2.2 %collective-permute-start = (bf16[512,128]{1,0:T(8,128)(2,1)S(1)}, bf16[512,128]{1,0:T(8,128)(2,1)S(1)}, u32[]{:S(2)}, u32[]{:S(2)}) collective-permute-start(bf16[512,128]{1,0:T(8,128)(2,1)S(1)} %get-tuple-element.1345), channel_id=1, source_target_pairs={{8,0},{16,8},{24,16},{9,1},{17,9},{25,17},{10,2},{18,10},{26,18},{... | collective-permute-start | bytes 393224 | tf_op jit(solution)/shard_map/while/body/eval_jaxpr/ppermute | solution.py:224
  81.0 2.5 %collective-permute-start.3 = (bf16[1,8,1,8,128]{4,0,3,2,1:T(2,128)(2,1)S(1)}, bf16[1,8,1,8,128]{4,0,3,2,1:T(2,128)(2,1)S(1)}, u32[]{:S(2)}, u32[]{:S(2)}) collective-permute-start(bf16[1,8,1,8,128]{4,0,3,2,1:T(2,128)(2,1)S(1)} %copy.121), channel_id=1, source_target_pairs={{8,1},{9,0},{10,3},{11,2},{12,5},{13,4},{14,7},{15,6},{16,9},{17,8... | collective-permute-start | bytes 49160 | tf_op jit(solution)/shard_map/while/body/eval_jaxpr/ppermute | solution.py:73
  83.5 1.9 %collective-permute-start.2 = (bf16[1,1,8,8,128]{4,0,3,2,1:T(2,128)(2,1)S(1)}, bf16[1,1,8,8,128]{4,0,3,2,1:T(2,128)(2,1)S(1)}, u32[]{:S(2)}, u32[]{:S(2)}) collective-permute-start(bf16[1,1,8,8,128]{4,0,3,2,1:T(2,128)(2,1)S(1)} %copy.120), channel_id=1, source_target_pairs={{8,2},{9,3},{10,4},{11,5},{12,6},{13,7},{16,10},{17,11},{18,12},{1... | collective-permute-start | bytes 49160 | tf_op jit(solution)/shard_map/while/body/eval_jaxpr/ppermute | solution.py:73
  85.5 2.0 %collective-permute-start.5 = (bf16[1,1,8,8,128]{4,0,3,2,1:T(2,128)(2,1)S(1)}, bf16[1,1,8,8,128]{4,0,3,2,1:T(2,128)(2,1)S(1)}, u32[]{:S(2)}, u32[]{:S(2)}) collective-permute-start(bf16[1,1,8,8,128]{4,0,3,2,1:T(2,128)(2,1)S(1)} %copy.122), channel_id=1, source_target_pairs={{10,0},{11,1},{12,2},{13,3},{14,4},{15,5},{18,8},{19,9},{20,10},{2... | collective-permute-start | bytes 49160 | tf_op jit(solution)/shard_map/while/body/eval_jaxpr/ppermute | solution.py:73
  87.5 1.9 %collective-permute-start.1 = (bf16[1,1,1,8,128]{4,0,3,2,1:T(2,128)(2,1)S(1)}, bf16[1,1,1,8,128]{4,0,3,2,1:T(2,128)(2,1)S(1)}, u32[]{:S(2)}, u32[]{:S(2)}) collective-permute-start(bf16[1,1,1,8,128]{4,0,3,2,1:T(2,128)(2,1)S(1)} %constant_dynamic-slice_fusion.14), channel_id=1, source_target_pairs={{8,3},{9,2},{10,5},{11,4},{12,7},{13,6},{16,11},{17,10},{18,13},{1... | collective-permute-start | bytes 6152 | tf_op jit(solution)/shard_map/while/body/eval_jaxpr/ppermute | solution.py:73
  89.5 4.8 %collective-permute-done.1 = bf16[1,1,1,8,128]{4,0,3,2,1:T(2,128)(2,1)S(1)} collective-permute-done((bf16[1,1,1,8,128]{4,0,3,2,1:T(2,128)(2,1)S(1)}, bf16[1,1,1,8,128]{4,0,3,2,1:T(2,128)(2,1)S(1)}, u32[]{:S(2)}, u32[]{:S(2)}) %collective-permute-start.1) | collective-permute-done | bytes 2080 | tf_op jit(solution)/shard_map/while/body/eval_jaxpr/ppermute | solution.py:73
  94.3 1.9 %collective-permute-start.4 = (bf16[1,1,1,8,128]{4,0,3,2,1:T(2,128)(2,1)S(1)}, bf16[1,1,1,8,128]{4,0,3,2,1:T(2,128)(2,1)S(1)}, u32[]{:S(2)}, u32[]{:S(2)}) collective-permute-start(bf16[1,1,1,8,128]{4,0,3,2,1:T(2,128)(2,1)S(1)} %constant_dynamic-slice_fusion.16), channel_id=1, source_target_pairs={{10,1},{11,0},{12,3},{13,2},{14,5},{15,4},{18,9},{19,8},{20,11},{2... | collective-permute-start | bytes 6152 | tf_op jit(solution)/shard_map/while/body/eval_jaxpr/ppermute | solution.py:73
  96.2 3.9 %collective-permute-done.4 = bf16[1,1,1,8,128]{4,0,3,2,1:T(2,128)(2,1)S(1)} collective-permute-done((bf16[1,1,1,8,128]{4,0,3,2,1:T(2,128)(2,1)S(1)}, bf16[1,1,1,8,128]{4,0,3,2,1:T(2,128)(2,1)S(1)}, u32[]{:S(2)}, u32[]{:S(2)}) %collective-permute-start.4) | collective-permute-done | bytes 2080 | tf_op jit(solution)/shard_map/while/body/eval_jaxpr/ppermute | solution.py:73
  101.1 3.0 %fusion.84 = f32[1,8,8,8,128]{4,0,3,2,1:T(1,128)S(1)} fusion(bf16[3,3,3,128,128]{4,3,2,1,0:T(8,128)(2,1)S(1)} %get-tuple-element.1495, bf16[1,1,1,1,128]{4,0,3,2,1:T(2,128)(2,1)S(1)} %get-tuple-element.1316, bf16[1,1,1,8,128]{4,0,3,2,1:T(2,128)(2,1)S(1)} %get-tuple-element.1317, bf16[1,1,1,1,128]{4,0,3,2,1:T(2,128)(2,1)S(1)} %get-tuple-element.1318, ...), kind=kOutput, calls=%fused_computation.4.clone.1 | convolution fusion | flops 459896832 | bytes 1402880 | tf_op jit(solution)/shard_map/while/body/eval_jaxpr/conv_general_dilated | solution.py:108
  104.6 0.7 compare_reduce_fusion.2
  105.3 0.4 broadcast_select_fusion.132
  105.7 1.9 %collective-permute-start = (bf16[512,128]{1,0:T(8,128)(2,1)S(1)}, bf16[512,128]{1,0:T(8,128)(2,1)S(1)}, u32[]{:S(2)}, u32[]{:S(2)}) collective-permute-start(bf16[512,128]{1,0:T(8,128)(2,1)S(1)} %get-tuple-element.1345), channel_id=1, source_target_pairs={{8,0},{16,8},{24,16},{9,1},{17,9},{25,17},{10,2},{18,10},{26,18},{... | collective-permute-start | bytes 393224 | tf_op jit(solution)/shard_map/while/body/eval_jaxpr/ppermute | solution.py:224
  107.7 1.9 %collective-permute-start.3 = (bf16[1,8,1,8,128]{4,0,3,2,1:T(2,128)(2,1)S(1)}, bf16[1,8,1,8,128]{4,0,3,2,1:T(2,128)(2,1)S(1)}, u32[]{:S(2)}, u32[]{:S(2)}) collective-permute-start(bf16[1,8,1,8,128]{4,0,3,2,1:T(2,128)(2,1)S(1)} %copy.121), channel_id=1, source_target_pairs={{8,1},{9,0},{10,3},{11,2},{12,5},{13,4},{14,7},{15,6},{16,9},{17,8... | collective-permute-start | bytes 49160 | tf_op jit(solution)/shard_map/while/body/eval_jaxpr/ppermute | solution.py:73
  109.6 1.9 %collective-permute-start.2 = (bf16[1,1,8,8,128]{4,0,3,2,1:T(2,128)(2,1)S(1)}, bf16[1,1,8,8,128]{4,0,3,2,1:T(2,128)(2,1)S(1)}, u32[]{:S(2)}, u32[]{:S(2)}) collective-permute-start(bf16[1,1,8,8,128]{4,0,3,2,1:T(2,128)(2,1)S(1)} %copy.120), channel_id=1, source_target_pairs={{8,2},{9,3},{10,4},{11,5},{12,6},{13,7},{16,10},{17,11},{18,12},{1... | collective-permute-start | bytes 49160 | tf_op jit(solution)/shard_map/while/body/eval_jaxpr/ppermute | solution.py:73
  111.6 3.7 %collective-permute-start.5 = (bf16[1,1,8,8,128]{4,0,3,2,1:T(2,128)(2,1)S(1)}, bf16[1,1,8,8,128]{4,0,3,2,1:T(2,128)(2,1)S(1)}, u32[]{:S(2)}, u32[]{:S(2)}) collective-permute-start(bf16[1,1,8,8,128]{4,0,3,2,1:T(2,128)(2,1)S(1)} %copy.122), channel_id=1, source_target_pairs={{10,0},{11,1},{12,2},{13,3},{14,4},{15,5},{18,8},{19,9},{20,10},{2... | collective-permute-start | bytes 49160 | tf_op jit(solution)/shard_map/while/body/eval_jaxpr/ppermute | solution.py:73
  115.3 1.9 %collective-permute-start.1 = (bf16[1,1,1,8,128]{4,0,3,2,1:T(2,128)(2,1)S(1)}, bf16[1,1,1,8,128]{4,0,3,2,1:T(2,128)(2,1)S(1)}, u32[]{:S(2)}, u32[]{:S(2)}) collective-permute-start(bf16[1,1,1,8,128]{4,0,3,2,1:T(2,128)(2,1)S(1)} %constant_dynamic-slice_fusion.14), channel_id=1, source_target_pairs={{8,3},{9,2},{10,5},{11,4},{12,7},{13,6},{16,11},{17,10},{18,13},{1... | collective-permute-start | bytes 6152 | tf_op jit(solution)/shard_map/while/body/eval_jaxpr/ppermute | solution.py:73
  117.3 4.8 %collective-permute-done.1 = bf16[1,1,1,8,128]{4,0,3,2,1:T(2,128)(2,1)S(1)} collective-permute-done((bf16[1,1,1,8,128]{4,0,3,2,1:T(2,128)(2,1)S(1)}, bf16[1,1,1,8,128]{4,0,3,2,1:T(2,128)(2,1)S(1)}, u32[]{:S(2)}, u32[]{:S(2)}) %collective-permute-start.1) | collective-permute-done | bytes 2080 | tf_op jit(solution)/shard_map/while/body/eval_jaxpr/ppermute | solution.py:73
  122.1 1.9 %collective-permute-start.4 = (bf16[1,1,1,8,128]{4,0,3,2,1:T(2,128)(2,1)S(1)}, bf16[1,1,1,8,128]{4,0,3,2,1:T(2,128)(2,1)S(1)}, u32[]{:S(2)}, u32[]{:S(2)}) collective-permute-start(bf16[1,1,1,8,128]{4,0,3,2,1:T(2,128)(2,1)S(1)} %constant_dynamic-slice_fusion.16), channel_id=1, source_target_pairs={{10,1},{11,0},{12,3},{13,2},{14,5},{15,4},{18,9},{19,8},{20,11},{2... | collective-permute-start | bytes 6152 | tf_op jit(solution)/shard_map/while/body/eval_jaxpr/ppermute | solution.py:73
  124.0 3.9 %collective-permute-done.4 = bf16[1,1,1,8,128]{4,0,3,2,1:T(2,128)(2,1)S(1)} collective-permute-done((bf16[1,1,1,8,128]{4,0,3,2,1:T(2,128)(2,1)S(1)}, bf16[1,1,1,8,128]{4,0,3,2,1:T(2,128)(2,1)S(1)}, u32[]{:S(2)}, u32[]{:S(2)}) %collective-permute-start.4) | collective-permute-done | bytes 2080 | tf_op jit(solution)/shard_map/while/body/eval_jaxpr/ppermute | solution.py:73
  128.1 3.8 %multiply_convert_fusion = bf16[3,3,3,128,128]{4,3,2,1,0:T(8,128)(2,1)S(1)} fusion(bf16[1,10,10,10,256]{4,0,3,2,1:T(2,128)(2,1)S(1)} %copy-done.8, bf16[1,8,8,8,128]{4,3,2,1,0:T(8,128)(2,1)S(1)} %bitcast.278), kind=kOutput, calls=%fused_computation.70 | convolution fusion | flops 453869568 | bytes 1527808 | tf_op jit(solution)/shard_map/transpose | solution.py:238
  132.1 0.6 collective-permute-start.19
  132.7 1.8 %collective-permute-start.20 = (bf16[864,128]{1,0:T(8,128)(2,1)S(1)}, bf16[864,128]{1,0:T(8,128)(2,1)S(1)}, u32[]{:S(2)}, u32[]{:S(2)}) collective-permute-start(bf16[864,128]{1,0:T(8,128)(2,1)S(1)} %get-tuple-element.912), channel_id=1, source_target_pairs={{0,6},{2,0},{4,2},{6,4},{1,7},{3,1},{5,3},{7,5},{8,14},{10,8},{12,... | collective-permute-start | bytes 663560 | tf_op jit(solution)/shard_map/ppermute | solution.py:151
  135.3 3.0 %fusion.20 = f32[1,8,8,8,128]{4,0,3,2,1:T(1,128)S(1)} fusion(bf16[3,3,3,128,128]{4,3,2,1,0:T(8,128)(2,1)S(1)} %bitcast.244, bf16[1,1,1,10,128]{4,0,3,2,1:T(2,128)(2,1)S(1)} %copy.89, bf16[1,1,8,1,128]{4,0,3,2,1:T(2,128)(2,1)S(1)} %get-tuple-element.935, bf16[1,1,8,8,128]{4,0,3,2,1:T(2,128)(2,1)S(1)} %broadcast_select_fusion.44, ...), kind=kOutput, calls=%fused_computation.84 | convolution fusion | flops 456824832 | bytes 1402880 | tf_op jit(solution)/shard_map/conv_general_dilated | solution.py:108
  138.4 0.3 fusion.49
  138.7 1.6 %collective-permute-done.18 = bf16[864,128]{1,0:T(8,128)(2,1)S(1)} collective-permute-done((bf16[864,128]{1,0:T(8,128)(2,1)S(1)}, bf16[864,128]{1,0:T(8,128)(2,1)S(1)}, u32[]{:S(2)}, u32[]{:S(2)}) %collective-permute-start.18) | collective-permute-done | bytes 221216 | tf_op jit(solution)/shard_map/ppermute | solution.py:151
  140.3 3.9 %collective-permute-done.19 = bf16[864,128]{1,0:T(8,128)(2,1)S(1)} collective-permute-done((bf16[864,128]{1,0:T(8,128)(2,1)S(1)}, bf16[864,128]{1,0:T(8,128)(2,1)S(1)}, u32[]{:S(2)}, u32[]{:S(2)}) %collective-permute-start.19) | collective-permute-done | bytes 221216 | tf_op jit(solution)/shard_map/ppermute | solution.py:151
  144.3 0.6 collective-permute-start.21
  145.0 1.0 fusion.52
  146.0 0.4 collective-permute-done.21
  146.4 0.8 add_bitcast_fusion
  (230 shorter events, 7.0 us)
Async XLA Ops:
  0.6 11.3 %copy-start.10 = (bf16[1,864,128]{2,1,0:T(8,128)(2,1)S(1)}, bf16[1,864,128]{2,1,0:T(8,128)(2,1)}, u32[]{:S(2)}) copy-start(bf16[1,864,128]{2,1,0:T(8,128)(2,1)} %param.13) | copy-start | bytes 663556
  1.7 54.4 %copy-start.16 = (f32[512]{0:T(512)}, f32[512]{0:T(512)S(1)}, u32[]{:S(2)}) copy-start(f32[512]{0:T(512)S(1)} %fusion.34) | copy-start | bytes 6148
  2.7 60.0 %copy-start.14 = (f32[512]{0:T(512)}, f32[512]{0:T(512)S(1)}, u32[]{:S(2)}) copy-start(f32[512]{0:T(512)S(1)} %get-tuple-element.976) | copy-start | bytes 6148
  2.8 10.9 %copy-start.11 = (s32[1,1,1,1,27]{4,3,2,1,0:T(1,128)S(1)}, s32[1,1,1,1,27]{4,3,2,1,0:T(1,128)}, u32[]{:S(2)}) copy-start(s32[1,1,1,1,27]{4,3,2,1,0:T(1,128)} %param.10) | copy-start | bytes 328
  4.6 11.9 %copy-start.12 = (f32[1,128]{1,0:T(1,128)S(1)}, f32[1,128]{1,0:T(1,128)}, u32[]{:S(2)}) copy-start(f32[1,128]{1,0:T(1,128)} %param.12) | copy-start | bytes 1540
  5.5 28.9 %collective-permute-start.6 = (bf16[1,1,1,8,256]{4,3,2,1,0:T(8,128)(2,1)S(1)}, bf16[1,1,1,8,256]{4,3,2,1,0:T(8,128)(2,1)S(1)}, u32[]{:S(2)}, u32[]{:S(2)}) collective-permute-start(bf16[1,1,1,8,256]{4,3,2,1,0:T(8,128)(2,1)S(1)} %constant_dynamic-slice_fusion.10), channel_id=1, source_target_pairs={{0,3},{1,2},{2,5},{3,4},{4,7},{5,6},{8,11},{9,10},{10,13},{11,12},... | collective-permute-start | bytes 12296 | tf_op jit(solution)/shard_map/ppermute | solution.py:73
  9.2 26.5 %collective-permute-start.8 = (bf16[1,1,1,8,256]{4,3,2,1,0:T(8,128)(2,1)S(1)}, bf16[1,1,1,8,256]{4,3,2,1,0:T(8,128)(2,1)S(1)}, u32[]{:S(2)}, u32[]{:S(2)}) collective-permute-start(bf16[1,1,1,8,256]{4,3,2,1,0:T(8,128)(2,1)S(1)} %constant_dynamic-slice_fusion.9), channel_id=1, source_target_pairs={{2,1},{3,0},{4,3},{5,2},{6,5},{7,4},{10,9},{11,8},{12,11},{13,10},... | collective-permute-start | bytes 12296 | tf_op jit(solution)/shard_map/ppermute | solution.py:73
  12.0 30.2 %collective-permute-start.11 = (bf16[864,128]{1,0:T(8,128)(2,1)S(1)}, bf16[864,128]{1,0:T(8,128)(2,1)}, u32[]{:S(2)}, u32[]{:S(2)}) collective-permute-start(bf16[864,128]{1,0:T(8,128)(2,1)S(1)} %bitcast.260), channel_id=1, source_target_pairs={{0,4},{2,6},{4,0},{6,2},{1,5},{3,7},{5,1},{7,3},{8,12},{10,14},{12... | collective-permute-start | bytes 663560 | tf_op jit(solution)/shard_map/ppermute | solution.py:137
  12.1 4.7 %copy-start.6 = (bf16[1,1,1,512,128]{4,3,2,1,0:T(8,128)(2,1)S(1)}, bf16[1,1,1,512,128]{4,3,2,1,0:T(8,128)(2,1)}, u32[]{:S(2)}) copy-start(bf16[1,1,1,512,128]{4,3,2,1,0:T(8,128)(2,1)} %param.9) | copy-start | bytes 393220
  12.2 24.7 %collective-permute-start.9 = (bf16[992,128]{1,0:T(8,128)(2,1)S(1)}, bf16[992,128]{1,0:T(8,128)(2,1)S(1)}, u32[]{:S(2)}, u32[]{:S(2)}) collective-permute-start(bf16[992,128]{1,0:T(8,128)(2,1)S(1)} %get-tuple-element.925), channel_id=1, source_target_pairs={{0,6},{1,7},{2,0},{3,1},{4,2},{5,3},{6,4},{7,5},{8,14},{9,15},{10,... | collective-permute-start | bytes 761864 | tf_op jit(solution)/shard_map/ppermute | solution.py:73
  18.2 44.5 %copy-start.18 = (pred[512]{0:T(512)(128)(4,1)}, pred[512]{0:T(512)(128)(4,1)S(1)}, u32[]{:S(2)}) copy-start(pred[512]{0:T(512)(128)(4,1)S(1)} %fusion.59) | copy-start | bytes 1540
  34.3 7.3 %collective-permute-start.7 = (bf16[992,128]{1,0:T(8,128)(2,1)S(1)}, bf16[992,128]{1,0:T(8,128)(2,1)S(1)}, u32[]{:S(2)}, u32[]{:S(2)}) collective-permute-start(bf16[992,128]{1,0:T(8,128)(2,1)S(1)} %get-tuple-element.924), channel_id=1, source_target_pairs={{0,2},{1,3},{2,4},{3,5},{4,6},{5,7},{6,0},{7,1},{8,10},{9,11},{10,... | collective-permute-start | bytes 761864 | tf_op jit(solution)/shard_map/ppermute | solution.py:73
  34.4 2.2 %collective-permute-start.10 = (bf16[1,8,1,8,256]{4,3,2,1,0:T(8,128)(2,1)S(1)}, bf16[1,8,1,8,256]{4,3,2,1,0:T(8,128)(2,1)S(1)}, u32[]{:S(2)}, u32[]{:S(2)}) collective-permute-start(bf16[1,8,1,8,256]{4,3,2,1,0:T(8,128)(2,1)S(1)} %fusion.56), channel_id=1, source_target_pairs={{0,1},{1,0},{2,3},{3,2},{4,5},{5,4},{6,7},{7,6},{8,9},{9,8},{10,11... | collective-permute-start | bytes 98312 | tf_op jit(solution)/shard_map/ppermute | solution.py:73
  44.0 19.0 %copy-start.2 = (bf16[4,864,128]{2,1,0:T(8,128)(2,1)}, bf16[4,864,128]{2,1,0:T(8,128)(2,1)S(1)}, u32[]{:S(2)}) copy-start(bf16[4,864,128]{2,1,0:T(8,128)(2,1)S(1)} %gather_fusion) | copy-start | bytes 2654212
  45.1 2.1 %copy-start.9 = (bf16[3,3,3,128,128]{4,3,2,1,0:T(8,128)(2,1)S(1)}, bf16[3,3,3,128,128]{4,3,2,1,0:T(8,128)(2,1)}, u32[]{:S(2)}) copy-start(bf16[3,3,3,128,128]{4,3,2,1,0:T(8,128)(2,1)} %rev.3) | copy-start | bytes 2654212
  47.3 3.0 %copy-start.7 = (bf16[1,10,10,10,256]{4,0,3,2,1:T(2,128)(2,1)}, bf16[1,10,10,10,256]{4,0,3,2,1:T(2,128)(2,1)S(1)}, u32[]{:S(2)}) copy-start(bf16[1,10,10,10,256]{4,0,3,2,1:T(2,128)(2,1)S(1)} %pad_maximum_fusion) | copy-start | bytes 1536004
  47.3 3.0 %copy-start = (bf16[1,1,1,1,512,128]{5,4,3,2,1,0:T(8,128)(2,1)S(1)}, bf16[1,1,1,1,512,128]{5,4,3,2,1,0:T(8,128)(2,1)}, u32[]{:S(2)}) copy-start(bf16[1,1,1,1,512,128]{5,4,3,2,1,0:T(8,128)(2,1)} %param.8) | copy-start | bytes 393220
  51.1 20.3 %collective-permute-start.17 = (bf16[1,1,8,8,128]{4,3,2,1,0:T(8,128)(2,1)S(1)}, bf16[1,1,8,8,128]{4,3,2,1,0:T(8,128)(2,1)S(1)}, u32[]{:S(2)}, u32[]{:S(2)}) collective-permute-start(bf16[1,1,8,8,128]{4,3,2,1,0:T(8,128)(2,1)S(1)} %get-tuple-element.930), channel_id=1, source_target_pairs={{10,0},{11,1},{12,2},{13,3},{14,4},{15,5},{18,8},{19,9},{20,10},{2... | collective-permute-start | bytes 49160 | tf_op jit(solution)/shard_map/ppermute | solution.py:73
  53.1 18.2 %collective-permute-start.14 = (bf16[1,1,8,8,128]{4,3,2,1,0:T(8,128)(2,1)S(1)}, bf16[1,1,8,8,128]{4,3,2,1,0:T(8,128)(2,1)S(1)}, u32[]{:S(2)}, u32[]{:S(2)}) collective-permute-start(bf16[1,1,8,8,128]{4,3,2,1,0:T(8,128)(2,1)S(1)} %get-tuple-element.931), channel_id=1, source_target_pairs={{8,2},{9,3},{10,4},{11,5},{12,6},{13,7},{16,10},{17,11},{18,12},{1... | collective-permute-start | bytes 49160 | tf_op jit(solution)/shard_map/ppermute | solution.py:73
  56.2 15.1 %collective-permute-start.15 = (bf16[1,8,1,8,128]{4,3,2,1,0:T(8,128)(2,1)S(1)}, bf16[1,8,1,8,128]{4,3,2,1,0:T(8,128)(2,1)S(1)}, u32[]{:S(2)}, u32[]{:S(2)}) collective-permute-start(bf16[1,8,1,8,128]{4,3,2,1,0:T(8,128)(2,1)S(1)} %constant_dynamic-slice_fusion.7), channel_id=1, source_target_pairs={{8,1},{9,0},{10,3},{11,2},{12,5},{13,4},{14,7},{15,6},{16,9},{17,8... | collective-permute-start | bytes 49160 | tf_op jit(solution)/shard_map/ppermute | solution.py:73
  59.5 6.9 %collective-permute-start.16 = (bf16[1,1,1,8,128]{4,3,2,1,0:T(8,128)(2,1)S(1)}, bf16[1,1,1,8,128]{4,3,2,1,0:T(8,128)(2,1)S(1)}, u32[]{:S(2)}, u32[]{:S(2)}) collective-permute-start(bf16[1,1,1,8,128]{4,3,2,1,0:T(8,128)(2,1)S(1)} %constant_dynamic-slice_fusion.6), channel_id=1, source_target_pairs={{10,1},{11,0},{12,3},{13,2},{14,5},{15,4},{18,9},{19,8},{20,11},{2... | collective-permute-start | bytes 6152 | tf_op jit(solution)/shard_map/ppermute | solution.py:73
  64.5 6.7 %collective-permute-start.13 = (bf16[1,1,1,8,128]{4,3,2,1,0:T(8,128)(2,1)S(1)}, bf16[1,1,1,8,128]{4,3,2,1,0:T(8,128)(2,1)S(1)}, u32[]{:S(2)}, u32[]{:S(2)}) collective-permute-start(bf16[1,1,1,8,128]{4,3,2,1,0:T(8,128)(2,1)S(1)} %constant_dynamic-slice_fusion.8), channel_id=1, source_target_pairs={{8,3},{9,2},{10,5},{11,4},{12,7},{13,6},{16,11},{17,10},{18,13},{1... | collective-permute-start | bytes 6152 | tf_op jit(solution)/shard_map/ppermute | solution.py:73
  66.4 6.8 %collective-permute-start.12 = (bf16[512,128]{1,0:T(8,128)(2,1)S(1)}, bf16[512,128]{1,0:T(8,128)(2,1)S(1)}, u32[]{:S(2)}, u32[]{:S(2)}) collective-permute-start(bf16[512,128]{1,0:T(8,128)(2,1)S(1)} %get-tuple-element.852), channel_id=1, source_target_pairs={{8,0},{16,8},{24,16},{9,1},{17,9},{25,17},{10,2},{18,10},{26,18},{... | collective-permute-start | bytes 393224 | tf_op jit(solution)/shard_map/ppermute | solution.py:249
  73.2 54.8 %copy-start.8 = (bf16[1,10,10,10,256]{4,0,3,2,1:T(2,128)(2,1)S(1)}, bf16[1,10,10,10,256]{4,0,3,2,1:T(2,128)(2,1)}, u32[]{:S(2)}) copy-start(bf16[1,10,10,10,256]{4,0,3,2,1:T(2,128)(2,1)} %copy-done.7) | copy-start | bytes 1536004
  78.7 21.5 %collective-permute-start = (bf16[512,128]{1,0:T(8,128)(2,1)S(1)}, bf16[512,128]{1,0:T(8,128)(2,1)S(1)}, u32[]{:S(2)}, u32[]{:S(2)}) collective-permute-start(bf16[512,128]{1,0:T(8,128)(2,1)S(1)} %get-tuple-element.1345), channel_id=1, source_target_pairs={{8,0},{16,8},{24,16},{9,1},{17,9},{25,17},{10,2},{18,10},{26,18},{... | collective-permute-start | bytes 393224 | tf_op jit(solution)/shard_map/while/body/eval_jaxpr/ppermute | solution.py:224
  81.0 19.1 %collective-permute-start.3 = (bf16[1,8,1,8,128]{4,0,3,2,1:T(2,128)(2,1)S(1)}, bf16[1,8,1,8,128]{4,0,3,2,1:T(2,128)(2,1)S(1)}, u32[]{:S(2)}, u32[]{:S(2)}) collective-permute-start(bf16[1,8,1,8,128]{4,0,3,2,1:T(2,128)(2,1)S(1)} %copy.121), channel_id=1, source_target_pairs={{8,1},{9,0},{10,3},{11,2},{12,5},{13,4},{14,7},{15,6},{16,9},{17,8... | collective-permute-start | bytes 49160 | tf_op jit(solution)/shard_map/while/body/eval_jaxpr/ppermute | solution.py:73
  83.5 16.6 %collective-permute-start.2 = (bf16[1,1,8,8,128]{4,0,3,2,1:T(2,128)(2,1)S(1)}, bf16[1,1,8,8,128]{4,0,3,2,1:T(2,128)(2,1)S(1)}, u32[]{:S(2)}, u32[]{:S(2)}) collective-permute-start(bf16[1,1,8,8,128]{4,0,3,2,1:T(2,128)(2,1)S(1)} %copy.120), channel_id=1, source_target_pairs={{8,2},{9,3},{10,4},{11,5},{12,6},{13,7},{16,10},{17,11},{18,12},{1... | collective-permute-start | bytes 49160 | tf_op jit(solution)/shard_map/while/body/eval_jaxpr/ppermute | solution.py:73
  85.5 14.7 %collective-permute-start.5 = (bf16[1,1,8,8,128]{4,0,3,2,1:T(2,128)(2,1)S(1)}, bf16[1,1,8,8,128]{4,0,3,2,1:T(2,128)(2,1)S(1)}, u32[]{:S(2)}, u32[]{:S(2)}) collective-permute-start(bf16[1,1,8,8,128]{4,0,3,2,1:T(2,128)(2,1)S(1)} %copy.122), channel_id=1, source_target_pairs={{10,0},{11,1},{12,2},{13,3},{14,4},{15,5},{18,8},{19,9},{20,10},{2... | collective-permute-start | bytes 49160 | tf_op jit(solution)/shard_map/while/body/eval_jaxpr/ppermute | solution.py:73
  87.5 6.7 %collective-permute-start.1 = (bf16[1,1,1,8,128]{4,0,3,2,1:T(2,128)(2,1)S(1)}, bf16[1,1,1,8,128]{4,0,3,2,1:T(2,128)(2,1)S(1)}, u32[]{:S(2)}, u32[]{:S(2)}) collective-permute-start(bf16[1,1,1,8,128]{4,0,3,2,1:T(2,128)(2,1)S(1)} %constant_dynamic-slice_fusion.14), channel_id=1, source_target_pairs={{8,3},{9,2},{10,5},{11,4},{12,7},{13,6},{16,11},{17,10},{18,13},{1... | collective-permute-start | bytes 6152 | tf_op jit(solution)/shard_map/while/body/eval_jaxpr/ppermute | solution.py:73
  94.3 5.8 %collective-permute-start.4 = (bf16[1,1,1,8,128]{4,0,3,2,1:T(2,128)(2,1)S(1)}, bf16[1,1,1,8,128]{4,0,3,2,1:T(2,128)(2,1)S(1)}, u32[]{:S(2)}, u32[]{:S(2)}) collective-permute-start(bf16[1,1,1,8,128]{4,0,3,2,1:T(2,128)(2,1)S(1)} %constant_dynamic-slice_fusion.16), channel_id=1, source_target_pairs={{10,1},{11,0},{12,3},{13,2},{14,5},{15,4},{18,9},{19,8},{20,11},{2... | collective-permute-start | bytes 6152 | tf_op jit(solution)/shard_map/while/body/eval_jaxpr/ppermute | solution.py:73
  105.7 22.3 %collective-permute-start = (bf16[512,128]{1,0:T(8,128)(2,1)S(1)}, bf16[512,128]{1,0:T(8,128)(2,1)S(1)}, u32[]{:S(2)}, u32[]{:S(2)}) collective-permute-start(bf16[512,128]{1,0:T(8,128)(2,1)S(1)} %get-tuple-element.1345), channel_id=1, source_target_pairs={{8,0},{16,8},{24,16},{9,1},{17,9},{25,17},{10,2},{18,10},{26,18},{... | collective-permute-start | bytes 393224 | tf_op jit(solution)/shard_map/while/body/eval_jaxpr/ppermute | solution.py:224
  107.7 20.3 %collective-permute-start.3 = (bf16[1,8,1,8,128]{4,0,3,2,1:T(2,128)(2,1)S(1)}, bf16[1,8,1,8,128]{4,0,3,2,1:T(2,128)(2,1)S(1)}, u32[]{:S(2)}, u32[]{:S(2)}) collective-permute-start(bf16[1,8,1,8,128]{4,0,3,2,1:T(2,128)(2,1)S(1)} %copy.121), channel_id=1, source_target_pairs={{8,1},{9,0},{10,3},{11,2},{12,5},{13,4},{14,7},{15,6},{16,9},{17,8... | collective-permute-start | bytes 49160 | tf_op jit(solution)/shard_map/while/body/eval_jaxpr/ppermute | solution.py:73
  109.6 18.4 %collective-permute-start.2 = (bf16[1,1,8,8,128]{4,0,3,2,1:T(2,128)(2,1)S(1)}, bf16[1,1,8,8,128]{4,0,3,2,1:T(2,128)(2,1)S(1)}, u32[]{:S(2)}, u32[]{:S(2)}) collective-permute-start(bf16[1,1,8,8,128]{4,0,3,2,1:T(2,128)(2,1)S(1)} %copy.120), channel_id=1, source_target_pairs={{8,2},{9,3},{10,4},{11,5},{12,6},{13,7},{16,10},{17,11},{18,12},{1... | collective-permute-start | bytes 49160 | tf_op jit(solution)/shard_map/while/body/eval_jaxpr/ppermute | solution.py:73
  111.6 16.4 %collective-permute-start.5 = (bf16[1,1,8,8,128]{4,0,3,2,1:T(2,128)(2,1)S(1)}, bf16[1,1,8,8,128]{4,0,3,2,1:T(2,128)(2,1)S(1)}, u32[]{:S(2)}, u32[]{:S(2)}) collective-permute-start(bf16[1,1,8,8,128]{4,0,3,2,1:T(2,128)(2,1)S(1)} %copy.122), channel_id=1, source_target_pairs={{10,0},{11,1},{12,2},{13,3},{14,4},{15,5},{18,8},{19,9},{20,10},{2... | collective-permute-start | bytes 49160 | tf_op jit(solution)/shard_map/while/body/eval_jaxpr/ppermute | solution.py:73
  115.3 6.7 %collective-permute-start.1 = (bf16[1,1,1,8,128]{4,0,3,2,1:T(2,128)(2,1)S(1)}, bf16[1,1,1,8,128]{4,0,3,2,1:T(2,128)(2,1)S(1)}, u32[]{:S(2)}, u32[]{:S(2)}) collective-permute-start(bf16[1,1,1,8,128]{4,0,3,2,1:T(2,128)(2,1)S(1)} %constant_dynamic-slice_fusion.14), channel_id=1, source_target_pairs={{8,3},{9,2},{10,5},{11,4},{12,7},{13,6},{16,11},{17,10},{18,13},{1... | collective-permute-start | bytes 6152 | tf_op jit(solution)/shard_map/while/body/eval_jaxpr/ppermute | solution.py:73
  122.1 5.8 %collective-permute-start.4 = (bf16[1,1,1,8,128]{4,0,3,2,1:T(2,128)(2,1)S(1)}, bf16[1,1,1,8,128]{4,0,3,2,1:T(2,128)(2,1)S(1)}, u32[]{:S(2)}, u32[]{:S(2)}) collective-permute-start(bf16[1,1,1,8,128]{4,0,3,2,1:T(2,128)(2,1)S(1)} %constant_dynamic-slice_fusion.16), channel_id=1, source_target_pairs={{10,1},{11,0},{12,3},{13,2},{14,5},{15,4},{18,9},{19,8},{20,11},{2... | collective-permute-start | bytes 6152 | tf_op jit(solution)/shard_map/while/body/eval_jaxpr/ppermute | solution.py:73
  128.0 3.8 %copy-start.4 = (bf16[512,128]{1,0:T(8,128)(2,1)}, bf16[512,128]{1,0:T(8,128)(2,1)S(1)}, u32[]{:S(2)}) copy-start(bf16[512,128]{1,0:T(8,128)(2,1)S(1)} %get-tuple-element.576) | copy-start | bytes 393220
  132.0 3.2 %copy-start.3 = (bf16[4,864,128]{2,1,0:T(8,128)(2,1)S(1)}, bf16[4,864,128]{2,1,0:T(8,128)(2,1)}, u32[]{:S(2)}) copy-start(bf16[4,864,128]{2,1,0:T(8,128)(2,1)} %copy-done.2) | copy-start | bytes 2654212
  132.1 8.3 %collective-permute-start.18 = (bf16[864,128]{1,0:T(8,128)(2,1)S(1)}, bf16[864,128]{1,0:T(8,128)(2,1)S(1)}, u32[]{:S(2)}, u32[]{:S(2)}) collective-permute-start(bf16[864,128]{1,0:T(8,128)(2,1)S(1)} %get-tuple-element.911), channel_id=1, source_target_pairs={{0,2},{2,4},{4,6},{6,0},{1,3},{3,5},{5,7},{7,1},{8,10},{10,12},{12... | collective-permute-start | bytes 663560 | tf_op jit(solution)/shard_map/ppermute | solution.py:151
  132.1 12.1 %collective-permute-start.19 = (bf16[864,128]{1,0:T(8,128)(2,1)S(1)}, bf16[864,128]{1,0:T(8,128)(2,1)S(1)}, u32[]{:S(2)}, u32[]{:S(2)}) collective-permute-start(bf16[864,128]{1,0:T(8,128)(2,1)S(1)} %get-tuple-element.913), channel_id=1, source_target_pairs={{0,4},{2,6},{4,0},{6,2},{1,5},{3,7},{5,1},{7,3},{8,12},{10,14},{12... | collective-permute-start | bytes 663560 | tf_op jit(solution)/shard_map/ppermute | solution.py:151
  132.7 11.5 %collective-permute-start.20 = (bf16[864,128]{1,0:T(8,128)(2,1)S(1)}, bf16[864,128]{1,0:T(8,128)(2,1)S(1)}, u32[]{:S(2)}, u32[]{:S(2)}) collective-permute-start(bf16[864,128]{1,0:T(8,128)(2,1)S(1)} %get-tuple-element.912), channel_id=1, source_target_pairs={{0,6},{2,0},{4,2},{6,4},{1,7},{3,1},{5,3},{7,5},{8,14},{10,8},{12,... | collective-permute-start | bytes 663560 | tf_op jit(solution)/shard_map/ppermute | solution.py:151
  135.3 3.1 %copy-start.1 = (bf16[1,1,1,1,512,128]{5,4,3,2,1,0:T(8,128)(2,1)S(1)}, bf16[1,1,1,1,512,128]{5,4,3,2,1,0:T(8,128)(2,1)}, u32[]{:S(2)}) copy-start(bf16[1,1,1,1,512,128]{5,4,3,2,1,0:T(8,128)(2,1)} %param.8) | copy-start | bytes 393220
  135.3 3.1 %copy-start.13 = (f32[1,128]{1,0:T(1,128)S(1)}, f32[1,128]{1,0:T(1,128)}, u32[]{:S(2)}) copy-start(f32[1,128]{1,0:T(1,128)} %param.12) | copy-start | bytes 1540
  135.3 3.1 %copy-start.15 = (f32[512]{0:T(512)S(1)}, f32[512]{0:T(512)}, u32[]{:S(2)}) copy-start(f32[512]{0:T(512)} %copy-done.14) | copy-start | bytes 6148
  138.4 6.6 %copy-start.17 = (f32[512]{0:T(512)S(1)}, f32[512]{0:T(512)}, u32[]{:S(2)}) copy-start(f32[512]{0:T(512)} %copy-done.16) | copy-start | bytes 6148
  138.4 6.6 %copy-start.5 = (bf16[512,128]{1,0:T(8,128)(2,1)S(1)}, bf16[512,128]{1,0:T(8,128)(2,1)}, u32[]{:S(2)}) copy-start(bf16[512,128]{1,0:T(8,128)(2,1)} %copy-done.4) | copy-start | bytes 393220
  138.4 6.6 %copy-start.19 = (pred[512]{0:T(512)(128)(4,1)S(1)}, pred[512]{0:T(512)(128)(4,1)}, u32[]{:S(2)}) copy-start(pred[512]{0:T(512)(128)(4,1)} %copy-done.18) | copy-start | bytes 1540
  144.3 2.0 %collective-permute-start.21 = (f32[864,128]{1,0:T(8,128)S(1)}, f32[864,128]{1,0:T(8,128)S(1)}, u32[]{:S(2)}, u32[]{:S(2)}) collective-permute-start(f32[864,128]{1,0:T(8,128)S(1)} %convert_add_fusion), channel_id=1, source_target_pairs={{0,1},{1,0},{2,3},{3,2},{4,5},{5,4},{6,7},{7,6},{8,9},{9,8},{10,11... | collective-permute-start | bytes 1327112 | tf_op jit(solution)/shard_map/ppermute | solution.py:254

commit v12 on v7

--- a/solution.py
+++ b/solution.py
@@ -52,7 +52,7 @@
             rows_y.append(jnp.concatenate(parts_z, axis=3))
         slabs_x.append(jnp.concatenate(rows_y, axis=2))
     if split:
-        slabs_x[0], slabs_x[2] = lax.optimization_barrier((slabs_x[0], slabs_x[2]))
+        slabs_x = list(lax.optimization_barrier(tuple(slabs_x)))
     return jnp.concatenate(slabs_x, axis=1)
 
 

time: 132 us -> 141 us (1.068)
  local copies, waits for them, and re-layouts: 6.65 us -> 10.7 us
  starting transfers between devices: 50.8 us -> 54.7 us
    ppermute x20, starting transfers between devices: 41.4 us -> 44.9 us  [send(): return lax.ppermute(piece, axes, route)]
    unnamed x33 -> x31, local copies, waits for them, and re-layouts: 0.47 us -> 3.01 us
    ppermute x3, waiting for transfers between devices: 7.33 us -> 4.98 us  [scattered_sum(): lax.ppermute(piece, axis, [(i, (i + step) % count) for i in range(count)])]
    ppermute x20, waiting for transfers between devices: 14.5 us -> 16.9 us  [send(): return lax.ppermute(piece, axes, route)]
    concatenate x1 -> x0, other arithmetic: 2.11 us -> none  [assemble(): return jnp.concatenate(slabs_x, axis=1)]
    concatenate x8 -> x9, other arithmetic: 0.55 us -> 2.04 us  [assemble(): slabs_x.append(jnp.concatenate(rows_y, axis=2))]
  transfers between devices with their start and end apart: 28 -> 28, of which waited for: 8 -> 8; matrix products, arithmetic and copies ran while one was open for 12% -> 13% of each run, Pallas kernels for 0% -> 0%
where the time goes in v12:
time: 141 us; the launch traced here: 139 us
  starting transfers between devices  54.7 us (39%)
  waiting for transfers between devices  22.2 us (16%)
  between operations  20 us (14%)
  matrix products  16.6 us (12%)
  other arithmetic  14.4 us (10%)
  local copies, waits for them, and re-layouts  10.7 us (8%)
    ppermute x20, starting transfers between devices, send(): return lax.ppermute(piece, axes, route)  44.9 us
    ppermute x20, waiting for transfers between devices, send(): return lax.ppermute(piece, axes, route)  16.9 us
    conv_general_dilated x4, matrix products, conv_data(): lax.conv_general_dilated(padded, filters, (1, 1, 1), 'VALID', dimension_n...  12.8 us
    ppermute x3, starting transfers between devices, shards(): centre = lax.ppermute(result, 'pipe', down)  5.76 us
    ppermute x3, waiting for transfers between devices, scattered_sum(): lax.ppermute(piece, axis, [(i, (i + step) % count) for i in range(count)])  4.98 us
    transpose x1, matrix products, shards(): per_tap.transpose(1, 2, 3, 0, 4).reshape(taps * channels, channels)  3.76 us
    unnamed x31, local copies, waits for them, and re-layouts  3.01 us
  transfers between devices with their start and end apart: 28, of which 8 were waited for; matrix products, arithmetic and copies ran while one was open for 13% of the time, Pallas kernels for 0%

profile of v12, /device:TPU:21, one launch (start us, length us, event | category | flops | bytes accessed | tf_op | source)
XLA Modules:
  0.0 138.6 jit_solution(596781900399943905)
XLA Ops:
  0.6 1.1 fusion.25
  1.7 0.9 convert_element_type.160
  3.5 1.0 broadcast_select_fusion.12
  4.5 0.8 multiply_convert_fusion.2
  5.4 3.6 %collective-permute-start.3 = (bf16[1,1,1,8,256]{4,3,2,1,0:T(8,128)(2,1)S(1)}, bf16[1,1,1,8,256]{4,3,2,1,0:T(8,128)(2,1)S(1)}, u32[]{:S(2)}, u32[]{:S(2)}) collective-permute-start(bf16[1,1,1,8,256]{4,3,2,1,0:T(8,128)(2,1)S(1)} %fusion.59), channel_id=1, source_target_pairs={{2,1},{3,0},{4,3},{5,2},{6,5},{7,4},{10,9},{11,8},{12,11},{13,10},... | collective-permute-start | bytes 12296 | tf_op jit(solution)/shard_map/ppermute | solution.py:73
  9.1 1.9 %collective-permute-start = (bf16[1,1,1,8,256]{4,3,2,1,0:T(8,128)(2,1)S(1)}, bf16[1,1,1,8,256]{4,3,2,1,0:T(8,128)(2,1)S(1)}, u32[]{:S(2)}, u32[]{:S(2)}) collective-permute-start(bf16[1,1,1,8,256]{4,3,2,1,0:T(8,128)(2,1)S(1)} %constant_dynamic-slice_fusion.14), channel_id=1, source_target_pairs={{0,3},{1,2},{2,5},{3,4},{4,7},{5,6},{8,11},{9,10},{10,13},{11,12},... | collective-permute-start | bytes 12296 | tf_op jit(solution)/shard_map/ppermute | solution.py:73
  11.0 0.3 collective-permute-start.5
  11.4 1.9 %collective-permute-start.4 = (bf16[992,128]{1,0:T(8,128)(2,1)S(1)}, bf16[992,128]{1,0:T(8,128)(2,1)}, u32[]{:S(2)}, u32[]{:S(2)}) collective-permute-start(bf16[992,128]{1,0:T(8,128)(2,1)S(1)} %get-tuple-element.62), channel_id=1, source_target_pairs={{0,6},{1,7},{2,0},{3,1},{4,2},{5,3},{6,4},{7,5},{8,14},{9,15},{10,... | collective-permute-start | bytes 761864 | tf_op jit(solution)/shard_map/ppermute | solution.py:73
  13.3 1.0 collective-permute-start.2
  14.4 0.7 fusion.76
  15.1 0.7 fusion.77
  18.2 0.6 scatter_custom_fusion
  18.8 0.4 copy_dynamic-update-slice_fusion
  19.2 0.6 broadcast_select_fusion
  35.1 0.3 collective-permute-start.1
  36.0 1.5 %pad_maximum_fusion.1 = bf16[1,8,10,10,256]{4,0,3,2,1:T(2,128)(2,1)S(1)} fusion(bf16[1,8,1,10,256]{4,0,3,2,1:T(2,128)(2,1)S(1)} %copy.42, bf16[1,8,8,1,256]{4,0,3,2,1:T(2,128)(2,1)S(1)} %get-tuple-element.55, bf16[1,8,8,8,256]{4,0,3,2,1:T(2,128)(2,1)S(1)} %broadcast_select_fusion, bf16[1,8,8,1,256]{4,0,3,2,1:T(2,128)(2,1)S(1)} %get-tuple-element.54, ...), kind=kLoop, calls=%fused_computation.5 | loop fusion | flops 819200 | bytes 819200 | tf_op jit(solution)/shard_map/concatenate | solution.py:53
  37.5 0.8 broadcast_select_fusion.15
  38.4 5.4 %collective-permute-done.1 = bf16[992,128]{1,0:T(8,128)(2,1)S(1)} collective-permute-done((bf16[992,128]{1,0:T(8,128)(2,1)S(1)}, bf16[992,128]{1,0:T(8,128)(2,1)S(1)}, u32[]{:S(2)}, u32[]{:S(2)}) %collective-permute-start.1) | collective-permute-done | bytes 253984 | tf_op jit(solution)/shard_map/ppermute | solution.py:73
  44.3 0.8 constant_dynamic-update-slice_fusion.2
  45.0 0.9 slice_bitcast_fusion
  46.0 1.0 pad_maximum_fusion
  47.1 0.7 gather_fusion
  47.8 1.0 rev.3
  48.8 1.8 %constant_dynamic-update-slice_fusion.1 = bf16[1,10,10,10,256]{4,0,3,2,1:T(2,128)(2,1)} fusion(bf16[1,10,10,10,256]{4,0,3,2,1:T(2,128)(2,1)} %constant_dynamic-update-slice_fusion.2, bf16[1,8,10,10,256]{4,0,3,2,1:T(2,128)(2,1)S(1)} %pad_maximum_fusion.1), kind=kLoop, calls=%fused_computation.176 | loop fusion | bytes 1228800
  50.6 0.7 constant_dynamic-update-slice_fusion
  51.3 4.0 %fusion.1 = f32[1,8,8,8,128]{4,0,3,2,1:T(1,128)S(1)} fusion(bf16[3,3,3,128,128]{4,3,2,1,0:T(8,128)(2,1)S(1)} %copy-done.2, bf16[1,10,10,10,256]{4,0,3,2,1:T(2,128)(2,1)} %constant_dynamic-update-slice_fusion), kind=kOutput, calls=%fused_computation.10 | convolution fusion | flops 452984832 | bytes 1658880 | tf_op jit(solution)/shard_map/conv_general_dilated | solution.py:108
  55.4 0.3 fusion.47
  56.1 1.9 %collective-permute-start.8 = (bf16[1,1,8,8,128]{4,3,2,1,0:T(8,128)(2,1)S(1)}, bf16[1,1,8,8,128]{4,3,2,1,0:T(8,128)(2,1)S(1)}, u32[]{:S(2)}, u32[]{:S(2)}) collective-permute-start(bf16[1,1,8,8,128]{4,3,2,1,0:T(8,128)(2,1)S(1)} %get-tuple-element.74), channel_id=1, source_target_pairs={{8,2},{9,3},{10,4},{11,5},{12,6},{13,7},{16,10},{17,11},{18,12},{1... | collective-permute-start | bytes 49160 | tf_op jit(solution)/shard_map/ppermute | solution.py:73
  58.1 4.0 %collective-permute-start.11 = (bf16[1,1,8,8,128]{4,3,2,1,0:T(8,128)(2,1)S(1)}, bf16[1,1,8,8,128]{4,3,2,1,0:T(8,128)(2,1)S(1)}, u32[]{:S(2)}, u32[]{:S(2)}) collective-permute-start(bf16[1,1,8,8,128]{4,3,2,1,0:T(8,128)(2,1)S(1)} %get-tuple-element.75), channel_id=1, source_target_pairs={{10,0},{11,1},{12,2},{13,3},{14,4},{15,5},{18,8},{19,9},{20,10},{2... | collective-permute-start | bytes 49160 | tf_op jit(solution)/shard_map/ppermute | solution.py:73
  62.2 1.9 %collective-permute-start.7 = (bf16[1,1,1,8,128]{4,3,2,1,0:T(8,128)(2,1)S(1)}, bf16[1,1,1,8,128]{4,3,2,1,0:T(8,128)(2,1)S(1)}, u32[]{:S(2)}, u32[]{:S(2)}) collective-permute-start(bf16[1,1,1,8,128]{4,3,2,1,0:T(8,128)(2,1)S(1)} %constant_dynamic-slice_fusion.11), channel_id=1, source_target_pairs={{8,3},{9,2},{10,5},{11,4},{12,7},{13,6},{16,11},{17,10},{18,13},{1... | collective-permute-start | bytes 6152 | tf_op jit(solution)/shard_map/ppermute | solution.py:73
  64.1 1.9 %collective-permute-start.9 = (bf16[1,8,1,8,128]{4,3,2,1,0:T(8,128)(2,1)S(1)}, bf16[1,8,1,8,128]{4,3,2,1,0:T(8,128)(2,1)S(1)}, u32[]{:S(2)}, u32[]{:S(2)}) collective-permute-start(bf16[1,8,1,8,128]{4,3,2,1,0:T(8,128)(2,1)S(1)} %constant_dynamic-slice_fusion.10), channel_id=1, source_target_pairs={{8,1},{9,0},{10,3},{11,2},{12,5},{13,4},{14,7},{15,6},{16,9},{17,8... | collective-permute-start | bytes 49160 | tf_op jit(solution)/shard_map/ppermute | solution.py:73
  66.3 1.9 %collective-permute-start.6 = (bf16[512,128]{1,0:T(8,128)(2,1)S(1)}, bf16[512,128]{1,0:T(8,128)(2,1)S(1)}, u32[]{:S(2)}, u32[]{:S(2)}) collective-permute-start(bf16[512,128]{1,0:T(8,128)(2,1)S(1)} %fusion.8), channel_id=1, source_target_pairs={{8,0},{16,8},{24,16},{9,1},{17,9},{25,17},{10,2},{18,10},{26,18},{... | collective-permute-start | bytes 393224 | tf_op jit(solution)/shard_map/ppermute | solution.py:229
  68.3 0.6 collective-permute-done.7
  68.9 2.5 %collective-permute-start.10 = (bf16[1,1,1,8,128]{4,3,2,1,0:T(8,128)(2,1)S(1)}, bf16[1,1,1,8,128]{4,3,2,1,0:T(8,128)(2,1)S(1)}, u32[]{:S(2)}, u32[]{:S(2)}) collective-permute-start(bf16[1,1,1,8,128]{4,3,2,1,0:T(8,128)(2,1)S(1)} %constant_dynamic-slice_fusion.9), channel_id=1, source_target_pairs={{10,1},{11,0},{12,3},{13,2},{14,5},{15,4},{18,9},{19,8},{20,11},{2... | collective-permute-start | bytes 6152 | tf_op jit(solution)/shard_map/ppermute | solution.py:73
  71.4 3.3 %collective-permute-done.10 = bf16[1,1,1,8,128]{4,3,2,1,0:T(8,128)(2,1)S(1)} collective-permute-done((bf16[1,1,1,8,128]{4,3,2,1,0:T(8,128)(2,1)S(1)}, bf16[1,1,1,8,128]{4,3,2,1,0:T(8,128)(2,1)S(1)}, u32[]{:S(2)}, u32[]{:S(2)}) %collective-permute-start.10) | collective-permute-done | bytes 2080 | tf_op jit(solution)/shard_map/ppermute | solution.py:73
  75.6 2.9 %fusion.5 = f32[1,8,8,8,128]{4,0,3,2,1:T(1,128)S(1)} fusion(bf16[3,3,3,128,128]{4,3,2,1,0:T(8,128)(2,1)S(1)} %bitcast.208, bf16[1,1,10,10,128]{4,0,3,2,1:T(2,128)(2,1)S(1)} %copy.56, bf16[1,8,1,10,128]{4,0,3,2,1:T(2,128)(2,1)S(1)} %copy.54, bf16[1,8,8,1,128]{4,0,3,2,1:T(2,128)(2,1)S(1)} %slice_bitcast_fusion.6, bf16[1,8,8,8,128]{4,0,3,2,1:T(2,128)(2,1)S(1)} %copy.52, ...), kind=kOutput, calls=%fused_computation.14 | convolution fusion | flops 454776832 | bytes 1402880 | tf_op jit(solution)/shard_map/conv_general_dilated | solution.py:108
  78.6 0.3 fusion.48
  78.9 0.3 fusion.18
  79.2 1.9 %collective-permute-start.14 = (bf16[1,1,8,8,128]{4,3,2,1,0:T(8,128)(2,1)S(1)}, bf16[1,1,8,8,128]{4,3,2,1,0:T(8,128)(2,1)S(1)}, u32[]{:S(2)}, u32[]{:S(2)}) collective-permute-start(bf16[1,1,8,8,128]{4,3,2,1,0:T(8,128)(2,1)S(1)} %get-tuple-element.69), channel_id=1, source_target_pairs={{8,2},{9,3},{10,4},{11,5},{12,6},{13,7},{16,10},{17,11},{18,12},{1... | collective-permute-start | bytes 49160 | tf_op jit(solution)/shard_map/ppermute | solution.py:73
  81.2 1.9 %collective-permute-start.12 = (bf16[512,128]{1,0:T(8,128)(2,1)S(1)}, bf16[512,128]{1,0:T(8,128)(2,1)S(1)}, u32[]{:S(2)}, u32[]{:S(2)}) collective-permute-start(bf16[512,128]{1,0:T(8,128)(2,1)S(1)} %fusion.18), channel_id=1, source_target_pairs={{8,0},{16,8},{24,16},{9,1},{17,9},{25,17},{10,2},{18,10},{26,18},{... | collective-permute-start | bytes 393224 | tf_op jit(solution)/shard_map/ppermute | solution.py:229
  83.1 1.9 %collective-permute-start.13 = (bf16[1,1,1,8,128]{4,3,2,1,0:T(8,128)(2,1)S(1)}, bf16[1,1,1,8,128]{4,3,2,1,0:T(8,128)(2,1)S(1)}, u32[]{:S(2)}, u32[]{:S(2)}) collective-permute-start(bf16[1,1,1,8,128]{4,3,2,1,0:T(8,128)(2,1)S(1)} %constant_dynamic-slice_fusion.8), channel_id=1, source_target_pairs={{8,3},{9,2},{10,5},{11,4},{12,7},{13,6},{16,11},{17,10},{18,13},{1... | collective-permute-start | bytes 6152 | tf_op jit(solution)/shard_map/ppermute | solution.py:73
  85.1 3.8 %collective-permute-start.17 = (bf16[1,1,8,8,128]{4,3,2,1,0:T(8,128)(2,1)S(1)}, bf16[1,1,8,8,128]{4,3,2,1,0:T(8,128)(2,1)S(1)}, u32[]{:S(2)}, u32[]{:S(2)}) collective-permute-start(bf16[1,1,8,8,128]{4,3,2,1,0:T(8,128)(2,1)S(1)} %get-tuple-element.70), channel_id=1, source_target_pairs={{10,0},{11,1},{12,2},{13,3},{14,4},{15,5},{18,8},{19,9},{20,10},{2... | collective-permute-start | bytes 49160 | tf_op jit(solution)/shard_map/ppermute | solution.py:73
  88.9 1.9 %collective-permute-start.15 = (bf16[1,8,1,8,128]{4,3,2,1,0:T(8,128)(2,1)S(1)}, bf16[1,8,1,8,128]{4,3,2,1,0:T(8,128)(2,1)S(1)}, u32[]{:S(2)}, u32[]{:S(2)}) collective-permute-start(bf16[1,8,1,8,128]{4,3,2,1,0:T(8,128)(2,1)S(1)} %constant_dynamic-slice_fusion.7), channel_id=1, source_target_pairs={{8,1},{9,0},{10,3},{11,2},{12,5},{13,4},{14,7},{15,6},{16,9},{17,8... | collective-permute-start | bytes 49160 | tf_op jit(solution)/shard_map/ppermute | solution.py:73
  90.8 2.7 %collective-permute-start.16 = (bf16[1,1,1,8,128]{4,3,2,1,0:T(8,128)(2,1)S(1)}, bf16[1,1,1,8,128]{4,3,2,1,0:T(8,128)(2,1)S(1)}, u32[]{:S(2)}, u32[]{:S(2)}) collective-permute-start(bf16[1,1,1,8,128]{4,3,2,1,0:T(8,128)(2,1)S(1)} %constant_dynamic-slice_fusion.6), channel_id=1, source_target_pairs={{10,1},{11,0},{12,3},{13,2},{14,5},{15,4},{18,9},{19,8},{20,11},{2... | collective-permute-start | bytes 6152 | tf_op jit(solution)/shard_map/ppermute | solution.py:73
  93.6 3.0 %collective-permute-done.16 = bf16[1,1,1,8,128]{4,3,2,1,0:T(8,128)(2,1)S(1)} collective-permute-done((bf16[1,1,1,8,128]{4,3,2,1,0:T(8,128)(2,1)S(1)}, bf16[1,1,1,8,128]{4,3,2,1,0:T(8,128)(2,1)S(1)}, u32[]{:S(2)}, u32[]{:S(2)}) %collective-permute-start.16) | collective-permute-done | bytes 2080 | tf_op jit(solution)/shard_map/ppermute | solution.py:73
  97.6 2.9 %fusion.4 = f32[1,8,8,8,128]{4,0,3,2,1:T(1,128)S(1)} fusion(bf16[3,3,3,128,128]{4,3,2,1,0:T(8,128)(2,1)S(1)} %bitcast.209, bf16[1,1,10,10,128]{4,0,3,2,1:T(2,128)(2,1)S(1)} %copy.63, bf16[1,8,1,10,128]{4,0,3,2,1:T(2,128)(2,1)S(1)} %copy.61, bf16[1,8,8,1,128]{4,0,3,2,1:T(2,128)(2,1)S(1)} %slice_bitcast_fusion.4, bf16[1,8,8,8,128]{4,0,3,2,1:T(2,128)(2,1)S(1)} %copy.59, ...), kind=kOutput, calls=%fused_computation.13 | convolution fusion | flops 454776832 | bytes 1402880 | tf_op jit(solution)/shard_map/conv_general_dilated | solution.py:108
  100.5 0.3 fusion.49
  101.2 1.9 %collective-permute-start.18 = (bf16[512,128]{1,0:T(8,128)(2,1)S(1)}, bf16[512,128]{1,0:T(8,128)(2,1)S(1)}, u32[]{:S(2)}, u32[]{:S(2)}) collective-permute-start(bf16[512,128]{1,0:T(8,128)(2,1)S(1)} %fusion.21), channel_id=1, source_target_pairs={{8,0},{16,8},{24,16},{9,1},{17,9},{25,17},{10,2},{18,10},{26,18},{... | collective-permute-start | bytes 393224 | tf_op jit(solution)/shard_map/ppermute | solution.py:229
  103.2 3.6 %collective-permute-start.22 = (bf16[1,1,1,8,128]{4,3,2,1,0:T(8,128)(2,1)S(1)}, bf16[1,1,1,8,128]{4,3,2,1,0:T(8,128)(2,1)S(1)}, u32[]{:S(2)}, u32[]{:S(2)}) collective-permute-start(bf16[1,1,1,8,128]{4,3,2,1,0:T(8,128)(2,1)S(1)} %constant_dynamic-slice_fusion.3), channel_id=1, source_target_pairs={{10,1},{11,0},{12,3},{13,2},{14,5},{15,4},{18,9},{19,8},{20,11},{2... | collective-permute-start | bytes 6152 | tf_op jit(solution)/shard_map/ppermute | solution.py:73
  106.8 1.9 %collective-permute-start.20 = (bf16[1,1,8,8,128]{4,3,2,1,0:T(8,128)(2,1)S(1)}, bf16[1,1,8,8,128]{4,3,2,1,0:T(8,128)(2,1)S(1)}, u32[]{:S(2)}, u32[]{:S(2)}) collective-permute-start(bf16[1,1,8,8,128]{4,3,2,1,0:T(8,128)(2,1)S(1)} %get-tuple-element.68), channel_id=1, source_target_pairs={{8,2},{9,3},{10,4},{11,5},{12,6},{13,7},{16,10},{17,11},{18,12},{1... | collective-permute-start | bytes 49160 | tf_op jit(solution)/shard_map/ppermute | solution.py:73
  108.8 1.9 %collective-permute-start.23 = (bf16[1,1,8,8,128]{4,3,2,1,0:T(8,128)(2,1)S(1)}, bf16[1,1,8,8,128]{4,3,2,1,0:T(8,128)(2,1)S(1)}, u32[]{:S(2)}, u32[]{:S(2)}) collective-permute-start(bf16[1,1,8,8,128]{4,3,2,1,0:T(8,128)(2,1)S(1)} %get-tuple-element.67), channel_id=1, source_target_pairs={{10,0},{11,1},{12,2},{13,3},{14,4},{15,5},{18,8},{19,9},{20,10},{2... | collective-permute-start | bytes 49160 | tf_op jit(solution)/shard_map/ppermute | solution.py:73
  110.7 1.9 %collective-permute-start.21 = (bf16[1,8,1,8,128]{4,3,2,1,0:T(8,128)(2,1)S(1)}, bf16[1,8,1,8,128]{4,3,2,1,0:T(8,128)(2,1)S(1)}, u32[]{:S(2)}, u32[]{:S(2)}) collective-permute-start(bf16[1,8,1,8,128]{4,3,2,1,0:T(8,128)(2,1)S(1)} %constant_dynamic-slice_fusion.4), channel_id=1, source_target_pairs={{8,1},{9,0},{10,3},{11,2},{12,5},{13,4},{14,7},{15,6},{16,9},{17,8... | collective-permute-start | bytes 49160 | tf_op jit(solution)/shard_map/ppermute | solution.py:73
  112.6 2.1 %collective-permute-start.19 = (bf16[1,1,1,8,128]{4,3,2,1,0:T(8,128)(2,1)S(1)}, bf16[1,1,1,8,128]{4,3,2,1,0:T(8,128)(2,1)S(1)}, u32[]{:S(2)}, u32[]{:S(2)}) collective-permute-start(bf16[1,1,1,8,128]{4,3,2,1,0:T(8,128)(2,1)S(1)} %constant_dynamic-slice_fusion.5), channel_id=1, source_target_pairs={{8,3},{9,2},{10,5},{11,4},{12,7},{13,6},{16,11},{17,10},{18,13},{1... | collective-permute-start | bytes 6152 | tf_op jit(solution)/shard_map/ppermute | solution.py:73
  114.8 4.5 %collective-permute-done.19 = bf16[1,1,1,8,128]{4,3,2,1,0:T(8,128)(2,1)S(1)} collective-permute-done((bf16[1,1,1,8,128]{4,3,2,1,0:T(8,128)(2,1)S(1)}, bf16[1,1,1,8,128]{4,3,2,1,0:T(8,128)(2,1)S(1)}, u32[]{:S(2)}, u32[]{:S(2)}) %collective-permute-start.19) | collective-permute-done | bytes 2080 | tf_op jit(solution)/shard_map/ppermute | solution.py:73
  119.5 3.8 %multiply_convert_fusion = bf16[3,3,3,128,128]{4,3,2,1,0:T(8,128)(2,1)S(1)} fusion(bf16[1,10,10,10,256]{4,0,3,2,1:T(2,128)(2,1)S(1)} %copy-done.10, bf16[1,8,8,8,128]{4,3,2,1,0:T(8,128)(2,1)S(1)} %bitcast.242), kind=kOutput, calls=%fused_computation.2 | convolution fusion | flops 453869568 | bytes 1527808 | tf_op jit(solution)/shard_map/transpose | solution.py:217
  123.7 2.3 %collective-permute-start.26 = (bf16[864,128]{1,0:T(8,128)(2,1)S(1)}, bf16[864,128]{1,0:T(8,128)(2,1)S(1)}, u32[]{:S(2)}, u32[]{:S(2)}) collective-permute-start(bf16[864,128]{1,0:T(8,128)(2,1)S(1)} %get-tuple-element.52), channel_id=1, source_target_pairs={{0,6},{2,0},{4,2},{6,4},{1,7},{3,1},{5,3},{7,5},{8,14},{10,8},{12,... | collective-permute-start | bytes 663560 | tf_op jit(solution)/shard_map/ppermute | solution.py:151
  126.7 3.0 %fusion.3 = f32[1,8,8,8,128]{4,0,3,2,1:T(1,128)S(1)} fusion(bf16[3,3,3,128,128]{4,3,2,1,0:T(8,128)(2,1)S(1)} %bitcast.210, bf16[1,1,10,10,128]{4,0,3,2,1:T(2,128)(2,1)S(1)} %copy.71, bf16[1,8,1,10,128]{4,0,3,2,1:T(2,128)(2,1)S(1)} %copy.69, bf16[1,8,8,1,128]{4,0,3,2,1:T(2,128)(2,1)S(1)} %slice_bitcast_fusion.2, bf16[1,8,8,8,128]{4,0,3,2,1:T(2,128)(2,1)S(1)} %copy.67, ...), kind=kOutput, calls=%fused_computation.12 | convolution fusion | flops 454776832 | bytes 1402880 | tf_op jit(solution)/shard_map/conv_general_dilated | solution.py:108
  129.7 0.3 fusion.50
  130.0 1.1 collective-permute-done.24
  131.1 3.9 %collective-permute-done.25 = bf16[864,128]{1,0:T(8,128)(2,1)S(1)} collective-permute-done((bf16[864,128]{1,0:T(8,128)(2,1)S(1)}, bf16[864,128]{1,0:T(8,128)(2,1)S(1)}, u32[]{:S(2)}, u32[]{:S(2)}) %collective-permute-start.25) | collective-permute-done | bytes 221216 | tf_op jit(solution)/shard_map/ppermute | solution.py:151
  135.1 1.3 collective-permute-start.27
  136.4 1.0 fusion.53
  137.5 0.4 collective-permute-done.27
  137.8 0.8 add_bitcast_fusion
  (215 shorter events, 5.7 us)
Async XLA Ops:
  0.6 10.4 %copy-start.3 = (bf16[1,864,128]{2,1,0:T(8,128)(2,1)S(1)}, bf16[1,864,128]{2,1,0:T(8,128)(2,1)}, u32[]{:S(2)}) copy-start(bf16[1,864,128]{2,1,0:T(8,128)(2,1)} %param.11) | copy-start | bytes 663556
  5.3 9.0 %copy-start.8 = (s32[1,1,1,1,27]{4,3,2,1,0:T(1,128)S(1)}, s32[1,1,1,1,27]{4,3,2,1,0:T(1,128)}, u32[]{:S(2)}) copy-start(s32[1,1,1,1,27]{4,3,2,1,0:T(1,128)} %param.8) | copy-start | bytes 328
  5.4 10.4 %copy-start.9 = (f32[1,128]{1,0:T(1,128)S(1)}, f32[1,128]{1,0:T(1,128)}, u32[]{:S(2)}) copy-start(f32[1,128]{1,0:T(1,128)} %param.10) | copy-start | bytes 1540
  5.4 29.7 %collective-permute-start.3 = (bf16[1,1,1,8,256]{4,3,2,1,0:T(8,128)(2,1)S(1)}, bf16[1,1,1,8,256]{4,3,2,1,0:T(8,128)(2,1)S(1)}, u32[]{:S(2)}, u32[]{:S(2)}) collective-permute-start(bf16[1,1,1,8,256]{4,3,2,1,0:T(8,128)(2,1)S(1)} %fusion.59), channel_id=1, source_target_pairs={{2,1},{3,0},{4,3},{5,2},{6,5},{7,4},{10,9},{11,8},{12,11},{13,10},... | collective-permute-start | bytes 12296 | tf_op jit(solution)/shard_map/ppermute | solution.py:73
  9.1 26.4 %collective-permute-start = (bf16[1,1,1,8,256]{4,3,2,1,0:T(8,128)(2,1)S(1)}, bf16[1,1,1,8,256]{4,3,2,1,0:T(8,128)(2,1)S(1)}, u32[]{:S(2)}, u32[]{:S(2)}) collective-permute-start(bf16[1,1,1,8,256]{4,3,2,1,0:T(8,128)(2,1)S(1)} %constant_dynamic-slice_fusion.14), channel_id=1, source_target_pairs={{0,3},{1,2},{2,5},{3,4},{4,7},{5,6},{8,11},{9,10},{10,13},{11,12},... | collective-permute-start | bytes 12296 | tf_op jit(solution)/shard_map/ppermute | solution.py:73
  11.0 35.0 %collective-permute-start.5 = (bf16[864,128]{1,0:T(8,128)(2,1)S(1)}, bf16[864,128]{1,0:T(8,128)(2,1)}, u32[]{:S(2)}, u32[]{:S(2)}) collective-permute-start(bf16[864,128]{1,0:T(8,128)(2,1)S(1)} %bitcast.223), channel_id=1, source_target_pairs={{0,4},{2,6},{4,0},{6,2},{1,5},{3,7},{5,1},{7,3},{8,12},{10,14},{12... | collective-permute-start | bytes 663560 | tf_op jit(solution)/shard_map/ppermute | solution.py:137
  11.4 4.8 %copy-start.1 = (bf16[1,1,1,512,128]{4,3,2,1,0:T(8,128)(2,1)S(1)}, bf16[1,1,1,512,128]{4,3,2,1,0:T(8,128)(2,1)}, u32[]{:S(2)}) copy-start(bf16[1,1,1,512,128]{4,3,2,1,0:T(8,128)(2,1)} %param.7) | copy-start | bytes 393220
  11.4 26.0 %collective-permute-start.4 = (bf16[992,128]{1,0:T(8,128)(2,1)S(1)}, bf16[992,128]{1,0:T(8,128)(2,1)}, u32[]{:S(2)}, u32[]{:S(2)}) collective-permute-start(bf16[992,128]{1,0:T(8,128)(2,1)S(1)} %get-tuple-element.62), channel_id=1, source_target_pairs={{0,6},{1,7},{2,0},{3,1},{4,2},{5,3},{6,4},{7,5},{8,14},{9,15},{10,... | collective-permute-start | bytes 761864 | tf_op jit(solution)/shard_map/ppermute | solution.py:73
  13.3 22.3 %collective-permute-start.2 = (bf16[1,8,1,8,256]{4,3,2,1,0:T(8,128)(2,1)S(1)}, bf16[1,8,1,8,256]{4,3,2,1,0:T(8,128)(2,1)S(1)}, u32[]{:S(2)}, u32[]{:S(2)}) collective-permute-start(bf16[1,8,1,8,256]{4,3,2,1,0:T(8,128)(2,1)S(1)} %fusion.56), channel_id=1, source_target_pairs={{0,1},{1,0},{2,3},{3,2},{4,5},{5,4},{6,7},{7,6},{8,9},{9,8},{10,11... | collective-permute-start | bytes 98312 | tf_op jit(solution)/shard_map/ppermute | solution.py:73
  35.1 8.7 %collective-permute-start.1 = (bf16[992,128]{1,0:T(8,128)(2,1)S(1)}, bf16[992,128]{1,0:T(8,128)(2,1)S(1)}, u32[]{:S(2)}, u32[]{:S(2)}) collective-permute-start(bf16[992,128]{1,0:T(8,128)(2,1)S(1)} %get-tuple-element.63), channel_id=1, source_target_pairs={{0,2},{1,3},{2,4},{3,5},{4,6},{5,7},{6,0},{7,1},{8,10},{9,11},{10,... | collective-permute-start | bytes 761864 | tf_op jit(solution)/shard_map/ppermute | solution.py:73
  48.8 2.5 %copy-start.2 = (bf16[3,3,3,128,128]{4,3,2,1,0:T(8,128)(2,1)S(1)}, bf16[3,3,3,128,128]{4,3,2,1,0:T(8,128)(2,1)}, u32[]{:S(2)}) copy-start(bf16[3,3,3,128,128]{4,3,2,1,0:T(8,128)(2,1)} %rev.3) | copy-start | bytes 2654212
  51.3 4.0 %copy-start = (bf16[1,1,1,1,512,128]{5,4,3,2,1,0:T(8,128)(2,1)S(1)}, bf16[1,1,1,1,512,128]{5,4,3,2,1,0:T(8,128)(2,1)}, u32[]{:S(2)}) copy-start(bf16[1,1,1,1,512,128]{5,4,3,2,1,0:T(8,128)(2,1)} %param.6) | copy-start | bytes 393220
  56.1 18.7 %collective-permute-start.8 = (bf16[1,1,8,8,128]{4,3,2,1,0:T(8,128)(2,1)S(1)}, bf16[1,1,8,8,128]{4,3,2,1,0:T(8,128)(2,1)S(1)}, u32[]{:S(2)}, u32[]{:S(2)}) collective-permute-start(bf16[1,1,8,8,128]{4,3,2,1,0:T(8,128)(2,1)S(1)} %get-tuple-element.74), channel_id=1, source_target_pairs={{8,2},{9,3},{10,4},{11,5},{12,6},{13,7},{16,10},{17,11},{18,12},{1... | collective-permute-start | bytes 49160 | tf_op jit(solution)/shard_map/ppermute | solution.py:73
  58.1 16.9 %collective-permute-start.11 = (bf16[1,1,8,8,128]{4,3,2,1,0:T(8,128)(2,1)S(1)}, bf16[1,1,8,8,128]{4,3,2,1,0:T(8,128)(2,1)S(1)}, u32[]{:S(2)}, u32[]{:S(2)}) collective-permute-start(bf16[1,1,8,8,128]{4,3,2,1,0:T(8,128)(2,1)S(1)} %get-tuple-element.75), channel_id=1, source_target_pairs={{10,0},{11,1},{12,2},{13,3},{14,4},{15,5},{18,8},{19,9},{20,10},{2... | collective-permute-start | bytes 49160 | tf_op jit(solution)/shard_map/ppermute | solution.py:73
  62.2 6.7 %collective-permute-start.7 = (bf16[1,1,1,8,128]{4,3,2,1,0:T(8,128)(2,1)S(1)}, bf16[1,1,1,8,128]{4,3,2,1,0:T(8,128)(2,1)S(1)}, u32[]{:S(2)}, u32[]{:S(2)}) collective-permute-start(bf16[1,1,1,8,128]{4,3,2,1,0:T(8,128)(2,1)S(1)} %constant_dynamic-slice_fusion.11), channel_id=1, source_target_pairs={{8,3},{9,2},{10,5},{11,4},{12,7},{13,6},{16,11},{17,10},{18,13},{1... | collective-permute-start | bytes 6152 | tf_op jit(solution)/shard_map/ppermute | solution.py:73
  64.1 10.7 %collective-permute-start.9 = (bf16[1,8,1,8,128]{4,3,2,1,0:T(8,128)(2,1)S(1)}, bf16[1,8,1,8,128]{4,3,2,1,0:T(8,128)(2,1)S(1)}, u32[]{:S(2)}, u32[]{:S(2)}) collective-permute-start(bf16[1,8,1,8,128]{4,3,2,1,0:T(8,128)(2,1)S(1)} %constant_dynamic-slice_fusion.10), channel_id=1, source_target_pairs={{8,1},{9,0},{10,3},{11,2},{12,5},{13,4},{14,7},{15,6},{16,9},{17,8... | collective-permute-start | bytes 49160 | tf_op jit(solution)/shard_map/ppermute | solution.py:73
  66.3 12.2 %copy-start.6 = (bf16[512,128]{1,0:T(8,128)(2,1)}, bf16[512,128]{1,0:T(8,128)(2,1)S(1)}, u32[]{:S(2)}) copy-start(bf16[512,128]{1,0:T(8,128)(2,1)S(1)} %fusion.8) | copy-start | bytes 393220
  66.3 8.9 %collective-permute-start.6 = (bf16[512,128]{1,0:T(8,128)(2,1)S(1)}, bf16[512,128]{1,0:T(8,128)(2,1)S(1)}, u32[]{:S(2)}, u32[]{:S(2)}) collective-permute-start(bf16[512,128]{1,0:T(8,128)(2,1)S(1)} %fusion.8), channel_id=1, source_target_pairs={{8,0},{16,8},{24,16},{9,1},{17,9},{25,17},{10,2},{18,10},{26,18},{... | collective-permute-start | bytes 393224 | tf_op jit(solution)/shard_map/ppermute | solution.py:229
  68.9 5.8 %collective-permute-start.10 = (bf16[1,1,1,8,128]{4,3,2,1,0:T(8,128)(2,1)S(1)}, bf16[1,1,1,8,128]{4,3,2,1,0:T(8,128)(2,1)S(1)}, u32[]{:S(2)}, u32[]{:S(2)}) collective-permute-start(bf16[1,1,1,8,128]{4,3,2,1,0:T(8,128)(2,1)S(1)} %constant_dynamic-slice_fusion.9), channel_id=1, source_target_pairs={{10,1},{11,0},{12,3},{13,2},{14,5},{15,4},{18,9},{19,8},{20,11},{2... | collective-permute-start | bytes 6152 | tf_op jit(solution)/shard_map/ppermute | solution.py:73
  79.2 18.4 %copy-start.4 = (bf16[512,128]{1,0:T(8,128)(2,1)}, bf16[512,128]{1,0:T(8,128)(2,1)S(1)}, u32[]{:S(2)}) copy-start(bf16[512,128]{1,0:T(8,128)(2,1)S(1)} %fusion.18) | copy-start | bytes 393220
  79.2 17.6 %collective-permute-start.14 = (bf16[1,1,8,8,128]{4,3,2,1,0:T(8,128)(2,1)S(1)}, bf16[1,1,8,8,128]{4,3,2,1,0:T(8,128)(2,1)S(1)}, u32[]{:S(2)}, u32[]{:S(2)}) collective-permute-start(bf16[1,1,8,8,128]{4,3,2,1,0:T(8,128)(2,1)S(1)} %get-tuple-element.69), channel_id=1, source_target_pairs={{8,2},{9,3},{10,4},{11,5},{12,6},{13,7},{16,10},{17,11},{18,12},{1... | collective-permute-start | bytes 49160 | tf_op jit(solution)/shard_map/ppermute | solution.py:73
  81.2 16.0 %collective-permute-start.12 = (bf16[512,128]{1,0:T(8,128)(2,1)S(1)}, bf16[512,128]{1,0:T(8,128)(2,1)S(1)}, u32[]{:S(2)}, u32[]{:S(2)}) collective-permute-start(bf16[512,128]{1,0:T(8,128)(2,1)S(1)} %fusion.18), channel_id=1, source_target_pairs={{8,0},{16,8},{24,16},{9,1},{17,9},{25,17},{10,2},{18,10},{26,18},{... | collective-permute-start | bytes 393224 | tf_op jit(solution)/shard_map/ppermute | solution.py:229
  83.1 7.7 %collective-permute-start.13 = (bf16[1,1,1,8,128]{4,3,2,1,0:T(8,128)(2,1)S(1)}, bf16[1,1,1,8,128]{4,3,2,1,0:T(8,128)(2,1)S(1)}, u32[]{:S(2)}, u32[]{:S(2)}) collective-permute-start(bf16[1,1,1,8,128]{4,3,2,1,0:T(8,128)(2,1)S(1)} %constant_dynamic-slice_fusion.8), channel_id=1, source_target_pairs={{8,3},{9,2},{10,5},{11,4},{12,7},{13,6},{16,11},{17,10},{18,13},{1... | collective-permute-start | bytes 6152 | tf_op jit(solution)/shard_map/ppermute | solution.py:73
  85.1 11.8 %collective-permute-start.17 = (bf16[1,1,8,8,128]{4,3,2,1,0:T(8,128)(2,1)S(1)}, bf16[1,1,8,8,128]{4,3,2,1,0:T(8,128)(2,1)S(1)}, u32[]{:S(2)}, u32[]{:S(2)}) collective-permute-start(bf16[1,1,8,8,128]{4,3,2,1,0:T(8,128)(2,1)S(1)} %get-tuple-element.70), channel_id=1, source_target_pairs={{10,0},{11,1},{12,2},{13,3},{14,4},{15,5},{18,8},{19,9},{20,10},{2... | collective-permute-start | bytes 49160 | tf_op jit(solution)/shard_map/ppermute | solution.py:73
  88.9 7.8 %collective-permute-start.15 = (bf16[1,8,1,8,128]{4,3,2,1,0:T(8,128)(2,1)S(1)}, bf16[1,8,1,8,128]{4,3,2,1,0:T(8,128)(2,1)S(1)}, u32[]{:S(2)}, u32[]{:S(2)}) collective-permute-start(bf16[1,8,1,8,128]{4,3,2,1,0:T(8,128)(2,1)S(1)} %constant_dynamic-slice_fusion.7), channel_id=1, source_target_pairs={{8,1},{9,0},{10,3},{11,2},{12,5},{13,4},{14,7},{15,6},{16,9},{17,8... | collective-permute-start | bytes 49160 | tf_op jit(solution)/shard_map/ppermute | solution.py:73
  90.8 5.8 %collective-permute-start.16 = (bf16[1,1,1,8,128]{4,3,2,1,0:T(8,128)(2,1)S(1)}, bf16[1,1,1,8,128]{4,3,2,1,0:T(8,128)(2,1)S(1)}, u32[]{:S(2)}, u32[]{:S(2)}) collective-permute-start(bf16[1,1,1,8,128]{4,3,2,1,0:T(8,128)(2,1)S(1)} %constant_dynamic-slice_fusion.6), channel_id=1, source_target_pairs={{10,1},{11,0},{12,3},{13,2},{14,5},{15,4},{18,9},{19,8},{20,11},{2... | collective-permute-start | bytes 6152 | tf_op jit(solution)/shard_map/ppermute | solution.py:73
  100.5 19.0 %copy-start.10 = (bf16[1,10,10,10,256]{4,0,3,2,1:T(2,128)(2,1)S(1)}, bf16[1,10,10,10,256]{4,0,3,2,1:T(2,128)(2,1)}, u32[]{:S(2)}) copy-start(bf16[1,10,10,10,256]{4,0,3,2,1:T(2,128)(2,1)} %constant_dynamic-update-slice_fusion) | copy-start | bytes 1536004
  101.2 18.2 %collective-permute-start.18 = (bf16[512,128]{1,0:T(8,128)(2,1)S(1)}, bf16[512,128]{1,0:T(8,128)(2,1)S(1)}, u32[]{:S(2)}, u32[]{:S(2)}) collective-permute-start(bf16[512,128]{1,0:T(8,128)(2,1)S(1)} %fusion.21), channel_id=1, source_target_pairs={{8,0},{16,8},{24,16},{9,1},{17,9},{25,17},{10,2},{18,10},{26,18},{... | collective-permute-start | bytes 393224 | tf_op jit(solution)/shard_map/ppermute | solution.py:229
  103.2 9.5 %collective-permute-start.22 = (bf16[1,1,1,8,128]{4,3,2,1,0:T(8,128)(2,1)S(1)}, bf16[1,1,1,8,128]{4,3,2,1,0:T(8,128)(2,1)S(1)}, u32[]{:S(2)}, u32[]{:S(2)}) collective-permute-start(bf16[1,1,1,8,128]{4,3,2,1,0:T(8,128)(2,1)S(1)} %constant_dynamic-slice_fusion.3), channel_id=1, source_target_pairs={{10,1},{11,0},{12,3},{13,2},{14,5},{15,4},{18,9},{19,8},{20,11},{2... | collective-permute-start | bytes 6152 | tf_op jit(solution)/shard_map/ppermute | solution.py:73
  106.8 16.5 %collective-permute-start.20 = (bf16[1,1,8,8,128]{4,3,2,1,0:T(8,128)(2,1)S(1)}, bf16[1,1,8,8,128]{4,3,2,1,0:T(8,128)(2,1)S(1)}, u32[]{:S(2)}, u32[]{:S(2)}) collective-permute-start(bf16[1,1,8,8,128]{4,3,2,1,0:T(8,128)(2,1)S(1)} %get-tuple-element.68), channel_id=1, source_target_pairs={{8,2},{9,3},{10,4},{11,5},{12,6},{13,7},{16,10},{17,11},{18,12},{1... | collective-permute-start | bytes 49160 | tf_op jit(solution)/shard_map/ppermute | solution.py:73
  108.8 14.5 %collective-permute-start.23 = (bf16[1,1,8,8,128]{4,3,2,1,0:T(8,128)(2,1)S(1)}, bf16[1,1,8,8,128]{4,3,2,1,0:T(8,128)(2,1)S(1)}, u32[]{:S(2)}, u32[]{:S(2)}) collective-permute-start(bf16[1,1,8,8,128]{4,3,2,1,0:T(8,128)(2,1)S(1)} %get-tuple-element.67), channel_id=1, source_target_pairs={{10,0},{11,1},{12,2},{13,3},{14,4},{15,5},{18,8},{19,9},{20,10},{2... | collective-permute-start | bytes 49160 | tf_op jit(solution)/shard_map/ppermute | solution.py:73
  110.7 8.7 %collective-permute-start.21 = (bf16[1,8,1,8,128]{4,3,2,1,0:T(8,128)(2,1)S(1)}, bf16[1,8,1,8,128]{4,3,2,1,0:T(8,128)(2,1)S(1)}, u32[]{:S(2)}, u32[]{:S(2)}) collective-permute-start(bf16[1,8,1,8,128]{4,3,2,1,0:T(8,128)(2,1)S(1)} %constant_dynamic-slice_fusion.4), channel_id=1, source_target_pairs={{8,1},{9,0},{10,3},{11,2},{12,5},{13,4},{14,7},{15,6},{16,9},{17,8... | collective-permute-start | bytes 49160 | tf_op jit(solution)/shard_map/ppermute | solution.py:73
  112.6 6.7 %collective-permute-start.19 = (bf16[1,1,1,8,128]{4,3,2,1,0:T(8,128)(2,1)S(1)}, bf16[1,1,1,8,128]{4,3,2,1,0:T(8,128)(2,1)S(1)}, u32[]{:S(2)}, u32[]{:S(2)}) collective-permute-start(bf16[1,1,1,8,128]{4,3,2,1,0:T(8,128)(2,1)S(1)} %constant_dynamic-slice_fusion.5), channel_id=1, source_target_pairs={{8,3},{9,2},{10,5},{11,4},{12,7},{13,6},{16,11},{17,10},{18,13},{1... | collective-permute-start | bytes 6152 | tf_op jit(solution)/shard_map/ppermute | solution.py:73
  123.5 7.6 %collective-permute-start.24 = (bf16[864,128]{1,0:T(8,128)(2,1)S(1)}, bf16[864,128]{1,0:T(8,128)(2,1)S(1)}, u32[]{:S(2)}, u32[]{:S(2)}) collective-permute-start(bf16[864,128]{1,0:T(8,128)(2,1)S(1)} %get-tuple-element.51), channel_id=1, source_target_pairs={{0,2},{2,4},{4,6},{6,0},{1,3},{3,5},{5,7},{7,1},{8,10},{10,12},{12... | collective-permute-start | bytes 663560 | tf_op jit(solution)/shard_map/ppermute | solution.py:151
  123.6 11.4 %collective-permute-start.25 = (bf16[864,128]{1,0:T(8,128)(2,1)S(1)}, bf16[864,128]{1,0:T(8,128)(2,1)S(1)}, u32[]{:S(2)}, u32[]{:S(2)}) collective-permute-start(bf16[864,128]{1,0:T(8,128)(2,1)S(1)} %get-tuple-element.53), channel_id=1, source_target_pairs={{0,4},{2,6},{4,0},{6,2},{1,5},{3,7},{5,1},{7,3},{8,12},{10,14},{12... | collective-permute-start | bytes 663560 | tf_op jit(solution)/shard_map/ppermute | solution.py:151
  123.7 11.4 %collective-permute-start.26 = (bf16[864,128]{1,0:T(8,128)(2,1)S(1)}, bf16[864,128]{1,0:T(8,128)(2,1)S(1)}, u32[]{:S(2)}, u32[]{:S(2)}) collective-permute-start(bf16[864,128]{1,0:T(8,128)(2,1)S(1)} %get-tuple-element.52), channel_id=1, source_target_pairs={{0,6},{2,0},{4,2},{6,4},{1,7},{3,1},{5,3},{7,5},{8,14},{10,8},{12,... | collective-permute-start | bytes 663560 | tf_op jit(solution)/shard_map/ppermute | solution.py:151
  129.7 6.7 %copy-start.5 = (bf16[512,128]{1,0:T(8,128)(2,1)S(1)}, bf16[512,128]{1,0:T(8,128)(2,1)}, u32[]{:S(2)}) copy-start(bf16[512,128]{1,0:T(8,128)(2,1)} %copy-done.4) | copy-start | bytes 393220
  129.7 6.7 %copy-start.7 = (bf16[512,128]{1,0:T(8,128)(2,1)S(1)}, bf16[512,128]{1,0:T(8,128)(2,1)}, u32[]{:S(2)}) copy-start(bf16[512,128]{1,0:T(8,128)(2,1)} %copy-done.6) | copy-start | bytes 393220
  135.1 2.7 %collective-permute-start.27 = (f32[864,128]{1,0:T(8,128)S(1)}, f32[864,128]{1,0:T(8,128)S(1)}, u32[]{:S(2)}, u32[]{:S(2)}) collective-permute-start(f32[864,128]{1,0:T(8,128)S(1)} %convert_add_fusion), channel_id=1, source_target_pairs={{0,1},{1,0},{2,3},{3,2},{4,5},{5,4},{6,7},{7,6},{8,9},{9,8},{10,11... | collective-permute-start | bytes 1327112 | tf_op jit(solution)/shard_map/ppermute | solution.py:234

commit v13 on v7

--- a/solution.py
+++ b/solution.py
@@ -90,9 +90,8 @@
                 received[(shift_x, 0)] = face_x(shift_x)
             row = lax.dynamic_slice_in_dim(cube[:, source_range(shift_x)], (1 - place_y) * 7, 1, axis=2)
             got = send(row, lambda a, b, i=shift_x: (a - i, 1 - b))
-            blank = jnp.zeros_like(got)
-            received[(shift_x, 1)] = jnp.where(place_y == 0, got, blank)
-            received[(shift_x, -1)] = jnp.where(place_y == 1, got, blank)
+            received[(shift_x, 1)] = got
+            received[(shift_x, -1)] = got
         return received
     for shift_x, shift_y in directions():
         if shift_y == 0:

time: 132 us -> 128 us (0.970)
  waiting for transfers between devices: 22.3 us -> 17.8 us
    ppermute x20, waiting for transfers between devices: 14.5 us -> 10.1 us  [send(): return lax.ppermute(piece, axes, route)]
  transfers between devices with their start and end apart: 28 -> 28, of which waited for: 8 -> 6; matrix products, arithmetic and copies ran while one was open for 12% -> 12% of each run, Pallas kernels for 0% -> 0%
where the time goes in v13:
time: 128 us; the launch traced here: 126 us
  starting transfers between devices  50.7 us (40%)
  between operations  19.9 us (16%)
  waiting for transfers between devices  17.8 us (14%)
  matrix products  15.8 us (12%)
  other arithmetic  15.3 us (12%)
  local copies, waits for them, and re-layouts  6.62 us (5%)
    ppermute x20, starting transfers between devices, send(): return lax.ppermute(piece, axes, route)  41.2 us
    conv_general_dilated x4, matrix products, conv_data(): lax.conv_general_dilated(padded, filters, (1, 1, 1), 'VALID', dimension_n...  11.8 us
    ppermute x20, waiting for transfers between devices, send(): return lax.ppermute(piece, axes, route)  10.1 us
    ppermute x3, waiting for transfers between devices, scattered_sum(): lax.ppermute(piece, axis, [(i, (i + step) % count) for i in range(count)])  7.34 us
    ppermute x3, starting transfers between devices, shards(): centre = lax.ppermute(result, 'pipe', down)  5.76 us
    transpose x1, matrix products, shards(): per_tap.transpose(1, 2, 3, 0, 4).reshape(taps * channels, channels)  3.93 us
  transfers between devices with their start and end apart: 28, of which 6 were waited for; matrix products, arithmetic and copies ran while one was open for 12% of the time, Pallas kernels for 0%

profile of v13, /device:TPU:21, one launch (start us, length us, event | category | flops | bytes accessed | tf_op | source)
XLA Modules:
  0.0 126.0 jit_solution(14778646630026231319)
XLA Ops:
  0.6 1.0 convert_element_type.160
  1.6 1.1 fusion.25
  3.5 1.0 broadcast_select_fusion.12
  4.5 0.9 multiply_convert_fusion.2
  5.5 3.7 %collective-permute-start = (bf16[1,1,1,8,256]{4,3,2,1,0:T(8,128)(2,1)S(1)}, bf16[1,1,1,8,256]{4,3,2,1,0:T(8,128)(2,1)S(1)}, u32[]{:S(2)}, u32[]{:S(2)}) collective-permute-start(bf16[1,1,1,8,256]{4,3,2,1,0:T(8,128)(2,1)S(1)} %constant_dynamic-slice_fusion.13), channel_id=1, source_target_pairs={{0,3},{1,2},{2,5},{3,4},{4,7},{5,6},{8,11},{9,10},{10,13},{11,12},... | collective-permute-start | bytes 12296 | tf_op jit(solution)/shard_map/ppermute | solution.py:73
  9.2 0.3 collective-permute-start.5
  9.5 1.3 %collective-permute-start.1 = (bf16[992,128]{1,0:T(8,128)(2,1)S(1)}, bf16[992,128]{1,0:T(8,128)(2,1)S(1)}, u32[]{:S(2)}, u32[]{:S(2)}) collective-permute-start(bf16[992,128]{1,0:T(8,128)(2,1)S(1)} %get-tuple-element.40), channel_id=1, source_target_pairs={{0,2},{1,3},{2,4},{3,5},{4,6},{5,7},{6,0},{7,1},{8,10},{9,11},{10,... | collective-permute-start | bytes 761864 | tf_op jit(solution)/shard_map/ppermute | solution.py:73
  10.8 3.3 %collective-permute-start.2 = (bf16[1,1,1,8,256]{4,3,2,1,0:T(8,128)(2,1)S(1)}, bf16[1,1,1,8,256]{4,3,2,1,0:T(8,128)(2,1)S(1)}, u32[]{:S(2)}, u32[]{:S(2)}) collective-permute-start(bf16[1,1,1,8,256]{4,3,2,1,0:T(8,128)(2,1)S(1)} %constant_dynamic-slice_fusion.12), channel_id=1, source_target_pairs={{2,1},{3,0},{4,3},{5,2},{6,5},{7,4},{10,9},{11,8},{12,11},{13,10},... | collective-permute-start | bytes 12296 | tf_op jit(solution)/shard_map/ppermute | solution.py:73
  14.2 0.7 fusion.76
  14.9 0.7 fusion.75
  15.9 0.2 copy_dynamic-update-slice_fusion.1
  18.1 0.6 scatter_custom_fusion
  18.7 0.6 pad_clamp_fusion
  19.3 0.5 fusion.60
  19.8 0.4 copy_dynamic-update-slice_fusion
  20.2 0.6 broadcast_select_fusion
  35.9 0.6 collective-permute-start.4
  36.7 0.7 collective-permute-done.4
  38.3 1.0 pad_maximum_fusion.1
  39.4 0.8 gather_fusion
  40.2 1.0 rev.3
  41.3 2.1 %pad_maximum_fusion = bf16[1,10,10,10,256]{4,0,3,2,1:T(2,128)(2,1)S(1)} fusion(bf16[1,1,10,10,256]{4,0,3,2,1:T(2,128)(2,1)S(1)} %pad_maximum_fusion.11, bf16[1,8,1,10,256]{4,0,3,2,1:T(2,128)(2,1)S(1)} %copy.47, bf16[1,8,8,1,256]{4,0,3,2,1:T(2,128)(2,1)S(1)} %get-tuple-element.30, bf16[1,8,8,8,256]{4,0,3,2,1:T(2,128)(2,1)S(1)} %broadcast_select_fusion, ...), kind=kLoop, calls=%fused_computation.4 | loop fusion | flops 1536000 | bytes 1024000 | tf_op jit(solution)/shard_map/concatenate | solution.py:56
  43.4 3.0 %fusion.1 = f32[1,8,8,8,128]{4,0,3,2,1:T(1,128)S(1)} fusion(bf16[3,3,3,128,128]{4,3,2,1,0:T(8,128)(2,1)S(1)} %copy-done.4, bf16[1,10,10,10,256]{4,0,3,2,1:T(2,128)(2,1)S(1)} %pad_maximum_fusion), kind=kOutput, calls=%fused_computation.10 | convolution fusion | flops 452984832 | bytes 1658880 | tf_op jit(solution)/shard_map/conv_general_dilated | solution.py:107
  46.4 0.3 fusion.47
  46.9 0.3 fusion.15
  47.2 1.9 %collective-permute-start.11 = (bf16[1,1,8,8,128]{4,3,2,1,0:T(8,128)(2,1)S(1)}, bf16[1,1,8,8,128]{4,3,2,1,0:T(8,128)(2,1)S(1)}, u32[]{:S(2)}, u32[]{:S(2)}) collective-permute-start(bf16[1,1,8,8,128]{4,3,2,1,0:T(8,128)(2,1)S(1)} %get-tuple-element.52), channel_id=1, source_target_pairs={{10,0},{11,1},{12,2},{13,3},{14,4},{15,5},{18,8},{19,9},{20,10},{2... | collective-permute-start | bytes 49160 | tf_op jit(solution)/shard_map/ppermute | solution.py:73
  49.2 3.1 %collective-permute-start.8 = (bf16[1,1,8,8,128]{4,3,2,1,0:T(8,128)(2,1)S(1)}, bf16[1,1,8,8,128]{4,3,2,1,0:T(8,128)(2,1)S(1)}, u32[]{:S(2)}, u32[]{:S(2)}) collective-permute-start(bf16[1,1,8,8,128]{4,3,2,1,0:T(8,128)(2,1)S(1)} %get-tuple-element.51), channel_id=1, source_target_pairs={{8,2},{9,3},{10,4},{11,5},{12,6},{13,7},{16,10},{17,11},{18,12},{1... | collective-permute-start | bytes 49160 | tf_op jit(solution)/shard_map/ppermute | solution.py:73
  52.3 3.6 %collective-permute-start.10 = (bf16[1,1,1,8,128]{4,3,2,1,0:T(8,128)(2,1)S(1)}, bf16[1,1,1,8,128]{4,3,2,1,0:T(8,128)(2,1)S(1)}, u32[]{:S(2)}, u32[]{:S(2)}) collective-permute-start(bf16[1,1,1,8,128]{4,3,2,1,0:T(8,128)(2,1)S(1)} %constant_dynamic-slice_fusion.9), channel_id=1, source_target_pairs={{10,1},{11,0},{12,3},{13,2},{14,5},{15,4},{18,9},{19,8},{20,11},{2... | collective-permute-start | bytes 6152 | tf_op jit(solution)/shard_map/ppermute | solution.py:73
  55.9 0.3 fusion.8
  56.2 1.9 %collective-permute-start.6 = (bf16[512,128]{1,0:T(8,128)(2,1)S(1)}, bf16[512,128]{1,0:T(8,128)(2,1)S(1)}, u32[]{:S(2)}, u32[]{:S(2)}) collective-permute-start(bf16[512,128]{1,0:T(8,128)(2,1)S(1)} %fusion.8), channel_id=1, source_target_pairs={{8,0},{16,8},{24,16},{9,1},{17,9},{25,17},{10,2},{18,10},{26,18},{... | collective-permute-start | bytes 393224 | tf_op jit(solution)/shard_map/ppermute | solution.py:228
  58.2 1.9 %collective-permute-start.9 = (bf16[1,8,1,8,128]{4,3,2,1,0:T(8,128)(2,1)S(1)}, bf16[1,8,1,8,128]{4,3,2,1,0:T(8,128)(2,1)S(1)}, u32[]{:S(2)}, u32[]{:S(2)}) collective-permute-start(bf16[1,8,1,8,128]{4,3,2,1,0:T(8,128)(2,1)S(1)} %constant_dynamic-slice_fusion.10), channel_id=1, source_target_pairs={{8,1},{9,0},{10,3},{11,2},{12,5},{13,4},{14,7},{15,6},{16,9},{17,8... | collective-permute-start | bytes 49160 | tf_op jit(solution)/shard_map/ppermute | solution.py:73
  60.1 2.1 %collective-permute-start.7 = (bf16[1,1,1,8,128]{4,3,2,1,0:T(8,128)(2,1)S(1)}, bf16[1,1,1,8,128]{4,3,2,1,0:T(8,128)(2,1)S(1)}, u32[]{:S(2)}, u32[]{:S(2)}) collective-permute-start(bf16[1,1,1,8,128]{4,3,2,1,0:T(8,128)(2,1)S(1)} %constant_dynamic-slice_fusion.11), channel_id=1, source_target_pairs={{8,3},{9,2},{10,5},{11,4},{12,7},{13,6},{16,11},{17,10},{18,13},{1... | collective-permute-start | bytes 6152 | tf_op jit(solution)/shard_map/ppermute | solution.py:73
  62.2 4.6 %collective-permute-done.7 = bf16[1,1,1,8,128]{4,3,2,1,0:T(8,128)(2,1)S(1)} collective-permute-done((bf16[1,1,1,8,128]{4,3,2,1,0:T(8,128)(2,1)S(1)}, bf16[1,1,1,8,128]{4,3,2,1,0:T(8,128)(2,1)S(1)}, u32[]{:S(2)}, u32[]{:S(2)}) %collective-permute-start.7) | collective-permute-done | bytes 2080 | tf_op jit(solution)/shard_map/ppermute | solution.py:73
  67.4 0.2 copy.52
  67.7 2.9 %fusion.5 = f32[1,8,8,8,128]{4,0,3,2,1:T(1,128)S(1)} fusion(bf16[3,3,3,128,128]{4,3,2,1,0:T(8,128)(2,1)S(1)} %bitcast.208, bf16[1,1,10,10,128]{4,0,3,2,1:T(2,128)(2,1)S(1)} %copy.56, bf16[1,8,1,10,128]{4,0,3,2,1:T(2,128)(2,1)S(1)} %copy.54, bf16[1,8,8,1,128]{4,0,3,2,1:T(2,128)(2,1)S(1)} %slice_bitcast_fusion.6, bf16[1,8,8,8,128]{4,0,3,2,1:T(2,128)(2,1)S(1)} %copy.52, ...), kind=kOutput, calls=%fused_computation.14 | convolution fusion | flops 454776832 | bytes 1402880 | tf_op jit(solution)/shard_map/conv_general_dilated | solution.py:107
  70.7 0.3 fusion.48
  71.0 0.3 fusion.18
  71.3 1.9 %collective-permute-start.12 = (bf16[512,128]{1,0:T(8,128)(2,1)S(1)}, bf16[512,128]{1,0:T(8,128)(2,1)S(1)}, u32[]{:S(2)}, u32[]{:S(2)}) collective-permute-start(bf16[512,128]{1,0:T(8,128)(2,1)S(1)} %fusion.18), channel_id=1, source_target_pairs={{8,0},{16,8},{24,16},{9,1},{17,9},{25,17},{10,2},{18,10},{26,18},{... | collective-permute-start | bytes 393224 | tf_op jit(solution)/shard_map/ppermute | solution.py:228
  73.3 1.9 %collective-permute-start.17 = (bf16[1,1,8,8,128]{4,3,2,1,0:T(8,128)(2,1)S(1)}, bf16[1,1,8,8,128]{4,3,2,1,0:T(8,128)(2,1)S(1)}, u32[]{:S(2)}, u32[]{:S(2)}) collective-permute-start(bf16[1,1,8,8,128]{4,3,2,1,0:T(8,128)(2,1)S(1)} %get-tuple-element.47), channel_id=1, source_target_pairs={{10,0},{11,1},{12,2},{13,3},{14,4},{15,5},{18,8},{19,9},{20,10},{2... | collective-permute-start | bytes 49160 | tf_op jit(solution)/shard_map/ppermute | solution.py:73
  75.3 1.9 %collective-permute-start.16 = (bf16[1,1,1,8,128]{4,3,2,1,0:T(8,128)(2,1)S(1)}, bf16[1,1,1,8,128]{4,3,2,1,0:T(8,128)(2,1)S(1)}, u32[]{:S(2)}, u32[]{:S(2)}) collective-permute-start(bf16[1,1,1,8,128]{4,3,2,1,0:T(8,128)(2,1)S(1)} %constant_dynamic-slice_fusion.6), channel_id=1, source_target_pairs={{10,1},{11,0},{12,3},{13,2},{14,5},{15,4},{18,9},{19,8},{20,11},{2... | collective-permute-start | bytes 6152 | tf_op jit(solution)/shard_map/ppermute | solution.py:73
  77.2 1.9 %collective-permute-start.14 = (bf16[1,1,8,8,128]{4,3,2,1,0:T(8,128)(2,1)S(1)}, bf16[1,1,8,8,128]{4,3,2,1,0:T(8,128)(2,1)S(1)}, u32[]{:S(2)}, u32[]{:S(2)}) collective-permute-start(bf16[1,1,8,8,128]{4,3,2,1,0:T(8,128)(2,1)S(1)} %get-tuple-element.46), channel_id=1, source_target_pairs={{8,2},{9,3},{10,4},{11,5},{12,6},{13,7},{16,10},{17,11},{18,12},{1... | collective-permute-start | bytes 49160 | tf_op jit(solution)/shard_map/ppermute | solution.py:73
  79.1 1.9 %collective-permute-start.15 = (bf16[1,8,1,8,128]{4,3,2,1,0:T(8,128)(2,1)S(1)}, bf16[1,8,1,8,128]{4,3,2,1,0:T(8,128)(2,1)S(1)}, u32[]{:S(2)}, u32[]{:S(2)}) collective-permute-start(bf16[1,8,1,8,128]{4,3,2,1,0:T(8,128)(2,1)S(1)} %constant_dynamic-slice_fusion.7), channel_id=1, source_target_pairs={{8,1},{9,0},{10,3},{11,2},{12,5},{13,4},{14,7},{15,6},{16,9},{17,8... | collective-permute-start | bytes 49160 | tf_op jit(solution)/shard_map/ppermute | solution.py:73
  81.1 1.9 %collective-permute-start.13 = (bf16[1,1,1,8,128]{4,3,2,1,0:T(8,128)(2,1)S(1)}, bf16[1,1,1,8,128]{4,3,2,1,0:T(8,128)(2,1)S(1)}, u32[]{:S(2)}, u32[]{:S(2)}) collective-permute-start(bf16[1,1,1,8,128]{4,3,2,1,0:T(8,128)(2,1)S(1)} %constant_dynamic-slice_fusion.8), channel_id=1, source_target_pairs={{8,3},{9,2},{10,5},{11,4},{12,7},{13,6},{16,11},{17,10},{18,13},{1... | collective-permute-start | bytes 6152 | tf_op jit(solution)/shard_map/ppermute | solution.py:73
  83.0 4.8 %collective-permute-done.13 = bf16[1,1,1,8,128]{4,3,2,1,0:T(8,128)(2,1)S(1)} collective-permute-done((bf16[1,1,1,8,128]{4,3,2,1,0:T(8,128)(2,1)S(1)}, bf16[1,1,1,8,128]{4,3,2,1,0:T(8,128)(2,1)S(1)}, u32[]{:S(2)}, u32[]{:S(2)}) %collective-permute-start.13) | collective-permute-done | bytes 2080 | tf_op jit(solution)/shard_map/ppermute | solution.py:73
  88.7 2.9 %fusion.4 = f32[1,8,8,8,128]{4,0,3,2,1:T(1,128)S(1)} fusion(bf16[3,3,3,128,128]{4,3,2,1,0:T(8,128)(2,1)S(1)} %bitcast.209, bf16[1,1,10,10,128]{4,0,3,2,1:T(2,128)(2,1)S(1)} %copy.63, bf16[1,8,1,10,128]{4,0,3,2,1:T(2,128)(2,1)S(1)} %copy.61, bf16[1,8,8,1,128]{4,0,3,2,1:T(2,128)(2,1)S(1)} %slice_bitcast_fusion.4, bf16[1,8,8,8,128]{4,0,3,2,1:T(2,128)(2,1)S(1)} %copy.59, ...), kind=kOutput, calls=%fused_computation.13 | convolution fusion | flops 454776832 | bytes 1402880 | tf_op jit(solution)/shard_map/conv_general_dilated | solution.py:107
  91.6 0.3 fusion.49
  92.0 0.3 fusion.21
  92.3 1.9 %collective-permute-start.18 = (bf16[512,128]{1,0:T(8,128)(2,1)S(1)}, bf16[512,128]{1,0:T(8,128)(2,1)S(1)}, u32[]{:S(2)}, u32[]{:S(2)}) collective-permute-start(bf16[512,128]{1,0:T(8,128)(2,1)S(1)} %fusion.21), channel_id=1, source_target_pairs={{8,0},{16,8},{24,16},{9,1},{17,9},{25,17},{10,2},{18,10},{26,18},{... | collective-permute-start | bytes 393224 | tf_op jit(solution)/shard_map/ppermute | solution.py:228
  94.3 1.9 %collective-permute-start.20 = (bf16[1,1,8,8,128]{4,3,2,1,0:T(8,128)(2,1)S(1)}, bf16[1,1,8,8,128]{4,3,2,1,0:T(8,128)(2,1)S(1)}, u32[]{:S(2)}, u32[]{:S(2)}) collective-permute-start(bf16[1,1,8,8,128]{4,3,2,1,0:T(8,128)(2,1)S(1)} %get-tuple-element.45), channel_id=1, source_target_pairs={{8,2},{9,3},{10,4},{11,5},{12,6},{13,7},{16,10},{17,11},{18,12},{1... | collective-permute-start | bytes 49160 | tf_op jit(solution)/shard_map/ppermute | solution.py:73
  96.2 1.9 %collective-permute-start.19 = (bf16[1,1,1,8,128]{4,3,2,1,0:T(8,128)(2,1)S(1)}, bf16[1,1,1,8,128]{4,3,2,1,0:T(8,128)(2,1)S(1)}, u32[]{:S(2)}, u32[]{:S(2)}) collective-permute-start(bf16[1,1,1,8,128]{4,3,2,1,0:T(8,128)(2,1)S(1)} %constant_dynamic-slice_fusion.5), channel_id=1, source_target_pairs={{8,3},{9,2},{10,5},{11,4},{12,7},{13,6},{16,11},{17,10},{18,13},{1... | collective-permute-start | bytes 6152 | tf_op jit(solution)/shard_map/ppermute | solution.py:73
  98.1 1.9 %collective-permute-start.21 = (bf16[1,8,1,8,128]{4,3,2,1,0:T(8,128)(2,1)S(1)}, bf16[1,8,1,8,128]{4,3,2,1,0:T(8,128)(2,1)S(1)}, u32[]{:S(2)}, u32[]{:S(2)}) collective-permute-start(bf16[1,8,1,8,128]{4,3,2,1,0:T(8,128)(2,1)S(1)} %constant_dynamic-slice_fusion.4), channel_id=1, source_target_pairs={{8,1},{9,0},{10,3},{11,2},{12,5},{13,4},{14,7},{15,6},{16,9},{17,8... | collective-permute-start | bytes 49160 | tf_op jit(solution)/shard_map/ppermute | solution.py:73
  100.1 1.9 %collective-permute-start.23 = (bf16[1,1,8,8,128]{4,3,2,1,0:T(8,128)(2,1)S(1)}, bf16[1,1,8,8,128]{4,3,2,1,0:T(8,128)(2,1)S(1)}, u32[]{:S(2)}, u32[]{:S(2)}) collective-permute-start(bf16[1,1,8,8,128]{4,3,2,1,0:T(8,128)(2,1)S(1)} %get-tuple-element.44), channel_id=1, source_target_pairs={{10,0},{11,1},{12,2},{13,3},{14,4},{15,5},{18,8},{19,9},{20,10},{2... | collective-permute-start | bytes 49160 | tf_op jit(solution)/shard_map/ppermute | solution.py:73
  102.0 2.4 %collective-permute-start.22 = (bf16[1,1,1,8,128]{4,3,2,1,0:T(8,128)(2,1)S(1)}, bf16[1,1,1,8,128]{4,3,2,1,0:T(8,128)(2,1)S(1)}, u32[]{:S(2)}, u32[]{:S(2)}) collective-permute-start(bf16[1,1,1,8,128]{4,3,2,1,0:T(8,128)(2,1)S(1)} %constant_dynamic-slice_fusion.3), channel_id=1, source_target_pairs={{10,1},{11,0},{12,3},{13,2},{14,5},{15,4},{18,9},{19,8},{20,11},{2... | collective-permute-start | bytes 6152 | tf_op jit(solution)/shard_map/ppermute | solution.py:73
  104.6 3.9 %multiply_convert_fusion = bf16[3,3,3,128,128]{4,3,2,1,0:T(8,128)(2,1)S(1)} fusion(bf16[1,10,10,10,256]{4,0,3,2,1:T(2,128)(2,1)S(1)} %copy-done.3, bf16[1,8,8,8,128]{4,3,2,1,0:T(8,128)(2,1)S(1)} %bitcast.242), kind=kOutput, calls=%fused_computation.2 | convolution fusion | flops 453869568 | bytes 1527808 | tf_op jit(solution)/shard_map/transpose | solution.py:216
  109.6 1.4 %collective-permute-start.26 = (bf16[864,128]{1,0:T(8,128)(2,1)S(1)}, bf16[864,128]{1,0:T(8,128)(2,1)S(1)}, u32[]{:S(2)}, u32[]{:S(2)}) collective-permute-start(bf16[864,128]{1,0:T(8,128)(2,1)S(1)} %get-tuple-element.27), channel_id=1, source_target_pairs={{0,6},{2,0},{4,2},{6,4},{1,7},{3,1},{5,3},{7,5},{8,14},{10,8},{12,... | collective-permute-start | bytes 663560 | tf_op jit(solution)/shard_map/ppermute | solution.py:150
  111.0 0.4 collective-permute-start.24
  111.4 3.0 %fusion.3 = f32[1,8,8,8,128]{4,0,3,2,1:T(1,128)S(1)} fusion(bf16[3,3,3,128,128]{4,3,2,1,0:T(8,128)(2,1)S(1)} %bitcast.210, bf16[1,1,10,10,128]{4,0,3,2,1:T(2,128)(2,1)S(1)} %copy.71, bf16[1,8,1,10,128]{4,0,3,2,1:T(2,128)(2,1)S(1)} %copy.69, bf16[1,8,8,1,128]{4,0,3,2,1:T(2,128)(2,1)S(1)} %slice_bitcast_fusion.2, bf16[1,8,8,8,128]{4,0,3,2,1:T(2,128)(2,1)S(1)} %copy.67, ...), kind=kOutput, calls=%fused_computation.12 | convolution fusion | flops 454776832 | bytes 1402880 | tf_op jit(solution)/shard_map/conv_general_dilated | solution.py:107
  114.4 0.3 fusion.50
  114.7 1.6 %collective-permute-done.26 = bf16[864,128]{1,0:T(8,128)(2,1)S(1)} collective-permute-done((bf16[864,128]{1,0:T(8,128)(2,1)S(1)}, bf16[864,128]{1,0:T(8,128)(2,1)S(1)}, u32[]{:S(2)}, u32[]{:S(2)}) %collective-permute-start.26) | collective-permute-done | bytes 221216 | tf_op jit(solution)/shard_map/ppermute | solution.py:150
  116.3 5.8 %collective-permute-done.25 = bf16[864,128]{1,0:T(8,128)(2,1)S(1)} collective-permute-done((bf16[864,128]{1,0:T(8,128)(2,1)S(1)}, bf16[864,128]{1,0:T(8,128)(2,1)S(1)}, u32[]{:S(2)}, u32[]{:S(2)}) %collective-permute-start.25) | collective-permute-done | bytes 221216 | tf_op jit(solution)/shard_map/ppermute | solution.py:150
  122.1 1.6 %collective-permute-start.27 = (f32[864,128]{1,0:T(8,128)S(1)}, f32[864,128]{1,0:T(8,128)S(1)}, u32[]{:S(2)}, u32[]{:S(2)}) collective-permute-start(f32[864,128]{1,0:T(8,128)S(1)} %convert_add_fusion), channel_id=1, source_target_pairs={{0,1},{1,0},{2,3},{3,2},{4,5},{5,4},{6,7},{7,6},{8,9},{9,8},{10,11... | collective-permute-start | bytes 1327112 | tf_op jit(solution)/shard_map/ppermute | solution.py:233
  123.8 1.0 fusion.53
  124.8 0.4 collective-permute-done.27
  125.2 0.8 add_bitcast_fusion
  (206 shorter events, 4.3 us)
Async XLA Ops:
  0.6 8.5 %copy-start.5 = (bf16[1,864,128]{2,1,0:T(8,128)(2,1)S(1)}, bf16[1,864,128]{2,1,0:T(8,128)(2,1)}, u32[]{:S(2)}) copy-start(bf16[1,864,128]{2,1,0:T(8,128)(2,1)} %param.11) | copy-start | bytes 663556
  2.8 11.4 %copy-start.10 = (s32[1,1,1,1,27]{4,3,2,1,0:T(1,128)S(1)}, s32[1,1,1,1,27]{4,3,2,1,0:T(1,128)}, u32[]{:S(2)}) copy-start(s32[1,1,1,1,27]{4,3,2,1,0:T(1,128)} %param.8) | copy-start | bytes 328
  4.5 11.2 %copy-start.11 = (f32[1,128]{1,0:T(1,128)S(1)}, f32[1,128]{1,0:T(1,128)}, u32[]{:S(2)}) copy-start(f32[1,128]{1,0:T(1,128)} %param.10) | copy-start | bytes 1540
  5.5 30.4 %collective-permute-start = (bf16[1,1,1,8,256]{4,3,2,1,0:T(8,128)(2,1)S(1)}, bf16[1,1,1,8,256]{4,3,2,1,0:T(8,128)(2,1)S(1)}, u32[]{:S(2)}, u32[]{:S(2)}) collective-permute-start(bf16[1,1,1,8,256]{4,3,2,1,0:T(8,128)(2,1)S(1)} %constant_dynamic-slice_fusion.13), channel_id=1, source_target_pairs={{0,3},{1,2},{2,5},{3,4},{4,7},{5,6},{8,11},{9,10},{10,13},{11,12},... | collective-permute-start | bytes 12296 | tf_op jit(solution)/shard_map/ppermute | solution.py:73
  9.2 29.2 %collective-permute-start.5 = (bf16[864,128]{1,0:T(8,128)(2,1)S(1)}, bf16[864,128]{1,0:T(8,128)(2,1)}, u32[]{:S(2)}, u32[]{:S(2)}) collective-permute-start(bf16[864,128]{1,0:T(8,128)(2,1)S(1)} %bitcast.223), channel_id=1, source_target_pairs={{0,4},{2,6},{4,0},{6,2},{1,5},{3,7},{5,1},{7,3},{8,12},{10,14},{12... | collective-permute-start | bytes 663560 | tf_op jit(solution)/shard_map/ppermute | solution.py:136
  9.5 6.6 %copy-start.1 = (bf16[1,1,1,512,128]{4,3,2,1,0:T(8,128)(2,1)S(1)}, bf16[1,1,1,512,128]{4,3,2,1,0:T(8,128)(2,1)}, u32[]{:S(2)}) copy-start(bf16[1,1,1,512,128]{4,3,2,1,0:T(8,128)(2,1)} %param.7) | copy-start | bytes 393220
  9.5 28.1 %collective-permute-start.1 = (bf16[992,128]{1,0:T(8,128)(2,1)S(1)}, bf16[992,128]{1,0:T(8,128)(2,1)S(1)}, u32[]{:S(2)}, u32[]{:S(2)}) collective-permute-start(bf16[992,128]{1,0:T(8,128)(2,1)S(1)} %get-tuple-element.40), channel_id=1, source_target_pairs={{0,2},{1,3},{2,4},{3,5},{4,6},{5,7},{6,0},{7,1},{8,10},{9,11},{10,... | collective-permute-start | bytes 761864 | tf_op jit(solution)/shard_map/ppermute | solution.py:73
  10.8 25.7 %collective-permute-start.2 = (bf16[1,1,1,8,256]{4,3,2,1,0:T(8,128)(2,1)S(1)}, bf16[1,1,1,8,256]{4,3,2,1,0:T(8,128)(2,1)S(1)}, u32[]{:S(2)}, u32[]{:S(2)}) collective-permute-start(bf16[1,1,1,8,256]{4,3,2,1,0:T(8,128)(2,1)S(1)} %constant_dynamic-slice_fusion.12), channel_id=1, source_target_pairs={{2,1},{3,0},{4,3},{5,2},{6,5},{7,4},{10,9},{11,8},{12,11},{13,10},... | collective-permute-start | bytes 12296 | tf_op jit(solution)/shard_map/ppermute | solution.py:73
  14.1 23.6 %collective-permute-start.3 = (bf16[992,128]{1,0:T(8,128)(2,1)S(1)}, bf16[992,128]{1,0:T(8,128)(2,1)S(1)}, u32[]{:S(2)}, u32[]{:S(2)}) collective-permute-start(bf16[992,128]{1,0:T(8,128)(2,1)S(1)} %get-tuple-element.39), channel_id=1, source_target_pairs={{0,6},{1,7},{2,0},{3,1},{4,2},{5,3},{6,4},{7,5},{8,14},{9,15},{10,... | collective-permute-start | bytes 761864 | tf_op jit(solution)/shard_map/ppermute | solution.py:73
  35.9 1.4 %collective-permute-start.4 = (bf16[1,8,1,8,256]{4,3,2,1,0:T(8,128)(2,1)S(1)}, bf16[1,8,1,8,256]{4,3,2,1,0:T(8,128)(2,1)S(1)}, u32[]{:S(2)}, u32[]{:S(2)}) collective-permute-start(bf16[1,8,1,8,256]{4,3,2,1,0:T(8,128)(2,1)S(1)} %fusion.57), channel_id=1, source_target_pairs={{0,1},{1,0},{2,3},{3,2},{4,5},{5,4},{6,7},{7,6},{8,9},{9,8},{10,11... | collective-permute-start | bytes 98312 | tf_op jit(solution)/shard_map/ppermute | solution.py:73
  41.3 2.1 %copy-start.4 = (bf16[3,3,3,128,128]{4,3,2,1,0:T(8,128)(2,1)S(1)}, bf16[3,3,3,128,128]{4,3,2,1,0:T(8,128)(2,1)}, u32[]{:S(2)}) copy-start(bf16[3,3,3,128,128]{4,3,2,1,0:T(8,128)(2,1)} %rev.3) | copy-start | bytes 2654212
  43.4 3.0 %copy-start.2 = (bf16[1,10,10,10,256]{4,0,3,2,1:T(2,128)(2,1)}, bf16[1,10,10,10,256]{4,0,3,2,1:T(2,128)(2,1)S(1)}, u32[]{:S(2)}) copy-start(bf16[1,10,10,10,256]{4,0,3,2,1:T(2,128)(2,1)S(1)} %pad_maximum_fusion) | copy-start | bytes 1536004
  43.4 3.0 %copy-start = (bf16[1,1,1,1,512,128]{5,4,3,2,1,0:T(8,128)(2,1)S(1)}, bf16[1,1,1,1,512,128]{5,4,3,2,1,0:T(8,128)(2,1)}, u32[]{:S(2)}) copy-start(bf16[1,1,1,1,512,128]{5,4,3,2,1,0:T(8,128)(2,1)} %param.6) | copy-start | bytes 393220
  46.4 9.5 %copy-start.12 = (pred[512]{0:T(512)(128)(4,1)S(1)}, pred[512]{0:T(512)(128)(4,1)}, u32[]{:S(2)}) copy-start(pred[512]{0:T(512)(128)(4,1)} %fusion.60) | copy-start | bytes 1540
  47.2 19.7 %collective-permute-start.11 = (bf16[1,1,8,8,128]{4,3,2,1,0:T(8,128)(2,1)S(1)}, bf16[1,1,8,8,128]{4,3,2,1,0:T(8,128)(2,1)S(1)}, u32[]{:S(2)}, u32[]{:S(2)}) collective-permute-start(bf16[1,1,8,8,128]{4,3,2,1,0:T(8,128)(2,1)S(1)} %get-tuple-element.52), channel_id=1, source_target_pairs={{10,0},{11,1},{12,2},{13,3},{14,4},{15,5},{18,8},{19,9},{20,10},{2... | collective-permute-start | bytes 49160 | tf_op jit(solution)/shard_map/ppermute | solution.py:73
  49.2 17.9 %collective-permute-start.8 = (bf16[1,1,8,8,128]{4,3,2,1,0:T(8,128)(2,1)S(1)}, bf16[1,1,8,8,128]{4,3,2,1,0:T(8,128)(2,1)S(1)}, u32[]{:S(2)}, u32[]{:S(2)}) collective-permute-start(bf16[1,1,8,8,128]{4,3,2,1,0:T(8,128)(2,1)S(1)} %get-tuple-element.51), channel_id=1, source_target_pairs={{8,2},{9,3},{10,4},{11,5},{12,6},{13,7},{16,10},{17,11},{18,12},{1... | collective-permute-start | bytes 49160 | tf_op jit(solution)/shard_map/ppermute | solution.py:73
  52.3 7.8 %collective-permute-start.10 = (bf16[1,1,1,8,128]{4,3,2,1,0:T(8,128)(2,1)S(1)}, bf16[1,1,1,8,128]{4,3,2,1,0:T(8,128)(2,1)S(1)}, u32[]{:S(2)}, u32[]{:S(2)}) collective-permute-start(bf16[1,1,1,8,128]{4,3,2,1,0:T(8,128)(2,1)S(1)} %constant_dynamic-slice_fusion.9), channel_id=1, source_target_pairs={{10,1},{11,0},{12,3},{13,2},{14,5},{15,4},{18,9},{19,8},{20,11},{2... | collective-permute-start | bytes 6152 | tf_op jit(solution)/shard_map/ppermute | solution.py:73
  56.2 14.4 %copy-start.8 = (bf16[512,128]{1,0:T(8,128)(2,1)}, bf16[512,128]{1,0:T(8,128)(2,1)S(1)}, u32[]{:S(2)}) copy-start(bf16[512,128]{1,0:T(8,128)(2,1)S(1)} %fusion.8) | copy-start | bytes 393220
  56.2 11.1 %collective-permute-start.6 = (bf16[512,128]{1,0:T(8,128)(2,1)S(1)}, bf16[512,128]{1,0:T(8,128)(2,1)S(1)}, u32[]{:S(2)}, u32[]{:S(2)}) collective-permute-start(bf16[512,128]{1,0:T(8,128)(2,1)S(1)} %fusion.8), channel_id=1, source_target_pairs={{8,0},{16,8},{24,16},{9,1},{17,9},{25,17},{10,2},{18,10},{26,18},{... | collective-permute-start | bytes 393224 | tf_op jit(solution)/shard_map/ppermute | solution.py:228
  58.2 8.8 %collective-permute-start.9 = (bf16[1,8,1,8,128]{4,3,2,1,0:T(8,128)(2,1)S(1)}, bf16[1,8,1,8,128]{4,3,2,1,0:T(8,128)(2,1)S(1)}, u32[]{:S(2)}, u32[]{:S(2)}) collective-permute-start(bf16[1,8,1,8,128]{4,3,2,1,0:T(8,128)(2,1)S(1)} %constant_dynamic-slice_fusion.10), channel_id=1, source_target_pairs={{8,1},{9,0},{10,3},{11,2},{12,5},{13,4},{14,7},{15,6},{16,9},{17,8... | collective-permute-start | bytes 49160 | tf_op jit(solution)/shard_map/ppermute | solution.py:73
  60.1 6.7 %collective-permute-start.7 = (bf16[1,1,1,8,128]{4,3,2,1,0:T(8,128)(2,1)S(1)}, bf16[1,1,1,8,128]{4,3,2,1,0:T(8,128)(2,1)S(1)}, u32[]{:S(2)}, u32[]{:S(2)}) collective-permute-start(bf16[1,1,1,8,128]{4,3,2,1,0:T(8,128)(2,1)S(1)} %constant_dynamic-slice_fusion.11), channel_id=1, source_target_pairs={{8,3},{9,2},{10,5},{11,4},{12,7},{13,6},{16,11},{17,10},{18,13},{1... | collective-permute-start | bytes 6152 | tf_op jit(solution)/shard_map/ppermute | solution.py:73
  71.3 20.3 %copy-start.6 = (bf16[512,128]{1,0:T(8,128)(2,1)}, bf16[512,128]{1,0:T(8,128)(2,1)S(1)}, u32[]{:S(2)}) copy-start(bf16[512,128]{1,0:T(8,128)(2,1)S(1)} %fusion.18) | copy-start | bytes 393220
  71.3 17.0 %collective-permute-start.12 = (bf16[512,128]{1,0:T(8,128)(2,1)S(1)}, bf16[512,128]{1,0:T(8,128)(2,1)S(1)}, u32[]{:S(2)}, u32[]{:S(2)}) collective-permute-start(bf16[512,128]{1,0:T(8,128)(2,1)S(1)} %fusion.18), channel_id=1, source_target_pairs={{8,0},{16,8},{24,16},{9,1},{17,9},{25,17},{10,2},{18,10},{26,18},{... | collective-permute-start | bytes 393224 | tf_op jit(solution)/shard_map/ppermute | solution.py:228
  73.3 14.6 %collective-permute-start.17 = (bf16[1,1,8,8,128]{4,3,2,1,0:T(8,128)(2,1)S(1)}, bf16[1,1,8,8,128]{4,3,2,1,0:T(8,128)(2,1)S(1)}, u32[]{:S(2)}, u32[]{:S(2)}) collective-permute-start(bf16[1,1,8,8,128]{4,3,2,1,0:T(8,128)(2,1)S(1)} %get-tuple-element.47), channel_id=1, source_target_pairs={{10,0},{11,1},{12,2},{13,3},{14,4},{15,5},{18,8},{19,9},{20,10},{2... | collective-permute-start | bytes 49160 | tf_op jit(solution)/shard_map/ppermute | solution.py:73
  75.3 5.8 %collective-permute-start.16 = (bf16[1,1,1,8,128]{4,3,2,1,0:T(8,128)(2,1)S(1)}, bf16[1,1,1,8,128]{4,3,2,1,0:T(8,128)(2,1)S(1)}, u32[]{:S(2)}, u32[]{:S(2)}) collective-permute-start(bf16[1,1,1,8,128]{4,3,2,1,0:T(8,128)(2,1)S(1)} %constant_dynamic-slice_fusion.6), channel_id=1, source_target_pairs={{10,1},{11,0},{12,3},{13,2},{14,5},{15,4},{18,9},{19,8},{20,11},{2... | collective-permute-start | bytes 6152 | tf_op jit(solution)/shard_map/ppermute | solution.py:73
  77.2 10.8 %collective-permute-start.14 = (bf16[1,1,8,8,128]{4,3,2,1,0:T(8,128)(2,1)S(1)}, bf16[1,1,8,8,128]{4,3,2,1,0:T(8,128)(2,1)S(1)}, u32[]{:S(2)}, u32[]{:S(2)}) collective-permute-start(bf16[1,1,8,8,128]{4,3,2,1,0:T(8,128)(2,1)S(1)} %get-tuple-element.46), channel_id=1, source_target_pairs={{8,2},{9,3},{10,4},{11,5},{12,6},{13,7},{16,10},{17,11},{18,12},{1... | collective-permute-start | bytes 49160 | tf_op jit(solution)/shard_map/ppermute | solution.py:73
  79.1 8.8 %collective-permute-start.15 = (bf16[1,8,1,8,128]{4,3,2,1,0:T(8,128)(2,1)S(1)}, bf16[1,8,1,8,128]{4,3,2,1,0:T(8,128)(2,1)S(1)}, u32[]{:S(2)}, u32[]{:S(2)}) collective-permute-start(bf16[1,8,1,8,128]{4,3,2,1,0:T(8,128)(2,1)S(1)} %constant_dynamic-slice_fusion.7), channel_id=1, source_target_pairs={{8,1},{9,0},{10,3},{11,2},{12,5},{13,4},{14,7},{15,6},{16,9},{17,8... | collective-permute-start | bytes 49160 | tf_op jit(solution)/shard_map/ppermute | solution.py:73
  81.1 6.7 %collective-permute-start.13 = (bf16[1,1,1,8,128]{4,3,2,1,0:T(8,128)(2,1)S(1)}, bf16[1,1,1,8,128]{4,3,2,1,0:T(8,128)(2,1)S(1)}, u32[]{:S(2)}, u32[]{:S(2)}) collective-permute-start(bf16[1,1,1,8,128]{4,3,2,1,0:T(8,128)(2,1)S(1)} %constant_dynamic-slice_fusion.8), channel_id=1, source_target_pairs={{8,3},{9,2},{10,5},{11,4},{12,7},{13,6},{16,11},{17,10},{18,13},{1... | collective-permute-start | bytes 6152 | tf_op jit(solution)/shard_map/ppermute | solution.py:73
  91.6 13.0 %copy-start.3 = (bf16[1,10,10,10,256]{4,0,3,2,1:T(2,128)(2,1)S(1)}, bf16[1,10,10,10,256]{4,0,3,2,1:T(2,128)(2,1)}, u32[]{:S(2)}) copy-start(bf16[1,10,10,10,256]{4,0,3,2,1:T(2,128)(2,1)} %copy-done.2) | copy-start | bytes 1536004
  92.3 9.7 %collective-permute-start.18 = (bf16[512,128]{1,0:T(8,128)(2,1)S(1)}, bf16[512,128]{1,0:T(8,128)(2,1)S(1)}, u32[]{:S(2)}, u32[]{:S(2)}) collective-permute-start(bf16[512,128]{1,0:T(8,128)(2,1)S(1)} %fusion.21), channel_id=1, source_target_pairs={{8,0},{16,8},{24,16},{9,1},{17,9},{25,17},{10,2},{18,10},{26,18},{... | collective-permute-start | bytes 393224 | tf_op jit(solution)/shard_map/ppermute | solution.py:228
  94.3 14.3 %collective-permute-start.20 = (bf16[1,1,8,8,128]{4,3,2,1,0:T(8,128)(2,1)S(1)}, bf16[1,1,8,8,128]{4,3,2,1,0:T(8,128)(2,1)S(1)}, u32[]{:S(2)}, u32[]{:S(2)}) collective-permute-start(bf16[1,1,8,8,128]{4,3,2,1,0:T(8,128)(2,1)S(1)} %get-tuple-element.45), channel_id=1, source_target_pairs={{8,2},{9,3},{10,4},{11,5},{12,6},{13,7},{16,10},{17,11},{18,12},{1... | collective-permute-start | bytes 49160 | tf_op jit(solution)/shard_map/ppermute | solution.py:73
  96.2 12.3 %collective-permute-start.19 = (bf16[1,1,1,8,128]{4,3,2,1,0:T(8,128)(2,1)S(1)}, bf16[1,1,1,8,128]{4,3,2,1,0:T(8,128)(2,1)S(1)}, u32[]{:S(2)}, u32[]{:S(2)}) collective-permute-start(bf16[1,1,1,8,128]{4,3,2,1,0:T(8,128)(2,1)S(1)} %constant_dynamic-slice_fusion.5), channel_id=1, source_target_pairs={{8,3},{9,2},{10,5},{11,4},{12,7},{13,6},{16,11},{17,10},{18,13},{1... | collective-permute-start | bytes 6152 | tf_op jit(solution)/shard_map/ppermute | solution.py:73
  98.1 10.4 %collective-permute-start.21 = (bf16[1,8,1,8,128]{4,3,2,1,0:T(8,128)(2,1)S(1)}, bf16[1,8,1,8,128]{4,3,2,1,0:T(8,128)(2,1)S(1)}, u32[]{:S(2)}, u32[]{:S(2)}) collective-permute-start(bf16[1,8,1,8,128]{4,3,2,1,0:T(8,128)(2,1)S(1)} %constant_dynamic-slice_fusion.4), channel_id=1, source_target_pairs={{8,1},{9,0},{10,3},{11,2},{12,5},{13,4},{14,7},{15,6},{16,9},{17,8... | collective-permute-start | bytes 49160 | tf_op jit(solution)/shard_map/ppermute | solution.py:73
  100.1 8.5 %collective-permute-start.23 = (bf16[1,1,8,8,128]{4,3,2,1,0:T(8,128)(2,1)S(1)}, bf16[1,1,8,8,128]{4,3,2,1,0:T(8,128)(2,1)S(1)}, u32[]{:S(2)}, u32[]{:S(2)}) collective-permute-start(bf16[1,1,8,8,128]{4,3,2,1,0:T(8,128)(2,1)S(1)} %get-tuple-element.44), channel_id=1, source_target_pairs={{10,0},{11,1},{12,2},{13,3},{14,4},{15,5},{18,8},{19,9},{20,10},{2... | collective-permute-start | bytes 49160 | tf_op jit(solution)/shard_map/ppermute | solution.py:73
  102.0 6.5 %collective-permute-start.22 = (bf16[1,1,1,8,128]{4,3,2,1,0:T(8,128)(2,1)S(1)}, bf16[1,1,1,8,128]{4,3,2,1,0:T(8,128)(2,1)S(1)}, u32[]{:S(2)}, u32[]{:S(2)}) collective-permute-start(bf16[1,1,1,8,128]{4,3,2,1,0:T(8,128)(2,1)S(1)} %constant_dynamic-slice_fusion.3), channel_id=1, source_target_pairs={{10,1},{11,0},{12,3},{13,2},{14,5},{15,4},{18,9},{19,8},{20,11},{2... | collective-permute-start | bytes 6152 | tf_op jit(solution)/shard_map/ppermute | solution.py:73
  109.6 6.7 %collective-permute-start.26 = (bf16[864,128]{1,0:T(8,128)(2,1)S(1)}, bf16[864,128]{1,0:T(8,128)(2,1)S(1)}, u32[]{:S(2)}, u32[]{:S(2)}) collective-permute-start(bf16[864,128]{1,0:T(8,128)(2,1)S(1)} %get-tuple-element.27), channel_id=1, source_target_pairs={{0,6},{2,0},{4,2},{6,4},{1,7},{3,1},{5,3},{7,5},{8,14},{10,8},{12,... | collective-permute-start | bytes 663560 | tf_op jit(solution)/shard_map/ppermute | solution.py:150
  111.0 11.0 %collective-permute-start.25 = (bf16[864,128]{1,0:T(8,128)(2,1)S(1)}, bf16[864,128]{1,0:T(8,128)(2,1)S(1)}, u32[]{:S(2)}, u32[]{:S(2)}) collective-permute-start(bf16[864,128]{1,0:T(8,128)(2,1)S(1)} %get-tuple-element.28), channel_id=1, source_target_pairs={{0,4},{2,6},{4,0},{6,2},{1,5},{3,7},{5,1},{7,3},{8,12},{10,14},{12... | collective-permute-start | bytes 663560 | tf_op jit(solution)/shard_map/ppermute | solution.py:150
  111.0 11.0 %collective-permute-start.24 = (bf16[864,128]{1,0:T(8,128)(2,1)S(1)}, bf16[864,128]{1,0:T(8,128)(2,1)S(1)}, u32[]{:S(2)}, u32[]{:S(2)}) collective-permute-start(bf16[864,128]{1,0:T(8,128)(2,1)S(1)} %get-tuple-element.26), channel_id=1, source_target_pairs={{0,2},{2,4},{4,6},{6,0},{1,3},{3,5},{5,7},{7,1},{8,10},{10,12},{12... | collective-permute-start | bytes 663560 | tf_op jit(solution)/shard_map/ppermute | solution.py:150
  114.3 9.4 %copy-start.7 = (bf16[512,128]{1,0:T(8,128)(2,1)S(1)}, bf16[512,128]{1,0:T(8,128)(2,1)}, u32[]{:S(2)}) copy-start(bf16[512,128]{1,0:T(8,128)(2,1)} %copy-done.6) | copy-start | bytes 393220
  114.4 9.4 %copy-start.9 = (bf16[512,128]{1,0:T(8,128)(2,1)S(1)}, bf16[512,128]{1,0:T(8,128)(2,1)}, u32[]{:S(2)}) copy-start(bf16[512,128]{1,0:T(8,128)(2,1)} %copy-done.8) | copy-start | bytes 393220
  122.1 3.0 %collective-permute-start.27 = (f32[864,128]{1,0:T(8,128)S(1)}, f32[864,128]{1,0:T(8,128)S(1)}, u32[]{:S(2)}, u32[]{:S(2)}) collective-permute-start(f32[864,128]{1,0:T(8,128)S(1)} %convert_add_fusion), channel_id=1, source_target_pairs={{0,1},{1,0},{2,3},{3,2},{4,5},{5,4},{6,7},{7,6},{8,9},{9,8},{10,11... | collective-permute-start | bytes 1327112 | tf_op jit(solution)/shard_map/ppermute | solution.py:233

commit v14 on v13

--- a/solution.py
+++ b/solution.py
@@ -88,7 +88,8 @@
         for shift_x in OFFSETS:
             if shift_x != 0:
                 received[(shift_x, 0)] = face_x(shift_x)
-            row = lax.dynamic_slice_in_dim(cube[:, source_range(shift_x)], (1 - place_y) * 7, 1, axis=2)
+            plane = cube[:, source_range(shift_x)]
+            row = jnp.where(place_y == 0, plane[:, :, 7:8], plane[:, :, 0:1])
             got = send(row, lambda a, b, i=shift_x: (a - i, 1 - b))
             received[(shift_x, 1)] = got
             received[(shift_x, -1)] = got

time: 128 us -> 128 us (level)
  the two profiles are of different devices: /device:TPU:21 before, /device:TPU:25 now
where the time goes in v14:
time: 128 us; the launch traced here: 127 us
  starting transfers between devices  61.4 us (48%)
  between operations  19.7 us (15%)
  matrix products  15.7 us (12%)
  other arithmetic  15.3 us (12%)
  waiting for transfers between devices  8.04 us (6%)
  local copies, waits for them, and re-layouts  6.53 us (5%)
    ppermute x20, starting transfers between devices, send(): return lax.ppermute(piece, axes, route)  46 us
    conv_general_dilated x4, matrix products, conv_data(): lax.conv_general_dilated(padded, filters, (1, 1, 1), 'VALID', dimension_n...  11.8 us
    ppermute x3, waiting for transfers between devices, scattered_sum(): lax.ppermute(piece, axis, [(i, (i + step) % count) for i in range(count)])  6.02 us
    ppermute x3, starting transfers between devices, shards(): centre = lax.ppermute(result, 'pipe', down)  5.88 us
    ppermute x3, starting transfers between devices, scattered_sum(): lax.ppermute(piece, axis, [(i, (i + step) % count) for i in range(count)])  5.85 us
    transpose x1, matrix products, shards(): per_tap.transpose(1, 2, 3, 0, 4).reshape(taps * channels, channels)  3.93 us
  transfers between devices with their start and end apart: 28, of which 6 were waited for; matrix products, arithmetic and copies ran while one was open for 12% of the time, Pallas kernels for 0%

profile of v14, /device:TPU:25, one launch (start us, length us, event | category | flops | bytes accessed | tf_op | source)
XLA Modules:
  0.0 126.8 jit_solution(13023230705684508700)
XLA Ops:
  0.6 1.0 convert_element_type.160
  1.6 1.1 fusion.25
  3.5 1.0 broadcast_select_fusion.12
  4.5 0.8 multiply_convert_fusion.2
  5.4 3.7 %collective-permute-start = (bf16[1,1,1,8,256]{4,3,2,1,0:T(8,128)(2,1)S(1)}, bf16[1,1,1,8,256]{4,3,2,1,0:T(8,128)(2,1)S(1)}, u32[]{:S(2)}, u32[]{:S(2)}) collective-permute-start(bf16[1,1,1,8,256]{4,3,2,1,0:T(8,128)(2,1)S(1)} %get-tuple-element.34), channel_id=1, source_target_pairs={{0,3},{1,2},{2,5},{3,4},{4,7},{5,6},{8,11},{9,10},{10,13},{11,12},... | collective-permute-start | bytes 12296 | tf_op jit(solution)/shard_map/ppermute | solution.py:73
  9.1 1.3 %collective-permute-start.5 = (bf16[864,128]{1,0:T(8,128)(2,1)S(1)}, bf16[864,128]{1,0:T(8,128)(2,1)}, u32[]{:S(2)}, u32[]{:S(2)}) collective-permute-start(bf16[864,128]{1,0:T(8,128)(2,1)S(1)} %bitcast.223), channel_id=1, source_target_pairs={{0,4},{2,6},{4,0},{6,2},{1,5},{3,7},{5,1},{7,3},{8,12},{10,14},{12... | collective-permute-start | bytes 663560 | tf_op jit(solution)/shard_map/ppermute | solution.py:137
  10.6 1.3 %collective-permute-start.2 = (bf16[1,1,1,8,256]{4,3,2,1,0:T(8,128)(2,1)S(1)}, bf16[1,1,1,8,256]{4,3,2,1,0:T(8,128)(2,1)S(1)}, u32[]{:S(2)}, u32[]{:S(2)}) collective-permute-start(bf16[1,1,1,8,256]{4,3,2,1,0:T(8,128)(2,1)S(1)} %get-tuple-element.33), channel_id=1, source_target_pairs={{2,1},{3,0},{4,3},{5,2},{6,5},{7,4},{10,9},{11,8},{12,11},{13,10},... | collective-permute-start | bytes 12296 | tf_op jit(solution)/shard_map/ppermute | solution.py:73
  11.9 3.5 %collective-permute-start.3 = (bf16[992,128]{1,0:T(8,128)(2,1)S(1)}, bf16[992,128]{1,0:T(8,128)(2,1)S(1)}, u32[]{:S(2)}, u32[]{:S(2)}) collective-permute-start(bf16[992,128]{1,0:T(8,128)(2,1)S(1)} %get-tuple-element.41), channel_id=1, source_target_pairs={{0,6},{1,7},{2,0},{3,1},{4,2},{5,3},{6,4},{7,5},{8,14},{9,15},{10,... | collective-permute-start | bytes 761864 | tf_op jit(solution)/shard_map/ppermute | solution.py:73
  15.4 0.7 fusion.74
  16.1 0.7 fusion.73
  17.0 0.2 copy_dynamic-update-slice_fusion.1
  19.3 0.6 scatter_custom_fusion
  20.0 0.6 pad_clamp_fusion
  20.6 0.5 fusion.58
  21.1 0.4 copy_dynamic-update-slice_fusion
  21.5 0.6 broadcast_select_fusion
  37.0 0.5 collective-permute-start.4
  37.7 0.7 collective-permute-done.4
  39.4 1.0 pad_maximum_fusion.1
  40.4 0.8 gather_fusion
  41.3 1.1 rev.3
  42.3 2.1 %pad_maximum_fusion = bf16[1,10,10,10,256]{4,0,3,2,1:T(2,128)(2,1)S(1)} fusion(bf16[1,1,10,10,256]{4,0,3,2,1:T(2,128)(2,1)S(1)} %pad_maximum_fusion.11, bf16[1,8,1,10,256]{4,0,3,2,1:T(2,128)(2,1)S(1)} %copy.57, bf16[1,8,8,1,256]{4,0,3,2,1:T(2,128)(2,1)S(1)} %get-tuple-element.30, bf16[1,8,8,8,256]{4,0,3,2,1:T(2,128)(2,1)S(1)} %broadcast_select_fusion, ...), kind=kLoop, calls=%fused_computation.4 | loop fusion | flops 1536000 | bytes 1024000 | tf_op jit(solution)/shard_map/concatenate | solution.py:56
  44.5 3.0 %fusion.1 = f32[1,8,8,8,128]{4,0,3,2,1:T(1,128)S(1)} fusion(bf16[3,3,3,128,128]{4,3,2,1,0:T(8,128)(2,1)S(1)} %copy-done.4, bf16[1,10,10,10,256]{4,0,3,2,1:T(2,128)(2,1)S(1)} %pad_maximum_fusion), kind=kOutput, calls=%fused_computation.10 | convolution fusion | flops 452984832 | bytes 1658880 | tf_op jit(solution)/shard_map/conv_general_dilated | solution.py:108
  47.5 0.3 fusion.47
  47.9 0.3 fusion.15
  48.3 0.7 collective-permute-start.10
  49.0 0.3 fusion.8
  49.3 2.7 %collective-permute-start.6 = (bf16[512,128]{1,0:T(8,128)(2,1)S(1)}, bf16[512,128]{1,0:T(8,128)(2,1)S(1)}, u32[]{:S(2)}, u32[]{:S(2)}) collective-permute-start(bf16[512,128]{1,0:T(8,128)(2,1)S(1)} %fusion.8), channel_id=1, source_target_pairs={{8,0},{16,8},{24,16},{9,1},{17,9},{25,17},{10,2},{18,10},{26,18},{... | collective-permute-start | bytes 393224 | tf_op jit(solution)/shard_map/ppermute | solution.py:229
  52.0 0.7 collective-permute-start.11
  52.7 3.2 %collective-permute-start.9 = (bf16[1,8,1,8,128]{4,3,2,1,0:T(8,128)(2,1)S(1)}, bf16[1,8,1,8,128]{4,3,2,1,0:T(8,128)(2,1)S(1)}, u32[]{:S(2)}, u32[]{:S(2)}) collective-permute-start(bf16[1,8,1,8,128]{4,3,2,1,0:T(8,128)(2,1)S(1)} %slice_select_fusion.2), channel_id=1, source_target_pairs={{8,1},{9,0},{10,3},{11,2},{12,5},{13,4},{14,7},{15,6},{16,9},{17,8... | collective-permute-start | bytes 49160 | tf_op jit(solution)/shard_map/ppermute | solution.py:73
  55.9 4.3 %collective-permute-start.7 = (bf16[1,1,1,8,128]{4,3,2,1,0:T(8,128)(2,1)S(1)}, bf16[1,1,1,8,128]{4,3,2,1,0:T(8,128)(2,1)S(1)}, u32[]{:S(2)}, u32[]{:S(2)}) collective-permute-start(bf16[1,1,1,8,128]{4,3,2,1,0:T(8,128)(2,1)S(1)} %get-tuple-element.59), channel_id=1, source_target_pairs={{8,3},{9,2},{10,5},{11,4},{12,7},{13,6},{16,11},{17,10},{18,13},{1... | collective-permute-start | bytes 6152 | tf_op jit(solution)/shard_map/ppermute | solution.py:73
  60.2 1.8 %collective-permute-start.8 = (bf16[1,1,8,8,128]{4,3,2,1,0:T(8,128)(2,1)S(1)}, bf16[1,1,8,8,128]{4,3,2,1,0:T(8,128)(2,1)S(1)}, u32[]{:S(2)}, u32[]{:S(2)}) collective-permute-start(bf16[1,1,8,8,128]{4,3,2,1,0:T(8,128)(2,1)S(1)} %get-tuple-element.57), channel_id=1, source_target_pairs={{8,2},{9,3},{10,4},{11,5},{12,6},{13,7},{16,10},{17,11},{18,12},{1... | collective-permute-start | bytes 49160 | tf_op jit(solution)/shard_map/ppermute | solution.py:73
  62.3 0.4 collective-permute-done.8
  63.3 2.9 %fusion.5 = f32[1,8,8,8,128]{4,0,3,2,1:T(1,128)S(1)} fusion(bf16[3,3,3,128,128]{4,3,2,1,0:T(8,128)(2,1)S(1)} %bitcast.208, bf16[1,1,10,10,128]{4,0,3,2,1:T(2,128)(2,1)S(1)} %copy.66, bf16[1,8,1,10,128]{4,0,3,2,1:T(2,128)(2,1)S(1)} %copy.64, bf16[1,8,8,1,128]{4,0,3,2,1:T(2,128)(2,1)S(1)} %slice_bitcast_fusion.6, bf16[1,8,8,8,128]{4,0,3,2,1:T(2,128)(2,1)S(1)} %copy.62, ...), kind=kOutput, calls=%fused_computation.14 | convolution fusion | flops 454776832 | bytes 1402880 | tf_op jit(solution)/shard_map/conv_general_dilated | solution.py:108
  66.3 0.3 fusion.48
  66.6 0.3 fusion.18
  67.0 1.9 %collective-permute-start.12 = (bf16[512,128]{1,0:T(8,128)(2,1)S(1)}, bf16[512,128]{1,0:T(8,128)(2,1)S(1)}, u32[]{:S(2)}, u32[]{:S(2)}) collective-permute-start(bf16[512,128]{1,0:T(8,128)(2,1)S(1)} %fusion.18), channel_id=1, source_target_pairs={{8,0},{16,8},{24,16},{9,1},{17,9},{25,17},{10,2},{18,10},{26,18},{... | collective-permute-start | bytes 393224 | tf_op jit(solution)/shard_map/ppermute | solution.py:229
  68.9 0.7 collective-permute-start.16
  69.6 0.7 collective-permute-start.17
  70.2 4.1 %collective-permute-start.15 = (bf16[1,8,1,8,128]{4,3,2,1,0:T(8,128)(2,1)S(1)}, bf16[1,8,1,8,128]{4,3,2,1,0:T(8,128)(2,1)S(1)}, u32[]{:S(2)}, u32[]{:S(2)}) collective-permute-start(bf16[1,8,1,8,128]{4,3,2,1,0:T(8,128)(2,1)S(1)} %slice_select_fusion.1), channel_id=1, source_target_pairs={{8,1},{9,0},{10,3},{11,2},{12,5},{13,4},{14,7},{15,6},{16,9},{17,8... | collective-permute-start | bytes 49160 | tf_op jit(solution)/shard_map/ppermute | solution.py:73
  74.3 6.4 %collective-permute-start.13 = (bf16[1,1,1,8,128]{4,3,2,1,0:T(8,128)(2,1)S(1)}, bf16[1,1,1,8,128]{4,3,2,1,0:T(8,128)(2,1)S(1)}, u32[]{:S(2)}, u32[]{:S(2)}) collective-permute-start(bf16[1,1,1,8,128]{4,3,2,1,0:T(8,128)(2,1)S(1)} %get-tuple-element.52), channel_id=1, source_target_pairs={{8,3},{9,2},{10,5},{11,4},{12,7},{13,6},{16,11},{17,10},{18,13},{1... | collective-permute-start | bytes 6152 | tf_op jit(solution)/shard_map/ppermute | solution.py:73
  80.7 2.5 %collective-permute-start.14 = (bf16[1,1,8,8,128]{4,3,2,1,0:T(8,128)(2,1)S(1)}, bf16[1,1,8,8,128]{4,3,2,1,0:T(8,128)(2,1)S(1)}, u32[]{:S(2)}, u32[]{:S(2)}) collective-permute-start(bf16[1,1,8,8,128]{4,3,2,1,0:T(8,128)(2,1)S(1)} %get-tuple-element.50), channel_id=1, source_target_pairs={{8,2},{9,3},{10,4},{11,5},{12,6},{13,7},{16,10},{17,11},{18,12},{1... | collective-permute-start | bytes 49160 | tf_op jit(solution)/shard_map/ppermute | solution.py:73
  83.5 0.5 collective-permute-done.14
  84.7 2.9 %fusion.4 = f32[1,8,8,8,128]{4,0,3,2,1:T(1,128)S(1)} fusion(bf16[3,3,3,128,128]{4,3,2,1,0:T(8,128)(2,1)S(1)} %bitcast.209, bf16[1,1,10,10,128]{4,0,3,2,1:T(2,128)(2,1)S(1)} %copy.73, bf16[1,8,1,10,128]{4,0,3,2,1:T(2,128)(2,1)S(1)} %copy.71, bf16[1,8,8,1,128]{4,0,3,2,1:T(2,128)(2,1)S(1)} %slice_bitcast_fusion.4, bf16[1,8,8,8,128]{4,0,3,2,1:T(2,128)(2,1)S(1)} %copy.69, ...), kind=kOutput, calls=%fused_computation.13 | convolution fusion | flops 454776832 | bytes 1402880 | tf_op jit(solution)/shard_map/conv_general_dilated | solution.py:108
  87.7 0.3 fusion.49
  88.0 0.3 fusion.21
  88.3 1.3 %collective-permute-start.18 = (bf16[512,128]{1,0:T(8,128)(2,1)S(1)}, bf16[512,128]{1,0:T(8,128)(2,1)S(1)}, u32[]{:S(2)}, u32[]{:S(2)}) collective-permute-start(bf16[512,128]{1,0:T(8,128)(2,1)S(1)} %fusion.21), channel_id=1, source_target_pairs={{8,0},{16,8},{24,16},{9,1},{17,9},{25,17},{10,2},{18,10},{26,18},{... | collective-permute-start | bytes 393224 | tf_op jit(solution)/shard_map/ppermute | solution.py:229
  89.7 5.8 %collective-permute-start.19 = (bf16[1,1,1,8,128]{4,3,2,1,0:T(8,128)(2,1)S(1)}, bf16[1,1,1,8,128]{4,3,2,1,0:T(8,128)(2,1)S(1)}, u32[]{:S(2)}, u32[]{:S(2)}) collective-permute-start(bf16[1,1,1,8,128]{4,3,2,1,0:T(8,128)(2,1)S(1)} %get-tuple-element.49), channel_id=1, source_target_pairs={{8,3},{9,2},{10,5},{11,4},{12,7},{13,6},{16,11},{17,10},{18,13},{1... | collective-permute-start | bytes 6152 | tf_op jit(solution)/shard_map/ppermute | solution.py:73
  95.5 3.3 %collective-permute-start.20 = (bf16[1,1,8,8,128]{4,3,2,1,0:T(8,128)(2,1)S(1)}, bf16[1,1,8,8,128]{4,3,2,1,0:T(8,128)(2,1)S(1)}, u32[]{:S(2)}, u32[]{:S(2)}) collective-permute-start(bf16[1,1,8,8,128]{4,3,2,1,0:T(8,128)(2,1)S(1)} %get-tuple-element.47), channel_id=1, source_target_pairs={{8,2},{9,3},{10,4},{11,5},{12,6},{13,7},{16,10},{17,11},{18,12},{1... | collective-permute-start | bytes 49160 | tf_op jit(solution)/shard_map/ppermute | solution.py:73
  98.8 1.3 %collective-permute-start.21 = (bf16[1,8,1,8,128]{4,3,2,1,0:T(8,128)(2,1)S(1)}, bf16[1,8,1,8,128]{4,3,2,1,0:T(8,128)(2,1)S(1)}, u32[]{:S(2)}, u32[]{:S(2)}) collective-permute-start(bf16[1,8,1,8,128]{4,3,2,1,0:T(8,128)(2,1)S(1)} %slice_select_fusion), channel_id=1, source_target_pairs={{8,1},{9,0},{10,3},{11,2},{12,5},{13,4},{14,7},{15,6},{16,9},{17,8... | collective-permute-start | bytes 49160 | tf_op jit(solution)/shard_map/ppermute | solution.py:73
  100.1 0.7 collective-permute-start.22
  100.8 0.9 collective-permute-start.23
  101.8 3.9 %multiply_convert_fusion = bf16[3,3,3,128,128]{4,3,2,1,0:T(8,128)(2,1)S(1)} fusion(bf16[1,10,10,10,256]{4,0,3,2,1:T(2,128)(2,1)S(1)} %copy-done.3, bf16[1,8,8,8,128]{4,3,2,1,0:T(8,128)(2,1)S(1)} %bitcast.244), kind=kOutput, calls=%fused_computation.2 | convolution fusion | flops 453869568 | bytes 1527808 | tf_op jit(solution)/shard_map/transpose | solution.py:217
  106.3 0.2 copy.77
  106.8 4.9 %collective-permute-start.26 = (bf16[864,128]{1,0:T(8,128)(2,1)S(1)}, bf16[864,128]{1,0:T(8,128)(2,1)S(1)}, u32[]{:S(2)}, u32[]{:S(2)}) collective-permute-start(bf16[864,128]{1,0:T(8,128)(2,1)S(1)} %get-tuple-element.27), channel_id=1, source_target_pairs={{0,6},{2,0},{4,2},{6,4},{1,7},{3,1},{5,3},{7,5},{8,14},{10,8},{12,... | collective-permute-start | bytes 663560 | tf_op jit(solution)/shard_map/ppermute | solution.py:151
  111.8 0.9 collective-permute-start.24
  112.7 2.9 %fusion.3 = f32[1,8,8,8,128]{4,0,3,2,1:T(1,128)S(1)} fusion(bf16[3,3,3,128,128]{4,3,2,1,0:T(8,128)(2,1)S(1)} %bitcast.210, bf16[1,1,10,10,128]{4,0,3,2,1:T(2,128)(2,1)S(1)} %copy.81, bf16[1,8,1,10,128]{4,0,3,2,1:T(2,128)(2,1)S(1)} %copy.79, bf16[1,8,8,1,128]{4,0,3,2,1:T(2,128)(2,1)S(1)} %slice_bitcast_fusion.2, bf16[1,8,8,8,128]{4,0,3,2,1:T(2,128)(2,1)S(1)} %copy.77, ...), kind=kOutput, calls=%fused_computation.12 | convolution fusion | flops 454776832 | bytes 1402880 | tf_op jit(solution)/shard_map/conv_general_dilated | solution.py:108
  115.7 0.3 fusion.50
  116.0 4.1 %collective-permute-done.25 = bf16[864,128]{1,0:T(8,128)(2,1)S(1)} collective-permute-done((bf16[864,128]{1,0:T(8,128)(2,1)S(1)}, bf16[864,128]{1,0:T(8,128)(2,1)S(1)}, u32[]{:S(2)}, u32[]{:S(2)}) %collective-permute-start.25) | collective-permute-done | bytes 221216 | tf_op jit(solution)/shard_map/ppermute | solution.py:151
  120.1 2.0 %collective-permute-done.24 = bf16[864,128]{1,0:T(8,128)(2,1)S(1)} collective-permute-done((bf16[864,128]{1,0:T(8,128)(2,1)S(1)}, bf16[864,128]{1,0:T(8,128)(2,1)S(1)}, u32[]{:S(2)}, u32[]{:S(2)}) %collective-permute-start.24) | collective-permute-done | bytes 221216 | tf_op jit(solution)/shard_map/ppermute | solution.py:151
  122.1 2.4 %collective-permute-start.27 = (f32[864,128]{1,0:T(8,128)S(1)}, f32[864,128]{1,0:T(8,128)S(1)}, u32[]{:S(2)}, u32[]{:S(2)}) collective-permute-start(f32[864,128]{1,0:T(8,128)S(1)} %convert_add_fusion), channel_id=1, source_target_pairs={{0,1},{1,0},{2,3},{3,2},{4,5},{5,4},{6,7},{7,6},{8,9},{9,8},{10,11... | collective-permute-start | bytes 1327112 | tf_op jit(solution)/shard_map/ppermute | solution.py:234
  124.5 1.0 fusion.53
  125.6 0.4 collective-permute-done.27
  125.9 0.8 add_bitcast_fusion
  (202 shorter events, 4.2 us)
Async XLA Ops:
  0.6 8.4 %copy-start.5 = (bf16[1,864,128]{2,1,0:T(8,128)(2,1)S(1)}, bf16[1,864,128]{2,1,0:T(8,128)(2,1)}, u32[]{:S(2)}) copy-start(bf16[1,864,128]{2,1,0:T(8,128)(2,1)} %param.11) | copy-start | bytes 663556
  4.5 10.9 %copy-start.10 = (s32[1,1,1,1,27]{4,3,2,1,0:T(1,128)S(1)}, s32[1,1,1,1,27]{4,3,2,1,0:T(1,128)}, u32[]{:S(2)}) copy-start(s32[1,1,1,1,27]{4,3,2,1,0:T(1,128)} %param.8) | copy-start | bytes 328
  5.4 11.5 %copy-start.11 = (f32[1,128]{1,0:T(1,128)S(1)}, f32[1,128]{1,0:T(1,128)}, u32[]{:S(2)}) copy-start(f32[1,128]{1,0:T(1,128)} %param.10) | copy-start | bytes 1540
  5.4 31.6 %collective-permute-start = (bf16[1,1,1,8,256]{4,3,2,1,0:T(8,128)(2,1)S(1)}, bf16[1,1,1,8,256]{4,3,2,1,0:T(8,128)(2,1)S(1)}, u32[]{:S(2)}, u32[]{:S(2)}) collective-permute-start(bf16[1,1,1,8,256]{4,3,2,1,0:T(8,128)(2,1)S(1)} %get-tuple-element.34), channel_id=1, source_target_pairs={{0,3},{1,2},{2,5},{3,4},{4,7},{5,6},{8,11},{9,10},{10,13},{11,12},... | collective-permute-start | bytes 12296 | tf_op jit(solution)/shard_map/ppermute | solution.py:73
  9.1 30.3 %collective-permute-start.5 = (bf16[864,128]{1,0:T(8,128)(2,1)S(1)}, bf16[864,128]{1,0:T(8,128)(2,1)}, u32[]{:S(2)}, u32[]{:S(2)}) collective-permute-start(bf16[864,128]{1,0:T(8,128)(2,1)S(1)} %bitcast.223), channel_id=1, source_target_pairs={{0,4},{2,6},{4,0},{6,2},{1,5},{3,7},{5,1},{7,3},{8,12},{10,14},{12... | collective-permute-start | bytes 663560 | tf_op jit(solution)/shard_map/ppermute | solution.py:137
  10.4 6.8 %copy-start.1 = (bf16[1,1,1,512,128]{4,3,2,1,0:T(8,128)(2,1)S(1)}, bf16[1,1,1,512,128]{4,3,2,1,0:T(8,128)(2,1)}, u32[]{:S(2)}) copy-start(bf16[1,1,1,512,128]{4,3,2,1,0:T(8,128)(2,1)} %param.7) | copy-start | bytes 393220
  10.5 28.2 %collective-permute-start.1 = (bf16[992,128]{1,0:T(8,128)(2,1)S(1)}, bf16[992,128]{1,0:T(8,128)(2,1)S(1)}, u32[]{:S(2)}, u32[]{:S(2)}) collective-permute-start(bf16[992,128]{1,0:T(8,128)(2,1)S(1)} %get-tuple-element.42), channel_id=1, source_target_pairs={{0,2},{1,3},{2,4},{3,5},{4,6},{5,7},{6,0},{7,1},{8,10},{9,11},{10,... | collective-permute-start | bytes 761864 | tf_op jit(solution)/shard_map/ppermute | solution.py:73
  10.6 27.0 %collective-permute-start.2 = (bf16[1,1,1,8,256]{4,3,2,1,0:T(8,128)(2,1)S(1)}, bf16[1,1,1,8,256]{4,3,2,1,0:T(8,128)(2,1)S(1)}, u32[]{:S(2)}, u32[]{:S(2)}) collective-permute-start(bf16[1,1,1,8,256]{4,3,2,1,0:T(8,128)(2,1)S(1)} %get-tuple-element.33), channel_id=1, source_target_pairs={{2,1},{3,0},{4,3},{5,2},{6,5},{7,4},{10,9},{11,8},{12,11},{13,10},... | collective-permute-start | bytes 12296 | tf_op jit(solution)/shard_map/ppermute | solution.py:73
  11.9 26.9 %collective-permute-start.3 = (bf16[992,128]{1,0:T(8,128)(2,1)S(1)}, bf16[992,128]{1,0:T(8,128)(2,1)S(1)}, u32[]{:S(2)}, u32[]{:S(2)}) collective-permute-start(bf16[992,128]{1,0:T(8,128)(2,1)S(1)} %get-tuple-element.41), channel_id=1, source_target_pairs={{0,6},{1,7},{2,0},{3,1},{4,2},{5,3},{6,4},{7,5},{8,14},{9,15},{10,... | collective-permute-start | bytes 761864 | tf_op jit(solution)/shard_map/ppermute | solution.py:73
  37.0 1.4 %collective-permute-start.4 = (bf16[1,8,1,8,256]{4,3,2,1,0:T(8,128)(2,1)S(1)}, bf16[1,8,1,8,256]{4,3,2,1,0:T(8,128)(2,1)S(1)}, u32[]{:S(2)}, u32[]{:S(2)}) collective-permute-start(bf16[1,8,1,8,256]{4,3,2,1,0:T(8,128)(2,1)S(1)} %fusion.56), channel_id=1, source_target_pairs={{0,1},{1,0},{2,3},{3,2},{4,5},{5,4},{6,7},{7,6},{8,9},{9,8},{10,11... | collective-permute-start | bytes 98312 | tf_op jit(solution)/shard_map/ppermute | solution.py:73
  42.3 2.1 %copy-start.4 = (bf16[3,3,3,128,128]{4,3,2,1,0:T(8,128)(2,1)S(1)}, bf16[3,3,3,128,128]{4,3,2,1,0:T(8,128)(2,1)}, u32[]{:S(2)}) copy-start(bf16[3,3,3,128,128]{4,3,2,1,0:T(8,128)(2,1)} %rev.3) | copy-start | bytes 2654212
  44.4 3.0 %copy-start.2 = (bf16[1,10,10,10,256]{4,0,3,2,1:T(2,128)(2,1)}, bf16[1,10,10,10,256]{4,0,3,2,1:T(2,128)(2,1)S(1)}, u32[]{:S(2)}) copy-start(bf16[1,10,10,10,256]{4,0,3,2,1:T(2,128)(2,1)S(1)} %pad_maximum_fusion) | copy-start | bytes 1536004
  44.5 3.0 %copy-start = (bf16[1,1,1,1,512,128]{5,4,3,2,1,0:T(8,128)(2,1)S(1)}, bf16[1,1,1,1,512,128]{5,4,3,2,1,0:T(8,128)(2,1)}, u32[]{:S(2)}) copy-start(bf16[1,1,1,1,512,128]{5,4,3,2,1,0:T(8,128)(2,1)} %param.6) | copy-start | bytes 393220
  47.5 1.5 %copy-start.12 = (pred[512]{0:T(512)(128)(4,1)S(1)}, pred[512]{0:T(512)(128)(4,1)}, u32[]{:S(2)}) copy-start(pred[512]{0:T(512)(128)(4,1)} %fusion.58) | copy-start | bytes 1540
  48.3 11.9 %collective-permute-start.10 = (bf16[1,1,1,8,128]{4,3,2,1,0:T(8,128)(2,1)S(1)}, bf16[1,1,1,8,128]{4,3,2,1,0:T(8,128)(2,1)S(1)}, u32[]{:S(2)}, u32[]{:S(2)}) collective-permute-start(bf16[1,1,1,8,128]{4,3,2,1,0:T(8,128)(2,1)S(1)} %get-tuple-element.60), channel_id=1, source_target_pairs={{10,1},{11,0},{12,3},{13,2},{14,5},{15,4},{18,9},{19,8},{20,11},{2... | collective-permute-start | bytes 6152 | tf_op jit(solution)/shard_map/ppermute | solution.py:73
  49.3 17.0 %copy-start.8 = (bf16[512,128]{1,0:T(8,128)(2,1)}, bf16[512,128]{1,0:T(8,128)(2,1)S(1)}, u32[]{:S(2)}) copy-start(bf16[512,128]{1,0:T(8,128)(2,1)S(1)} %fusion.8) | copy-start | bytes 393220
  49.3 13.7 %collective-permute-start.6 = (bf16[512,128]{1,0:T(8,128)(2,1)S(1)}, bf16[512,128]{1,0:T(8,128)(2,1)S(1)}, u32[]{:S(2)}, u32[]{:S(2)}) collective-permute-start(bf16[512,128]{1,0:T(8,128)(2,1)S(1)} %fusion.8), channel_id=1, source_target_pairs={{8,0},{16,8},{24,16},{9,1},{17,9},{25,17},{10,2},{18,10},{26,18},{... | collective-permute-start | bytes 393224 | tf_op jit(solution)/shard_map/ppermute | solution.py:229
  52.0 10.2 %collective-permute-start.11 = (bf16[1,1,8,8,128]{4,3,2,1,0:T(8,128)(2,1)S(1)}, bf16[1,1,8,8,128]{4,3,2,1,0:T(8,128)(2,1)S(1)}, u32[]{:S(2)}, u32[]{:S(2)}) collective-permute-start(bf16[1,1,8,8,128]{4,3,2,1,0:T(8,128)(2,1)S(1)} %get-tuple-element.58), channel_id=1, source_target_pairs={{10,0},{11,1},{12,2},{13,3},{14,4},{15,5},{18,8},{19,9},{20,10},{2... | collective-permute-start | bytes 49160 | tf_op jit(solution)/shard_map/ppermute | solution.py:73
  52.7 9.6 %collective-permute-start.9 = (bf16[1,8,1,8,128]{4,3,2,1,0:T(8,128)(2,1)S(1)}, bf16[1,8,1,8,128]{4,3,2,1,0:T(8,128)(2,1)S(1)}, u32[]{:S(2)}, u32[]{:S(2)}) collective-permute-start(bf16[1,8,1,8,128]{4,3,2,1,0:T(8,128)(2,1)S(1)} %slice_select_fusion.2), channel_id=1, source_target_pairs={{8,1},{9,0},{10,3},{11,2},{12,5},{13,4},{14,7},{15,6},{16,9},{17,8... | collective-permute-start | bytes 49160 | tf_op jit(solution)/shard_map/ppermute | solution.py:73
  55.9 6.1 %collective-permute-start.7 = (bf16[1,1,1,8,128]{4,3,2,1,0:T(8,128)(2,1)S(1)}, bf16[1,1,1,8,128]{4,3,2,1,0:T(8,128)(2,1)S(1)}, u32[]{:S(2)}, u32[]{:S(2)}) collective-permute-start(bf16[1,1,1,8,128]{4,3,2,1,0:T(8,128)(2,1)S(1)} %get-tuple-element.59), channel_id=1, source_target_pairs={{8,3},{9,2},{10,5},{11,4},{12,7},{13,6},{16,11},{17,10},{18,13},{1... | collective-permute-start | bytes 6152 | tf_op jit(solution)/shard_map/ppermute | solution.py:73
  60.2 2.5 %collective-permute-start.8 = (bf16[1,1,8,8,128]{4,3,2,1,0:T(8,128)(2,1)S(1)}, bf16[1,1,8,8,128]{4,3,2,1,0:T(8,128)(2,1)S(1)}, u32[]{:S(2)}, u32[]{:S(2)}) collective-permute-start(bf16[1,1,8,8,128]{4,3,2,1,0:T(8,128)(2,1)S(1)} %get-tuple-element.57), channel_id=1, source_target_pairs={{8,2},{9,3},{10,4},{11,5},{12,6},{13,7},{16,10},{17,11},{18,12},{1... | collective-permute-start | bytes 49160 | tf_op jit(solution)/shard_map/ppermute | solution.py:73
  66.9 17.8 %copy-start.6 = (bf16[512,128]{1,0:T(8,128)(2,1)}, bf16[512,128]{1,0:T(8,128)(2,1)S(1)}, u32[]{:S(2)}) copy-start(bf16[512,128]{1,0:T(8,128)(2,1)S(1)} %fusion.18) | copy-start | bytes 393220
  67.0 17.4 %collective-permute-start.12 = (bf16[512,128]{1,0:T(8,128)(2,1)S(1)}, bf16[512,128]{1,0:T(8,128)(2,1)S(1)}, u32[]{:S(2)}, u32[]{:S(2)}) collective-permute-start(bf16[512,128]{1,0:T(8,128)(2,1)S(1)} %fusion.18), channel_id=1, source_target_pairs={{8,0},{16,8},{24,16},{9,1},{17,9},{25,17},{10,2},{18,10},{26,18},{... | collective-permute-start | bytes 393224 | tf_op jit(solution)/shard_map/ppermute | solution.py:229
  68.9 11.8 %collective-permute-start.16 = (bf16[1,1,1,8,128]{4,3,2,1,0:T(8,128)(2,1)S(1)}, bf16[1,1,1,8,128]{4,3,2,1,0:T(8,128)(2,1)S(1)}, u32[]{:S(2)}, u32[]{:S(2)}) collective-permute-start(bf16[1,1,1,8,128]{4,3,2,1,0:T(8,128)(2,1)S(1)} %get-tuple-element.53), channel_id=1, source_target_pairs={{10,1},{11,0},{12,3},{13,2},{14,5},{15,4},{18,9},{19,8},{20,11},{2... | collective-permute-start | bytes 6152 | tf_op jit(solution)/shard_map/ppermute | solution.py:73
  69.6 13.8 %collective-permute-start.17 = (bf16[1,1,8,8,128]{4,3,2,1,0:T(8,128)(2,1)S(1)}, bf16[1,1,8,8,128]{4,3,2,1,0:T(8,128)(2,1)S(1)}, u32[]{:S(2)}, u32[]{:S(2)}) collective-permute-start(bf16[1,1,8,8,128]{4,3,2,1,0:T(8,128)(2,1)S(1)} %get-tuple-element.51), channel_id=1, source_target_pairs={{10,0},{11,1},{12,2},{13,3},{14,4},{15,5},{18,8},{19,9},{20,10},{2... | collective-permute-start | bytes 49160 | tf_op jit(solution)/shard_map/ppermute | solution.py:73
  70.2 13.2 %collective-permute-start.15 = (bf16[1,8,1,8,128]{4,3,2,1,0:T(8,128)(2,1)S(1)}, bf16[1,8,1,8,128]{4,3,2,1,0:T(8,128)(2,1)S(1)}, u32[]{:S(2)}, u32[]{:S(2)}) collective-permute-start(bf16[1,8,1,8,128]{4,3,2,1,0:T(8,128)(2,1)S(1)} %slice_select_fusion.1), channel_id=1, source_target_pairs={{8,1},{9,0},{10,3},{11,2},{12,5},{13,4},{14,7},{15,6},{16,9},{17,8... | collective-permute-start | bytes 49160 | tf_op jit(solution)/shard_map/ppermute | solution.py:73
  74.3 8.9 %collective-permute-start.13 = (bf16[1,1,1,8,128]{4,3,2,1,0:T(8,128)(2,1)S(1)}, bf16[1,1,1,8,128]{4,3,2,1,0:T(8,128)(2,1)S(1)}, u32[]{:S(2)}, u32[]{:S(2)}) collective-permute-start(bf16[1,1,1,8,128]{4,3,2,1,0:T(8,128)(2,1)S(1)} %get-tuple-element.52), channel_id=1, source_target_pairs={{8,3},{9,2},{10,5},{11,4},{12,7},{13,6},{16,11},{17,10},{18,13},{1... | collective-permute-start | bytes 6152 | tf_op jit(solution)/shard_map/ppermute | solution.py:73
  80.7 3.4 %collective-permute-start.14 = (bf16[1,1,8,8,128]{4,3,2,1,0:T(8,128)(2,1)S(1)}, bf16[1,1,8,8,128]{4,3,2,1,0:T(8,128)(2,1)S(1)}, u32[]{:S(2)}, u32[]{:S(2)}) collective-permute-start(bf16[1,1,8,8,128]{4,3,2,1,0:T(8,128)(2,1)S(1)} %get-tuple-element.50), channel_id=1, source_target_pairs={{8,2},{9,3},{10,4},{11,5},{12,6},{13,7},{16,10},{17,11},{18,12},{1... | collective-permute-start | bytes 49160 | tf_op jit(solution)/shard_map/ppermute | solution.py:73
  87.7 14.2 %copy-start.3 = (bf16[1,10,10,10,256]{4,0,3,2,1:T(2,128)(2,1)S(1)}, bf16[1,10,10,10,256]{4,0,3,2,1:T(2,128)(2,1)}, u32[]{:S(2)}) copy-start(bf16[1,10,10,10,256]{4,0,3,2,1:T(2,128)(2,1)} %copy-done.2) | copy-start | bytes 1536004
  88.3 12.4 %collective-permute-start.18 = (bf16[512,128]{1,0:T(8,128)(2,1)S(1)}, bf16[512,128]{1,0:T(8,128)(2,1)S(1)}, u32[]{:S(2)}, u32[]{:S(2)}) collective-permute-start(bf16[512,128]{1,0:T(8,128)(2,1)S(1)} %fusion.21), channel_id=1, source_target_pairs={{8,0},{16,8},{24,16},{9,1},{17,9},{25,17},{10,2},{18,10},{26,18},{... | collective-permute-start | bytes 393224 | tf_op jit(solution)/shard_map/ppermute | solution.py:229
  89.7 16.1 %collective-permute-start.19 = (bf16[1,1,1,8,128]{4,3,2,1,0:T(8,128)(2,1)S(1)}, bf16[1,1,1,8,128]{4,3,2,1,0:T(8,128)(2,1)S(1)}, u32[]{:S(2)}, u32[]{:S(2)}) collective-permute-start(bf16[1,1,1,8,128]{4,3,2,1,0:T(8,128)(2,1)S(1)} %get-tuple-element.49), channel_id=1, source_target_pairs={{8,3},{9,2},{10,5},{11,4},{12,7},{13,6},{16,11},{17,10},{18,13},{1... | collective-permute-start | bytes 6152 | tf_op jit(solution)/shard_map/ppermute | solution.py:73
  95.5 10.3 %collective-permute-start.20 = (bf16[1,1,8,8,128]{4,3,2,1,0:T(8,128)(2,1)S(1)}, bf16[1,1,8,8,128]{4,3,2,1,0:T(8,128)(2,1)S(1)}, u32[]{:S(2)}, u32[]{:S(2)}) collective-permute-start(bf16[1,1,8,8,128]{4,3,2,1,0:T(8,128)(2,1)S(1)} %get-tuple-element.47), channel_id=1, source_target_pairs={{8,2},{9,3},{10,4},{11,5},{12,6},{13,7},{16,10},{17,11},{18,12},{1... | collective-permute-start | bytes 49160 | tf_op jit(solution)/shard_map/ppermute | solution.py:73
  98.8 7.0 %collective-permute-start.21 = (bf16[1,8,1,8,128]{4,3,2,1,0:T(8,128)(2,1)S(1)}, bf16[1,8,1,8,128]{4,3,2,1,0:T(8,128)(2,1)S(1)}, u32[]{:S(2)}, u32[]{:S(2)}) collective-permute-start(bf16[1,8,1,8,128]{4,3,2,1,0:T(8,128)(2,1)S(1)} %slice_select_fusion), channel_id=1, source_target_pairs={{8,1},{9,0},{10,3},{11,2},{12,5},{13,4},{14,7},{15,6},{16,9},{17,8... | collective-permute-start | bytes 49160 | tf_op jit(solution)/shard_map/ppermute | solution.py:73
  100.1 5.7 %collective-permute-start.22 = (bf16[1,1,1,8,128]{4,3,2,1,0:T(8,128)(2,1)S(1)}, bf16[1,1,1,8,128]{4,3,2,1,0:T(8,128)(2,1)S(1)}, u32[]{:S(2)}, u32[]{:S(2)}) collective-permute-start(bf16[1,1,1,8,128]{4,3,2,1,0:T(8,128)(2,1)S(1)} %get-tuple-element.48), channel_id=1, source_target_pairs={{10,1},{11,0},{12,3},{13,2},{14,5},{15,4},{18,9},{19,8},{20,11},{2... | collective-permute-start | bytes 6152 | tf_op jit(solution)/shard_map/ppermute | solution.py:73
  100.8 5.0 %collective-permute-start.23 = (bf16[1,1,8,8,128]{4,3,2,1,0:T(8,128)(2,1)S(1)}, bf16[1,1,8,8,128]{4,3,2,1,0:T(8,128)(2,1)S(1)}, u32[]{:S(2)}, u32[]{:S(2)}) collective-permute-start(bf16[1,1,8,8,128]{4,3,2,1,0:T(8,128)(2,1)S(1)} %get-tuple-element.46), channel_id=1, source_target_pairs={{10,0},{11,1},{12,2},{13,3},{14,4},{15,5},{18,8},{19,9},{20,10},{2... | collective-permute-start | bytes 49160 | tf_op jit(solution)/shard_map/ppermute | solution.py:73
  106.8 9.2 %collective-permute-start.26 = (bf16[864,128]{1,0:T(8,128)(2,1)S(1)}, bf16[864,128]{1,0:T(8,128)(2,1)S(1)}, u32[]{:S(2)}, u32[]{:S(2)}) collective-permute-start(bf16[864,128]{1,0:T(8,128)(2,1)S(1)} %get-tuple-element.27), channel_id=1, source_target_pairs={{0,6},{2,0},{4,2},{6,4},{1,7},{3,1},{5,3},{7,5},{8,14},{10,8},{12,... | collective-permute-start | bytes 663560 | tf_op jit(solution)/shard_map/ppermute | solution.py:151
  111.8 8.3 %collective-permute-start.25 = (bf16[864,128]{1,0:T(8,128)(2,1)S(1)}, bf16[864,128]{1,0:T(8,128)(2,1)S(1)}, u32[]{:S(2)}, u32[]{:S(2)}) collective-permute-start(bf16[864,128]{1,0:T(8,128)(2,1)S(1)} %get-tuple-element.28), channel_id=1, source_target_pairs={{0,4},{2,6},{4,0},{6,2},{1,5},{3,7},{5,1},{7,3},{8,12},{10,14},{12... | collective-permute-start | bytes 663560 | tf_op jit(solution)/shard_map/ppermute | solution.py:151
  111.8 10.2 %collective-permute-start.24 = (bf16[864,128]{1,0:T(8,128)(2,1)S(1)}, bf16[864,128]{1,0:T(8,128)(2,1)S(1)}, u32[]{:S(2)}, u32[]{:S(2)}) collective-permute-start(bf16[864,128]{1,0:T(8,128)(2,1)S(1)} %get-tuple-element.26), channel_id=1, source_target_pairs={{0,2},{2,4},{4,6},{6,0},{1,3},{3,5},{5,7},{7,1},{8,10},{10,12},{12... | collective-permute-start | bytes 663560 | tf_op jit(solution)/shard_map/ppermute | solution.py:151
  115.6 8.9 %copy-start.7 = (bf16[512,128]{1,0:T(8,128)(2,1)S(1)}, bf16[512,128]{1,0:T(8,128)(2,1)}, u32[]{:S(2)}) copy-start(bf16[512,128]{1,0:T(8,128)(2,1)} %copy-done.6) | copy-start | bytes 393220
  115.6 8.9 %copy-start.9 = (bf16[512,128]{1,0:T(8,128)(2,1)S(1)}, bf16[512,128]{1,0:T(8,128)(2,1)}, u32[]{:S(2)}) copy-start(bf16[512,128]{1,0:T(8,128)(2,1)} %copy-done.8) | copy-start | bytes 393220
  122.1 3.8 %collective-permute-start.27 = (f32[864,128]{1,0:T(8,128)S(1)}, f32[864,128]{1,0:T(8,128)S(1)}, u32[]{:S(2)}, u32[]{:S(2)}) collective-permute-start(f32[864,128]{1,0:T(8,128)S(1)} %convert_add_fusion), channel_id=1, source_target_pairs={{0,1},{1,0},{2,3},{3,2},{4,5},{5,4},{6,7},{7,6},{8,9},{9,8},{10,11... | collective-permute-start | bytes 1327112 | tf_op jit(solution)/shard_map/ppermute | solution.py:234

commit v15 on v13

--- a/solution.py
+++ b/solution.py
@@ -134,10 +134,9 @@
             parts.append(given[step])
         else:
             parts.append(lax.ppermute(shard, axis, [(i, (i + step) % count) for i in range(count)]))
-    ordered = jnp.stack(parts)
-    index = (place - jnp.arange(count)) % count
-    slots = jnp.zeros((count,), jnp.int32).at[index].set(jnp.arange(count, dtype=jnp.int32))
-    return ordered[slots].reshape(count * shard.shape[0], *shard.shape[1:])
+    backwards = jnp.stack(parts[::-1] * 2)
+    ordered = lax.dynamic_slice_in_dim(backwards, count - 1 - place, count, axis=0)
+    return ordered.reshape(count * shard.shape[0], *shard.shape[1:])
 
 
 def scattered_sum(full, axis, share_rows):

time: 128 us -> 131 us (1.023)
  starting transfers between devices: 50.7 us -> 53.7 us
  waiting for transfers between devices: 17.8 us -> 20.4 us
  other arithmetic: 15.3 us -> 13.1 us
    ppermute x20, waiting for transfers between devices: 10.1 us -> 15 us  [send(): return lax.ppermute(piece, axes, route)]
    ppermute x20, starting transfers between devices: 41.2 us -> 44.2 us  [send(): return lax.ppermute(piece, axes, route)]
    ppermute x3, waiting for transfers between devices: 7.34 us -> 4.97 us  [scattered_sum(): lax.ppermute(piece, axis, [(i, (i + step) % count) for i in range(count)])]
  transfers between devices with their start and end apart: 28 -> 28, of which waited for: 6 -> 7; matrix products, arithmetic and copies ran while one was open for 12% -> 11% of each run, Pallas kernels for 0% -> 0%
where the time goes in v15:
time: 131 us; the launch traced here: 128 us
  starting transfers between devices  53.7 us (41%)
  waiting for transfers between devices  20.4 us (16%)
  between operations  19.8 us (15%)
  matrix products  15.6 us (12%)
  other arithmetic  13.1 us (10%)
  local copies, waits for them, and re-layouts  5.45 us (4%)
    ppermute x20, starting transfers between devices, send(): return lax.ppermute(piece, axes, route)  44.2 us
    ppermute x20, waiting for transfers between devices, send(): return lax.ppermute(piece, axes, route)  15 us
    conv_general_dilated x4, matrix products, conv_data(): lax.conv_general_dilated(padded, filters, (1, 1, 1), 'VALID', dimension_n...  11.8 us
    ppermute x3, starting transfers between devices, shards(): centre = lax.ppermute(result, 'pipe', down)  5.76 us
    ppermute x3, waiting for transfers between devices, scattered_sum(): lax.ppermute(piece, axis, [(i, (i + step) % count) for i in range(count)])  4.97 us
    transpose x1, matrix products, shards(): per_tap.transpose(1, 2, 3, 0, 4).reshape(taps * channels, channels)  3.76 us
  transfers between devices with their start and end apart: 28, of which 7 were waited for; matrix products, arithmetic and copies ran while one was open for 11% of the time, Pallas kernels for 0%

profile of v15, /device:TPU:21, one launch (start us, length us, event | category | flops | bytes accessed | tf_op | source)
XLA Modules:
  0.0 128.0 jit_solution(3826733082070502493)
XLA Ops:
  0.7 1.1 fusion.25
  1.8 1.0 convert_element_type.160
  3.5 1.0 broadcast_select_fusion.12
  4.6 0.8 multiply_convert_fusion.2
  5.4 0.7 collective-permute-start.4
  6.2 3.0 %collective-permute-start.2 = (bf16[1,1,1,8,256]{4,3,2,1,0:T(8,128)(2,1)S(1)}, bf16[1,1,1,8,256]{4,3,2,1,0:T(8,128)(2,1)S(1)}, u32[]{:S(2)}, u32[]{:S(2)}) collective-permute-start(bf16[1,1,1,8,256]{4,3,2,1,0:T(8,128)(2,1)S(1)} %constant_dynamic-slice_fusion.13), channel_id=1, source_target_pairs={{2,1},{3,0},{4,3},{5,2},{6,5},{7,4},{10,9},{11,8},{12,11},{13,10},... | collective-permute-start | bytes 12296 | tf_op jit(solution)/shard_map/ppermute | solution.py:73
  9.4 1.5 %collective-permute-start.3 = (bf16[992,128]{1,0:T(8,128)(2,1)S(1)}, bf16[992,128]{1,0:T(8,128)(2,1)S(1)}, u32[]{:S(2)}, u32[]{:S(2)}) collective-permute-start(bf16[992,128]{1,0:T(8,128)(2,1)S(1)} %get-tuple-element.39), channel_id=1, source_target_pairs={{0,6},{1,7},{2,0},{3,1},{4,2},{5,3},{6,4},{7,5},{8,14},{9,15},{10,... | collective-permute-start | bytes 761864 | tf_op jit(solution)/shard_map/ppermute | solution.py:73
  10.9 2.5 %collective-permute-start = (bf16[1,1,1,8,256]{4,3,2,1,0:T(8,128)(2,1)S(1)}, bf16[1,1,1,8,256]{4,3,2,1,0:T(8,128)(2,1)S(1)}, u32[]{:S(2)}, u32[]{:S(2)}) collective-permute-start(bf16[1,1,1,8,256]{4,3,2,1,0:T(8,128)(2,1)S(1)} %constant_dynamic-slice_fusion.14), channel_id=1, source_target_pairs={{0,3},{1,2},{2,5},{3,4},{4,7},{5,6},{8,11},{9,10},{10,13},{11,12},... | collective-permute-start | bytes 12296 | tf_op jit(solution)/shard_map/ppermute | solution.py:73
  13.5 0.7 fusion.75
  14.2 0.7 fusion.76
  14.9 0.2 fusion.58
  15.0 0.2 copy_dynamic-update-slice_fusion.1
  17.3 0.4 copy_dynamic-update-slice_fusion
  17.7 0.6 broadcast_select_fusion
  34.1 8.2 %collective-permute-done.1 = bf16[992,128]{1,0:T(8,128)(2,1)S(1)} collective-permute-done((bf16[992,128]{1,0:T(8,128)(2,1)S(1)}, bf16[992,128]{1,0:T(8,128)(2,1)S(1)}, u32[]{:S(2)}, u32[]{:S(2)}) %collective-permute-start.1) | collective-permute-done | bytes 253984 | tf_op jit(solution)/shard_map/ppermute | solution.py:73
  42.4 0.2 pad_maximum_fusion.10
  42.5 0.2 pad_maximum_fusion.9
  43.1 1.0 rev.3
  44.1 2.1 %pad_maximum_fusion = bf16[1,10,10,10,256]{4,0,3,2,1:T(2,128)(2,1)S(1)} fusion(bf16[1,1,10,10,256]{4,0,3,2,1:T(2,128)(2,1)S(1)} %pad_maximum_fusion.10, bf16[1,8,1,10,256]{4,0,3,2,1:T(2,128)(2,1)S(1)} %copy.47, bf16[1,8,8,1,256]{4,0,3,2,1:T(2,128)(2,1)S(1)} %get-tuple-element.30, bf16[1,8,8,8,256]{4,0,3,2,1:T(2,128)(2,1)S(1)} %broadcast_select_fusion, ...), kind=kLoop, calls=%fused_computation.2 | loop fusion | flops 1536000 | bytes 1024000 | tf_op jit(solution)/shard_map/concatenate | solution.py:56
  46.3 2.9 %fusion.1 = f32[1,8,8,8,128]{4,0,3,2,1:T(1,128)S(1)} fusion(bf16[3,3,3,128,128]{4,3,2,1,0:T(8,128)(2,1)S(1)} %copy-done.3, bf16[1,10,10,10,256]{4,0,3,2,1:T(2,128)(2,1)S(1)} %pad_maximum_fusion), kind=kOutput, calls=%fused_computation.7 | convolution fusion | flops 452984832 | bytes 1658880 | tf_op jit(solution)/shard_map/conv_general_dilated | solution.py:107
  49.2 0.3 fusion.47
  49.7 0.3 fusion.15
  50.0 1.9 %collective-permute-start.8 = (bf16[1,1,8,8,128]{4,3,2,1,0:T(8,128)(2,1)S(1)}, bf16[1,1,8,8,128]{4,3,2,1,0:T(8,128)(2,1)S(1)}, u32[]{:S(2)}, u32[]{:S(2)}) collective-permute-start(bf16[1,1,8,8,128]{4,3,2,1,0:T(8,128)(2,1)S(1)} %get-tuple-element.51), channel_id=1, source_target_pairs={{8,2},{9,3},{10,4},{11,5},{12,6},{13,7},{16,10},{17,11},{18,12},{1... | collective-permute-start | bytes 49160 | tf_op jit(solution)/shard_map/ppermute | solution.py:73
  52.0 4.0 %collective-permute-start.11 = (bf16[1,1,8,8,128]{4,3,2,1,0:T(8,128)(2,1)S(1)}, bf16[1,1,8,8,128]{4,3,2,1,0:T(8,128)(2,1)S(1)}, u32[]{:S(2)}, u32[]{:S(2)}) collective-permute-start(bf16[1,1,8,8,128]{4,3,2,1,0:T(8,128)(2,1)S(1)} %get-tuple-element.52), channel_id=1, source_target_pairs={{10,0},{11,1},{12,2},{13,3},{14,4},{15,5},{18,8},{19,9},{20,10},{2... | collective-permute-start | bytes 49160 | tf_op jit(solution)/shard_map/ppermute | solution.py:73
  56.0 1.9 %collective-permute-start.7 = (bf16[1,1,1,8,128]{4,3,2,1,0:T(8,128)(2,1)S(1)}, bf16[1,1,1,8,128]{4,3,2,1,0:T(8,128)(2,1)S(1)}, u32[]{:S(2)}, u32[]{:S(2)}) collective-permute-start(bf16[1,1,1,8,128]{4,3,2,1,0:T(8,128)(2,1)S(1)} %constant_dynamic-slice_fusion.11), channel_id=1, source_target_pairs={{8,3},{9,2},{10,5},{11,4},{12,7},{13,6},{16,11},{17,10},{18,13},{1... | collective-permute-start | bytes 6152 | tf_op jit(solution)/shard_map/ppermute | solution.py:73
  58.0 1.9 %collective-permute-start.9 = (bf16[1,8,1,8,128]{4,3,2,1,0:T(8,128)(2,1)S(1)}, bf16[1,8,1,8,128]{4,3,2,1,0:T(8,128)(2,1)S(1)}, u32[]{:S(2)}, u32[]{:S(2)}) collective-permute-start(bf16[1,8,1,8,128]{4,3,2,1,0:T(8,128)(2,1)S(1)} %constant_dynamic-slice_fusion.10), channel_id=1, source_target_pairs={{8,1},{9,0},{10,3},{11,2},{12,5},{13,4},{14,7},{15,6},{16,9},{17,8... | collective-permute-start | bytes 49160 | tf_op jit(solution)/shard_map/ppermute | solution.py:73
  59.9 0.3 fusion.8
  60.2 1.9 %collective-permute-start.6 = (bf16[512,128]{1,0:T(8,128)(2,1)S(1)}, bf16[512,128]{1,0:T(8,128)(2,1)S(1)}, u32[]{:S(2)}, u32[]{:S(2)}) collective-permute-start(bf16[512,128]{1,0:T(8,128)(2,1)S(1)} %fusion.8), channel_id=1, source_target_pairs={{8,0},{16,8},{24,16},{9,1},{17,9},{25,17},{10,2},{18,10},{26,18},{... | collective-permute-start | bytes 393224 | tf_op jit(solution)/shard_map/ppermute | solution.py:227
  62.1 0.6 collective-permute-done.7
  62.7 2.6 %collective-permute-start.10 = (bf16[1,1,1,8,128]{4,3,2,1,0:T(8,128)(2,1)S(1)}, bf16[1,1,1,8,128]{4,3,2,1,0:T(8,128)(2,1)S(1)}, u32[]{:S(2)}, u32[]{:S(2)}) collective-permute-start(bf16[1,1,1,8,128]{4,3,2,1,0:T(8,128)(2,1)S(1)} %constant_dynamic-slice_fusion.9), channel_id=1, source_target_pairs={{10,1},{11,0},{12,3},{13,2},{14,5},{15,4},{18,9},{19,8},{20,11},{2... | collective-permute-start | bytes 6152 | tf_op jit(solution)/shard_map/ppermute | solution.py:73
  65.4 3.2 %collective-permute-done.10 = bf16[1,1,1,8,128]{4,3,2,1,0:T(8,128)(2,1)S(1)} collective-permute-done((bf16[1,1,1,8,128]{4,3,2,1,0:T(8,128)(2,1)S(1)}, bf16[1,1,1,8,128]{4,3,2,1,0:T(8,128)(2,1)S(1)}, u32[]{:S(2)}, u32[]{:S(2)}) %collective-permute-start.10) | collective-permute-done | bytes 2080 | tf_op jit(solution)/shard_map/ppermute | solution.py:73
  69.2 0.2 copy.52
  69.4 3.0 %fusion.5 = f32[1,8,8,8,128]{4,0,3,2,1:T(1,128)S(1)} fusion(bf16[3,3,3,128,128]{4,3,2,1,0:T(8,128)(2,1)S(1)} %bitcast.216, bf16[1,1,10,10,128]{4,0,3,2,1:T(2,128)(2,1)S(1)} %copy.56, bf16[1,8,1,10,128]{4,0,3,2,1:T(2,128)(2,1)S(1)} %copy.54, bf16[1,8,8,1,128]{4,0,3,2,1:T(2,128)(2,1)S(1)} %slice_bitcast_fusion.6, bf16[1,8,8,8,128]{4,0,3,2,1:T(2,128)(2,1)S(1)} %copy.52, ...), kind=kOutput, calls=%fused_computation.11 | convolution fusion | flops 454776832 | bytes 1402880 | tf_op jit(solution)/shard_map/conv_general_dilated | solution.py:107
  72.4 0.3 fusion.48
  72.8 0.3 fusion.18
  73.1 1.9 %collective-permute-start.14 = (bf16[1,1,8,8,128]{4,3,2,1,0:T(8,128)(2,1)S(1)}, bf16[1,1,8,8,128]{4,3,2,1,0:T(8,128)(2,1)S(1)}, u32[]{:S(2)}, u32[]{:S(2)}) collective-permute-start(bf16[1,1,8,8,128]{4,3,2,1,0:T(8,128)(2,1)S(1)} %get-tuple-element.46), channel_id=1, source_target_pairs={{8,2},{9,3},{10,4},{11,5},{12,6},{13,7},{16,10},{17,11},{18,12},{1... | collective-permute-start | bytes 49160 | tf_op jit(solution)/shard_map/ppermute | solution.py:73
  75.1 1.9 %collective-permute-start.12 = (bf16[512,128]{1,0:T(8,128)(2,1)S(1)}, bf16[512,128]{1,0:T(8,128)(2,1)S(1)}, u32[]{:S(2)}, u32[]{:S(2)}) collective-permute-start(bf16[512,128]{1,0:T(8,128)(2,1)S(1)} %fusion.18), channel_id=1, source_target_pairs={{8,0},{16,8},{24,16},{9,1},{17,9},{25,17},{10,2},{18,10},{26,18},{... | collective-permute-start | bytes 393224 | tf_op jit(solution)/shard_map/ppermute | solution.py:227
  77.0 1.9 %collective-permute-start.13 = (bf16[1,1,1,8,128]{4,3,2,1,0:T(8,128)(2,1)S(1)}, bf16[1,1,1,8,128]{4,3,2,1,0:T(8,128)(2,1)S(1)}, u32[]{:S(2)}, u32[]{:S(2)}) collective-permute-start(bf16[1,1,1,8,128]{4,3,2,1,0:T(8,128)(2,1)S(1)} %constant_dynamic-slice_fusion.8), channel_id=1, source_target_pairs={{8,3},{9,2},{10,5},{11,4},{12,7},{13,6},{16,11},{17,10},{18,13},{1... | collective-permute-start | bytes 6152 | tf_op jit(solution)/shard_map/ppermute | solution.py:73
  78.9 3.9 %collective-permute-start.17 = (bf16[1,1,8,8,128]{4,3,2,1,0:T(8,128)(2,1)S(1)}, bf16[1,1,8,8,128]{4,3,2,1,0:T(8,128)(2,1)S(1)}, u32[]{:S(2)}, u32[]{:S(2)}) collective-permute-start(bf16[1,1,8,8,128]{4,3,2,1,0:T(8,128)(2,1)S(1)} %get-tuple-element.47), channel_id=1, source_target_pairs={{10,0},{11,1},{12,2},{13,3},{14,4},{15,5},{18,8},{19,9},{20,10},{2... | collective-permute-start | bytes 49160 | tf_op jit(solution)/shard_map/ppermute | solution.py:73
  82.8 1.9 %collective-permute-start.15 = (bf16[1,8,1,8,128]{4,3,2,1,0:T(8,128)(2,1)S(1)}, bf16[1,8,1,8,128]{4,3,2,1,0:T(8,128)(2,1)S(1)}, u32[]{:S(2)}, u32[]{:S(2)}) collective-permute-start(bf16[1,8,1,8,128]{4,3,2,1,0:T(8,128)(2,1)S(1)} %constant_dynamic-slice_fusion.7), channel_id=1, source_target_pairs={{8,1},{9,0},{10,3},{11,2},{12,5},{13,4},{14,7},{15,6},{16,9},{17,8... | collective-permute-start | bytes 49160 | tf_op jit(solution)/shard_map/ppermute | solution.py:73
  84.8 2.8 %collective-permute-start.16 = (bf16[1,1,1,8,128]{4,3,2,1,0:T(8,128)(2,1)S(1)}, bf16[1,1,1,8,128]{4,3,2,1,0:T(8,128)(2,1)S(1)}, u32[]{:S(2)}, u32[]{:S(2)}) collective-permute-start(bf16[1,1,1,8,128]{4,3,2,1,0:T(8,128)(2,1)S(1)} %constant_dynamic-slice_fusion.6), channel_id=1, source_target_pairs={{10,1},{11,0},{12,3},{13,2},{14,5},{15,4},{18,9},{19,8},{20,11},{2... | collective-permute-start | bytes 6152 | tf_op jit(solution)/shard_map/ppermute | solution.py:73
  87.6 3.0 %collective-permute-done.16 = bf16[1,1,1,8,128]{4,3,2,1,0:T(8,128)(2,1)S(1)} collective-permute-done((bf16[1,1,1,8,128]{4,3,2,1,0:T(8,128)(2,1)S(1)}, bf16[1,1,1,8,128]{4,3,2,1,0:T(8,128)(2,1)S(1)}, u32[]{:S(2)}, u32[]{:S(2)}) %collective-permute-start.16) | collective-permute-done | bytes 2080 | tf_op jit(solution)/shard_map/ppermute | solution.py:73
  91.2 0.2 copy.59
  91.5 3.0 %fusion.4 = f32[1,8,8,8,128]{4,0,3,2,1:T(1,128)S(1)} fusion(bf16[3,3,3,128,128]{4,3,2,1,0:T(8,128)(2,1)S(1)} %bitcast.217, bf16[1,1,10,10,128]{4,0,3,2,1:T(2,128)(2,1)S(1)} %copy.63, bf16[1,8,1,10,128]{4,0,3,2,1:T(2,128)(2,1)S(1)} %copy.61, bf16[1,8,8,1,128]{4,0,3,2,1:T(2,128)(2,1)S(1)} %slice_bitcast_fusion.4, bf16[1,8,8,8,128]{4,0,3,2,1:T(2,128)(2,1)S(1)} %copy.59, ...), kind=kOutput, calls=%fused_computation.10 | convolution fusion | flops 454776832 | bytes 1402880 | tf_op jit(solution)/shard_map/conv_general_dilated | solution.py:107
  94.5 0.3 fusion.49
  94.8 0.3 fusion.21
  95.1 1.9 %collective-permute-start.18 = (bf16[512,128]{1,0:T(8,128)(2,1)S(1)}, bf16[512,128]{1,0:T(8,128)(2,1)S(1)}, u32[]{:S(2)}, u32[]{:S(2)}) collective-permute-start(bf16[512,128]{1,0:T(8,128)(2,1)S(1)} %fusion.21), channel_id=1, source_target_pairs={{8,0},{16,8},{24,16},{9,1},{17,9},{25,17},{10,2},{18,10},{26,18},{... | collective-permute-start | bytes 393224 | tf_op jit(solution)/shard_map/ppermute | solution.py:227
  97.1 1.9 %collective-permute-start.20 = (bf16[1,1,8,8,128]{4,3,2,1,0:T(8,128)(2,1)S(1)}, bf16[1,1,8,8,128]{4,3,2,1,0:T(8,128)(2,1)S(1)}, u32[]{:S(2)}, u32[]{:S(2)}) collective-permute-start(bf16[1,1,8,8,128]{4,3,2,1,0:T(8,128)(2,1)S(1)} %get-tuple-element.45), channel_id=1, source_target_pairs={{8,2},{9,3},{10,4},{11,5},{12,6},{13,7},{16,10},{17,11},{18,12},{1... | collective-permute-start | bytes 49160 | tf_op jit(solution)/shard_map/ppermute | solution.py:73
  99.0 3.4 %collective-permute-start.23 = (bf16[1,1,8,8,128]{4,3,2,1,0:T(8,128)(2,1)S(1)}, bf16[1,1,8,8,128]{4,3,2,1,0:T(8,128)(2,1)S(1)}, u32[]{:S(2)}, u32[]{:S(2)}) collective-permute-start(bf16[1,1,8,8,128]{4,3,2,1,0:T(8,128)(2,1)S(1)} %get-tuple-element.44), channel_id=1, source_target_pairs={{10,0},{11,1},{12,2},{13,3},{14,4},{15,5},{18,8},{19,9},{20,10},{2... | collective-permute-start | bytes 49160 | tf_op jit(solution)/shard_map/ppermute | solution.py:73
  102.4 1.9 %collective-permute-start.19 = (bf16[1,1,1,8,128]{4,3,2,1,0:T(8,128)(2,1)S(1)}, bf16[1,1,1,8,128]{4,3,2,1,0:T(8,128)(2,1)S(1)}, u32[]{:S(2)}, u32[]{:S(2)}) collective-permute-start(bf16[1,1,1,8,128]{4,3,2,1,0:T(8,128)(2,1)S(1)} %constant_dynamic-slice_fusion.5), channel_id=1, source_target_pairs={{8,3},{9,2},{10,5},{11,4},{12,7},{13,6},{16,11},{17,10},{18,13},{1... | collective-permute-start | bytes 6152 | tf_op jit(solution)/shard_map/ppermute | solution.py:73
  104.3 2.2 %collective-permute-start.22 = (bf16[1,1,1,8,128]{4,3,2,1,0:T(8,128)(2,1)S(1)}, bf16[1,1,1,8,128]{4,3,2,1,0:T(8,128)(2,1)S(1)}, u32[]{:S(2)}, u32[]{:S(2)}) collective-permute-start(bf16[1,1,1,8,128]{4,3,2,1,0:T(8,128)(2,1)S(1)} %constant_dynamic-slice_fusion.3), channel_id=1, source_target_pairs={{10,1},{11,0},{12,3},{13,2},{14,5},{15,4},{18,9},{19,8},{20,11},{2... | collective-permute-start | bytes 6152 | tf_op jit(solution)/shard_map/ppermute | solution.py:73
  106.6 2.1 %collective-permute-start.21 = (bf16[1,8,1,8,128]{4,3,2,1,0:T(8,128)(2,1)S(1)}, bf16[1,8,1,8,128]{4,3,2,1,0:T(8,128)(2,1)S(1)}, u32[]{:S(2)}, u32[]{:S(2)}) collective-permute-start(bf16[1,8,1,8,128]{4,3,2,1,0:T(8,128)(2,1)S(1)} %constant_dynamic-slice_fusion.4), channel_id=1, source_target_pairs={{8,1},{9,0},{10,3},{11,2},{12,5},{13,4},{14,7},{15,6},{16,9},{17,8... | collective-permute-start | bytes 49160 | tf_op jit(solution)/shard_map/ppermute | solution.py:73
  108.9 3.8 %multiply_convert_fusion = bf16[3,3,3,128,128]{4,3,2,1,0:T(8,128)(2,1)S(1)} fusion(bf16[1,10,10,10,256]{4,0,3,2,1:T(2,128)(2,1)S(1)} %pad_maximum_fusion, bf16[1,8,8,8,128]{4,3,2,1,0:T(8,128)(2,1)S(1)} %bitcast.250), kind=kOutput, calls=%fused_computation | convolution fusion | flops 453869568 | bytes 1527808 | tf_op jit(solution)/shard_map/transpose | solution.py:215
  113.0 0.6 collective-permute-start.25
  113.6 1.7 %collective-permute-start.26 = (bf16[864,128]{1,0:T(8,128)(2,1)S(1)}, bf16[864,128]{1,0:T(8,128)(2,1)S(1)}, u32[]{:S(2)}, u32[]{:S(2)}) collective-permute-start(bf16[864,128]{1,0:T(8,128)(2,1)S(1)} %get-tuple-element.27), channel_id=1, source_target_pairs={{0,6},{2,0},{4,2},{6,4},{1,7},{3,1},{5,3},{7,5},{8,14},{10,8},{12,... | collective-permute-start | bytes 663560 | tf_op jit(solution)/shard_map/ppermute | solution.py:149
  115.6 0.2 copy.67
  116.1 3.0 %fusion.3 = f32[1,8,8,8,128]{4,0,3,2,1:T(1,128)S(1)} fusion(bf16[3,3,3,128,128]{4,3,2,1,0:T(8,128)(2,1)S(1)} %bitcast.218, bf16[1,1,10,10,128]{4,0,3,2,1:T(2,128)(2,1)S(1)} %copy.71, bf16[1,8,1,10,128]{4,0,3,2,1:T(2,128)(2,1)S(1)} %copy.69, bf16[1,8,8,1,128]{4,0,3,2,1:T(2,128)(2,1)S(1)} %slice_bitcast_fusion.2, bf16[1,8,8,8,128]{4,0,3,2,1:T(2,128)(2,1)S(1)} %copy.67, ...), kind=kOutput, calls=%fused_computation.9 | convolution fusion | flops 454776832 | bytes 1402880 | tf_op jit(solution)/shard_map/conv_general_dilated | solution.py:107
  119.1 0.3 fusion.50
  119.4 1.1 collective-permute-done.24
  120.5 3.9 %collective-permute-done.25 = bf16[864,128]{1,0:T(8,128)(2,1)S(1)} collective-permute-done((bf16[864,128]{1,0:T(8,128)(2,1)S(1)}, bf16[864,128]{1,0:T(8,128)(2,1)S(1)}, u32[]{:S(2)}, u32[]{:S(2)}) %collective-permute-start.25) | collective-permute-done | bytes 221216 | tf_op jit(solution)/shard_map/ppermute | solution.py:149
  124.5 1.3 %collective-permute-start.27 = (f32[864,128]{1,0:T(8,128)S(1)}, f32[864,128]{1,0:T(8,128)S(1)}, u32[]{:S(2)}, u32[]{:S(2)}) collective-permute-start(f32[864,128]{1,0:T(8,128)S(1)} %convert_add_fusion), channel_id=1, source_target_pairs={{0,1},{1,0},{2,3},{3,2},{4,5},{5,4},{6,7},{7,6},{8,9},{9,8},{10,11... | collective-permute-start | bytes 1327112 | tf_op jit(solution)/shard_map/ppermute | solution.py:232
  125.8 1.0 fusion.57
  126.8 0.4 collective-permute-done.27
  127.2 0.8 add_bitcast_fusion
  (200 shorter events, 3.7 us)
Async XLA Ops:
  0.6 14.2 %copy-start.9 = (f32[1,128]{1,0:T(1,128)S(1)}, f32[1,128]{1,0:T(1,128)}, u32[]{:S(2)}) copy-start(f32[1,128]{1,0:T(1,128)} %param.10) | copy-start | bytes 1540
  0.6 8.5 %copy-start.2 = (bf16[1,864,128]{2,1,0:T(8,128)(2,1)S(1)}, bf16[1,864,128]{2,1,0:T(8,128)(2,1)}, u32[]{:S(2)}) copy-start(bf16[1,864,128]{2,1,0:T(8,128)(2,1)} %param.11) | copy-start | bytes 663556
  0.7 12.8 %copy-start.8 = (s32[1,1,1,1,27]{4,3,2,1,0:T(1,128)S(1)}, s32[1,1,1,1,27]{4,3,2,1,0:T(1,128)}, u32[]{:S(2)}) copy-start(s32[1,1,1,1,27]{4,3,2,1,0:T(1,128)} %param.8) | copy-start | bytes 328
  1.8 13.5 %copy-start.1 = (bf16[1,1,1,512,128]{4,3,2,1,0:T(8,128)(2,1)S(1)}, bf16[1,1,1,512,128]{4,3,2,1,0:T(8,128)(2,1)}, u32[]{:S(2)}) copy-start(bf16[1,1,1,512,128]{4,3,2,1,0:T(8,128)(2,1)} %param.7) | copy-start | bytes 393220
  5.4 28.2 %collective-permute-start.4 = (bf16[1,8,1,8,256]{4,3,2,1,0:T(8,128)(2,1)S(1)}, bf16[1,8,1,8,256]{4,3,2,1,0:T(8,128)(2,1)S(1)}, u32[]{:S(2)}, u32[]{:S(2)}) collective-permute-start(bf16[1,8,1,8,256]{4,3,2,1,0:T(8,128)(2,1)S(1)} %fusion.61), channel_id=1, source_target_pairs={{0,1},{1,0},{2,3},{3,2},{4,5},{5,4},{6,7},{7,6},{8,9},{9,8},{10,11... | collective-permute-start | bytes 98312 | tf_op jit(solution)/shard_map/ppermute | solution.py:73
  6.2 27.1 %collective-permute-start.2 = (bf16[1,1,1,8,256]{4,3,2,1,0:T(8,128)(2,1)S(1)}, bf16[1,1,1,8,256]{4,3,2,1,0:T(8,128)(2,1)S(1)}, u32[]{:S(2)}, u32[]{:S(2)}) collective-permute-start(bf16[1,1,1,8,256]{4,3,2,1,0:T(8,128)(2,1)S(1)} %constant_dynamic-slice_fusion.13), channel_id=1, source_target_pairs={{2,1},{3,0},{4,3},{5,2},{6,5},{7,4},{10,9},{11,8},{12,11},{13,10},... | collective-permute-start | bytes 12296 | tf_op jit(solution)/shard_map/ppermute | solution.py:73
  9.2 33.6 %collective-permute-start.5 = (bf16[864,128]{1,0:T(8,128)(2,1)S(1)}, bf16[864,128]{1,0:T(8,128)(2,1)S(1)}, u32[]{:S(2)}, u32[]{:S(2)}) collective-permute-start(bf16[864,128]{1,0:T(8,128)(2,1)S(1)} %bitcast.225), channel_id=1, source_target_pairs={{0,4},{2,6},{4,0},{6,2},{1,5},{3,7},{5,1},{7,3},{8,12},{10,14},{12... | collective-permute-start | bytes 663560 | tf_op jit(solution)/shard_map/ppermute | solution.py:136
  9.4 24.6 %collective-permute-start.3 = (bf16[992,128]{1,0:T(8,128)(2,1)S(1)}, bf16[992,128]{1,0:T(8,128)(2,1)S(1)}, u32[]{:S(2)}, u32[]{:S(2)}) collective-permute-start(bf16[992,128]{1,0:T(8,128)(2,1)S(1)} %get-tuple-element.39), channel_id=1, source_target_pairs={{0,6},{1,7},{2,0},{3,1},{4,2},{5,3},{6,4},{7,5},{8,14},{9,15},{10,... | collective-permute-start | bytes 761864 | tf_op jit(solution)/shard_map/ppermute | solution.py:73
  10.9 22.6 %collective-permute-start = (bf16[1,1,1,8,256]{4,3,2,1,0:T(8,128)(2,1)S(1)}, bf16[1,1,1,8,256]{4,3,2,1,0:T(8,128)(2,1)S(1)}, u32[]{:S(2)}, u32[]{:S(2)}) collective-permute-start(bf16[1,1,1,8,256]{4,3,2,1,0:T(8,128)(2,1)S(1)} %constant_dynamic-slice_fusion.14), channel_id=1, source_target_pairs={{0,3},{1,2},{2,5},{3,4},{4,7},{5,6},{8,11},{9,10},{10,13},{11,12},... | collective-permute-start | bytes 12296 | tf_op jit(solution)/shard_map/ppermute | solution.py:73
  33.4 8.9 %collective-permute-start.1 = (bf16[992,128]{1,0:T(8,128)(2,1)S(1)}, bf16[992,128]{1,0:T(8,128)(2,1)S(1)}, u32[]{:S(2)}, u32[]{:S(2)}) collective-permute-start(bf16[992,128]{1,0:T(8,128)(2,1)S(1)} %get-tuple-element.40), channel_id=1, source_target_pairs={{0,2},{1,3},{2,4},{3,5},{4,6},{5,7},{6,0},{7,1},{8,10},{9,11},{10,... | collective-permute-start | bytes 761864 | tf_op jit(solution)/shard_map/ppermute | solution.py:73
  44.1 2.1 %copy-start.3 = (bf16[3,3,3,128,128]{4,3,2,1,0:T(8,128)(2,1)S(1)}, bf16[3,3,3,128,128]{4,3,2,1,0:T(8,128)(2,1)}, u32[]{:S(2)}) copy-start(bf16[3,3,3,128,128]{4,3,2,1,0:T(8,128)(2,1)} %rev.3) | copy-start | bytes 2654212
  46.3 3.0 %copy-start = (bf16[1,1,1,1,512,128]{5,4,3,2,1,0:T(8,128)(2,1)S(1)}, bf16[1,1,1,1,512,128]{5,4,3,2,1,0:T(8,128)(2,1)}, u32[]{:S(2)}) copy-start(bf16[1,1,1,1,512,128]{5,4,3,2,1,0:T(8,128)(2,1)} %param.6) | copy-start | bytes 393220
  50.0 18.6 %collective-permute-start.8 = (bf16[1,1,8,8,128]{4,3,2,1,0:T(8,128)(2,1)S(1)}, bf16[1,1,8,8,128]{4,3,2,1,0:T(8,128)(2,1)S(1)}, u32[]{:S(2)}, u32[]{:S(2)}) collective-permute-start(bf16[1,1,8,8,128]{4,3,2,1,0:T(8,128)(2,1)S(1)} %get-tuple-element.51), channel_id=1, source_target_pairs={{8,2},{9,3},{10,4},{11,5},{12,6},{13,7},{16,10},{17,11},{18,12},{1... | collective-permute-start | bytes 49160 | tf_op jit(solution)/shard_map/ppermute | solution.py:73
  52.0 16.8 %collective-permute-start.11 = (bf16[1,1,8,8,128]{4,3,2,1,0:T(8,128)(2,1)S(1)}, bf16[1,1,8,8,128]{4,3,2,1,0:T(8,128)(2,1)S(1)}, u32[]{:S(2)}, u32[]{:S(2)}) collective-permute-start(bf16[1,1,8,8,128]{4,3,2,1,0:T(8,128)(2,1)S(1)} %get-tuple-element.52), channel_id=1, source_target_pairs={{10,0},{11,1},{12,2},{13,3},{14,4},{15,5},{18,8},{19,9},{20,10},{2... | collective-permute-start | bytes 49160 | tf_op jit(solution)/shard_map/ppermute | solution.py:73
  56.0 6.7 %collective-permute-start.7 = (bf16[1,1,1,8,128]{4,3,2,1,0:T(8,128)(2,1)S(1)}, bf16[1,1,1,8,128]{4,3,2,1,0:T(8,128)(2,1)S(1)}, u32[]{:S(2)}, u32[]{:S(2)}) collective-permute-start(bf16[1,1,1,8,128]{4,3,2,1,0:T(8,128)(2,1)S(1)} %constant_dynamic-slice_fusion.11), channel_id=1, source_target_pairs={{8,3},{9,2},{10,5},{11,4},{12,7},{13,6},{16,11},{17,10},{18,13},{1... | collective-permute-start | bytes 6152 | tf_op jit(solution)/shard_map/ppermute | solution.py:73
  58.0 10.7 %collective-permute-start.9 = (bf16[1,8,1,8,128]{4,3,2,1,0:T(8,128)(2,1)S(1)}, bf16[1,8,1,8,128]{4,3,2,1,0:T(8,128)(2,1)S(1)}, u32[]{:S(2)}, u32[]{:S(2)}) collective-permute-start(bf16[1,8,1,8,128]{4,3,2,1,0:T(8,128)(2,1)S(1)} %constant_dynamic-slice_fusion.10), channel_id=1, source_target_pairs={{8,1},{9,0},{10,3},{11,2},{12,5},{13,4},{14,7},{15,6},{16,9},{17,8... | collective-permute-start | bytes 49160 | tf_op jit(solution)/shard_map/ppermute | solution.py:73
  60.2 12.2 %copy-start.6 = (bf16[512,128]{1,0:T(8,128)(2,1)}, bf16[512,128]{1,0:T(8,128)(2,1)S(1)}, u32[]{:S(2)}) copy-start(bf16[512,128]{1,0:T(8,128)(2,1)S(1)} %fusion.8) | copy-start | bytes 393220
  60.2 8.9 %collective-permute-start.6 = (bf16[512,128]{1,0:T(8,128)(2,1)S(1)}, bf16[512,128]{1,0:T(8,128)(2,1)S(1)}, u32[]{:S(2)}, u32[]{:S(2)}) collective-permute-start(bf16[512,128]{1,0:T(8,128)(2,1)S(1)} %fusion.8), channel_id=1, source_target_pairs={{8,0},{16,8},{24,16},{9,1},{17,9},{25,17},{10,2},{18,10},{26,18},{... | collective-permute-start | bytes 393224 | tf_op jit(solution)/shard_map/ppermute | solution.py:227
  62.7 5.8 %collective-permute-start.10 = (bf16[1,1,1,8,128]{4,3,2,1,0:T(8,128)(2,1)S(1)}, bf16[1,1,1,8,128]{4,3,2,1,0:T(8,128)(2,1)S(1)}, u32[]{:S(2)}, u32[]{:S(2)}) collective-permute-start(bf16[1,1,1,8,128]{4,3,2,1,0:T(8,128)(2,1)S(1)} %constant_dynamic-slice_fusion.9), channel_id=1, source_target_pairs={{10,1},{11,0},{12,3},{13,2},{14,5},{15,4},{18,9},{19,8},{20,11},{2... | collective-permute-start | bytes 6152 | tf_op jit(solution)/shard_map/ppermute | solution.py:73
  73.1 21.4 %copy-start.4 = (bf16[512,128]{1,0:T(8,128)(2,1)}, bf16[512,128]{1,0:T(8,128)(2,1)S(1)}, u32[]{:S(2)}) copy-start(bf16[512,128]{1,0:T(8,128)(2,1)S(1)} %fusion.18) | copy-start | bytes 393220
  73.1 17.6 %collective-permute-start.14 = (bf16[1,1,8,8,128]{4,3,2,1,0:T(8,128)(2,1)S(1)}, bf16[1,1,8,8,128]{4,3,2,1,0:T(8,128)(2,1)S(1)}, u32[]{:S(2)}, u32[]{:S(2)}) collective-permute-start(bf16[1,1,8,8,128]{4,3,2,1,0:T(8,128)(2,1)S(1)} %get-tuple-element.46), channel_id=1, source_target_pairs={{8,2},{9,3},{10,4},{11,5},{12,6},{13,7},{16,10},{17,11},{18,12},{1... | collective-permute-start | bytes 49160 | tf_op jit(solution)/shard_map/ppermute | solution.py:73
  75.1 16.1 %collective-permute-start.12 = (bf16[512,128]{1,0:T(8,128)(2,1)S(1)}, bf16[512,128]{1,0:T(8,128)(2,1)S(1)}, u32[]{:S(2)}, u32[]{:S(2)}) collective-permute-start(bf16[512,128]{1,0:T(8,128)(2,1)S(1)} %fusion.18), channel_id=1, source_target_pairs={{8,0},{16,8},{24,16},{9,1},{17,9},{25,17},{10,2},{18,10},{26,18},{... | collective-permute-start | bytes 393224 | tf_op jit(solution)/shard_map/ppermute | solution.py:227
  77.0 7.8 %collective-permute-start.13 = (bf16[1,1,1,8,128]{4,3,2,1,0:T(8,128)(2,1)S(1)}, bf16[1,1,1,8,128]{4,3,2,1,0:T(8,128)(2,1)S(1)}, u32[]{:S(2)}, u32[]{:S(2)}) collective-permute-start(bf16[1,1,1,8,128]{4,3,2,1,0:T(8,128)(2,1)S(1)} %constant_dynamic-slice_fusion.8), channel_id=1, source_target_pairs={{8,3},{9,2},{10,5},{11,4},{12,7},{13,6},{16,11},{17,10},{18,13},{1... | collective-permute-start | bytes 6152 | tf_op jit(solution)/shard_map/ppermute | solution.py:73
  78.9 11.9 %collective-permute-start.17 = (bf16[1,1,8,8,128]{4,3,2,1,0:T(8,128)(2,1)S(1)}, bf16[1,1,8,8,128]{4,3,2,1,0:T(8,128)(2,1)S(1)}, u32[]{:S(2)}, u32[]{:S(2)}) collective-permute-start(bf16[1,1,8,8,128]{4,3,2,1,0:T(8,128)(2,1)S(1)} %get-tuple-element.47), channel_id=1, source_target_pairs={{10,0},{11,1},{12,2},{13,3},{14,4},{15,5},{18,8},{19,9},{20,10},{2... | collective-permute-start | bytes 49160 | tf_op jit(solution)/shard_map/ppermute | solution.py:73
  82.8 7.9 %collective-permute-start.15 = (bf16[1,8,1,8,128]{4,3,2,1,0:T(8,128)(2,1)S(1)}, bf16[1,8,1,8,128]{4,3,2,1,0:T(8,128)(2,1)S(1)}, u32[]{:S(2)}, u32[]{:S(2)}) collective-permute-start(bf16[1,8,1,8,128]{4,3,2,1,0:T(8,128)(2,1)S(1)} %constant_dynamic-slice_fusion.7), channel_id=1, source_target_pairs={{8,1},{9,0},{10,3},{11,2},{12,5},{13,4},{14,7},{15,6},{16,9},{17,8... | collective-permute-start | bytes 49160 | tf_op jit(solution)/shard_map/ppermute | solution.py:73
  84.8 5.8 %collective-permute-start.16 = (bf16[1,1,1,8,128]{4,3,2,1,0:T(8,128)(2,1)S(1)}, bf16[1,1,1,8,128]{4,3,2,1,0:T(8,128)(2,1)S(1)}, u32[]{:S(2)}, u32[]{:S(2)}) collective-permute-start(bf16[1,1,1,8,128]{4,3,2,1,0:T(8,128)(2,1)S(1)} %constant_dynamic-slice_fusion.6), channel_id=1, source_target_pairs={{10,1},{11,0},{12,3},{13,2},{14,5},{15,4},{18,9},{19,8},{20,11},{2... | collective-permute-start | bytes 6152 | tf_op jit(solution)/shard_map/ppermute | solution.py:73
  95.1 11.4 %collective-permute-start.18 = (bf16[512,128]{1,0:T(8,128)(2,1)S(1)}, bf16[512,128]{1,0:T(8,128)(2,1)S(1)}, u32[]{:S(2)}, u32[]{:S(2)}) collective-permute-start(bf16[512,128]{1,0:T(8,128)(2,1)S(1)} %fusion.21), channel_id=1, source_target_pairs={{8,0},{16,8},{24,16},{9,1},{17,9},{25,17},{10,2},{18,10},{26,18},{... | collective-permute-start | bytes 393224 | tf_op jit(solution)/shard_map/ppermute | solution.py:227
  97.1 15.6 %collective-permute-start.20 = (bf16[1,1,8,8,128]{4,3,2,1,0:T(8,128)(2,1)S(1)}, bf16[1,1,8,8,128]{4,3,2,1,0:T(8,128)(2,1)S(1)}, u32[]{:S(2)}, u32[]{:S(2)}) collective-permute-start(bf16[1,1,8,8,128]{4,3,2,1,0:T(8,128)(2,1)S(1)} %get-tuple-element.45), channel_id=1, source_target_pairs={{8,2},{9,3},{10,4},{11,5},{12,6},{13,7},{16,10},{17,11},{18,12},{1... | collective-permute-start | bytes 49160 | tf_op jit(solution)/shard_map/ppermute | solution.py:73
  99.0 13.7 %collective-permute-start.23 = (bf16[1,1,8,8,128]{4,3,2,1,0:T(8,128)(2,1)S(1)}, bf16[1,1,8,8,128]{4,3,2,1,0:T(8,128)(2,1)S(1)}, u32[]{:S(2)}, u32[]{:S(2)}) collective-permute-start(bf16[1,1,8,8,128]{4,3,2,1,0:T(8,128)(2,1)S(1)} %get-tuple-element.44), channel_id=1, source_target_pairs={{10,0},{11,1},{12,2},{13,3},{14,4},{15,5},{18,8},{19,9},{20,10},{2... | collective-permute-start | bytes 49160 | tf_op jit(solution)/shard_map/ppermute | solution.py:73
  102.4 10.2 %collective-permute-start.19 = (bf16[1,1,1,8,128]{4,3,2,1,0:T(8,128)(2,1)S(1)}, bf16[1,1,1,8,128]{4,3,2,1,0:T(8,128)(2,1)S(1)}, u32[]{:S(2)}, u32[]{:S(2)}) collective-permute-start(bf16[1,1,1,8,128]{4,3,2,1,0:T(8,128)(2,1)S(1)} %constant_dynamic-slice_fusion.5), channel_id=1, source_target_pairs={{8,3},{9,2},{10,5},{11,4},{12,7},{13,6},{16,11},{17,10},{18,13},{1... | collective-permute-start | bytes 6152 | tf_op jit(solution)/shard_map/ppermute | solution.py:73
  104.3 8.3 %collective-permute-start.22 = (bf16[1,1,1,8,128]{4,3,2,1,0:T(8,128)(2,1)S(1)}, bf16[1,1,1,8,128]{4,3,2,1,0:T(8,128)(2,1)S(1)}, u32[]{:S(2)}, u32[]{:S(2)}) collective-permute-start(bf16[1,1,1,8,128]{4,3,2,1,0:T(8,128)(2,1)S(1)} %constant_dynamic-slice_fusion.3), channel_id=1, source_target_pairs={{10,1},{11,0},{12,3},{13,2},{14,5},{15,4},{18,9},{19,8},{20,11},{2... | collective-permute-start | bytes 6152 | tf_op jit(solution)/shard_map/ppermute | solution.py:73
  106.6 6.1 %collective-permute-start.21 = (bf16[1,8,1,8,128]{4,3,2,1,0:T(8,128)(2,1)S(1)}, bf16[1,8,1,8,128]{4,3,2,1,0:T(8,128)(2,1)S(1)}, u32[]{:S(2)}, u32[]{:S(2)}) collective-permute-start(bf16[1,8,1,8,128]{4,3,2,1,0:T(8,128)(2,1)S(1)} %constant_dynamic-slice_fusion.4), channel_id=1, source_target_pairs={{8,1},{9,0},{10,3},{11,2},{12,5},{13,4},{14,7},{15,6},{16,9},{17,8... | collective-permute-start | bytes 49160 | tf_op jit(solution)/shard_map/ppermute | solution.py:73
  112.9 7.6 %collective-permute-start.24 = (bf16[864,128]{1,0:T(8,128)(2,1)S(1)}, bf16[864,128]{1,0:T(8,128)(2,1)S(1)}, u32[]{:S(2)}, u32[]{:S(2)}) collective-permute-start(bf16[864,128]{1,0:T(8,128)(2,1)S(1)} %get-tuple-element.26), channel_id=1, source_target_pairs={{0,2},{2,4},{4,6},{6,0},{1,3},{3,5},{5,7},{7,1},{8,10},{10,12},{12... | collective-permute-start | bytes 663560 | tf_op jit(solution)/shard_map/ppermute | solution.py:149
  113.0 11.4 %collective-permute-start.25 = (bf16[864,128]{1,0:T(8,128)(2,1)S(1)}, bf16[864,128]{1,0:T(8,128)(2,1)S(1)}, u32[]{:S(2)}, u32[]{:S(2)}) collective-permute-start(bf16[864,128]{1,0:T(8,128)(2,1)S(1)} %get-tuple-element.28), channel_id=1, source_target_pairs={{0,4},{2,6},{4,0},{6,2},{1,5},{3,7},{5,1},{7,3},{8,12},{10,14},{12... | collective-permute-start | bytes 663560 | tf_op jit(solution)/shard_map/ppermute | solution.py:149
  113.6 10.8 %collective-permute-start.26 = (bf16[864,128]{1,0:T(8,128)(2,1)S(1)}, bf16[864,128]{1,0:T(8,128)(2,1)S(1)}, u32[]{:S(2)}, u32[]{:S(2)}) collective-permute-start(bf16[864,128]{1,0:T(8,128)(2,1)S(1)} %get-tuple-element.27), channel_id=1, source_target_pairs={{0,6},{2,0},{4,2},{6,4},{1,7},{3,1},{5,3},{7,5},{8,14},{10,8},{12,... | collective-permute-start | bytes 663560 | tf_op jit(solution)/shard_map/ppermute | solution.py:149
  119.1 6.7 %copy-start.5 = (bf16[512,128]{1,0:T(8,128)(2,1)S(1)}, bf16[512,128]{1,0:T(8,128)(2,1)}, u32[]{:S(2)}) copy-start(bf16[512,128]{1,0:T(8,128)(2,1)} %copy-done.4) | copy-start | bytes 393220
  119.1 6.7 %copy-start.7 = (bf16[512,128]{1,0:T(8,128)(2,1)S(1)}, bf16[512,128]{1,0:T(8,128)(2,1)}, u32[]{:S(2)}) copy-start(bf16[512,128]{1,0:T(8,128)(2,1)} %copy-done.6) | copy-start | bytes 393220
  124.5 2.7 %collective-permute-start.27 = (f32[864,128]{1,0:T(8,128)S(1)}, f32[864,128]{1,0:T(8,128)S(1)}, u32[]{:S(2)}, u32[]{:S(2)}) collective-permute-start(f32[864,128]{1,0:T(8,128)S(1)} %convert_add_fusion), channel_id=1, source_target_pairs={{0,1},{1,0},{2,3},{3,2},{4,5},{5,4},{6,7},{7,6},{8,9},{9,8},{10,11... | collective-permute-start | bytes 1327112 | tf_op jit(solution)/shard_map/ppermute | solution.py:232

commit v16 on v13

--- a/solution.py
+++ b/solution.py
@@ -193,7 +193,8 @@
         activation = activate(values, gain_row).astype(jnp.bfloat16)
         start = cotangent[micro]
         start = jnp.where(live_now[:, None], start, jnp.zeros_like(start))
-        both = jnp.concatenate([cube(activation), cube(start)], axis=-1)
+        both = jnp.concatenate([cube(activation), cube(cotangent[micro])], axis=-1)
+        own = jnp.concatenate([cube(activation), cube(start)], axis=-1)
         if micro == 0:
             carried = {}
             riding = kernel[0] if n_x >= 3 else None
@@ -202,7 +203,7 @@
             flipped = weights.reshape(3, 3, 3, channels, channels)[::-1, ::-1, ::-1].transpose(0, 1, 2, 4, 3)
         else:
             got = exchange(both, ("sx", "sy"), (n_x, n_y), 0)
-        both_pad = assemble(both, got, table, split=True)
+        both_pad = assemble(own, got, table, split=True)
         act_pad = both_pad[..., :channels]
         centre = start
         received = None

time: 128 us -> 125 us (0.977)
  other arithmetic: 15.3 us -> 12.2 us
where the time goes in v16:
time: 125 us; the launch traced here: 123 us
  starting transfers between devices  50.7 us (41%)
  between operations  20.2 us (16%)
  waiting for transfers between devices  17.8 us (14%)
  matrix products  15.8 us (13%)
  other arithmetic  12.2 us (10%)
  local copies, waits for them, and re-layouts  6.49 us (5%)
    ppermute x20, starting transfers between devices, send(): return lax.ppermute(piece, axes, route)  41.2 us
    conv_general_dilated x4, matrix products, conv_data(): lax.conv_general_dilated(padded, filters, (1, 1, 1), 'VALID', dimension_n...  11.9 us
    ppermute x20, waiting for transfers between devices, send(): return lax.ppermute(piece, axes, route)  10.1 us
    ppermute x3, waiting for transfers between devices, scattered_sum(): lax.ppermute(piece, axis, [(i, (i + step) % count) for i in range(count)])  7.31 us
    ppermute x3, starting transfers between devices, shards(): centre = lax.ppermute(result, 'pipe', down)  5.76 us
    transpose x1, matrix products, shards(): per_tap.transpose(1, 2, 3, 0, 4).reshape(taps * channels, channels)  3.93 us
  transfers between devices with their start and end apart: 28, of which 6 were waited for; matrix products, arithmetic and copies ran while one was open for 12% of the time, Pallas kernels for 0%

profile of v16, /device:TPU:21, one launch (start us, length us, event | category | flops | bytes accessed | tf_op | source)
XLA Modules:
  0.0 123.2 jit_solution(6959732888467094006)
XLA Ops:
  0.6 1.0 convert_element_type.160
  1.6 1.1 fusion.25
  2.8 0.9 multiply_convert_fusion.2
  3.8 3.7 %collective-permute-start = (bf16[1,1,1,8,256]{4,3,2,1,0:T(8,128)(2,1)S(1)}, bf16[1,1,1,8,256]{4,3,2,1,0:T(8,128)(2,1)S(1)}, u32[]{:S(2)}, u32[]{:S(2)}) collective-permute-start(bf16[1,1,1,8,256]{4,3,2,1,0:T(8,128)(2,1)S(1)} %constant_dynamic-slice_fusion.13), channel_id=1, source_target_pairs={{0,3},{1,2},{2,5},{3,4},{4,7},{5,6},{8,11},{9,10},{10,13},{11,12},... | collective-permute-start | bytes 12296 | tf_op jit(solution)/shard_map/ppermute | solution.py:73
  7.5 0.3 collective-permute-start.5
  7.8 1.3 %collective-permute-start.1 = (bf16[992,128]{1,0:T(8,128)(2,1)S(1)}, bf16[992,128]{1,0:T(8,128)(2,1)S(1)}, u32[]{:S(2)}, u32[]{:S(2)}) collective-permute-start(bf16[992,128]{1,0:T(8,128)(2,1)S(1)} %get-tuple-element.40), channel_id=1, source_target_pairs={{0,2},{1,3},{2,4},{3,5},{4,6},{5,7},{6,0},{7,1},{8,10},{9,11},{10,... | collective-permute-start | bytes 761864 | tf_op jit(solution)/shard_map/ppermute | solution.py:73
  9.1 3.3 %collective-permute-start.2 = (bf16[1,1,1,8,256]{4,3,2,1,0:T(8,128)(2,1)S(1)}, bf16[1,1,1,8,256]{4,3,2,1,0:T(8,128)(2,1)S(1)}, u32[]{:S(2)}, u32[]{:S(2)}) collective-permute-start(bf16[1,1,1,8,256]{4,3,2,1,0:T(8,128)(2,1)S(1)} %constant_dynamic-slice_fusion.12), channel_id=1, source_target_pairs={{2,1},{3,0},{4,3},{5,2},{6,5},{7,4},{10,9},{11,8},{12,11},{13,10},... | collective-permute-start | bytes 12296 | tf_op jit(solution)/shard_map/ppermute | solution.py:73
  12.5 0.7 fusion.76
  13.2 0.7 fusion.75
  14.2 0.2 copy_dynamic-update-slice_fusion.1
  16.9 0.6 scatter_custom_fusion
  17.7 0.4 copy_dynamic-update-slice_fusion
  18.1 0.6 broadcast_select_fusion
  34.1 0.6 collective-permute-start.4
  34.9 0.7 collective-permute-done.4
  36.1 0.2 pad_maximum_fusion.10
  36.3 0.2 pad_maximum_fusion.11
  36.7 0.7 gather_fusion
  37.4 1.0 rev.3
  38.4 2.1 %pad_maximum_fusion = bf16[1,10,10,10,256]{4,0,3,2,1:T(2,128)(2,1)S(1)} fusion(bf16[1,1,10,10,256]{4,0,3,2,1:T(2,128)(2,1)S(1)} %pad_maximum_fusion.11, bf16[1,8,1,10,256]{4,0,3,2,1:T(2,128)(2,1)S(1)} %copy.48, bf16[1,8,8,1,256]{4,0,3,2,1:T(2,128)(2,1)S(1)} %get-tuple-element.30, bf16[1,8,8,8,256]{4,0,3,2,1:T(2,128)(2,1)S(1)} %broadcast_select_fusion, ...), kind=kLoop, calls=%fused_computation.4 | loop fusion | flops 1536000 | bytes 1024000 | tf_op jit(solution)/shard_map/concatenate | solution.py:56
  40.6 3.0 %fusion.1 = f32[1,8,8,8,128]{4,0,3,2,1:T(1,128)S(1)} fusion(bf16[3,3,3,128,128]{4,3,2,1,0:T(8,128)(2,1)S(1)} %copy-done.4, bf16[1,10,10,10,256]{4,0,3,2,1:T(2,128)(2,1)S(1)} %pad_maximum_fusion), kind=kOutput, calls=%fused_computation.10 | convolution fusion | flops 452984832 | bytes 1658880 | tf_op jit(solution)/shard_map/conv_general_dilated | solution.py:107
  43.6 0.3 fusion.47
  44.0 0.3 fusion.15
  44.4 1.9 %collective-permute-start.11 = (bf16[1,1,8,8,128]{4,3,2,1,0:T(8,128)(2,1)S(1)}, bf16[1,1,8,8,128]{4,3,2,1,0:T(8,128)(2,1)S(1)}, u32[]{:S(2)}, u32[]{:S(2)}) collective-permute-start(bf16[1,1,8,8,128]{4,3,2,1,0:T(8,128)(2,1)S(1)} %get-tuple-element.52), channel_id=1, source_target_pairs={{10,0},{11,1},{12,2},{13,3},{14,4},{15,5},{18,8},{19,9},{20,10},{2... | collective-permute-start | bytes 49160 | tf_op jit(solution)/shard_map/ppermute | solution.py:73
  46.3 3.1 %collective-permute-start.8 = (bf16[1,1,8,8,128]{4,3,2,1,0:T(8,128)(2,1)S(1)}, bf16[1,1,8,8,128]{4,3,2,1,0:T(8,128)(2,1)S(1)}, u32[]{:S(2)}, u32[]{:S(2)}) collective-permute-start(bf16[1,1,8,8,128]{4,3,2,1,0:T(8,128)(2,1)S(1)} %get-tuple-element.51), channel_id=1, source_target_pairs={{8,2},{9,3},{10,4},{11,5},{12,6},{13,7},{16,10},{17,11},{18,12},{1... | collective-permute-start | bytes 49160 | tf_op jit(solution)/shard_map/ppermute | solution.py:73
  49.5 3.6 %collective-permute-start.10 = (bf16[1,1,1,8,128]{4,3,2,1,0:T(8,128)(2,1)S(1)}, bf16[1,1,1,8,128]{4,3,2,1,0:T(8,128)(2,1)S(1)}, u32[]{:S(2)}, u32[]{:S(2)}) collective-permute-start(bf16[1,1,1,8,128]{4,3,2,1,0:T(8,128)(2,1)S(1)} %constant_dynamic-slice_fusion.9), channel_id=1, source_target_pairs={{10,1},{11,0},{12,3},{13,2},{14,5},{15,4},{18,9},{19,8},{20,11},{2... | collective-permute-start | bytes 6152 | tf_op jit(solution)/shard_map/ppermute | solution.py:73
  53.0 0.3 fusion.8
  53.4 1.9 %collective-permute-start.6 = (bf16[512,128]{1,0:T(8,128)(2,1)S(1)}, bf16[512,128]{1,0:T(8,128)(2,1)S(1)}, u32[]{:S(2)}, u32[]{:S(2)}) collective-permute-start(bf16[512,128]{1,0:T(8,128)(2,1)S(1)} %fusion.8), channel_id=1, source_target_pairs={{8,0},{16,8},{24,16},{9,1},{17,9},{25,17},{10,2},{18,10},{26,18},{... | collective-permute-start | bytes 393224 | tf_op jit(solution)/shard_map/ppermute | solution.py:229
  55.3 1.9 %collective-permute-start.9 = (bf16[1,8,1,8,128]{4,3,2,1,0:T(8,128)(2,1)S(1)}, bf16[1,8,1,8,128]{4,3,2,1,0:T(8,128)(2,1)S(1)}, u32[]{:S(2)}, u32[]{:S(2)}) collective-permute-start(bf16[1,8,1,8,128]{4,3,2,1,0:T(8,128)(2,1)S(1)} %constant_dynamic-slice_fusion.10), channel_id=1, source_target_pairs={{8,1},{9,0},{10,3},{11,2},{12,5},{13,4},{14,7},{15,6},{16,9},{17,8... | collective-permute-start | bytes 49160 | tf_op jit(solution)/shard_map/ppermute | solution.py:73
  57.2 2.1 %collective-permute-start.7 = (bf16[1,1,1,8,128]{4,3,2,1,0:T(8,128)(2,1)S(1)}, bf16[1,1,1,8,128]{4,3,2,1,0:T(8,128)(2,1)S(1)}, u32[]{:S(2)}, u32[]{:S(2)}) collective-permute-start(bf16[1,1,1,8,128]{4,3,2,1,0:T(8,128)(2,1)S(1)} %constant_dynamic-slice_fusion.11), channel_id=1, source_target_pairs={{8,3},{9,2},{10,5},{11,4},{12,7},{13,6},{16,11},{17,10},{18,13},{1... | collective-permute-start | bytes 6152 | tf_op jit(solution)/shard_map/ppermute | solution.py:73
  59.4 4.6 %collective-permute-done.7 = bf16[1,1,1,8,128]{4,3,2,1,0:T(8,128)(2,1)S(1)} collective-permute-done((bf16[1,1,1,8,128]{4,3,2,1,0:T(8,128)(2,1)S(1)}, bf16[1,1,1,8,128]{4,3,2,1,0:T(8,128)(2,1)S(1)}, u32[]{:S(2)}, u32[]{:S(2)}) %collective-permute-start.7) | collective-permute-done | bytes 2080 | tf_op jit(solution)/shard_map/ppermute | solution.py:73
  64.6 0.2 copy.53
  64.8 3.0 %fusion.5 = f32[1,8,8,8,128]{4,0,3,2,1:T(1,128)S(1)} fusion(bf16[3,3,3,128,128]{4,3,2,1,0:T(8,128)(2,1)S(1)} %bitcast.212, bf16[1,1,10,10,128]{4,0,3,2,1:T(2,128)(2,1)S(1)} %copy.57, bf16[1,8,1,10,128]{4,0,3,2,1:T(2,128)(2,1)S(1)} %copy.55, bf16[1,8,8,1,128]{4,0,3,2,1:T(2,128)(2,1)S(1)} %slice_bitcast_fusion.6, bf16[1,8,8,8,128]{4,0,3,2,1:T(2,128)(2,1)S(1)} %copy.53, ...), kind=kOutput, calls=%fused_computation.14 | convolution fusion | flops 454776832 | bytes 1402880 | tf_op jit(solution)/shard_map/conv_general_dilated | solution.py:107
  67.8 0.3 fusion.48
  68.2 0.3 fusion.18
  68.5 1.9 %collective-permute-start.12 = (bf16[512,128]{1,0:T(8,128)(2,1)S(1)}, bf16[512,128]{1,0:T(8,128)(2,1)S(1)}, u32[]{:S(2)}, u32[]{:S(2)}) collective-permute-start(bf16[512,128]{1,0:T(8,128)(2,1)S(1)} %fusion.18), channel_id=1, source_target_pairs={{8,0},{16,8},{24,16},{9,1},{17,9},{25,17},{10,2},{18,10},{26,18},{... | collective-permute-start | bytes 393224 | tf_op jit(solution)/shard_map/ppermute | solution.py:229
  70.5 1.9 %collective-permute-start.17 = (bf16[1,1,8,8,128]{4,3,2,1,0:T(8,128)(2,1)S(1)}, bf16[1,1,8,8,128]{4,3,2,1,0:T(8,128)(2,1)S(1)}, u32[]{:S(2)}, u32[]{:S(2)}) collective-permute-start(bf16[1,1,8,8,128]{4,3,2,1,0:T(8,128)(2,1)S(1)} %get-tuple-element.47), channel_id=1, source_target_pairs={{10,0},{11,1},{12,2},{13,3},{14,4},{15,5},{18,8},{19,9},{20,10},{2... | collective-permute-start | bytes 49160 | tf_op jit(solution)/shard_map/ppermute | solution.py:73
  72.4 1.9 %collective-permute-start.16 = (bf16[1,1,1,8,128]{4,3,2,1,0:T(8,128)(2,1)S(1)}, bf16[1,1,1,8,128]{4,3,2,1,0:T(8,128)(2,1)S(1)}, u32[]{:S(2)}, u32[]{:S(2)}) collective-permute-start(bf16[1,1,1,8,128]{4,3,2,1,0:T(8,128)(2,1)S(1)} %constant_dynamic-slice_fusion.6), channel_id=1, source_target_pairs={{10,1},{11,0},{12,3},{13,2},{14,5},{15,4},{18,9},{19,8},{20,11},{2... | collective-permute-start | bytes 6152 | tf_op jit(solution)/shard_map/ppermute | solution.py:73
  74.4 1.9 %collective-permute-start.14 = (bf16[1,1,8,8,128]{4,3,2,1,0:T(8,128)(2,1)S(1)}, bf16[1,1,8,8,128]{4,3,2,1,0:T(8,128)(2,1)S(1)}, u32[]{:S(2)}, u32[]{:S(2)}) collective-permute-start(bf16[1,1,8,8,128]{4,3,2,1,0:T(8,128)(2,1)S(1)} %get-tuple-element.46), channel_id=1, source_target_pairs={{8,2},{9,3},{10,4},{11,5},{12,6},{13,7},{16,10},{17,11},{18,12},{1... | collective-permute-start | bytes 49160 | tf_op jit(solution)/shard_map/ppermute | solution.py:73
  76.3 1.9 %collective-permute-start.15 = (bf16[1,8,1,8,128]{4,3,2,1,0:T(8,128)(2,1)S(1)}, bf16[1,8,1,8,128]{4,3,2,1,0:T(8,128)(2,1)S(1)}, u32[]{:S(2)}, u32[]{:S(2)}) collective-permute-start(bf16[1,8,1,8,128]{4,3,2,1,0:T(8,128)(2,1)S(1)} %constant_dynamic-slice_fusion.7), channel_id=1, source_target_pairs={{8,1},{9,0},{10,3},{11,2},{12,5},{13,4},{14,7},{15,6},{16,9},{17,8... | collective-permute-start | bytes 49160 | tf_op jit(solution)/shard_map/ppermute | solution.py:73
  78.2 1.9 %collective-permute-start.13 = (bf16[1,1,1,8,128]{4,3,2,1,0:T(8,128)(2,1)S(1)}, bf16[1,1,1,8,128]{4,3,2,1,0:T(8,128)(2,1)S(1)}, u32[]{:S(2)}, u32[]{:S(2)}) collective-permute-start(bf16[1,1,1,8,128]{4,3,2,1,0:T(8,128)(2,1)S(1)} %constant_dynamic-slice_fusion.8), channel_id=1, source_target_pairs={{8,3},{9,2},{10,5},{11,4},{12,7},{13,6},{16,11},{17,10},{18,13},{1... | collective-permute-start | bytes 6152 | tf_op jit(solution)/shard_map/ppermute | solution.py:73
  80.2 4.8 %collective-permute-done.13 = bf16[1,1,1,8,128]{4,3,2,1,0:T(8,128)(2,1)S(1)} collective-permute-done((bf16[1,1,1,8,128]{4,3,2,1,0:T(8,128)(2,1)S(1)}, bf16[1,1,1,8,128]{4,3,2,1,0:T(8,128)(2,1)S(1)}, u32[]{:S(2)}, u32[]{:S(2)}) %collective-permute-start.13) | collective-permute-done | bytes 2080 | tf_op jit(solution)/shard_map/ppermute | solution.py:73
  85.6 0.2 copy.60
  85.8 3.0 %fusion.4 = f32[1,8,8,8,128]{4,0,3,2,1:T(1,128)S(1)} fusion(bf16[3,3,3,128,128]{4,3,2,1,0:T(8,128)(2,1)S(1)} %bitcast.213, bf16[1,1,10,10,128]{4,0,3,2,1:T(2,128)(2,1)S(1)} %copy.64, bf16[1,8,1,10,128]{4,0,3,2,1:T(2,128)(2,1)S(1)} %copy.62, bf16[1,8,8,1,128]{4,0,3,2,1:T(2,128)(2,1)S(1)} %slice_bitcast_fusion.4, bf16[1,8,8,8,128]{4,0,3,2,1:T(2,128)(2,1)S(1)} %copy.60, ...), kind=kOutput, calls=%fused_computation.13 | convolution fusion | flops 454776832 | bytes 1402880 | tf_op jit(solution)/shard_map/conv_general_dilated | solution.py:107
  88.8 0.3 fusion.49
  89.2 0.3 fusion.21
  89.5 1.9 %collective-permute-start.18 = (bf16[512,128]{1,0:T(8,128)(2,1)S(1)}, bf16[512,128]{1,0:T(8,128)(2,1)S(1)}, u32[]{:S(2)}, u32[]{:S(2)}) collective-permute-start(bf16[512,128]{1,0:T(8,128)(2,1)S(1)} %fusion.21), channel_id=1, source_target_pairs={{8,0},{16,8},{24,16},{9,1},{17,9},{25,17},{10,2},{18,10},{26,18},{... | collective-permute-start | bytes 393224 | tf_op jit(solution)/shard_map/ppermute | solution.py:229
  91.4 1.9 %collective-permute-start.20 = (bf16[1,1,8,8,128]{4,3,2,1,0:T(8,128)(2,1)S(1)}, bf16[1,1,8,8,128]{4,3,2,1,0:T(8,128)(2,1)S(1)}, u32[]{:S(2)}, u32[]{:S(2)}) collective-permute-start(bf16[1,1,8,8,128]{4,3,2,1,0:T(8,128)(2,1)S(1)} %get-tuple-element.45), channel_id=1, source_target_pairs={{8,2},{9,3},{10,4},{11,5},{12,6},{13,7},{16,10},{17,11},{18,12},{1... | collective-permute-start | bytes 49160 | tf_op jit(solution)/shard_map/ppermute | solution.py:73
  93.4 1.9 %collective-permute-start.19 = (bf16[1,1,1,8,128]{4,3,2,1,0:T(8,128)(2,1)S(1)}, bf16[1,1,1,8,128]{4,3,2,1,0:T(8,128)(2,1)S(1)}, u32[]{:S(2)}, u32[]{:S(2)}) collective-permute-start(bf16[1,1,1,8,128]{4,3,2,1,0:T(8,128)(2,1)S(1)} %constant_dynamic-slice_fusion.5), channel_id=1, source_target_pairs={{8,3},{9,2},{10,5},{11,4},{12,7},{13,6},{16,11},{17,10},{18,13},{1... | collective-permute-start | bytes 6152 | tf_op jit(solution)/shard_map/ppermute | solution.py:73
  95.3 1.9 %collective-permute-start.21 = (bf16[1,8,1,8,128]{4,3,2,1,0:T(8,128)(2,1)S(1)}, bf16[1,8,1,8,128]{4,3,2,1,0:T(8,128)(2,1)S(1)}, u32[]{:S(2)}, u32[]{:S(2)}) collective-permute-start(bf16[1,8,1,8,128]{4,3,2,1,0:T(8,128)(2,1)S(1)} %constant_dynamic-slice_fusion.4), channel_id=1, source_target_pairs={{8,1},{9,0},{10,3},{11,2},{12,5},{13,4},{14,7},{15,6},{16,9},{17,8... | collective-permute-start | bytes 49160 | tf_op jit(solution)/shard_map/ppermute | solution.py:73
  97.2 1.9 %collective-permute-start.23 = (bf16[1,1,8,8,128]{4,3,2,1,0:T(8,128)(2,1)S(1)}, bf16[1,1,8,8,128]{4,3,2,1,0:T(8,128)(2,1)S(1)}, u32[]{:S(2)}, u32[]{:S(2)}) collective-permute-start(bf16[1,1,8,8,128]{4,3,2,1,0:T(8,128)(2,1)S(1)} %get-tuple-element.44), channel_id=1, source_target_pairs={{10,0},{11,1},{12,2},{13,3},{14,4},{15,5},{18,8},{19,9},{20,10},{2... | collective-permute-start | bytes 49160 | tf_op jit(solution)/shard_map/ppermute | solution.py:73
  99.2 2.4 %collective-permute-start.22 = (bf16[1,1,1,8,128]{4,3,2,1,0:T(8,128)(2,1)S(1)}, bf16[1,1,1,8,128]{4,3,2,1,0:T(8,128)(2,1)S(1)}, u32[]{:S(2)}, u32[]{:S(2)}) collective-permute-start(bf16[1,1,1,8,128]{4,3,2,1,0:T(8,128)(2,1)S(1)} %constant_dynamic-slice_fusion.3), channel_id=1, source_target_pairs={{10,1},{11,0},{12,3},{13,2},{14,5},{15,4},{18,9},{19,8},{20,11},{2... | collective-permute-start | bytes 6152 | tf_op jit(solution)/shard_map/ppermute | solution.py:73
  101.8 3.9 %multiply_convert_fusion = bf16[3,3,3,128,128]{4,3,2,1,0:T(8,128)(2,1)S(1)} fusion(bf16[1,10,10,10,256]{4,0,3,2,1:T(2,128)(2,1)S(1)} %copy-done.3, bf16[1,8,8,8,128]{4,3,2,1,0:T(8,128)(2,1)S(1)} %bitcast.244), kind=kOutput, calls=%fused_computation.2 | convolution fusion | flops 453869568 | bytes 1527808 | tf_op jit(solution)/shard_map/transpose | solution.py:217
  106.2 0.2 copy.68
  106.8 1.4 %collective-permute-start.26 = (bf16[864,128]{1,0:T(8,128)(2,1)S(1)}, bf16[864,128]{1,0:T(8,128)(2,1)S(1)}, u32[]{:S(2)}, u32[]{:S(2)}) collective-permute-start(bf16[864,128]{1,0:T(8,128)(2,1)S(1)} %get-tuple-element.27), channel_id=1, source_target_pairs={{0,6},{2,0},{4,2},{6,4},{1,7},{3,1},{5,3},{7,5},{8,14},{10,8},{12,... | collective-permute-start | bytes 663560 | tf_op jit(solution)/shard_map/ppermute | solution.py:150
  108.2 0.4 collective-permute-start.24
  108.5 3.0 %fusion.3 = f32[1,8,8,8,128]{4,0,3,2,1:T(1,128)S(1)} fusion(bf16[3,3,3,128,128]{4,3,2,1,0:T(8,128)(2,1)S(1)} %bitcast.214, bf16[1,1,10,10,128]{4,0,3,2,1:T(2,128)(2,1)S(1)} %copy.72, bf16[1,8,1,10,128]{4,0,3,2,1:T(2,128)(2,1)S(1)} %copy.70, bf16[1,8,8,1,128]{4,0,3,2,1:T(2,128)(2,1)S(1)} %slice_bitcast_fusion.2, bf16[1,8,8,8,128]{4,0,3,2,1:T(2,128)(2,1)S(1)} %copy.68, ...), kind=kOutput, calls=%fused_computation.12 | convolution fusion | flops 454776832 | bytes 1402880 | tf_op jit(solution)/shard_map/conv_general_dilated | solution.py:107
  111.6 0.3 fusion.50
  111.9 1.6 %collective-permute-done.26 = bf16[864,128]{1,0:T(8,128)(2,1)S(1)} collective-permute-done((bf16[864,128]{1,0:T(8,128)(2,1)S(1)}, bf16[864,128]{1,0:T(8,128)(2,1)S(1)}, u32[]{:S(2)}, u32[]{:S(2)}) %collective-permute-start.26) | collective-permute-done | bytes 221216 | tf_op jit(solution)/shard_map/ppermute | solution.py:150
  113.5 5.8 %collective-permute-done.25 = bf16[864,128]{1,0:T(8,128)(2,1)S(1)} collective-permute-done((bf16[864,128]{1,0:T(8,128)(2,1)S(1)}, bf16[864,128]{1,0:T(8,128)(2,1)S(1)}, u32[]{:S(2)}, u32[]{:S(2)}) %collective-permute-start.25) | collective-permute-done | bytes 221216 | tf_op jit(solution)/shard_map/ppermute | solution.py:150
  119.3 1.6 %collective-permute-start.27 = (f32[864,128]{1,0:T(8,128)S(1)}, f32[864,128]{1,0:T(8,128)S(1)}, u32[]{:S(2)}, u32[]{:S(2)}) collective-permute-start(f32[864,128]{1,0:T(8,128)S(1)} %convert_add_fusion), channel_id=1, source_target_pairs={{0,1},{1,0},{2,3},{3,2},{4,5},{5,4},{6,7},{7,6},{8,9},{9,8},{10,11... | collective-permute-start | bytes 1327112 | tf_op jit(solution)/shard_map/ppermute | solution.py:234
  121.0 1.0 fusion.53
  122.0 0.4 collective-permute-done.27
  122.4 0.8 add_bitcast_fusion
  (203 shorter events, 3.6 us)
Async XLA Ops:
  0.6 3.1 %copy-start.1 = (bf16[1,1,1,512,128]{4,3,2,1,0:T(8,128)(2,1)S(1)}, bf16[1,1,1,512,128]{4,3,2,1,0:T(8,128)(2,1)}, u32[]{:S(2)}) copy-start(bf16[1,1,1,512,128]{4,3,2,1,0:T(8,128)(2,1)} %param.7) | copy-start | bytes 393220
  0.6 6.8 %copy-start.5 = (bf16[1,864,128]{2,1,0:T(8,128)(2,1)S(1)}, bf16[1,864,128]{2,1,0:T(8,128)(2,1)}, u32[]{:S(2)}) copy-start(bf16[1,864,128]{2,1,0:T(8,128)(2,1)} %param.11) | copy-start | bytes 663556
  1.6 10.9 %copy-start.10 = (s32[1,1,1,1,27]{4,3,2,1,0:T(1,128)S(1)}, s32[1,1,1,1,27]{4,3,2,1,0:T(1,128)}, u32[]{:S(2)}) copy-start(s32[1,1,1,1,27]{4,3,2,1,0:T(1,128)} %param.8) | copy-start | bytes 328
  2.8 11.2 %copy-start.11 = (f32[1,128]{1,0:T(1,128)S(1)}, f32[1,128]{1,0:T(1,128)}, u32[]{:S(2)}) copy-start(f32[1,128]{1,0:T(1,128)} %param.10) | copy-start | bytes 1540
  3.8 30.4 %collective-permute-start = (bf16[1,1,1,8,256]{4,3,2,1,0:T(8,128)(2,1)S(1)}, bf16[1,1,1,8,256]{4,3,2,1,0:T(8,128)(2,1)S(1)}, u32[]{:S(2)}, u32[]{:S(2)}) collective-permute-start(bf16[1,1,1,8,256]{4,3,2,1,0:T(8,128)(2,1)S(1)} %constant_dynamic-slice_fusion.13), channel_id=1, source_target_pairs={{0,3},{1,2},{2,5},{3,4},{4,7},{5,6},{8,11},{9,10},{10,13},{11,12},... | collective-permute-start | bytes 12296 | tf_op jit(solution)/shard_map/ppermute | solution.py:73
  7.5 29.1 %collective-permute-start.5 = (bf16[864,128]{1,0:T(8,128)(2,1)S(1)}, bf16[864,128]{1,0:T(8,128)(2,1)S(1)}, u32[]{:S(2)}, u32[]{:S(2)}) collective-permute-start(bf16[864,128]{1,0:T(8,128)(2,1)S(1)} %bitcast.224), channel_id=1, source_target_pairs={{0,4},{2,6},{4,0},{6,2},{1,5},{3,7},{5,1},{7,3},{8,12},{10,14},{12... | collective-permute-start | bytes 663560 | tf_op jit(solution)/shard_map/ppermute | solution.py:136
  7.8 28.0 %collective-permute-start.1 = (bf16[992,128]{1,0:T(8,128)(2,1)S(1)}, bf16[992,128]{1,0:T(8,128)(2,1)S(1)}, u32[]{:S(2)}, u32[]{:S(2)}) collective-permute-start(bf16[992,128]{1,0:T(8,128)(2,1)S(1)} %get-tuple-element.40), channel_id=1, source_target_pairs={{0,2},{1,3},{2,4},{3,5},{4,6},{5,7},{6,0},{7,1},{8,10},{9,11},{10,... | collective-permute-start | bytes 761864 | tf_op jit(solution)/shard_map/ppermute | solution.py:73
  9.1 25.6 %collective-permute-start.2 = (bf16[1,1,1,8,256]{4,3,2,1,0:T(8,128)(2,1)S(1)}, bf16[1,1,1,8,256]{4,3,2,1,0:T(8,128)(2,1)S(1)}, u32[]{:S(2)}, u32[]{:S(2)}) collective-permute-start(bf16[1,1,1,8,256]{4,3,2,1,0:T(8,128)(2,1)S(1)} %constant_dynamic-slice_fusion.12), channel_id=1, source_target_pairs={{2,1},{3,0},{4,3},{5,2},{6,5},{7,4},{10,9},{11,8},{12,11},{13,10},... | collective-permute-start | bytes 12296 | tf_op jit(solution)/shard_map/ppermute | solution.py:73
  12.4 23.5 %collective-permute-start.3 = (bf16[992,128]{1,0:T(8,128)(2,1)S(1)}, bf16[992,128]{1,0:T(8,128)(2,1)S(1)}, u32[]{:S(2)}, u32[]{:S(2)}) collective-permute-start(bf16[992,128]{1,0:T(8,128)(2,1)S(1)} %get-tuple-element.39), channel_id=1, source_target_pairs={{0,6},{1,7},{2,0},{3,1},{4,2},{5,3},{6,4},{7,5},{8,14},{9,15},{10,... | collective-permute-start | bytes 761864 | tf_op jit(solution)/shard_map/ppermute | solution.py:73
  34.1 1.4 %collective-permute-start.4 = (bf16[1,8,1,8,256]{4,3,2,1,0:T(8,128)(2,1)S(1)}, bf16[1,8,1,8,256]{4,3,2,1,0:T(8,128)(2,1)S(1)}, u32[]{:S(2)}, u32[]{:S(2)}) collective-permute-start(bf16[1,8,1,8,256]{4,3,2,1,0:T(8,128)(2,1)S(1)} %fusion.57), channel_id=1, source_target_pairs={{0,1},{1,0},{2,3},{3,2},{4,5},{5,4},{6,7},{7,6},{8,9},{9,8},{10,11... | collective-permute-start | bytes 98312 | tf_op jit(solution)/shard_map/ppermute | solution.py:73
  38.4 2.1 %copy-start.4 = (bf16[3,3,3,128,128]{4,3,2,1,0:T(8,128)(2,1)S(1)}, bf16[3,3,3,128,128]{4,3,2,1,0:T(8,128)(2,1)}, u32[]{:S(2)}) copy-start(bf16[3,3,3,128,128]{4,3,2,1,0:T(8,128)(2,1)} %rev.3) | copy-start | bytes 2654212
  40.5 3.0 %copy-start.2 = (bf16[1,10,10,10,256]{4,0,3,2,1:T(2,128)(2,1)}, bf16[1,10,10,10,256]{4,0,3,2,1:T(2,128)(2,1)S(1)}, u32[]{:S(2)}) copy-start(bf16[1,10,10,10,256]{4,0,3,2,1:T(2,128)(2,1)S(1)} %pad_maximum_fusion) | copy-start | bytes 1536004
  40.6 3.0 %copy-start = (bf16[1,1,1,1,512,128]{5,4,3,2,1,0:T(8,128)(2,1)S(1)}, bf16[1,1,1,1,512,128]{5,4,3,2,1,0:T(8,128)(2,1)}, u32[]{:S(2)}) copy-start(bf16[1,1,1,1,512,128]{5,4,3,2,1,0:T(8,128)(2,1)} %param.6) | copy-start | bytes 393220
  44.4 19.7 %collective-permute-start.11 = (bf16[1,1,8,8,128]{4,3,2,1,0:T(8,128)(2,1)S(1)}, bf16[1,1,8,8,128]{4,3,2,1,0:T(8,128)(2,1)S(1)}, u32[]{:S(2)}, u32[]{:S(2)}) collective-permute-start(bf16[1,1,8,8,128]{4,3,2,1,0:T(8,128)(2,1)S(1)} %get-tuple-element.52), channel_id=1, source_target_pairs={{10,0},{11,1},{12,2},{13,3},{14,4},{15,5},{18,8},{19,9},{20,10},{2... | collective-permute-start | bytes 49160 | tf_op jit(solution)/shard_map/ppermute | solution.py:73
  46.3 17.9 %collective-permute-start.8 = (bf16[1,1,8,8,128]{4,3,2,1,0:T(8,128)(2,1)S(1)}, bf16[1,1,8,8,128]{4,3,2,1,0:T(8,128)(2,1)S(1)}, u32[]{:S(2)}, u32[]{:S(2)}) collective-permute-start(bf16[1,1,8,8,128]{4,3,2,1,0:T(8,128)(2,1)S(1)} %get-tuple-element.51), channel_id=1, source_target_pairs={{8,2},{9,3},{10,4},{11,5},{12,6},{13,7},{16,10},{17,11},{18,12},{1... | collective-permute-start | bytes 49160 | tf_op jit(solution)/shard_map/ppermute | solution.py:73
  49.5 7.8 %collective-permute-start.10 = (bf16[1,1,1,8,128]{4,3,2,1,0:T(8,128)(2,1)S(1)}, bf16[1,1,1,8,128]{4,3,2,1,0:T(8,128)(2,1)S(1)}, u32[]{:S(2)}, u32[]{:S(2)}) collective-permute-start(bf16[1,1,1,8,128]{4,3,2,1,0:T(8,128)(2,1)S(1)} %constant_dynamic-slice_fusion.9), channel_id=1, source_target_pairs={{10,1},{11,0},{12,3},{13,2},{14,5},{15,4},{18,9},{19,8},{20,11},{2... | collective-permute-start | bytes 6152 | tf_op jit(solution)/shard_map/ppermute | solution.py:73
  53.4 14.5 %copy-start.8 = (bf16[512,128]{1,0:T(8,128)(2,1)}, bf16[512,128]{1,0:T(8,128)(2,1)S(1)}, u32[]{:S(2)}) copy-start(bf16[512,128]{1,0:T(8,128)(2,1)S(1)} %fusion.8) | copy-start | bytes 393220
  53.4 11.1 %collective-permute-start.6 = (bf16[512,128]{1,0:T(8,128)(2,1)S(1)}, bf16[512,128]{1,0:T(8,128)(2,1)S(1)}, u32[]{:S(2)}, u32[]{:S(2)}) collective-permute-start(bf16[512,128]{1,0:T(8,128)(2,1)S(1)} %fusion.8), channel_id=1, source_target_pairs={{8,0},{16,8},{24,16},{9,1},{17,9},{25,17},{10,2},{18,10},{26,18},{... | collective-permute-start | bytes 393224 | tf_op jit(solution)/shard_map/ppermute | solution.py:229
  55.3 8.8 %collective-permute-start.9 = (bf16[1,8,1,8,128]{4,3,2,1,0:T(8,128)(2,1)S(1)}, bf16[1,8,1,8,128]{4,3,2,1,0:T(8,128)(2,1)S(1)}, u32[]{:S(2)}, u32[]{:S(2)}) collective-permute-start(bf16[1,8,1,8,128]{4,3,2,1,0:T(8,128)(2,1)S(1)} %constant_dynamic-slice_fusion.10), channel_id=1, source_target_pairs={{8,1},{9,0},{10,3},{11,2},{12,5},{13,4},{14,7},{15,6},{16,9},{17,8... | collective-permute-start | bytes 49160 | tf_op jit(solution)/shard_map/ppermute | solution.py:73
  57.2 6.7 %collective-permute-start.7 = (bf16[1,1,1,8,128]{4,3,2,1,0:T(8,128)(2,1)S(1)}, bf16[1,1,1,8,128]{4,3,2,1,0:T(8,128)(2,1)S(1)}, u32[]{:S(2)}, u32[]{:S(2)}) collective-permute-start(bf16[1,1,1,8,128]{4,3,2,1,0:T(8,128)(2,1)S(1)} %constant_dynamic-slice_fusion.11), channel_id=1, source_target_pairs={{8,3},{9,2},{10,5},{11,4},{12,7},{13,6},{16,11},{17,10},{18,13},{1... | collective-permute-start | bytes 6152 | tf_op jit(solution)/shard_map/ppermute | solution.py:73
  68.5 20.3 %copy-start.6 = (bf16[512,128]{1,0:T(8,128)(2,1)}, bf16[512,128]{1,0:T(8,128)(2,1)S(1)}, u32[]{:S(2)}) copy-start(bf16[512,128]{1,0:T(8,128)(2,1)S(1)} %fusion.18) | copy-start | bytes 393220
  68.5 17.0 %collective-permute-start.12 = (bf16[512,128]{1,0:T(8,128)(2,1)S(1)}, bf16[512,128]{1,0:T(8,128)(2,1)S(1)}, u32[]{:S(2)}, u32[]{:S(2)}) collective-permute-start(bf16[512,128]{1,0:T(8,128)(2,1)S(1)} %fusion.18), channel_id=1, source_target_pairs={{8,0},{16,8},{24,16},{9,1},{17,9},{25,17},{10,2},{18,10},{26,18},{... | collective-permute-start | bytes 393224 | tf_op jit(solution)/shard_map/ppermute | solution.py:229
  70.5 14.6 %collective-permute-start.17 = (bf16[1,1,8,8,128]{4,3,2,1,0:T(8,128)(2,1)S(1)}, bf16[1,1,8,8,128]{4,3,2,1,0:T(8,128)(2,1)S(1)}, u32[]{:S(2)}, u32[]{:S(2)}) collective-permute-start(bf16[1,1,8,8,128]{4,3,2,1,0:T(8,128)(2,1)S(1)} %get-tuple-element.47), channel_id=1, source_target_pairs={{10,0},{11,1},{12,2},{13,3},{14,4},{15,5},{18,8},{19,9},{20,10},{2... | collective-permute-start | bytes 49160 | tf_op jit(solution)/shard_map/ppermute | solution.py:73
  72.4 5.8 %collective-permute-start.16 = (bf16[1,1,1,8,128]{4,3,2,1,0:T(8,128)(2,1)S(1)}, bf16[1,1,1,8,128]{4,3,2,1,0:T(8,128)(2,1)S(1)}, u32[]{:S(2)}, u32[]{:S(2)}) collective-permute-start(bf16[1,1,1,8,128]{4,3,2,1,0:T(8,128)(2,1)S(1)} %constant_dynamic-slice_fusion.6), channel_id=1, source_target_pairs={{10,1},{11,0},{12,3},{13,2},{14,5},{15,4},{18,9},{19,8},{20,11},{2... | collective-permute-start | bytes 6152 | tf_op jit(solution)/shard_map/ppermute | solution.py:73
  74.4 10.8 %collective-permute-start.14 = (bf16[1,1,8,8,128]{4,3,2,1,0:T(8,128)(2,1)S(1)}, bf16[1,1,8,8,128]{4,3,2,1,0:T(8,128)(2,1)S(1)}, u32[]{:S(2)}, u32[]{:S(2)}) collective-permute-start(bf16[1,1,8,8,128]{4,3,2,1,0:T(8,128)(2,1)S(1)} %get-tuple-element.46), channel_id=1, source_target_pairs={{8,2},{9,3},{10,4},{11,5},{12,6},{13,7},{16,10},{17,11},{18,12},{1... | collective-permute-start | bytes 49160 | tf_op jit(solution)/shard_map/ppermute | solution.py:73
  76.3 8.8 %collective-permute-start.15 = (bf16[1,8,1,8,128]{4,3,2,1,0:T(8,128)(2,1)S(1)}, bf16[1,8,1,8,128]{4,3,2,1,0:T(8,128)(2,1)S(1)}, u32[]{:S(2)}, u32[]{:S(2)}) collective-permute-start(bf16[1,8,1,8,128]{4,3,2,1,0:T(8,128)(2,1)S(1)} %constant_dynamic-slice_fusion.7), channel_id=1, source_target_pairs={{8,1},{9,0},{10,3},{11,2},{12,5},{13,4},{14,7},{15,6},{16,9},{17,8... | collective-permute-start | bytes 49160 | tf_op jit(solution)/shard_map/ppermute | solution.py:73
  78.2 6.7 %collective-permute-start.13 = (bf16[1,1,1,8,128]{4,3,2,1,0:T(8,128)(2,1)S(1)}, bf16[1,1,1,8,128]{4,3,2,1,0:T(8,128)(2,1)S(1)}, u32[]{:S(2)}, u32[]{:S(2)}) collective-permute-start(bf16[1,1,1,8,128]{4,3,2,1,0:T(8,128)(2,1)S(1)} %constant_dynamic-slice_fusion.8), channel_id=1, source_target_pairs={{8,3},{9,2},{10,5},{11,4},{12,7},{13,6},{16,11},{17,10},{18,13},{1... | collective-permute-start | bytes 6152 | tf_op jit(solution)/shard_map/ppermute | solution.py:73
  88.8 13.0 %copy-start.3 = (bf16[1,10,10,10,256]{4,0,3,2,1:T(2,128)(2,1)S(1)}, bf16[1,10,10,10,256]{4,0,3,2,1:T(2,128)(2,1)}, u32[]{:S(2)}) copy-start(bf16[1,10,10,10,256]{4,0,3,2,1:T(2,128)(2,1)} %copy-done.2) | copy-start | bytes 1536004
  89.5 9.7 %collective-permute-start.18 = (bf16[512,128]{1,0:T(8,128)(2,1)S(1)}, bf16[512,128]{1,0:T(8,128)(2,1)S(1)}, u32[]{:S(2)}, u32[]{:S(2)}) collective-permute-start(bf16[512,128]{1,0:T(8,128)(2,1)S(1)} %fusion.21), channel_id=1, source_target_pairs={{8,0},{16,8},{24,16},{9,1},{17,9},{25,17},{10,2},{18,10},{26,18},{... | collective-permute-start | bytes 393224 | tf_op jit(solution)/shard_map/ppermute | solution.py:229
  91.4 14.3 %collective-permute-start.20 = (bf16[1,1,8,8,128]{4,3,2,1,0:T(8,128)(2,1)S(1)}, bf16[1,1,8,8,128]{4,3,2,1,0:T(8,128)(2,1)S(1)}, u32[]{:S(2)}, u32[]{:S(2)}) collective-permute-start(bf16[1,1,8,8,128]{4,3,2,1,0:T(8,128)(2,1)S(1)} %get-tuple-element.45), channel_id=1, source_target_pairs={{8,2},{9,3},{10,4},{11,5},{12,6},{13,7},{16,10},{17,11},{18,12},{1... | collective-permute-start | bytes 49160 | tf_op jit(solution)/shard_map/ppermute | solution.py:73
  93.4 12.3 %collective-permute-start.19 = (bf16[1,1,1,8,128]{4,3,2,1,0:T(8,128)(2,1)S(1)}, bf16[1,1,1,8,128]{4,3,2,1,0:T(8,128)(2,1)S(1)}, u32[]{:S(2)}, u32[]{:S(2)}) collective-permute-start(bf16[1,1,1,8,128]{4,3,2,1,0:T(8,128)(2,1)S(1)} %constant_dynamic-slice_fusion.5), channel_id=1, source_target_pairs={{8,3},{9,2},{10,5},{11,4},{12,7},{13,6},{16,11},{17,10},{18,13},{1... | collective-permute-start | bytes 6152 | tf_op jit(solution)/shard_map/ppermute | solution.py:73
  95.3 10.4 %collective-permute-start.21 = (bf16[1,8,1,8,128]{4,3,2,1,0:T(8,128)(2,1)S(1)}, bf16[1,8,1,8,128]{4,3,2,1,0:T(8,128)(2,1)S(1)}, u32[]{:S(2)}, u32[]{:S(2)}) collective-permute-start(bf16[1,8,1,8,128]{4,3,2,1,0:T(8,128)(2,1)S(1)} %constant_dynamic-slice_fusion.4), channel_id=1, source_target_pairs={{8,1},{9,0},{10,3},{11,2},{12,5},{13,4},{14,7},{15,6},{16,9},{17,8... | collective-permute-start | bytes 49160 | tf_op jit(solution)/shard_map/ppermute | solution.py:73
  97.2 8.5 %collective-permute-start.23 = (bf16[1,1,8,8,128]{4,3,2,1,0:T(8,128)(2,1)S(1)}, bf16[1,1,8,8,128]{4,3,2,1,0:T(8,128)(2,1)S(1)}, u32[]{:S(2)}, u32[]{:S(2)}) collective-permute-start(bf16[1,1,8,8,128]{4,3,2,1,0:T(8,128)(2,1)S(1)} %get-tuple-element.44), channel_id=1, source_target_pairs={{10,0},{11,1},{12,2},{13,3},{14,4},{15,5},{18,8},{19,9},{20,10},{2... | collective-permute-start | bytes 49160 | tf_op jit(solution)/shard_map/ppermute | solution.py:73
  99.2 6.5 %collective-permute-start.22 = (bf16[1,1,1,8,128]{4,3,2,1,0:T(8,128)(2,1)S(1)}, bf16[1,1,1,8,128]{4,3,2,1,0:T(8,128)(2,1)S(1)}, u32[]{:S(2)}, u32[]{:S(2)}) collective-permute-start(bf16[1,1,1,8,128]{4,3,2,1,0:T(8,128)(2,1)S(1)} %constant_dynamic-slice_fusion.3), channel_id=1, source_target_pairs={{10,1},{11,0},{12,3},{13,2},{14,5},{15,4},{18,9},{19,8},{20,11},{2... | collective-permute-start | bytes 6152 | tf_op jit(solution)/shard_map/ppermute | solution.py:73
  106.8 6.7 %collective-permute-start.26 = (bf16[864,128]{1,0:T(8,128)(2,1)S(1)}, bf16[864,128]{1,0:T(8,128)(2,1)S(1)}, u32[]{:S(2)}, u32[]{:S(2)}) collective-permute-start(bf16[864,128]{1,0:T(8,128)(2,1)S(1)} %get-tuple-element.27), channel_id=1, source_target_pairs={{0,6},{2,0},{4,2},{6,4},{1,7},{3,1},{5,3},{7,5},{8,14},{10,8},{12,... | collective-permute-start | bytes 663560 | tf_op jit(solution)/shard_map/ppermute | solution.py:150
  108.2 11.0 %collective-permute-start.25 = (bf16[864,128]{1,0:T(8,128)(2,1)S(1)}, bf16[864,128]{1,0:T(8,128)(2,1)S(1)}, u32[]{:S(2)}, u32[]{:S(2)}) collective-permute-start(bf16[864,128]{1,0:T(8,128)(2,1)S(1)} %get-tuple-element.28), channel_id=1, source_target_pairs={{0,4},{2,6},{4,0},{6,2},{1,5},{3,7},{5,1},{7,3},{8,12},{10,14},{12... | collective-permute-start | bytes 663560 | tf_op jit(solution)/shard_map/ppermute | solution.py:150
  108.2 11.0 %collective-permute-start.24 = (bf16[864,128]{1,0:T(8,128)(2,1)S(1)}, bf16[864,128]{1,0:T(8,128)(2,1)S(1)}, u32[]{:S(2)}, u32[]{:S(2)}) collective-permute-start(bf16[864,128]{1,0:T(8,128)(2,1)S(1)} %get-tuple-element.26), channel_id=1, source_target_pairs={{0,2},{2,4},{4,6},{6,0},{1,3},{3,5},{5,7},{7,1},{8,10},{10,12},{12... | collective-permute-start | bytes 663560 | tf_op jit(solution)/shard_map/ppermute | solution.py:150
  111.6 9.4 %copy-start.7 = (bf16[512,128]{1,0:T(8,128)(2,1)S(1)}, bf16[512,128]{1,0:T(8,128)(2,1)}, u32[]{:S(2)}) copy-start(bf16[512,128]{1,0:T(8,128)(2,1)} %copy-done.6) | copy-start | bytes 393220
  111.6 9.4 %copy-start.9 = (bf16[512,128]{1,0:T(8,128)(2,1)S(1)}, bf16[512,128]{1,0:T(8,128)(2,1)}, u32[]{:S(2)}) copy-start(bf16[512,128]{1,0:T(8,128)(2,1)} %copy-done.8) | copy-start | bytes 393220
  119.3 3.0 %collective-permute-start.27 = (f32[864,128]{1,0:T(8,128)S(1)}, f32[864,128]{1,0:T(8,128)S(1)}, u32[]{:S(2)}, u32[]{:S(2)}) collective-permute-start(f32[864,128]{1,0:T(8,128)S(1)} %convert_add_fusion), channel_id=1, source_target_pairs={{0,1},{1,0},{2,3},{3,2},{4,5},{5,4},{6,7},{7,6},{8,9},{9,8},{10,11... | collective-permute-start | bytes 1327112 | tf_op jit(solution)/shard_map/ppermute | solution.py:234
